TPU v7x, 32 devices: a whole 2x2x4 slice. The times are simulated.
32 devices in a mesh: groups: 2 (over y), tok: 8 (over z, x), section: 2 (over core).
Axes of the slice: x: 2, y: 2, z: 4, core: 2. Of those that a mesh axis runs over, the one named last changes fastest.
Arguments:
- inputs: bfloat16 [4, 1024, 2048], P('groups', 'tok'), parts along dimension 0, may hold values from -11 to 11
- obs: bfloat16 [2048, 2048], P(('groups', 'tok')), parts along dimension 0, may hold values from -11 to 11
- weights: bfloat16 [2, 2048, 2048], P('section', 'tok'), may hold values from -0.125 to 0.125
- gains: float32 [2, 2048], P('section'), may hold values from 0.25 to 1.75
Outputs:
- section_grads: bfloat16 [2, 4, 1024, 2048], P('section', 'groups', 'tok'), parts along dimension 1
- energy: float32 [2], P('groups'), parts along dimension 0
There are 2 independent parts, one for each index of `groups`. A program takes and returns all parts, laid end to end along the dimension named above; an argument that names none is the same for every part. Nothing has to cross between parts.
All inputs are finite; a program needn't handle non-finite values.
Results may differ from a plain program's by a relative error of at most 0.008.
Values may be sent and summed in bfloat16 or wider, within the bound.
No kernel may reach another device: no remote copies, remote signals or barrier semaphores. Data moves between devices by JAX's collectives and lax.ppermute only.
A program may use at most 64 MiB of HBM per device.

v0:
```python
import math

import jax
import jax.numpy as jnp
from jax import lax
from jax.sharding import PartitionSpec as P

epsilon = 1e-05
gelu_scale = math.sqrt(2.0 / math.pi)
cubic_term = 0.044715


def shifted(x, axis, by):
    size = lax.axis_size(axis)
    pairs = [(i, i + by) for i in range(size) if 0 <= i + by < size]
    return lax.ppermute(x, axis, pairs)


def gelu_value(pre_act):
    inner = jnp.tanh(gelu_scale * (pre_act + cubic_term * pre_act * pre_act * pre_act))
    return 0.5 * pre_act * (1.0 + inner)


def gelu_slope(pre_act):
    inner = jnp.tanh(gelu_scale * (pre_act + cubic_term * pre_act * pre_act * pre_act))
    return 0.5 * (1.0 + inner) + 0.5 * pre_act * (1.0 - inner * inner) * gelu_scale * (
        1.0 + 3.0 * cubic_term * pre_act * pre_act
    )


def norm_part(rows_in, gain):
    values = rows_in.astype(jnp.float32)
    row_mean = jnp.mean(values, axis=-1, keepdims=True)
    centred = values - row_mean
    inv_std = lax.rsqrt(jnp.mean(centred * centred, axis=-1, keepdims=True) + epsilon)
    unit_rows = centred * inv_std
    normed = (unit_rows * gain).astype(jnp.bfloat16)
    return (values, unit_rows, inv_std, normed)


def finish_forward(values, pre_act):
    return (values + gelu_value(pre_act)).astype(jnp.bfloat16)


def section_forward(rows_in, gain, weight):
    values, unit_rows, inv_std, normed = norm_part(rows_in, gain)
    pre_act = jnp.dot(normed, weight, preferred_element_type=jnp.float32)
    return (finish_forward(values, pre_act), unit_rows, inv_std, pre_act)


def section_backward(grad_out, gain, weight, unit_rows, inv_std, pre_act):
    grad_pre = (grad_out * gelu_slope(pre_act)).astype(jnp.bfloat16)
    grad_norm = lax.dot_general(
        grad_pre, weight, (((1,), (1,)), ((), ())), preferred_element_type=jnp.float32
    )
    scaled = grad_norm * gain
    grad_in = grad_out + inv_std * (
        scaled
        - jnp.mean(scaled, axis=-1, keepdims=True)
        - unit_rows * jnp.mean(scaled * unit_rows, axis=-1, keepdims=True)
    )
    return grad_in.astype(jnp.bfloat16)


def score_terms(member_gram, member_obs, obs_sq, size):
    count = member_gram.shape[0]
    diag_vals = jnp.diagonal(member_gram)
    apart = diag_vals[:, None] + diag_vals[None, :] - 2.0 * member_gram
    same = jnp.eye(count, dtype=jnp.float32)
    others = 1.0 - same
    pair_dist = jnp.sqrt(jnp.where(same > 0.5, size, apart) / size + epsilon)
    to_obs = jnp.sqrt((diag_vals - 2.0 * member_obs + obs_sq) / size + epsilon)
    energy = jnp.mean(to_obs) - jnp.sum(others * pair_dist) / (2.0 * count * (count - 1))
    pair_coeff = others / (count * (count - 1) * pair_dist)
    obs_coeff = 1.0 / (count * to_obs)
    member_coeff = pair_coeff + same * (obs_coeff - jnp.sum(pair_coeff, axis=1))[:, None]
    return (energy, member_coeff, -obs_coeff)


def put_row(store, member, valid, value):
    previous = lax.dynamic_index_in_dim(store, member, 0, keepdims=False)
    return lax.dynamic_update_index_in_dim(store, jnp.where(valid, value, previous), member, 0)


def take_row(store, member):
    return lax.dynamic_index_in_dim(store, member, 0, keepdims=False)


def per_device(inputs, obs, weights, gains):
    section_pos = lax.axis_index("section")
    gain = gains[0]
    members = inputs.shape[0]
    tok_rows = obs.shape[0]
    width = obs.shape[1]
    size = float(tok_rows * lax.axis_size("tok") * width)
    arrived = jnp.zeros((tok_rows, width), jnp.bfloat16)
    rows_first = jnp.where(section_pos == 0, inputs[0], arrived)
    weight = lax.all_gather(weights, "tok", axis=1, tiled=True)[0]
    first_result = section_forward(rows_first, gain, weight)
    outs_all = jnp.zeros((members, tok_rows, width), jnp.bfloat16)
    unit_store = jnp.zeros((members, tok_rows, width), jnp.float32)
    pre_store = jnp.zeros((members, tok_rows, width), jnp.float32)
    std_store = jnp.zeros((members, tok_rows, 1), jnp.float32)
    square_part = jnp.einsum("rd,rd->", obs, obs, preferred_element_type=jnp.float32)
    for moment in range(members + 1):
        member_raw = moment - section_pos
        valid = (member_raw >= 0) & (member_raw < members)
        member = jnp.clip(member_raw, 0, members - 1)
        if moment == 0:
            output, unit_rows, inv_std, pre_act = first_result
        else:
            rows_in = jnp.where(section_pos == 0, take_row(inputs, member), arrived)
            output, unit_rows, inv_std, pre_act = section_forward(rows_in, gain, weight)
        outs_all = put_row(outs_all, member, valid, output)
        unit_store = put_row(unit_store, member, valid, unit_rows)
        std_store = put_row(std_store, member, valid, inv_std)
        pre_store = put_row(pre_store, member, valid, pre_act)
        if moment < members:
            arrived = shifted(output, "section", 1)
    gram_part = jnp.einsum("mrd,nrd->mn", outs_all, outs_all, preferred_element_type=jnp.float32)
    obs_part = jnp.einsum("mrd,rd->m", outs_all, obs, preferred_element_type=jnp.float32)
    member_gram, obs_rows, obs_sq = lax.psum((gram_part, obs_part, square_part), "tok")
    energy, member_coeff, obs_coeff = score_terms(member_gram, obs_rows, obs_sq, size)
    energy_arr = jnp.reshape(energy, (1,))
    energy_peer = shifted(energy_arr, "section", -1)
    energy_out = jnp.where(section_pos == 1, energy_arr, energy_peer)
    obs_f = obs.astype(jnp.float32)
    grads = jnp.zeros((members, tok_rows, width), jnp.bfloat16)
    returned = jnp.zeros((tok_rows, width), jnp.bfloat16)
    for moment in range(members + 1):
        member_raw = moment - 1 + section_pos
        valid = (member_raw >= 0) & (member_raw < members)
        member = jnp.clip(member_raw, 0, members - 1)
        coeff_row = take_row(member_coeff, member)
        target_coeff = take_row(obs_coeff, member)
        cotangent = (
            jnp.einsum("k,krd->rd", coeff_row, outs_all, preferred_element_type=jnp.float32)
            + target_coeff * obs_f
        )
        grad_out = jnp.where(section_pos == 1, cotangent, returned.astype(jnp.float32))
        unit_rows = take_row(unit_store, member)
        inv_std = take_row(std_store, member)
        pre_act = take_row(pre_store, member)
        grad_in = section_backward(grad_out, gain, weight, unit_rows, inv_std, pre_act)
        grads = put_row(grads, member, valid, grad_in)
        if moment < members:
            returned = shifted(grad_in, "section", -1)
    return (grads[None], energy_out)


def solution(mesh):
    in_specs = (
        P("groups", "tok", None),
        P(("groups", "tok"), None),
        P("section", "tok", None),
        P("section", None),
    )
    out_specs = (P("section", "groups", "tok", None), P("groups"))
    return jax.shard_map(
        per_device, mesh=mesh, in_specs=in_specs, out_specs=out_specs, check_vma=False
    )
```

profile of v0, /device:TPU:0, one launch (start us, length us, event | category | flops | bytes accessed | tf_op | source)
XLA Modules:
  0.0 264.5 jit_solution(9906071324537823886)
XLA Ops:
  7.2 0.7 all-gather.2.cloned.1.call-update
  7.9 1.9 fusion.109
  9.8 1.2 convert_reduce_fusion.2
  11.9 1.1 constant_dynamic-slice_fusion.6
  12.9 124.4 %all-gather.2.cloned.1.call-done = bf16[1,2048,2048]{2,1,0:T(8,128)(2,1)} async-done(((bf16[1,256,2048]{2,1,0:T(8,128)(2,1)}), bf16[1,2048,2048]{2,1,0:T(8,128)(2,1)}) %all-gather.2.cloned.1.call-update) | async-done | bytes 8388624 | tf_op jit(solution)/shard_map/all_gather | solution.py:98
  137.3 1.6 broadcast.301.clone.1
  139.0 5.9 %bitcast_dynamic-update-slice_fusion.2 = (f32[2,128,2048]{2,1,0:T(8,128)}, f32[128,2048]{1,0:T(8,128)S(1)}) fusion(f32[2,128,2048]{2,1,0:T(8,128)} %broadcast.301.clone.1, s32[]{:T(128)S(6)} %min.19, pred[]{:T(512)S(6)} %and.20, bf16[1,2048,2048]{2,1,0:T(8,128)(2,1)} %all-gather.2.cloned.1.call-done, f32[2048]{0:T(1024)S(1)} %bitcast.283, ...), kind=kOutput, calls=%fused_computation.140 | convolution fusion | flops 1075576832 | bytes 11019270 | tf_op jit(solution)/shard_map/dot_general | solution.py:47
  144.9 1.1 broadcast.282.clone
  146.0 1.5 bitcast_dynamic-update-slice_fusion.7
  147.5 2.1 collective-permute-start
  149.6 2.0 copy.10
  151.6 1.2 constant_dynamic-slice_fusion.14
  152.8 1.4 constant_dynamic-slice_fusion.8
  154.5 0.3 fusion.38
  154.8 0.4 fusion.33
  155.2 6.0 %bitcast_dynamic-update-slice_fusion.1 = (f32[2,128,2048]{2,1,0:T(8,128)}, f32[128,2048]{1,0:T(8,128)S(1)}) fusion(f32[2,128,2048]{2,1,0:T(8,128)} %get-tuple-element.37, s32[]{:T(128)S(6)} %min.20, f32[1,128,2048]{2,1,0:T(8,128)S(1)} %constant_dynamic-slice_fusion.8, pred[]{:T(512)S(6)} %and.21, bf16[1,2048,2048]{2,1,0:T(8,128)(2,1)} %all-gather.2.cloned.1.call-done, ...), kind=kOutput, calls=%fused_computation.138 | convolution fusion | flops 1075314688 | bytes 12067845 | tf_op jit(solution)/shard_map/dot_general | solution.py:47
  161.2 1.3 bitcast_dynamic-update-slice_fusion.6
  162.5 1.5 collective-permute-start.1
  164.0 1.1 constant_dynamic-slice_fusion.13
  165.1 2.4 constant_dynamic-slice_fusion.5
  167.8 0.3 fusion.37
  168.1 2.4 bitcast_dynamic-update-slice_fusion
  170.5 1.3 bitcast_dynamic-update-slice_fusion.5
  171.8 3.7 %copy.8 = bf16[2,128,2048]{1,0,2:T(2,128)(2,1)} copy(bf16[2,128,2048]{2,1,0:T(8,128)(2,1)} %bitcast_dynamic-update-slice_fusion.5) | data formatting | bytes 2097152 | tf_op jit(solution)/shard_map/jit(dynamic_update_index_in_dim)/dynamic_update_slice | solution.py:82
  175.5 4.7 %convolution_bitcast_fusion = f32[2,2]{1,0:T(2,128)S(1)} fusion(bf16[2,128,2048]{1,0,2:T(2,128)(2,1)} %copy.8), kind=kOutput, calls=%fused_computation.47 | convolution fusion | flops 2097152 | bytes 1048592 | tf_op jit(solution)/shard_map/mrd,nrd->mn/dot_general | solution.py:120
  180.2 2.8 %convolution_bitcast_fusion.1 = f32[2]{0:T(128)S(1)} fusion(bf16[2,128,2048]{1,0,2:T(2,128)(2,1)S(1)} %copy-done.8, bf16[128,2048,1]{0,2,1:T(2,128)(2,1)S(1)} %copy-done.6), kind=kOutput, calls=%fused_computation.48 | convolution fusion | flops 1048576 | bytes 1572872 | tf_op jit(solution)/shard_map/mrd,rd->m/dot_general | solution.py:121
  183.0 0.4 fusion.36
  183.4 19.9 %all-reduce = (f32[2,2]{1,0:T(2,128)S(1)}, f32[2]{0:T(128)S(1)}, f32[]{:T(128)}) all-reduce(f32[2,2]{1,0:T(2,128)S(1)} %convolution_bitcast_fusion, f32[2]{0:T(128)S(1)} %convolution_bitcast_fusion.1, f32[]{:T(128)} %fusion.109), channel_id=1, replica_groups=mesh['groups'=2,'tok'=8,'section'=2] {'tok'}, use_global_device_ids=true, to_apply=%region_6.7 | all-reduce | flops 7 | bytes 56 | tf_op jit(solution)/shard_map/psum | solution.py:122
  203.3 0.6 gather_fusion
  204.0 0.7 fusion.161
  204.8 1.3 fusion.196
  206.2 2.5 fusion.154
  208.7 0.6 fusion.204
  209.3 7.6 %fusion.194 = (f32[128]{0:T(128)S(1)}, f32[128]{0:T(128)S(1)}, f32[128,2048]{1,0:T(8,128)S(1)}) fusion(f32[2,128,2048]{2,1,0:T(8,128)S(1)} %fusion.36, s32[]{:T(128)S(6)} %min.22, f32[2048]{0:T(1024)S(1)} %bitcast.286, bf16[1,2048,2048]{2,1,0:T(8,128)(2,1)} %all-gather.2.cloned.1.call-done, f32[2,128,2048]{2,1,0:T(8,128)} %get-tuple-element.41, ...), kind=kOutput, calls=%fused_computation.266 | convolution fusion | flops 1080819456 | bytes 13118464 | tf_op jit(solution)/shard_map/dot_general | solution.py:53
  217.0 1.1 broadcast.282
  218.1 2.2 bitcast_dynamic-update-slice_fusion.4
  220.3 1.5 collective-permute-start.2
  221.8 1.1 constant_dynamic-slice_fusion.2
  222.9 2.5 fusion.152
  225.4 7.9 %fusion.193 = (f32[128]{0:T(128)S(1)}, f32[128]{0:T(128)S(1)}, f32[128,2048]{1,0:T(8,128)S(1)}) fusion(f32[2,128,2048]{2,1,0:T(8,128)S(1)} %fusion.36, s32[]{:T(128)S(6)} %min.23, f32[2048]{0:T(1024)S(1)} %bitcast.287, bf16[1,2048,2048]{2,1,0:T(8,128)(2,1)} %all-gather.2.cloned.1.call-done, f32[2,128,2048]{2,1,0:T(8,128)} %get-tuple-element.41, ...), kind=kOutput, calls=%fused_computation.265 | convolution fusion | flops 1081081600 | bytes 13642752 | tf_op jit(solution)/shard_map/dot_general | solution.py:53
  233.3 3.6 %bitcast_dynamic-update-slice_fusion.3 = (bf16[2,128,2048]{2,1,0:T(8,128)(2,1)}, bf16[128,2048]{1,0:T(8,128)(2,1)}) fusion(bf16[2,128,2048]{2,1,0:T(8,128)(2,1)} %get-tuple-element.17, s32[]{:T(128)S(6)} %min.23, bf16[1,128,2048]{2,1,0:T(8,128)(2,1)S(1)} %constant_dynamic-slice_fusion.2, pred[]{:T(512)S(6)} %and.23, f32[128]{0:T(128)S(1)} %broadcast_multiply_fusion.2, ...), kind=kLoop, calls=%fused_computation.148 | loop fusion | flops 3145728 | bytes 5769733 | tf_op jit(solution)/shard_map/jit(dynamic_update_index_in_dim)/dynamic_update_slice | solution.py:82
  237.0 1.3 collective-permute-start.3
  239.5 1.3 collective-permute-start.4
  240.8 2.5 fusion.150
  243.9 1.2 copy.66
  245.1 7.8 %fusion.192 = (f32[128]{0:T(128)S(1)}, f32[128]{0:T(128)S(1)}, f32[128,2048]{1,0:T(8,128)S(1)}) fusion(f32[2,128,2048]{2,1,0:T(8,128)S(1)} %fusion.36, s32[]{:T(128)S(6)} %min.24, f32[2048]{0:T(1024)S(1)} %bitcast.288, bf16[1,2048,2048]{2,1,0:T(8,128)(2,1)} %all-gather.2.cloned.1.call-done, f32[2,128,2048]{2,1,0:T(8,128)} %get-tuple-element.41, ...), kind=kOutput, calls=%fused_computation.264 | convolution fusion | flops 1081081600 | bytes 13642752 | tf_op jit(solution)/shard_map/dot_general | solution.py:53
  252.9 2.6 %fusion.112 = bf16[1,2,128,2048]{3,2,1,0:T(8,128)(2,1)S(1)} fusion(bf16[1,2,128,2048]{3,2,1,0:T(8,128)(2,1)S(1)} %copy.66, s32[]{:T(128)S(6)} %min.24, f32[2,128,2048]{2,1,0:T(8,128)S(1)} %fusion.36, f32[128,2048]{1,0:T(8,128)S(1)} %get-tuple-element.45, bf16[2,128,2048]{2,1,0:T(8,128)(2,1)} %get-tuple-element.15, f32[128]{0:T(128)S(1)} %broadcast_multiply_fusion, ...), kind=kLoop, calls=%fused_computation.145 | loop fusion | flops 3145728 | bytes 5244426 | tf_op jit(solution)/shard_map/jit(dynamic_update_index_in_dim)/dynamic_update_slice | solution.py:82
  255.6 1.0 copy-done.7
  (57 shorter events, 1.7 us)
Async XLA Ops:
  7.2 3.9 %copy-start.1 = (bf16[2,128,2048]{2,1,0:T(8,128)(2,1)S(1)}, bf16[2,128,2048]{2,1,0:T(8,128)(2,1)}, u32[]{:S(2)}) copy-start(bf16[2,128,2048]{2,1,0:T(8,128)(2,1)} %param.4) | copy-start | bytes 3145732
  7.2 130.2 %all-gather.2.cloned.1.call-start = ((), (), s32[]{:S(2)}) async-start(), calls=%async_computation | async-start | bytes 9437184 | tf_op jit(solution)/shard_map/all_gather | solution.py:98
  11.8 127.1 %copy-start.9 = (f32[1,2048]{1,0:T(1,128)S(1)}, f32[1,2048]{1,0:T(1,128)}, u32[]{:S(2)}) copy-start(f32[1,2048]{1,0:T(1,128)} %param.7) | copy-start | bytes 24580
  139.0 7.0 %copy-start.2 = (bf16[2,128,2048]{2,1,0:T(8,128)(2,1)S(1)}, bf16[2,128,2048]{2,1,0:T(8,128)(2,1)}, u32[]{:S(2)}) copy-start(bf16[2,128,2048]{2,1,0:T(8,128)(2,1)} %param.4) | copy-start | bytes 3145732
  144.9 4.7 %copy-start = (bf16[128,2048]{1,0:T(8,128)(2,1)S(1)}, bf16[128,2048]{1,0:T(8,128)(2,1)}, u32[]{:S(2)}) copy-start(bf16[128,2048]{1,0:T(8,128)(2,1)} %param.5) | copy-start | bytes 1572868
  147.5 6.7 %collective-permute-start = (bf16[128,2048]{1,0:T(8,128)(2,1)}, bf16[128,2048]{1,0:T(8,128)(2,1)}, u32[]{:S(2)}, u32[]{:S(2)}) collective-permute-start(bf16[128,2048]{1,0:T(8,128)(2,1)} %get-tuple-element.26), channel_id=1, source_target_pairs={{0,1},{2,3},{4,5},{6,7},{8,9},{10,11},{12,13},{14,15},{16,17},{18,... | collective-permute-start | bytes 1572872 | tf_op jit(solution)/shard_map/ppermute | solution.py:16
  151.6 2.6 copy-start.3
  152.8 2.0 copy-start.5
  154.8 13.3 %slice-start = ((s8[8388608]{0:T(1024)(128)(4,1)}), s8[4194304]{0:T(1024)(128)(4,1)S(1)}, s32[]{:S(2)}) async-start(s8[8388608]{0:T(1024)(128)(4,1)} %bitcast.280), calls=%async_computation.1 | async-start | bytes 8388608
  155.2 12.9 %slice-start.1 = ((s8[8388608]{0:T(1024)(128)(4,1)}), s8[4194304]{0:T(1024)(128)(4,1)S(1)}, s32[]{:S(2)}) async-start(s8[8388608]{0:T(1024)(128)(4,1)} %bitcast.280), calls=%async_computation.2 | async-start | bytes 8388608
  162.5 5.0 %collective-permute-start.1 = (bf16[128,2048]{1,0:T(8,128)(2,1)S(1)}, bf16[128,2048]{1,0:T(8,128)(2,1)S(1)}, u32[]{:S(2)}, u32[]{:S(2)}) collective-permute-start(bf16[128,2048]{1,0:T(8,128)(2,1)S(1)} %get-tuple-element.24), channel_id=1, source_target_pairs={{0,1},{2,3},{4,5},{6,7},{8,9},{10,11},{12,13},{14,15},{16,17},{18,... | collective-permute-start | bytes 1572872 | tf_op jit(solution)/shard_map/ppermute | solution.py:16
  175.4 4.7 %copy-start.6 = (bf16[128,2048,1]{0,2,1:T(2,128)(2,1)S(1)}, bf16[128,2048,1]{0,2,1:T(2,128)(2,1)}, u32[]{:S(2)}) copy-start(bf16[128,2048,1]{0,2,1:T(2,128)(2,1)} %copy.10) | copy-start | bytes 1572868
  175.4 4.7 %copy-start.8 = (bf16[2,128,2048]{1,0,2:T(2,128)(2,1)S(1)}, bf16[2,128,2048]{1,0,2:T(2,128)(2,1)}, u32[]{:S(2)}) copy-start(bf16[2,128,2048]{1,0,2:T(2,128)(2,1)} %copy.8) | copy-start | bytes 3145732
  180.2 2.8 %copy-start.4 = (f32[1,128,2048]{2,1,0:T(8,128)S(1)}, f32[1,128,2048]{2,1,0:T(8,128)}, u32[]{:S(2)}) copy-start(f32[1,128,2048]{2,1,0:T(8,128)} %get-tuple-element.46) | copy-start | bytes 3145732
  220.3 5.1 %collective-permute-start.2 = (bf16[128,2048]{1,0:T(8,128)(2,1)}, bf16[128,2048]{1,0:T(8,128)(2,1)}, u32[]{:S(2)}, u32[]{:S(2)}) collective-permute-start(bf16[128,2048]{1,0:T(8,128)(2,1)} %get-tuple-element.18), channel_id=1, source_target_pairs={{1,0},{3,2},{5,4},{7,6},{9,8},{11,10},{13,12},{15,14},{17,16},{19,... | collective-permute-start | bytes 1572872 | tf_op jit(solution)/shard_map/ppermute | solution.py:16
  237.0 8.2 %collective-permute-start.3 = (bf16[128,2048]{1,0:T(8,128)(2,1)}, bf16[128,2048]{1,0:T(8,128)(2,1)S(1)}, u32[]{:S(2)}, u32[]{:S(2)}) collective-permute-start(bf16[128,2048]{1,0:T(8,128)(2,1)} %get-tuple-element.16), channel_id=1, source_target_pairs={{1,0},{3,2},{5,4},{7,6},{9,8},{11,10},{13,12},{15,14},{17,16},{19,... | collective-permute-start | bytes 1572872 | tf_op jit(solution)/shard_map/ppermute | solution.py:16
  239.5 3.8 %collective-permute-start.4 = (f32[1]{0:T(128)}, f32[1]{0:T(128)}, u32[]{:S(2)}, u32[]{:S(2)}) collective-permute-start(f32[1]{0:T(128)} %bitcast.57), channel_id=1, source_target_pairs={{1,0},{3,2},{5,4},{7,6},{9,8},{11,10},{13,12},{15,14},{17,16},{19,... | collective-permute-start | bytes 20 | tf_op jit(solution)/shard_map/ppermute | solution.py:16
  255.6 1.0 copy-start.7
Sparse Core Ops, SparseCore 0:
  10.1 127.1 all-gather.1
where the time goes:
time: 268 us; the launch traced here: 265 us
  waiting for transfers between devices  125 us (47%)
  matrix products  52.5 us (20%)
  local copies, waits for them, and re-layouts  21.4 us (8%)
  other arithmetic  20.4 us (8%)
  blocking collectives  19.9 us (7%)
  between operations  17.3 us (6%)
  starting transfers between devices  7.77 us (3%)
    all_gather x1, waiting for transfers between devices, per_device(): weight = lax.all_gather(weights, 'tok', axis=1, tiled=True)[0]  124 us
    dot_general x3, matrix products, section_backward(): lax.dot_general(grad_pre, weight, (((1,), (1,)), ((), ())), preferred_ele...  23.3 us
    psum x1, blocking collectives, per_device(): lax.psum((gram_part, obs_part, square_part), 'tok')  19.9 us
    dot_general x3, matrix products, section_forward(): pre_act = jnp.dot(normed, weight, preferred_element_type=jnp.float32)  14.3 us
    dynamic_update_slice x12, other arithmetic, put_row(): lax.dynamic_update_index_in_dim(store, jnp.where(valid, value, previous),...  13.5 us
    dynamic_slice x6, local copies, waits for them, and re-layouts, put_row(): previous = lax.dynamic_index_in_dim(store, member, 0, keepdims=False)  8.18 us
    ppermute x5, starting transfers between devices, shifted(): return lax.ppermute(x, axis, pairs)  7.73 us
    dot_general x3, matrix products, per_device(): jnp.einsum('k,krd->rd', coeff_row, outs_all, preferred_element_type=jnp.f...  7.36 us
  transfers between devices with their start and end apart: 6, of which 1 were waited for; matrix products, arithmetic and copies ran while one was open for 8% of the time, Pallas kernels for 0%

commit v1 on v0

v1 whole, which is shorter than its diff:
```python
import math

import jax
import jax.numpy as jnp
from jax import lax
from jax.sharding import PartitionSpec as P

epsilon = 1e-05
gelu_scale = math.sqrt(2.0 / math.pi)
cubic_term = 0.044715

RING_GATHER = True


def shifted(x, axis, by):
    size = lax.axis_size(axis)
    pairs = [(i, i + by) for i in range(size) if 0 <= i + by < size]
    return lax.ppermute(x, axis, pairs)


def gelu_value(pre_act):
    inner = jnp.tanh(gelu_scale * (pre_act + cubic_term * pre_act * pre_act * pre_act))
    return 0.5 * pre_act * (1.0 + inner)


def gelu_slope(pre_act):
    inner = jnp.tanh(gelu_scale * (pre_act + cubic_term * pre_act * pre_act * pre_act))
    return 0.5 * (1.0 + inner) + 0.5 * pre_act * (1.0 - inner * inner) * gelu_scale * (
        1.0 + 3.0 * cubic_term * pre_act * pre_act
    )


def section_forward(rows_in, gain, weight):
    values = rows_in.astype(jnp.float32)
    row_mean = jnp.mean(values, axis=-1, keepdims=True)
    centred = values - row_mean
    inv_std = lax.rsqrt(jnp.mean(centred * centred, axis=-1, keepdims=True) + epsilon)
    unit_rows = centred * inv_std
    normed = (unit_rows * gain).astype(jnp.bfloat16)
    pre_act = jnp.dot(normed, weight, preferred_element_type=jnp.float32)
    output = (values + gelu_value(pre_act)).astype(jnp.bfloat16)
    return (output, unit_rows, inv_std, pre_act)


def section_backward(grad_out, gain, weight, unit_rows, inv_std, pre_act):
    grad_pre = (grad_out * gelu_slope(pre_act)).astype(jnp.bfloat16)
    grad_norm = lax.dot_general(
        grad_pre, weight, (((1,), (1,)), ((), ())), preferred_element_type=jnp.float32
    )
    scaled = grad_norm * gain
    grad_in = grad_out + inv_std * (
        scaled
        - jnp.mean(scaled, axis=-1, keepdims=True)
        - unit_rows * jnp.mean(scaled * unit_rows, axis=-1, keepdims=True)
    )
    return grad_in.astype(jnp.bfloat16)


def score_terms(member_gram, member_obs, obs_sq, size):
    count = member_gram.shape[0]
    diag_vals = jnp.diagonal(member_gram)
    apart = diag_vals[:, None] + diag_vals[None, :] - 2.0 * member_gram
    same = jnp.eye(count, dtype=jnp.float32)
    others = 1.0 - same
    pair_dist = jnp.sqrt(jnp.where(same > 0.5, size, apart) / size + epsilon)
    to_obs = jnp.sqrt((diag_vals - 2.0 * member_obs + obs_sq) / size + epsilon)
    energy = jnp.mean(to_obs) - jnp.sum(others * pair_dist) / (2.0 * count * (count - 1))
    pair_coeff = others / (count * (count - 1) * pair_dist)
    obs_coeff = 1.0 / (count * to_obs)
    member_coeff = pair_coeff + same * (obs_coeff - jnp.sum(pair_coeff, axis=1))[:, None]
    return (energy, member_coeff, -obs_coeff)


def snake_ring(n):
    if n % 2:
        return list(range(n))
    return list(range(0, n, 2)) + list(range(n - 1, 0, -2))


def ring_gather(local, axis):
    n = lax.axis_size(axis)
    rows, cols = local.shape
    if n == 1:
        return local
    ring = snake_ring(n)
    pos_of = [0] * n
    for p, t in enumerate(ring):
        pos_of[t] = p
    me = lax.axis_index(axis)
    my_pos = jnp.asarray(pos_of, jnp.int32)[me]
    ring_arr = jnp.asarray(ring, jnp.int32)
    cw = [(ring[i], ring[(i + 1) % n]) for i in range(n)]
    ccw = [(ring[(i + 1) % n], ring[i]) for i in range(n)]
    half = cols // 2
    left = local[:, :half]
    right = local[:, half:]
    full = jnp.zeros((n * rows, cols), local.dtype)
    full = lax.dynamic_update_slice(full, local, (me * rows, 0))
    for k in range(1, n):
        left = lax.ppermute(left, axis, cw)
        right = lax.ppermute(right, axis, ccw)
        from_left = ring_arr[(my_pos - k) % n]
        from_right = ring_arr[(my_pos + k) % n]
        full = lax.dynamic_update_slice(full, left, (from_left * rows, 0))
        full = lax.dynamic_update_slice(full, right, (from_right * rows, half))
    return full


def tree_sum(v, axis):
    n = lax.axis_size(axis)
    if n & (n - 1):
        return lax.psum(v, axis)
    b = 1
    while b < n:
        v = v + lax.ppermute(v, axis, [(i, i ^ b) for i in range(n)])
        b *= 2
    return v


def per_device(inputs, obs, weights, gains):
    sec = lax.axis_index("section")
    on_first = sec == 0
    gain = gains[0]
    tok_rows = obs.shape[0]
    width = obs.shape[1]
    size = float(tok_rows * lax.axis_size("tok") * width)

    obs_sq = jnp.einsum("rd,rd->", obs, obs, preferred_element_type=jnp.float32)

    if RING_GATHER:
        weight = ring_gather(weights[0], "tok")
    else:
        weight = lax.all_gather(weights, "tok", axis=1, tiled=True)[0]

    fa = section_forward(inputs[0], gain, weight)
    arrived0 = shifted(fa[0], "section", 1)
    fb = section_forward(jnp.where(on_first, inputs[1], arrived0), gain, weight)
    arrived1 = shifted(fb[0], "section", 1)
    fc = section_forward(arrived1, gain, weight)

    y0 = fb[0]
    y1 = fc[0]
    gram = jnp.einsum(
        "mrd,nrd->mn", jnp.stack([y0, y1]), jnp.stack([y0, y1]),
        preferred_element_type=jnp.float32,
    )
    obs_part = jnp.einsum(
        "mrd,rd->m", jnp.stack([y0, y1]), obs, preferred_element_type=jnp.float32
    )
    packed = jnp.concatenate([gram.reshape(4), obs_part, obs_sq.reshape(1)])
    packed = tree_sum(packed, "tok")
    member_gram = packed[:4].reshape(2, 2)
    obs_rows = packed[4:6]
    obs_total = packed[6]
    energy, member_coeff, obs_coeff = score_terms(member_gram, obs_rows, obs_total, size)
    energy_arr = jnp.reshape(energy, (1,))
    energy_peer = shifted(energy_arr, "section", -1)
    energy_out = jnp.where(on_first, energy_peer, energy_arr)

    obs_f = obs.astype(jnp.float32)
    y0f = y0.astype(jnp.float32)
    y1f = y1.astype(jnp.float32)

    def cotangent(m):
        return member_coeff[m, 0] * y0f + member_coeff[m, 1] * y1f + obs_coeff[m] * obs_f

    d0 = section_backward(cotangent(0), gain, weight, fb[1], fb[2], fb[3])
    back0 = shifted(d0, "section", -1)
    g1 = jnp.where(on_first, back0.astype(jnp.float32), cotangent(1))
    h1 = jnp.where(on_first, fa[1], fc[1])
    q1 = jnp.where(on_first, fa[2], fc[2])
    p1 = jnp.where(on_first, fa[3], fc[3])
    d1 = section_backward(g1, gain, weight, h1, q1, p1)
    back1 = shifted(d1, "section", -1)
    d2 = section_backward(back1.astype(jnp.float32), gain, weight, fb[1], fb[2], fb[3])

    first_m0 = jnp.where(on_first, d1, d0)
    first_m1 = jnp.where(on_first, d2, d1)
    grads = jnp.stack([first_m0, first_m1])
    return (grads[None], energy_out)


def solution(mesh):
    in_specs = (
        P("groups", "tok", None),
        P(("groups", "tok"), None),
        P("section", "tok", None),
        P("section", None),
    )
    out_specs = (P("section", "groups", "tok", None), P("groups"))
    return jax.shard_map(
        per_device, mesh=mesh, in_specs=in_specs, out_specs=out_specs, check_vma=False
    )
```

time: 268 us -> 216 us (0.81)
  waiting for transfers between devices: 125 us -> 64.1 us
  blocking collectives: 19.9 us -> 0 us
  starting transfers between devices: 7.77 us -> 27.1 us
  local copies, waits for them, and re-layouts: 21.4 us -> 33.6 us
  other arithmetic: 20.4 us -> 15 us
  between operations: 17.3 us -> 21.9 us
    all_gather x1 -> x0, waiting for transfers between devices: 124 us -> none  [per_device(): weight = lax.all_gather(weights, 'tok', axis=1, tiled=True)[0]]
    ppermute x0 -> x17, waiting for transfers between devices: none -> 58.6 us  [the longest x7 37.7 us: ring_gather(): left = lax.ppermute(left, axis, cw)]
    psum x1 -> x0, blocking collectives: 19.9 us -> none  [per_device(): lax.psum((gram_part, obs_part, square_part), 'tok')]
    ppermute x0 -> x17, starting transfers between devices: none -> 19.2 us  [the longest x7 11.5 us: ring_gather(): left = lax.ppermute(left, axis, cw)]
    dynamic_update_slice x1 -> x15, local copies, waits for them, and re-layouts: 3.67 us -> 18.3 us  [the longest x7 9.14 us: ring_gather(): full = lax.dynamic_update_slice(full, left, (from_left * rows, 0))]
    dynamic_update_slice x12 -> x0, other arithmetic: 13.5 us -> none  [put_row(): lax.dynamic_update_index_in_dim(store, jnp.where(valid, value, previous),...]
    dynamic_slice x7 -> x2, local copies, waits for them, and re-layouts: 8.81 us -> 1.31 us  [the longest x1 0.72 us: ring_gather(): from_right = ring_arr[(my_pos + k) % n]]
    dot_general x5 -> x2, matrix products: 14.9 us -> 8.83 us  [the longest x1 4.48 us: per_device(): jnp.einsum('mrd,nrd->mn', jnp.stack([y0, y1]), jnp.stack([y0, y1]), prefe...]
  transfers between devices with their start and end apart: 6 -> 22, of which waited for: 1 -> 13; matrix products, arithmetic and copies ran while one was open for 8% -> 12% of each run, Pallas kernels for 0% -> 0%
where the time goes in v1:
time: 216 us; the launch traced here: 214 us
  waiting for transfers between devices  64.1 us (30%)
  matrix products  51.9 us (24%)
  local copies, waits for them, and re-layouts  33.6 us (16%)
  starting transfers between devices  27.1 us (13%)
  between operations  21.9 us (10%)
  other arithmetic  15 us (7%)
    ppermute x7, waiting for transfers between devices, ring_gather(): left = lax.ppermute(left, axis, cw)  37.7 us
    dot_general x3, matrix products, section_backward(): lax.dot_general(grad_pre, weight, (((1,), (1,)), ((), ())), preferred_ele...  24.9 us
    dot_general x3, matrix products, section_forward(): pre_act = jnp.dot(normed, weight, preferred_element_type=jnp.float32)  18.2 us
    ppermute x7, waiting for transfers between devices, ring_gather(): right = lax.ppermute(right, axis, ccw)  13.7 us
    ppermute x7, starting transfers between devices, ring_gather(): left = lax.ppermute(left, axis, cw)  11.5 us
    dynamic_update_slice x7, local copies, waits for them, and re-layouts, ring_gather(): full = lax.dynamic_update_slice(full, left, (from_left * rows, 0))  9.14 us
    dynamic_update_slice x7, local copies, waits for them, and re-layouts, ring_gather(): full = lax.dynamic_update_slice(full, right, (from_right * rows, half))  8.15 us
    ppermute x5, starting transfers between devices, shifted(): return lax.ppermute(x, axis, pairs)  7.87 us
  transfers between devices with their start and end apart: 22, of which 13 were waited for; matrix products, arithmetic and copies ran while one was open for 12% of the time, Pallas kernels for 0%

profile of v1, /device:TPU:0, one launch (start us, length us, event | category | flops | bytes accessed | tf_op | source)
XLA Modules:
  0.0 213.7 jit_solution(745551468157031046)
XLA Ops:
  0.7 1.4 fusion.110
  2.1 3.1 %collective-permute-start = (bf16[256,1024]{1,0:T(8,128)(2,1)S(1)}, bf16[256,1024]{1,0:T(8,128)(2,1)S(1)}, u32[]{:S(2)}, u32[]{:S(2)}) collective-permute-start(bf16[256,1024]{1,0:T(8,128)(2,1)S(1)} %get-tuple-element.21), channel_id=1, source_target_pairs={{0,4},{4,8},{8,12},{12,14},{14,10},{10,6},{6,2},{2,0},{1,5},{5,9},... | collective-permute-start | bytes 1572872 | tf_op jit(solution)/shard_map/ppermute | solution.py:100
  5.2 11.8 %collective-permute-done = bf16[256,1024]{1,0:T(8,128)(2,1)S(1)} collective-permute-done((bf16[256,1024]{1,0:T(8,128)(2,1)S(1)}, bf16[256,1024]{1,0:T(8,128)(2,1)S(1)}, u32[]{:S(2)}, u32[]{:S(2)}) %collective-permute-start) | collective-permute-done | bytes 524320 | tf_op jit(solution)/shard_map/ppermute | solution.py:100
  17.0 1.8 collective-permute-start.2
  19.1 11.1 %collective-permute-done.2 = bf16[256,1024]{1,0:T(8,128)(2,1)S(1)} collective-permute-done((bf16[256,1024]{1,0:T(8,128)(2,1)S(1)}, bf16[256,1024]{1,0:T(8,128)(2,1)S(1)}, u32[]{:S(2)}, u32[]{:S(2)}) %collective-permute-start.2) | collective-permute-done | bytes 524320 | tf_op jit(solution)/shard_map/ppermute | solution.py:100
  30.1 1.5 collective-permute-start.4
  32.2 10.3 %collective-permute-done.4 = bf16[256,1024]{1,0:T(8,128)(2,1)} collective-permute-done((bf16[256,1024]{1,0:T(8,128)(2,1)S(1)}, bf16[256,1024]{1,0:T(8,128)(2,1)}, u32[]{:S(2)}, u32[]{:S(2)}) %collective-permute-start.4) | collective-permute-done | bytes 524320 | tf_op jit(solution)/shard_map/ppermute | solution.py:100
  42.5 1.3 collective-permute-start.6
  43.7 4.3 %broadcast_in_dim.15 = bf16[2048,2048]{1,0:T(8,128)(2,1)} broadcast(bf16[]{:T(256)} %constant.169.clone.1), dimensions={} | broadcast | bytes 8388610 | tf_op jit(solution)/shard_map/broadcast_in_dim | solution.py:97
  50.0 4.5 %collective-permute-done.6 = bf16[256,1024]{1,0:T(8,128)(2,1)} collective-permute-done((bf16[256,1024]{1,0:T(8,128)(2,1)}, bf16[256,1024]{1,0:T(8,128)(2,1)}, u32[]{:S(2)}, u32[]{:S(2)}) %collective-permute-start.6) | collective-permute-done | bytes 524320 | tf_op jit(solution)/shard_map/ppermute | solution.py:100
  54.6 1.3 collective-permute-start.8
  76.3 1.9 constant_dynamic-update-slice_fusion.13
  78.2 2.0 constant_dynamic-update-slice_fusion.6
  80.1 1.2 collective-permute-start.10
  82.2 5.4 %collective-permute-done.9 = bf16[256,1024]{1,0:T(8,128)(2,1)S(1)} collective-permute-done((bf16[256,1024]{1,0:T(8,128)(2,1)S(1)}, bf16[256,1024]{1,0:T(8,128)(2,1)S(1)}, u32[]{:S(2)}, u32[]{:S(2)}) %collective-permute-start.9) | collective-permute-done | bytes 524320 | tf_op jit(solution)/shard_map/ppermute | solution.py:101
  89.2 1.9 constant_dynamic-update-slice_fusion.11
  91.1 1.9 constant_dynamic-update-slice_fusion.4
  93.0 1.9 constant_dynamic-update-slice_fusion.10
  95.0 1.3 collective-permute-start.12
  97.1 3.7 %collective-permute-done.11 = bf16[256,1024]{1,0:T(8,128)(2,1)S(1)} collective-permute-done((bf16[256,1024]{1,0:T(8,128)(2,1)S(1)}, bf16[256,1024]{1,0:T(8,128)(2,1)S(1)}, u32[]{:S(2)}, u32[]{:S(2)}) %collective-permute-start.11) | collective-permute-done | bytes 524320 | tf_op jit(solution)/shard_map/ppermute | solution.py:101
  105.2 4.7 %collective-permute-done.13 = bf16[256,1024]{1,0:T(8,128)(2,1)S(1)} collective-permute-done((bf16[256,1024]{1,0:T(8,128)(2,1)S(1)}, bf16[256,1024]{1,0:T(8,128)(2,1)S(1)}, u32[]{:S(2)}, u32[]{:S(2)}) %collective-permute-start.13) | collective-permute-done | bytes 524320 | tf_op jit(solution)/shard_map/ppermute | solution.py:101
  110.7 6.0 %fusion.30 = (bf16[128,2048]{1,0:T(8,128)(2,1)S(1)}, f32[128,2048]{1,0:T(8,128)}) fusion(bf16[2,128,2048]{2,1,0:T(8,128)(2,1)S(1)} %copy-done.2, bf16[2048,2048]{1,0:T(8,128)(2,1)} %constant_dynamic-update-slice_fusion, f32[2048]{0:T(1024)S(1)} %bitcast.106, f32[128]{0:T(128)S(1)} %add_rsqrt_fusion.2, f32[128]{0:T(128)S(1)} %broadcast_multiply_fusion.8), kind=kOutput, calls=%fused_computation.58 | convolution fusion | flops 1077936128 | bytes 11019264 | tf_op jit(solution)/shard_map/dot_general | solution.py:40
  116.8 1.3 collective-permute-start.14
  118.1 1.5 collective-permute-done.14
  120.1 6.2 %fusion.42 = (bf16[128,2048]{1,0:T(8,128)(2,1)S(1)}, f32[128,2048]{1,0:T(8,128)}) fusion(bf16[128,2048]{1,0:T(8,128)(2,1)S(1)} %get-tuple-element.19, bf16[2048,2048]{1,0:T(8,128)(2,1)} %constant_dynamic-update-slice_fusion, f32[128]{0:T(128)S(1)} %add_rsqrt_fusion.1, f32[128]{0:T(128)S(1)} %broadcast_multiply_fusion.7, f32[2048]{0:T(1024)S(1)} %bitcast.107), kind=kOutput, calls=%fused_computation.70 | convolution fusion | flops 1077936128 | bytes 10494976 | tf_op jit(solution)/shard_map/dot_general | solution.py:40
  126.3 2.5 %collective-permute-start.15 = (bf16[128,2048]{1,0:T(8,128)(2,1)S(1)}, bf16[128,2048]{1,0:T(8,128)(2,1)S(1)}, u32[]{:S(2)}, u32[]{:S(2)}) collective-permute-start(bf16[128,2048]{1,0:T(8,128)(2,1)S(1)} %get-tuple-element.46), channel_id=1, source_target_pairs={{0,1},{2,3},{4,5},{6,7},{8,9},{10,11},{12,13},{14,15},{16,17},{18,... | collective-permute-start | bytes 1572872 | tf_op jit(solution)/shard_map/ppermute | solution.py:18
  128.8 2.0 copy.12
  132.1 6.0 %fusion.45 = (bf16[128,2048]{1,0:T(8,128)(2,1)S(1)}, f32[128,2048]{1,0:T(8,128)}) fusion(bf16[128,2048]{1,0:T(8,128)(2,1)S(1)} %collective-permute-done.15, bf16[2048,2048]{1,0:T(8,128)(2,1)} %constant_dynamic-update-slice_fusion, f32[128]{0:T(128)S(1)} %get-tuple-element.27, f32[128]{0:T(128)S(1)} %broadcast_multiply_fusion.6, f32[2048]{0:T(1024)S(1)} %bitcast.108), kind=kOutput, calls=%fused_computation.73 | convolution fusion | flops 1077936128 | bytes 10494976 | tf_op jit(solution)/shard_map/dot_general | solution.py:40
  138.1 1.1 pad_maximum_fusion
  139.2 3.6 %copy.10 = bf16[2,128,2048]{1,0,2:T(2,128)(2,1)} copy(bf16[2,128,2048]{2,1,0:T(8,128)(2,1)} %pad_maximum_fusion) | data formatting | bytes 2097152 | tf_op jit(solution)/shard_map/stack | solution.py:144
  142.9 4.5 %convolution_bitcast_fusion = f32[2,2]{1,0:T(2,128)S(1)} fusion(bf16[2,128,2048]{1,0,2:T(2,128)(2,1)} %copy.10), kind=kOutput, calls=%fused_computation.42 | convolution fusion | flops 2097152 | bytes 1048592 | tf_op jit(solution)/shard_map/mrd,nrd->mn/dot_general | solution.py:143
  147.4 4.3 %convolution_bitcast_fusion.1 = f32[2]{0:T(128)S(1)} fusion(bf16[2,128,2048]{1,0,2:T(2,128)(2,1)} %copy.10, bf16[128,2048,1]{0,2,1:T(2,128)(2,1)} %copy.12), kind=kOutput, calls=%fused_computation.43 | convolution fusion | flops 1048576 | bytes 1572872 | tf_op jit(solution)/shard_map/mrd,rd->m/dot_general | solution.py:147
  152.8 3.3 %collective-permute-done.16 = f32[7]{0:T(128)S(1)} collective-permute-done((f32[7]{0:T(128)S(1)}, f32[7]{0:T(128)S(1)}, u32[]{:S(2)}, u32[]{:S(2)}) %collective-permute-start.16) | collective-permute-done | bytes 60 | tf_op jit(solution)/shard_map/ppermute | solution.py:115
  156.8 1.6 collective-permute-start.17
  158.4 2.0 collective-permute-done.17
  160.4 2.7 %collective-permute-start.18 = (f32[7]{0:T(128)S(1)}, f32[7]{0:T(128)S(1)}, u32[]{:S(2)}, u32[]{:S(2)}) collective-permute-start(f32[7]{0:T(128)S(1)} %add.411), channel_id=1, source_target_pairs={{0,8},{2,10},{4,12},{6,14},{8,0},{10,2},{12,4},{14,6},{1,9},{3,11}... | collective-permute-start | bytes 92 | tf_op jit(solution)/shard_map/ppermute | solution.py:115
  163.1 1.8 collective-permute-done.18
  166.9 1.3 fusion.106
  169.6 9.3 %fusion.104 = (f32[128]{0:T(128)S(1)}, f32[128]{0:T(128)S(1)}, f32[128,2048]{1,0:T(8,128)S(1)}) fusion(f32[128]{0:T(128)S(1)} %add_rsqrt_fusion.1, f32[128]{0:T(128)S(1)} %broadcast_multiply_fusion.7, bf16[128,2048]{1,0:T(8,128)(2,1)S(1)} %get-tuple-element.19, f32[2048]{0:T(1024)S(1)} %bitcast.109, ...), kind=kOutput, calls=%fused_computation.167 | convolution fusion | flops 1082654464 | bytes 12593164 | tf_op jit(solution)/shard_map/dot_general | solution.py:47
  179.0 2.6 %fusion.24 = bf16[128,2048]{1,0:T(8,128)(2,1)S(1)} fusion(bf16[128,2048]{1,0:T(8,128)(2,1)S(1)} %get-tuple-element.19, f32[128,2048]{1,0:T(8,128)S(1)} %get-tuple-element.50, f32[128]{0:T(128)S(1)} %get-tuple-element.53, f32[128]{0:T(128)S(1)} %get-tuple-element.54, f32[128]{0:T(128)S(1)} %add_rsqrt_fusion.1, f32[128]{0:T(128)S(1)} %broadcast_multiply_fusion.7, ...), kind=kLoop, calls=%fused_computation.52 | loop fusion | flops 4456448 | bytes 3672076 | tf_op jit(solution)/shard_map/convert_element_type | solution.py:56
  181.6 1.5 collective-permute-start.19
  183.1 2.3 %collective-permute-done.19 = bf16[128,2048]{1,0:T(8,128)(2,1)S(1)} collective-permute-done((bf16[128,2048]{1,0:T(8,128)(2,1)S(1)}, bf16[128,2048]{1,0:T(8,128)(2,1)S(1)}, u32[]{:S(2)}, u32[]{:S(2)}) %collective-permute-start.19) | collective-permute-done | bytes 524320 | tf_op jit(solution)/shard_map/ppermute | solution.py:18
  185.4 8.7 %fusion.103 = (f32[128]{0:T(128)S(1)}, f32[128]{0:T(128)S(1)}, f32[128,2048]{1,0:T(8,128)S(1)}) fusion(f32[128]{0:T(128)S(1)} %get-tuple-element.27, f32[128]{0:T(128)S(1)} %broadcast_multiply_fusion.6, bf16[128,2048]{1,0:T(8,128)(2,1)S(1)} %collective-permute-done.15, f32[128]{0:T(128)S(1)} %add_rsqrt_fusion.2, f32[128]{0:T(128)S(1)} %broadcast_multiply_fusion.8, ...), kind=kOutput, calls=%fused_computation.166 | convolution fusion | flops 1084489472 | bytes 14693888 | tf_op jit(solution)/shard_map/dot_general | solution.py:47
  194.1 3.6 %select_bitcast_fusion = (bf16[1,128,2048]{2,1,0:T(8,128)(2,1)S(1)}, bf16[128,2048]{1,0:T(8,128)(2,1)}) fusion(bf16[128,2048]{1,0:T(8,128)(2,1)S(1)} %fusion.24, pred[]{:T(512)} %eq.31, f32[128]{0:T(128)S(1)} %broadcast_multiply_fusion.2, f32[128]{0:T(128)S(1)} %get-tuple-element.27, f32[128]{0:T(128)S(1)} %broadcast_multiply_fusion.6, ...), kind=kLoop, calls=%fused_computation.101 | loop fusion | flops 6291456 | bytes 5770765 | tf_op jit(solution)/shard_map/stack | solution.py:179
  197.7 1.3 collective-permute-start.20
  200.3 1.3 collective-permute-start.21
  201.6 1.8 collective-permute-done.21
  204.0 6.9 %fusion.102 = (f32[128]{0:T(128)S(1)}, f32[128]{0:T(128)S(1)}, f32[128,2048]{1,0:T(8,128)S(1)}) fusion(f32[128]{0:T(128)S(1)} %add_rsqrt_fusion.1, f32[128]{0:T(128)S(1)} %broadcast_multiply_fusion.7, bf16[128,2048]{1,0:T(8,128)(2,1)S(1)} %get-tuple-element.19, f32[2048]{0:T(1024)S(1)} %bitcast.111, ...), kind=kOutput, calls=%fused_computation.165 | convolution fusion | flops 1080819456 | bytes 11544576 | tf_op jit(solution)/shard_map/dot_general | solution.py:47
  (87 shorter events, 22.6 us)
Async XLA Ops:
  0.6 55.5 %copy-start.8 = (s32[8]{0:T(128)S(1)}, s32[8]{0:T(128)}, u32[]{:S(2)}) copy-start(s32[8]{0:T(128)} %constant.197.clone) | copy-start | bytes 100
  0.6 65.4 %copy-start.6 = (s32[8]{0:T(128)S(1)}, s32[8]{0:T(128)}, u32[]{:S(2)}) copy-start(s32[8]{0:T(128)} %constant.198.clone) | copy-start | bytes 100
  0.7 47.4 %copy-start.1 = (bf16[1,256,2048]{2,1,0:T(8,128)(2,1)S(1)}, bf16[1,256,2048]{2,1,0:T(8,128)(2,1)}, u32[]{:S(2)}) copy-start(bf16[1,256,2048]{2,1,0:T(8,128)(2,1)} %param.8) | copy-start | bytes 3145732
  0.7 49.2 %copy-start.2 = (bf16[2,128,2048]{2,1,0:T(8,128)(2,1)S(1)}, bf16[2,128,2048]{2,1,0:T(8,128)(2,1)}, u32[]{:S(2)}) copy-start(bf16[2,128,2048]{2,1,0:T(8,128)(2,1)} %param.6) | copy-start | bytes 3145732
  2.1 14.9 %collective-permute-start = (bf16[256,1024]{1,0:T(8,128)(2,1)S(1)}, bf16[256,1024]{1,0:T(8,128)(2,1)S(1)}, u32[]{:S(2)}, u32[]{:S(2)}) collective-permute-start(bf16[256,1024]{1,0:T(8,128)(2,1)S(1)} %get-tuple-element.21), channel_id=1, source_target_pairs={{0,4},{4,8},{8,12},{12,14},{14,10},{10,6},{6,2},{2,0},{1,5},{5,9},... | collective-permute-start | bytes 1572872 | tf_op jit(solution)/shard_map/ppermute | solution.py:100
  5.2 13.7 %collective-permute-start.1 = (bf16[256,1024]{1,0:T(8,128)(2,1)S(1)}, bf16[256,1024]{1,0:T(8,128)(2,1)S(1)}, u32[]{:S(2)}, u32[]{:S(2)}) collective-permute-start(bf16[256,1024]{1,0:T(8,128)(2,1)S(1)} %get-tuple-element.20), channel_id=1, source_target_pairs={{4,0},{8,4},{12,8},{14,12},{10,14},{6,10},{2,6},{0,2},{5,1},{9,5},... | collective-permute-start | bytes 1572872 | tf_op jit(solution)/shard_map/ppermute | solution.py:101
  17.0 14.6 %copy-start.4 = (bf16[256,1024]{1,0:T(8,128)(2,1)}, bf16[256,1024]{1,0:T(8,128)(2,1)S(1)}, u32[]{:S(2)}) copy-start(bf16[256,1024]{1,0:T(8,128)(2,1)S(1)} %collective-permute-done) | copy-start | bytes 1572868
  17.0 13.1 %collective-permute-start.2 = (bf16[256,1024]{1,0:T(8,128)(2,1)S(1)}, bf16[256,1024]{1,0:T(8,128)(2,1)S(1)}, u32[]{:S(2)}, u32[]{:S(2)}) collective-permute-start(bf16[256,1024]{1,0:T(8,128)(2,1)S(1)} %collective-permute-done), channel_id=1, source_target_pairs={{0,4},{4,8},{8,12},{12,14},{14,10},{10,6},{6,2},{2,0},{1,5},{5,9},... | collective-permute-start | bytes 1572872 | tf_op jit(solution)/shard_map/ppermute | solution.py:100
  18.9 13.3 %copy-start.5 = (bf16[256,1024]{1,0:T(8,128)(2,1)}, bf16[256,1024]{1,0:T(8,128)(2,1)S(1)}, u32[]{:S(2)}) copy-start(bf16[256,1024]{1,0:T(8,128)(2,1)S(1)} %collective-permute-done.1) | copy-start | bytes 1572868
  18.9 12.8 %collective-permute-start.3 = (bf16[256,1024]{1,0:T(8,128)(2,1)S(1)}, bf16[256,1024]{1,0:T(8,128)(2,1)S(1)}, u32[]{:S(2)}, u32[]{:S(2)}) collective-permute-start(bf16[256,1024]{1,0:T(8,128)(2,1)S(1)} %collective-permute-done.1), channel_id=1, source_target_pairs={{4,0},{8,4},{12,8},{14,12},{10,14},{6,10},{2,6},{0,2},{5,1},{9,5},... | collective-permute-start | bytes 1572872 | tf_op jit(solution)/shard_map/ppermute | solution.py:101
  30.1 12.3 %collective-permute-start.4 = (bf16[256,1024]{1,0:T(8,128)(2,1)S(1)}, bf16[256,1024]{1,0:T(8,128)(2,1)}, u32[]{:S(2)}, u32[]{:S(2)}) collective-permute-start(bf16[256,1024]{1,0:T(8,128)(2,1)S(1)} %collective-permute-done.2), channel_id=1, source_target_pairs={{0,4},{4,8},{8,12},{12,14},{14,10},{10,6},{6,2},{2,0},{1,5},{5,9},... | collective-permute-start | bytes 1572872 | tf_op jit(solution)/shard_map/ppermute | solution.py:100
  31.7 17.4 %collective-permute-start.5 = (bf16[256,1024]{1,0:T(8,128)(2,1)S(1)}, bf16[256,1024]{1,0:T(8,128)(2,1)}, u32[]{:S(2)}, u32[]{:S(2)}) collective-permute-start(bf16[256,1024]{1,0:T(8,128)(2,1)S(1)} %collective-permute-done.3), channel_id=1, source_target_pairs={{4,0},{8,4},{12,8},{14,12},{10,14},{6,10},{2,6},{0,2},{5,1},{9,5},... | collective-permute-start | bytes 1572872 | tf_op jit(solution)/shard_map/ppermute | solution.py:101
  42.5 12.1 %collective-permute-start.6 = (bf16[256,1024]{1,0:T(8,128)(2,1)}, bf16[256,1024]{1,0:T(8,128)(2,1)}, u32[]{:S(2)}, u32[]{:S(2)}) collective-permute-start(bf16[256,1024]{1,0:T(8,128)(2,1)} %collective-permute-done.4), channel_id=1, source_target_pairs={{0,4},{4,8},{8,12},{12,14},{14,10},{10,6},{6,2},{2,0},{1,5},{5,9},... | collective-permute-start | bytes 1572872 | tf_op jit(solution)/shard_map/ppermute | solution.py:100
  49.1 61.7 %copy-start.7 = (f32[1,2048]{1,0:T(1,128)S(1)}, f32[1,2048]{1,0:T(1,128)}, u32[]{:S(2)}) copy-start(f32[1,2048]{1,0:T(1,128)} %param.9) | copy-start | bytes 24580
  49.1 26.4 %collective-permute-start.7 = (bf16[256,1024]{1,0:T(8,128)(2,1)}, bf16[256,1024]{1,0:T(8,128)(2,1)S(1)}, u32[]{:S(2)}, u32[]{:S(2)}) collective-permute-start(bf16[256,1024]{1,0:T(8,128)(2,1)} %collective-permute-done.5), channel_id=1, source_target_pairs={{4,0},{8,4},{12,8},{14,12},{10,14},{6,10},{2,6},{0,2},{5,1},{9,5},... | collective-permute-start | bytes 1572872 | tf_op jit(solution)/shard_map/ppermute | solution.py:101
  54.6 25.6 %collective-permute-start.8 = (bf16[256,1024]{1,0:T(8,128)(2,1)}, bf16[256,1024]{1,0:T(8,128)(2,1)S(1)}, u32[]{:S(2)}, u32[]{:S(2)}) collective-permute-start(bf16[256,1024]{1,0:T(8,128)(2,1)} %collective-permute-done.6), channel_id=1, source_target_pairs={{0,4},{4,8},{8,12},{12,14},{14,10},{10,6},{6,2},{2,0},{1,5},{5,9},... | collective-permute-start | bytes 1572872 | tf_op jit(solution)/shard_map/ppermute | solution.py:100
  75.5 12.1 %collective-permute-start.9 = (bf16[256,1024]{1,0:T(8,128)(2,1)S(1)}, bf16[256,1024]{1,0:T(8,128)(2,1)S(1)}, u32[]{:S(2)}, u32[]{:S(2)}) collective-permute-start(bf16[256,1024]{1,0:T(8,128)(2,1)S(1)} %collective-permute-done.7), channel_id=1, source_target_pairs={{4,0},{8,4},{12,8},{14,12},{10,14},{6,10},{2,6},{0,2},{5,1},{9,5},... | collective-permute-start | bytes 1572872 | tf_op jit(solution)/shard_map/ppermute | solution.py:101
  80.1 14.8 %collective-permute-start.10 = (bf16[256,1024]{1,0:T(8,128)(2,1)S(1)}, bf16[256,1024]{1,0:T(8,128)(2,1)S(1)}, u32[]{:S(2)}, u32[]{:S(2)}) collective-permute-start(bf16[256,1024]{1,0:T(8,128)(2,1)S(1)} %collective-permute-done.8), channel_id=1, source_target_pairs={{0,4},{4,8},{8,12},{12,14},{14,10},{10,6},{6,2},{2,0},{1,5},{5,9},... | collective-permute-start | bytes 1572872 | tf_op jit(solution)/shard_map/ppermute | solution.py:100
  87.6 13.1 %collective-permute-start.11 = (bf16[256,1024]{1,0:T(8,128)(2,1)S(1)}, bf16[256,1024]{1,0:T(8,128)(2,1)S(1)}, u32[]{:S(2)}, u32[]{:S(2)}) collective-permute-start(bf16[256,1024]{1,0:T(8,128)(2,1)S(1)} %collective-permute-done.9), channel_id=1, source_target_pairs={{4,0},{8,4},{12,8},{14,12},{10,14},{6,10},{2,6},{0,2},{5,1},{9,5},... | collective-permute-start | bytes 1572872 | tf_op jit(solution)/shard_map/ppermute | solution.py:101
  95.0 9.4 %collective-permute-start.12 = (bf16[256,1024]{1,0:T(8,128)(2,1)S(1)}, bf16[256,1024]{1,0:T(8,128)(2,1)S(1)}, u32[]{:S(2)}, u32[]{:S(2)}) collective-permute-start(bf16[256,1024]{1,0:T(8,128)(2,1)S(1)} %collective-permute-done.10), channel_id=1, source_target_pairs={{0,4},{4,8},{8,12},{12,14},{14,10},{10,6},{6,2},{2,0},{1,5},{5,9},... | collective-permute-start | bytes 1572872 | tf_op jit(solution)/shard_map/ppermute | solution.py:100
  100.7 9.2 %collective-permute-start.13 = (bf16[256,1024]{1,0:T(8,128)(2,1)S(1)}, bf16[256,1024]{1,0:T(8,128)(2,1)S(1)}, u32[]{:S(2)}, u32[]{:S(2)}) collective-permute-start(bf16[256,1024]{1,0:T(8,128)(2,1)S(1)} %collective-permute-done.11), channel_id=1, source_target_pairs={{4,0},{8,4},{12,8},{14,12},{10,14},{6,10},{2,6},{0,2},{5,1},{9,5},... | collective-permute-start | bytes 1572872 | tf_op jit(solution)/shard_map/ppermute | solution.py:101
  116.8 2.8 %collective-permute-start.14 = (bf16[128,2048]{1,0:T(8,128)(2,1)S(1)}, bf16[128,2048]{1,0:T(8,128)(2,1)S(1)}, u32[]{:S(2)}, u32[]{:S(2)}) collective-permute-start(bf16[128,2048]{1,0:T(8,128)(2,1)S(1)} %get-tuple-element.44), channel_id=1, source_target_pairs={{0,1},{2,3},{4,5},{6,7},{8,9},{10,11},{12,13},{14,15},{16,17},{18,... | collective-permute-start | bytes 1572872 | tf_op jit(solution)/shard_map/ppermute | solution.py:18
  120.1 8.7 %copy-start = (bf16[128,2048]{1,0:T(8,128)(2,1)S(1)}, bf16[128,2048]{1,0:T(8,128)(2,1)}, u32[]{:S(2)}) copy-start(bf16[128,2048]{1,0:T(8,128)(2,1)} %param.7) | copy-start | bytes 1572868
  126.3 5.3 %collective-permute-start.15 = (bf16[128,2048]{1,0:T(8,128)(2,1)S(1)}, bf16[128,2048]{1,0:T(8,128)(2,1)S(1)}, u32[]{:S(2)}, u32[]{:S(2)}) collective-permute-start(bf16[128,2048]{1,0:T(8,128)(2,1)S(1)} %get-tuple-element.46), channel_id=1, source_target_pairs={{0,1},{2,3},{4,5},{6,7},{8,9},{10,11},{12,13},{14,15},{16,17},{18,... | collective-permute-start | bytes 1572872 | tf_op jit(solution)/shard_map/ppermute | solution.py:18
  152.5 3.6 %collective-permute-start.16 = (f32[7]{0:T(128)S(1)}, f32[7]{0:T(128)S(1)}, u32[]{:S(2)}, u32[]{:S(2)}) collective-permute-start(f32[7]{0:T(128)S(1)} %pad_maximum_fusion.1), channel_id=1, source_target_pairs={{0,2},{2,0},{4,6},{6,4},{8,10},{10,8},{12,14},{14,12},{1,3},{3,1},... | collective-permute-start | bytes 92 | tf_op jit(solution)/shard_map/ppermute | solution.py:115
  156.8 3.6 %collective-permute-start.17 = (f32[7]{0:T(128)S(1)}, f32[7]{0:T(128)S(1)}, u32[]{:S(2)}, u32[]{:S(2)}) collective-permute-start(f32[7]{0:T(128)S(1)} %fusion.124), channel_id=1, source_target_pairs={{0,4},{2,6},{4,0},{6,2},{8,12},{10,14},{12,8},{14,10},{1,5},{3,7},... | collective-permute-start | bytes 92 | tf_op jit(solution)/shard_map/ppermute | solution.py:115
  160.4 4.5 %collective-permute-start.18 = (f32[7]{0:T(128)S(1)}, f32[7]{0:T(128)S(1)}, u32[]{:S(2)}, u32[]{:S(2)}) collective-permute-start(f32[7]{0:T(128)S(1)} %add.411), channel_id=1, source_target_pairs={{0,8},{2,10},{4,12},{6,14},{8,0},{10,2},{12,4},{14,6},{1,9},{3,11}... | collective-permute-start | bytes 92 | tf_op jit(solution)/shard_map/ppermute | solution.py:115
  169.6 15.8 %copy-start.3 = (bf16[2,128,2048]{2,1,0:T(8,128)(2,1)S(1)}, bf16[2,128,2048]{2,1,0:T(8,128)(2,1)}, u32[]{:S(2)}) copy-start(bf16[2,128,2048]{2,1,0:T(8,128)(2,1)} %param.6) | copy-start | bytes 3145732
  169.6 15.8 %copy-start.9 = (f32[128,2048]{1,0:T(8,128)S(1)}, f32[128,2048]{1,0:T(8,128)}, u32[]{:S(2)}) copy-start(f32[128,2048]{1,0:T(8,128)} %get-tuple-element.49) | copy-start | bytes 3145732
  169.6 15.8 %copy-start.10 = (f32[128,2048]{1,0:T(8,128)S(1)}, f32[128,2048]{1,0:T(8,128)}, u32[]{:S(2)}) copy-start(f32[128,2048]{1,0:T(8,128)} %get-tuple-element.45) | copy-start | bytes 3145732
  181.6 3.8 %collective-permute-start.19 = (bf16[128,2048]{1,0:T(8,128)(2,1)S(1)}, bf16[128,2048]{1,0:T(8,128)(2,1)S(1)}, u32[]{:S(2)}, u32[]{:S(2)}) collective-permute-start(bf16[128,2048]{1,0:T(8,128)(2,1)S(1)} %fusion.24), channel_id=1, source_target_pairs={{1,0},{3,2},{5,4},{7,6},{9,8},{11,10},{13,12},{15,14},{17,16},{19,... | collective-permute-start | bytes 1572872 | tf_op jit(solution)/shard_map/ppermute | solution.py:18
  197.7 6.3 %collective-permute-start.20 = (bf16[128,2048]{1,0:T(8,128)(2,1)}, bf16[128,2048]{1,0:T(8,128)(2,1)S(1)}, u32[]{:S(2)}, u32[]{:S(2)}) collective-permute-start(bf16[128,2048]{1,0:T(8,128)(2,1)} %get-tuple-element.13), channel_id=1, source_target_pairs={{1,0},{3,2},{5,4},{7,6},{9,8},{11,10},{13,12},{15,14},{17,16},{19,... | collective-permute-start | bytes 1572872 | tf_op jit(solution)/shard_map/ppermute | solution.py:18
  200.3 3.1 %collective-permute-start.21 = (f32[1]{0:T(128)}, f32[1]{0:T(128)}, u32[]{:S(2)}, u32[]{:S(2)}) collective-permute-start(f32[1]{0:T(128)} %bitcast.52), channel_id=1, source_target_pairs={{1,0},{3,2},{5,4},{7,6},{9,8},{11,10},{13,12},{15,14},{17,16},{19,... | collective-permute-start | bytes 20 | tf_op jit(solution)/shard_map/ppermute | solution.py:18

commit v2 on v1

--- a/solution.py
+++ b/solution.py
@@ -132,51 +132,43 @@
     else:
         weight = lax.all_gather(weights, "tok", axis=1, tiled=True)[0]
 
-    fa = section_forward(inputs[0], gain, weight)
-    arrived0 = shifted(fa[0], "section", 1)
-    fb = section_forward(jnp.where(on_first, inputs[1], arrived0), gain, weight)
-    arrived1 = shifted(fb[0], "section", 1)
-    fc = section_forward(arrived1, gain, weight)
+    members = inputs.shape[0]
+    rows_all = inputs.reshape(members * tok_rows, width)
 
-    y0 = fb[0]
-    y1 = fc[0]
-    gram = jnp.einsum(
-        "mrd,nrd->mn", jnp.stack([y0, y1]), jnp.stack([y0, y1]),
-        preferred_element_type=jnp.float32,
-    )
-    obs_part = jnp.einsum(
-        "mrd,rd->m", jnp.stack([y0, y1]), obs, preferred_element_type=jnp.float32
-    )
-    packed = jnp.concatenate([gram.reshape(4), obs_part, obs_sq.reshape(1)])
-    packed = tree_sum(packed, "tok")
-    member_gram = packed[:4].reshape(2, 2)
-    obs_rows = packed[4:6]
-    obs_total = packed[6]
+    fa = section_forward(rows_all, gain, weight)
+    arrived = shifted(fa[0], "section", 1)
+    fb = section_forward(arrived, gain, weight)
+
+    y = fb[0].astype(jnp.float32).reshape(members, tok_rows, width)
+    obs_f = obs.astype(jnp.float32)
+    terms = []
+    for m in range(members):
+        for k in range(members):
+            terms.append(jnp.sum(y[m] * y[k]))
+    for m in range(members):
+        terms.append(jnp.sum(y[m] * obs_f))
+    terms.append(obs_sq)
+    packed = tree_sum(jnp.stack(terms), "tok")
+    member_gram = packed[: members * members].reshape(members, members)
+    obs_rows = packed[members * members : members * members + members]
+    obs_total = packed[members * members + members]
     energy, member_coeff, obs_coeff = score_terms(member_gram, obs_rows, obs_total, size)
     energy_arr = jnp.reshape(energy, (1,))
     energy_peer = shifted(energy_arr, "section", -1)
     energy_out = jnp.where(on_first, energy_peer, energy_arr)
 
-    obs_f = obs.astype(jnp.float32)
-    y0f = y0.astype(jnp.float32)
-    y1f = y1.astype(jnp.float32)
+    cots = []
+    for m in range(members):
+        c = obs_coeff[m] * obs_f
+        for k in range(members):
+            c = c + member_coeff[m, k] * y[k]
+        cots.append(c)
+    cot = jnp.concatenate(cots, axis=0)
 
-    def cotangent(m):
-        return member_coeff[m, 0] * y0f + member_coeff[m, 1] * y1f + obs_coeff[m] * obs_f
-
-    d0 = section_backward(cotangent(0), gain, weight, fb[1], fb[2], fb[3])
-    back0 = shifted(d0, "section", -1)
-    g1 = jnp.where(on_first, back0.astype(jnp.float32), cotangent(1))
-    h1 = jnp.where(on_first, fa[1], fc[1])
-    q1 = jnp.where(on_first, fa[2], fc[2])
-    p1 = jnp.where(on_first, fa[3], fc[3])
-    d1 = section_backward(g1, gain, weight, h1, q1, p1)
-    back1 = shifted(d1, "section", -1)
-    d2 = section_backward(back1.astype(jnp.float32), gain, weight, fb[1], fb[2], fb[3])
-
-    first_m0 = jnp.where(on_first, d1, d0)
-    first_m1 = jnp.where(on_first, d2, d1)
-    grads = jnp.stack([first_m0, first_m1])
+    da = section_backward(cot, gain, weight, fb[1], fb[2], fb[3])
+    back = shifted(da, "section", -1)
+    db = section_backward(back.astype(jnp.float32), gain, weight, fa[1], fa[2], fa[3])
+    grads = jnp.where(on_first, db, da).reshape(members, tok_rows, width)
     return (grads[None], energy_out)
 
 

time: 216 us -> 186 us (0.86)
  matrix products: 51.9 us -> 29.6 us
  waiting for transfers between devices: 64.1 us -> 56.2 us
  local copies, waits for them, and re-layouts: 33.6 us -> 37.1 us
  starting transfers between devices: 27.1 us -> 24.9 us
    ppermute x7, waiting for transfers between devices: 13.7 us -> 1.78 us  [ring_gather(): right = lax.ppermute(right, axis, ccw)]
    dot_general x3 -> x2, matrix products: 24.9 us -> 14.5 us  [section_backward(): lax.dot_general(grad_pre, weight, (((1,), (1,)), ((), ())), preferred_ele...]
    dot_general x2 -> x0, matrix products: 8.83 us -> none  [the longest x1 4.48 us: per_device(): jnp.einsum('mrd,nrd->mn', jnp.stack([y0, y1]), jnp.stack([y0, y1]), prefe...]
    ppermute x7, waiting for transfers between devices: 37.7 us -> 45.3 us  [ring_gather(): left = lax.ppermute(left, axis, cw)]
    add x0 -> x1, other arithmetic: none -> 6.03 us  [per_device(): c = c + member_coeff[m, k] * y[k]]
    another operation x3 -> x0, other arithmetic: 5.34 us -> none  [the longest x2 4.22 us: per_device(): grads = jnp.stack([first_m0, first_m1])]
    ppermute x5 -> x3, starting transfers between devices: 7.87 us -> 4.33 us  [shifted(): return lax.ppermute(x, axis, pairs)]
    dot_general x3 -> x2, matrix products: 18.2 us -> 15.2 us  [section_forward(): pre_act = jnp.dot(normed, weight, preferred_element_type=jnp.float32)]
  transfers between devices with their start and end apart: 22 -> 20, of which waited for: 13 -> 11; matrix products, arithmetic and copies ran while one was open for 12% -> 15% of each run, Pallas kernels for 0% -> 0%
where the time goes in v2:
time: 186 us; the launch traced here: 185 us
  waiting for transfers between devices  56.2 us (30%)
  local copies, waits for them, and re-layouts  37.1 us (20%)
  matrix products  29.6 us (16%)
  starting transfers between devices  24.9 us (13%)
  between operations  21.8 us (12%)
  other arithmetic  15.1 us (8%)
    ppermute x7, waiting for transfers between devices, ring_gather(): left = lax.ppermute(left, axis, cw)  45.3 us
    dot_general x2, matrix products, section_forward(): pre_act = jnp.dot(normed, weight, preferred_element_type=jnp.float32)  15.2 us
    dot_general x2, matrix products, section_backward(): lax.dot_general(grad_pre, weight, (((1,), (1,)), ((), ())), preferred_ele...  14.5 us
    ppermute x7, starting transfers between devices, ring_gather(): left = lax.ppermute(left, axis, cw)  11.2 us
    dynamic_update_slice x7, local copies, waits for them, and re-layouts, ring_gather(): full = lax.dynamic_update_slice(full, right, (from_right * rows, half))  10.2 us
    dynamic_update_slice x7, local copies, waits for them, and re-layouts, ring_gather(): full = lax.dynamic_update_slice(full, left, (from_left * rows, 0))  10.2 us
    ppermute x3, waiting for transfers between devices, tree_sum(): v = v + lax.ppermute(v, axis, [(i, i ^ b) for i in range(n)])  6.27 us
    add x1, other arithmetic, per_device(): c = c + member_coeff[m, k] * y[k]  6.03 us
  transfers between devices with their start and end apart: 20, of which 11 were waited for; matrix products, arithmetic and copies ran while one was open for 15% of the time, Pallas kernels for 0%

profile of v2, /device:TPU:0, one launch (start us, length us, event | category | flops | bytes accessed | tf_op | source)
XLA Modules:
  0.0 184.8 jit_solution(13300986410749645758)
XLA Ops:
  0.6 1.4 fusion.89
  2.0 3.1 %collective-permute-start = (bf16[256,1024]{1,0:T(8,128)(2,1)S(1)}, bf16[256,1024]{1,0:T(8,128)(2,1)}, u32[]{:S(2)}, u32[]{:S(2)}) collective-permute-start(bf16[256,1024]{1,0:T(8,128)(2,1)S(1)} %get-tuple-element.22), channel_id=1, source_target_pairs={{0,4},{4,8},{8,12},{12,14},{14,10},{10,6},{6,2},{2,0},{1,5},{5,9},... | collective-permute-start | bytes 1572872 | tf_op jit(solution)/shard_map/ppermute | solution.py:100
  5.1 11.9 %collective-permute-done = bf16[256,1024]{1,0:T(8,128)(2,1)} collective-permute-done((bf16[256,1024]{1,0:T(8,128)(2,1)S(1)}, bf16[256,1024]{1,0:T(8,128)(2,1)}, u32[]{:S(2)}, u32[]{:S(2)}) %collective-permute-start) | collective-permute-done | bytes 524320 | tf_op jit(solution)/shard_map/ppermute | solution.py:100
  17.1 1.8 collective-permute-start.2
  19.1 11.3 %collective-permute-done.2 = bf16[256,1024]{1,0:T(8,128)(2,1)S(1)} collective-permute-done((bf16[256,1024]{1,0:T(8,128)(2,1)}, bf16[256,1024]{1,0:T(8,128)(2,1)S(1)}, u32[]{:S(2)}, u32[]{:S(2)}) %collective-permute-start.2) | collective-permute-done | bytes 524320 | tf_op jit(solution)/shard_map/ppermute | solution.py:100
  30.4 1.5 collective-permute-start.4
  33.0 9.7 %collective-permute-done.4 = bf16[256,1024]{1,0:T(8,128)(2,1)} collective-permute-done((bf16[256,1024]{1,0:T(8,128)(2,1)S(1)}, bf16[256,1024]{1,0:T(8,128)(2,1)}, u32[]{:S(2)}, u32[]{:S(2)}) %collective-permute-start.4) | collective-permute-done | bytes 524320 | tf_op jit(solution)/shard_map/ppermute | solution.py:100
  42.7 1.3 collective-permute-start.6
  45.2 9.6 %collective-permute-done.6 = bf16[256,1024]{1,0:T(8,128)(2,1)} collective-permute-done((bf16[256,1024]{1,0:T(8,128)(2,1)}, bf16[256,1024]{1,0:T(8,128)(2,1)}, u32[]{:S(2)}, u32[]{:S(2)}) %collective-permute-start.6) | collective-permute-done | bytes 524320 | tf_op jit(solution)/shard_map/ppermute | solution.py:100
  54.8 1.3 collective-permute-start.8
  56.8 4.3 %broadcast_in_dim.11 = bf16[2048,2048]{1,0:T(8,128)(2,1)} broadcast(bf16[]{:T(256)} %constant.163.clone.1), dimensions={} | broadcast | bytes 8388610 | tf_op jit(solution)/shard_map/broadcast_in_dim | solution.py:97
  61.1 1.1 constant_dynamic-update-slice_fusion.14
  81.5 1.9 %constant_dynamic-update-slice_fusion.13 = bf16[2048,2048]{1,0:T(8,128)(2,1)} fusion(bf16[2048,2048]{1,0:T(8,128)(2,1)} %constant_dynamic-update-slice_fusion.14, bf16[256,1024]{1,0:T(8,128)(2,1)} %collective-permute-done, s32[]{:T(128)S(6)} %select_n.182), kind=kLoop, calls=%fused_computation.99 | loop fusion | bytes 1048580 | tf_op jit(solution)/shard_map/dynamic_update_slice | solution.py:104
  83.4 1.9 %constant_dynamic-update-slice_fusion.6 = bf16[2048,2048]{1,0:T(8,128)(2,1)} fusion(bf16[2048,2048]{1,0:T(8,128)(2,1)} %constant_dynamic-update-slice_fusion.13, bf16[256,1024]{1,0:T(8,128)(2,1)} %collective-permute-done.1, s32[]{:T(128)S(6)} %select_n.185), kind=kLoop, calls=%fused_computation.92 | loop fusion | bytes 1048580 | tf_op jit(solution)/shard_map/dynamic_update_slice | solution.py:105
  85.4 1.2 collective-permute-start.10
  89.1 1.9 %constant_dynamic-update-slice_fusion.11 = bf16[2048,2048]{1,0:T(8,128)(2,1)} fusion(bf16[2048,2048]{1,0:T(8,128)(2,1)} %constant_dynamic-update-slice_fusion.5, bf16[256,1024]{1,0:T(8,128)(2,1)} %collective-permute-done.4, s32[]{:T(128)S(6)} %select_n.194), kind=kLoop, calls=%fused_computation.97 | loop fusion | bytes 1048580 | tf_op jit(solution)/shard_map/dynamic_update_slice | solution.py:104
  91.1 1.9 %constant_dynamic-update-slice_fusion.4 = bf16[2048,2048]{1,0:T(8,128)(2,1)} fusion(bf16[2048,2048]{1,0:T(8,128)(2,1)} %constant_dynamic-update-slice_fusion.11, bf16[256,1024]{1,0:T(8,128)(2,1)} %collective-permute-done.5, s32[]{:T(128)S(6)} %select_n.197), kind=kLoop, calls=%fused_computation.90 | loop fusion | bytes 1048580 | tf_op jit(solution)/shard_map/dynamic_update_slice | solution.py:105
  93.0 1.9 %constant_dynamic-update-slice_fusion.10 = bf16[2048,2048]{1,0:T(8,128)(2,1)} fusion(bf16[2048,2048]{1,0:T(8,128)(2,1)} %constant_dynamic-update-slice_fusion.4, bf16[256,1024]{1,0:T(8,128)(2,1)} %collective-permute-done.6, s32[]{:T(128)S(6)} %select_n.200), kind=kLoop, calls=%fused_computation.96 | loop fusion | bytes 1048580 | tf_op jit(solution)/shard_map/dynamic_update_slice | solution.py:104
  94.9 2.8 %collective-permute-done.10 = bf16[256,1024]{1,0:T(8,128)(2,1)S(1)} collective-permute-done((bf16[256,1024]{1,0:T(8,128)(2,1)}, bf16[256,1024]{1,0:T(8,128)(2,1)S(1)}, u32[]{:S(2)}, u32[]{:S(2)}) %collective-permute-start.10) | collective-permute-done | bytes 524320 | tf_op jit(solution)/shard_map/ppermute | solution.py:100
  97.7 1.0 collective-permute-start.12
  98.7 1.9 %constant_dynamic-update-slice_fusion.3 = bf16[2048,2048]{1,0:T(8,128)(2,1)} fusion(bf16[2048,2048]{1,0:T(8,128)(2,1)} %constant_dynamic-update-slice_fusion.10, bf16[256,1024]{1,0:T(8,128)(2,1)} %collective-permute-done.7, s32[]{:T(128)S(6)} %select_n.203), kind=kLoop, calls=%fused_computation.89 | loop fusion | bytes 1048580 | tf_op jit(solution)/shard_map/dynamic_update_slice | solution.py:105
  100.6 1.0 collective-permute-start.13
  101.6 1.9 %constant_dynamic-update-slice_fusion.9 = bf16[2048,2048]{1,0:T(8,128)(2,1)} fusion(bf16[2048,2048]{1,0:T(8,128)(2,1)} %constant_dynamic-update-slice_fusion.3, bf16[256,1024]{1,0:T(8,128)(2,1)} %collective-permute-done.8, s32[]{:T(128)S(6)} %select_n.206), kind=kLoop, calls=%fused_computation.95 | loop fusion | bytes 1048580 | tf_op jit(solution)/shard_map/dynamic_update_slice | solution.py:104
  103.5 1.9 %constant_dynamic-update-slice_fusion.2 = bf16[2048,2048]{1,0:T(8,128)(2,1)} fusion(bf16[2048,2048]{1,0:T(8,128)(2,1)} %constant_dynamic-update-slice_fusion.9, bf16[256,1024]{1,0:T(8,128)(2,1)} %collective-permute-done.9, s32[]{:T(128)S(6)} %select_n.209), kind=kLoop, calls=%fused_computation.88 | loop fusion | bytes 1048580 | tf_op jit(solution)/shard_map/dynamic_update_slice | solution.py:105
  106.3 0.9 constant_dynamic-update-slice_fusion.1
  108.0 1.8 collective-permute-done.13
  110.6 7.6 %fusion.37 = (bf16[256,2048]{1,0:T(8,128)(2,1)S(1)}, f32[256,2048]{1,0:T(8,128)}) fusion(bf16[2,128,2048]{2,1,0:T(8,128)(2,1)S(1)} %copy-done, bf16[256,2048]{1,0:T(8,128)(2,1)S(1)} %fusion.33, bf16[2048,2048]{1,0:T(8,128)(2,1)} %constant_dynamic-update-slice_fusion), kind=kOutput, calls=%fused_computation.54 | convolution fusion | flops 2153250816 | bytes 13631488 | tf_op jit(solution)/shard_map/dot_general | solution.py:40
  118.3 1.5 collective-permute-start.14
  119.8 0.9 fusion.50
  120.8 1.1 collective-permute-done.14
  122.5 7.5 %fusion.46 = (f32[256,2048]{1,0:T(8,128)S(1)}, f32[256,2048]{1,0:T(8,128)}) fusion(bf16[256,2048]{1,0:T(8,128)(2,1)S(1)} %collective-permute-done.14, bf16[2048,2048]{1,0:T(8,128)(2,1)} %constant_dynamic-update-slice_fusion, f32[256]{0:T(256)S(1)} %add_rsqrt_fusion, f32[256]{0:T(256)S(1)} %broadcast_multiply_fusion.4, f32[2048]{0:T(1024)S(1)} %bitcast.90), kind=kOutput, calls=%fused_computation.65 | convolution fusion | flops 2156396544 | bytes 13641728 | tf_op jit(solution)/shard_map/dot_general | solution.py:40
  130.0 1.4 copy-done.1
  131.4 1.4 fusion.41
  132.8 4.6 %stack.28 = f32[7]{0:T(128)S(1)} concatenate(f32[1]{0:T(128)} %bitcast.35, f32[1]{0:T(128)} %bitcast.36, f32[1]{0:T(128)} %bitcast.36, f32[1]{0:T(128)} %bitcast.37, f32[1]{0:T(128)} %bitcast.38, f32[1]{0:T(128)} %bitcast.39, f32[1]{0:T(128)} %bitcast.40), dimensions={0} | concatenate | bytes 56 | tf_op jit(solution)/shard_map/stack | solution.py:151
  137.4 1.0 collective-permute-start.15
  138.5 2.5 %collective-permute-done.15 = f32[7]{0:T(128)S(1)} collective-permute-done((f32[7]{0:T(128)S(1)}, f32[7]{0:T(128)S(1)}, u32[]{:S(2)}, u32[]{:S(2)}) %collective-permute-start.15) | collective-permute-done | bytes 60 | tf_op jit(solution)/shard_map/ppermute | solution.py:115
  141.0 1.6 collective-permute-start.16
  142.6 2.0 %collective-permute-done.16 = f32[7]{0:T(128)S(1)} collective-permute-done((f32[7]{0:T(128)S(1)}, f32[7]{0:T(128)S(1)}, u32[]{:S(2)}, u32[]{:S(2)}) %collective-permute-start.16) | collective-permute-done | bytes 60 | tf_op jit(solution)/shard_map/ppermute | solution.py:115
  144.6 2.7 %collective-permute-start.17 = (f32[7]{0:T(128)S(1)}, f32[7]{0:T(128)S(1)}, u32[]{:S(2)}, u32[]{:S(2)}) collective-permute-start(f32[7]{0:T(128)S(1)} %add.374), channel_id=1, source_target_pairs={{0,8},{2,10},{4,12},{6,14},{8,0},{10,2},{12,4},{14,6},{1,9},{3,11}... | collective-permute-start | bytes 92 | tf_op jit(solution)/shard_map/ppermute | solution.py:115
  147.3 1.8 collective-permute-done.17
  151.0 1.4 fusion.85
  154.0 6.0 %fusion.43 = (f32[128,2048]{1,0:T(8,128)S(1)}, f32[128,2048]{1,0:T(8,128)S(1)}) fusion(bf16[128,2048]{1,0:T(8,128)(2,1)S(1)} %copy-done.2, f32[256,2048]{1,0:T(8,128)} %copy-done.1, f32[]{:T(128)} %bitcast.45, f32[]{:T(128)} %bitcast.44, f32[]{:T(128)} %bitcast.43, f32[]{:T(128)} %bitcast.48, f32[]{:T(128)} %bitcast.47, f32[]{:T(128)} %bitcast.46), kind=kLoop, calls=%fused_computation.62 | loop fusion | flops 2883584 | bytes 4718616 | tf_op jit(solution)/shard_map/add | solution.py:164
  160.0 6.9 %fusion.83 = (f32[256]{0:T(256)S(1)}, f32[256]{0:T(256)S(1)}, f32[256,2048]{1,0:T(8,128)S(1)}) fusion(f32[256]{0:T(256)S(1)} %add_rsqrt_fusion, f32[256]{0:T(256)S(1)} %broadcast_multiply_fusion.4, bf16[256,2048]{1,0:T(8,128)(2,1)S(1)} %collective-permute-done.14, f32[2048]{0:T(1024)S(1)} %bitcast.91, ...), kind=kOutput, calls=%fused_computation.135 | convolution fusion | flops 2161638912 | bytes 15740928 | tf_op jit(solution)/shard_map/dot_general | solution.py:47
  167.7 1.3 collective-permute-start.18
  170.3 1.5 collective-permute-start.19
  171.8 1.7 collective-permute-done.19
  174.1 7.6 %fusion.82 = (f32[256]{0:T(256)S(1)}, f32[256]{0:T(256)S(1)}, f32[256,2048]{1,0:T(8,128)S(1)}) fusion(f32[256]{0:T(256)S(1)} %rsqrt_bitcast_fusion, f32[256]{0:T(256)S(1)} %get-tuple-element.27, bf16[2,128,2048]{2,1,0:T(8,128)(2,1)S(1)} %copy-done, f32[2048]{0:T(1024)S(1)} %bitcast.92, bf16[2048,2048]{1,0:T(8,128)(2,1)} %constant_dynamic-update-slice_fusion, ...), kind=kOutput, calls=%fused_computation.134 | convolution fusion | flops 2161638912 | bytes 14692352 | tf_op jit(solution)/shard_map/dot_general | solution.py:47
  181.7 2.0 %fusion.47 = bf16[256,2048]{1,0:T(8,128)(2,1)} fusion(bf16[256,2048]{1,0:T(8,128)(2,1)S(1)} %fusion.10, bf16[2,128,2048]{2,1,0:T(8,128)(2,1)S(1)} %copy-done, f32[256,2048]{1,0:T(8,128)S(1)} %get-tuple-element.50, bf16[256,2048]{1,0:T(8,128)(2,1)S(1)} %collective-permute-done.18, f32[256]{0:T(256)S(1)} %broadcast_multiply_fusion, ...), kind=kLoop, calls=%fused_computation.66 | loop fusion | flops 5767168 | bytes 6295553 | tf_op jit(solution)/shard_map/jit(_where)/select_n | solution.py:171
  (64 shorter events, 14.6 us)
Async XLA Ops:
  0.6 31.8 %copy-start = (bf16[2,128,2048]{2,1,0:T(8,128)(2,1)S(1)}, bf16[2,128,2048]{2,1,0:T(8,128)(2,1)}, u32[]{:S(2)}) copy-start(bf16[2,128,2048]{2,1,0:T(8,128)(2,1)} %param.6) | copy-start | bytes 3145732
  0.6 44.1 %copy-start.5 = (f32[1,2048]{1,0:T(1,128)S(1)}, f32[1,2048]{1,0:T(1,128)}, u32[]{:S(2)}) copy-start(f32[1,2048]{1,0:T(1,128)} %param.9) | copy-start | bytes 24580
  2.0 15.0 %collective-permute-start = (bf16[256,1024]{1,0:T(8,128)(2,1)S(1)}, bf16[256,1024]{1,0:T(8,128)(2,1)}, u32[]{:S(2)}, u32[]{:S(2)}) collective-permute-start(bf16[256,1024]{1,0:T(8,128)(2,1)S(1)} %get-tuple-element.22), channel_id=1, source_target_pairs={{0,4},{4,8},{8,12},{12,14},{14,10},{10,6},{6,2},{2,0},{1,5},{5,9},... | collective-permute-start | bytes 1572872 | tf_op jit(solution)/shard_map/ppermute | solution.py:100
  5.1 13.8 %collective-permute-start.1 = (bf16[256,1024]{1,0:T(8,128)(2,1)S(1)}, bf16[256,1024]{1,0:T(8,128)(2,1)}, u32[]{:S(2)}, u32[]{:S(2)}) collective-permute-start(bf16[256,1024]{1,0:T(8,128)(2,1)S(1)} %get-tuple-element.21), channel_id=1, source_target_pairs={{4,0},{8,4},{12,8},{14,12},{10,14},{6,10},{2,6},{0,2},{5,1},{9,5},... | collective-permute-start | bytes 1572872 | tf_op jit(solution)/shard_map/ppermute | solution.py:101
  17.1 13.3 %collective-permute-start.2 = (bf16[256,1024]{1,0:T(8,128)(2,1)}, bf16[256,1024]{1,0:T(8,128)(2,1)S(1)}, u32[]{:S(2)}, u32[]{:S(2)}) collective-permute-start(bf16[256,1024]{1,0:T(8,128)(2,1)} %collective-permute-done), channel_id=1, source_target_pairs={{0,4},{4,8},{8,12},{12,14},{14,10},{10,6},{6,2},{2,0},{1,5},{5,9},... | collective-permute-start | bytes 1572872 | tf_op jit(solution)/shard_map/ppermute | solution.py:100
  18.9 13.0 %collective-permute-start.3 = (bf16[256,1024]{1,0:T(8,128)(2,1)}, bf16[256,1024]{1,0:T(8,128)(2,1)S(1)}, u32[]{:S(2)}, u32[]{:S(2)}) collective-permute-start(bf16[256,1024]{1,0:T(8,128)(2,1)} %collective-permute-done.1), channel_id=1, source_target_pairs={{4,0},{8,4},{12,8},{14,12},{10,14},{6,10},{2,6},{0,2},{5,1},{9,5},... | collective-permute-start | bytes 1572872 | tf_op jit(solution)/shard_map/ppermute | solution.py:101
  30.4 12.3 %collective-permute-start.4 = (bf16[256,1024]{1,0:T(8,128)(2,1)S(1)}, bf16[256,1024]{1,0:T(8,128)(2,1)}, u32[]{:S(2)}, u32[]{:S(2)}) collective-permute-start(bf16[256,1024]{1,0:T(8,128)(2,1)S(1)} %collective-permute-done.2), channel_id=1, source_target_pairs={{0,4},{4,8},{8,12},{12,14},{14,10},{10,6},{6,2},{2,0},{1,5},{5,9},... | collective-permute-start | bytes 1572872 | tf_op jit(solution)/shard_map/ppermute | solution.py:100
  31.9 12.1 %collective-permute-start.5 = (bf16[256,1024]{1,0:T(8,128)(2,1)S(1)}, bf16[256,1024]{1,0:T(8,128)(2,1)}, u32[]{:S(2)}, u32[]{:S(2)}) collective-permute-start(bf16[256,1024]{1,0:T(8,128)(2,1)S(1)} %collective-permute-done.3), channel_id=1, source_target_pairs={{4,0},{8,4},{12,8},{14,12},{10,14},{6,10},{2,6},{0,2},{5,1},{9,5},... | collective-permute-start | bytes 1572872 | tf_op jit(solution)/shard_map/ppermute | solution.py:101
  42.7 12.1 %collective-permute-start.6 = (bf16[256,1024]{1,0:T(8,128)(2,1)}, bf16[256,1024]{1,0:T(8,128)(2,1)}, u32[]{:S(2)}, u32[]{:S(2)}) collective-permute-start(bf16[256,1024]{1,0:T(8,128)(2,1)} %collective-permute-done.4), channel_id=1, source_target_pairs={{0,4},{4,8},{8,12},{12,14},{14,10},{10,6},{6,2},{2,0},{1,5},{5,9},... | collective-permute-start | bytes 1572872 | tf_op jit(solution)/shard_map/ppermute | solution.py:100
  44.0 12.1 %collective-permute-start.7 = (bf16[256,1024]{1,0:T(8,128)(2,1)}, bf16[256,1024]{1,0:T(8,128)(2,1)}, u32[]{:S(2)}, u32[]{:S(2)}) collective-permute-start(bf16[256,1024]{1,0:T(8,128)(2,1)} %collective-permute-done.5), channel_id=1, source_target_pairs={{4,0},{8,4},{12,8},{14,12},{10,14},{6,10},{2,6},{0,2},{5,1},{9,5},... | collective-permute-start | bytes 1572872 | tf_op jit(solution)/shard_map/ppermute | solution.py:101
  45.1 16.0 %copy-start.3 = (bf16[1,256,2048]{2,1,0:T(8,128)(2,1)S(1)}, bf16[1,256,2048]{2,1,0:T(8,128)(2,1)}, u32[]{:S(2)}) copy-start(bf16[1,256,2048]{2,1,0:T(8,128)(2,1)} %param.8) | copy-start | bytes 3145732
  54.8 30.6 %collective-permute-start.8 = (bf16[256,1024]{1,0:T(8,128)(2,1)}, bf16[256,1024]{1,0:T(8,128)(2,1)}, u32[]{:S(2)}, u32[]{:S(2)}) collective-permute-start(bf16[256,1024]{1,0:T(8,128)(2,1)} %collective-permute-done.6), channel_id=1, source_target_pairs={{0,4},{4,8},{8,12},{12,14},{14,10},{10,6},{6,2},{2,0},{1,5},{5,9},... | collective-permute-start | bytes 1572872 | tf_op jit(solution)/shard_map/ppermute | solution.py:100
  56.1 31.4 %collective-permute-start.9 = (bf16[256,1024]{1,0:T(8,128)(2,1)}, bf16[256,1024]{1,0:T(8,128)(2,1)}, u32[]{:S(2)}, u32[]{:S(2)}) collective-permute-start(bf16[256,1024]{1,0:T(8,128)(2,1)} %collective-permute-done.7), channel_id=1, source_target_pairs={{4,0},{8,4},{12,8},{14,12},{10,14},{6,10},{2,6},{0,2},{5,1},{9,5},... | collective-permute-start | bytes 1572872 | tf_op jit(solution)/shard_map/ppermute | solution.py:101
  61.1 1.1 copy-start.6
  61.1 11.0 %copy-start.4 = (s32[8]{0:T(128)S(1)}, s32[8]{0:T(128)}, u32[]{:S(2)}) copy-start(s32[8]{0:T(128)} %constant.194.clone) | copy-start | bytes 100
  85.4 12.3 %collective-permute-start.10 = (bf16[256,1024]{1,0:T(8,128)(2,1)}, bf16[256,1024]{1,0:T(8,128)(2,1)S(1)}, u32[]{:S(2)}, u32[]{:S(2)}) collective-permute-start(bf16[256,1024]{1,0:T(8,128)(2,1)} %collective-permute-done.8), channel_id=1, source_target_pairs={{0,4},{4,8},{8,12},{12,14},{14,10},{10,6},{6,2},{2,0},{1,5},{5,9},... | collective-permute-start | bytes 1572872 | tf_op jit(solution)/shard_map/ppermute | solution.py:100
  87.5 13.1 %collective-permute-start.11 = (bf16[256,1024]{1,0:T(8,128)(2,1)}, bf16[256,1024]{1,0:T(8,128)(2,1)S(1)}, u32[]{:S(2)}, u32[]{:S(2)}) collective-permute-start(bf16[256,1024]{1,0:T(8,128)(2,1)} %collective-permute-done.9), channel_id=1, source_target_pairs={{4,0},{8,4},{12,8},{14,12},{10,14},{6,10},{2,6},{0,2},{5,1},{9,5},... | collective-permute-start | bytes 1572872 | tf_op jit(solution)/shard_map/ppermute | solution.py:101
  97.7 9.5 %collective-permute-start.12 = (bf16[256,1024]{1,0:T(8,128)(2,1)S(1)}, bf16[256,1024]{1,0:T(8,128)(2,1)S(1)}, u32[]{:S(2)}, u32[]{:S(2)}) collective-permute-start(bf16[256,1024]{1,0:T(8,128)(2,1)S(1)} %collective-permute-done.10), channel_id=1, source_target_pairs={{0,4},{4,8},{8,12},{12,14},{14,10},{10,6},{6,2},{2,0},{1,5},{5,9},... | collective-permute-start | bytes 1572872 | tf_op jit(solution)/shard_map/ppermute | solution.py:100
  100.6 9.2 %collective-permute-start.13 = (bf16[256,1024]{1,0:T(8,128)(2,1)S(1)}, bf16[256,1024]{1,0:T(8,128)(2,1)S(1)}, u32[]{:S(2)}, u32[]{:S(2)}) collective-permute-start(bf16[256,1024]{1,0:T(8,128)(2,1)S(1)} %collective-permute-done.11), channel_id=1, source_target_pairs={{4,0},{8,4},{12,8},{14,12},{10,14},{6,10},{2,6},{0,2},{5,1},{9,5},... | collective-permute-start | bytes 1572872 | tf_op jit(solution)/shard_map/ppermute | solution.py:101
  110.6 9.2 %copy-start.2 = (bf16[128,2048]{1,0:T(8,128)(2,1)S(1)}, bf16[128,2048]{1,0:T(8,128)(2,1)}, u32[]{:S(2)}) copy-start(bf16[128,2048]{1,0:T(8,128)(2,1)} %param.7) | copy-start | bytes 1572868
  118.3 3.6 %collective-permute-start.14 = (bf16[256,2048]{1,0:T(8,128)(2,1)S(1)}, bf16[256,2048]{1,0:T(8,128)(2,1)S(1)}, u32[]{:S(2)}, u32[]{:S(2)}) collective-permute-start(bf16[256,2048]{1,0:T(8,128)(2,1)S(1)} %get-tuple-element.45), channel_id=1, source_target_pairs={{0,1},{2,3},{4,5},{6,7},{8,9},{10,11},{12,13},{14,15},{16,17},{18,... | collective-permute-start | bytes 3145736 | tf_op jit(solution)/shard_map/ppermute | solution.py:18
  130.0 1.4 copy-start.1
  137.4 3.6 %collective-permute-start.15 = (f32[7]{0:T(128)S(1)}, f32[7]{0:T(128)S(1)}, u32[]{:S(2)}, u32[]{:S(2)}) collective-permute-start(f32[7]{0:T(128)S(1)} %stack.28), channel_id=1, source_target_pairs={{0,2},{2,0},{4,6},{6,4},{8,10},{10,8},{12,14},{14,12},{1,3},{3,1},... | collective-permute-start | bytes 92 | tf_op jit(solution)/shard_map/ppermute | solution.py:115
  141.0 3.6 %collective-permute-start.16 = (f32[7]{0:T(128)S(1)}, f32[7]{0:T(128)S(1)}, u32[]{:S(2)}, u32[]{:S(2)}) collective-permute-start(f32[7]{0:T(128)S(1)} %add.373), channel_id=1, source_target_pairs={{0,4},{2,6},{4,0},{6,2},{8,12},{10,14},{12,8},{14,10},{1,5},{3,7},... | collective-permute-start | bytes 92 | tf_op jit(solution)/shard_map/ppermute | solution.py:115
  144.6 4.5 %collective-permute-start.17 = (f32[7]{0:T(128)S(1)}, f32[7]{0:T(128)S(1)}, u32[]{:S(2)}, u32[]{:S(2)}) collective-permute-start(f32[7]{0:T(128)S(1)} %add.374), channel_id=1, source_target_pairs={{0,8},{2,10},{4,12},{6,14},{8,0},{10,2},{12,4},{14,6},{1,9},{3,11}... | collective-permute-start | bytes 92 | tf_op jit(solution)/shard_map/ppermute | solution.py:115
  154.0 6.0 %copy-start.7 = (f32[256,2048]{1,0:T(8,128)S(1)}, f32[256,2048]{1,0:T(8,128)}, u32[]{:S(2)}) copy-start(f32[256,2048]{1,0:T(8,128)} %get-tuple-element.48) | copy-start | bytes 6291460
  167.7 6.4 %collective-permute-start.18 = (bf16[256,2048]{1,0:T(8,128)(2,1)S(1)}, bf16[256,2048]{1,0:T(8,128)(2,1)S(1)}, u32[]{:S(2)}, u32[]{:S(2)}) collective-permute-start(bf16[256,2048]{1,0:T(8,128)(2,1)S(1)} %fusion.10), channel_id=1, source_target_pairs={{1,0},{3,2},{5,4},{7,6},{9,8},{11,10},{13,12},{15,14},{17,16},{19,... | collective-permute-start | bytes 3145736 | tf_op jit(solution)/shard_map/ppermute | solution.py:18
  170.3 3.3 %collective-permute-start.19 = (f32[1]{0:T(128)}, f32[1]{0:T(128)}, u32[]{:S(2)}, u32[]{:S(2)}) collective-permute-start(f32[1]{0:T(128)} %bitcast.51), channel_id=1, source_target_pairs={{1,0},{3,2},{5,4},{7,6},{9,8},{11,10},{13,12},{15,14},{17,16},{19,... | collective-permute-start | bytes 20 | tf_op jit(solution)/shard_map/ppermute | solution.py:18

commit v3 on v2

--- a/solution.py
+++ b/solution.py
@@ -77,7 +77,7 @@
     return list(range(0, n, 2)) + list(range(n - 1, 0, -2))
 
 
-def ring_gather(local, axis):
+def ring_gather(local, axis, pieces=2):
     n = lax.axis_size(axis)
     rows, cols = local.shape
     if n == 1:
@@ -91,18 +91,18 @@
     ring_arr = jnp.asarray(ring, jnp.int32)
     cw = [(ring[i], ring[(i + 1) % n]) for i in range(n)]
     ccw = [(ring[(i + 1) % n], ring[i]) for i in range(n)]
-    half = cols // 2
-    left = local[:, :half]
-    right = local[:, half:]
+    width = cols // (2 * pieces)
+    parts = [local[:, j * width:(j + 1) * width] for j in range(2 * pieces)]
     full = jnp.zeros((n * rows, cols), local.dtype)
     full = lax.dynamic_update_slice(full, local, (me * rows, 0))
     for k in range(1, n):
-        left = lax.ppermute(left, axis, cw)
-        right = lax.ppermute(right, axis, ccw)
-        from_left = ring_arr[(my_pos - k) % n]
-        from_right = ring_arr[(my_pos + k) % n]
-        full = lax.dynamic_update_slice(full, left, (from_left * rows, 0))
-        full = lax.dynamic_update_slice(full, right, (from_right * rows, half))
+        from_cw = ring_arr[(my_pos - k) % n]
+        from_ccw = ring_arr[(my_pos + k) % n]
+        for j in range(2 * pieces):
+            clockwise = j % 2 == 0
+            parts[j] = lax.ppermute(parts[j], axis, cw if clockwise else ccw)
+            origin = from_cw if clockwise else from_ccw
+            full = lax.dynamic_update_slice(full, parts[j], (origin * rows, j * width))
     return full
 
 

time: 186 us -> 168 us (0.903)
  local copies, waits for them, and re-layouts: 37.1 us -> 13.2 us
  starting transfers between devices: 24.9 us -> 38.4 us
  matrix products: 29.6 us -> 23 us
    dynamic_update_slice x14 -> x28, local copies, waits for them, and re-layouts: 20.4 us -> 0.73 us  [ring_gather(): full = lax.dynamic_update_slice(full, parts[j], (origin * rows, j * width))]
    ppermute x14 -> x28, starting transfers between devices: 15.3 us -> 29.6 us  [ring_gather(): parts[j] = lax.ppermute(parts[j], axis, cw if clockwise else ccw)]
    dot_general x2, matrix products: 15.2 us -> 8.52 us  [section_forward(): pre_act = jnp.dot(normed, weight, preferred_element_type=jnp.float32)]
    broadcast_in_dim x1, local copies, waits for them, and re-layouts: 4.29 us -> 1.05 us  [ring_gather(): full = jnp.zeros((n * rows, cols), local.dtype)]
    ppermute x14 -> x28, waiting for transfers between devices: 47.1 us -> 45.1 us  [ring_gather(): parts[j] = lax.ppermute(parts[j], axis, cw if clockwise else ccw)]
  transfers between devices with their start and end apart: 20 -> 34, of which waited for: 11 -> 19; matrix products, arithmetic and copies ran while one was open for 15% -> 3% of each run, Pallas kernels for 0% -> 0%
where the time goes in v3:
time: 168 us; the launch traced here: 167 us
  waiting for transfers between devices  55 us (33%)
  starting transfers between devices  38.4 us (23%)
  matrix products  23 us (14%)
  between operations  22.4 us (13%)
  other arithmetic  15 us (9%)
  local copies, waits for them, and re-layouts  13.2 us (8%)
    ppermute x28, waiting for transfers between devices, ring_gather(): parts[j] = lax.ppermute(parts[j], axis, cw if clockwise else ccw)  45.1 us
    ppermute x28, starting transfers between devices, ring_gather(): parts[j] = lax.ppermute(parts[j], axis, cw if clockwise else ccw)  29.6 us
    dot_general x2, matrix products, section_backward(): lax.dot_general(grad_pre, weight, (((1,), (1,)), ((), ())), preferred_ele...  14.5 us
    dot_general x2, matrix products, section_forward(): pre_act = jnp.dot(normed, weight, preferred_element_type=jnp.float32)  8.52 us
    ppermute x3, waiting for transfers between devices, tree_sum(): v = v + lax.ppermute(v, axis, [(i, i ^ b) for i in range(n)])  7.15 us
    add x1, other arithmetic, per_device(): c = c + member_coeff[m, k] * y[k]  5.92 us
    another operation x1, local copies, waits for them, and re-layouts, per_device(): packed = tree_sum(jnp.stack(terms), 'tok')  4.51 us
    ppermute x3, starting transfers between devices, tree_sum(): v = v + lax.ppermute(v, axis, [(i, i ^ b) for i in range(n)])  4.45 us
  transfers between devices with their start and end apart: 34, of which 19 were waited for; matrix products, arithmetic and copies ran while one was open for 3% of the time, Pallas kernels for 0%

profile of v3, /device:TPU:0, one launch (start us, length us, event | category | flops | bytes accessed | tf_op | source)
XLA Modules:
  0.0 167.1 jit_solution(1156337706104788999)
XLA Ops:
  0.7 1.4 fusion.89
  2.0 3.1 %collective-permute-start = (bf16[256,512]{1,0:T(8,128)(2,1)S(1)}, bf16[256,512]{1,0:T(8,128)(2,1)S(1)}, u32[]{:S(2)}, u32[]{:S(2)}) collective-permute-start(bf16[256,512]{1,0:T(8,128)(2,1)S(1)} %get-tuple-element.24), channel_id=1, source_target_pairs={{0,4},{4,8},{8,12},{12,14},{14,10},{10,6},{6,2},{2,0},{1,5},{5,9},... | collective-permute-start | bytes 786440 | tf_op jit(solution)/shard_map/ppermute | solution.py:103
  5.1 2.0 %collective-permute-start.2 = (bf16[256,512]{1,0:T(8,128)(2,1)S(1)}, bf16[256,512]{1,0:T(8,128)(2,1)S(1)}, u32[]{:S(2)}, u32[]{:S(2)}) collective-permute-start(bf16[256,512]{1,0:T(8,128)(2,1)S(1)} %get-tuple-element.22), channel_id=1, source_target_pairs={{0,4},{4,8},{8,12},{12,14},{14,10},{10,6},{6,2},{2,0},{1,5},{5,9},... | collective-permute-start | bytes 786440 | tf_op jit(solution)/shard_map/ppermute | solution.py:103
  29.2 2.1 %collective-permute-start.4 = (bf16[256,512]{1,0:T(8,128)(2,1)S(1)}, bf16[256,512]{1,0:T(8,128)(2,1)S(1)}, u32[]{:S(2)}, u32[]{:S(2)}) collective-permute-start(bf16[256,512]{1,0:T(8,128)(2,1)S(1)} %collective-permute-done), channel_id=1, source_target_pairs={{0,4},{4,8},{8,12},{12,14},{14,10},{10,6},{6,2},{2,0},{1,5},{5,9},... | collective-permute-start | bytes 786440 | tf_op jit(solution)/shard_map/ppermute | solution.py:103
  31.3 2.0 %collective-permute-start.6 = (bf16[256,512]{1,0:T(8,128)(2,1)S(1)}, bf16[256,512]{1,0:T(8,128)(2,1)S(1)}, u32[]{:S(2)}, u32[]{:S(2)}) collective-permute-start(bf16[256,512]{1,0:T(8,128)(2,1)S(1)} %collective-permute-done.2), channel_id=1, source_target_pairs={{0,4},{4,8},{8,12},{12,14},{14,10},{10,6},{6,2},{2,0},{1,5},{5,9},... | collective-permute-start | bytes 786440 | tf_op jit(solution)/shard_map/ppermute | solution.py:103
  33.5 4.9 %collective-permute-done.4 = bf16[256,512]{1,0:T(8,128)(2,1)S(1)} collective-permute-done((bf16[256,512]{1,0:T(8,128)(2,1)S(1)}, bf16[256,512]{1,0:T(8,128)(2,1)S(1)}, u32[]{:S(2)}, u32[]{:S(2)}) %collective-permute-start.4) | collective-permute-done | bytes 262176 | tf_op jit(solution)/shard_map/ppermute | solution.py:103
  38.4 2.0 %collective-permute-start.8 = (bf16[256,512]{1,0:T(8,128)(2,1)S(1)}, bf16[256,512]{1,0:T(8,128)(2,1)S(1)}, u32[]{:S(2)}, u32[]{:S(2)}) collective-permute-start(bf16[256,512]{1,0:T(8,128)(2,1)S(1)} %collective-permute-done.4), channel_id=1, source_target_pairs={{0,4},{4,8},{8,12},{12,14},{14,10},{10,6},{6,2},{2,0},{1,5},{5,9},... | collective-permute-start | bytes 786440 | tf_op jit(solution)/shard_map/ppermute | solution.py:103
  40.5 3.6 %collective-permute-done.6 = bf16[256,512]{1,0:T(8,128)(2,1)S(1)} collective-permute-done((bf16[256,512]{1,0:T(8,128)(2,1)S(1)}, bf16[256,512]{1,0:T(8,128)(2,1)S(1)}, u32[]{:S(2)}, u32[]{:S(2)}) %collective-permute-start.6) | collective-permute-done | bytes 262176 | tf_op jit(solution)/shard_map/ppermute | solution.py:103
  44.0 2.0 %collective-permute-start.10 = (bf16[256,512]{1,0:T(8,128)(2,1)S(1)}, bf16[256,512]{1,0:T(8,128)(2,1)S(1)}, u32[]{:S(2)}, u32[]{:S(2)}) collective-permute-start(bf16[256,512]{1,0:T(8,128)(2,1)S(1)} %collective-permute-done.6), channel_id=1, source_target_pairs={{0,4},{4,8},{8,12},{12,14},{14,10},{10,6},{6,2},{2,0},{1,5},{5,9},... | collective-permute-start | bytes 786440 | tf_op jit(solution)/shard_map/ppermute | solution.py:103
  46.2 3.4 %collective-permute-done.8 = bf16[256,512]{1,0:T(8,128)(2,1)S(1)} collective-permute-done((bf16[256,512]{1,0:T(8,128)(2,1)S(1)}, bf16[256,512]{1,0:T(8,128)(2,1)S(1)}, u32[]{:S(2)}, u32[]{:S(2)}) %collective-permute-start.8) | collective-permute-done | bytes 262176 | tf_op jit(solution)/shard_map/ppermute | solution.py:103
  49.7 2.0 %collective-permute-start.12 = (bf16[256,512]{1,0:T(8,128)(2,1)S(1)}, bf16[256,512]{1,0:T(8,128)(2,1)S(1)}, u32[]{:S(2)}, u32[]{:S(2)}) collective-permute-start(bf16[256,512]{1,0:T(8,128)(2,1)S(1)} %collective-permute-done.8), channel_id=1, source_target_pairs={{0,4},{4,8},{8,12},{12,14},{14,10},{10,6},{6,2},{2,0},{1,5},{5,9},... | collective-permute-start | bytes 786440 | tf_op jit(solution)/shard_map/ppermute | solution.py:103
  51.7 3.6 %collective-permute-done.10 = bf16[256,512]{1,0:T(8,128)(2,1)S(1)} collective-permute-done((bf16[256,512]{1,0:T(8,128)(2,1)S(1)}, bf16[256,512]{1,0:T(8,128)(2,1)S(1)}, u32[]{:S(2)}, u32[]{:S(2)}) %collective-permute-start.10) | collective-permute-done | bytes 262176 | tf_op jit(solution)/shard_map/ppermute | solution.py:103
  55.3 2.0 %collective-permute-start.14 = (bf16[256,512]{1,0:T(8,128)(2,1)S(1)}, bf16[256,512]{1,0:T(8,128)(2,1)S(1)}, u32[]{:S(2)}, u32[]{:S(2)}) collective-permute-start(bf16[256,512]{1,0:T(8,128)(2,1)S(1)} %collective-permute-done.10), channel_id=1, source_target_pairs={{0,4},{4,8},{8,12},{12,14},{14,10},{10,6},{6,2},{2,0},{1,5},{5,9},... | collective-permute-start | bytes 786440 | tf_op jit(solution)/shard_map/ppermute | solution.py:103
  57.4 3.4 %collective-permute-done.12 = bf16[256,512]{1,0:T(8,128)(2,1)S(1)} collective-permute-done((bf16[256,512]{1,0:T(8,128)(2,1)S(1)}, bf16[256,512]{1,0:T(8,128)(2,1)S(1)}, u32[]{:S(2)}, u32[]{:S(2)}) %collective-permute-start.12) | collective-permute-done | bytes 262176 | tf_op jit(solution)/shard_map/ppermute | solution.py:103
  60.9 2.0 %collective-permute-start.16 = (bf16[256,512]{1,0:T(8,128)(2,1)S(1)}, bf16[256,512]{1,0:T(8,128)(2,1)S(1)}, u32[]{:S(2)}, u32[]{:S(2)}) collective-permute-start(bf16[256,512]{1,0:T(8,128)(2,1)S(1)} %collective-permute-done.12), channel_id=1, source_target_pairs={{0,4},{4,8},{8,12},{12,14},{14,10},{10,6},{6,2},{2,0},{1,5},{5,9},... | collective-permute-start | bytes 786440 | tf_op jit(solution)/shard_map/ppermute | solution.py:103
  62.9 3.6 %collective-permute-done.14 = bf16[256,512]{1,0:T(8,128)(2,1)S(1)} collective-permute-done((bf16[256,512]{1,0:T(8,128)(2,1)S(1)}, bf16[256,512]{1,0:T(8,128)(2,1)S(1)}, u32[]{:S(2)}, u32[]{:S(2)}) %collective-permute-start.14) | collective-permute-done | bytes 262176 | tf_op jit(solution)/shard_map/ppermute | solution.py:103
  66.5 2.0 %collective-permute-start.18 = (bf16[256,512]{1,0:T(8,128)(2,1)S(1)}, bf16[256,512]{1,0:T(8,128)(2,1)S(1)}, u32[]{:S(2)}, u32[]{:S(2)}) collective-permute-start(bf16[256,512]{1,0:T(8,128)(2,1)S(1)} %collective-permute-done.14), channel_id=1, source_target_pairs={{0,4},{4,8},{8,12},{12,14},{14,10},{10,6},{6,2},{2,0},{1,5},{5,9},... | collective-permute-start | bytes 786440 | tf_op jit(solution)/shard_map/ppermute | solution.py:103
  68.7 3.4 %collective-permute-done.16 = bf16[256,512]{1,0:T(8,128)(2,1)S(1)} collective-permute-done((bf16[256,512]{1,0:T(8,128)(2,1)S(1)}, bf16[256,512]{1,0:T(8,128)(2,1)S(1)}, u32[]{:S(2)}, u32[]{:S(2)}) %collective-permute-start.16) | collective-permute-done | bytes 262176 | tf_op jit(solution)/shard_map/ppermute | solution.py:103
  72.1 2.0 %collective-permute-start.20 = (bf16[256,512]{1,0:T(8,128)(2,1)S(1)}, bf16[256,512]{1,0:T(8,128)(2,1)S(1)}, u32[]{:S(2)}, u32[]{:S(2)}) collective-permute-start(bf16[256,512]{1,0:T(8,128)(2,1)S(1)} %collective-permute-done.16), channel_id=1, source_target_pairs={{0,4},{4,8},{8,12},{12,14},{14,10},{10,6},{6,2},{2,0},{1,5},{5,9},... | collective-permute-start | bytes 786440 | tf_op jit(solution)/shard_map/ppermute | solution.py:103
  74.2 3.6 %collective-permute-done.18 = bf16[256,512]{1,0:T(8,128)(2,1)S(1)} collective-permute-done((bf16[256,512]{1,0:T(8,128)(2,1)S(1)}, bf16[256,512]{1,0:T(8,128)(2,1)S(1)}, u32[]{:S(2)}, u32[]{:S(2)}) %collective-permute-start.18) | collective-permute-done | bytes 262176 | tf_op jit(solution)/shard_map/ppermute | solution.py:103
  77.8 2.0 %collective-permute-start.22 = (bf16[256,512]{1,0:T(8,128)(2,1)S(1)}, bf16[256,512]{1,0:T(8,128)(2,1)S(1)}, u32[]{:S(2)}, u32[]{:S(2)}) collective-permute-start(bf16[256,512]{1,0:T(8,128)(2,1)S(1)} %collective-permute-done.18), channel_id=1, source_target_pairs={{0,4},{4,8},{8,12},{12,14},{14,10},{10,6},{6,2},{2,0},{1,5},{5,9},... | collective-permute-start | bytes 786440 | tf_op jit(solution)/shard_map/ppermute | solution.py:103
  79.9 3.4 %collective-permute-done.20 = bf16[256,512]{1,0:T(8,128)(2,1)S(1)} collective-permute-done((bf16[256,512]{1,0:T(8,128)(2,1)S(1)}, bf16[256,512]{1,0:T(8,128)(2,1)S(1)}, u32[]{:S(2)}, u32[]{:S(2)}) %collective-permute-start.20) | collective-permute-done | bytes 262176 | tf_op jit(solution)/shard_map/ppermute | solution.py:103
  83.4 2.0 %collective-permute-start.24 = (bf16[256,512]{1,0:T(8,128)(2,1)S(1)}, bf16[256,512]{1,0:T(8,128)(2,1)S(1)}, u32[]{:S(2)}, u32[]{:S(2)}) collective-permute-start(bf16[256,512]{1,0:T(8,128)(2,1)S(1)} %collective-permute-done.20), channel_id=1, source_target_pairs={{0,4},{4,8},{8,12},{12,14},{14,10},{10,6},{6,2},{2,0},{1,5},{5,9},... | collective-permute-start | bytes 786440 | tf_op jit(solution)/shard_map/ppermute | solution.py:103
  85.4 3.6 %collective-permute-done.22 = bf16[256,512]{1,0:T(8,128)(2,1)S(1)} collective-permute-done((bf16[256,512]{1,0:T(8,128)(2,1)S(1)}, bf16[256,512]{1,0:T(8,128)(2,1)S(1)}, u32[]{:S(2)}, u32[]{:S(2)}) %collective-permute-start.22) | collective-permute-done | bytes 262176 | tf_op jit(solution)/shard_map/ppermute | solution.py:103
  89.0 2.0 %collective-permute-start.26 = (bf16[256,512]{1,0:T(8,128)(2,1)S(1)}, bf16[256,512]{1,0:T(8,128)(2,1)S(1)}, u32[]{:S(2)}, u32[]{:S(2)}) collective-permute-start(bf16[256,512]{1,0:T(8,128)(2,1)S(1)} %collective-permute-done.22), channel_id=1, source_target_pairs={{0,4},{4,8},{8,12},{12,14},{14,10},{10,6},{6,2},{2,0},{1,5},{5,9},... | collective-permute-start | bytes 786440 | tf_op jit(solution)/shard_map/ppermute | solution.py:103
  91.2 3.4 %collective-permute-done.24 = bf16[256,512]{1,0:T(8,128)(2,1)S(1)} collective-permute-done((bf16[256,512]{1,0:T(8,128)(2,1)S(1)}, bf16[256,512]{1,0:T(8,128)(2,1)S(1)}, u32[]{:S(2)}, u32[]{:S(2)}) %collective-permute-start.24) | collective-permute-done | bytes 262176 | tf_op jit(solution)/shard_map/ppermute | solution.py:103
  94.6 2.0 %collective-permute-done.25 = bf16[256,512]{1,0:T(8,128)(2,1)S(1)} collective-permute-done((bf16[256,512]{1,0:T(8,128)(2,1)S(1)}, bf16[256,512]{1,0:T(8,128)(2,1)S(1)}, u32[]{:S(2)}, u32[]{:S(2)}) %collective-permute-start.25) | collective-permute-done | bytes 262176 | tf_op jit(solution)/shard_map/ppermute | solution.py:103
  96.7 1.6 collective-permute-done.26
  98.3 1.4 collective-permute-done.27
  99.8 4.2 %fusion.37 = (bf16[256,2048]{1,0:T(8,128)(2,1)S(1)}, f32[256,2048]{1,0:T(8,128)}) fusion(bf16[2,128,2048]{2,1,0:T(8,128)(2,1)S(1)} %copy-done, bf16[256,2048]{1,0:T(8,128)(2,1)S(1)} %fusion.33, bf16[2048,2048]{1,0:T(8,128)(2,1)S(1)} %constant_dynamic-update-slice_fusion), kind=kOutput, calls=%fused_computation.54 | convolution fusion | flops 2153250816 | bytes 13631488 | tf_op jit(solution)/shard_map/dot_general | solution.py:40
  104.0 1.5 collective-permute-start.28
  108.2 4.3 %fusion.46 = (f32[256,2048]{1,0:T(8,128)S(1)}, f32[256,2048]{1,0:T(8,128)}) fusion(bf16[256,2048]{1,0:T(8,128)(2,1)S(1)} %collective-permute-done.28, bf16[2048,2048]{1,0:T(8,128)(2,1)S(1)} %constant_dynamic-update-slice_fusion, f32[256]{0:T(256)S(1)} %add_rsqrt_fusion, f32[256]{0:T(256)S(1)} %broadcast_multiply_fusion.4, f32[2048]{0:T(1024)S(1)} %bitcast.90), kind=kOutput, calls=%fused_computation.65 | convolution fusion | flops 2156396544 | bytes 13641728 | tf_op jit(solution)/shard_map/dot_general | solution.py:40
  112.5 1.3 copy-done.1
  113.8 1.4 fusion.41
  115.3 4.5 %stack.28 = f32[7]{0:T(128)S(1)} concatenate(f32[1]{0:T(128)} %bitcast.35, f32[1]{0:T(128)} %bitcast.36, f32[1]{0:T(128)} %bitcast.36, f32[1]{0:T(128)} %bitcast.37, f32[1]{0:T(128)} %bitcast.38, f32[1]{0:T(128)} %bitcast.39, f32[1]{0:T(128)} %bitcast.40), dimensions={0} | concatenate | bytes 56 | tf_op jit(solution)/shard_map/stack | solution.py:151
  120.1 3.3 %collective-permute-done.29 = f32[7]{0:T(128)S(1)} collective-permute-done((f32[7]{0:T(128)S(1)}, f32[7]{0:T(128)S(1)}, u32[]{:S(2)}, u32[]{:S(2)}) %collective-permute-start.29) | collective-permute-done | bytes 60 | tf_op jit(solution)/shard_map/ppermute | solution.py:115
  123.3 1.6 collective-permute-start.30
  124.9 2.0 %collective-permute-done.30 = f32[7]{0:T(128)S(1)} collective-permute-done((f32[7]{0:T(128)S(1)}, f32[7]{0:T(128)S(1)}, u32[]{:S(2)}, u32[]{:S(2)}) %collective-permute-start.30) | collective-permute-done | bytes 60 | tf_op jit(solution)/shard_map/ppermute | solution.py:115
  126.9 2.6 %collective-permute-start.31 = (f32[7]{0:T(128)S(1)}, f32[7]{0:T(128)S(1)}, u32[]{:S(2)}, u32[]{:S(2)}) collective-permute-start(f32[7]{0:T(128)S(1)} %add.388), channel_id=1, source_target_pairs={{0,8},{2,10},{4,12},{6,14},{8,0},{10,2},{12,4},{14,6},{1,9},{3,11}... | collective-permute-start | bytes 92 | tf_op jit(solution)/shard_map/ppermute | solution.py:115
  129.5 1.9 %collective-permute-done.31 = f32[7]{0:T(128)S(1)} collective-permute-done((f32[7]{0:T(128)S(1)}, f32[7]{0:T(128)S(1)}, u32[]{:S(2)}, u32[]{:S(2)}) %collective-permute-start.31) | collective-permute-done | bytes 60 | tf_op jit(solution)/shard_map/ppermute | solution.py:115
  133.4 1.4 fusion.85
  136.3 5.9 %fusion.43 = (f32[128,2048]{1,0:T(8,128)S(1)}, f32[128,2048]{1,0:T(8,128)S(1)}) fusion(bf16[128,2048]{1,0:T(8,128)(2,1)S(1)} %copy-done.3, f32[256,2048]{1,0:T(8,128)} %copy-done.1, f32[]{:T(128)} %bitcast.45, f32[]{:T(128)} %bitcast.44, f32[]{:T(128)} %bitcast.43, f32[]{:T(128)} %bitcast.48, f32[]{:T(128)} %bitcast.47, f32[]{:T(128)} %bitcast.46), kind=kLoop, calls=%fused_computation.62 | loop fusion | flops 2883584 | bytes 4718616 | tf_op jit(solution)/shard_map/add | solution.py:164
  142.2 6.9 %fusion.83 = (f32[256]{0:T(256)S(1)}, f32[256]{0:T(256)S(1)}, f32[256,2048]{1,0:T(8,128)S(1)}) fusion(f32[256]{0:T(256)S(1)} %add_rsqrt_fusion, f32[256]{0:T(256)S(1)} %broadcast_multiply_fusion.4, bf16[256,2048]{1,0:T(8,128)(2,1)S(1)} %collective-permute-done.28, f32[2048]{0:T(1024)S(1)} %bitcast.91, bf16[2048,2048]{1,0:T(8,128)(2,1)} %copy-done.2, ...), kind=kOutput, calls=%fused_computation.149 | convolution fusion | flops 2161638912 | bytes 15740928 | tf_op jit(solution)/shard_map/dot_general | solution.py:47
  149.9 1.3 collective-permute-start.32
  152.5 1.5 collective-permute-start.33
  154.1 1.7 %collective-permute-done.33 = f32[1]{0:T(128)} collective-permute-done((f32[1]{0:T(128)}, f32[1]{0:T(128)}, u32[]{:S(2)}, u32[]{:S(2)}) %collective-permute-start.33) | collective-permute-done | bytes 36 | tf_op jit(solution)/shard_map/ppermute | solution.py:18
  156.4 7.6 %fusion.82 = (f32[256]{0:T(256)S(1)}, f32[256]{0:T(256)S(1)}, f32[256,2048]{1,0:T(8,128)S(1)}) fusion(f32[256]{0:T(256)S(1)} %rsqrt_bitcast_fusion, f32[256]{0:T(256)S(1)} %get-tuple-element.29, bf16[2,128,2048]{2,1,0:T(8,128)(2,1)S(1)} %copy-done, f32[2048]{0:T(1024)S(1)} %bitcast.92, bf16[2048,2048]{1,0:T(8,128)(2,1)} %copy-done.2, ...), kind=kOutput, calls=%fused_computation.148 | convolution fusion | flops 2161638912 | bytes 14692352 | tf_op jit(solution)/shard_map/dot_general | solution.py:47
  164.0 2.0 %fusion.47 = bf16[256,2048]{1,0:T(8,128)(2,1)} fusion(bf16[256,2048]{1,0:T(8,128)(2,1)S(1)} %fusion.10, bf16[2,128,2048]{2,1,0:T(8,128)(2,1)S(1)} %copy-done, f32[256,2048]{1,0:T(8,128)S(1)} %get-tuple-element.52, bf16[256,2048]{1,0:T(8,128)(2,1)S(1)} %collective-permute-done.32, f32[256]{0:T(256)S(1)} %broadcast_multiply_fusion, ...), kind=kLoop, calls=%fused_computation.66 | loop fusion | flops 5767168 | bytes 6295553 | tf_op jit(solution)/shard_map/jit(_where)/select_n | solution.py:171
  (108 shorter events, 11.9 us)
Async XLA Ops:
  0.6 6.5 %copy-start.7 = (s32[8]{0:T(128)S(1)}, s32[8]{0:T(128)}, u32[]{:S(2)}) copy-start(s32[8]{0:T(128)} %constant.197.clone) | copy-start | bytes 100
  0.6 16.4 %copy-start.5 = (s32[8]{0:T(128)S(1)}, s32[8]{0:T(128)}, u32[]{:S(2)}) copy-start(s32[8]{0:T(128)} %constant.198.clone) | copy-start | bytes 100
  0.7 26.0 %copy-start = (bf16[2,128,2048]{2,1,0:T(8,128)(2,1)S(1)}, bf16[2,128,2048]{2,1,0:T(8,128)(2,1)}, u32[]{:S(2)}) copy-start(bf16[2,128,2048]{2,1,0:T(8,128)(2,1)} %param.6) | copy-start | bytes 3145732
  0.7 26.8 %copy-start.6 = (f32[1,2048]{1,0:T(1,128)S(1)}, f32[1,2048]{1,0:T(1,128)}, u32[]{:S(2)}) copy-start(f32[1,2048]{1,0:T(1,128)} %param.9) | copy-start | bytes 24580
  2.0 27.2 %collective-permute-start = (bf16[256,512]{1,0:T(8,128)(2,1)S(1)}, bf16[256,512]{1,0:T(8,128)(2,1)S(1)}, u32[]{:S(2)}, u32[]{:S(2)}) collective-permute-start(bf16[256,512]{1,0:T(8,128)(2,1)S(1)} %get-tuple-element.24), channel_id=1, source_target_pairs={{0,4},{4,8},{8,12},{12,14},{14,10},{10,6},{6,2},{2,0},{1,5},{5,9},... | collective-permute-start | bytes 786440 | tf_op jit(solution)/shard_map/ppermute | solution.py:103
  5.1 26.1 %collective-permute-start.1 = (bf16[256,512]{1,0:T(8,128)(2,1)S(1)}, bf16[256,512]{1,0:T(8,128)(2,1)S(1)}, u32[]{:S(2)}, u32[]{:S(2)}) collective-permute-start(bf16[256,512]{1,0:T(8,128)(2,1)S(1)} %get-tuple-element.23), channel_id=1, source_target_pairs={{4,0},{8,4},{12,8},{14,12},{10,14},{6,10},{2,6},{0,2},{5,1},{9,5},... | collective-permute-start | bytes 786440 | tf_op jit(solution)/shard_map/ppermute | solution.py:103
  5.1 26.1 %collective-permute-start.2 = (bf16[256,512]{1,0:T(8,128)(2,1)S(1)}, bf16[256,512]{1,0:T(8,128)(2,1)S(1)}, u32[]{:S(2)}, u32[]{:S(2)}) collective-permute-start(bf16[256,512]{1,0:T(8,128)(2,1)S(1)} %get-tuple-element.22), channel_id=1, source_target_pairs={{0,4},{4,8},{8,12},{12,14},{14,10},{10,6},{6,2},{2,0},{1,5},{5,9},... | collective-permute-start | bytes 786440 | tf_op jit(solution)/shard_map/ppermute | solution.py:103
  7.2 26.1 %collective-permute-start.3 = (bf16[256,512]{1,0:T(8,128)(2,1)S(1)}, bf16[256,512]{1,0:T(8,128)(2,1)S(1)}, u32[]{:S(2)}, u32[]{:S(2)}) collective-permute-start(bf16[256,512]{1,0:T(8,128)(2,1)S(1)} %get-tuple-element.21), channel_id=1, source_target_pairs={{4,0},{8,4},{12,8},{14,12},{10,14},{6,10},{2,6},{0,2},{5,1},{9,5},... | collective-permute-start | bytes 786440 | tf_op jit(solution)/shard_map/ppermute | solution.py:103
  27.8 1.2 copy-start.4
  29.2 9.2 %collective-permute-start.4 = (bf16[256,512]{1,0:T(8,128)(2,1)S(1)}, bf16[256,512]{1,0:T(8,128)(2,1)S(1)}, u32[]{:S(2)}, u32[]{:S(2)}) collective-permute-start(bf16[256,512]{1,0:T(8,128)(2,1)S(1)} %collective-permute-done), channel_id=1, source_target_pairs={{0,4},{4,8},{8,12},{12,14},{14,10},{10,6},{6,2},{2,0},{1,5},{5,9},... | collective-permute-start | bytes 786440 | tf_op jit(solution)/shard_map/ppermute | solution.py:103
  31.3 9.2 %collective-permute-start.5 = (bf16[256,512]{1,0:T(8,128)(2,1)S(1)}, bf16[256,512]{1,0:T(8,128)(2,1)S(1)}, u32[]{:S(2)}, u32[]{:S(2)}) collective-permute-start(bf16[256,512]{1,0:T(8,128)(2,1)S(1)} %collective-permute-done.1), channel_id=1, source_target_pairs={{4,0},{8,4},{12,8},{14,12},{10,14},{6,10},{2,6},{0,2},{5,1},{9,5},... | collective-permute-start | bytes 786440 | tf_op jit(solution)/shard_map/ppermute | solution.py:103
  31.3 12.8 %collective-permute-start.6 = (bf16[256,512]{1,0:T(8,128)(2,1)S(1)}, bf16[256,512]{1,0:T(8,128)(2,1)S(1)}, u32[]{:S(2)}, u32[]{:S(2)}) collective-permute-start(bf16[256,512]{1,0:T(8,128)(2,1)S(1)} %collective-permute-done.2), channel_id=1, source_target_pairs={{0,4},{4,8},{8,12},{12,14},{14,10},{10,6},{6,2},{2,0},{1,5},{5,9},... | collective-permute-start | bytes 786440 | tf_op jit(solution)/shard_map/ppermute | solution.py:103
  33.3 12.8 %collective-permute-start.7 = (bf16[256,512]{1,0:T(8,128)(2,1)S(1)}, bf16[256,512]{1,0:T(8,128)(2,1)S(1)}, u32[]{:S(2)}, u32[]{:S(2)}) collective-permute-start(bf16[256,512]{1,0:T(8,128)(2,1)S(1)} %collective-permute-done.3), channel_id=1, source_target_pairs={{4,0},{8,4},{12,8},{14,12},{10,14},{6,10},{2,6},{0,2},{5,1},{9,5},... | collective-permute-start | bytes 786440 | tf_op jit(solution)/shard_map/ppermute | solution.py:103
  38.4 11.2 %collective-permute-start.8 = (bf16[256,512]{1,0:T(8,128)(2,1)S(1)}, bf16[256,512]{1,0:T(8,128)(2,1)S(1)}, u32[]{:S(2)}, u32[]{:S(2)}) collective-permute-start(bf16[256,512]{1,0:T(8,128)(2,1)S(1)} %collective-permute-done.4), channel_id=1, source_target_pairs={{0,4},{4,8},{8,12},{12,14},{14,10},{10,6},{6,2},{2,0},{1,5},{5,9},... | collective-permute-start | bytes 786440 | tf_op jit(solution)/shard_map/ppermute | solution.py:103
  40.5 11.2 %collective-permute-start.9 = (bf16[256,512]{1,0:T(8,128)(2,1)S(1)}, bf16[256,512]{1,0:T(8,128)(2,1)S(1)}, u32[]{:S(2)}, u32[]{:S(2)}) collective-permute-start(bf16[256,512]{1,0:T(8,128)(2,1)S(1)} %collective-permute-done.5), channel_id=1, source_target_pairs={{4,0},{8,4},{12,8},{14,12},{10,14},{6,10},{2,6},{0,2},{5,1},{9,5},... | collective-permute-start | bytes 786440 | tf_op jit(solution)/shard_map/ppermute | solution.py:103
  44.0 11.2 %collective-permute-start.10 = (bf16[256,512]{1,0:T(8,128)(2,1)S(1)}, bf16[256,512]{1,0:T(8,128)(2,1)S(1)}, u32[]{:S(2)}, u32[]{:S(2)}) collective-permute-start(bf16[256,512]{1,0:T(8,128)(2,1)S(1)} %collective-permute-done.6), channel_id=1, source_target_pairs={{0,4},{4,8},{8,12},{12,14},{14,10},{10,6},{6,2},{2,0},{1,5},{5,9},... | collective-permute-start | bytes 786440 | tf_op jit(solution)/shard_map/ppermute | solution.py:103
  46.1 11.2 %collective-permute-start.11 = (bf16[256,512]{1,0:T(8,128)(2,1)S(1)}, bf16[256,512]{1,0:T(8,128)(2,1)S(1)}, u32[]{:S(2)}, u32[]{:S(2)}) collective-permute-start(bf16[256,512]{1,0:T(8,128)(2,1)S(1)} %collective-permute-done.7), channel_id=1, source_target_pairs={{4,0},{8,4},{12,8},{14,12},{10,14},{6,10},{2,6},{0,2},{5,1},{9,5},... | collective-permute-start | bytes 786440 | tf_op jit(solution)/shard_map/ppermute | solution.py:103
  49.7 11.2 %collective-permute-start.12 = (bf16[256,512]{1,0:T(8,128)(2,1)S(1)}, bf16[256,512]{1,0:T(8,128)(2,1)S(1)}, u32[]{:S(2)}, u32[]{:S(2)}) collective-permute-start(bf16[256,512]{1,0:T(8,128)(2,1)S(1)} %collective-permute-done.8), channel_id=1, source_target_pairs={{0,4},{4,8},{8,12},{12,14},{14,10},{10,6},{6,2},{2,0},{1,5},{5,9},... | collective-permute-start | bytes 786440 | tf_op jit(solution)/shard_map/ppermute | solution.py:103
  51.7 11.2 %collective-permute-start.13 = (bf16[256,512]{1,0:T(8,128)(2,1)S(1)}, bf16[256,512]{1,0:T(8,128)(2,1)S(1)}, u32[]{:S(2)}, u32[]{:S(2)}) collective-permute-start(bf16[256,512]{1,0:T(8,128)(2,1)S(1)} %collective-permute-done.9), channel_id=1, source_target_pairs={{4,0},{8,4},{12,8},{14,12},{10,14},{6,10},{2,6},{0,2},{5,1},{9,5},... | collective-permute-start | bytes 786440 | tf_op jit(solution)/shard_map/ppermute | solution.py:103
  55.3 11.2 %collective-permute-start.14 = (bf16[256,512]{1,0:T(8,128)(2,1)S(1)}, bf16[256,512]{1,0:T(8,128)(2,1)S(1)}, u32[]{:S(2)}, u32[]{:S(2)}) collective-permute-start(bf16[256,512]{1,0:T(8,128)(2,1)S(1)} %collective-permute-done.10), channel_id=1, source_target_pairs={{0,4},{4,8},{8,12},{12,14},{14,10},{10,6},{6,2},{2,0},{1,5},{5,9},... | collective-permute-start | bytes 786440 | tf_op jit(solution)/shard_map/ppermute | solution.py:103
  57.3 11.2 %collective-permute-start.15 = (bf16[256,512]{1,0:T(8,128)(2,1)S(1)}, bf16[256,512]{1,0:T(8,128)(2,1)S(1)}, u32[]{:S(2)}, u32[]{:S(2)}) collective-permute-start(bf16[256,512]{1,0:T(8,128)(2,1)S(1)} %collective-permute-done.11), channel_id=1, source_target_pairs={{4,0},{8,4},{12,8},{14,12},{10,14},{6,10},{2,6},{0,2},{5,1},{9,5},... | collective-permute-start | bytes 786440 | tf_op jit(solution)/shard_map/ppermute | solution.py:103
  60.9 11.2 %collective-permute-start.16 = (bf16[256,512]{1,0:T(8,128)(2,1)S(1)}, bf16[256,512]{1,0:T(8,128)(2,1)S(1)}, u32[]{:S(2)}, u32[]{:S(2)}) collective-permute-start(bf16[256,512]{1,0:T(8,128)(2,1)S(1)} %collective-permute-done.12), channel_id=1, source_target_pairs={{0,4},{4,8},{8,12},{12,14},{14,10},{10,6},{6,2},{2,0},{1,5},{5,9},... | collective-permute-start | bytes 786440 | tf_op jit(solution)/shard_map/ppermute | solution.py:103
  62.9 11.2 %collective-permute-start.17 = (bf16[256,512]{1,0:T(8,128)(2,1)S(1)}, bf16[256,512]{1,0:T(8,128)(2,1)S(1)}, u32[]{:S(2)}, u32[]{:S(2)}) collective-permute-start(bf16[256,512]{1,0:T(8,128)(2,1)S(1)} %collective-permute-done.13), channel_id=1, source_target_pairs={{4,0},{8,4},{12,8},{14,12},{10,14},{6,10},{2,6},{0,2},{5,1},{9,5},... | collective-permute-start | bytes 786440 | tf_op jit(solution)/shard_map/ppermute | solution.py:103
  66.5 11.2 %collective-permute-start.18 = (bf16[256,512]{1,0:T(8,128)(2,1)S(1)}, bf16[256,512]{1,0:T(8,128)(2,1)S(1)}, u32[]{:S(2)}, u32[]{:S(2)}) collective-permute-start(bf16[256,512]{1,0:T(8,128)(2,1)S(1)} %collective-permute-done.14), channel_id=1, source_target_pairs={{0,4},{4,8},{8,12},{12,14},{14,10},{10,6},{6,2},{2,0},{1,5},{5,9},... | collective-permute-start | bytes 786440 | tf_op jit(solution)/shard_map/ppermute | solution.py:103
  68.5 11.2 %collective-permute-start.19 = (bf16[256,512]{1,0:T(8,128)(2,1)S(1)}, bf16[256,512]{1,0:T(8,128)(2,1)S(1)}, u32[]{:S(2)}, u32[]{:S(2)}) collective-permute-start(bf16[256,512]{1,0:T(8,128)(2,1)S(1)} %collective-permute-done.15), channel_id=1, source_target_pairs={{4,0},{8,4},{12,8},{14,12},{10,14},{6,10},{2,6},{0,2},{5,1},{9,5},... | collective-permute-start | bytes 786440 | tf_op jit(solution)/shard_map/ppermute | solution.py:103
  72.1 11.2 %collective-permute-start.20 = (bf16[256,512]{1,0:T(8,128)(2,1)S(1)}, bf16[256,512]{1,0:T(8,128)(2,1)S(1)}, u32[]{:S(2)}, u32[]{:S(2)}) collective-permute-start(bf16[256,512]{1,0:T(8,128)(2,1)S(1)} %collective-permute-done.16), channel_id=1, source_target_pairs={{0,4},{4,8},{8,12},{12,14},{14,10},{10,6},{6,2},{2,0},{1,5},{5,9},... | collective-permute-start | bytes 786440 | tf_op jit(solution)/shard_map/ppermute | solution.py:103
  74.2 11.2 %collective-permute-start.21 = (bf16[256,512]{1,0:T(8,128)(2,1)S(1)}, bf16[256,512]{1,0:T(8,128)(2,1)S(1)}, u32[]{:S(2)}, u32[]{:S(2)}) collective-permute-start(bf16[256,512]{1,0:T(8,128)(2,1)S(1)} %collective-permute-done.17), channel_id=1, source_target_pairs={{4,0},{8,4},{12,8},{14,12},{10,14},{6,10},{2,6},{0,2},{5,1},{9,5},... | collective-permute-start | bytes 786440 | tf_op jit(solution)/shard_map/ppermute | solution.py:103
  77.8 11.2 %collective-permute-start.22 = (bf16[256,512]{1,0:T(8,128)(2,1)S(1)}, bf16[256,512]{1,0:T(8,128)(2,1)S(1)}, u32[]{:S(2)}, u32[]{:S(2)}) collective-permute-start(bf16[256,512]{1,0:T(8,128)(2,1)S(1)} %collective-permute-done.18), channel_id=1, source_target_pairs={{0,4},{4,8},{8,12},{12,14},{14,10},{10,6},{6,2},{2,0},{1,5},{5,9},... | collective-permute-start | bytes 786440 | tf_op jit(solution)/shard_map/ppermute | solution.py:103
  79.8 11.3 %collective-permute-start.23 = (bf16[256,512]{1,0:T(8,128)(2,1)S(1)}, bf16[256,512]{1,0:T(8,128)(2,1)S(1)}, u32[]{:S(2)}, u32[]{:S(2)}) collective-permute-start(bf16[256,512]{1,0:T(8,128)(2,1)S(1)} %collective-permute-done.19), channel_id=1, source_target_pairs={{4,0},{8,4},{12,8},{14,12},{10,14},{6,10},{2,6},{0,2},{5,1},{9,5},... | collective-permute-start | bytes 786440 | tf_op jit(solution)/shard_map/ppermute | solution.py:103
  83.4 11.2 %collective-permute-start.24 = (bf16[256,512]{1,0:T(8,128)(2,1)S(1)}, bf16[256,512]{1,0:T(8,128)(2,1)S(1)}, u32[]{:S(2)}, u32[]{:S(2)}) collective-permute-start(bf16[256,512]{1,0:T(8,128)(2,1)S(1)} %collective-permute-done.20), channel_id=1, source_target_pairs={{0,4},{4,8},{8,12},{12,14},{14,10},{10,6},{6,2},{2,0},{1,5},{5,9},... | collective-permute-start | bytes 786440 | tf_op jit(solution)/shard_map/ppermute | solution.py:103
  85.4 11.2 %collective-permute-start.25 = (bf16[256,512]{1,0:T(8,128)(2,1)S(1)}, bf16[256,512]{1,0:T(8,128)(2,1)S(1)}, u32[]{:S(2)}, u32[]{:S(2)}) collective-permute-start(bf16[256,512]{1,0:T(8,128)(2,1)S(1)} %collective-permute-done.21), channel_id=1, source_target_pairs={{4,0},{8,4},{12,8},{14,12},{10,14},{6,10},{2,6},{0,2},{5,1},{9,5},... | collective-permute-start | bytes 786440 | tf_op jit(solution)/shard_map/ppermute | solution.py:103
  89.0 9.3 %collective-permute-start.26 = (bf16[256,512]{1,0:T(8,128)(2,1)S(1)}, bf16[256,512]{1,0:T(8,128)(2,1)S(1)}, u32[]{:S(2)}, u32[]{:S(2)}) collective-permute-start(bf16[256,512]{1,0:T(8,128)(2,1)S(1)} %collective-permute-done.22), channel_id=1, source_target_pairs={{0,4},{4,8},{8,12},{12,14},{14,10},{10,6},{6,2},{2,0},{1,5},{5,9},... | collective-permute-start | bytes 786440 | tf_op jit(solution)/shard_map/ppermute | solution.py:103
  91.1 8.6 %collective-permute-start.27 = (bf16[256,512]{1,0:T(8,128)(2,1)S(1)}, bf16[256,512]{1,0:T(8,128)(2,1)S(1)}, u32[]{:S(2)}, u32[]{:S(2)}) collective-permute-start(bf16[256,512]{1,0:T(8,128)(2,1)S(1)} %collective-permute-done.23), channel_id=1, source_target_pairs={{4,0},{8,4},{12,8},{14,12},{10,14},{6,10},{2,6},{0,2},{5,1},{9,5},... | collective-permute-start | bytes 786440 | tf_op jit(solution)/shard_map/ppermute | solution.py:103
  99.7 8.5 %copy-start.2 = (bf16[2048,2048]{1,0:T(8,128)(2,1)}, bf16[2048,2048]{1,0:T(8,128)(2,1)S(1)}, u32[]{:S(2)}) copy-start(bf16[2048,2048]{1,0:T(8,128)(2,1)S(1)} %constant_dynamic-update-slice_fusion) | copy-start | bytes 25165828
  99.8 5.8 %copy-start.3 = (bf16[128,2048]{1,0:T(8,128)(2,1)S(1)}, bf16[128,2048]{1,0:T(8,128)(2,1)}, u32[]{:S(2)}) copy-start(bf16[128,2048]{1,0:T(8,128)(2,1)} %param.7) | copy-start | bytes 1572868
  104.0 3.6 %collective-permute-start.28 = (bf16[256,2048]{1,0:T(8,128)(2,1)S(1)}, bf16[256,2048]{1,0:T(8,128)(2,1)S(1)}, u32[]{:S(2)}, u32[]{:S(2)}) collective-permute-start(bf16[256,2048]{1,0:T(8,128)(2,1)S(1)} %get-tuple-element.47), channel_id=1, source_target_pairs={{0,1},{2,3},{4,5},{6,7},{8,9},{10,11},{12,13},{14,15},{16,17},{18,... | collective-permute-start | bytes 3145736 | tf_op jit(solution)/shard_map/ppermute | solution.py:18
  112.5 1.3 copy-start.1
  119.8 3.6 %collective-permute-start.29 = (f32[7]{0:T(128)S(1)}, f32[7]{0:T(128)S(1)}, u32[]{:S(2)}, u32[]{:S(2)}) collective-permute-start(f32[7]{0:T(128)S(1)} %stack.28), channel_id=1, source_target_pairs={{0,2},{2,0},{4,6},{6,4},{8,10},{10,8},{12,14},{14,12},{1,3},{3,1},... | collective-permute-start | bytes 92 | tf_op jit(solution)/shard_map/ppermute | solution.py:115
  123.3 3.6 %collective-permute-start.30 = (f32[7]{0:T(128)S(1)}, f32[7]{0:T(128)S(1)}, u32[]{:S(2)}, u32[]{:S(2)}) collective-permute-start(f32[7]{0:T(128)S(1)} %add.387), channel_id=1, source_target_pairs={{0,4},{2,6},{4,0},{6,2},{8,12},{10,14},{12,8},{14,10},{1,5},{3,7},... | collective-permute-start | bytes 92 | tf_op jit(solution)/shard_map/ppermute | solution.py:115
  126.9 4.5 %collective-permute-start.31 = (f32[7]{0:T(128)S(1)}, f32[7]{0:T(128)S(1)}, u32[]{:S(2)}, u32[]{:S(2)}) collective-permute-start(f32[7]{0:T(128)S(1)} %add.388), channel_id=1, source_target_pairs={{0,8},{2,10},{4,12},{6,14},{8,0},{10,2},{12,4},{14,6},{1,9},{3,11}... | collective-permute-start | bytes 92 | tf_op jit(solution)/shard_map/ppermute | solution.py:115
  136.3 5.9 %copy-start.8 = (f32[256,2048]{1,0:T(8,128)S(1)}, f32[256,2048]{1,0:T(8,128)}, u32[]{:S(2)}) copy-start(f32[256,2048]{1,0:T(8,128)} %get-tuple-element.50) | copy-start | bytes 6291460
  149.9 6.5 %collective-permute-start.32 = (bf16[256,2048]{1,0:T(8,128)(2,1)S(1)}, bf16[256,2048]{1,0:T(8,128)(2,1)S(1)}, u32[]{:S(2)}, u32[]{:S(2)}) collective-permute-start(bf16[256,2048]{1,0:T(8,128)(2,1)S(1)} %fusion.10), channel_id=1, source_target_pairs={{1,0},{3,2},{5,4},{7,6},{9,8},{11,10},{13,12},{15,14},{17,16},{19,... | collective-permute-start | bytes 3145736 | tf_op jit(solution)/shard_map/ppermute | solution.py:18
  152.5 3.3 %collective-permute-start.33 = (f32[1]{0:T(128)}, f32[1]{0:T(128)}, u32[]{:S(2)}, u32[]{:S(2)}) collective-permute-start(f32[1]{0:T(128)} %bitcast.51), channel_id=1, source_target_pairs={{1,0},{3,2},{5,4},{7,6},{9,8},{11,10},{13,12},{15,14},{17,16},{19,... | collective-permute-start | bytes 20 | tf_op jit(solution)/shard_map/ppermute | solution.py:18

commit v4 on v3

--- a/solution.py
+++ b/solution.py
@@ -42,8 +42,8 @@
     return (output, unit_rows, inv_std, pre_act)
 
 
-def section_backward(grad_out, gain, weight, unit_rows, inv_std, pre_act):
-    grad_pre = (grad_out * gelu_slope(pre_act)).astype(jnp.bfloat16)
+def section_backward(grad_out, gain, weight, unit_rows, inv_std, slope):
+    grad_pre = (grad_out * slope).astype(jnp.bfloat16)
     grad_norm = lax.dot_general(
         grad_pre, weight, (((1,), (1,)), ((), ())), preferred_element_type=jnp.float32
     )
@@ -132,6 +132,7 @@
     else:
         weight = lax.all_gather(weights, "tok", axis=1, tiled=True)[0]
 
+    inputs, weight = lax.optimization_barrier((inputs, weight))
     members = inputs.shape[0]
     rows_all = inputs.reshape(members * tok_rows, width)
 
@@ -144,11 +145,12 @@
     terms = []
     for m in range(members):
         for k in range(members):
-            terms.append(jnp.sum(y[m] * y[k]))
+            terms.append(jnp.sum(y[m] * y[k], axis=-1))
     for m in range(members):
-        terms.append(jnp.sum(y[m] * obs_f))
-    terms.append(obs_sq)
-    packed = tree_sum(jnp.stack(terms), "tok")
+        terms.append(jnp.sum(y[m] * obs_f, axis=-1))
+    terms = jnp.sum(jnp.stack(terms), axis=-1)
+    packed = tree_sum(jnp.concatenate([terms, obs_sq.reshape(1)]), "tok")
+    slope_a, slope_b = lax.optimization_barrier((gelu_slope(fa[3]), gelu_slope(fb[3])))
     member_gram = packed[: members * members].reshape(members, members)
     obs_rows = packed[members * members : members * members + members]
     obs_total = packed[members * members + members]
@@ -165,9 +167,9 @@
         cots.append(c)
     cot = jnp.concatenate(cots, axis=0)
 
-    da = section_backward(cot, gain, weight, fb[1], fb[2], fb[3])
+    da = section_backward(cot, gain, weight, fb[1], fb[2], slope_b)
     back = shifted(da, "section", -1)
-    db = section_backward(back.astype(jnp.float32), gain, weight, fa[1], fa[2], fa[3])
+    db = section_backward(back.astype(jnp.float32), gain, weight, fa[1], fa[2], slope_a)
     grads = jnp.where(on_first, db, da).reshape(members, tok_rows, width)
     return (grads[None], energy_out)
 

time: 168 us -> 164 us (0.976)
  local copies, waits for them, and re-layouts: 13.2 us -> 8.61 us
    another operation x1, local copies, waits for them, and re-layouts: 4.51 us -> 0.03 us  [per_device(): terms = jnp.sum(jnp.stack(terms), axis=-1)]
    dot_general x2, matrix products: 8.52 us -> 10.3 us  [section_forward(): pre_act = jnp.dot(normed, weight, preferred_element_type=jnp.float32)]
    dot_general x2, matrix products: 14.5 us -> 12.8 us  [section_backward(): lax.dot_general(grad_pre, weight, (((1,), (1,)), ((), ())), preferred_ele...]
  transfers between devices with their start and end apart: 34 -> 34, of which waited for: 19 -> 19; matrix products, arithmetic and copies ran while one was open for 3% -> 2% of each run, Pallas kernels for 0% -> 0%
where the time goes in v4:
time: 164 us; the launch traced here: 163 us
  waiting for transfers between devices  55.1 us (34%)
  starting transfers between devices  38.4 us (23%)
  matrix products  23.1 us (14%)
  between operations  22.2 us (14%)
  other arithmetic  15.6 us (10%)
  local copies, waits for them, and re-layouts  8.61 us (5%)
    ppermute x28, waiting for transfers between devices, ring_gather(): parts[j] = lax.ppermute(parts[j], axis, cw if clockwise else ccw)  45.1 us
    ppermute x28, starting transfers between devices, ring_gather(): parts[j] = lax.ppermute(parts[j], axis, cw if clockwise else ccw)  29.6 us
    dot_general x2, matrix products, section_backward(): lax.dot_general(grad_pre, weight, (((1,), (1,)), ((), ())), preferred_ele...  12.8 us
    dot_general x2, matrix products, section_forward(): pre_act = jnp.dot(normed, weight, preferred_element_type=jnp.float32)  10.3 us
    ppermute x3, waiting for transfers between devices, tree_sum(): v = v + lax.ppermute(v, axis, [(i, i ^ b) for i in range(n)])  7.18 us
    add x1, other arithmetic, per_device(): c = c + member_coeff[m, k] * y[k]  5.9 us
    ppermute x3, starting transfers between devices, tree_sum(): v = v + lax.ppermute(v, axis, [(i, i ^ b) for i in range(n)])  4.44 us
    ppermute x3, starting transfers between devices, shifted(): return lax.ppermute(x, axis, pairs)  4.33 us
  transfers between devices with their start and end apart: 34, of which 19 were waited for; matrix products, arithmetic and copies ran while one was open for 2% of the time, Pallas kernels for 0%

profile of v4, /device:TPU:0, one launch (start us, length us, event | category | flops | bytes accessed | tf_op | source)
XLA Modules:
  0.0 162.9 jit_solution(10363119111143846203)
XLA Ops:
  0.7 1.3 fusion.66
  1.9 3.1 %collective-permute-start = (bf16[256,512]{1,0:T(8,128)(2,1)S(1)}, bf16[256,512]{1,0:T(8,128)(2,1)S(1)}, u32[]{:S(2)}, u32[]{:S(2)}) collective-permute-start(bf16[256,512]{1,0:T(8,128)(2,1)S(1)} %get-tuple-element.36), channel_id=1, source_target_pairs={{0,4},{4,8},{8,12},{12,14},{14,10},{10,6},{6,2},{2,0},{1,5},{5,9},... | collective-permute-start | bytes 786440 | tf_op jit(solution)/shard_map/ppermute | solution.py:103
  5.0 2.0 %collective-permute-start.2 = (bf16[256,512]{1,0:T(8,128)(2,1)S(1)}, bf16[256,512]{1,0:T(8,128)(2,1)S(1)}, u32[]{:S(2)}, u32[]{:S(2)}) collective-permute-start(bf16[256,512]{1,0:T(8,128)(2,1)S(1)} %get-tuple-element.34), channel_id=1, source_target_pairs={{0,4},{4,8},{8,12},{12,14},{14,10},{10,6},{6,2},{2,0},{1,5},{5,9},... | collective-permute-start | bytes 786440 | tf_op jit(solution)/shard_map/ppermute | solution.py:103
  26.4 1.1 broadcast_in_dim.11
  27.7 2.1 %collective-permute-start.4 = (bf16[256,512]{1,0:T(8,128)(2,1)S(1)}, bf16[256,512]{1,0:T(8,128)(2,1)S(1)}, u32[]{:S(2)}, u32[]{:S(2)}) collective-permute-start(bf16[256,512]{1,0:T(8,128)(2,1)S(1)} %collective-permute-done), channel_id=1, source_target_pairs={{0,4},{4,8},{8,12},{12,14},{14,10},{10,6},{6,2},{2,0},{1,5},{5,9},... | collective-permute-start | bytes 786440 | tf_op jit(solution)/shard_map/ppermute | solution.py:103
  29.8 2.0 %collective-permute-start.6 = (bf16[256,512]{1,0:T(8,128)(2,1)S(1)}, bf16[256,512]{1,0:T(8,128)(2,1)S(1)}, u32[]{:S(2)}, u32[]{:S(2)}) collective-permute-start(bf16[256,512]{1,0:T(8,128)(2,1)S(1)} %collective-permute-done.2), channel_id=1, source_target_pairs={{0,4},{4,8},{8,12},{12,14},{14,10},{10,6},{6,2},{2,0},{1,5},{5,9},... | collective-permute-start | bytes 786440 | tf_op jit(solution)/shard_map/ppermute | solution.py:103
  32.0 4.9 %collective-permute-done.4 = bf16[256,512]{1,0:T(8,128)(2,1)S(1)} collective-permute-done((bf16[256,512]{1,0:T(8,128)(2,1)S(1)}, bf16[256,512]{1,0:T(8,128)(2,1)S(1)}, u32[]{:S(2)}, u32[]{:S(2)}) %collective-permute-start.4) | collective-permute-done | bytes 262176 | tf_op jit(solution)/shard_map/ppermute | solution.py:103
  37.0 2.0 %collective-permute-start.8 = (bf16[256,512]{1,0:T(8,128)(2,1)S(1)}, bf16[256,512]{1,0:T(8,128)(2,1)S(1)}, u32[]{:S(2)}, u32[]{:S(2)}) collective-permute-start(bf16[256,512]{1,0:T(8,128)(2,1)S(1)} %collective-permute-done.4), channel_id=1, source_target_pairs={{0,4},{4,8},{8,12},{12,14},{14,10},{10,6},{6,2},{2,0},{1,5},{5,9},... | collective-permute-start | bytes 786440 | tf_op jit(solution)/shard_map/ppermute | solution.py:103
  39.0 3.6 %collective-permute-done.6 = bf16[256,512]{1,0:T(8,128)(2,1)S(1)} collective-permute-done((bf16[256,512]{1,0:T(8,128)(2,1)S(1)}, bf16[256,512]{1,0:T(8,128)(2,1)S(1)}, u32[]{:S(2)}, u32[]{:S(2)}) %collective-permute-start.6) | collective-permute-done | bytes 262176 | tf_op jit(solution)/shard_map/ppermute | solution.py:103
  42.6 2.0 %collective-permute-start.10 = (bf16[256,512]{1,0:T(8,128)(2,1)S(1)}, bf16[256,512]{1,0:T(8,128)(2,1)S(1)}, u32[]{:S(2)}, u32[]{:S(2)}) collective-permute-start(bf16[256,512]{1,0:T(8,128)(2,1)S(1)} %collective-permute-done.6), channel_id=1, source_target_pairs={{0,4},{4,8},{8,12},{12,14},{14,10},{10,6},{6,2},{2,0},{1,5},{5,9},... | collective-permute-start | bytes 786440 | tf_op jit(solution)/shard_map/ppermute | solution.py:103
  44.8 3.4 %collective-permute-done.8 = bf16[256,512]{1,0:T(8,128)(2,1)S(1)} collective-permute-done((bf16[256,512]{1,0:T(8,128)(2,1)S(1)}, bf16[256,512]{1,0:T(8,128)(2,1)S(1)}, u32[]{:S(2)}, u32[]{:S(2)}) %collective-permute-start.8) | collective-permute-done | bytes 262176 | tf_op jit(solution)/shard_map/ppermute | solution.py:103
  48.2 2.0 %collective-permute-start.12 = (bf16[256,512]{1,0:T(8,128)(2,1)S(1)}, bf16[256,512]{1,0:T(8,128)(2,1)S(1)}, u32[]{:S(2)}, u32[]{:S(2)}) collective-permute-start(bf16[256,512]{1,0:T(8,128)(2,1)S(1)} %collective-permute-done.8), channel_id=1, source_target_pairs={{0,4},{4,8},{8,12},{12,14},{14,10},{10,6},{6,2},{2,0},{1,5},{5,9},... | collective-permute-start | bytes 786440 | tf_op jit(solution)/shard_map/ppermute | solution.py:103
  50.2 3.6 %collective-permute-done.10 = bf16[256,512]{1,0:T(8,128)(2,1)S(1)} collective-permute-done((bf16[256,512]{1,0:T(8,128)(2,1)S(1)}, bf16[256,512]{1,0:T(8,128)(2,1)S(1)}, u32[]{:S(2)}, u32[]{:S(2)}) %collective-permute-start.10) | collective-permute-done | bytes 262176 | tf_op jit(solution)/shard_map/ppermute | solution.py:103
  53.8 2.0 %collective-permute-start.14 = (bf16[256,512]{1,0:T(8,128)(2,1)S(1)}, bf16[256,512]{1,0:T(8,128)(2,1)S(1)}, u32[]{:S(2)}, u32[]{:S(2)}) collective-permute-start(bf16[256,512]{1,0:T(8,128)(2,1)S(1)} %collective-permute-done.10), channel_id=1, source_target_pairs={{0,4},{4,8},{8,12},{12,14},{14,10},{10,6},{6,2},{2,0},{1,5},{5,9},... | collective-permute-start | bytes 786440 | tf_op jit(solution)/shard_map/ppermute | solution.py:103
  56.0 3.4 %collective-permute-done.12 = bf16[256,512]{1,0:T(8,128)(2,1)S(1)} collective-permute-done((bf16[256,512]{1,0:T(8,128)(2,1)S(1)}, bf16[256,512]{1,0:T(8,128)(2,1)S(1)}, u32[]{:S(2)}, u32[]{:S(2)}) %collective-permute-start.12) | collective-permute-done | bytes 262176 | tf_op jit(solution)/shard_map/ppermute | solution.py:103
  59.4 2.0 %collective-permute-start.16 = (bf16[256,512]{1,0:T(8,128)(2,1)S(1)}, bf16[256,512]{1,0:T(8,128)(2,1)S(1)}, u32[]{:S(2)}, u32[]{:S(2)}) collective-permute-start(bf16[256,512]{1,0:T(8,128)(2,1)S(1)} %collective-permute-done.12), channel_id=1, source_target_pairs={{0,4},{4,8},{8,12},{12,14},{14,10},{10,6},{6,2},{2,0},{1,5},{5,9},... | collective-permute-start | bytes 786440 | tf_op jit(solution)/shard_map/ppermute | solution.py:103
  61.5 3.6 %collective-permute-done.14 = bf16[256,512]{1,0:T(8,128)(2,1)S(1)} collective-permute-done((bf16[256,512]{1,0:T(8,128)(2,1)S(1)}, bf16[256,512]{1,0:T(8,128)(2,1)S(1)}, u32[]{:S(2)}, u32[]{:S(2)}) %collective-permute-start.14) | collective-permute-done | bytes 262176 | tf_op jit(solution)/shard_map/ppermute | solution.py:103
  65.1 2.0 %collective-permute-start.18 = (bf16[256,512]{1,0:T(8,128)(2,1)S(1)}, bf16[256,512]{1,0:T(8,128)(2,1)S(1)}, u32[]{:S(2)}, u32[]{:S(2)}) collective-permute-start(bf16[256,512]{1,0:T(8,128)(2,1)S(1)} %collective-permute-done.14), channel_id=1, source_target_pairs={{0,4},{4,8},{8,12},{12,14},{14,10},{10,6},{6,2},{2,0},{1,5},{5,9},... | collective-permute-start | bytes 786440 | tf_op jit(solution)/shard_map/ppermute | solution.py:103
  67.2 3.4 %collective-permute-done.16 = bf16[256,512]{1,0:T(8,128)(2,1)S(1)} collective-permute-done((bf16[256,512]{1,0:T(8,128)(2,1)S(1)}, bf16[256,512]{1,0:T(8,128)(2,1)S(1)}, u32[]{:S(2)}, u32[]{:S(2)}) %collective-permute-start.16) | collective-permute-done | bytes 262176 | tf_op jit(solution)/shard_map/ppermute | solution.py:103
  70.7 2.0 %collective-permute-start.20 = (bf16[256,512]{1,0:T(8,128)(2,1)S(1)}, bf16[256,512]{1,0:T(8,128)(2,1)S(1)}, u32[]{:S(2)}, u32[]{:S(2)}) collective-permute-start(bf16[256,512]{1,0:T(8,128)(2,1)S(1)} %collective-permute-done.16), channel_id=1, source_target_pairs={{0,4},{4,8},{8,12},{12,14},{14,10},{10,6},{6,2},{2,0},{1,5},{5,9},... | collective-permute-start | bytes 786440 | tf_op jit(solution)/shard_map/ppermute | solution.py:103
  72.7 3.6 %collective-permute-done.18 = bf16[256,512]{1,0:T(8,128)(2,1)S(1)} collective-permute-done((bf16[256,512]{1,0:T(8,128)(2,1)S(1)}, bf16[256,512]{1,0:T(8,128)(2,1)S(1)}, u32[]{:S(2)}, u32[]{:S(2)}) %collective-permute-start.18) | collective-permute-done | bytes 262176 | tf_op jit(solution)/shard_map/ppermute | solution.py:103
  76.3 2.0 %collective-permute-start.22 = (bf16[256,512]{1,0:T(8,128)(2,1)S(1)}, bf16[256,512]{1,0:T(8,128)(2,1)S(1)}, u32[]{:S(2)}, u32[]{:S(2)}) collective-permute-start(bf16[256,512]{1,0:T(8,128)(2,1)S(1)} %collective-permute-done.18), channel_id=1, source_target_pairs={{0,4},{4,8},{8,12},{12,14},{14,10},{10,6},{6,2},{2,0},{1,5},{5,9},... | collective-permute-start | bytes 786440 | tf_op jit(solution)/shard_map/ppermute | solution.py:103
  78.5 3.4 %collective-permute-done.20 = bf16[256,512]{1,0:T(8,128)(2,1)S(1)} collective-permute-done((bf16[256,512]{1,0:T(8,128)(2,1)S(1)}, bf16[256,512]{1,0:T(8,128)(2,1)S(1)}, u32[]{:S(2)}, u32[]{:S(2)}) %collective-permute-start.20) | collective-permute-done | bytes 262176 | tf_op jit(solution)/shard_map/ppermute | solution.py:103
  81.9 2.0 %collective-permute-start.24 = (bf16[256,512]{1,0:T(8,128)(2,1)S(1)}, bf16[256,512]{1,0:T(8,128)(2,1)S(1)}, u32[]{:S(2)}, u32[]{:S(2)}) collective-permute-start(bf16[256,512]{1,0:T(8,128)(2,1)S(1)} %collective-permute-done.20), channel_id=1, source_target_pairs={{0,4},{4,8},{8,12},{12,14},{14,10},{10,6},{6,2},{2,0},{1,5},{5,9},... | collective-permute-start | bytes 786440 | tf_op jit(solution)/shard_map/ppermute | solution.py:103
  83.9 3.6 %collective-permute-done.22 = bf16[256,512]{1,0:T(8,128)(2,1)S(1)} collective-permute-done((bf16[256,512]{1,0:T(8,128)(2,1)S(1)}, bf16[256,512]{1,0:T(8,128)(2,1)S(1)}, u32[]{:S(2)}, u32[]{:S(2)}) %collective-permute-start.22) | collective-permute-done | bytes 262176 | tf_op jit(solution)/shard_map/ppermute | solution.py:103
  87.5 2.0 %collective-permute-start.26 = (bf16[256,512]{1,0:T(8,128)(2,1)S(1)}, bf16[256,512]{1,0:T(8,128)(2,1)S(1)}, u32[]{:S(2)}, u32[]{:S(2)}) collective-permute-start(bf16[256,512]{1,0:T(8,128)(2,1)S(1)} %collective-permute-done.22), channel_id=1, source_target_pairs={{0,4},{4,8},{8,12},{12,14},{14,10},{10,6},{6,2},{2,0},{1,5},{5,9},... | collective-permute-start | bytes 786440 | tf_op jit(solution)/shard_map/ppermute | solution.py:103
  89.8 3.4 %collective-permute-done.24 = bf16[256,512]{1,0:T(8,128)(2,1)S(1)} collective-permute-done((bf16[256,512]{1,0:T(8,128)(2,1)S(1)}, bf16[256,512]{1,0:T(8,128)(2,1)S(1)}, u32[]{:S(2)}, u32[]{:S(2)}) %collective-permute-start.24) | collective-permute-done | bytes 262176 | tf_op jit(solution)/shard_map/ppermute | solution.py:103
  93.2 2.0 %collective-permute-done.25 = bf16[256,512]{1,0:T(8,128)(2,1)S(1)} collective-permute-done((bf16[256,512]{1,0:T(8,128)(2,1)S(1)}, bf16[256,512]{1,0:T(8,128)(2,1)S(1)}, u32[]{:S(2)}, u32[]{:S(2)}) %collective-permute-start.25) | collective-permute-done | bytes 262176 | tf_op jit(solution)/shard_map/ppermute | solution.py:103
  95.2 1.6 collective-permute-done.26
  96.8 1.4 collective-permute-done.27
  99.4 5.1 %fusion.21 = (f32[256,2048]{1,0:T(8,128)}, bf16[256,2048]{1,0:T(8,128)(2,1)S(1)}) fusion(bf16[2,128,2048]{2,1,0:T(8,128)(2,1)S(1)} %copy-done, bf16[256,2048]{1,0:T(8,128)(2,1)S(1)} %fusion.31, bf16[2048,2048]{1,0:T(8,128)(2,1)S(1)} %constant_dynamic-update-slice_fusion), kind=kOutput, calls=%fused_computation.33 | convolution fusion | flops 2158493696 | bytes 13631488 | tf_op jit(solution)/shard_map/dot_general | solution.py:40
  104.5 1.5 collective-permute-start.28
  106.9 1.1 collective-permute-done.28
  108.7 5.1 %fusion.42 = (f32[256,2048]{1,0:T(8,128)S(1)}, f32[256,2048]{1,0:T(8,128)}) fusion(bf16[256,2048]{1,0:T(8,128)(2,1)S(1)} %collective-permute-done.28, bf16[2048,2048]{1,0:T(8,128)(2,1)S(1)} %constant_dynamic-update-slice_fusion, f32[256]{0:T(256)S(1)} %add_rsqrt_fusion, f32[256]{0:T(256)S(1)} %broadcast_multiply_fusion.4, f32[2048]{0:T(1024)S(1)} %bitcast.90), kind=kOutput, calls=%fused_computation.64 | convolution fusion | flops 2161639424 | bytes 13641728 | tf_op jit(solution)/shard_map/dot_general | solution.py:40
  113.9 1.3 copy-done.1
  116.9 3.3 %collective-permute-done.29 = f32[7]{0:T(128)S(1)} collective-permute-done((f32[7]{0:T(128)S(1)}, f32[7]{0:T(128)S(1)}, u32[]{:S(2)}, u32[]{:S(2)}) %collective-permute-start.29) | collective-permute-done | bytes 60 | tf_op jit(solution)/shard_map/ppermute | solution.py:115
  120.9 1.6 collective-permute-start.30
  122.5 2.0 %collective-permute-done.30 = f32[7]{0:T(128)S(1)} collective-permute-done((f32[7]{0:T(128)S(1)}, f32[7]{0:T(128)S(1)}, u32[]{:S(2)}, u32[]{:S(2)}) %collective-permute-start.30) | collective-permute-done | bytes 60 | tf_op jit(solution)/shard_map/ppermute | solution.py:115
  124.5 2.6 %collective-permute-start.31 = (f32[7]{0:T(128)S(1)}, f32[7]{0:T(128)S(1)}, u32[]{:S(2)}, u32[]{:S(2)}) collective-permute-start(f32[7]{0:T(128)S(1)} %add.388), channel_id=1, source_target_pairs={{0,8},{2,10},{4,12},{6,14},{8,0},{10,2},{12,4},{14,6},{1,9},{3,11}... | collective-permute-start | bytes 92 | tf_op jit(solution)/shard_map/ppermute | solution.py:115
  127.1 1.9 %collective-permute-done.31 = f32[7]{0:T(128)S(1)} collective-permute-done((f32[7]{0:T(128)S(1)}, f32[7]{0:T(128)S(1)}, u32[]{:S(2)}, u32[]{:S(2)}) %collective-permute-start.31) | collective-permute-done | bytes 60 | tf_op jit(solution)/shard_map/ppermute | solution.py:115
  130.9 1.4 fusion.62
  133.8 5.9 %fusion.39 = (f32[128,2048]{1,0:T(8,128)S(1)}, f32[128,2048]{1,0:T(8,128)S(1)}) fusion(bf16[128,2048]{1,0:T(8,128)(2,1)S(1)} %copy-done.3, f32[256,2048]{1,0:T(8,128)} %copy-done.1, f32[]{:T(128)} %bitcast.45, f32[]{:T(128)} %bitcast.44, f32[]{:T(128)} %bitcast.43, f32[]{:T(128)} %bitcast.48, f32[]{:T(128)} %bitcast.47, f32[]{:T(128)} %bitcast.46), kind=kLoop, calls=%fused_computation.61 | loop fusion | flops 2883584 | bytes 4718616 | tf_op jit(solution)/shard_map/add | solution.py:166
  139.7 6.1 %fusion.60 = (f32[256]{0:T(256)S(1)}, f32[256]{0:T(256)S(1)}, f32[256,2048]{1,0:T(8,128)S(1)}) fusion(f32[256]{0:T(256)S(1)} %add_rsqrt_fusion, f32[256]{0:T(256)S(1)} %broadcast_multiply_fusion.4, bf16[256,2048]{1,0:T(8,128)(2,1)S(1)} %collective-permute-done.28, f32[2048]{0:T(1024)S(1)} %bitcast.91, bf16[2048,2048]{1,0:T(8,128)(2,1)} %copy-done.2, ...), kind=kOutput, calls=%fused_computation.129 | convolution fusion | flops 2152726016 | bytes 15740928 | tf_op jit(solution)/shard_map/dot_general | solution.py:47
  146.6 1.3 collective-permute-start.32
  149.2 1.5 collective-permute-start.33
  150.7 1.7 %collective-permute-done.33 = f32[1]{0:T(128)} collective-permute-done((f32[1]{0:T(128)}, f32[1]{0:T(128)}, u32[]{:S(2)}, u32[]{:S(2)}) %collective-permute-start.33) | collective-permute-done | bytes 36 | tf_op jit(solution)/shard_map/ppermute | solution.py:18
  153.1 6.7 %fusion.59 = (f32[256]{0:T(256)S(1)}, f32[256]{0:T(256)S(1)}, f32[256,2048]{1,0:T(8,128)S(1)}) fusion(f32[256]{0:T(256)S(1)} %rsqrt_bitcast_fusion, f32[256]{0:T(256)S(1)} %get-tuple-element.41, bf16[2,128,2048]{2,1,0:T(8,128)(2,1)S(1)} %copy-done, f32[2048]{0:T(1024)S(1)} %bitcast.92, bf16[2048,2048]{1,0:T(8,128)(2,1)} %copy-done.2, ...), kind=kOutput, calls=%fused_computation.128 | convolution fusion | flops 2152726016 | bytes 14692352 | tf_op jit(solution)/shard_map/dot_general | solution.py:47
  159.8 2.0 %fusion.43 = bf16[256,2048]{1,0:T(8,128)(2,1)} fusion(bf16[256,2048]{1,0:T(8,128)(2,1)S(1)} %fusion.10, bf16[2,128,2048]{2,1,0:T(8,128)(2,1)S(1)} %copy-done, f32[256,2048]{1,0:T(8,128)S(1)} %get-tuple-element.60, bf16[256,2048]{1,0:T(8,128)(2,1)S(1)} %collective-permute-done.32, f32[256]{0:T(256)S(1)} %broadcast_multiply_fusion, ...), kind=kLoop, calls=%fused_computation.65 | loop fusion | flops 5767168 | bytes 6295553 | tf_op jit(solution)/shard_map/jit(_where)/select_n | solution.py:173
  (110 shorter events, 11.7 us)
Async XLA Ops:
  0.6 6.4 %copy-start.7 = (s32[8]{0:T(128)S(1)}, s32[8]{0:T(128)}, u32[]{:S(2)}) copy-start(s32[8]{0:T(128)} %constant.197.clone) | copy-start | bytes 100
  0.6 16.3 %copy-start.5 = (s32[8]{0:T(128)S(1)}, s32[8]{0:T(128)}, u32[]{:S(2)}) copy-start(s32[8]{0:T(128)} %constant.198.clone) | copy-start | bytes 100
  1.9 25.8 %collective-permute-start = (bf16[256,512]{1,0:T(8,128)(2,1)S(1)}, bf16[256,512]{1,0:T(8,128)(2,1)S(1)}, u32[]{:S(2)}, u32[]{:S(2)}) collective-permute-start(bf16[256,512]{1,0:T(8,128)(2,1)S(1)} %get-tuple-element.36), channel_id=1, source_target_pairs={{0,4},{4,8},{8,12},{12,14},{14,10},{10,6},{6,2},{2,0},{1,5},{5,9},... | collective-permute-start | bytes 786440 | tf_op jit(solution)/shard_map/ppermute | solution.py:103
  5.0 24.8 %collective-permute-start.1 = (bf16[256,512]{1,0:T(8,128)(2,1)S(1)}, bf16[256,512]{1,0:T(8,128)(2,1)S(1)}, u32[]{:S(2)}, u32[]{:S(2)}) collective-permute-start(bf16[256,512]{1,0:T(8,128)(2,1)S(1)} %get-tuple-element.35), channel_id=1, source_target_pairs={{4,0},{8,4},{12,8},{14,12},{10,14},{6,10},{2,6},{0,2},{5,1},{9,5},... | collective-permute-start | bytes 786440 | tf_op jit(solution)/shard_map/ppermute | solution.py:103
  5.0 24.8 %collective-permute-start.2 = (bf16[256,512]{1,0:T(8,128)(2,1)S(1)}, bf16[256,512]{1,0:T(8,128)(2,1)S(1)}, u32[]{:S(2)}, u32[]{:S(2)}) collective-permute-start(bf16[256,512]{1,0:T(8,128)(2,1)S(1)} %get-tuple-element.34), channel_id=1, source_target_pairs={{0,4},{4,8},{8,12},{12,14},{14,10},{10,6},{6,2},{2,0},{1,5},{5,9},... | collective-permute-start | bytes 786440 | tf_op jit(solution)/shard_map/ppermute | solution.py:103
  7.1 24.8 %collective-permute-start.3 = (bf16[256,512]{1,0:T(8,128)(2,1)S(1)}, bf16[256,512]{1,0:T(8,128)(2,1)S(1)}, u32[]{:S(2)}, u32[]{:S(2)}) collective-permute-start(bf16[256,512]{1,0:T(8,128)(2,1)S(1)} %get-tuple-element.33), channel_id=1, source_target_pairs={{4,0},{8,4},{12,8},{14,12},{10,14},{6,10},{2,6},{0,2},{5,1},{9,5},... | collective-permute-start | bytes 786440 | tf_op jit(solution)/shard_map/ppermute | solution.py:103
  26.4 1.2 copy-start.4
  27.7 9.2 %collective-permute-start.4 = (bf16[256,512]{1,0:T(8,128)(2,1)S(1)}, bf16[256,512]{1,0:T(8,128)(2,1)S(1)}, u32[]{:S(2)}, u32[]{:S(2)}) collective-permute-start(bf16[256,512]{1,0:T(8,128)(2,1)S(1)} %collective-permute-done), channel_id=1, source_target_pairs={{0,4},{4,8},{8,12},{12,14},{14,10},{10,6},{6,2},{2,0},{1,5},{5,9},... | collective-permute-start | bytes 786440 | tf_op jit(solution)/shard_map/ppermute | solution.py:103
  29.8 9.2 %collective-permute-start.5 = (bf16[256,512]{1,0:T(8,128)(2,1)S(1)}, bf16[256,512]{1,0:T(8,128)(2,1)S(1)}, u32[]{:S(2)}, u32[]{:S(2)}) collective-permute-start(bf16[256,512]{1,0:T(8,128)(2,1)S(1)} %collective-permute-done.1), channel_id=1, source_target_pairs={{4,0},{8,4},{12,8},{14,12},{10,14},{6,10},{2,6},{0,2},{5,1},{9,5},... | collective-permute-start | bytes 786440 | tf_op jit(solution)/shard_map/ppermute | solution.py:103
  29.8 12.8 %collective-permute-start.6 = (bf16[256,512]{1,0:T(8,128)(2,1)S(1)}, bf16[256,512]{1,0:T(8,128)(2,1)S(1)}, u32[]{:S(2)}, u32[]{:S(2)}) collective-permute-start(bf16[256,512]{1,0:T(8,128)(2,1)S(1)} %collective-permute-done.2), channel_id=1, source_target_pairs={{0,4},{4,8},{8,12},{12,14},{14,10},{10,6},{6,2},{2,0},{1,5},{5,9},... | collective-permute-start | bytes 786440 | tf_op jit(solution)/shard_map/ppermute | solution.py:103
  31.8 12.8 %collective-permute-start.7 = (bf16[256,512]{1,0:T(8,128)(2,1)S(1)}, bf16[256,512]{1,0:T(8,128)(2,1)S(1)}, u32[]{:S(2)}, u32[]{:S(2)}) collective-permute-start(bf16[256,512]{1,0:T(8,128)(2,1)S(1)} %collective-permute-done.3), channel_id=1, source_target_pairs={{4,0},{8,4},{12,8},{14,12},{10,14},{6,10},{2,6},{0,2},{5,1},{9,5},... | collective-permute-start | bytes 786440 | tf_op jit(solution)/shard_map/ppermute | solution.py:103
  37.0 11.2 %collective-permute-start.8 = (bf16[256,512]{1,0:T(8,128)(2,1)S(1)}, bf16[256,512]{1,0:T(8,128)(2,1)S(1)}, u32[]{:S(2)}, u32[]{:S(2)}) collective-permute-start(bf16[256,512]{1,0:T(8,128)(2,1)S(1)} %collective-permute-done.4), channel_id=1, source_target_pairs={{0,4},{4,8},{8,12},{12,14},{14,10},{10,6},{6,2},{2,0},{1,5},{5,9},... | collective-permute-start | bytes 786440 | tf_op jit(solution)/shard_map/ppermute | solution.py:103
  39.0 11.2 %collective-permute-start.9 = (bf16[256,512]{1,0:T(8,128)(2,1)S(1)}, bf16[256,512]{1,0:T(8,128)(2,1)S(1)}, u32[]{:S(2)}, u32[]{:S(2)}) collective-permute-start(bf16[256,512]{1,0:T(8,128)(2,1)S(1)} %collective-permute-done.5), channel_id=1, source_target_pairs={{4,0},{8,4},{12,8},{14,12},{10,14},{6,10},{2,6},{0,2},{5,1},{9,5},... | collective-permute-start | bytes 786440 | tf_op jit(solution)/shard_map/ppermute | solution.py:103
  42.6 11.2 %collective-permute-start.10 = (bf16[256,512]{1,0:T(8,128)(2,1)S(1)}, bf16[256,512]{1,0:T(8,128)(2,1)S(1)}, u32[]{:S(2)}, u32[]{:S(2)}) collective-permute-start(bf16[256,512]{1,0:T(8,128)(2,1)S(1)} %collective-permute-done.6), channel_id=1, source_target_pairs={{0,4},{4,8},{8,12},{12,14},{14,10},{10,6},{6,2},{2,0},{1,5},{5,9},... | collective-permute-start | bytes 786440 | tf_op jit(solution)/shard_map/ppermute | solution.py:103
  44.6 11.2 %collective-permute-start.11 = (bf16[256,512]{1,0:T(8,128)(2,1)S(1)}, bf16[256,512]{1,0:T(8,128)(2,1)S(1)}, u32[]{:S(2)}, u32[]{:S(2)}) collective-permute-start(bf16[256,512]{1,0:T(8,128)(2,1)S(1)} %collective-permute-done.7), channel_id=1, source_target_pairs={{4,0},{8,4},{12,8},{14,12},{10,14},{6,10},{2,6},{0,2},{5,1},{9,5},... | collective-permute-start | bytes 786440 | tf_op jit(solution)/shard_map/ppermute | solution.py:103
  48.2 11.2 %collective-permute-start.12 = (bf16[256,512]{1,0:T(8,128)(2,1)S(1)}, bf16[256,512]{1,0:T(8,128)(2,1)S(1)}, u32[]{:S(2)}, u32[]{:S(2)}) collective-permute-start(bf16[256,512]{1,0:T(8,128)(2,1)S(1)} %collective-permute-done.8), channel_id=1, source_target_pairs={{0,4},{4,8},{8,12},{12,14},{14,10},{10,6},{6,2},{2,0},{1,5},{5,9},... | collective-permute-start | bytes 786440 | tf_op jit(solution)/shard_map/ppermute | solution.py:103
  50.2 11.2 %collective-permute-start.13 = (bf16[256,512]{1,0:T(8,128)(2,1)S(1)}, bf16[256,512]{1,0:T(8,128)(2,1)S(1)}, u32[]{:S(2)}, u32[]{:S(2)}) collective-permute-start(bf16[256,512]{1,0:T(8,128)(2,1)S(1)} %collective-permute-done.9), channel_id=1, source_target_pairs={{4,0},{8,4},{12,8},{14,12},{10,14},{6,10},{2,6},{0,2},{5,1},{9,5},... | collective-permute-start | bytes 786440 | tf_op jit(solution)/shard_map/ppermute | solution.py:103
  53.8 11.2 %collective-permute-start.14 = (bf16[256,512]{1,0:T(8,128)(2,1)S(1)}, bf16[256,512]{1,0:T(8,128)(2,1)S(1)}, u32[]{:S(2)}, u32[]{:S(2)}) collective-permute-start(bf16[256,512]{1,0:T(8,128)(2,1)S(1)} %collective-permute-done.10), channel_id=1, source_target_pairs={{0,4},{4,8},{8,12},{12,14},{14,10},{10,6},{6,2},{2,0},{1,5},{5,9},... | collective-permute-start | bytes 786440 | tf_op jit(solution)/shard_map/ppermute | solution.py:103
  55.8 11.2 %collective-permute-start.15 = (bf16[256,512]{1,0:T(8,128)(2,1)S(1)}, bf16[256,512]{1,0:T(8,128)(2,1)S(1)}, u32[]{:S(2)}, u32[]{:S(2)}) collective-permute-start(bf16[256,512]{1,0:T(8,128)(2,1)S(1)} %collective-permute-done.11), channel_id=1, source_target_pairs={{4,0},{8,4},{12,8},{14,12},{10,14},{6,10},{2,6},{0,2},{5,1},{9,5},... | collective-permute-start | bytes 786440 | tf_op jit(solution)/shard_map/ppermute | solution.py:103
  59.4 11.2 %collective-permute-start.16 = (bf16[256,512]{1,0:T(8,128)(2,1)S(1)}, bf16[256,512]{1,0:T(8,128)(2,1)S(1)}, u32[]{:S(2)}, u32[]{:S(2)}) collective-permute-start(bf16[256,512]{1,0:T(8,128)(2,1)S(1)} %collective-permute-done.12), channel_id=1, source_target_pairs={{0,4},{4,8},{8,12},{12,14},{14,10},{10,6},{6,2},{2,0},{1,5},{5,9},... | collective-permute-start | bytes 786440 | tf_op jit(solution)/shard_map/ppermute | solution.py:103
  61.5 11.2 %collective-permute-start.17 = (bf16[256,512]{1,0:T(8,128)(2,1)S(1)}, bf16[256,512]{1,0:T(8,128)(2,1)S(1)}, u32[]{:S(2)}, u32[]{:S(2)}) collective-permute-start(bf16[256,512]{1,0:T(8,128)(2,1)S(1)} %collective-permute-done.13), channel_id=1, source_target_pairs={{4,0},{8,4},{12,8},{14,12},{10,14},{6,10},{2,6},{0,2},{5,1},{9,5},... | collective-permute-start | bytes 786440 | tf_op jit(solution)/shard_map/ppermute | solution.py:103
  65.1 11.2 %collective-permute-start.18 = (bf16[256,512]{1,0:T(8,128)(2,1)S(1)}, bf16[256,512]{1,0:T(8,128)(2,1)S(1)}, u32[]{:S(2)}, u32[]{:S(2)}) collective-permute-start(bf16[256,512]{1,0:T(8,128)(2,1)S(1)} %collective-permute-done.14), channel_id=1, source_target_pairs={{0,4},{4,8},{8,12},{12,14},{14,10},{10,6},{6,2},{2,0},{1,5},{5,9},... | collective-permute-start | bytes 786440 | tf_op jit(solution)/shard_map/ppermute | solution.py:103
  67.1 11.2 %collective-permute-start.19 = (bf16[256,512]{1,0:T(8,128)(2,1)S(1)}, bf16[256,512]{1,0:T(8,128)(2,1)S(1)}, u32[]{:S(2)}, u32[]{:S(2)}) collective-permute-start(bf16[256,512]{1,0:T(8,128)(2,1)S(1)} %collective-permute-done.15), channel_id=1, source_target_pairs={{4,0},{8,4},{12,8},{14,12},{10,14},{6,10},{2,6},{0,2},{5,1},{9,5},... | collective-permute-start | bytes 786440 | tf_op jit(solution)/shard_map/ppermute | solution.py:103
  70.7 11.2 %collective-permute-start.20 = (bf16[256,512]{1,0:T(8,128)(2,1)S(1)}, bf16[256,512]{1,0:T(8,128)(2,1)S(1)}, u32[]{:S(2)}, u32[]{:S(2)}) collective-permute-start(bf16[256,512]{1,0:T(8,128)(2,1)S(1)} %collective-permute-done.16), channel_id=1, source_target_pairs={{0,4},{4,8},{8,12},{12,14},{14,10},{10,6},{6,2},{2,0},{1,5},{5,9},... | collective-permute-start | bytes 786440 | tf_op jit(solution)/shard_map/ppermute | solution.py:103
  72.7 11.2 %collective-permute-start.21 = (bf16[256,512]{1,0:T(8,128)(2,1)S(1)}, bf16[256,512]{1,0:T(8,128)(2,1)S(1)}, u32[]{:S(2)}, u32[]{:S(2)}) collective-permute-start(bf16[256,512]{1,0:T(8,128)(2,1)S(1)} %collective-permute-done.17), channel_id=1, source_target_pairs={{4,0},{8,4},{12,8},{14,12},{10,14},{6,10},{2,6},{0,2},{5,1},{9,5},... | collective-permute-start | bytes 786440 | tf_op jit(solution)/shard_map/ppermute | solution.py:103
  76.3 11.2 %collective-permute-start.22 = (bf16[256,512]{1,0:T(8,128)(2,1)S(1)}, bf16[256,512]{1,0:T(8,128)(2,1)S(1)}, u32[]{:S(2)}, u32[]{:S(2)}) collective-permute-start(bf16[256,512]{1,0:T(8,128)(2,1)S(1)} %collective-permute-done.18), channel_id=1, source_target_pairs={{0,4},{4,8},{8,12},{12,14},{14,10},{10,6},{6,2},{2,0},{1,5},{5,9},... | collective-permute-start | bytes 786440 | tf_op jit(solution)/shard_map/ppermute | solution.py:103
  78.3 11.3 %collective-permute-start.23 = (bf16[256,512]{1,0:T(8,128)(2,1)S(1)}, bf16[256,512]{1,0:T(8,128)(2,1)S(1)}, u32[]{:S(2)}, u32[]{:S(2)}) collective-permute-start(bf16[256,512]{1,0:T(8,128)(2,1)S(1)} %collective-permute-done.19), channel_id=1, source_target_pairs={{4,0},{8,4},{12,8},{14,12},{10,14},{6,10},{2,6},{0,2},{5,1},{9,5},... | collective-permute-start | bytes 786440 | tf_op jit(solution)/shard_map/ppermute | solution.py:103
  78.5 19.8 %copy-start = (bf16[2,128,2048]{2,1,0:T(8,128)(2,1)S(1)}, bf16[2,128,2048]{2,1,0:T(8,128)(2,1)}, u32[]{:S(2)}) copy-start(bf16[2,128,2048]{2,1,0:T(8,128)(2,1)} %param.6) | copy-start | bytes 3145732
  81.9 11.2 %collective-permute-start.24 = (bf16[256,512]{1,0:T(8,128)(2,1)S(1)}, bf16[256,512]{1,0:T(8,128)(2,1)S(1)}, u32[]{:S(2)}, u32[]{:S(2)}) collective-permute-start(bf16[256,512]{1,0:T(8,128)(2,1)S(1)} %collective-permute-done.20), channel_id=1, source_target_pairs={{0,4},{4,8},{8,12},{12,14},{14,10},{10,6},{6,2},{2,0},{1,5},{5,9},... | collective-permute-start | bytes 786440 | tf_op jit(solution)/shard_map/ppermute | solution.py:103
  83.9 11.2 %collective-permute-start.25 = (bf16[256,512]{1,0:T(8,128)(2,1)S(1)}, bf16[256,512]{1,0:T(8,128)(2,1)S(1)}, u32[]{:S(2)}, u32[]{:S(2)}) collective-permute-start(bf16[256,512]{1,0:T(8,128)(2,1)S(1)} %collective-permute-done.21), channel_id=1, source_target_pairs={{4,0},{8,4},{12,8},{14,12},{10,14},{6,10},{2,6},{0,2},{5,1},{9,5},... | collective-permute-start | bytes 786440 | tf_op jit(solution)/shard_map/ppermute | solution.py:103
  87.5 9.3 %collective-permute-start.26 = (bf16[256,512]{1,0:T(8,128)(2,1)S(1)}, bf16[256,512]{1,0:T(8,128)(2,1)S(1)}, u32[]{:S(2)}, u32[]{:S(2)}) collective-permute-start(bf16[256,512]{1,0:T(8,128)(2,1)S(1)} %collective-permute-done.22), channel_id=1, source_target_pairs={{0,4},{4,8},{8,12},{12,14},{14,10},{10,6},{6,2},{2,0},{1,5},{5,9},... | collective-permute-start | bytes 786440 | tf_op jit(solution)/shard_map/ppermute | solution.py:103
  89.7 8.6 %collective-permute-start.27 = (bf16[256,512]{1,0:T(8,128)(2,1)S(1)}, bf16[256,512]{1,0:T(8,128)(2,1)S(1)}, u32[]{:S(2)}, u32[]{:S(2)}) collective-permute-start(bf16[256,512]{1,0:T(8,128)(2,1)S(1)} %collective-permute-done.23), channel_id=1, source_target_pairs={{4,0},{8,4},{12,8},{14,12},{10,14},{6,10},{2,6},{0,2},{5,1},{9,5},... | collective-permute-start | bytes 786440 | tf_op jit(solution)/shard_map/ppermute | solution.py:103
  89.8 9.2 %copy-start.6 = (f32[1,2048]{1,0:T(1,128)S(1)}, f32[1,2048]{1,0:T(1,128)}, u32[]{:S(2)}) copy-start(f32[1,2048]{1,0:T(1,128)} %param.9) | copy-start | bytes 24580
  98.3 10.4 %copy-start.2 = (bf16[2048,2048]{1,0:T(8,128)(2,1)}, bf16[2048,2048]{1,0:T(8,128)(2,1)S(1)}, u32[]{:S(2)}) copy-start(bf16[2048,2048]{1,0:T(8,128)(2,1)S(1)} %constant_dynamic-update-slice_fusion) | copy-start | bytes 25165828
  99.4 6.7 %copy-start.3 = (bf16[128,2048]{1,0:T(8,128)(2,1)S(1)}, bf16[128,2048]{1,0:T(8,128)(2,1)}, u32[]{:S(2)}) copy-start(bf16[128,2048]{1,0:T(8,128)(2,1)} %param.7) | copy-start | bytes 1572868
  104.5 3.6 %collective-permute-start.28 = (bf16[256,2048]{1,0:T(8,128)(2,1)S(1)}, bf16[256,2048]{1,0:T(8,128)(2,1)S(1)}, u32[]{:S(2)}, u32[]{:S(2)}) collective-permute-start(bf16[256,2048]{1,0:T(8,128)(2,1)S(1)} %get-tuple-element.32), channel_id=1, source_target_pairs={{0,1},{2,3},{4,5},{6,7},{8,9},{10,11},{12,13},{14,15},{16,17},{18,... | collective-permute-start | bytes 3145736 | tf_op jit(solution)/shard_map/ppermute | solution.py:18
  113.9 1.3 copy-start.1
  116.6 3.6 %collective-permute-start.29 = (f32[7]{0:T(128)S(1)}, f32[7]{0:T(128)S(1)}, u32[]{:S(2)}, u32[]{:S(2)}) collective-permute-start(f32[7]{0:T(128)S(1)} %pad_maximum_fusion.1), channel_id=1, source_target_pairs={{0,2},{2,0},{4,6},{6,4},{8,10},{10,8},{12,14},{14,12},{1,3},{3,1},... | collective-permute-start | bytes 92 | tf_op jit(solution)/shard_map/ppermute | solution.py:115
  120.9 3.6 %collective-permute-start.30 = (f32[7]{0:T(128)S(1)}, f32[7]{0:T(128)S(1)}, u32[]{:S(2)}, u32[]{:S(2)}) collective-permute-start(f32[7]{0:T(128)S(1)} %fusion.75), channel_id=1, source_target_pairs={{0,4},{2,6},{4,0},{6,2},{8,12},{10,14},{12,8},{14,10},{1,5},{3,7},... | collective-permute-start | bytes 92 | tf_op jit(solution)/shard_map/ppermute | solution.py:115
  124.5 4.5 %collective-permute-start.31 = (f32[7]{0:T(128)S(1)}, f32[7]{0:T(128)S(1)}, u32[]{:S(2)}, u32[]{:S(2)}) collective-permute-start(f32[7]{0:T(128)S(1)} %add.388), channel_id=1, source_target_pairs={{0,8},{2,10},{4,12},{6,14},{8,0},{10,2},{12,4},{14,6},{1,9},{3,11}... | collective-permute-start | bytes 92 | tf_op jit(solution)/shard_map/ppermute | solution.py:115
  133.8 5.9 %copy-start.8 = (f32[256,2048]{1,0:T(8,128)S(1)}, f32[256,2048]{1,0:T(8,128)}, u32[]{:S(2)}) copy-start(f32[256,2048]{1,0:T(8,128)} %get-tuple-element.8) | copy-start | bytes 6291460
  146.6 6.4 %collective-permute-start.32 = (bf16[256,2048]{1,0:T(8,128)(2,1)S(1)}, bf16[256,2048]{1,0:T(8,128)(2,1)S(1)}, u32[]{:S(2)}, u32[]{:S(2)}) collective-permute-start(bf16[256,2048]{1,0:T(8,128)(2,1)S(1)} %fusion.10), channel_id=1, source_target_pairs={{1,0},{3,2},{5,4},{7,6},{9,8},{11,10},{13,12},{15,14},{17,16},{19,... | collective-permute-start | bytes 3145736 | tf_op jit(solution)/shard_map/ppermute | solution.py:18
  149.2 3.3 %collective-permute-start.33 = (f32[1]{0:T(128)}, f32[1]{0:T(128)}, u32[]{:S(2)}, u32[]{:S(2)}) collective-permute-start(f32[1]{0:T(128)} %bitcast.51), channel_id=1, source_target_pairs={{1,0},{3,2},{5,4},{7,6},{9,8},{11,10},{13,12},{15,14},{17,16},{19,... | collective-permute-start | bytes 20 | tf_op jit(solution)/shard_map/ppermute | solution.py:18

commit v5 on v4

--- a/solution.py
+++ b/solution.py
@@ -80,30 +80,31 @@
 def ring_gather(local, axis, pieces=2):
     n = lax.axis_size(axis)
     rows, cols = local.shape
-    if n == 1:
-        return local
+    if n == 1 or n % 2:
+        return lax.all_gather(local, axis, axis=0, tiled=True)
     ring = snake_ring(n)
-    pos_of = [0] * n
-    for p, t in enumerate(ring):
-        pos_of[t] = p
     me = lax.axis_index(axis)
-    my_pos = jnp.asarray(pos_of, jnp.int32)[me]
-    ring_arr = jnp.asarray(ring, jnp.int32)
+    my_pos = jnp.where(me % 2 == 0, me // 2, n - (me + 1) // 2)
+
+    def tok_at(p):
+        p = p % n
+        return jnp.where(p < n // 2, 2 * p, 2 * (n - 1 - p) + 1)
+
     cw = [(ring[i], ring[(i + 1) % n]) for i in range(n)]
     ccw = [(ring[(i + 1) % n], ring[i]) for i in range(n)]
     width = cols // (2 * pieces)
     parts = [local[:, j * width:(j + 1) * width] for j in range(2 * pieces)]
     full = jnp.zeros((n * rows, cols), local.dtype)
-    full = lax.dynamic_update_slice(full, local, (me * rows, 0))
     for k in range(1, n):
-        from_cw = ring_arr[(my_pos - k) % n]
-        from_ccw = ring_arr[(my_pos + k) % n]
+        from_cw = tok_at(my_pos - k + n)
+        from_ccw = tok_at(my_pos + k)
         for j in range(2 * pieces):
             clockwise = j % 2 == 0
             parts[j] = lax.ppermute(parts[j], axis, cw if clockwise else ccw)
             origin = from_cw if clockwise else from_ccw
             full = lax.dynamic_update_slice(full, parts[j], (origin * rows, j * width))
-    return full
+    full, local = lax.optimization_barrier((full, local))
+    return lax.dynamic_update_slice(full, local, (me * rows, 0))
 
 
 def tree_sum(v, axis):

time: 164 us -> 151 us (0.921)
  between operations: 22.2 us -> 4.28 us
  waiting for transfers between devices: 55.1 us -> 61.1 us
    ppermute x28, waiting for transfers between devices: 45.1 us -> 51.1 us  [ring_gather(): parts[j] = lax.ppermute(parts[j], axis, cw if clockwise else ccw)]
  transfers between devices with their start and end apart: 34 -> 34, of which waited for: 19 -> 21; matrix products, arithmetic and copies ran while one was open for 2% -> 2% of each run, Pallas kernels for 0% -> 0%
where the time goes in v5:
time: 151 us
  waiting for transfers between devices  61.1 us (40%)
  starting transfers between devices  39.5 us (26%)
  matrix products  23 us (15%)
  other arithmetic  15.7 us (10%)
  local copies, waits for them, and re-layouts  7.15 us (5%)
  between operations  4.28 us (3%)
    ppermute x28, waiting for transfers between devices, ring_gather(): parts[j] = lax.ppermute(parts[j], axis, cw if clockwise else ccw)  51.1 us
    ppermute x28, starting transfers between devices, ring_gather(): parts[j] = lax.ppermute(parts[j], axis, cw if clockwise else ccw)  30.7 us
    dot_general x2, matrix products, section_backward(): lax.dot_general(grad_pre, weight, (((1,), (1,)), ((), ())), preferred_ele...  12.8 us
    dot_general x2, matrix products, section_forward(): pre_act = jnp.dot(normed, weight, preferred_element_type=jnp.float32)  10.2 us
    ppermute x3, waiting for transfers between devices, tree_sum(): v = v + lax.ppermute(v, axis, [(i, i ^ b) for i in range(n)])  7.16 us
    add x1, other arithmetic, per_device(): c = c + member_coeff[m, k] * y[k]  5.93 us
    ppermute x3, starting transfers between devices, tree_sum(): v = v + lax.ppermute(v, axis, [(i, i ^ b) for i in range(n)])  4.45 us
    ppermute x3, starting transfers between devices, shifted(): return lax.ppermute(x, axis, pairs)  4.33 us
  transfers between devices with their start and end apart: 34, of which 21 were waited for; matrix products, arithmetic and copies ran while one was open for 2% of the time, Pallas kernels for 0%

profile of v5, /device:TPU:0, one launch (start us, length us, event | category | flops | bytes accessed | tf_op | source)
XLA Modules:
  0.0 150.7 jit_solution(15237090703075337826)
XLA Ops:
  0.6 1.3 fusion.66
  1.9 3.1 %collective-permute-start = (bf16[256,512]{1,0:T(8,128)(2,1)S(1)}, bf16[256,512]{1,0:T(8,128)(2,1)S(1)}, u32[]{:S(2)}, u32[]{:S(2)}) collective-permute-start(bf16[256,512]{1,0:T(8,128)(2,1)S(1)} %get-tuple-element.40), channel_id=1, source_target_pairs={{0,4},{4,8},{8,12},{12,14},{14,10},{10,6},{6,2},{2,0},{1,5},{5,9},... | collective-permute-start | bytes 786440 | tf_op jit(solution)/shard_map/ppermute | solution.py:103
  5.0 2.0 %collective-permute-start.2 = (bf16[256,512]{1,0:T(8,128)(2,1)S(1)}, bf16[256,512]{1,0:T(8,128)(2,1)S(1)}, u32[]{:S(2)}, u32[]{:S(2)}) collective-permute-start(bf16[256,512]{1,0:T(8,128)(2,1)S(1)} %get-tuple-element.38), channel_id=1, source_target_pairs={{0,4},{4,8},{8,12},{12,14},{14,10},{10,6},{6,2},{2,0},{1,5},{5,9},... | collective-permute-start | bytes 786440 | tf_op jit(solution)/shard_map/ppermute | solution.py:103
  7.0 5.0 %collective-permute-done = bf16[256,512]{1,0:T(8,128)(2,1)S(1)} collective-permute-done((bf16[256,512]{1,0:T(8,128)(2,1)S(1)}, bf16[256,512]{1,0:T(8,128)(2,1)S(1)}, u32[]{:S(2)}, u32[]{:S(2)}) %collective-permute-start) | collective-permute-done | bytes 262176 | tf_op jit(solution)/shard_map/ppermute | solution.py:103
  12.1 2.1 %collective-permute-start.4 = (bf16[256,512]{1,0:T(8,128)(2,1)S(1)}, bf16[256,512]{1,0:T(8,128)(2,1)S(1)}, u32[]{:S(2)}, u32[]{:S(2)}) collective-permute-start(bf16[256,512]{1,0:T(8,128)(2,1)S(1)} %collective-permute-done), channel_id=1, source_target_pairs={{0,4},{4,8},{8,12},{12,14},{14,10},{10,6},{6,2},{2,0},{1,5},{5,9},... | collective-permute-start | bytes 786440 | tf_op jit(solution)/shard_map/ppermute | solution.py:103
  14.2 3.5 %collective-permute-done.2 = bf16[256,512]{1,0:T(8,128)(2,1)S(1)} collective-permute-done((bf16[256,512]{1,0:T(8,128)(2,1)S(1)}, bf16[256,512]{1,0:T(8,128)(2,1)S(1)}, u32[]{:S(2)}, u32[]{:S(2)}) %collective-permute-start.2) | collective-permute-done | bytes 262176 | tf_op jit(solution)/shard_map/ppermute | solution.py:103
  17.7 2.1 %collective-permute-start.6 = (bf16[256,512]{1,0:T(8,128)(2,1)S(1)}, bf16[256,512]{1,0:T(8,128)(2,1)S(1)}, u32[]{:S(2)}, u32[]{:S(2)}) collective-permute-start(bf16[256,512]{1,0:T(8,128)(2,1)S(1)} %collective-permute-done.2), channel_id=1, source_target_pairs={{0,4},{4,8},{8,12},{12,14},{14,10},{10,6},{6,2},{2,0},{1,5},{5,9},... | collective-permute-start | bytes 786440 | tf_op jit(solution)/shard_map/ppermute | solution.py:103
  21.0 2.3 %collective-permute-done.4 = bf16[256,512]{1,0:T(8,128)(2,1)S(1)} collective-permute-done((bf16[256,512]{1,0:T(8,128)(2,1)S(1)}, bf16[256,512]{1,0:T(8,128)(2,1)S(1)}, u32[]{:S(2)}, u32[]{:S(2)}) %collective-permute-start.4) | collective-permute-done | bytes 262176 | tf_op jit(solution)/shard_map/ppermute | solution.py:103
  23.3 2.1 %collective-permute-start.8 = (bf16[256,512]{1,0:T(8,128)(2,1)S(1)}, bf16[256,512]{1,0:T(8,128)(2,1)S(1)}, u32[]{:S(2)}, u32[]{:S(2)}) collective-permute-start(bf16[256,512]{1,0:T(8,128)(2,1)S(1)} %collective-permute-done.4), channel_id=1, source_target_pairs={{0,4},{4,8},{8,12},{12,14},{14,10},{10,6},{6,2},{2,0},{1,5},{5,9},... | collective-permute-start | bytes 786440 | tf_op jit(solution)/shard_map/ppermute | solution.py:103
  25.4 3.5 %collective-permute-done.6 = bf16[256,512]{1,0:T(8,128)(2,1)S(1)} collective-permute-done((bf16[256,512]{1,0:T(8,128)(2,1)S(1)}, bf16[256,512]{1,0:T(8,128)(2,1)S(1)}, u32[]{:S(2)}, u32[]{:S(2)}) %collective-permute-start.6) | collective-permute-done | bytes 262176 | tf_op jit(solution)/shard_map/ppermute | solution.py:103
  28.9 2.1 %collective-permute-start.10 = (bf16[256,512]{1,0:T(8,128)(2,1)S(1)}, bf16[256,512]{1,0:T(8,128)(2,1)S(1)}, u32[]{:S(2)}, u32[]{:S(2)}) collective-permute-start(bf16[256,512]{1,0:T(8,128)(2,1)S(1)} %collective-permute-done.6), channel_id=1, source_target_pairs={{0,4},{4,8},{8,12},{12,14},{14,10},{10,6},{6,2},{2,0},{1,5},{5,9},... | collective-permute-start | bytes 786440 | tf_op jit(solution)/shard_map/ppermute | solution.py:103
  31.2 3.4 %collective-permute-done.8 = bf16[256,512]{1,0:T(8,128)(2,1)S(1)} collective-permute-done((bf16[256,512]{1,0:T(8,128)(2,1)S(1)}, bf16[256,512]{1,0:T(8,128)(2,1)S(1)}, u32[]{:S(2)}, u32[]{:S(2)}) %collective-permute-start.8) | collective-permute-done | bytes 262176 | tf_op jit(solution)/shard_map/ppermute | solution.py:103
  34.5 2.1 %collective-permute-start.12 = (bf16[256,512]{1,0:T(8,128)(2,1)S(1)}, bf16[256,512]{1,0:T(8,128)(2,1)S(1)}, u32[]{:S(2)}, u32[]{:S(2)}) collective-permute-start(bf16[256,512]{1,0:T(8,128)(2,1)S(1)} %collective-permute-done.8), channel_id=1, source_target_pairs={{0,4},{4,8},{8,12},{12,14},{14,10},{10,6},{6,2},{2,0},{1,5},{5,9},... | collective-permute-start | bytes 786440 | tf_op jit(solution)/shard_map/ppermute | solution.py:103
  36.7 3.5 %collective-permute-done.10 = bf16[256,512]{1,0:T(8,128)(2,1)S(1)} collective-permute-done((bf16[256,512]{1,0:T(8,128)(2,1)S(1)}, bf16[256,512]{1,0:T(8,128)(2,1)S(1)}, u32[]{:S(2)}, u32[]{:S(2)}) %collective-permute-start.10) | collective-permute-done | bytes 262176 | tf_op jit(solution)/shard_map/ppermute | solution.py:103
  40.2 2.1 %collective-permute-start.14 = (bf16[256,512]{1,0:T(8,128)(2,1)S(1)}, bf16[256,512]{1,0:T(8,128)(2,1)S(1)}, u32[]{:S(2)}, u32[]{:S(2)}) collective-permute-start(bf16[256,512]{1,0:T(8,128)(2,1)S(1)} %collective-permute-done.10), channel_id=1, source_target_pairs={{0,4},{4,8},{8,12},{12,14},{14,10},{10,6},{6,2},{2,0},{1,5},{5,9},... | collective-permute-start | bytes 786440 | tf_op jit(solution)/shard_map/ppermute | solution.py:103
  42.4 3.4 %collective-permute-done.12 = bf16[256,512]{1,0:T(8,128)(2,1)S(1)} collective-permute-done((bf16[256,512]{1,0:T(8,128)(2,1)S(1)}, bf16[256,512]{1,0:T(8,128)(2,1)S(1)}, u32[]{:S(2)}, u32[]{:S(2)}) %collective-permute-start.12) | collective-permute-done | bytes 262176 | tf_op jit(solution)/shard_map/ppermute | solution.py:103
  45.8 2.1 %collective-permute-start.16 = (bf16[256,512]{1,0:T(8,128)(2,1)S(1)}, bf16[256,512]{1,0:T(8,128)(2,1)S(1)}, u32[]{:S(2)}, u32[]{:S(2)}) collective-permute-start(bf16[256,512]{1,0:T(8,128)(2,1)S(1)} %collective-permute-done.12), channel_id=1, source_target_pairs={{0,4},{4,8},{8,12},{12,14},{14,10},{10,6},{6,2},{2,0},{1,5},{5,9},... | collective-permute-start | bytes 786440 | tf_op jit(solution)/shard_map/ppermute | solution.py:103
  48.0 3.4 %collective-permute-done.14 = bf16[256,512]{1,0:T(8,128)(2,1)S(1)} collective-permute-done((bf16[256,512]{1,0:T(8,128)(2,1)S(1)}, bf16[256,512]{1,0:T(8,128)(2,1)S(1)}, u32[]{:S(2)}, u32[]{:S(2)}) %collective-permute-start.14) | collective-permute-done | bytes 262176 | tf_op jit(solution)/shard_map/ppermute | solution.py:103
  51.4 2.1 %collective-permute-start.18 = (bf16[256,512]{1,0:T(8,128)(2,1)S(1)}, bf16[256,512]{1,0:T(8,128)(2,1)S(1)}, u32[]{:S(2)}, u32[]{:S(2)}) collective-permute-start(bf16[256,512]{1,0:T(8,128)(2,1)S(1)} %collective-permute-done.14), channel_id=1, source_target_pairs={{0,4},{4,8},{8,12},{12,14},{14,10},{10,6},{6,2},{2,0},{1,5},{5,9},... | collective-permute-start | bytes 786440 | tf_op jit(solution)/shard_map/ppermute | solution.py:103
  53.6 3.4 %collective-permute-done.16 = bf16[256,512]{1,0:T(8,128)(2,1)S(1)} collective-permute-done((bf16[256,512]{1,0:T(8,128)(2,1)S(1)}, bf16[256,512]{1,0:T(8,128)(2,1)S(1)}, u32[]{:S(2)}, u32[]{:S(2)}) %collective-permute-start.16) | collective-permute-done | bytes 262176 | tf_op jit(solution)/shard_map/ppermute | solution.py:103
  57.0 2.1 %collective-permute-start.20 = (bf16[256,512]{1,0:T(8,128)(2,1)S(1)}, bf16[256,512]{1,0:T(8,128)(2,1)S(1)}, u32[]{:S(2)}, u32[]{:S(2)}) collective-permute-start(bf16[256,512]{1,0:T(8,128)(2,1)S(1)} %collective-permute-done.16), channel_id=1, source_target_pairs={{0,4},{4,8},{8,12},{12,14},{14,10},{10,6},{6,2},{2,0},{1,5},{5,9},... | collective-permute-start | bytes 786440 | tf_op jit(solution)/shard_map/ppermute | solution.py:103
  59.3 3.4 %collective-permute-done.18 = bf16[256,512]{1,0:T(8,128)(2,1)S(1)} collective-permute-done((bf16[256,512]{1,0:T(8,128)(2,1)S(1)}, bf16[256,512]{1,0:T(8,128)(2,1)S(1)}, u32[]{:S(2)}, u32[]{:S(2)}) %collective-permute-start.18) | collective-permute-done | bytes 262176 | tf_op jit(solution)/shard_map/ppermute | solution.py:103
  62.6 2.1 %collective-permute-start.22 = (bf16[256,512]{1,0:T(8,128)(2,1)S(1)}, bf16[256,512]{1,0:T(8,128)(2,1)S(1)}, u32[]{:S(2)}, u32[]{:S(2)}) collective-permute-start(bf16[256,512]{1,0:T(8,128)(2,1)S(1)} %collective-permute-done.18), channel_id=1, source_target_pairs={{0,4},{4,8},{8,12},{12,14},{14,10},{10,6},{6,2},{2,0},{1,5},{5,9},... | collective-permute-start | bytes 786440 | tf_op jit(solution)/shard_map/ppermute | solution.py:103
  64.9 3.4 %collective-permute-done.20 = bf16[256,512]{1,0:T(8,128)(2,1)S(1)} collective-permute-done((bf16[256,512]{1,0:T(8,128)(2,1)S(1)}, bf16[256,512]{1,0:T(8,128)(2,1)S(1)}, u32[]{:S(2)}, u32[]{:S(2)}) %collective-permute-start.20) | collective-permute-done | bytes 262176 | tf_op jit(solution)/shard_map/ppermute | solution.py:103
  68.3 2.1 %collective-permute-start.24 = (bf16[256,512]{1,0:T(8,128)(2,1)S(1)}, bf16[256,512]{1,0:T(8,128)(2,1)S(1)}, u32[]{:S(2)}, u32[]{:S(2)}) collective-permute-start(bf16[256,512]{1,0:T(8,128)(2,1)S(1)} %collective-permute-done.20), channel_id=1, source_target_pairs={{0,4},{4,8},{8,12},{12,14},{14,10},{10,6},{6,2},{2,0},{1,5},{5,9},... | collective-permute-start | bytes 786440 | tf_op jit(solution)/shard_map/ppermute | solution.py:103
  70.5 3.4 %collective-permute-done.22 = bf16[256,512]{1,0:T(8,128)(2,1)S(1)} collective-permute-done((bf16[256,512]{1,0:T(8,128)(2,1)S(1)}, bf16[256,512]{1,0:T(8,128)(2,1)S(1)}, u32[]{:S(2)}, u32[]{:S(2)}) %collective-permute-start.22) | collective-permute-done | bytes 262176 | tf_op jit(solution)/shard_map/ppermute | solution.py:103
  73.9 2.1 %collective-permute-start.26 = (bf16[256,512]{1,0:T(8,128)(2,1)S(1)}, bf16[256,512]{1,0:T(8,128)(2,1)S(1)}, u32[]{:S(2)}, u32[]{:S(2)}) collective-permute-start(bf16[256,512]{1,0:T(8,128)(2,1)S(1)} %collective-permute-done.22), channel_id=1, source_target_pairs={{0,4},{4,8},{8,12},{12,14},{14,10},{10,6},{6,2},{2,0},{1,5},{5,9},... | collective-permute-start | bytes 786440 | tf_op jit(solution)/shard_map/ppermute | solution.py:103
  76.1 3.4 %collective-permute-done.24 = bf16[256,512]{1,0:T(8,128)(2,1)S(1)} collective-permute-done((bf16[256,512]{1,0:T(8,128)(2,1)S(1)}, bf16[256,512]{1,0:T(8,128)(2,1)S(1)}, u32[]{:S(2)}, u32[]{:S(2)}) %collective-permute-start.24) | collective-permute-done | bytes 262176 | tf_op jit(solution)/shard_map/ppermute | solution.py:103
  79.5 2.1 %collective-permute-done.25 = bf16[256,512]{1,0:T(8,128)(2,1)S(1)} collective-permute-done((bf16[256,512]{1,0:T(8,128)(2,1)S(1)}, bf16[256,512]{1,0:T(8,128)(2,1)S(1)}, u32[]{:S(2)}, u32[]{:S(2)}) %collective-permute-start.25) | collective-permute-done | bytes 262176 | tf_op jit(solution)/shard_map/ppermute | solution.py:103
  81.6 2.6 %collective-permute-done.26 = bf16[256,512]{1,0:T(8,128)(2,1)S(1)} collective-permute-done((bf16[256,512]{1,0:T(8,128)(2,1)S(1)}, bf16[256,512]{1,0:T(8,128)(2,1)S(1)}, u32[]{:S(2)}, u32[]{:S(2)}) %collective-permute-start.26) | collective-permute-done | bytes 262176 | tf_op jit(solution)/shard_map/ppermute | solution.py:103
  84.3 1.5 %collective-permute-done.27 = bf16[256,512]{1,0:T(8,128)(2,1)S(1)} collective-permute-done((bf16[256,512]{1,0:T(8,128)(2,1)S(1)}, bf16[256,512]{1,0:T(8,128)(2,1)S(1)}, u32[]{:S(2)}, u32[]{:S(2)}) %collective-permute-start.27) | collective-permute-done | bytes 262176 | tf_op jit(solution)/shard_map/ppermute | solution.py:103
  87.1 5.1 %fusion.21 = (f32[256,2048]{1,0:T(8,128)}, bf16[256,2048]{1,0:T(8,128)(2,1)S(1)}) fusion(bf16[2,128,2048]{2,1,0:T(8,128)(2,1)S(1)} %copy-done, bf16[256,2048]{1,0:T(8,128)(2,1)S(1)} %fusion.31, bf16[2048,2048]{1,0:T(8,128)(2,1)S(1)} %constant_dynamic-update-slice_fusion.21), kind=kOutput, calls=%fused_computation.33 | convolution fusion | flops 2158493696 | bytes 13631488 | tf_op jit(solution)/shard_map/dot_general | solution.py:40
  92.2 1.5 %collective-permute-start.28 = (bf16[256,2048]{1,0:T(8,128)(2,1)S(1)}, bf16[256,2048]{1,0:T(8,128)(2,1)S(1)}, u32[]{:S(2)}, u32[]{:S(2)}) collective-permute-start(bf16[256,2048]{1,0:T(8,128)(2,1)S(1)} %get-tuple-element.36), channel_id=1, source_target_pairs={{0,1},{2,3},{4,5},{6,7},{8,9},{10,11},{12,13},{14,15},{16,17},{18,... | collective-permute-start | bytes 3145736 | tf_op jit(solution)/shard_map/ppermute | solution.py:18
  96.5 5.1 %fusion.42 = (f32[256,2048]{1,0:T(8,128)S(1)}, f32[256,2048]{1,0:T(8,128)}) fusion(bf16[256,2048]{1,0:T(8,128)(2,1)S(1)} %collective-permute-done.28, bf16[2048,2048]{1,0:T(8,128)(2,1)S(1)} %constant_dynamic-update-slice_fusion.21, f32[256]{0:T(256)S(1)} %add_rsqrt_fusion, f32[256]{0:T(256)S(1)} %broadcast_multiply_fusion.4, f32[2048]{0:T(1024)S(1)} %bitcast.62), kind=kOutput, calls=%fused_computation.64 | convolution fusion | flops 2161639424 | bytes 13641728 | tf_op jit(solution)/shard_map/dot_general | solution.py:40
  101.5 1.3 copy-done.1
  104.6 3.3 %collective-permute-done.29 = f32[7]{0:T(128)S(1)} collective-permute-done((f32[7]{0:T(128)S(1)}, f32[7]{0:T(128)S(1)}, u32[]{:S(2)}, u32[]{:S(2)}) %collective-permute-start.29) | collective-permute-done | bytes 60 | tf_op jit(solution)/shard_map/ppermute | solution.py:116
  108.6 1.6 %collective-permute-start.30 = (f32[7]{0:T(128)S(1)}, f32[7]{0:T(128)S(1)}, u32[]{:S(2)}, u32[]{:S(2)}) collective-permute-start(f32[7]{0:T(128)S(1)} %fusion.74), channel_id=1, source_target_pairs={{0,4},{2,6},{4,0},{6,2},{8,12},{10,14},{12,8},{14,10},{1,5},{3,7},... | collective-permute-start | bytes 92 | tf_op jit(solution)/shard_map/ppermute | solution.py:116
  110.2 2.0 %collective-permute-done.30 = f32[7]{0:T(128)S(1)} collective-permute-done((f32[7]{0:T(128)S(1)}, f32[7]{0:T(128)S(1)}, u32[]{:S(2)}, u32[]{:S(2)}) %collective-permute-start.30) | collective-permute-done | bytes 60 | tf_op jit(solution)/shard_map/ppermute | solution.py:116
  112.2 2.6 %collective-permute-start.31 = (f32[7]{0:T(128)S(1)}, f32[7]{0:T(128)S(1)}, u32[]{:S(2)}, u32[]{:S(2)}) collective-permute-start(f32[7]{0:T(128)S(1)} %add.317), channel_id=1, source_target_pairs={{0,8},{2,10},{4,12},{6,14},{8,0},{10,2},{12,4},{14,6},{1,9},{3,11}... | collective-permute-start | bytes 92 | tf_op jit(solution)/shard_map/ppermute | solution.py:116
  114.8 1.9 %collective-permute-done.31 = f32[7]{0:T(128)S(1)} collective-permute-done((f32[7]{0:T(128)S(1)}, f32[7]{0:T(128)S(1)}, u32[]{:S(2)}, u32[]{:S(2)}) %collective-permute-start.31) | collective-permute-done | bytes 60 | tf_op jit(solution)/shard_map/ppermute | solution.py:116
  118.6 1.4 fusion.62
  121.5 5.9 %fusion.39 = (f32[128,2048]{1,0:T(8,128)S(1)}, f32[128,2048]{1,0:T(8,128)S(1)}) fusion(bf16[128,2048]{1,0:T(8,128)(2,1)S(1)} %copy-done.3, f32[256,2048]{1,0:T(8,128)} %copy-done.1, f32[]{:T(128)} %bitcast.17, f32[]{:T(128)} %bitcast.16, f32[]{:T(128)} %bitcast.15, f32[]{:T(128)} %bitcast.20, f32[]{:T(128)} %bitcast.19, f32[]{:T(128)} %bitcast.18), kind=kLoop, calls=%fused_computation.61 | loop fusion | flops 2883584 | bytes 4718616 | tf_op jit(solution)/shard_map/add | solution.py:167
  127.5 6.1 %fusion.60 = (f32[256]{0:T(256)S(1)}, f32[256]{0:T(256)S(1)}, f32[256,2048]{1,0:T(8,128)S(1)}) fusion(f32[256]{0:T(256)S(1)} %add_rsqrt_fusion, f32[256]{0:T(256)S(1)} %broadcast_multiply_fusion.4, bf16[256,2048]{1,0:T(8,128)(2,1)S(1)} %collective-permute-done.28, f32[2048]{0:T(1024)S(1)} %bitcast.63, bf16[2048,2048]{1,0:T(8,128)(2,1)} %copy-done.2, ...), kind=kOutput, calls=%fused_computation.129 | convolution fusion | flops 2152726016 | bytes 15740928 | tf_op jit(solution)/shard_map/dot_general | solution.py:47
  134.3 1.3 collective-permute-start.32
  137.0 1.5 %collective-permute-start.33 = (f32[1]{0:T(128)}, f32[1]{0:T(128)}, u32[]{:S(2)}, u32[]{:S(2)}) collective-permute-start(f32[1]{0:T(128)} %bitcast.23), channel_id=1, source_target_pairs={{1,0},{3,2},{5,4},{7,6},{9,8},{11,10},{13,12},{15,14},{17,16},{19,... | collective-permute-start | bytes 20 | tf_op jit(solution)/shard_map/ppermute | solution.py:18
  138.5 1.7 %collective-permute-done.33 = f32[1]{0:T(128)} collective-permute-done((f32[1]{0:T(128)}, f32[1]{0:T(128)}, u32[]{:S(2)}, u32[]{:S(2)}) %collective-permute-start.33) | collective-permute-done | bytes 36 | tf_op jit(solution)/shard_map/ppermute | solution.py:18
  140.9 6.7 %fusion.59 = (f32[256]{0:T(256)S(1)}, f32[256]{0:T(256)S(1)}, f32[256,2048]{1,0:T(8,128)S(1)}) fusion(f32[256]{0:T(256)S(1)} %rsqrt_bitcast_fusion, f32[256]{0:T(256)S(1)} %get-tuple-element.45, bf16[2,128,2048]{2,1,0:T(8,128)(2,1)S(1)} %copy-done, f32[2048]{0:T(1024)S(1)} %bitcast.64, bf16[2048,2048]{1,0:T(8,128)(2,1)} %copy-done.2, ...), kind=kOutput, calls=%fused_computation.128 | convolution fusion | flops 2152726016 | bytes 14692352 | tf_op jit(solution)/shard_map/dot_general | solution.py:47
  147.6 2.0 %fusion.43 = bf16[256,2048]{1,0:T(8,128)(2,1)} fusion(bf16[256,2048]{1,0:T(8,128)(2,1)S(1)} %fusion.10, bf16[2,128,2048]{2,1,0:T(8,128)(2,1)S(1)} %copy-done, f32[256,2048]{1,0:T(8,128)S(1)} %get-tuple-element.50, bf16[256,2048]{1,0:T(8,128)(2,1)S(1)} %collective-permute-done.32, f32[256]{0:T(256)S(1)} %broadcast_multiply_fusion, ...), kind=kLoop, calls=%fused_computation.65 | loop fusion | flops 5767168 | bytes 6295553 | tf_op jit(solution)/shard_map/jit(_where)/select_n | solution.py:174
  (104 shorter events, 12.6 us)
Async XLA Ops:
  1.9 10.2 %collective-permute-start = (bf16[256,512]{1,0:T(8,128)(2,1)S(1)}, bf16[256,512]{1,0:T(8,128)(2,1)S(1)}, u32[]{:S(2)}, u32[]{:S(2)}) collective-permute-start(bf16[256,512]{1,0:T(8,128)(2,1)S(1)} %get-tuple-element.40), channel_id=1, source_target_pairs={{0,4},{4,8},{8,12},{12,14},{14,10},{10,6},{6,2},{2,0},{1,5},{5,9},... | collective-permute-start | bytes 786440 | tf_op jit(solution)/shard_map/ppermute | solution.py:103
  5.0 9.2 %collective-permute-start.1 = (bf16[256,512]{1,0:T(8,128)(2,1)S(1)}, bf16[256,512]{1,0:T(8,128)(2,1)S(1)}, u32[]{:S(2)}, u32[]{:S(2)}) collective-permute-start(bf16[256,512]{1,0:T(8,128)(2,1)S(1)} %get-tuple-element.39), channel_id=1, source_target_pairs={{4,0},{8,4},{12,8},{14,12},{10,14},{6,10},{2,6},{0,2},{5,1},{9,5},... | collective-permute-start | bytes 786440 | tf_op jit(solution)/shard_map/ppermute | solution.py:103
  5.0 12.7 %collective-permute-start.2 = (bf16[256,512]{1,0:T(8,128)(2,1)S(1)}, bf16[256,512]{1,0:T(8,128)(2,1)S(1)}, u32[]{:S(2)}, u32[]{:S(2)}) collective-permute-start(bf16[256,512]{1,0:T(8,128)(2,1)S(1)} %get-tuple-element.38), channel_id=1, source_target_pairs={{0,4},{4,8},{8,12},{12,14},{14,10},{10,6},{6,2},{2,0},{1,5},{5,9},... | collective-permute-start | bytes 786440 | tf_op jit(solution)/shard_map/ppermute | solution.py:103
  7.0 12.8 %collective-permute-start.3 = (bf16[256,512]{1,0:T(8,128)(2,1)S(1)}, bf16[256,512]{1,0:T(8,128)(2,1)S(1)}, u32[]{:S(2)}, u32[]{:S(2)}) collective-permute-start(bf16[256,512]{1,0:T(8,128)(2,1)S(1)} %get-tuple-element.37), channel_id=1, source_target_pairs={{4,0},{8,4},{12,8},{14,12},{10,14},{6,10},{2,6},{0,2},{5,1},{9,5},... | collective-permute-start | bytes 786440 | tf_op jit(solution)/shard_map/ppermute | solution.py:103
  12.1 11.2 %collective-permute-start.4 = (bf16[256,512]{1,0:T(8,128)(2,1)S(1)}, bf16[256,512]{1,0:T(8,128)(2,1)S(1)}, u32[]{:S(2)}, u32[]{:S(2)}) collective-permute-start(bf16[256,512]{1,0:T(8,128)(2,1)S(1)} %collective-permute-done), channel_id=1, source_target_pairs={{0,4},{4,8},{8,12},{12,14},{14,10},{10,6},{6,2},{2,0},{1,5},{5,9},... | collective-permute-start | bytes 786440 | tf_op jit(solution)/shard_map/ppermute | solution.py:103
  14.2 11.2 %collective-permute-start.5 = (bf16[256,512]{1,0:T(8,128)(2,1)S(1)}, bf16[256,512]{1,0:T(8,128)(2,1)S(1)}, u32[]{:S(2)}, u32[]{:S(2)}) collective-permute-start(bf16[256,512]{1,0:T(8,128)(2,1)S(1)} %collective-permute-done.1), channel_id=1, source_target_pairs={{4,0},{8,4},{12,8},{14,12},{10,14},{6,10},{2,6},{0,2},{5,1},{9,5},... | collective-permute-start | bytes 786440 | tf_op jit(solution)/shard_map/ppermute | solution.py:103
  17.7 11.2 %collective-permute-start.6 = (bf16[256,512]{1,0:T(8,128)(2,1)S(1)}, bf16[256,512]{1,0:T(8,128)(2,1)S(1)}, u32[]{:S(2)}, u32[]{:S(2)}) collective-permute-start(bf16[256,512]{1,0:T(8,128)(2,1)S(1)} %collective-permute-done.2), channel_id=1, source_target_pairs={{0,4},{4,8},{8,12},{12,14},{14,10},{10,6},{6,2},{2,0},{1,5},{5,9},... | collective-permute-start | bytes 786440 | tf_op jit(solution)/shard_map/ppermute | solution.py:103
  19.8 11.2 %collective-permute-start.7 = (bf16[256,512]{1,0:T(8,128)(2,1)S(1)}, bf16[256,512]{1,0:T(8,128)(2,1)S(1)}, u32[]{:S(2)}, u32[]{:S(2)}) collective-permute-start(bf16[256,512]{1,0:T(8,128)(2,1)S(1)} %collective-permute-done.3), channel_id=1, source_target_pairs={{4,0},{8,4},{12,8},{14,12},{10,14},{6,10},{2,6},{0,2},{5,1},{9,5},... | collective-permute-start | bytes 786440 | tf_op jit(solution)/shard_map/ppermute | solution.py:103
  23.3 11.2 %collective-permute-start.8 = (bf16[256,512]{1,0:T(8,128)(2,1)S(1)}, bf16[256,512]{1,0:T(8,128)(2,1)S(1)}, u32[]{:S(2)}, u32[]{:S(2)}) collective-permute-start(bf16[256,512]{1,0:T(8,128)(2,1)S(1)} %collective-permute-done.4), channel_id=1, source_target_pairs={{0,4},{4,8},{8,12},{12,14},{14,10},{10,6},{6,2},{2,0},{1,5},{5,9},... | collective-permute-start | bytes 786440 | tf_op jit(solution)/shard_map/ppermute | solution.py:103
  25.4 11.2 %collective-permute-start.9 = (bf16[256,512]{1,0:T(8,128)(2,1)S(1)}, bf16[256,512]{1,0:T(8,128)(2,1)S(1)}, u32[]{:S(2)}, u32[]{:S(2)}) collective-permute-start(bf16[256,512]{1,0:T(8,128)(2,1)S(1)} %collective-permute-done.5), channel_id=1, source_target_pairs={{4,0},{8,4},{12,8},{14,12},{10,14},{6,10},{2,6},{0,2},{5,1},{9,5},... | collective-permute-start | bytes 786440 | tf_op jit(solution)/shard_map/ppermute | solution.py:103
  28.9 11.2 %collective-permute-start.10 = (bf16[256,512]{1,0:T(8,128)(2,1)S(1)}, bf16[256,512]{1,0:T(8,128)(2,1)S(1)}, u32[]{:S(2)}, u32[]{:S(2)}) collective-permute-start(bf16[256,512]{1,0:T(8,128)(2,1)S(1)} %collective-permute-done.6), channel_id=1, source_target_pairs={{0,4},{4,8},{8,12},{12,14},{14,10},{10,6},{6,2},{2,0},{1,5},{5,9},... | collective-permute-start | bytes 786440 | tf_op jit(solution)/shard_map/ppermute | solution.py:103
  31.0 11.2 %collective-permute-start.11 = (bf16[256,512]{1,0:T(8,128)(2,1)S(1)}, bf16[256,512]{1,0:T(8,128)(2,1)S(1)}, u32[]{:S(2)}, u32[]{:S(2)}) collective-permute-start(bf16[256,512]{1,0:T(8,128)(2,1)S(1)} %collective-permute-done.7), channel_id=1, source_target_pairs={{4,0},{8,4},{12,8},{14,12},{10,14},{6,10},{2,6},{0,2},{5,1},{9,5},... | collective-permute-start | bytes 786440 | tf_op jit(solution)/shard_map/ppermute | solution.py:103
  34.5 11.2 %collective-permute-start.12 = (bf16[256,512]{1,0:T(8,128)(2,1)S(1)}, bf16[256,512]{1,0:T(8,128)(2,1)S(1)}, u32[]{:S(2)}, u32[]{:S(2)}) collective-permute-start(bf16[256,512]{1,0:T(8,128)(2,1)S(1)} %collective-permute-done.8), channel_id=1, source_target_pairs={{0,4},{4,8},{8,12},{12,14},{14,10},{10,6},{6,2},{2,0},{1,5},{5,9},... | collective-permute-start | bytes 786440 | tf_op jit(solution)/shard_map/ppermute | solution.py:103
  36.7 11.2 %collective-permute-start.13 = (bf16[256,512]{1,0:T(8,128)(2,1)S(1)}, bf16[256,512]{1,0:T(8,128)(2,1)S(1)}, u32[]{:S(2)}, u32[]{:S(2)}) collective-permute-start(bf16[256,512]{1,0:T(8,128)(2,1)S(1)} %collective-permute-done.9), channel_id=1, source_target_pairs={{4,0},{8,4},{12,8},{14,12},{10,14},{6,10},{2,6},{0,2},{5,1},{9,5},... | collective-permute-start | bytes 786440 | tf_op jit(solution)/shard_map/ppermute | solution.py:103
  40.2 11.2 %collective-permute-start.14 = (bf16[256,512]{1,0:T(8,128)(2,1)S(1)}, bf16[256,512]{1,0:T(8,128)(2,1)S(1)}, u32[]{:S(2)}, u32[]{:S(2)}) collective-permute-start(bf16[256,512]{1,0:T(8,128)(2,1)S(1)} %collective-permute-done.10), channel_id=1, source_target_pairs={{0,4},{4,8},{8,12},{12,14},{14,10},{10,6},{6,2},{2,0},{1,5},{5,9},... | collective-permute-start | bytes 786440 | tf_op jit(solution)/shard_map/ppermute | solution.py:103
  42.3 11.3 %collective-permute-start.15 = (bf16[256,512]{1,0:T(8,128)(2,1)S(1)}, bf16[256,512]{1,0:T(8,128)(2,1)S(1)}, u32[]{:S(2)}, u32[]{:S(2)}) collective-permute-start(bf16[256,512]{1,0:T(8,128)(2,1)S(1)} %collective-permute-done.11), channel_id=1, source_target_pairs={{4,0},{8,4},{12,8},{14,12},{10,14},{6,10},{2,6},{0,2},{5,1},{9,5},... | collective-permute-start | bytes 786440 | tf_op jit(solution)/shard_map/ppermute | solution.py:103
  45.8 11.2 %collective-permute-start.16 = (bf16[256,512]{1,0:T(8,128)(2,1)S(1)}, bf16[256,512]{1,0:T(8,128)(2,1)S(1)}, u32[]{:S(2)}, u32[]{:S(2)}) collective-permute-start(bf16[256,512]{1,0:T(8,128)(2,1)S(1)} %collective-permute-done.12), channel_id=1, source_target_pairs={{0,4},{4,8},{8,12},{12,14},{14,10},{10,6},{6,2},{2,0},{1,5},{5,9},... | collective-permute-start | bytes 786440 | tf_op jit(solution)/shard_map/ppermute | solution.py:103
  47.9 11.3 %collective-permute-start.17 = (bf16[256,512]{1,0:T(8,128)(2,1)S(1)}, bf16[256,512]{1,0:T(8,128)(2,1)S(1)}, u32[]{:S(2)}, u32[]{:S(2)}) collective-permute-start(bf16[256,512]{1,0:T(8,128)(2,1)S(1)} %collective-permute-done.13), channel_id=1, source_target_pairs={{4,0},{8,4},{12,8},{14,12},{10,14},{6,10},{2,6},{0,2},{5,1},{9,5},... | collective-permute-start | bytes 786440 | tf_op jit(solution)/shard_map/ppermute | solution.py:103
  51.4 11.2 %collective-permute-start.18 = (bf16[256,512]{1,0:T(8,128)(2,1)S(1)}, bf16[256,512]{1,0:T(8,128)(2,1)S(1)}, u32[]{:S(2)}, u32[]{:S(2)}) collective-permute-start(bf16[256,512]{1,0:T(8,128)(2,1)S(1)} %collective-permute-done.14), channel_id=1, source_target_pairs={{0,4},{4,8},{8,12},{12,14},{14,10},{10,6},{6,2},{2,0},{1,5},{5,9},... | collective-permute-start | bytes 786440 | tf_op jit(solution)/shard_map/ppermute | solution.py:103
  53.5 11.2 %collective-permute-start.19 = (bf16[256,512]{1,0:T(8,128)(2,1)S(1)}, bf16[256,512]{1,0:T(8,128)(2,1)S(1)}, u32[]{:S(2)}, u32[]{:S(2)}) collective-permute-start(bf16[256,512]{1,0:T(8,128)(2,1)S(1)} %collective-permute-done.15), channel_id=1, source_target_pairs={{4,0},{8,4},{12,8},{14,12},{10,14},{6,10},{2,6},{0,2},{5,1},{9,5},... | collective-permute-start | bytes 786440 | tf_op jit(solution)/shard_map/ppermute | solution.py:103
  57.0 11.2 %collective-permute-start.20 = (bf16[256,512]{1,0:T(8,128)(2,1)S(1)}, bf16[256,512]{1,0:T(8,128)(2,1)S(1)}, u32[]{:S(2)}, u32[]{:S(2)}) collective-permute-start(bf16[256,512]{1,0:T(8,128)(2,1)S(1)} %collective-permute-done.16), channel_id=1, source_target_pairs={{0,4},{4,8},{8,12},{12,14},{14,10},{10,6},{6,2},{2,0},{1,5},{5,9},... | collective-permute-start | bytes 786440 | tf_op jit(solution)/shard_map/ppermute | solution.py:103
  59.2 11.2 %collective-permute-start.21 = (bf16[256,512]{1,0:T(8,128)(2,1)S(1)}, bf16[256,512]{1,0:T(8,128)(2,1)S(1)}, u32[]{:S(2)}, u32[]{:S(2)}) collective-permute-start(bf16[256,512]{1,0:T(8,128)(2,1)S(1)} %collective-permute-done.17), channel_id=1, source_target_pairs={{4,0},{8,4},{12,8},{14,12},{10,14},{6,10},{2,6},{0,2},{5,1},{9,5},... | collective-permute-start | bytes 786440 | tf_op jit(solution)/shard_map/ppermute | solution.py:103
  62.6 11.2 %collective-permute-start.22 = (bf16[256,512]{1,0:T(8,128)(2,1)S(1)}, bf16[256,512]{1,0:T(8,128)(2,1)S(1)}, u32[]{:S(2)}, u32[]{:S(2)}) collective-permute-start(bf16[256,512]{1,0:T(8,128)(2,1)S(1)} %collective-permute-done.18), channel_id=1, source_target_pairs={{0,4},{4,8},{8,12},{12,14},{14,10},{10,6},{6,2},{2,0},{1,5},{5,9},... | collective-permute-start | bytes 786440 | tf_op jit(solution)/shard_map/ppermute | solution.py:103
  64.8 11.2 %collective-permute-start.23 = (bf16[256,512]{1,0:T(8,128)(2,1)S(1)}, bf16[256,512]{1,0:T(8,128)(2,1)S(1)}, u32[]{:S(2)}, u32[]{:S(2)}) collective-permute-start(bf16[256,512]{1,0:T(8,128)(2,1)S(1)} %collective-permute-done.19), channel_id=1, source_target_pairs={{4,0},{8,4},{12,8},{14,12},{10,14},{6,10},{2,6},{0,2},{5,1},{9,5},... | collective-permute-start | bytes 786440 | tf_op jit(solution)/shard_map/ppermute | solution.py:103
  64.9 21.0 %copy-start.4 = (bf16[1,256,2048]{2,1,0:T(8,128)(2,1)S(1)}, bf16[1,256,2048]{2,1,0:T(8,128)(2,1)}, u32[]{:S(2)}) copy-start(bf16[1,256,2048]{2,1,0:T(8,128)(2,1)} %param.6) | copy-start | bytes 3145732
  68.3 11.2 %collective-permute-start.24 = (bf16[256,512]{1,0:T(8,128)(2,1)S(1)}, bf16[256,512]{1,0:T(8,128)(2,1)S(1)}, u32[]{:S(2)}, u32[]{:S(2)}) collective-permute-start(bf16[256,512]{1,0:T(8,128)(2,1)S(1)} %collective-permute-done.20), channel_id=1, source_target_pairs={{0,4},{4,8},{8,12},{12,14},{14,10},{10,6},{6,2},{2,0},{1,5},{5,9},... | collective-permute-start | bytes 786440 | tf_op jit(solution)/shard_map/ppermute | solution.py:103
  70.4 11.2 %collective-permute-start.25 = (bf16[256,512]{1,0:T(8,128)(2,1)S(1)}, bf16[256,512]{1,0:T(8,128)(2,1)S(1)}, u32[]{:S(2)}, u32[]{:S(2)}) collective-permute-start(bf16[256,512]{1,0:T(8,128)(2,1)S(1)} %collective-permute-done.21), channel_id=1, source_target_pairs={{4,0},{8,4},{12,8},{14,12},{10,14},{6,10},{2,6},{0,2},{5,1},{9,5},... | collective-permute-start | bytes 786440 | tf_op jit(solution)/shard_map/ppermute | solution.py:103
  73.9 10.4 %collective-permute-start.26 = (bf16[256,512]{1,0:T(8,128)(2,1)S(1)}, bf16[256,512]{1,0:T(8,128)(2,1)S(1)}, u32[]{:S(2)}, u32[]{:S(2)}) collective-permute-start(bf16[256,512]{1,0:T(8,128)(2,1)S(1)} %collective-permute-done.22), channel_id=1, source_target_pairs={{0,4},{4,8},{8,12},{12,14},{14,10},{10,6},{6,2},{2,0},{1,5},{5,9},... | collective-permute-start | bytes 786440 | tf_op jit(solution)/shard_map/ppermute | solution.py:103
  76.0 9.8 %collective-permute-start.27 = (bf16[256,512]{1,0:T(8,128)(2,1)S(1)}, bf16[256,512]{1,0:T(8,128)(2,1)S(1)}, u32[]{:S(2)}, u32[]{:S(2)}) collective-permute-start(bf16[256,512]{1,0:T(8,128)(2,1)S(1)} %collective-permute-done.23), channel_id=1, source_target_pairs={{4,0},{8,4},{12,8},{14,12},{10,14},{6,10},{2,6},{0,2},{5,1},{9,5},... | collective-permute-start | bytes 786440 | tf_op jit(solution)/shard_map/ppermute | solution.py:103
  76.1 9.9 %copy-start = (bf16[2,128,2048]{2,1,0:T(8,128)(2,1)S(1)}, bf16[2,128,2048]{2,1,0:T(8,128)(2,1)}, u32[]{:S(2)}) copy-start(bf16[2,128,2048]{2,1,0:T(8,128)(2,1)} %param.4) | copy-start | bytes 3145732
  85.8 0.8 copy-start.5
  86.0 10.4 %copy-start.2 = (bf16[2048,2048]{1,0:T(8,128)(2,1)}, bf16[2048,2048]{1,0:T(8,128)(2,1)S(1)}, u32[]{:S(2)}) copy-start(bf16[2048,2048]{1,0:T(8,128)(2,1)S(1)} %constant_dynamic-update-slice_fusion.21) | copy-start | bytes 25165828
  87.1 6.7 %copy-start.3 = (bf16[128,2048]{1,0:T(8,128)(2,1)S(1)}, bf16[128,2048]{1,0:T(8,128)(2,1)}, u32[]{:S(2)}) copy-start(bf16[128,2048]{1,0:T(8,128)(2,1)} %param.5) | copy-start | bytes 1572868
  92.2 3.6 %collective-permute-start.28 = (bf16[256,2048]{1,0:T(8,128)(2,1)S(1)}, bf16[256,2048]{1,0:T(8,128)(2,1)S(1)}, u32[]{:S(2)}, u32[]{:S(2)}) collective-permute-start(bf16[256,2048]{1,0:T(8,128)(2,1)S(1)} %get-tuple-element.36), channel_id=1, source_target_pairs={{0,1},{2,3},{4,5},{6,7},{8,9},{10,11},{12,13},{14,15},{16,17},{18,... | collective-permute-start | bytes 3145736 | tf_op jit(solution)/shard_map/ppermute | solution.py:18
  101.5 1.3 copy-start.1
  104.3 3.6 %collective-permute-start.29 = (f32[7]{0:T(128)S(1)}, f32[7]{0:T(128)S(1)}, u32[]{:S(2)}, u32[]{:S(2)}) collective-permute-start(f32[7]{0:T(128)S(1)} %pad_maximum_fusion.1), channel_id=1, source_target_pairs={{0,2},{2,0},{4,6},{6,4},{8,10},{10,8},{12,14},{14,12},{1,3},{3,1},... | collective-permute-start | bytes 92 | tf_op jit(solution)/shard_map/ppermute | solution.py:116
  108.6 3.6 %collective-permute-start.30 = (f32[7]{0:T(128)S(1)}, f32[7]{0:T(128)S(1)}, u32[]{:S(2)}, u32[]{:S(2)}) collective-permute-start(f32[7]{0:T(128)S(1)} %fusion.74), channel_id=1, source_target_pairs={{0,4},{2,6},{4,0},{6,2},{8,12},{10,14},{12,8},{14,10},{1,5},{3,7},... | collective-permute-start | bytes 92 | tf_op jit(solution)/shard_map/ppermute | solution.py:116
  112.2 4.5 %collective-permute-start.31 = (f32[7]{0:T(128)S(1)}, f32[7]{0:T(128)S(1)}, u32[]{:S(2)}, u32[]{:S(2)}) collective-permute-start(f32[7]{0:T(128)S(1)} %add.317), channel_id=1, source_target_pairs={{0,8},{2,10},{4,12},{6,14},{8,0},{10,2},{12,4},{14,6},{1,9},{3,11}... | collective-permute-start | bytes 92 | tf_op jit(solution)/shard_map/ppermute | solution.py:116
  121.5 5.9 %copy-start.6 = (f32[256,2048]{1,0:T(8,128)S(1)}, f32[256,2048]{1,0:T(8,128)}, u32[]{:S(2)}) copy-start(f32[256,2048]{1,0:T(8,128)} %get-tuple-element.12) | copy-start | bytes 6291460
  134.3 6.5 %collective-permute-start.32 = (bf16[256,2048]{1,0:T(8,128)(2,1)S(1)}, bf16[256,2048]{1,0:T(8,128)(2,1)S(1)}, u32[]{:S(2)}, u32[]{:S(2)}) collective-permute-start(bf16[256,2048]{1,0:T(8,128)(2,1)S(1)} %fusion.10), channel_id=1, source_target_pairs={{1,0},{3,2},{5,4},{7,6},{9,8},{11,10},{13,12},{15,14},{17,16},{19,... | collective-permute-start | bytes 3145736 | tf_op jit(solution)/shard_map/ppermute | solution.py:18
  137.0 3.3 %collective-permute-start.33 = (f32[1]{0:T(128)}, f32[1]{0:T(128)}, u32[]{:S(2)}, u32[]{:S(2)}) collective-permute-start(f32[1]{0:T(128)} %bitcast.23), channel_id=1, source_target_pairs={{1,0},{3,2},{5,4},{7,6},{9,8},{11,10},{13,12},{15,14},{17,16},{19,... | collective-permute-start | bytes 20 | tf_op jit(solution)/shard_map/ppermute | solution.py:18

commit v6 on v5

--- a/solution.py
+++ b/solution.py
@@ -118,6 +118,37 @@
     return v
 
 
+def packed_score(packed, count, size):
+    gram = [[packed[m * count + k] for k in range(count)] for m in range(count)]
+    member_obs = [packed[count * count + m] for m in range(count)]
+    obs_sq = packed[count * count + count]
+    diag = [gram[m][m] for m in range(count)]
+    to_obs = [jnp.sqrt((diag[m] - 2.0 * member_obs[m] + obs_sq) / size + epsilon) for m in range(count)]
+    pair = [[None] * count for _ in range(count)]
+    pair_total = 0.0
+    for m in range(count):
+        for k in range(count):
+            if m != k:
+                pair[m][k] = jnp.sqrt((diag[m] + diag[k] - 2.0 * gram[m][k]) / size + epsilon)
+                pair_total = pair_total + pair[m][k]
+    energy = sum(to_obs) / count - pair_total / (2.0 * count * (count - 1))
+    obs_coeff = [1.0 / (count * to_obs[m]) for m in range(count)]
+    rows = []
+    for m in range(count):
+        row = []
+        off = 0.0
+        for k in range(count):
+            if m != k:
+                c = 1.0 / (count * (count - 1) * pair[m][k])
+                off = off + c
+                row.append(c)
+            else:
+                row.append(None)
+        row[m] = obs_coeff[m] - off
+        rows.append(jnp.stack(row))
+    return (energy, jnp.stack(rows), -jnp.stack(obs_coeff))
+
+
 def per_device(inputs, obs, weights, gains):
     sec = lax.axis_index("section")
     on_first = sec == 0
@@ -141,35 +172,31 @@
     arrived = shifted(fa[0], "section", 1)
     fb = section_forward(arrived, gain, weight)
 
-    y = fb[0].astype(jnp.float32).reshape(members, tok_rows, width)
+    y = fb[0].reshape(members, tok_rows, width)
     obs_f = obs.astype(jnp.float32)
+    yf = y.astype(jnp.float32)
     terms = []
     for m in range(members):
         for k in range(members):
-            terms.append(jnp.sum(y[m] * y[k], axis=-1))
+            terms.append(jnp.sum(yf[m] * yf[k], axis=-1))
     for m in range(members):
-        terms.append(jnp.sum(y[m] * obs_f, axis=-1))
+        terms.append(jnp.sum(yf[m] * obs_f, axis=-1))
     terms = jnp.sum(jnp.stack(terms), axis=-1)
     packed = tree_sum(jnp.concatenate([terms, obs_sq.reshape(1)]), "tok")
     slope_a, slope_b = lax.optimization_barrier((gelu_slope(fa[3]), gelu_slope(fb[3])))
-    member_gram = packed[: members * members].reshape(members, members)
-    obs_rows = packed[members * members : members * members + members]
-    obs_total = packed[members * members + members]
-    energy, member_coeff, obs_coeff = score_terms(member_gram, obs_rows, obs_total, size)
+    energy, member_coeff, obs_coeff = packed_score(packed, members, size)
     energy_arr = jnp.reshape(energy, (1,))
+
+    cot = obs_coeff[:, None, None] * obs_f[None]
+    for k in range(members):
+        cot = cot + member_coeff[:, k, None, None] * y[k].astype(jnp.float32)[None]
+    cot = cot.reshape(members * tok_rows, width)
+
+    da = section_backward(cot, gain, weight, fb[1], fb[2], slope_b)
+    back = shifted(da, "section", -1)
+    energy_arr, back = lax.optimization_barrier((energy_arr, back))
     energy_peer = shifted(energy_arr, "section", -1)
     energy_out = jnp.where(on_first, energy_peer, energy_arr)
-
-    cots = []
-    for m in range(members):
-        c = obs_coeff[m] * obs_f
-        for k in range(members):
-            c = c + member_coeff[m, k] * y[k]
-        cots.append(c)
-    cot = jnp.concatenate(cots, axis=0)
-
-    da = section_backward(cot, gain, weight, fb[1], fb[2], slope_b)
-    back = shifted(da, "section", -1)
     db = section_backward(back.astype(jnp.float32), gain, weight, fa[1], fa[2], slope_a)
     grads = jnp.where(on_first, db, da).reshape(members, tok_rows, width)
     return (grads[None], energy_out)

time: 151 us -> 150 us (level); the launches traced: 151 us -> 148 us
  between operations: 4.28 us -> 9.82 us
  matrix products: 23 us -> 20.1 us
  local copies, waits for them, and re-layouts: 7.15 us -> 4.3 us
  other arithmetic: 15.7 us -> 12.9 us
    add x2 -> x0, other arithmetic: 6.01 us -> none  [the longest x1 5.93 us: per_device(): c = c + member_coeff[m, k] * y[k]]
    convert_element_type x0 -> x3, other arithmetic: none -> 3.81 us  [the longest x1 2.14 us: section_backward(): grad_pre = (grad_out * slope).astype(jnp.bfloat16)]
    dot_general x2, matrix products: 12.8 us -> 9.43 us  [section_backward(): lax.dot_general(grad_pre, weight, (((1,), (1,)), ((), ())), preferred_ele...]
    reduce_sum x4 -> x1, other arithmetic: 2.75 us -> 0.56 us  [per_device(): terms.append(jnp.sum(yf[m] * obs_f, axis=-1))]
    ppermute x3, waiting for transfers between devices: 2.86 us -> 4.49 us  [shifted(): return lax.ppermute(x, axis, pairs)]
    ppermute x3, waiting for transfers between devices: 7.16 us -> 5.57 us  [tree_sum(): v = v + lax.ppermute(v, axis, [(i, i ^ b) for i in range(n)])]
  transfers between devices with their start and end apart: 34 -> 34, of which waited for: 21 -> 21; matrix products, arithmetic and copies ran while one was open for 2% -> 9% of each run, Pallas kernels for 0% -> 0%
where the time goes in v6:
time: 150 us; the launch traced here: 148 us
  waiting for transfers between devices  61.2 us (41%)
  starting transfers between devices  39.5 us (26%)
  matrix products  20.1 us (13%)
  other arithmetic  12.9 us (9%)
  between operations  9.82 us (7%)
  local copies, waits for them, and re-layouts  4.3 us (3%)
    ppermute x28, waiting for transfers between devices, ring_gather(): parts[j] = lax.ppermute(parts[j], axis, cw if clockwise else ccw)  51.1 us
    ppermute x28, starting transfers between devices, ring_gather(): parts[j] = lax.ppermute(parts[j], axis, cw if clockwise else ccw)  30.7 us
    dot_general x2, matrix products, section_forward(): pre_act = jnp.dot(normed, weight, preferred_element_type=jnp.float32)  10.6 us
    dot_general x2, matrix products, section_backward(): lax.dot_general(grad_pre, weight, (((1,), (1,)), ((), ())), preferred_ele...  9.43 us
    ppermute x3, waiting for transfers between devices, tree_sum(): v = v + lax.ppermute(v, axis, [(i, i ^ b) for i in range(n)])  5.57 us
    ppermute x3, waiting for transfers between devices, shifted(): return lax.ppermute(x, axis, pairs)  4.49 us
    ppermute x3, starting transfers between devices, tree_sum(): v = v + lax.ppermute(v, axis, [(i, i ^ b) for i in range(n)])  4.45 us
    ppermute x3, starting transfers between devices, shifted(): return lax.ppermute(x, axis, pairs)  4.31 us
  transfers between devices with their start and end apart: 34, of which 21 were waited for; matrix products, arithmetic and copies ran while one was open for 9% of the time, Pallas kernels for 0%

profile of v6, /device:TPU:0, one launch (start us, length us, event | category | flops | bytes accessed | tf_op | source)
XLA Modules:
  0.0 147.7 jit_solution(2648585384928790621)
XLA Ops:
  0.6 1.3 fusion.53
  1.9 3.1 %collective-permute-start = (bf16[256,512]{1,0:T(8,128)(2,1)S(1)}, bf16[256,512]{1,0:T(8,128)(2,1)S(1)}, u32[]{:S(2)}, u32[]{:S(2)}) collective-permute-start(bf16[256,512]{1,0:T(8,128)(2,1)S(1)} %get-tuple-element.39), channel_id=1, source_target_pairs={{0,4},{4,8},{8,12},{12,14},{14,10},{10,6},{6,2},{2,0},{1,5},{5,9},... | collective-permute-start | bytes 786440 | tf_op jit(solution)/shard_map/ppermute | solution.py:103
  5.0 2.0 %collective-permute-start.2 = (bf16[256,512]{1,0:T(8,128)(2,1)S(1)}, bf16[256,512]{1,0:T(8,128)(2,1)S(1)}, u32[]{:S(2)}, u32[]{:S(2)}) collective-permute-start(bf16[256,512]{1,0:T(8,128)(2,1)S(1)} %get-tuple-element.37), channel_id=1, source_target_pairs={{0,4},{4,8},{8,12},{12,14},{14,10},{10,6},{6,2},{2,0},{1,5},{5,9},... | collective-permute-start | bytes 786440 | tf_op jit(solution)/shard_map/ppermute | solution.py:103
  7.0 5.0 %collective-permute-done = bf16[256,512]{1,0:T(8,128)(2,1)S(1)} collective-permute-done((bf16[256,512]{1,0:T(8,128)(2,1)S(1)}, bf16[256,512]{1,0:T(8,128)(2,1)S(1)}, u32[]{:S(2)}, u32[]{:S(2)}) %collective-permute-start) | collective-permute-done | bytes 262176 | tf_op jit(solution)/shard_map/ppermute | solution.py:103
  12.1 2.1 %collective-permute-start.4 = (bf16[256,512]{1,0:T(8,128)(2,1)S(1)}, bf16[256,512]{1,0:T(8,128)(2,1)S(1)}, u32[]{:S(2)}, u32[]{:S(2)}) collective-permute-start(bf16[256,512]{1,0:T(8,128)(2,1)S(1)} %collective-permute-done), channel_id=1, source_target_pairs={{0,4},{4,8},{8,12},{12,14},{14,10},{10,6},{6,2},{2,0},{1,5},{5,9},... | collective-permute-start | bytes 786440 | tf_op jit(solution)/shard_map/ppermute | solution.py:103
  14.2 3.5 %collective-permute-done.2 = bf16[256,512]{1,0:T(8,128)(2,1)S(1)} collective-permute-done((bf16[256,512]{1,0:T(8,128)(2,1)S(1)}, bf16[256,512]{1,0:T(8,128)(2,1)S(1)}, u32[]{:S(2)}, u32[]{:S(2)}) %collective-permute-start.2) | collective-permute-done | bytes 262176 | tf_op jit(solution)/shard_map/ppermute | solution.py:103
  17.7 2.1 %collective-permute-start.6 = (bf16[256,512]{1,0:T(8,128)(2,1)S(1)}, bf16[256,512]{1,0:T(8,128)(2,1)S(1)}, u32[]{:S(2)}, u32[]{:S(2)}) collective-permute-start(bf16[256,512]{1,0:T(8,128)(2,1)S(1)} %collective-permute-done.2), channel_id=1, source_target_pairs={{0,4},{4,8},{8,12},{12,14},{14,10},{10,6},{6,2},{2,0},{1,5},{5,9},... | collective-permute-start | bytes 786440 | tf_op jit(solution)/shard_map/ppermute | solution.py:103
  21.0 2.3 %collective-permute-done.4 = bf16[256,512]{1,0:T(8,128)(2,1)S(1)} collective-permute-done((bf16[256,512]{1,0:T(8,128)(2,1)S(1)}, bf16[256,512]{1,0:T(8,128)(2,1)S(1)}, u32[]{:S(2)}, u32[]{:S(2)}) %collective-permute-start.4) | collective-permute-done | bytes 262176 | tf_op jit(solution)/shard_map/ppermute | solution.py:103
  23.3 2.1 %collective-permute-start.8 = (bf16[256,512]{1,0:T(8,128)(2,1)S(1)}, bf16[256,512]{1,0:T(8,128)(2,1)S(1)}, u32[]{:S(2)}, u32[]{:S(2)}) collective-permute-start(bf16[256,512]{1,0:T(8,128)(2,1)S(1)} %collective-permute-done.4), channel_id=1, source_target_pairs={{0,4},{4,8},{8,12},{12,14},{14,10},{10,6},{6,2},{2,0},{1,5},{5,9},... | collective-permute-start | bytes 786440 | tf_op jit(solution)/shard_map/ppermute | solution.py:103
  25.4 3.5 %collective-permute-done.6 = bf16[256,512]{1,0:T(8,128)(2,1)S(1)} collective-permute-done((bf16[256,512]{1,0:T(8,128)(2,1)S(1)}, bf16[256,512]{1,0:T(8,128)(2,1)S(1)}, u32[]{:S(2)}, u32[]{:S(2)}) %collective-permute-start.6) | collective-permute-done | bytes 262176 | tf_op jit(solution)/shard_map/ppermute | solution.py:103
  28.9 2.1 %collective-permute-start.10 = (bf16[256,512]{1,0:T(8,128)(2,1)S(1)}, bf16[256,512]{1,0:T(8,128)(2,1)S(1)}, u32[]{:S(2)}, u32[]{:S(2)}) collective-permute-start(bf16[256,512]{1,0:T(8,128)(2,1)S(1)} %collective-permute-done.6), channel_id=1, source_target_pairs={{0,4},{4,8},{8,12},{12,14},{14,10},{10,6},{6,2},{2,0},{1,5},{5,9},... | collective-permute-start | bytes 786440 | tf_op jit(solution)/shard_map/ppermute | solution.py:103
  31.2 3.4 %collective-permute-done.8 = bf16[256,512]{1,0:T(8,128)(2,1)S(1)} collective-permute-done((bf16[256,512]{1,0:T(8,128)(2,1)S(1)}, bf16[256,512]{1,0:T(8,128)(2,1)S(1)}, u32[]{:S(2)}, u32[]{:S(2)}) %collective-permute-start.8) | collective-permute-done | bytes 262176 | tf_op jit(solution)/shard_map/ppermute | solution.py:103
  34.5 2.1 %collective-permute-start.12 = (bf16[256,512]{1,0:T(8,128)(2,1)S(1)}, bf16[256,512]{1,0:T(8,128)(2,1)S(1)}, u32[]{:S(2)}, u32[]{:S(2)}) collective-permute-start(bf16[256,512]{1,0:T(8,128)(2,1)S(1)} %collective-permute-done.8), channel_id=1, source_target_pairs={{0,4},{4,8},{8,12},{12,14},{14,10},{10,6},{6,2},{2,0},{1,5},{5,9},... | collective-permute-start | bytes 786440 | tf_op jit(solution)/shard_map/ppermute | solution.py:103
  36.7 3.5 %collective-permute-done.10 = bf16[256,512]{1,0:T(8,128)(2,1)S(1)} collective-permute-done((bf16[256,512]{1,0:T(8,128)(2,1)S(1)}, bf16[256,512]{1,0:T(8,128)(2,1)S(1)}, u32[]{:S(2)}, u32[]{:S(2)}) %collective-permute-start.10) | collective-permute-done | bytes 262176 | tf_op jit(solution)/shard_map/ppermute | solution.py:103
  40.2 2.1 %collective-permute-start.14 = (bf16[256,512]{1,0:T(8,128)(2,1)S(1)}, bf16[256,512]{1,0:T(8,128)(2,1)S(1)}, u32[]{:S(2)}, u32[]{:S(2)}) collective-permute-start(bf16[256,512]{1,0:T(8,128)(2,1)S(1)} %collective-permute-done.10), channel_id=1, source_target_pairs={{0,4},{4,8},{8,12},{12,14},{14,10},{10,6},{6,2},{2,0},{1,5},{5,9},... | collective-permute-start | bytes 786440 | tf_op jit(solution)/shard_map/ppermute | solution.py:103
  42.4 3.4 %collective-permute-done.12 = bf16[256,512]{1,0:T(8,128)(2,1)S(1)} collective-permute-done((bf16[256,512]{1,0:T(8,128)(2,1)S(1)}, bf16[256,512]{1,0:T(8,128)(2,1)S(1)}, u32[]{:S(2)}, u32[]{:S(2)}) %collective-permute-start.12) | collective-permute-done | bytes 262176 | tf_op jit(solution)/shard_map/ppermute | solution.py:103
  45.8 2.1 %collective-permute-start.16 = (bf16[256,512]{1,0:T(8,128)(2,1)S(1)}, bf16[256,512]{1,0:T(8,128)(2,1)S(1)}, u32[]{:S(2)}, u32[]{:S(2)}) collective-permute-start(bf16[256,512]{1,0:T(8,128)(2,1)S(1)} %collective-permute-done.12), channel_id=1, source_target_pairs={{0,4},{4,8},{8,12},{12,14},{14,10},{10,6},{6,2},{2,0},{1,5},{5,9},... | collective-permute-start | bytes 786440 | tf_op jit(solution)/shard_map/ppermute | solution.py:103
  48.0 3.4 %collective-permute-done.14 = bf16[256,512]{1,0:T(8,128)(2,1)S(1)} collective-permute-done((bf16[256,512]{1,0:T(8,128)(2,1)S(1)}, bf16[256,512]{1,0:T(8,128)(2,1)S(1)}, u32[]{:S(2)}, u32[]{:S(2)}) %collective-permute-start.14) | collective-permute-done | bytes 262176 | tf_op jit(solution)/shard_map/ppermute | solution.py:103
  51.4 2.1 %collective-permute-start.18 = (bf16[256,512]{1,0:T(8,128)(2,1)S(1)}, bf16[256,512]{1,0:T(8,128)(2,1)S(1)}, u32[]{:S(2)}, u32[]{:S(2)}) collective-permute-start(bf16[256,512]{1,0:T(8,128)(2,1)S(1)} %collective-permute-done.14), channel_id=1, source_target_pairs={{0,4},{4,8},{8,12},{12,14},{14,10},{10,6},{6,2},{2,0},{1,5},{5,9},... | collective-permute-start | bytes 786440 | tf_op jit(solution)/shard_map/ppermute | solution.py:103
  53.6 3.4 %collective-permute-done.16 = bf16[256,512]{1,0:T(8,128)(2,1)S(1)} collective-permute-done((bf16[256,512]{1,0:T(8,128)(2,1)S(1)}, bf16[256,512]{1,0:T(8,128)(2,1)S(1)}, u32[]{:S(2)}, u32[]{:S(2)}) %collective-permute-start.16) | collective-permute-done | bytes 262176 | tf_op jit(solution)/shard_map/ppermute | solution.py:103
  57.0 2.1 %collective-permute-start.20 = (bf16[256,512]{1,0:T(8,128)(2,1)S(1)}, bf16[256,512]{1,0:T(8,128)(2,1)S(1)}, u32[]{:S(2)}, u32[]{:S(2)}) collective-permute-start(bf16[256,512]{1,0:T(8,128)(2,1)S(1)} %collective-permute-done.16), channel_id=1, source_target_pairs={{0,4},{4,8},{8,12},{12,14},{14,10},{10,6},{6,2},{2,0},{1,5},{5,9},... | collective-permute-start | bytes 786440 | tf_op jit(solution)/shard_map/ppermute | solution.py:103
  59.3 3.4 %collective-permute-done.18 = bf16[256,512]{1,0:T(8,128)(2,1)S(1)} collective-permute-done((bf16[256,512]{1,0:T(8,128)(2,1)S(1)}, bf16[256,512]{1,0:T(8,128)(2,1)S(1)}, u32[]{:S(2)}, u32[]{:S(2)}) %collective-permute-start.18) | collective-permute-done | bytes 262176 | tf_op jit(solution)/shard_map/ppermute | solution.py:103
  62.6 2.1 %collective-permute-start.22 = (bf16[256,512]{1,0:T(8,128)(2,1)S(1)}, bf16[256,512]{1,0:T(8,128)(2,1)S(1)}, u32[]{:S(2)}, u32[]{:S(2)}) collective-permute-start(bf16[256,512]{1,0:T(8,128)(2,1)S(1)} %collective-permute-done.18), channel_id=1, source_target_pairs={{0,4},{4,8},{8,12},{12,14},{14,10},{10,6},{6,2},{2,0},{1,5},{5,9},... | collective-permute-start | bytes 786440 | tf_op jit(solution)/shard_map/ppermute | solution.py:103
  64.9 3.4 %collective-permute-done.20 = bf16[256,512]{1,0:T(8,128)(2,1)S(1)} collective-permute-done((bf16[256,512]{1,0:T(8,128)(2,1)S(1)}, bf16[256,512]{1,0:T(8,128)(2,1)S(1)}, u32[]{:S(2)}, u32[]{:S(2)}) %collective-permute-start.20) | collective-permute-done | bytes 262176 | tf_op jit(solution)/shard_map/ppermute | solution.py:103
  68.3 2.1 %collective-permute-start.24 = (bf16[256,512]{1,0:T(8,128)(2,1)S(1)}, bf16[256,512]{1,0:T(8,128)(2,1)S(1)}, u32[]{:S(2)}, u32[]{:S(2)}) collective-permute-start(bf16[256,512]{1,0:T(8,128)(2,1)S(1)} %collective-permute-done.20), channel_id=1, source_target_pairs={{0,4},{4,8},{8,12},{12,14},{14,10},{10,6},{6,2},{2,0},{1,5},{5,9},... | collective-permute-start | bytes 786440 | tf_op jit(solution)/shard_map/ppermute | solution.py:103
  70.5 3.4 %collective-permute-done.22 = bf16[256,512]{1,0:T(8,128)(2,1)S(1)} collective-permute-done((bf16[256,512]{1,0:T(8,128)(2,1)S(1)}, bf16[256,512]{1,0:T(8,128)(2,1)S(1)}, u32[]{:S(2)}, u32[]{:S(2)}) %collective-permute-start.22) | collective-permute-done | bytes 262176 | tf_op jit(solution)/shard_map/ppermute | solution.py:103
  73.9 2.1 %collective-permute-start.26 = (bf16[256,512]{1,0:T(8,128)(2,1)S(1)}, bf16[256,512]{1,0:T(8,128)(2,1)S(1)}, u32[]{:S(2)}, u32[]{:S(2)}) collective-permute-start(bf16[256,512]{1,0:T(8,128)(2,1)S(1)} %collective-permute-done.22), channel_id=1, source_target_pairs={{0,4},{4,8},{8,12},{12,14},{14,10},{10,6},{6,2},{2,0},{1,5},{5,9},... | collective-permute-start | bytes 786440 | tf_op jit(solution)/shard_map/ppermute | solution.py:103
  76.1 3.4 %collective-permute-done.24 = bf16[256,512]{1,0:T(8,128)(2,1)S(1)} collective-permute-done((bf16[256,512]{1,0:T(8,128)(2,1)S(1)}, bf16[256,512]{1,0:T(8,128)(2,1)S(1)}, u32[]{:S(2)}, u32[]{:S(2)}) %collective-permute-start.24) | collective-permute-done | bytes 262176 | tf_op jit(solution)/shard_map/ppermute | solution.py:103
  79.5 2.1 %collective-permute-done.25 = bf16[256,512]{1,0:T(8,128)(2,1)S(1)} collective-permute-done((bf16[256,512]{1,0:T(8,128)(2,1)S(1)}, bf16[256,512]{1,0:T(8,128)(2,1)S(1)}, u32[]{:S(2)}, u32[]{:S(2)}) %collective-permute-start.25) | collective-permute-done | bytes 262176 | tf_op jit(solution)/shard_map/ppermute | solution.py:103
  81.6 2.6 %collective-permute-done.26 = bf16[256,512]{1,0:T(8,128)(2,1)S(1)} collective-permute-done((bf16[256,512]{1,0:T(8,128)(2,1)S(1)}, bf16[256,512]{1,0:T(8,128)(2,1)S(1)}, u32[]{:S(2)}, u32[]{:S(2)}) %collective-permute-start.26) | collective-permute-done | bytes 262176 | tf_op jit(solution)/shard_map/ppermute | solution.py:103
  84.3 1.5 %collective-permute-done.27 = bf16[256,512]{1,0:T(8,128)(2,1)S(1)} collective-permute-done((bf16[256,512]{1,0:T(8,128)(2,1)S(1)}, bf16[256,512]{1,0:T(8,128)(2,1)S(1)}, u32[]{:S(2)}, u32[]{:S(2)}) %collective-permute-start.27) | collective-permute-done | bytes 262176 | tf_op jit(solution)/shard_map/ppermute | solution.py:103
  87.1 5.1 %fusion.21 = (f32[256,2048]{1,0:T(8,128)}, bf16[256,2048]{1,0:T(8,128)(2,1)S(1)}) fusion(bf16[2,128,2048]{2,1,0:T(8,128)(2,1)S(1)} %copy-done, bf16[256,2048]{1,0:T(8,128)(2,1)S(1)} %fusion.35, bf16[2048,2048]{1,0:T(8,128)(2,1)S(1)} %constant_dynamic-update-slice_fusion.21), kind=kOutput, calls=%fused_computation.32 | convolution fusion | flops 2158493696 | bytes 13631488 | tf_op jit(solution)/shard_map/dot_general | solution.py:40
  92.2 1.5 %collective-permute-start.28 = (bf16[256,2048]{1,0:T(8,128)(2,1)S(1)}, bf16[256,2048]{1,0:T(8,128)(2,1)S(1)}, u32[]{:S(2)}, u32[]{:S(2)}) collective-permute-start(bf16[256,2048]{1,0:T(8,128)(2,1)S(1)} %get-tuple-element.33), channel_id=1, source_target_pairs={{0,1},{2,3},{4,5},{6,7},{8,9},{10,11},{12,13},{14,15},{16,17},{18,... | collective-permute-start | bytes 3145736 | tf_op jit(solution)/shard_map/ppermute | solution.py:18
  96.4 5.5 %fusion.51 = (f32[256,2048]{1,0:T(8,128)S(1)}, bf16[256,2048]{1,0:T(8,128)(2,1)}, f32[256,2048]{1,0:T(8,128)}) fusion(bf16[256,2048]{1,0:T(8,128)(2,1)S(1)} %collective-permute-done.28, bf16[2048,2048]{1,0:T(8,128)(2,1)S(1)} %constant_dynamic-update-slice_fusion.21, f32[256]{0:T(256)S(1)} %add_rsqrt_fusion, f32[256]{0:T(256)S(1)} %broadcast_multiply_fusion.4, ...), kind=kOutput, calls=%fused_computation.122 | convolution fusion | flops 2161639424 | bytes 14690304 | tf_op jit(solution)/shard_map/dot_general | solution.py:40
  103.7 1.6 %slice_convert_fusion.1 = (f32[128,2048]{1,0:T(8,128)S(1)}, f32[128,2048]{1,0:T(8,128)S(1)}) fusion(bf16[256,2048]{1,0:T(8,128)(2,1)} %get-tuple-element.30), kind=kLoop, calls=%fused_computation.71 | loop fusion | flops 524288 | bytes 3145728 | tf_op jit(solution)/shard_map/convert_element_type | solution.py:192
  105.2 1.7 %collective-permute-done.29 = f32[7]{0:T(128)S(1)} collective-permute-done((f32[7]{0:T(128)S(1)}, f32[7]{0:T(128)S(1)}, u32[]{:S(2)}, u32[]{:S(2)}) %collective-permute-start.29) | collective-permute-done | bytes 60 | tf_op jit(solution)/shard_map/ppermute | solution.py:116
  107.7 1.6 %collective-permute-start.30 = (f32[7]{0:T(128)S(1)}, f32[7]{0:T(128)S(1)}, u32[]{:S(2)}, u32[]{:S(2)}) collective-permute-start(f32[7]{0:T(128)S(1)} %fusion.61), channel_id=1, source_target_pairs={{0,4},{2,6},{4,0},{6,2},{8,12},{10,14},{12,8},{14,10},{1,5},{3,7},... | collective-permute-start | bytes 92 | tf_op jit(solution)/shard_map/ppermute | solution.py:116
  109.2 2.0 %collective-permute-done.30 = f32[7]{0:T(128)S(1)} collective-permute-done((f32[7]{0:T(128)S(1)}, f32[7]{0:T(128)S(1)}, u32[]{:S(2)}, u32[]{:S(2)}) %collective-permute-start.30) | collective-permute-done | bytes 60 | tf_op jit(solution)/shard_map/ppermute | solution.py:116
  111.2 2.6 %collective-permute-start.31 = (f32[7]{0:T(128)S(1)}, f32[7]{0:T(128)S(1)}, u32[]{:S(2)}, u32[]{:S(2)}) collective-permute-start(f32[7]{0:T(128)S(1)} %add.304), channel_id=1, source_target_pairs={{0,8},{2,10},{4,12},{6,14},{8,0},{10,2},{12,4},{14,6},{1,9},{3,11}... | collective-permute-start | bytes 92 | tf_op jit(solution)/shard_map/ppermute | solution.py:116
  113.8 1.9 %collective-permute-done.31 = f32[7]{0:T(128)S(1)} collective-permute-done((f32[7]{0:T(128)S(1)}, f32[7]{0:T(128)S(1)}, u32[]{:S(2)}, u32[]{:S(2)}) %collective-permute-start.31) | collective-permute-done | bytes 60 | tf_op jit(solution)/shard_map/ppermute | solution.py:116
  123.8 2.1 %fusion.28 = bf16[256,2048]{1,0:T(8,128)(2,1)S(1)} fusion(f32[256,2048]{1,0:T(8,128)} %get-tuple-element.14, f32[128,2048]{1,0:T(8,128)S(1)} %get-tuple-element.35, f32[256]{0:T(256)S(1)} %broadcast_bitcast_fusion, f32[128,2048]{1,0:T(8,128)S(1)} %get-tuple-element.34, f32[256]{0:T(256)S(1)} %broadcast_bitcast_fusion.1, ...), kind=kLoop, calls=%fused_computation.42 | loop fusion | flops 3670016 | bytes 6294528 | tf_op jit(solution)/shard_map/convert_element_type | solution.py:46
  125.9 2.8 %fusion.50 = (f32[256]{0:T(256)S(1)}, f32[256]{0:T(256)S(1)}, f32[256,2048]{1,0:T(8,128)S(1)}) fusion(f32[256]{0:T(256)S(1)} %add_rsqrt_fusion, f32[256]{0:T(256)S(1)} %broadcast_multiply_fusion.4, bf16[256,2048]{1,0:T(8,128)(2,1)S(1)} %collective-permute-done.28, f32[2048]{0:T(1024)S(1)} %bitcast.95, bf16[256,2048]{1,0:T(8,128)(2,1)S(1)} %fusion.28, ...), kind=kOutput, calls=%fused_computation.121 | convolution fusion | flops 2151153152 | bytes 12595200 | tf_op jit(solution)/shard_map/dot_general | solution.py:47
  128.7 2.1 %fusion.10 = bf16[256,2048]{1,0:T(8,128)(2,1)} fusion(bf16[256,2048]{1,0:T(8,128)(2,1)S(1)} %collective-permute-done.28, f32[256,2048]{1,0:T(8,128)S(1)} %get-tuple-element.49, f32[256]{0:T(256)S(1)} %broadcast_multiply_fusion.2, f32[256]{0:T(256)S(1)} %broadcast_multiply_fusion.3, f32[128,2048]{1,0:T(8,128)S(1)} %get-tuple-element.35, ...), kind=kLoop, calls=%fused_computation.21 | loop fusion | flops 7340032 | bytes 7347200 | tf_op jit(solution)/shard_map/convert_element_type | solution.py:56
  130.9 1.3 collective-permute-start.32
  132.2 3.4 %collective-permute-done.32 = bf16[256,2048]{1,0:T(8,128)(2,1)S(1)} collective-permute-done((bf16[256,2048]{1,0:T(8,128)(2,1)}, bf16[256,2048]{1,0:T(8,128)(2,1)S(1)}, u32[]{:S(2)}, u32[]{:S(2)}) %collective-permute-start.32) | collective-permute-done | bytes 1048608 | tf_op jit(solution)/shard_map/ppermute | solution.py:18
  135.6 1.5 %collective-permute-start.33 = (f32[1]{0:T(128)}, f32[1]{0:T(128)}, u32[]{:S(2)}, u32[]{:S(2)}) collective-permute-start(f32[1]{0:T(128)} %sub.150), channel_id=1, source_target_pairs={{1,0},{3,2},{5,4},{7,6},{9,8},{11,10},{13,12},{15,14},{17,16},{19,... | collective-permute-start | bytes 20 | tf_op jit(solution)/shard_map/ppermute | solution.py:18
  137.1 6.7 %fusion.49 = (f32[256]{0:T(256)S(1)}, f32[256]{0:T(256)S(1)}, f32[256,2048]{1,0:T(8,128)S(1)}) fusion(f32[256]{0:T(256)S(1)} %rsqrt_bitcast_fusion, f32[256]{0:T(256)S(1)} %get-tuple-element.40, bf16[2,128,2048]{2,1,0:T(8,128)(2,1)S(1)} %copy-done, f32[2048]{0:T(1024)S(1)} %bitcast.96, bf16[2048,2048]{1,0:T(8,128)(2,1)} %copy-done.1, ...), kind=kOutput, calls=%fused_computation.120 | convolution fusion | flops 2152726016 | bytes 14692352 | tf_op jit(solution)/shard_map/dot_general | solution.py:47
  143.8 2.0 %fusion.40 = bf16[256,2048]{1,0:T(8,128)(2,1)} fusion(bf16[256,2048]{1,0:T(8,128)(2,1)} %fusion.10, bf16[2,128,2048]{2,1,0:T(8,128)(2,1)S(1)} %copy-done, f32[256,2048]{1,0:T(8,128)S(1)} %get-tuple-element.50, bf16[256,2048]{1,0:T(8,128)(2,1)S(1)} %collective-permute-done.32, f32[256]{0:T(256)S(1)} %broadcast_multiply_fusion, ...), kind=kLoop, calls=%fused_computation.58 | loop fusion | flops 5767168 | bytes 6295553 | tf_op jit(solution)/shard_map/jit(_where)/select_n | solution.py:201
  (101 shorter events, 9.7 us)
Async XLA Ops:
  1.9 10.2 %collective-permute-start = (bf16[256,512]{1,0:T(8,128)(2,1)S(1)}, bf16[256,512]{1,0:T(8,128)(2,1)S(1)}, u32[]{:S(2)}, u32[]{:S(2)}) collective-permute-start(bf16[256,512]{1,0:T(8,128)(2,1)S(1)} %get-tuple-element.39), channel_id=1, source_target_pairs={{0,4},{4,8},{8,12},{12,14},{14,10},{10,6},{6,2},{2,0},{1,5},{5,9},... | collective-permute-start | bytes 786440 | tf_op jit(solution)/shard_map/ppermute | solution.py:103
  5.0 9.2 %collective-permute-start.1 = (bf16[256,512]{1,0:T(8,128)(2,1)S(1)}, bf16[256,512]{1,0:T(8,128)(2,1)S(1)}, u32[]{:S(2)}, u32[]{:S(2)}) collective-permute-start(bf16[256,512]{1,0:T(8,128)(2,1)S(1)} %get-tuple-element.38), channel_id=1, source_target_pairs={{4,0},{8,4},{12,8},{14,12},{10,14},{6,10},{2,6},{0,2},{5,1},{9,5},... | collective-permute-start | bytes 786440 | tf_op jit(solution)/shard_map/ppermute | solution.py:103
  5.0 12.7 %collective-permute-start.2 = (bf16[256,512]{1,0:T(8,128)(2,1)S(1)}, bf16[256,512]{1,0:T(8,128)(2,1)S(1)}, u32[]{:S(2)}, u32[]{:S(2)}) collective-permute-start(bf16[256,512]{1,0:T(8,128)(2,1)S(1)} %get-tuple-element.37), channel_id=1, source_target_pairs={{0,4},{4,8},{8,12},{12,14},{14,10},{10,6},{6,2},{2,0},{1,5},{5,9},... | collective-permute-start | bytes 786440 | tf_op jit(solution)/shard_map/ppermute | solution.py:103
  7.0 12.8 %collective-permute-start.3 = (bf16[256,512]{1,0:T(8,128)(2,1)S(1)}, bf16[256,512]{1,0:T(8,128)(2,1)S(1)}, u32[]{:S(2)}, u32[]{:S(2)}) collective-permute-start(bf16[256,512]{1,0:T(8,128)(2,1)S(1)} %get-tuple-element.36), channel_id=1, source_target_pairs={{4,0},{8,4},{12,8},{14,12},{10,14},{6,10},{2,6},{0,2},{5,1},{9,5},... | collective-permute-start | bytes 786440 | tf_op jit(solution)/shard_map/ppermute | solution.py:103
  12.1 11.2 %collective-permute-start.4 = (bf16[256,512]{1,0:T(8,128)(2,1)S(1)}, bf16[256,512]{1,0:T(8,128)(2,1)S(1)}, u32[]{:S(2)}, u32[]{:S(2)}) collective-permute-start(bf16[256,512]{1,0:T(8,128)(2,1)S(1)} %collective-permute-done), channel_id=1, source_target_pairs={{0,4},{4,8},{8,12},{12,14},{14,10},{10,6},{6,2},{2,0},{1,5},{5,9},... | collective-permute-start | bytes 786440 | tf_op jit(solution)/shard_map/ppermute | solution.py:103
  14.2 11.2 %collective-permute-start.5 = (bf16[256,512]{1,0:T(8,128)(2,1)S(1)}, bf16[256,512]{1,0:T(8,128)(2,1)S(1)}, u32[]{:S(2)}, u32[]{:S(2)}) collective-permute-start(bf16[256,512]{1,0:T(8,128)(2,1)S(1)} %collective-permute-done.1), channel_id=1, source_target_pairs={{4,0},{8,4},{12,8},{14,12},{10,14},{6,10},{2,6},{0,2},{5,1},{9,5},... | collective-permute-start | bytes 786440 | tf_op jit(solution)/shard_map/ppermute | solution.py:103
  17.7 11.2 %collective-permute-start.6 = (bf16[256,512]{1,0:T(8,128)(2,1)S(1)}, bf16[256,512]{1,0:T(8,128)(2,1)S(1)}, u32[]{:S(2)}, u32[]{:S(2)}) collective-permute-start(bf16[256,512]{1,0:T(8,128)(2,1)S(1)} %collective-permute-done.2), channel_id=1, source_target_pairs={{0,4},{4,8},{8,12},{12,14},{14,10},{10,6},{6,2},{2,0},{1,5},{5,9},... | collective-permute-start | bytes 786440 | tf_op jit(solution)/shard_map/ppermute | solution.py:103
  19.8 11.2 %collective-permute-start.7 = (bf16[256,512]{1,0:T(8,128)(2,1)S(1)}, bf16[256,512]{1,0:T(8,128)(2,1)S(1)}, u32[]{:S(2)}, u32[]{:S(2)}) collective-permute-start(bf16[256,512]{1,0:T(8,128)(2,1)S(1)} %collective-permute-done.3), channel_id=1, source_target_pairs={{4,0},{8,4},{12,8},{14,12},{10,14},{6,10},{2,6},{0,2},{5,1},{9,5},... | collective-permute-start | bytes 786440 | tf_op jit(solution)/shard_map/ppermute | solution.py:103
  23.3 11.2 %collective-permute-start.8 = (bf16[256,512]{1,0:T(8,128)(2,1)S(1)}, bf16[256,512]{1,0:T(8,128)(2,1)S(1)}, u32[]{:S(2)}, u32[]{:S(2)}) collective-permute-start(bf16[256,512]{1,0:T(8,128)(2,1)S(1)} %collective-permute-done.4), channel_id=1, source_target_pairs={{0,4},{4,8},{8,12},{12,14},{14,10},{10,6},{6,2},{2,0},{1,5},{5,9},... | collective-permute-start | bytes 786440 | tf_op jit(solution)/shard_map/ppermute | solution.py:103
  25.4 11.2 %collective-permute-start.9 = (bf16[256,512]{1,0:T(8,128)(2,1)S(1)}, bf16[256,512]{1,0:T(8,128)(2,1)S(1)}, u32[]{:S(2)}, u32[]{:S(2)}) collective-permute-start(bf16[256,512]{1,0:T(8,128)(2,1)S(1)} %collective-permute-done.5), channel_id=1, source_target_pairs={{4,0},{8,4},{12,8},{14,12},{10,14},{6,10},{2,6},{0,2},{5,1},{9,5},... | collective-permute-start | bytes 786440 | tf_op jit(solution)/shard_map/ppermute | solution.py:103
  28.9 11.2 %collective-permute-start.10 = (bf16[256,512]{1,0:T(8,128)(2,1)S(1)}, bf16[256,512]{1,0:T(8,128)(2,1)S(1)}, u32[]{:S(2)}, u32[]{:S(2)}) collective-permute-start(bf16[256,512]{1,0:T(8,128)(2,1)S(1)} %collective-permute-done.6), channel_id=1, source_target_pairs={{0,4},{4,8},{8,12},{12,14},{14,10},{10,6},{6,2},{2,0},{1,5},{5,9},... | collective-permute-start | bytes 786440 | tf_op jit(solution)/shard_map/ppermute | solution.py:103
  31.0 11.2 %collective-permute-start.11 = (bf16[256,512]{1,0:T(8,128)(2,1)S(1)}, bf16[256,512]{1,0:T(8,128)(2,1)S(1)}, u32[]{:S(2)}, u32[]{:S(2)}) collective-permute-start(bf16[256,512]{1,0:T(8,128)(2,1)S(1)} %collective-permute-done.7), channel_id=1, source_target_pairs={{4,0},{8,4},{12,8},{14,12},{10,14},{6,10},{2,6},{0,2},{5,1},{9,5},... | collective-permute-start | bytes 786440 | tf_op jit(solution)/shard_map/ppermute | solution.py:103
  34.5 11.2 %collective-permute-start.12 = (bf16[256,512]{1,0:T(8,128)(2,1)S(1)}, bf16[256,512]{1,0:T(8,128)(2,1)S(1)}, u32[]{:S(2)}, u32[]{:S(2)}) collective-permute-start(bf16[256,512]{1,0:T(8,128)(2,1)S(1)} %collective-permute-done.8), channel_id=1, source_target_pairs={{0,4},{4,8},{8,12},{12,14},{14,10},{10,6},{6,2},{2,0},{1,5},{5,9},... | collective-permute-start | bytes 786440 | tf_op jit(solution)/shard_map/ppermute | solution.py:103
  36.7 11.2 %collective-permute-start.13 = (bf16[256,512]{1,0:T(8,128)(2,1)S(1)}, bf16[256,512]{1,0:T(8,128)(2,1)S(1)}, u32[]{:S(2)}, u32[]{:S(2)}) collective-permute-start(bf16[256,512]{1,0:T(8,128)(2,1)S(1)} %collective-permute-done.9), channel_id=1, source_target_pairs={{4,0},{8,4},{12,8},{14,12},{10,14},{6,10},{2,6},{0,2},{5,1},{9,5},... | collective-permute-start | bytes 786440 | tf_op jit(solution)/shard_map/ppermute | solution.py:103
  40.2 11.2 %collective-permute-start.14 = (bf16[256,512]{1,0:T(8,128)(2,1)S(1)}, bf16[256,512]{1,0:T(8,128)(2,1)S(1)}, u32[]{:S(2)}, u32[]{:S(2)}) collective-permute-start(bf16[256,512]{1,0:T(8,128)(2,1)S(1)} %collective-permute-done.10), channel_id=1, source_target_pairs={{0,4},{4,8},{8,12},{12,14},{14,10},{10,6},{6,2},{2,0},{1,5},{5,9},... | collective-permute-start | bytes 786440 | tf_op jit(solution)/shard_map/ppermute | solution.py:103
  42.3 11.3 %collective-permute-start.15 = (bf16[256,512]{1,0:T(8,128)(2,1)S(1)}, bf16[256,512]{1,0:T(8,128)(2,1)S(1)}, u32[]{:S(2)}, u32[]{:S(2)}) collective-permute-start(bf16[256,512]{1,0:T(8,128)(2,1)S(1)} %collective-permute-done.11), channel_id=1, source_target_pairs={{4,0},{8,4},{12,8},{14,12},{10,14},{6,10},{2,6},{0,2},{5,1},{9,5},... | collective-permute-start | bytes 786440 | tf_op jit(solution)/shard_map/ppermute | solution.py:103
  45.8 11.2 %collective-permute-start.16 = (bf16[256,512]{1,0:T(8,128)(2,1)S(1)}, bf16[256,512]{1,0:T(8,128)(2,1)S(1)}, u32[]{:S(2)}, u32[]{:S(2)}) collective-permute-start(bf16[256,512]{1,0:T(8,128)(2,1)S(1)} %collective-permute-done.12), channel_id=1, source_target_pairs={{0,4},{4,8},{8,12},{12,14},{14,10},{10,6},{6,2},{2,0},{1,5},{5,9},... | collective-permute-start | bytes 786440 | tf_op jit(solution)/shard_map/ppermute | solution.py:103
  47.9 11.3 %collective-permute-start.17 = (bf16[256,512]{1,0:T(8,128)(2,1)S(1)}, bf16[256,512]{1,0:T(8,128)(2,1)S(1)}, u32[]{:S(2)}, u32[]{:S(2)}) collective-permute-start(bf16[256,512]{1,0:T(8,128)(2,1)S(1)} %collective-permute-done.13), channel_id=1, source_target_pairs={{4,0},{8,4},{12,8},{14,12},{10,14},{6,10},{2,6},{0,2},{5,1},{9,5},... | collective-permute-start | bytes 786440 | tf_op jit(solution)/shard_map/ppermute | solution.py:103
  51.4 11.2 %collective-permute-start.18 = (bf16[256,512]{1,0:T(8,128)(2,1)S(1)}, bf16[256,512]{1,0:T(8,128)(2,1)S(1)}, u32[]{:S(2)}, u32[]{:S(2)}) collective-permute-start(bf16[256,512]{1,0:T(8,128)(2,1)S(1)} %collective-permute-done.14), channel_id=1, source_target_pairs={{0,4},{4,8},{8,12},{12,14},{14,10},{10,6},{6,2},{2,0},{1,5},{5,9},... | collective-permute-start | bytes 786440 | tf_op jit(solution)/shard_map/ppermute | solution.py:103
  53.5 11.2 %collective-permute-start.19 = (bf16[256,512]{1,0:T(8,128)(2,1)S(1)}, bf16[256,512]{1,0:T(8,128)(2,1)S(1)}, u32[]{:S(2)}, u32[]{:S(2)}) collective-permute-start(bf16[256,512]{1,0:T(8,128)(2,1)S(1)} %collective-permute-done.15), channel_id=1, source_target_pairs={{4,0},{8,4},{12,8},{14,12},{10,14},{6,10},{2,6},{0,2},{5,1},{9,5},... | collective-permute-start | bytes 786440 | tf_op jit(solution)/shard_map/ppermute | solution.py:103
  57.0 11.2 %collective-permute-start.20 = (bf16[256,512]{1,0:T(8,128)(2,1)S(1)}, bf16[256,512]{1,0:T(8,128)(2,1)S(1)}, u32[]{:S(2)}, u32[]{:S(2)}) collective-permute-start(bf16[256,512]{1,0:T(8,128)(2,1)S(1)} %collective-permute-done.16), channel_id=1, source_target_pairs={{0,4},{4,8},{8,12},{12,14},{14,10},{10,6},{6,2},{2,0},{1,5},{5,9},... | collective-permute-start | bytes 786440 | tf_op jit(solution)/shard_map/ppermute | solution.py:103
  59.2 11.2 %collective-permute-start.21 = (bf16[256,512]{1,0:T(8,128)(2,1)S(1)}, bf16[256,512]{1,0:T(8,128)(2,1)S(1)}, u32[]{:S(2)}, u32[]{:S(2)}) collective-permute-start(bf16[256,512]{1,0:T(8,128)(2,1)S(1)} %collective-permute-done.17), channel_id=1, source_target_pairs={{4,0},{8,4},{12,8},{14,12},{10,14},{6,10},{2,6},{0,2},{5,1},{9,5},... | collective-permute-start | bytes 786440 | tf_op jit(solution)/shard_map/ppermute | solution.py:103
  62.6 11.2 %collective-permute-start.22 = (bf16[256,512]{1,0:T(8,128)(2,1)S(1)}, bf16[256,512]{1,0:T(8,128)(2,1)S(1)}, u32[]{:S(2)}, u32[]{:S(2)}) collective-permute-start(bf16[256,512]{1,0:T(8,128)(2,1)S(1)} %collective-permute-done.18), channel_id=1, source_target_pairs={{0,4},{4,8},{8,12},{12,14},{14,10},{10,6},{6,2},{2,0},{1,5},{5,9},... | collective-permute-start | bytes 786440 | tf_op jit(solution)/shard_map/ppermute | solution.py:103
  64.8 11.2 %collective-permute-start.23 = (bf16[256,512]{1,0:T(8,128)(2,1)S(1)}, bf16[256,512]{1,0:T(8,128)(2,1)S(1)}, u32[]{:S(2)}, u32[]{:S(2)}) collective-permute-start(bf16[256,512]{1,0:T(8,128)(2,1)S(1)} %collective-permute-done.19), channel_id=1, source_target_pairs={{4,0},{8,4},{12,8},{14,12},{10,14},{6,10},{2,6},{0,2},{5,1},{9,5},... | collective-permute-start | bytes 786440 | tf_op jit(solution)/shard_map/ppermute | solution.py:103
  64.9 21.0 %copy-start.4 = (bf16[1,256,2048]{2,1,0:T(8,128)(2,1)S(1)}, bf16[1,256,2048]{2,1,0:T(8,128)(2,1)}, u32[]{:S(2)}) copy-start(bf16[1,256,2048]{2,1,0:T(8,128)(2,1)} %param.6) | copy-start | bytes 3145732
  68.3 11.2 %collective-permute-start.24 = (bf16[256,512]{1,0:T(8,128)(2,1)S(1)}, bf16[256,512]{1,0:T(8,128)(2,1)S(1)}, u32[]{:S(2)}, u32[]{:S(2)}) collective-permute-start(bf16[256,512]{1,0:T(8,128)(2,1)S(1)} %collective-permute-done.20), channel_id=1, source_target_pairs={{0,4},{4,8},{8,12},{12,14},{14,10},{10,6},{6,2},{2,0},{1,5},{5,9},... | collective-permute-start | bytes 786440 | tf_op jit(solution)/shard_map/ppermute | solution.py:103
  70.4 11.2 %collective-permute-start.25 = (bf16[256,512]{1,0:T(8,128)(2,1)S(1)}, bf16[256,512]{1,0:T(8,128)(2,1)S(1)}, u32[]{:S(2)}, u32[]{:S(2)}) collective-permute-start(bf16[256,512]{1,0:T(8,128)(2,1)S(1)} %collective-permute-done.21), channel_id=1, source_target_pairs={{4,0},{8,4},{12,8},{14,12},{10,14},{6,10},{2,6},{0,2},{5,1},{9,5},... | collective-permute-start | bytes 786440 | tf_op jit(solution)/shard_map/ppermute | solution.py:103
  73.9 10.4 %collective-permute-start.26 = (bf16[256,512]{1,0:T(8,128)(2,1)S(1)}, bf16[256,512]{1,0:T(8,128)(2,1)S(1)}, u32[]{:S(2)}, u32[]{:S(2)}) collective-permute-start(bf16[256,512]{1,0:T(8,128)(2,1)S(1)} %collective-permute-done.22), channel_id=1, source_target_pairs={{0,4},{4,8},{8,12},{12,14},{14,10},{10,6},{6,2},{2,0},{1,5},{5,9},... | collective-permute-start | bytes 786440 | tf_op jit(solution)/shard_map/ppermute | solution.py:103
  76.0 9.8 %collective-permute-start.27 = (bf16[256,512]{1,0:T(8,128)(2,1)S(1)}, bf16[256,512]{1,0:T(8,128)(2,1)S(1)}, u32[]{:S(2)}, u32[]{:S(2)}) collective-permute-start(bf16[256,512]{1,0:T(8,128)(2,1)S(1)} %collective-permute-done.23), channel_id=1, source_target_pairs={{4,0},{8,4},{12,8},{14,12},{10,14},{6,10},{2,6},{0,2},{5,1},{9,5},... | collective-permute-start | bytes 786440 | tf_op jit(solution)/shard_map/ppermute | solution.py:103
  76.1 9.9 %copy-start = (bf16[2,128,2048]{2,1,0:T(8,128)(2,1)S(1)}, bf16[2,128,2048]{2,1,0:T(8,128)(2,1)}, u32[]{:S(2)}) copy-start(bf16[2,128,2048]{2,1,0:T(8,128)(2,1)} %param.4) | copy-start | bytes 3145732
  85.8 0.8 copy-start.5
  86.0 10.4 %copy-start.1 = (bf16[2048,2048]{1,0:T(8,128)(2,1)}, bf16[2048,2048]{1,0:T(8,128)(2,1)S(1)}, u32[]{:S(2)}) copy-start(bf16[2048,2048]{1,0:T(8,128)(2,1)S(1)} %constant_dynamic-update-slice_fusion.21) | copy-start | bytes 25165828
  87.1 6.7 %copy-start.3 = (bf16[128,2048]{1,0:T(8,128)(2,1)S(1)}, bf16[128,2048]{1,0:T(8,128)(2,1)}, u32[]{:S(2)}) copy-start(bf16[128,2048]{1,0:T(8,128)(2,1)} %param.5) | copy-start | bytes 1572868
  92.2 3.6 %collective-permute-start.28 = (bf16[256,2048]{1,0:T(8,128)(2,1)S(1)}, bf16[256,2048]{1,0:T(8,128)(2,1)S(1)}, u32[]{:S(2)}, u32[]{:S(2)}) collective-permute-start(bf16[256,2048]{1,0:T(8,128)(2,1)S(1)} %get-tuple-element.33), channel_id=1, source_target_pairs={{0,1},{2,3},{4,5},{6,7},{8,9},{10,11},{12,13},{14,15},{16,17},{18,... | collective-permute-start | bytes 3145736 | tf_op jit(solution)/shard_map/ppermute | solution.py:18
  103.4 3.6 %collective-permute-start.29 = (f32[7]{0:T(128)S(1)}, f32[7]{0:T(128)S(1)}, u32[]{:S(2)}, u32[]{:S(2)}) collective-permute-start(f32[7]{0:T(128)S(1)} %pad_maximum_fusion.1), channel_id=1, source_target_pairs={{0,2},{2,0},{4,6},{6,4},{8,10},{10,8},{12,14},{14,12},{1,3},{3,1},... | collective-permute-start | bytes 92 | tf_op jit(solution)/shard_map/ppermute | solution.py:116
  103.7 22.3 %copy-start.2 = (bf16[2048,2048]{1,0:T(8,128)(2,1)S(1)}, bf16[2048,2048]{1,0:T(8,128)(2,1)}, u32[]{:S(2)}) copy-start(bf16[2048,2048]{1,0:T(8,128)(2,1)} %copy-done.1) | copy-start | bytes 25165828
  107.7 3.6 %collective-permute-start.30 = (f32[7]{0:T(128)S(1)}, f32[7]{0:T(128)S(1)}, u32[]{:S(2)}, u32[]{:S(2)}) collective-permute-start(f32[7]{0:T(128)S(1)} %fusion.61), channel_id=1, source_target_pairs={{0,4},{2,6},{4,0},{6,2},{8,12},{10,14},{12,8},{14,10},{1,5},{3,7},... | collective-permute-start | bytes 92 | tf_op jit(solution)/shard_map/ppermute | solution.py:116
  111.2 4.5 %collective-permute-start.31 = (f32[7]{0:T(128)S(1)}, f32[7]{0:T(128)S(1)}, u32[]{:S(2)}, u32[]{:S(2)}) collective-permute-start(f32[7]{0:T(128)S(1)} %add.304), channel_id=1, source_target_pairs={{0,8},{2,10},{4,12},{6,14},{8,0},{10,2},{12,4},{14,6},{1,9},{3,11}... | collective-permute-start | bytes 92 | tf_op jit(solution)/shard_map/ppermute | solution.py:116
  130.9 4.8 %collective-permute-start.32 = (bf16[256,2048]{1,0:T(8,128)(2,1)}, bf16[256,2048]{1,0:T(8,128)(2,1)S(1)}, u32[]{:S(2)}, u32[]{:S(2)}) collective-permute-start(bf16[256,2048]{1,0:T(8,128)(2,1)} %fusion.10), channel_id=1, source_target_pairs={{1,0},{3,2},{5,4},{7,6},{9,8},{11,10},{13,12},{15,14},{17,16},{19,... | collective-permute-start | bytes 3145736 | tf_op jit(solution)/shard_map/ppermute | solution.py:18
  135.6 10.2 %collective-permute-start.33 = (f32[1]{0:T(128)}, f32[1]{0:T(128)}, u32[]{:S(2)}, u32[]{:S(2)}) collective-permute-start(f32[1]{0:T(128)} %sub.150), channel_id=1, source_target_pairs={{1,0},{3,2},{5,4},{7,6},{9,8},{11,10},{13,12},{15,14},{17,16},{19,... | collective-permute-start | bytes 20 | tf_op jit(solution)/shard_map/ppermute | solution.py:18

commit v7 on v6

--- a/solution.py
+++ b/solution.py
@@ -28,6 +28,16 @@
     return 0.5 * (1.0 + inner) + 0.5 * pre_act * (1.0 - inner * inner) * gelu_scale * (
         1.0 + 3.0 * cubic_term * pre_act * pre_act
     )
+
+
+def norm_part(rows_in, gain):
+    values = rows_in.astype(jnp.float32)
+    row_mean = jnp.mean(values, axis=-1, keepdims=True)
+    centred = values - row_mean
+    inv_std = lax.rsqrt(jnp.mean(centred * centred, axis=-1, keepdims=True) + epsilon)
+    unit_rows = centred * inv_std
+    normed = (unit_rows * gain).astype(jnp.bfloat16)
+    return (values, unit_rows, inv_std, normed)
 
 
 def section_forward(rows_in, gain, weight):
@@ -77,7 +87,7 @@
     return list(range(0, n, 2)) + list(range(n - 1, 0, -2))
 
 
-def ring_gather(local, axis, pieces=2):
+def ring_gather(local, axis, pieces=2, on_piece=None):
     n = lax.axis_size(axis)
     rows, cols = local.shape
     if n == 1 or n % 2:
@@ -103,6 +113,8 @@
             parts[j] = lax.ppermute(parts[j], axis, cw if clockwise else ccw)
             origin = from_cw if clockwise else from_ccw
             full = lax.dynamic_update_slice(full, parts[j], (origin * rows, j * width))
+            if on_piece is not None:
+                on_piece(origin, j, parts[j])
     full, local = lax.optimization_barrier((full, local))
     return lax.dynamic_update_slice(full, local, (me * rows, 0))
 
@@ -159,16 +171,42 @@
 
     obs_sq = jnp.einsum("rd,rd->", obs, obs, preferred_element_type=jnp.float32)
 
-    if RING_GATHER:
-        weight = ring_gather(weights[0], "tok")
-    else:
-        weight = lax.all_gather(weights, "tok", axis=1, tiled=True)[0]
-
-    inputs, weight = lax.optimization_barrier((inputs, weight))
     members = inputs.shape[0]
     rows_all = inputs.reshape(members * tok_rows, width)
-
-    fa = section_forward(rows_all, gain, weight)
+    n_tok = lax.axis_size("tok")
+    local = weights[0]
+    rows_w = local.shape[0]
+    pieces = 2
+    piece_w = width // (2 * pieces)
+    overlap = RING_GATHER and n_tok % 2 == 0 and 2 < n_tok <= 16
+
+    if overlap:
+        values_a, unit_a, std_a, normed_a = norm_part(rows_all, gain)
+        acc = [None] * (2 * pieces)
+
+        def on_piece(origin, j, piece):
+            lhs = lax.dynamic_slice(normed_a, (0, origin * rows_w), (normed_a.shape[0], rows_w))
+            term = jnp.dot(lhs, piece, preferred_element_type=jnp.float32)
+            acc[j] = term if acc[j] is None else acc[j] + term
+
+        weight = ring_gather(local, "tok", pieces, on_piece)
+        me = lax.axis_index("tok")
+        lhs = lax.dynamic_slice(normed_a, (0, me * rows_w), (normed_a.shape[0], rows_w))
+        for j in range(2 * pieces):
+            acc[j] = acc[j] + jnp.dot(
+                lhs, local[:, j * piece_w:(j + 1) * piece_w], preferred_element_type=jnp.float32
+            )
+        pre_a = jnp.concatenate(acc, axis=1)
+        out_a = (values_a + gelu_value(pre_a)).astype(jnp.bfloat16)
+        fa = (out_a, unit_a, std_a, pre_a)
+    else:
+        if RING_GATHER:
+            weight = ring_gather(local, "tok")
+        else:
+            weight = lax.all_gather(weights, "tok", axis=1, tiled=True)[0]
+        inputs, weight = lax.optimization_barrier((inputs, weight))
+        rows_all = inputs.reshape(members * tok_rows, width)
+        fa = section_forward(rows_all, gain, weight)
     arrived = shifted(fa[0], "section", 1)
     fb = section_forward(arrived, gain, weight)
 

time: 150 us -> 155 us (1.033)
  the two profiles are of different devices: /device:TPU:0 before, /device:TPU:1 now
where the time goes in v7:
time: 155 us; the launch traced here: 154 us
  waiting for transfers between devices  49.1 us (32%)
  starting transfers between devices  37 us (24%)
  matrix products  31.1 us (20%)
  other arithmetic  17 us (11%)
  local copies, waits for them, and re-layouts  10 us (6%)
  between operations  9.87 us (6%)
    ppermute x28, waiting for transfers between devices, ring_gather(): parts[j] = lax.ppermute(parts[j], axis, cw if clockwise else ccw)  38.5 us
    ppermute x28, starting transfers between devices, ring_gather(): parts[j] = lax.ppermute(parts[j], axis, cw if clockwise else ccw)  23.3 us
    dot_general x2, matrix products, section_backward(): lax.dot_general(grad_pre, weight, (((1,), (1,)), ((), ())), preferred_ele...  13.1 us
    ppermute x3, starting transfers between devices, shifted(): return lax.ppermute(x, axis, pairs)  10.1 us
    dot_general x28, matrix products, on_piece(): term = jnp.dot(lhs, piece, preferred_element_type=jnp.float32)  9.21 us
    ppermute x3, waiting for transfers between devices, shifted(): return lax.ppermute(x, axis, pairs)  7.48 us
    dot_general x1, matrix products, section_forward(): pre_act = jnp.dot(normed, weight, preferred_element_type=jnp.float32)  5.49 us
    dynamic_update_slice x28, local copies, waits for them, and re-layouts, ring_gather(): full = lax.dynamic_update_slice(full, parts[j], (origin * rows, j * width))  3.64 us
  transfers between devices with their start and end apart: 34, of which 27 were waited for; matrix products, arithmetic and copies ran while one was open for 21% of the time, Pallas kernels for 0%

profile of v7, /device:TPU:1, one launch (start us, length us, event | category | flops | bytes accessed | tf_op | source)
XLA Modules:
  0.0 154.1 jit_solution(3774598841935122023)
XLA Ops:
  0.6 2.3 %fusion.133 = (bf16[256,512]{1,0:T(8,128)(2,1)}, bf16[256,512]{1,0:T(8,128)(2,1)}, bf16[256,512]{1,0:T(8,128)(2,1)}, bf16[256,512]{1,0:T(8,128)(2,1)}) fusion(bf16[256,2048]{1,0:T(8,128)(2,1)} %bitcast.116), kind=kLoop, calls=%fused_computation.228 | loop fusion | bytes 2097152 | tf_op jit(solution)/shard_map/slice | solution.py:106
  3.0 2.1 %collective-permute-start = (bf16[256,512]{1,0:T(8,128)(2,1)}, bf16[256,512]{1,0:T(8,128)(2,1)}, u32[]{:S(2)}, u32[]{:S(2)}) collective-permute-start(bf16[256,512]{1,0:T(8,128)(2,1)} %get-tuple-element.32), channel_id=1, source_target_pairs={{0,4},{4,8},{8,12},{12,14},{14,10},{10,6},{6,2},{2,0},{1,5},{5,9},... | collective-permute-start | bytes 786440 | tf_op jit(solution)/shard_map/ppermute | solution.py:113
  5.1 1.5 collective-permute-start.14
  11.7 2.2 %convert_element_type.66 = f32[128,2048]{1,0:T(8,128)} convert(bf16[128,2048]{1,0:T(8,128)(2,1)} %param.5) | non-fusion elementwise | flops 262144 | bytes 1572864 | tf_op jit(solution)/shard_map/convert_element_type | solution.py:214
  14.1 1.5 collective-permute-start.1
  15.7 1.1 broadcast_in_dim.2
  17.7 1.2 fusion.90
  20.0 1.2 fusion.63
  21.2 1.5 collective-permute-start.15
  23.7 1.2 fusion.87
  25.2 1.5 collective-permute-start.2
  27.2 1.2 collective-permute-start.16
  28.5 1.9 %collective-permute-done.22 = bf16[256,512]{1,0:T(8,128)(2,1)S(1)} collective-permute-done((bf16[256,512]{1,0:T(8,128)(2,1)S(1)}, bf16[256,512]{1,0:T(8,128)(2,1)S(1)}, u32[]{:S(2)}, u32[]{:S(2)}) %collective-permute-start.22) | collective-permute-done | bytes 262176 | tf_op jit(solution)/shard_map/ppermute | solution.py:113
  31.4 2.2 %collective-permute-done.2 = bf16[256,512]{1,0:T(8,128)(2,1)S(1)} collective-permute-done((bf16[256,512]{1,0:T(8,128)(2,1)S(1)}, bf16[256,512]{1,0:T(8,128)(2,1)S(1)}, u32[]{:S(2)}, u32[]{:S(2)}) %collective-permute-start.2) | collective-permute-done | bytes 262176 | tf_op jit(solution)/shard_map/ppermute | solution.py:113
  33.6 1.4 collective-permute-start.3
  36.1 3.2 %collective-permute-done.16 = bf16[256,512]{1,0:T(8,128)(2,1)S(1)} collective-permute-done((bf16[256,512]{1,0:T(8,128)(2,1)S(1)}, bf16[256,512]{1,0:T(8,128)(2,1)S(1)}, u32[]{:S(2)}, u32[]{:S(2)}) %collective-permute-start.16) | collective-permute-done | bytes 262176 | tf_op jit(solution)/shard_map/ppermute | solution.py:113
  39.2 1.4 collective-permute-start.17
  42.6 2.2 %collective-permute-done.3 = bf16[256,512]{1,0:T(8,128)(2,1)S(1)} collective-permute-done((bf16[256,512]{1,0:T(8,128)(2,1)S(1)}, bf16[256,512]{1,0:T(8,128)(2,1)S(1)}, u32[]{:S(2)}, u32[]{:S(2)}) %collective-permute-start.3) | collective-permute-done | bytes 262176 | tf_op jit(solution)/shard_map/ppermute | solution.py:113
  44.8 1.4 collective-permute-start.4
  47.3 3.2 %collective-permute-done.17 = bf16[256,512]{1,0:T(8,128)(2,1)S(1)} collective-permute-done((bf16[256,512]{1,0:T(8,128)(2,1)S(1)}, bf16[256,512]{1,0:T(8,128)(2,1)S(1)}, u32[]{:S(2)}, u32[]{:S(2)}) %collective-permute-start.17) | collective-permute-done | bytes 262176 | tf_op jit(solution)/shard_map/ppermute | solution.py:113
  50.4 1.4 collective-permute-start.18
  54.0 2.1 %collective-permute-done.4 = bf16[256,512]{1,0:T(8,128)(2,1)S(1)} collective-permute-done((bf16[256,512]{1,0:T(8,128)(2,1)S(1)}, bf16[256,512]{1,0:T(8,128)(2,1)S(1)}, u32[]{:S(2)}, u32[]{:S(2)}) %collective-permute-start.4) | collective-permute-done | bytes 262176 | tf_op jit(solution)/shard_map/ppermute | solution.py:113
  56.1 1.4 collective-permute-start.5
  58.5 3.2 %collective-permute-done.18 = bf16[256,512]{1,0:T(8,128)(2,1)S(1)} collective-permute-done((bf16[256,512]{1,0:T(8,128)(2,1)S(1)}, bf16[256,512]{1,0:T(8,128)(2,1)S(1)}, u32[]{:S(2)}, u32[]{:S(2)}) %collective-permute-start.18) | collective-permute-done | bytes 262176 | tf_op jit(solution)/shard_map/ppermute | solution.py:113
  61.7 1.4 collective-permute-start.19
  65.2 2.1 %collective-permute-done.5 = bf16[256,512]{1,0:T(8,128)(2,1)S(1)} collective-permute-done((bf16[256,512]{1,0:T(8,128)(2,1)S(1)}, bf16[256,512]{1,0:T(8,128)(2,1)S(1)}, u32[]{:S(2)}, u32[]{:S(2)}) %collective-permute-start.5) | collective-permute-done | bytes 262176 | tf_op jit(solution)/shard_map/ppermute | solution.py:113
  67.3 1.4 collective-permute-start.6
  69.8 3.2 %collective-permute-done.19 = bf16[256,512]{1,0:T(8,128)(2,1)S(1)} collective-permute-done((bf16[256,512]{1,0:T(8,128)(2,1)S(1)}, bf16[256,512]{1,0:T(8,128)(2,1)S(1)}, u32[]{:S(2)}, u32[]{:S(2)}) %collective-permute-start.19) | collective-permute-done | bytes 262176 | tf_op jit(solution)/shard_map/ppermute | solution.py:113
  72.9 1.4 collective-permute-start.20
  76.4 2.2 %collective-permute-done.6 = bf16[256,512]{1,0:T(8,128)(2,1)S(1)} collective-permute-done((bf16[256,512]{1,0:T(8,128)(2,1)S(1)}, bf16[256,512]{1,0:T(8,128)(2,1)S(1)}, u32[]{:S(2)}, u32[]{:S(2)}) %collective-permute-start.6) | collective-permute-done | bytes 262176 | tf_op jit(solution)/shard_map/ppermute | solution.py:113
  78.8 1.9 %collective-permute-done.13 = bf16[256,512]{1,0:T(8,128)(2,1)S(1)} collective-permute-done((bf16[256,512]{1,0:T(8,128)(2,1)S(1)}, bf16[256,512]{1,0:T(8,128)(2,1)S(1)}, u32[]{:S(2)}, u32[]{:S(2)}) %collective-permute-start.13) | collective-permute-done | bytes 262176 | tf_op jit(solution)/shard_map/ppermute | solution.py:113
  80.9 3.2 %collective-permute-done.20 = bf16[256,512]{1,0:T(8,128)(2,1)S(1)} collective-permute-done((bf16[256,512]{1,0:T(8,128)(2,1)S(1)}, bf16[256,512]{1,0:T(8,128)(2,1)S(1)}, u32[]{:S(2)}, u32[]{:S(2)}) %collective-permute-start.20) | collective-permute-done | bytes 262176 | tf_op jit(solution)/shard_map/ppermute | solution.py:113
  84.4 1.9 %collective-permute-done.27 = bf16[256,512]{1,0:T(8,128)(2,1)S(1)} collective-permute-done((bf16[256,512]{1,0:T(8,128)(2,1)S(1)}, bf16[256,512]{1,0:T(8,128)(2,1)S(1)}, u32[]{:S(2)}, u32[]{:S(2)}) %collective-permute-start.27) | collective-permute-done | bytes 262176 | tf_op jit(solution)/shard_map/ppermute | solution.py:113
  86.6 2.5 %fusion.21 = (f32[256,2048]{1,0:T(8,128)}, bf16[256,2048]{1,0:T(8,128)(2,1)S(1)}) fusion(f32[256,512]{1,0:T(8,128)S(1)} %fusion.40, f32[256,512]{1,0:T(8,128)S(1)} %fusion.41, f32[256,512]{1,0:T(8,128)S(1)} %fusion.42, f32[256,512]{1,0:T(8,128)S(1)} %fusion.43, bf16[2,128,2048]{2,1,0:T(8,128)(2,1)S(1)} %copy-done), kind=kLoop, calls=%fused_computation.32 | loop fusion | flops 12582912 | bytes 6291456 | tf_op jit(solution)/shard_map/add | solution.py:28
  89.0 1.5 collective-permute-start.28
  90.9 5.1 %collective-permute-done.28 = bf16[256,2048]{1,0:T(8,128)(2,1)S(1)} collective-permute-done((bf16[256,2048]{1,0:T(8,128)(2,1)S(1)}, bf16[256,2048]{1,0:T(8,128)(2,1)S(1)}, u32[]{:S(2)}, u32[]{:S(2)}) %collective-permute-start.28) | collective-permute-done | bytes 1048608 | tf_op jit(solution)/shard_map/ppermute | solution.py:18
  96.6 5.5 %fusion.131 = (f32[256,2048]{1,0:T(8,128)S(1)}, bf16[256,2048]{1,0:T(8,128)(2,1)}, f32[256,2048]{1,0:T(8,128)}) fusion(bf16[256,2048]{1,0:T(8,128)(2,1)S(1)} %collective-permute-done.28, bf16[2048,2048]{1,0:T(8,128)(2,1)S(1)} %constant_dynamic-update-slice_fusion, f32[256]{0:T(256)S(1)} %add_rsqrt_fusion, f32[256]{0:T(256)S(1)} %broadcast_multiply_fusion.4, ...), kind=kOutput, calls=%fused_computation.227 | convolution fusion | flops 2161639424 | bytes 14690304 | tf_op jit(solution)/shard_map/dot_general | solution.py:50
  103.7 1.4 slice_convert_fusion.1
  106.9 1.3 collective-permute-start.30
  108.2 1.1 collective-permute-done.30
  109.3 2.3 %collective-permute-start.31 = (f32[7]{0:T(128)S(1)}, f32[7]{0:T(128)S(1)}, u32[]{:S(2)}, u32[]{:S(2)}) collective-permute-start(f32[7]{0:T(128)S(1)} %add.445), channel_id=1, source_target_pairs={{0,8},{2,10},{4,12},{6,14},{8,0},{10,2},{12,4},{14,6},{1,9},{3,11}... | collective-permute-start | bytes 92 | tf_op jit(solution)/shard_map/ppermute | solution.py:128
  121.9 6.0 %fusion.130 = (f32[256]{0:T(256)S(1)}, f32[256]{0:T(256)S(1)}, f32[256,2048]{1,0:T(8,128)S(1)}) fusion(f32[256]{0:T(256)S(1)} %add_rsqrt_fusion, f32[256]{0:T(256)S(1)} %broadcast_multiply_fusion.4, bf16[256,2048]{1,0:T(8,128)(2,1)S(1)} %copy-done.4, f32[2048]{0:T(1024)S(1)} %bitcast.125, bf16[256,2048]{1,0:T(8,128)(2,1)S(1)} %fusion.28, ...), kind=kOutput, calls=%fused_computation.226 | convolution fusion | flops 2151153152 | bytes 12595200 | tf_op jit(solution)/shard_map/dot_general | solution.py:57
  127.9 2.1 %fusion.10 = bf16[256,2048]{1,0:T(8,128)(2,1)} fusion(bf16[256,2048]{1,0:T(8,128)(2,1)S(1)} %copy-done.4, f32[256,2048]{1,0:T(8,128)S(1)} %get-tuple-element.45, f32[256]{0:T(256)S(1)} %broadcast_multiply_fusion.2, f32[256]{0:T(256)S(1)} %broadcast_multiply_fusion.3, f32[128,2048]{1,0:T(8,128)S(1)} %get-tuple-element.31, f32[256]{0:T(256)S(1)} %broadcast_bitcast_fusion, ...), kind=kLoop, calls=%fused_computation.21 | loop fusion | flops 7340032 | bytes 7347200 | tf_op jit(solution)/shard_map/convert_element_type | solution.py:66
  130.0 5.5 %collective-permute-start.32 = (bf16[256,2048]{1,0:T(8,128)(2,1)}, bf16[256,2048]{1,0:T(8,128)(2,1)S(1)}, u32[]{:S(2)}, u32[]{:S(2)}) collective-permute-start(bf16[256,2048]{1,0:T(8,128)(2,1)} %fusion.10), channel_id=1, source_target_pairs={{1,0},{3,2},{5,4},{7,6},{9,8},{11,10},{13,12},{15,14},{17,16},{19,... | collective-permute-start | bytes 3145736 | tf_op jit(solution)/shard_map/ppermute | solution.py:18
  135.6 2.4 %collective-permute-done.32 = bf16[256,2048]{1,0:T(8,128)(2,1)S(1)} collective-permute-done((bf16[256,2048]{1,0:T(8,128)(2,1)}, bf16[256,2048]{1,0:T(8,128)(2,1)S(1)}, u32[]{:S(2)}, u32[]{:S(2)}) %collective-permute-start.32) | collective-permute-done | bytes 1048608 | tf_op jit(solution)/shard_map/ppermute | solution.py:18
  139.0 3.1 %collective-permute-start.33 = (f32[1]{0:T(128)}, f32[1]{0:T(128)}, u32[]{:S(2)}, u32[]{:S(2)}) collective-permute-start(f32[1]{0:T(128)} %sub.150), channel_id=1, source_target_pairs={{1,0},{3,2},{5,4},{7,6},{9,8},{11,10},{13,12},{15,14},{17,16},{19,... | collective-permute-start | bytes 20 | tf_op jit(solution)/shard_map/ppermute | solution.py:18
  142.0 7.1 %fusion.129 = (f32[256]{0:T(256)S(1)}, f32[256]{0:T(256)S(1)}, f32[256,2048]{1,0:T(8,128)S(1)}) fusion(f32[256]{0:T(256)S(1)} %rsqrt_bitcast_fusion, f32[256]{0:T(256)S(1)} %get-tuple-element.36, bf16[2,128,2048]{2,1,0:T(8,128)(2,1)S(1)} %copy-done, f32[2048]{0:T(1024)S(1)} %bitcast.126, bf16[2048,2048]{1,0:T(8,128)(2,1)} %copy-done.5, ...), kind=kOutput, calls=%fused_computation.225 | convolution fusion | flops 2152726016 | bytes 14692352 | tf_op jit(solution)/shard_map/dot_general | solution.py:57
  149.1 3.2 %fusion.44 = bf16[256,2048]{1,0:T(8,128)(2,1)} fusion(bf16[256,2048]{1,0:T(8,128)(2,1)} %fusion.10, bf16[2,128,2048]{2,1,0:T(8,128)(2,1)S(1)} %copy-done, f32[256,2048]{1,0:T(8,128)S(1)} %get-tuple-element.46, bf16[256,2048]{1,0:T(8,128)(2,1)S(1)} %copy-done.13, f32[256]{0:T(256)S(1)} %broadcast_multiply_fusion, f32[256]{0:T(256)S(1)} %broadcast_multiply_fusion.1, ...), kind=kLoop, calls=%fused_computation.87 | loop fusion | flops 5767168 | bytes 6295553 | tf_op jit(solution)/shard_map/jit(_where)/select_n | solution.py:239
  (151 shorter events, 31.8 us)
Async XLA Ops:
  0.6 5.9 %copy-start = (bf16[2,128,2048]{2,1,0:T(8,128)(2,1)S(1)}, bf16[2,128,2048]{2,1,0:T(8,128)(2,1)}, u32[]{:S(2)}) copy-start(bf16[2,128,2048]{2,1,0:T(8,128)(2,1)} %param.4) | copy-start | bytes 3145732
  0.6 6.6 %copy-start.14 = (f32[1,2048]{1,0:T(1,128)S(1)}, f32[1,2048]{1,0:T(1,128)}, u32[]{:S(2)}) copy-start(f32[1,2048]{1,0:T(1,128)} %param.7) | copy-start | bytes 24580
  3.0 11.2 %collective-permute-start = (bf16[256,512]{1,0:T(8,128)(2,1)}, bf16[256,512]{1,0:T(8,128)(2,1)}, u32[]{:S(2)}, u32[]{:S(2)}) collective-permute-start(bf16[256,512]{1,0:T(8,128)(2,1)} %get-tuple-element.32), channel_id=1, source_target_pairs={{0,4},{4,8},{8,12},{12,14},{14,10},{10,6},{6,2},{2,0},{1,5},{5,9},... | collective-permute-start | bytes 786440 | tf_op jit(solution)/shard_map/ppermute | solution.py:113
  5.1 13.8 %collective-permute-start.7 = (bf16[256,512]{1,0:T(8,128)(2,1)}, bf16[256,512]{1,0:T(8,128)(2,1)}, u32[]{:S(2)}, u32[]{:S(2)}) collective-permute-start(bf16[256,512]{1,0:T(8,128)(2,1)} %get-tuple-element.35), channel_id=1, source_target_pairs={{4,0},{8,4},{12,8},{14,12},{10,14},{6,10},{2,6},{0,2},{5,1},{9,5},... | collective-permute-start | bytes 786440 | tf_op jit(solution)/shard_map/ppermute | solution.py:113
  5.1 16.1 %collective-permute-start.14 = (bf16[256,512]{1,0:T(8,128)(2,1)}, bf16[256,512]{1,0:T(8,128)(2,1)}, u32[]{:S(2)}, u32[]{:S(2)}) collective-permute-start(bf16[256,512]{1,0:T(8,128)(2,1)} %get-tuple-element.34), channel_id=1, source_target_pairs={{0,4},{4,8},{8,12},{12,14},{14,10},{10,6},{6,2},{2,0},{1,5},{5,9},... | collective-permute-start | bytes 786440 | tf_op jit(solution)/shard_map/ppermute | solution.py:113
  6.5 18.3 %collective-permute-start.21 = (bf16[256,512]{1,0:T(8,128)(2,1)}, bf16[256,512]{1,0:T(8,128)(2,1)S(1)}, u32[]{:S(2)}, u32[]{:S(2)}) collective-permute-start(bf16[256,512]{1,0:T(8,128)(2,1)} %get-tuple-element.33), channel_id=1, source_target_pairs={{4,0},{8,4},{12,8},{14,12},{10,14},{6,10},{2,6},{0,2},{5,1},{9,5},... | collective-permute-start | bytes 786440 | tf_op jit(solution)/shard_map/ppermute | solution.py:113
  6.5 1.2 copy-start.1
  7.2 3.6 %copy-start.6 = (bf16[128,2048]{1,0:T(8,128)(2,1)S(1)}, bf16[128,2048]{1,0:T(8,128)(2,1)}, u32[]{:S(2)}) copy-start(bf16[128,2048]{1,0:T(8,128)(2,1)} %param.5) | copy-start | bytes 1572868
  14.1 11.1 %collective-permute-start.1 = (bf16[256,512]{1,0:T(8,128)(2,1)}, bf16[256,512]{1,0:T(8,128)(2,1)S(1)}, u32[]{:S(2)}, u32[]{:S(2)}) collective-permute-start(bf16[256,512]{1,0:T(8,128)(2,1)} %collective-permute-done), channel_id=1, source_target_pairs={{0,4},{4,8},{8,12},{12,14},{14,10},{10,6},{6,2},{2,0},{1,5},{5,9},... | collective-permute-start | bytes 786440 | tf_op jit(solution)/shard_map/ppermute | solution.py:113
  18.9 7.8 %collective-permute-start.8 = (bf16[256,512]{1,0:T(8,128)(2,1)}, bf16[256,512]{1,0:T(8,128)(2,1)S(1)}, u32[]{:S(2)}, u32[]{:S(2)}) collective-permute-start(bf16[256,512]{1,0:T(8,128)(2,1)} %collective-permute-done.7), channel_id=1, source_target_pairs={{4,0},{8,4},{12,8},{14,12},{10,14},{6,10},{2,6},{0,2},{5,1},{9,5},... | collective-permute-start | bytes 786440 | tf_op jit(solution)/shard_map/ppermute | solution.py:113
  21.2 6.1 %collective-permute-start.15 = (bf16[256,512]{1,0:T(8,128)(2,1)}, bf16[256,512]{1,0:T(8,128)(2,1)S(1)}, u32[]{:S(2)}, u32[]{:S(2)}) collective-permute-start(bf16[256,512]{1,0:T(8,128)(2,1)} %collective-permute-done.14), channel_id=1, source_target_pairs={{0,4},{4,8},{8,12},{12,14},{14,10},{10,6},{6,2},{2,0},{1,5},{5,9},... | collective-permute-start | bytes 786440 | tf_op jit(solution)/shard_map/ppermute | solution.py:113
  24.9 5.6 %collective-permute-start.22 = (bf16[256,512]{1,0:T(8,128)(2,1)S(1)}, bf16[256,512]{1,0:T(8,128)(2,1)S(1)}, u32[]{:S(2)}, u32[]{:S(2)}) collective-permute-start(bf16[256,512]{1,0:T(8,128)(2,1)S(1)} %collective-permute-done.21), channel_id=1, source_target_pairs={{4,0},{8,4},{12,8},{14,12},{10,14},{6,10},{2,6},{0,2},{5,1},{9,5},... | collective-permute-start | bytes 786440 | tf_op jit(solution)/shard_map/ppermute | solution.py:113
  25.2 8.4 %collective-permute-start.2 = (bf16[256,512]{1,0:T(8,128)(2,1)S(1)}, bf16[256,512]{1,0:T(8,128)(2,1)S(1)}, u32[]{:S(2)}, u32[]{:S(2)}) collective-permute-start(bf16[256,512]{1,0:T(8,128)(2,1)S(1)} %collective-permute-done.1), channel_id=1, source_target_pairs={{0,4},{4,8},{8,12},{12,14},{14,10},{10,6},{6,2},{2,0},{1,5},{5,9},... | collective-permute-start | bytes 786440 | tf_op jit(solution)/shard_map/ppermute | solution.py:113
  26.7 9.0 %collective-permute-start.9 = (bf16[256,512]{1,0:T(8,128)(2,1)S(1)}, bf16[256,512]{1,0:T(8,128)(2,1)S(1)}, u32[]{:S(2)}, u32[]{:S(2)}) collective-permute-start(bf16[256,512]{1,0:T(8,128)(2,1)S(1)} %collective-permute-done.8), channel_id=1, source_target_pairs={{4,0},{8,4},{12,8},{14,12},{10,14},{6,10},{2,6},{0,2},{5,1},{9,5},... | collective-permute-start | bytes 786440 | tf_op jit(solution)/shard_map/ppermute | solution.py:113
  27.2 12.0 %collective-permute-start.16 = (bf16[256,512]{1,0:T(8,128)(2,1)S(1)}, bf16[256,512]{1,0:T(8,128)(2,1)S(1)}, u32[]{:S(2)}, u32[]{:S(2)}) collective-permute-start(bf16[256,512]{1,0:T(8,128)(2,1)S(1)} %collective-permute-done.15), channel_id=1, source_target_pairs={{0,4},{4,8},{8,12},{12,14},{14,10},{10,6},{6,2},{2,0},{1,5},{5,9},... | collective-permute-start | bytes 786440 | tf_op jit(solution)/shard_map/ppermute | solution.py:113
  30.4 10.9 %collective-permute-start.23 = (bf16[256,512]{1,0:T(8,128)(2,1)S(1)}, bf16[256,512]{1,0:T(8,128)(2,1)S(1)}, u32[]{:S(2)}, u32[]{:S(2)}) collective-permute-start(bf16[256,512]{1,0:T(8,128)(2,1)S(1)} %collective-permute-done.22), channel_id=1, source_target_pairs={{4,0},{8,4},{12,8},{14,12},{10,14},{6,10},{2,6},{0,2},{5,1},{9,5},... | collective-permute-start | bytes 786440 | tf_op jit(solution)/shard_map/ppermute | solution.py:113
  33.6 11.2 %collective-permute-start.3 = (bf16[256,512]{1,0:T(8,128)(2,1)S(1)}, bf16[256,512]{1,0:T(8,128)(2,1)S(1)}, u32[]{:S(2)}, u32[]{:S(2)}) collective-permute-start(bf16[256,512]{1,0:T(8,128)(2,1)S(1)} %collective-permute-done.2), channel_id=1, source_target_pairs={{0,4},{4,8},{8,12},{12,14},{14,10},{10,6},{6,2},{2,0},{1,5},{5,9},... | collective-permute-start | bytes 786440 | tf_op jit(solution)/shard_map/ppermute | solution.py:113
  35.8 11.2 %collective-permute-start.10 = (bf16[256,512]{1,0:T(8,128)(2,1)S(1)}, bf16[256,512]{1,0:T(8,128)(2,1)S(1)}, u32[]{:S(2)}, u32[]{:S(2)}) collective-permute-start(bf16[256,512]{1,0:T(8,128)(2,1)S(1)} %collective-permute-done.9), channel_id=1, source_target_pairs={{4,0},{8,4},{12,8},{14,12},{10,14},{6,10},{2,6},{0,2},{5,1},{9,5},... | collective-permute-start | bytes 786440 | tf_op jit(solution)/shard_map/ppermute | solution.py:113
  39.2 11.2 %collective-permute-start.17 = (bf16[256,512]{1,0:T(8,128)(2,1)S(1)}, bf16[256,512]{1,0:T(8,128)(2,1)S(1)}, u32[]{:S(2)}, u32[]{:S(2)}) collective-permute-start(bf16[256,512]{1,0:T(8,128)(2,1)S(1)} %collective-permute-done.16), channel_id=1, source_target_pairs={{0,4},{4,8},{8,12},{12,14},{14,10},{10,6},{6,2},{2,0},{1,5},{5,9},... | collective-permute-start | bytes 786440 | tf_op jit(solution)/shard_map/ppermute | solution.py:113
  41.4 11.2 %collective-permute-start.24 = (bf16[256,512]{1,0:T(8,128)(2,1)S(1)}, bf16[256,512]{1,0:T(8,128)(2,1)S(1)}, u32[]{:S(2)}, u32[]{:S(2)}) collective-permute-start(bf16[256,512]{1,0:T(8,128)(2,1)S(1)} %collective-permute-done.23), channel_id=1, source_target_pairs={{4,0},{8,4},{12,8},{14,12},{10,14},{6,10},{2,6},{0,2},{5,1},{9,5},... | collective-permute-start | bytes 786440 | tf_op jit(solution)/shard_map/ppermute | solution.py:113
  44.8 11.2 %collective-permute-start.4 = (bf16[256,512]{1,0:T(8,128)(2,1)S(1)}, bf16[256,512]{1,0:T(8,128)(2,1)S(1)}, u32[]{:S(2)}, u32[]{:S(2)}) collective-permute-start(bf16[256,512]{1,0:T(8,128)(2,1)S(1)} %collective-permute-done.3), channel_id=1, source_target_pairs={{0,4},{4,8},{8,12},{12,14},{14,10},{10,6},{6,2},{2,0},{1,5},{5,9},... | collective-permute-start | bytes 786440 | tf_op jit(solution)/shard_map/ppermute | solution.py:113
  47.0 11.2 %collective-permute-start.11 = (bf16[256,512]{1,0:T(8,128)(2,1)S(1)}, bf16[256,512]{1,0:T(8,128)(2,1)S(1)}, u32[]{:S(2)}, u32[]{:S(2)}) collective-permute-start(bf16[256,512]{1,0:T(8,128)(2,1)S(1)} %collective-permute-done.10), channel_id=1, source_target_pairs={{4,0},{8,4},{12,8},{14,12},{10,14},{6,10},{2,6},{0,2},{5,1},{9,5},... | collective-permute-start | bytes 786440 | tf_op jit(solution)/shard_map/ppermute | solution.py:113
  50.4 11.2 %collective-permute-start.18 = (bf16[256,512]{1,0:T(8,128)(2,1)S(1)}, bf16[256,512]{1,0:T(8,128)(2,1)S(1)}, u32[]{:S(2)}, u32[]{:S(2)}) collective-permute-start(bf16[256,512]{1,0:T(8,128)(2,1)S(1)} %collective-permute-done.17), channel_id=1, source_target_pairs={{0,4},{4,8},{8,12},{12,14},{14,10},{10,6},{6,2},{2,0},{1,5},{5,9},... | collective-permute-start | bytes 786440 | tf_op jit(solution)/shard_map/ppermute | solution.py:113
  52.6 11.2 %collective-permute-start.25 = (bf16[256,512]{1,0:T(8,128)(2,1)S(1)}, bf16[256,512]{1,0:T(8,128)(2,1)S(1)}, u32[]{:S(2)}, u32[]{:S(2)}) collective-permute-start(bf16[256,512]{1,0:T(8,128)(2,1)S(1)} %collective-permute-done.24), channel_id=1, source_target_pairs={{4,0},{8,4},{12,8},{14,12},{10,14},{6,10},{2,6},{0,2},{5,1},{9,5},... | collective-permute-start | bytes 786440 | tf_op jit(solution)/shard_map/ppermute | solution.py:113
  56.1 11.2 %collective-permute-start.5 = (bf16[256,512]{1,0:T(8,128)(2,1)S(1)}, bf16[256,512]{1,0:T(8,128)(2,1)S(1)}, u32[]{:S(2)}, u32[]{:S(2)}) collective-permute-start(bf16[256,512]{1,0:T(8,128)(2,1)S(1)} %collective-permute-done.4), channel_id=1, source_target_pairs={{0,4},{4,8},{8,12},{12,14},{14,10},{10,6},{6,2},{2,0},{1,5},{5,9},... | collective-permute-start | bytes 786440 | tf_op jit(solution)/shard_map/ppermute | solution.py:113
  58.2 11.2 %collective-permute-start.12 = (bf16[256,512]{1,0:T(8,128)(2,1)S(1)}, bf16[256,512]{1,0:T(8,128)(2,1)S(1)}, u32[]{:S(2)}, u32[]{:S(2)}) collective-permute-start(bf16[256,512]{1,0:T(8,128)(2,1)S(1)} %collective-permute-done.11), channel_id=1, source_target_pairs={{4,0},{8,4},{12,8},{14,12},{10,14},{6,10},{2,6},{0,2},{5,1},{9,5},... | collective-permute-start | bytes 786440 | tf_op jit(solution)/shard_map/ppermute | solution.py:113
  61.7 11.2 %collective-permute-start.19 = (bf16[256,512]{1,0:T(8,128)(2,1)S(1)}, bf16[256,512]{1,0:T(8,128)(2,1)S(1)}, u32[]{:S(2)}, u32[]{:S(2)}) collective-permute-start(bf16[256,512]{1,0:T(8,128)(2,1)S(1)} %collective-permute-done.18), channel_id=1, source_target_pairs={{0,4},{4,8},{8,12},{12,14},{14,10},{10,6},{6,2},{2,0},{1,5},{5,9},... | collective-permute-start | bytes 786440 | tf_op jit(solution)/shard_map/ppermute | solution.py:113
  63.9 11.2 %collective-permute-start.26 = (bf16[256,512]{1,0:T(8,128)(2,1)S(1)}, bf16[256,512]{1,0:T(8,128)(2,1)S(1)}, u32[]{:S(2)}, u32[]{:S(2)}) collective-permute-start(bf16[256,512]{1,0:T(8,128)(2,1)S(1)} %collective-permute-done.25), channel_id=1, source_target_pairs={{4,0},{8,4},{12,8},{14,12},{10,14},{6,10},{2,6},{0,2},{5,1},{9,5},... | collective-permute-start | bytes 786440 | tf_op jit(solution)/shard_map/ppermute | solution.py:113
  67.3 11.2 %collective-permute-start.6 = (bf16[256,512]{1,0:T(8,128)(2,1)S(1)}, bf16[256,512]{1,0:T(8,128)(2,1)S(1)}, u32[]{:S(2)}, u32[]{:S(2)}) collective-permute-start(bf16[256,512]{1,0:T(8,128)(2,1)S(1)} %collective-permute-done.5), channel_id=1, source_target_pairs={{0,4},{4,8},{8,12},{12,14},{14,10},{10,6},{6,2},{2,0},{1,5},{5,9},... | collective-permute-start | bytes 786440 | tf_op jit(solution)/shard_map/ppermute | solution.py:113
  69.5 11.2 %collective-permute-start.13 = (bf16[256,512]{1,0:T(8,128)(2,1)S(1)}, bf16[256,512]{1,0:T(8,128)(2,1)S(1)}, u32[]{:S(2)}, u32[]{:S(2)}) collective-permute-start(bf16[256,512]{1,0:T(8,128)(2,1)S(1)} %collective-permute-done.12), channel_id=1, source_target_pairs={{4,0},{8,4},{12,8},{14,12},{10,14},{6,10},{2,6},{0,2},{5,1},{9,5},... | collective-permute-start | bytes 786440 | tf_op jit(solution)/shard_map/ppermute | solution.py:113
  72.9 11.2 %collective-permute-start.20 = (bf16[256,512]{1,0:T(8,128)(2,1)S(1)}, bf16[256,512]{1,0:T(8,128)(2,1)S(1)}, u32[]{:S(2)}, u32[]{:S(2)}) collective-permute-start(bf16[256,512]{1,0:T(8,128)(2,1)S(1)} %collective-permute-done.19), channel_id=1, source_target_pairs={{0,4},{4,8},{8,12},{12,14},{14,10},{10,6},{6,2},{2,0},{1,5},{5,9},... | collective-permute-start | bytes 786440 | tf_op jit(solution)/shard_map/ppermute | solution.py:113
  75.1 11.2 %collective-permute-start.27 = (bf16[256,512]{1,0:T(8,128)(2,1)S(1)}, bf16[256,512]{1,0:T(8,128)(2,1)S(1)}, u32[]{:S(2)}, u32[]{:S(2)}) collective-permute-start(bf16[256,512]{1,0:T(8,128)(2,1)S(1)} %collective-permute-done.26), channel_id=1, source_target_pairs={{4,0},{8,4},{12,8},{14,12},{10,14},{6,10},{2,6},{0,2},{5,1},{9,5},... | collective-permute-start | bytes 786440 | tf_op jit(solution)/shard_map/ppermute | solution.py:113
  75.6 2.9 %copy-start.10 = (f32[256,512]{1,0:T(8,128)S(1)}, f32[256,512]{1,0:T(8,128)}, u32[]{:S(2)}) copy-start(f32[256,512]{1,0:T(8,128)} %fusion.58) | copy-start | bytes 1572868
  75.9 4.9 %copy-start.9 = (f32[256,512]{1,0:T(8,128)S(1)}, f32[256,512]{1,0:T(8,128)}, u32[]{:S(2)}) copy-start(f32[256,512]{1,0:T(8,128)} %fusion.56) | copy-start | bytes 1572868
  76.3 7.8 %copy-start.8 = (f32[256,512]{1,0:T(8,128)S(1)}, f32[256,512]{1,0:T(8,128)}, u32[]{:S(2)}) copy-start(f32[256,512]{1,0:T(8,128)} %fusion.54) | copy-start | bytes 1572868
  89.0 6.9 %collective-permute-start.28 = (bf16[256,2048]{1,0:T(8,128)(2,1)S(1)}, bf16[256,2048]{1,0:T(8,128)(2,1)S(1)}, u32[]{:S(2)}, u32[]{:S(2)}) collective-permute-start(bf16[256,2048]{1,0:T(8,128)(2,1)S(1)} %get-tuple-element.29), channel_id=1, source_target_pairs={{0,1},{2,3},{4,5},{6,7},{8,9},{10,11},{12,13},{14,15},{16,17},{18,... | collective-permute-start | bytes 3145736 | tf_op jit(solution)/shard_map/ppermute | solution.py:18
  90.9 11.3 %copy-start.5 = (bf16[2048,2048]{1,0:T(8,128)(2,1)}, bf16[2048,2048]{1,0:T(8,128)(2,1)S(1)}, u32[]{:S(2)}) copy-start(bf16[2048,2048]{1,0:T(8,128)(2,1)S(1)} %constant_dynamic-update-slice_fusion) | copy-start | bytes 25165828
  95.9 6.2 %copy-start.3 = (bf16[256,2048]{1,0:T(8,128)(2,1)}, bf16[256,2048]{1,0:T(8,128)(2,1)S(1)}, u32[]{:S(2)}) copy-start(bf16[256,2048]{1,0:T(8,128)(2,1)S(1)} %collective-permute-done.28) | copy-start | bytes 3145732
  96.6 5.5 %copy-start.7 = (bf16[128,2048]{1,0:T(8,128)(2,1)S(1)}, bf16[128,2048]{1,0:T(8,128)(2,1)}, u32[]{:S(2)}) copy-start(bf16[128,2048]{1,0:T(8,128)(2,1)} %param.5) | copy-start | bytes 1572868
  102.7 17.9 %copy-start.2 = (f32[128,2048]{1,0:T(8,128)S(1)}, f32[128,2048]{1,0:T(8,128)}, u32[]{:S(2)}) copy-start(f32[128,2048]{1,0:T(8,128)} %convert_element_type.66) | copy-start | bytes 3145732
  102.9 17.8 %copy-start.11 = (f32[256,2048]{1,0:T(8,128)S(1)}, f32[256,2048]{1,0:T(8,128)}, u32[]{:S(2)}) copy-start(f32[256,2048]{1,0:T(8,128)} %get-tuple-element.10) | copy-start | bytes 6291460
  103.7 2.4 %collective-permute-start.29 = (f32[7]{0:T(128)S(1)}, f32[7]{0:T(128)S(1)}, u32[]{:S(2)}, u32[]{:S(2)}) collective-permute-start(f32[7]{0:T(128)S(1)} %pad_maximum_fusion.2), channel_id=1, source_target_pairs={{0,2},{2,0},{4,6},{6,4},{8,10},{10,8},{12,14},{14,12},{1,3},{3,1},... | collective-permute-start | bytes 92 | tf_op jit(solution)/shard_map/ppermute | solution.py:128
  106.9 2.4 %collective-permute-start.30 = (f32[7]{0:T(128)S(1)}, f32[7]{0:T(128)S(1)}, u32[]{:S(2)}, u32[]{:S(2)}) collective-permute-start(f32[7]{0:T(128)S(1)} %fusion.167), channel_id=1, source_target_pairs={{0,4},{2,6},{4,0},{6,2},{8,12},{10,14},{12,8},{14,10},{1,5},{3,7},... | collective-permute-start | bytes 92 | tf_op jit(solution)/shard_map/ppermute | solution.py:128
  109.3 3.3 %collective-permute-start.31 = (f32[7]{0:T(128)S(1)}, f32[7]{0:T(128)S(1)}, u32[]{:S(2)}, u32[]{:S(2)}) collective-permute-start(f32[7]{0:T(128)S(1)} %add.445), channel_id=1, source_target_pairs={{0,8},{2,10},{4,12},{6,14},{8,0},{10,2},{12,4},{14,6},{1,9},{3,11}... | collective-permute-start | bytes 92 | tf_op jit(solution)/shard_map/ppermute | solution.py:128
  120.6 1.2 copy-start.4
  130.0 8.0 %collective-permute-start.32 = (bf16[256,2048]{1,0:T(8,128)(2,1)}, bf16[256,2048]{1,0:T(8,128)(2,1)S(1)}, u32[]{:S(2)}, u32[]{:S(2)}) collective-permute-start(bf16[256,2048]{1,0:T(8,128)(2,1)} %fusion.10), channel_id=1, source_target_pairs={{1,0},{3,2},{5,4},{7,6},{9,8},{11,10},{13,12},{15,14},{17,16},{19,... | collective-permute-start | bytes 3145736 | tf_op jit(solution)/shard_map/ppermute | solution.py:18
  139.0 13.4 %collective-permute-start.33 = (f32[1]{0:T(128)}, f32[1]{0:T(128)}, u32[]{:S(2)}, u32[]{:S(2)}) collective-permute-start(f32[1]{0:T(128)} %sub.150), channel_id=1, source_target_pairs={{1,0},{3,2},{5,4},{7,6},{9,8},{11,10},{13,12},{15,14},{17,16},{19,... | collective-permute-start | bytes 20 | tf_op jit(solution)/shard_map/ppermute | solution.py:18
  142.0 7.1 %copy-start.13 = (bf16[256,2048]{1,0:T(8,128)(2,1)S(1)}, bf16[256,2048]{1,0:T(8,128)(2,1)}, u32[]{:S(2)}) copy-start(bf16[256,2048]{1,0:T(8,128)(2,1)} %copy-done.12) | copy-start | bytes 3145732
  (1 other events, 1.0 us)

commit v8 on v7

--- a/solution.py
+++ b/solution.py
@@ -181,15 +181,20 @@
     overlap = RING_GATHER and n_tok % 2 == 0 and 2 < n_tok <= 16
 
     if overlap:
-        values_a, unit_a, std_a, normed_a = norm_part(rows_all, gain)
         acc = [None] * (2 * pieces)
+        normed = []
 
         def on_piece(origin, j, piece):
+            if not normed:
+                rows_in, piece = lax.optimization_barrier((rows_all, piece))
+                normed.append(norm_part(rows_in, gain))
+            normed_a = normed[0][3]
             lhs = lax.dynamic_slice(normed_a, (0, origin * rows_w), (normed_a.shape[0], rows_w))
             term = jnp.dot(lhs, piece, preferred_element_type=jnp.float32)
             acc[j] = term if acc[j] is None else acc[j] + term
 
         weight = ring_gather(local, "tok", pieces, on_piece)
+        values_a, unit_a, std_a, normed_a = normed[0]
         me = lax.axis_index("tok")
         lhs = lax.dynamic_slice(normed_a, (0, me * rows_w), (normed_a.shape[0], rows_w))
         for j in range(2 * pieces):

time: 155 us -> 149 us (0.961)
  the two profiles are of different devices: /device:TPU:1 before, /device:TPU:0 now
where the time goes in v8:
time: 149 us; the launch traced here: 147 us
  waiting for transfers between devices  52.5 us (35%)
  starting transfers between devices  39.3 us (26%)
  matrix products  23 us (15%)
  other arithmetic  15.3 us (10%)
  between operations  10 us (7%)
  local copies, waits for them, and re-layouts  6.43 us (4%)
    ppermute x28, waiting for transfers between devices, ring_gather(): parts[j] = lax.ppermute(parts[j], axis, cw if clockwise else ccw)  42 us
    ppermute x28, starting transfers between devices, ring_gather(): parts[j] = lax.ppermute(parts[j], axis, cw if clockwise else ccw)  30.4 us
    dot_general x2, matrix products, section_backward(): lax.dot_general(grad_pre, weight, (((1,), (1,)), ((), ())), preferred_ele...  9.32 us
    dot_general x28, matrix products, on_piece(): term = jnp.dot(lhs, piece, preferred_element_type=jnp.float32)  7.31 us
    dot_general x1, matrix products, section_forward(): pre_act = jnp.dot(normed, weight, preferred_element_type=jnp.float32)  5.5 us
    ppermute x3, waiting for transfers between devices, tree_sum(): v = v + lax.ppermute(v, axis, [(i, i ^ b) for i in range(n)])  5.41 us
    ppermute x3, waiting for transfers between devices, shifted(): return lax.ppermute(x, axis, pairs)  5.09 us
    ppermute x3, starting transfers between devices, tree_sum(): v = v + lax.ppermute(v, axis, [(i, i ^ b) for i in range(n)])  4.61 us
  transfers between devices with their start and end apart: 34, of which 24 were waited for; matrix products, arithmetic and copies ran while one was open for 16% of the time, Pallas kernels for 0%

profile of v8, /device:TPU:0, one launch (start us, length us, event | category | flops | bytes accessed | tf_op | source)
XLA Modules:
  0.0 146.6 jit_solution(13685995498046214477)
XLA Ops:
  0.7 2.3 %fusion.132 = (bf16[256,512]{1,0:T(8,128)(2,1)}, bf16[256,512]{1,0:T(8,128)(2,1)}, bf16[256,512]{1,0:T(8,128)(2,1)}, bf16[256,512]{1,0:T(8,128)(2,1)}) fusion(bf16[256,2048]{1,0:T(8,128)(2,1)} %bitcast.94), kind=kLoop, calls=%fused_computation.226 | loop fusion | bytes 2097152 | tf_op jit(solution)/shard_map/slice | solution.py:106
  2.9 3.1 %collective-permute-start = (bf16[256,512]{1,0:T(8,128)(2,1)}, bf16[256,512]{1,0:T(8,128)(2,1)}, u32[]{:S(2)}, u32[]{:S(2)}) collective-permute-start(bf16[256,512]{1,0:T(8,128)(2,1)} %get-tuple-element.39), channel_id=1, source_target_pairs={{0,4},{4,8},{8,12},{12,14},{14,10},{10,6},{6,2},{2,0},{1,5},{5,9},... | collective-permute-start | bytes 786440 | tf_op jit(solution)/shard_map/ppermute | solution.py:113
  6.0 2.0 %collective-permute-start.14 = (bf16[256,512]{1,0:T(8,128)(2,1)}, bf16[256,512]{1,0:T(8,128)(2,1)S(1)}, u32[]{:S(2)}, u32[]{:S(2)}) collective-permute-start(bf16[256,512]{1,0:T(8,128)(2,1)} %get-tuple-element.38), channel_id=1, source_target_pairs={{0,4},{4,8},{8,12},{12,14},{14,10},{10,6},{6,2},{2,0},{1,5},{5,9},... | collective-permute-start | bytes 786440 | tf_op jit(solution)/shard_map/ppermute | solution.py:113
  9.0 4.3 %collective-permute-done = bf16[256,512]{1,0:T(8,128)(2,1)} collective-permute-done((bf16[256,512]{1,0:T(8,128)(2,1)}, bf16[256,512]{1,0:T(8,128)(2,1)}, u32[]{:S(2)}, u32[]{:S(2)}) %collective-permute-start) | collective-permute-done | bytes 262176 | tf_op jit(solution)/shard_map/ppermute | solution.py:113
  15.5 2.2 %collective-permute-start.1 = (bf16[256,512]{1,0:T(8,128)(2,1)}, bf16[256,512]{1,0:T(8,128)(2,1)S(1)}, u32[]{:S(2)}, u32[]{:S(2)}) collective-permute-start(bf16[256,512]{1,0:T(8,128)(2,1)} %collective-permute-done), channel_id=1, source_target_pairs={{0,4},{4,8},{8,12},{12,14},{14,10},{10,6},{6,2},{2,0},{1,5},{5,9},... | collective-permute-start | bytes 786440 | tf_op jit(solution)/shard_map/ppermute | solution.py:113
  17.7 1.1 broadcast_in_dim.2
  19.7 1.2 fusion.90
  21.3 2.1 %collective-permute-start.15 = (bf16[256,512]{1,0:T(8,128)(2,1)S(1)}, bf16[256,512]{1,0:T(8,128)(2,1)S(1)}, u32[]{:S(2)}, u32[]{:S(2)}) collective-permute-start(bf16[256,512]{1,0:T(8,128)(2,1)S(1)} %collective-permute-done.14), channel_id=1, source_target_pairs={{0,4},{4,8},{8,12},{12,14},{14,10},{10,6},{6,2},{2,0},{1,5},{5,9},... | collective-permute-start | bytes 786440 | tf_op jit(solution)/shard_map/ppermute | solution.py:113
  25.0 2.1 %collective-permute-start.2 = (bf16[256,512]{1,0:T(8,128)(2,1)S(1)}, bf16[256,512]{1,0:T(8,128)(2,1)S(1)}, u32[]{:S(2)}, u32[]{:S(2)}) collective-permute-start(bf16[256,512]{1,0:T(8,128)(2,1)S(1)} %collective-permute-done.1), channel_id=1, source_target_pairs={{0,4},{4,8},{8,12},{12,14},{14,10},{10,6},{6,2},{2,0},{1,5},{5,9},... | collective-permute-start | bytes 786440 | tf_op jit(solution)/shard_map/ppermute | solution.py:113
  27.1 3.1 %collective-permute-done.8 = bf16[256,512]{1,0:T(8,128)(2,1)S(1)} collective-permute-done((bf16[256,512]{1,0:T(8,128)(2,1)S(1)}, bf16[256,512]{1,0:T(8,128)(2,1)S(1)}, u32[]{:S(2)}, u32[]{:S(2)}) %collective-permute-start.8) | collective-permute-done | bytes 262176 | tf_op jit(solution)/shard_map/ppermute | solution.py:113
  30.6 2.1 %collective-permute-start.16 = (bf16[256,512]{1,0:T(8,128)(2,1)S(1)}, bf16[256,512]{1,0:T(8,128)(2,1)S(1)}, u32[]{:S(2)}, u32[]{:S(2)}) collective-permute-start(bf16[256,512]{1,0:T(8,128)(2,1)S(1)} %collective-permute-done.15), channel_id=1, source_target_pairs={{0,4},{4,8},{8,12},{12,14},{14,10},{10,6},{6,2},{2,0},{1,5},{5,9},... | collective-permute-start | bytes 786440 | tf_op jit(solution)/shard_map/ppermute | solution.py:113
  32.8 3.0 %collective-permute-done.22 = bf16[256,512]{1,0:T(8,128)(2,1)S(1)} collective-permute-done((bf16[256,512]{1,0:T(8,128)(2,1)S(1)}, bf16[256,512]{1,0:T(8,128)(2,1)S(1)}, u32[]{:S(2)}, u32[]{:S(2)}) %collective-permute-start.22) | collective-permute-done | bytes 262176 | tf_op jit(solution)/shard_map/ppermute | solution.py:113
  36.8 2.1 %collective-permute-start.3 = (bf16[256,512]{1,0:T(8,128)(2,1)S(1)}, bf16[256,512]{1,0:T(8,128)(2,1)S(1)}, u32[]{:S(2)}, u32[]{:S(2)}) collective-permute-start(bf16[256,512]{1,0:T(8,128)(2,1)S(1)} %collective-permute-done.2), channel_id=1, source_target_pairs={{0,4},{4,8},{8,12},{12,14},{14,10},{10,6},{6,2},{2,0},{1,5},{5,9},... | collective-permute-start | bytes 786440 | tf_op jit(solution)/shard_map/ppermute | solution.py:113
  38.9 2.5 %collective-permute-done.9 = bf16[256,512]{1,0:T(8,128)(2,1)S(1)} collective-permute-done((bf16[256,512]{1,0:T(8,128)(2,1)S(1)}, bf16[256,512]{1,0:T(8,128)(2,1)S(1)}, u32[]{:S(2)}, u32[]{:S(2)}) %collective-permute-start.9) | collective-permute-done | bytes 262176 | tf_op jit(solution)/shard_map/ppermute | solution.py:113
  41.8 2.1 %collective-permute-start.17 = (bf16[256,512]{1,0:T(8,128)(2,1)S(1)}, bf16[256,512]{1,0:T(8,128)(2,1)S(1)}, u32[]{:S(2)}, u32[]{:S(2)}) collective-permute-start(bf16[256,512]{1,0:T(8,128)(2,1)S(1)} %collective-permute-done.16), channel_id=1, source_target_pairs={{0,4},{4,8},{8,12},{12,14},{14,10},{10,6},{6,2},{2,0},{1,5},{5,9},... | collective-permute-start | bytes 786440 | tf_op jit(solution)/shard_map/ppermute | solution.py:113
  44.0 3.0 %collective-permute-done.23 = bf16[256,512]{1,0:T(8,128)(2,1)S(1)} collective-permute-done((bf16[256,512]{1,0:T(8,128)(2,1)S(1)}, bf16[256,512]{1,0:T(8,128)(2,1)S(1)}, u32[]{:S(2)}, u32[]{:S(2)}) %collective-permute-start.23) | collective-permute-done | bytes 262176 | tf_op jit(solution)/shard_map/ppermute | solution.py:113
  48.0 2.1 %collective-permute-start.4 = (bf16[256,512]{1,0:T(8,128)(2,1)S(1)}, bf16[256,512]{1,0:T(8,128)(2,1)S(1)}, u32[]{:S(2)}, u32[]{:S(2)}) collective-permute-start(bf16[256,512]{1,0:T(8,128)(2,1)S(1)} %collective-permute-done.3), channel_id=1, source_target_pairs={{0,4},{4,8},{8,12},{12,14},{14,10},{10,6},{6,2},{2,0},{1,5},{5,9},... | collective-permute-start | bytes 786440 | tf_op jit(solution)/shard_map/ppermute | solution.py:113
  50.1 2.6 %collective-permute-done.10 = bf16[256,512]{1,0:T(8,128)(2,1)S(1)} collective-permute-done((bf16[256,512]{1,0:T(8,128)(2,1)S(1)}, bf16[256,512]{1,0:T(8,128)(2,1)S(1)}, u32[]{:S(2)}, u32[]{:S(2)}) %collective-permute-start.10) | collective-permute-done | bytes 262176 | tf_op jit(solution)/shard_map/ppermute | solution.py:113
  53.1 2.1 %collective-permute-start.18 = (bf16[256,512]{1,0:T(8,128)(2,1)S(1)}, bf16[256,512]{1,0:T(8,128)(2,1)S(1)}, u32[]{:S(2)}, u32[]{:S(2)}) collective-permute-start(bf16[256,512]{1,0:T(8,128)(2,1)S(1)} %collective-permute-done.17), channel_id=1, source_target_pairs={{0,4},{4,8},{8,12},{12,14},{14,10},{10,6},{6,2},{2,0},{1,5},{5,9},... | collective-permute-start | bytes 786440 | tf_op jit(solution)/shard_map/ppermute | solution.py:113
  55.2 3.1 %collective-permute-done.24 = bf16[256,512]{1,0:T(8,128)(2,1)S(1)} collective-permute-done((bf16[256,512]{1,0:T(8,128)(2,1)S(1)}, bf16[256,512]{1,0:T(8,128)(2,1)S(1)}, u32[]{:S(2)}, u32[]{:S(2)}) %collective-permute-start.24) | collective-permute-done | bytes 262176 | tf_op jit(solution)/shard_map/ppermute | solution.py:113
  59.3 2.1 %collective-permute-start.5 = (bf16[256,512]{1,0:T(8,128)(2,1)S(1)}, bf16[256,512]{1,0:T(8,128)(2,1)S(1)}, u32[]{:S(2)}, u32[]{:S(2)}) collective-permute-start(bf16[256,512]{1,0:T(8,128)(2,1)S(1)} %collective-permute-done.4), channel_id=1, source_target_pairs={{0,4},{4,8},{8,12},{12,14},{14,10},{10,6},{6,2},{2,0},{1,5},{5,9},... | collective-permute-start | bytes 786440 | tf_op jit(solution)/shard_map/ppermute | solution.py:113
  61.4 2.4 %collective-permute-done.11 = bf16[256,512]{1,0:T(8,128)(2,1)S(1)} collective-permute-done((bf16[256,512]{1,0:T(8,128)(2,1)S(1)}, bf16[256,512]{1,0:T(8,128)(2,1)S(1)}, u32[]{:S(2)}, u32[]{:S(2)}) %collective-permute-start.11) | collective-permute-done | bytes 262176 | tf_op jit(solution)/shard_map/ppermute | solution.py:113
  64.3 2.1 %collective-permute-start.19 = (bf16[256,512]{1,0:T(8,128)(2,1)S(1)}, bf16[256,512]{1,0:T(8,128)(2,1)S(1)}, u32[]{:S(2)}, u32[]{:S(2)}) collective-permute-start(bf16[256,512]{1,0:T(8,128)(2,1)S(1)} %collective-permute-done.18), channel_id=1, source_target_pairs={{0,4},{4,8},{8,12},{12,14},{14,10},{10,6},{6,2},{2,0},{1,5},{5,9},... | collective-permute-start | bytes 786440 | tf_op jit(solution)/shard_map/ppermute | solution.py:113
  66.4 3.0 %collective-permute-done.25 = bf16[256,512]{1,0:T(8,128)(2,1)S(1)} collective-permute-done((bf16[256,512]{1,0:T(8,128)(2,1)S(1)}, bf16[256,512]{1,0:T(8,128)(2,1)S(1)}, u32[]{:S(2)}, u32[]{:S(2)}) %collective-permute-start.25) | collective-permute-done | bytes 262176 | tf_op jit(solution)/shard_map/ppermute | solution.py:113
  70.5 2.1 %collective-permute-start.6 = (bf16[256,512]{1,0:T(8,128)(2,1)S(1)}, bf16[256,512]{1,0:T(8,128)(2,1)S(1)}, u32[]{:S(2)}, u32[]{:S(2)}) collective-permute-start(bf16[256,512]{1,0:T(8,128)(2,1)S(1)} %collective-permute-done.5), channel_id=1, source_target_pairs={{0,4},{4,8},{8,12},{12,14},{14,10},{10,6},{6,2},{2,0},{1,5},{5,9},... | collective-permute-start | bytes 786440 | tf_op jit(solution)/shard_map/ppermute | solution.py:113
  72.6 2.5 %collective-permute-done.12 = bf16[256,512]{1,0:T(8,128)(2,1)S(1)} collective-permute-done((bf16[256,512]{1,0:T(8,128)(2,1)S(1)}, bf16[256,512]{1,0:T(8,128)(2,1)S(1)}, u32[]{:S(2)}, u32[]{:S(2)}) %collective-permute-start.12) | collective-permute-done | bytes 262176 | tf_op jit(solution)/shard_map/ppermute | solution.py:113
  75.5 2.1 %collective-permute-start.20 = (bf16[256,512]{1,0:T(8,128)(2,1)S(1)}, bf16[256,512]{1,0:T(8,128)(2,1)S(1)}, u32[]{:S(2)}, u32[]{:S(2)}) collective-permute-start(bf16[256,512]{1,0:T(8,128)(2,1)S(1)} %collective-permute-done.19), channel_id=1, source_target_pairs={{0,4},{4,8},{8,12},{12,14},{14,10},{10,6},{6,2},{2,0},{1,5},{5,9},... | collective-permute-start | bytes 786440 | tf_op jit(solution)/shard_map/ppermute | solution.py:113
  77.7 3.0 %collective-permute-done.26 = bf16[256,512]{1,0:T(8,128)(2,1)S(1)} collective-permute-done((bf16[256,512]{1,0:T(8,128)(2,1)S(1)}, bf16[256,512]{1,0:T(8,128)(2,1)S(1)}, u32[]{:S(2)}, u32[]{:S(2)}) %collective-permute-start.26) | collective-permute-done | bytes 262176 | tf_op jit(solution)/shard_map/ppermute | solution.py:113
  81.9 3.8 %collective-permute-done.13 = bf16[256,512]{1,0:T(8,128)(2,1)S(1)} collective-permute-done((bf16[256,512]{1,0:T(8,128)(2,1)S(1)}, bf16[256,512]{1,0:T(8,128)(2,1)S(1)}, u32[]{:S(2)}, u32[]{:S(2)}) %collective-permute-start.13) | collective-permute-done | bytes 262176 | tf_op jit(solution)/shard_map/ppermute | solution.py:113
  86.2 2.3 %collective-permute-done.27 = bf16[256,512]{1,0:T(8,128)(2,1)S(1)} collective-permute-done((bf16[256,512]{1,0:T(8,128)(2,1)S(1)}, bf16[256,512]{1,0:T(8,128)(2,1)S(1)}, u32[]{:S(2)}, u32[]{:S(2)}) %collective-permute-start.27) | collective-permute-done | bytes 262176 | tf_op jit(solution)/shard_map/ppermute | solution.py:113
  88.8 2.5 %fusion.32 = (f32[256,2048]{1,0:T(8,128)}, bf16[256,2048]{1,0:T(8,128)(2,1)S(1)}) fusion(f32[256,512]{1,0:T(8,128)S(1)} %fusion.40, f32[256,512]{1,0:T(8,128)S(1)} %fusion.41, f32[256,512]{1,0:T(8,128)S(1)} %fusion.42, f32[256,512]{1,0:T(8,128)S(1)} %fusion.43, bf16[256,2048]{1,0:T(8,128)(2,1)S(1)} %bitcast.91), kind=kLoop, calls=%fused_computation.46 | loop fusion | flops 12582912 | bytes 6291456 | tf_op jit(solution)/shard_map/add | solution.py:28
  91.3 1.5 %collective-permute-start.28 = (bf16[256,2048]{1,0:T(8,128)(2,1)S(1)}, bf16[256,2048]{1,0:T(8,128)(2,1)S(1)}, u32[]{:S(2)}, u32[]{:S(2)}) collective-permute-start(bf16[256,2048]{1,0:T(8,128)(2,1)S(1)} %get-tuple-element.33), channel_id=1, source_target_pairs={{0,1},{2,3},{4,5},{6,7},{8,9},{10,11},{12,13},{14,15},{16,17},{18,... | collective-permute-start | bytes 3145736 | tf_op jit(solution)/shard_map/ppermute | solution.py:18
  93.2 1.6 %collective-permute-done.28 = bf16[256,2048]{1,0:T(8,128)(2,1)S(1)} collective-permute-done((bf16[256,2048]{1,0:T(8,128)(2,1)S(1)}, bf16[256,2048]{1,0:T(8,128)(2,1)S(1)}, u32[]{:S(2)}, u32[]{:S(2)}) %collective-permute-start.28) | collective-permute-done | bytes 1048608 | tf_op jit(solution)/shard_map/ppermute | solution.py:18
  95.5 5.5 %fusion.130 = (f32[256,2048]{1,0:T(8,128)S(1)}, bf16[256,2048]{1,0:T(8,128)(2,1)}, f32[256,2048]{1,0:T(8,128)}) fusion(bf16[256,2048]{1,0:T(8,128)(2,1)S(1)} %collective-permute-done.28, bf16[2048,2048]{1,0:T(8,128)(2,1)S(1)} %constant_dynamic-update-slice_fusion, f32[256]{0:T(256)S(1)} %add_rsqrt_fusion, f32[256]{0:T(256)S(1)} %broadcast_multiply_fusion.4, ...), kind=kOutput, calls=%fused_computation.225 | convolution fusion | flops 2161639424 | bytes 14690304 | tf_op jit(solution)/shard_map/dot_general | solution.py:50
  102.9 1.6 %slice_convert_fusion.1 = (f32[128,2048]{1,0:T(8,128)S(1)}, f32[128,2048]{1,0:T(8,128)S(1)}) fusion(bf16[256,2048]{1,0:T(8,128)(2,1)} %get-tuple-element.30), kind=kLoop, calls=%fused_computation.99 | loop fusion | flops 524288 | bytes 3145728 | tf_op jit(solution)/shard_map/convert_element_type | solution.py:235
  104.5 1.5 %collective-permute-done.29 = f32[7]{0:T(128)S(1)} collective-permute-done((f32[7]{0:T(128)S(1)}, f32[7]{0:T(128)S(1)}, u32[]{:S(2)}, u32[]{:S(2)}) %collective-permute-start.29) | collective-permute-done | bytes 60 | tf_op jit(solution)/shard_map/ppermute | solution.py:128
  106.7 1.6 %collective-permute-start.30 = (f32[7]{0:T(128)S(1)}, f32[7]{0:T(128)S(1)}, u32[]{:S(2)}, u32[]{:S(2)}) collective-permute-start(f32[7]{0:T(128)S(1)} %fusion.166), channel_id=1, source_target_pairs={{0,4},{2,6},{4,0},{6,2},{8,12},{10,14},{12,8},{14,10},{1,5},{3,7},... | collective-permute-start | bytes 92 | tf_op jit(solution)/shard_map/ppermute | solution.py:128
  108.3 2.0 %collective-permute-done.30 = f32[7]{0:T(128)S(1)} collective-permute-done((f32[7]{0:T(128)S(1)}, f32[7]{0:T(128)S(1)}, u32[]{:S(2)}, u32[]{:S(2)}) %collective-permute-start.30) | collective-permute-done | bytes 60 | tf_op jit(solution)/shard_map/ppermute | solution.py:128
  110.3 2.6 %collective-permute-start.31 = (f32[7]{0:T(128)S(1)}, f32[7]{0:T(128)S(1)}, u32[]{:S(2)}, u32[]{:S(2)}) collective-permute-start(f32[7]{0:T(128)S(1)} %add.444), channel_id=1, source_target_pairs={{0,8},{2,10},{4,12},{6,14},{8,0},{10,2},{12,4},{14,6},{1,9},{3,11}... | collective-permute-start | bytes 92 | tf_op jit(solution)/shard_map/ppermute | solution.py:128
  112.9 1.9 %collective-permute-done.31 = f32[7]{0:T(128)S(1)} collective-permute-done((f32[7]{0:T(128)S(1)}, f32[7]{0:T(128)S(1)}, u32[]{:S(2)}, u32[]{:S(2)}) %collective-permute-start.31) | collective-permute-done | bytes 60 | tf_op jit(solution)/shard_map/ppermute | solution.py:128
  122.9 2.1 %fusion.39 = bf16[256,2048]{1,0:T(8,128)(2,1)S(1)} fusion(f32[256,2048]{1,0:T(8,128)} %get-tuple-element.14, f32[128,2048]{1,0:T(8,128)S(1)} %get-tuple-element.35, f32[256]{0:T(256)S(1)} %broadcast_bitcast_fusion, f32[128,2048]{1,0:T(8,128)S(1)} %get-tuple-element.34, f32[256]{0:T(256)S(1)} %broadcast_bitcast_fusion.1, ...), kind=kLoop, calls=%fused_computation.57 | loop fusion | flops 3670016 | bytes 6294528 | tf_op jit(solution)/shard_map/convert_element_type | solution.py:56
  125.0 2.6 %fusion.129 = (f32[256]{0:T(256)S(1)}, f32[256]{0:T(256)S(1)}, f32[256,2048]{1,0:T(8,128)S(1)}) fusion(f32[256]{0:T(256)S(1)} %add_rsqrt_fusion, f32[256]{0:T(256)S(1)} %broadcast_multiply_fusion.4, bf16[256,2048]{1,0:T(8,128)(2,1)S(1)} %collective-permute-done.28, f32[2048]{0:T(1024)S(1)} %bitcast.103, bf16[256,2048]{1,0:T(8,128)(2,1)S(1)} %fusion.39, ...), kind=kOutput, calls=%fused_computation.224 | convolution fusion | flops 2151153152 | bytes 12595200 | tf_op jit(solution)/shard_map/dot_general | solution.py:57
  127.7 2.1 %fusion.15 = bf16[256,2048]{1,0:T(8,128)(2,1)} fusion(bf16[256,2048]{1,0:T(8,128)(2,1)S(1)} %collective-permute-done.28, f32[256,2048]{1,0:T(8,128)S(1)} %get-tuple-element.47, f32[256]{0:T(256)S(1)} %broadcast_multiply_fusion.2, f32[256]{0:T(256)S(1)} %broadcast_multiply_fusion.3, f32[128,2048]{1,0:T(8,128)S(1)} %get-tuple-element.35, ...), kind=kLoop, calls=%fused_computation.29 | loop fusion | flops 7340032 | bytes 7347200 | tf_op jit(solution)/shard_map/convert_element_type | solution.py:66
  129.8 1.3 collective-permute-start.32
  131.1 3.4 %collective-permute-done.32 = bf16[256,2048]{1,0:T(8,128)(2,1)S(1)} collective-permute-done((bf16[256,2048]{1,0:T(8,128)(2,1)}, bf16[256,2048]{1,0:T(8,128)(2,1)S(1)}, u32[]{:S(2)}, u32[]{:S(2)}) %collective-permute-start.32) | collective-permute-done | bytes 1048608 | tf_op jit(solution)/shard_map/ppermute | solution.py:18
  134.5 1.5 %collective-permute-start.33 = (f32[1]{0:T(128)}, f32[1]{0:T(128)}, u32[]{:S(2)}, u32[]{:S(2)}) collective-permute-start(f32[1]{0:T(128)} %sub.143), channel_id=1, source_target_pairs={{1,0},{3,2},{5,4},{7,6},{9,8},{11,10},{13,12},{15,14},{17,16},{19,... | collective-permute-start | bytes 20 | tf_op jit(solution)/shard_map/ppermute | solution.py:18
  136.1 6.7 %fusion.128 = (f32[256]{0:T(256)S(1)}, f32[256]{0:T(256)S(1)}, f32[256,2048]{1,0:T(8,128)S(1)}) fusion(f32[256]{0:T(256)S(1)} %add_rsqrt_fusion.1, f32[256]{0:T(256)S(1)} %broadcast_multiply_fusion.5, bf16[256,2048]{1,0:T(8,128)(2,1)S(1)} %bitcast.92, f32[2048]{0:T(1024)S(1)} %bitcast.104, bf16[2048,2048]{1,0:T(8,128)(2,1)} %copy-done.2, ...), kind=kOutput, calls=%fused_computation.223 | convolution fusion | flops 2152726016 | bytes 14692352 | tf_op jit(solution)/shard_map/dot_general | solution.py:57
  142.8 2.0 %fusion.44 = bf16[256,2048]{1,0:T(8,128)(2,1)} fusion(bf16[256,2048]{1,0:T(8,128)(2,1)} %fusion.15, bf16[256,2048]{1,0:T(8,128)(2,1)S(1)} %bitcast.93, f32[256,2048]{1,0:T(8,128)S(1)} %get-tuple-element.48, bf16[256,2048]{1,0:T(8,128)(2,1)S(1)} %collective-permute-done.32, f32[256]{0:T(256)S(1)} %broadcast_multiply_fusion, ...), kind=kLoop, calls=%fused_computation.86 | loop fusion | flops 5767168 | bytes 6295553 | tf_op jit(solution)/shard_map/jit(_where)/select_n | solution.py:244
  (135 shorter events, 19.0 us)
Async XLA Ops:
  0.6 7.4 %copy-start.4 = (bf16[128,2048]{1,0:T(8,128)(2,1)S(1)}, bf16[128,2048]{1,0:T(8,128)(2,1)}, u32[]{:S(2)}) copy-start(bf16[128,2048]{1,0:T(8,128)(2,1)} %param.5) | copy-start | bytes 1572868
  0.6 12.7 %copy-start = (bf16[2,128,2048]{2,1,0:T(8,128)(2,1)S(1)}, bf16[2,128,2048]{2,1,0:T(8,128)(2,1)}, u32[]{:S(2)}) copy-start(bf16[2,128,2048]{2,1,0:T(8,128)(2,1)} %param.4) | copy-start | bytes 3145732
  2.9 10.4 %collective-permute-start = (bf16[256,512]{1,0:T(8,128)(2,1)}, bf16[256,512]{1,0:T(8,128)(2,1)}, u32[]{:S(2)}, u32[]{:S(2)}) collective-permute-start(bf16[256,512]{1,0:T(8,128)(2,1)} %get-tuple-element.39), channel_id=1, source_target_pairs={{0,4},{4,8},{8,12},{12,14},{14,10},{10,6},{6,2},{2,0},{1,5},{5,9},... | collective-permute-start | bytes 786440 | tf_op jit(solution)/shard_map/ppermute | solution.py:113
  6.0 14.9 %collective-permute-start.7 = (bf16[256,512]{1,0:T(8,128)(2,1)}, bf16[256,512]{1,0:T(8,128)(2,1)S(1)}, u32[]{:S(2)}, u32[]{:S(2)}) collective-permute-start(bf16[256,512]{1,0:T(8,128)(2,1)} %get-tuple-element.36), channel_id=1, source_target_pairs={{4,0},{8,4},{12,8},{14,12},{10,14},{6,10},{2,6},{0,2},{5,1},{9,5},... | collective-permute-start | bytes 786440 | tf_op jit(solution)/shard_map/ppermute | solution.py:113
  6.0 15.3 %collective-permute-start.14 = (bf16[256,512]{1,0:T(8,128)(2,1)}, bf16[256,512]{1,0:T(8,128)(2,1)S(1)}, u32[]{:S(2)}, u32[]{:S(2)}) collective-permute-start(bf16[256,512]{1,0:T(8,128)(2,1)} %get-tuple-element.38), channel_id=1, source_target_pairs={{0,4},{4,8},{8,12},{12,14},{14,10},{10,6},{6,2},{2,0},{1,5},{5,9},... | collective-permute-start | bytes 786440 | tf_op jit(solution)/shard_map/ppermute | solution.py:113
  8.0 15.6 %collective-permute-start.21 = (bf16[256,512]{1,0:T(8,128)(2,1)}, bf16[256,512]{1,0:T(8,128)(2,1)S(1)}, u32[]{:S(2)}, u32[]{:S(2)}) collective-permute-start(bf16[256,512]{1,0:T(8,128)(2,1)} %get-tuple-element.37), channel_id=1, source_target_pairs={{4,0},{8,4},{12,8},{14,12},{10,14},{6,10},{2,6},{0,2},{5,1},{9,5},... | collective-permute-start | bytes 786440 | tf_op jit(solution)/shard_map/ppermute | solution.py:113
  8.0 6.0 %copy-start.6 = (f32[1,2048]{1,0:T(1,128)S(1)}, f32[1,2048]{1,0:T(1,128)}, u32[]{:S(2)}) copy-start(f32[1,2048]{1,0:T(1,128)} %param.7) | copy-start | bytes 24580
  13.4 1.2 copy-start.1
  15.5 9.4 %collective-permute-start.1 = (bf16[256,512]{1,0:T(8,128)(2,1)}, bf16[256,512]{1,0:T(8,128)(2,1)S(1)}, u32[]{:S(2)}, u32[]{:S(2)}) collective-permute-start(bf16[256,512]{1,0:T(8,128)(2,1)} %collective-permute-done), channel_id=1, source_target_pairs={{0,4},{4,8},{8,12},{12,14},{14,10},{10,6},{6,2},{2,0},{1,5},{5,9},... | collective-permute-start | bytes 786440 | tf_op jit(solution)/shard_map/ppermute | solution.py:113
  20.9 9.2 %collective-permute-start.8 = (bf16[256,512]{1,0:T(8,128)(2,1)S(1)}, bf16[256,512]{1,0:T(8,128)(2,1)S(1)}, u32[]{:S(2)}, u32[]{:S(2)}) collective-permute-start(bf16[256,512]{1,0:T(8,128)(2,1)S(1)} %collective-permute-done.7), channel_id=1, source_target_pairs={{4,0},{8,4},{12,8},{14,12},{10,14},{6,10},{2,6},{0,2},{5,1},{9,5},... | collective-permute-start | bytes 786440 | tf_op jit(solution)/shard_map/ppermute | solution.py:113
  21.3 9.3 %collective-permute-start.15 = (bf16[256,512]{1,0:T(8,128)(2,1)S(1)}, bf16[256,512]{1,0:T(8,128)(2,1)S(1)}, u32[]{:S(2)}, u32[]{:S(2)}) collective-permute-start(bf16[256,512]{1,0:T(8,128)(2,1)S(1)} %collective-permute-done.14), channel_id=1, source_target_pairs={{0,4},{4,8},{8,12},{12,14},{14,10},{10,6},{6,2},{2,0},{1,5},{5,9},... | collective-permute-start | bytes 786440 | tf_op jit(solution)/shard_map/ppermute | solution.py:113
  23.6 12.2 %collective-permute-start.22 = (bf16[256,512]{1,0:T(8,128)(2,1)S(1)}, bf16[256,512]{1,0:T(8,128)(2,1)S(1)}, u32[]{:S(2)}, u32[]{:S(2)}) collective-permute-start(bf16[256,512]{1,0:T(8,128)(2,1)S(1)} %collective-permute-done.21), channel_id=1, source_target_pairs={{4,0},{8,4},{12,8},{14,12},{10,14},{6,10},{2,6},{0,2},{5,1},{9,5},... | collective-permute-start | bytes 786440 | tf_op jit(solution)/shard_map/ppermute | solution.py:113
  25.0 11.8 %collective-permute-start.2 = (bf16[256,512]{1,0:T(8,128)(2,1)S(1)}, bf16[256,512]{1,0:T(8,128)(2,1)S(1)}, u32[]{:S(2)}, u32[]{:S(2)}) collective-permute-start(bf16[256,512]{1,0:T(8,128)(2,1)S(1)} %collective-permute-done.1), channel_id=1, source_target_pairs={{0,4},{4,8},{8,12},{12,14},{14,10},{10,6},{6,2},{2,0},{1,5},{5,9},... | collective-permute-start | bytes 786440 | tf_op jit(solution)/shard_map/ppermute | solution.py:113
  30.2 11.2 %collective-permute-start.9 = (bf16[256,512]{1,0:T(8,128)(2,1)S(1)}, bf16[256,512]{1,0:T(8,128)(2,1)S(1)}, u32[]{:S(2)}, u32[]{:S(2)}) collective-permute-start(bf16[256,512]{1,0:T(8,128)(2,1)S(1)} %collective-permute-done.8), channel_id=1, source_target_pairs={{4,0},{8,4},{12,8},{14,12},{10,14},{6,10},{2,6},{0,2},{5,1},{9,5},... | collective-permute-start | bytes 786440 | tf_op jit(solution)/shard_map/ppermute | solution.py:113
  30.6 11.2 %collective-permute-start.16 = (bf16[256,512]{1,0:T(8,128)(2,1)S(1)}, bf16[256,512]{1,0:T(8,128)(2,1)S(1)}, u32[]{:S(2)}, u32[]{:S(2)}) collective-permute-start(bf16[256,512]{1,0:T(8,128)(2,1)S(1)} %collective-permute-done.15), channel_id=1, source_target_pairs={{0,4},{4,8},{8,12},{12,14},{14,10},{10,6},{6,2},{2,0},{1,5},{5,9},... | collective-permute-start | bytes 786440 | tf_op jit(solution)/shard_map/ppermute | solution.py:113
  35.8 11.2 %collective-permute-start.23 = (bf16[256,512]{1,0:T(8,128)(2,1)S(1)}, bf16[256,512]{1,0:T(8,128)(2,1)S(1)}, u32[]{:S(2)}, u32[]{:S(2)}) collective-permute-start(bf16[256,512]{1,0:T(8,128)(2,1)S(1)} %collective-permute-done.22), channel_id=1, source_target_pairs={{4,0},{8,4},{12,8},{14,12},{10,14},{6,10},{2,6},{0,2},{5,1},{9,5},... | collective-permute-start | bytes 786440 | tf_op jit(solution)/shard_map/ppermute | solution.py:113
  36.8 11.2 %collective-permute-start.3 = (bf16[256,512]{1,0:T(8,128)(2,1)S(1)}, bf16[256,512]{1,0:T(8,128)(2,1)S(1)}, u32[]{:S(2)}, u32[]{:S(2)}) collective-permute-start(bf16[256,512]{1,0:T(8,128)(2,1)S(1)} %collective-permute-done.2), channel_id=1, source_target_pairs={{0,4},{4,8},{8,12},{12,14},{14,10},{10,6},{6,2},{2,0},{1,5},{5,9},... | collective-permute-start | bytes 786440 | tf_op jit(solution)/shard_map/ppermute | solution.py:113
  41.4 11.2 %collective-permute-start.10 = (bf16[256,512]{1,0:T(8,128)(2,1)S(1)}, bf16[256,512]{1,0:T(8,128)(2,1)S(1)}, u32[]{:S(2)}, u32[]{:S(2)}) collective-permute-start(bf16[256,512]{1,0:T(8,128)(2,1)S(1)} %collective-permute-done.9), channel_id=1, source_target_pairs={{4,0},{8,4},{12,8},{14,12},{10,14},{6,10},{2,6},{0,2},{5,1},{9,5},... | collective-permute-start | bytes 786440 | tf_op jit(solution)/shard_map/ppermute | solution.py:113
  41.8 11.2 %collective-permute-start.17 = (bf16[256,512]{1,0:T(8,128)(2,1)S(1)}, bf16[256,512]{1,0:T(8,128)(2,1)S(1)}, u32[]{:S(2)}, u32[]{:S(2)}) collective-permute-start(bf16[256,512]{1,0:T(8,128)(2,1)S(1)} %collective-permute-done.16), channel_id=1, source_target_pairs={{0,4},{4,8},{8,12},{12,14},{14,10},{10,6},{6,2},{2,0},{1,5},{5,9},... | collective-permute-start | bytes 786440 | tf_op jit(solution)/shard_map/ppermute | solution.py:113
  47.0 11.2 %collective-permute-start.24 = (bf16[256,512]{1,0:T(8,128)(2,1)S(1)}, bf16[256,512]{1,0:T(8,128)(2,1)S(1)}, u32[]{:S(2)}, u32[]{:S(2)}) collective-permute-start(bf16[256,512]{1,0:T(8,128)(2,1)S(1)} %collective-permute-done.23), channel_id=1, source_target_pairs={{4,0},{8,4},{12,8},{14,12},{10,14},{6,10},{2,6},{0,2},{5,1},{9,5},... | collective-permute-start | bytes 786440 | tf_op jit(solution)/shard_map/ppermute | solution.py:113
  48.0 11.3 %collective-permute-start.4 = (bf16[256,512]{1,0:T(8,128)(2,1)S(1)}, bf16[256,512]{1,0:T(8,128)(2,1)S(1)}, u32[]{:S(2)}, u32[]{:S(2)}) collective-permute-start(bf16[256,512]{1,0:T(8,128)(2,1)S(1)} %collective-permute-done.3), channel_id=1, source_target_pairs={{0,4},{4,8},{8,12},{12,14},{14,10},{10,6},{6,2},{2,0},{1,5},{5,9},... | collective-permute-start | bytes 786440 | tf_op jit(solution)/shard_map/ppermute | solution.py:113
  52.6 11.2 %collective-permute-start.11 = (bf16[256,512]{1,0:T(8,128)(2,1)S(1)}, bf16[256,512]{1,0:T(8,128)(2,1)S(1)}, u32[]{:S(2)}, u32[]{:S(2)}) collective-permute-start(bf16[256,512]{1,0:T(8,128)(2,1)S(1)} %collective-permute-done.10), channel_id=1, source_target_pairs={{4,0},{8,4},{12,8},{14,12},{10,14},{6,10},{2,6},{0,2},{5,1},{9,5},... | collective-permute-start | bytes 786440 | tf_op jit(solution)/shard_map/ppermute | solution.py:113
  53.1 11.2 %collective-permute-start.18 = (bf16[256,512]{1,0:T(8,128)(2,1)S(1)}, bf16[256,512]{1,0:T(8,128)(2,1)S(1)}, u32[]{:S(2)}, u32[]{:S(2)}) collective-permute-start(bf16[256,512]{1,0:T(8,128)(2,1)S(1)} %collective-permute-done.17), channel_id=1, source_target_pairs={{0,4},{4,8},{8,12},{12,14},{14,10},{10,6},{6,2},{2,0},{1,5},{5,9},... | collective-permute-start | bytes 786440 | tf_op jit(solution)/shard_map/ppermute | solution.py:113
  58.3 11.2 %collective-permute-start.25 = (bf16[256,512]{1,0:T(8,128)(2,1)S(1)}, bf16[256,512]{1,0:T(8,128)(2,1)S(1)}, u32[]{:S(2)}, u32[]{:S(2)}) collective-permute-start(bf16[256,512]{1,0:T(8,128)(2,1)S(1)} %collective-permute-done.24), channel_id=1, source_target_pairs={{4,0},{8,4},{12,8},{14,12},{10,14},{6,10},{2,6},{0,2},{5,1},{9,5},... | collective-permute-start | bytes 786440 | tf_op jit(solution)/shard_map/ppermute | solution.py:113
  59.3 11.2 %collective-permute-start.5 = (bf16[256,512]{1,0:T(8,128)(2,1)S(1)}, bf16[256,512]{1,0:T(8,128)(2,1)S(1)}, u32[]{:S(2)}, u32[]{:S(2)}) collective-permute-start(bf16[256,512]{1,0:T(8,128)(2,1)S(1)} %collective-permute-done.4), channel_id=1, source_target_pairs={{0,4},{4,8},{8,12},{12,14},{14,10},{10,6},{6,2},{2,0},{1,5},{5,9},... | collective-permute-start | bytes 786440 | tf_op jit(solution)/shard_map/ppermute | solution.py:113
  63.9 11.2 %collective-permute-start.12 = (bf16[256,512]{1,0:T(8,128)(2,1)S(1)}, bf16[256,512]{1,0:T(8,128)(2,1)S(1)}, u32[]{:S(2)}, u32[]{:S(2)}) collective-permute-start(bf16[256,512]{1,0:T(8,128)(2,1)S(1)} %collective-permute-done.11), channel_id=1, source_target_pairs={{4,0},{8,4},{12,8},{14,12},{10,14},{6,10},{2,6},{0,2},{5,1},{9,5},... | collective-permute-start | bytes 786440 | tf_op jit(solution)/shard_map/ppermute | solution.py:113
  64.3 11.2 %collective-permute-start.19 = (bf16[256,512]{1,0:T(8,128)(2,1)S(1)}, bf16[256,512]{1,0:T(8,128)(2,1)S(1)}, u32[]{:S(2)}, u32[]{:S(2)}) collective-permute-start(bf16[256,512]{1,0:T(8,128)(2,1)S(1)} %collective-permute-done.18), channel_id=1, source_target_pairs={{0,4},{4,8},{8,12},{12,14},{14,10},{10,6},{6,2},{2,0},{1,5},{5,9},... | collective-permute-start | bytes 786440 | tf_op jit(solution)/shard_map/ppermute | solution.py:113
  69.5 11.2 %collective-permute-start.26 = (bf16[256,512]{1,0:T(8,128)(2,1)S(1)}, bf16[256,512]{1,0:T(8,128)(2,1)S(1)}, u32[]{:S(2)}, u32[]{:S(2)}) collective-permute-start(bf16[256,512]{1,0:T(8,128)(2,1)S(1)} %collective-permute-done.25), channel_id=1, source_target_pairs={{4,0},{8,4},{12,8},{14,12},{10,14},{6,10},{2,6},{0,2},{5,1},{9,5},... | collective-permute-start | bytes 786440 | tf_op jit(solution)/shard_map/ppermute | solution.py:113
  70.5 11.1 %collective-permute-start.6 = (bf16[256,512]{1,0:T(8,128)(2,1)S(1)}, bf16[256,512]{1,0:T(8,128)(2,1)S(1)}, u32[]{:S(2)}, u32[]{:S(2)}) collective-permute-start(bf16[256,512]{1,0:T(8,128)(2,1)S(1)} %collective-permute-done.5), channel_id=1, source_target_pairs={{0,4},{4,8},{8,12},{12,14},{14,10},{10,6},{6,2},{2,0},{1,5},{5,9},... | collective-permute-start | bytes 786440 | tf_op jit(solution)/shard_map/ppermute | solution.py:113
  75.1 10.6 %collective-permute-start.13 = (bf16[256,512]{1,0:T(8,128)(2,1)S(1)}, bf16[256,512]{1,0:T(8,128)(2,1)S(1)}, u32[]{:S(2)}, u32[]{:S(2)}) collective-permute-start(bf16[256,512]{1,0:T(8,128)(2,1)S(1)} %collective-permute-done.12), channel_id=1, source_target_pairs={{4,0},{8,4},{12,8},{14,12},{10,14},{6,10},{2,6},{0,2},{5,1},{9,5},... | collective-permute-start | bytes 786440 | tf_op jit(solution)/shard_map/ppermute | solution.py:113
  75.5 10.5 %collective-permute-start.20 = (bf16[256,512]{1,0:T(8,128)(2,1)S(1)}, bf16[256,512]{1,0:T(8,128)(2,1)S(1)}, u32[]{:S(2)}, u32[]{:S(2)}) collective-permute-start(bf16[256,512]{1,0:T(8,128)(2,1)S(1)} %collective-permute-done.19), channel_id=1, source_target_pairs={{0,4},{4,8},{8,12},{12,14},{14,10},{10,6},{6,2},{2,0},{1,5},{5,9},... | collective-permute-start | bytes 786440 | tf_op jit(solution)/shard_map/ppermute | solution.py:113
  80.7 7.8 %collective-permute-start.27 = (bf16[256,512]{1,0:T(8,128)(2,1)S(1)}, bf16[256,512]{1,0:T(8,128)(2,1)S(1)}, u32[]{:S(2)}, u32[]{:S(2)}) collective-permute-start(bf16[256,512]{1,0:T(8,128)(2,1)S(1)} %collective-permute-done.26), channel_id=1, source_target_pairs={{4,0},{8,4},{12,8},{14,12},{10,14},{6,10},{2,6},{0,2},{5,1},{9,5},... | collective-permute-start | bytes 786440 | tf_op jit(solution)/shard_map/ppermute | solution.py:113
  91.3 3.6 %collective-permute-start.28 = (bf16[256,2048]{1,0:T(8,128)(2,1)S(1)}, bf16[256,2048]{1,0:T(8,128)(2,1)S(1)}, u32[]{:S(2)}, u32[]{:S(2)}) collective-permute-start(bf16[256,2048]{1,0:T(8,128)(2,1)S(1)} %get-tuple-element.33), channel_id=1, source_target_pairs={{0,1},{2,3},{4,5},{6,7},{8,9},{10,11},{12,13},{14,15},{16,17},{18,... | collective-permute-start | bytes 3145736 | tf_op jit(solution)/shard_map/ppermute | solution.py:18
  93.2 7.8 %copy-start.2 = (bf16[2048,2048]{1,0:T(8,128)(2,1)}, bf16[2048,2048]{1,0:T(8,128)(2,1)S(1)}, u32[]{:S(2)}) copy-start(bf16[2048,2048]{1,0:T(8,128)(2,1)S(1)} %constant_dynamic-update-slice_fusion) | copy-start | bytes 25165828
  95.5 5.5 %copy-start.5 = (bf16[128,2048]{1,0:T(8,128)(2,1)S(1)}, bf16[128,2048]{1,0:T(8,128)(2,1)}, u32[]{:S(2)}) copy-start(bf16[128,2048]{1,0:T(8,128)(2,1)} %param.5) | copy-start | bytes 1572868
  102.4 3.6 %collective-permute-start.29 = (f32[7]{0:T(128)S(1)}, f32[7]{0:T(128)S(1)}, u32[]{:S(2)}, u32[]{:S(2)}) collective-permute-start(f32[7]{0:T(128)S(1)} %pad_maximum_fusion.2), channel_id=1, source_target_pairs={{0,2},{2,0},{4,6},{6,4},{8,10},{10,8},{12,14},{14,12},{1,3},{3,1},... | collective-permute-start | bytes 92 | tf_op jit(solution)/shard_map/ppermute | solution.py:128
  102.9 22.1 %copy-start.3 = (bf16[2048,2048]{1,0:T(8,128)(2,1)S(1)}, bf16[2048,2048]{1,0:T(8,128)(2,1)}, u32[]{:S(2)}) copy-start(bf16[2048,2048]{1,0:T(8,128)(2,1)} %copy-done.2) | copy-start | bytes 25165828
  106.7 3.6 %collective-permute-start.30 = (f32[7]{0:T(128)S(1)}, f32[7]{0:T(128)S(1)}, u32[]{:S(2)}, u32[]{:S(2)}) collective-permute-start(f32[7]{0:T(128)S(1)} %fusion.166), channel_id=1, source_target_pairs={{0,4},{2,6},{4,0},{6,2},{8,12},{10,14},{12,8},{14,10},{1,5},{3,7},... | collective-permute-start | bytes 92 | tf_op jit(solution)/shard_map/ppermute | solution.py:128
  110.3 4.5 %collective-permute-start.31 = (f32[7]{0:T(128)S(1)}, f32[7]{0:T(128)S(1)}, u32[]{:S(2)}, u32[]{:S(2)}) collective-permute-start(f32[7]{0:T(128)S(1)} %add.444), channel_id=1, source_target_pairs={{0,8},{2,10},{4,12},{6,14},{8,0},{10,2},{12,4},{14,6},{1,9},{3,11}... | collective-permute-start | bytes 92 | tf_op jit(solution)/shard_map/ppermute | solution.py:128
  129.8 4.8 %collective-permute-start.32 = (bf16[256,2048]{1,0:T(8,128)(2,1)}, bf16[256,2048]{1,0:T(8,128)(2,1)S(1)}, u32[]{:S(2)}, u32[]{:S(2)}) collective-permute-start(bf16[256,2048]{1,0:T(8,128)(2,1)} %fusion.15), channel_id=1, source_target_pairs={{1,0},{3,2},{5,4},{7,6},{9,8},{11,10},{13,12},{15,14},{17,16},{19,... | collective-permute-start | bytes 3145736 | tf_op jit(solution)/shard_map/ppermute | solution.py:18
  134.5 10.2 %collective-permute-start.33 = (f32[1]{0:T(128)}, f32[1]{0:T(128)}, u32[]{:S(2)}, u32[]{:S(2)}) collective-permute-start(f32[1]{0:T(128)} %sub.143), channel_id=1, source_target_pairs={{1,0},{3,2},{5,4},{7,6},{9,8},{11,10},{13,12},{15,14},{17,16},{19,... | collective-permute-start | bytes 20 | tf_op jit(solution)/shard_map/ppermute | solution.py:18

commit v9 on v8

--- a/solution.py
+++ b/solution.py
@@ -227,7 +227,10 @@
     terms = jnp.sum(jnp.stack(terms), axis=-1)
     packed = tree_sum(jnp.concatenate([terms, obs_sq.reshape(1)]), "tok")
     slope_a, slope_b = lax.optimization_barrier((gelu_slope(fa[3]), gelu_slope(fb[3])))
-    energy, member_coeff, obs_coeff = packed_score(packed, members, size)
+    member_gram = packed[: members * members].reshape(members, members)
+    obs_rows = packed[members * members : members * members + members]
+    obs_total = packed[members * members + members]
+    energy, member_coeff, obs_coeff = score_terms(member_gram, obs_rows, obs_total, size)
     energy_arr = jnp.reshape(energy, (1,))
 
     cot = obs_coeff[:, None, None] * obs_f[None]
@@ -236,9 +239,7 @@
     cot = cot.reshape(members * tok_rows, width)
 
     da = section_backward(cot, gain, weight, fb[1], fb[2], slope_b)
-    back = shifted(da, "section", -1)
-    energy_arr, back = lax.optimization_barrier((energy_arr, back))
-    energy_peer = shifted(energy_arr, "section", -1)
+    back, energy_peer = shifted((da, energy_arr), "section", -1)
     energy_out = jnp.where(on_first, energy_peer, energy_arr)
     db = section_backward(back.astype(jnp.float32), gain, weight, fa[1], fa[2], slope_a)
     grads = jnp.where(on_first, db, da).reshape(members, tok_rows, width)

time: 149 us -> 145 us (0.973)
  between operations: 10 us -> 4.24 us
  other arithmetic: 15.3 us -> 18.6 us
  waiting for transfers between devices: 52.5 us -> 49.7 us
  matrix products: 23 us -> 25.5 us
    dot_general x2, matrix products: 9.32 us -> 12.8 us  [section_backward(): lax.dot_general(grad_pre, weight, (((1,), (1,)), ((), ())), preferred_ele...]
    reduce_sum x0 -> x3, other arithmetic: none -> 2.05 us  [the longest x1 1.25 us: score_terms(): jnp.mean(to_obs) - jnp.sum(others * pair_dist) / (2.0 * count * (count - 1))]
    ppermute x3, waiting for transfers between devices: 5.09 us -> 3.37 us  [shifted(): return lax.ppermute(x, axis, pairs)]
  transfers between devices with their start and end apart: 34 -> 34, of which waited for: 24 -> 30; matrix products, arithmetic and copies ran while one was open for 16% -> 9% of each run, Pallas kernels for 0% -> 0%
where the time goes in v9:
time: 145 us; the launch traced here: 143 us
  waiting for transfers between devices  49.7 us (34%)
  starting transfers between devices  39.7 us (27%)
  matrix products  25.5 us (18%)
  other arithmetic  18.6 us (13%)
  local copies, waits for them, and re-layouts  5.81 us (4%)
  between operations  4.24 us (3%)
    ppermute x28, waiting for transfers between devices, ring_gather(): parts[j] = lax.ppermute(parts[j], axis, cw if clockwise else ccw)  41 us
    ppermute x28, starting transfers between devices, ring_gather(): parts[j] = lax.ppermute(parts[j], axis, cw if clockwise else ccw)  30.5 us
    dot_general x2, matrix products, section_backward(): lax.dot_general(grad_pre, weight, (((1,), (1,)), ((), ())), preferred_ele...  12.8 us
    dot_general x28, matrix products, on_piece(): term = jnp.dot(lhs, piece, preferred_element_type=jnp.float32)  6.36 us
    dot_general x1, matrix products, section_forward(): pre_act = jnp.dot(normed, weight, preferred_element_type=jnp.float32)  5.43 us
    ppermute x3, waiting for transfers between devices, tree_sum(): v = v + lax.ppermute(v, axis, [(i, i ^ b) for i in range(n)])  5.35 us
    ppermute x3, starting transfers between devices, tree_sum(): v = v + lax.ppermute(v, axis, [(i, i ^ b) for i in range(n)])  4.83 us
    ppermute x3, starting transfers between devices, shifted(): return lax.ppermute(x, axis, pairs)  4.32 us
  transfers between devices with their start and end apart: 34, of which 30 were waited for; matrix products, arithmetic and copies ran while one was open for 9% of the time, Pallas kernels for 0%

profile of v9, /device:TPU:0, one launch (start us, length us, event | category | flops | bytes accessed | tf_op | source)
XLA Modules:
  0.0 143.5 jit_solution(6103961832267484637)
XLA Ops:
  0.6 2.1 %fusion.143 = (bf16[256,512]{1,0:T(8,128)(2,1)S(1)}, bf16[256,512]{1,0:T(8,128)(2,1)S(1)}, bf16[256,512]{1,0:T(8,128)(2,1)S(1)}, bf16[256,512]{1,0:T(8,128)(2,1)}) fusion(bf16[256,2048]{1,0:T(8,128)(2,1)} %bitcast.95), kind=kLoop, calls=%fused_computation.239 | loop fusion | bytes 2097152 | tf_op jit(solution)/shard_map/slice | solution.py:106
  2.7 3.1 %collective-permute-start = (bf16[256,512]{1,0:T(8,128)(2,1)}, bf16[256,512]{1,0:T(8,128)(2,1)S(1)}, u32[]{:S(2)}, u32[]{:S(2)}) collective-permute-start(bf16[256,512]{1,0:T(8,128)(2,1)} %get-tuple-element.43), channel_id=1, source_target_pairs={{0,4},{4,8},{8,12},{12,14},{14,10},{10,6},{6,2},{2,0},{1,5},{5,9},... | collective-permute-start | bytes 786440 | tf_op jit(solution)/shard_map/ppermute | solution.py:113
  5.8 2.0 %collective-permute-start.14 = (bf16[256,512]{1,0:T(8,128)(2,1)S(1)}, bf16[256,512]{1,0:T(8,128)(2,1)S(1)}, u32[]{:S(2)}, u32[]{:S(2)}) collective-permute-start(bf16[256,512]{1,0:T(8,128)(2,1)S(1)} %get-tuple-element.42), channel_id=1, source_target_pairs={{0,4},{4,8},{8,12},{12,14},{14,10},{10,6},{6,2},{2,0},{1,5},{5,9},... | collective-permute-start | bytes 786440 | tf_op jit(solution)/shard_map/ppermute | solution.py:113
  9.8 3.2 %collective-permute-done = bf16[256,512]{1,0:T(8,128)(2,1)S(1)} collective-permute-done((bf16[256,512]{1,0:T(8,128)(2,1)}, bf16[256,512]{1,0:T(8,128)(2,1)S(1)}, u32[]{:S(2)}, u32[]{:S(2)}) %collective-permute-start) | collective-permute-done | bytes 262176 | tf_op jit(solution)/shard_map/ppermute | solution.py:113
  15.2 2.2 %collective-permute-start.1 = (bf16[256,512]{1,0:T(8,128)(2,1)S(1)}, bf16[256,512]{1,0:T(8,128)(2,1)S(1)}, u32[]{:S(2)}, u32[]{:S(2)}) collective-permute-start(bf16[256,512]{1,0:T(8,128)(2,1)S(1)} %collective-permute-done), channel_id=1, source_target_pairs={{0,4},{4,8},{8,12},{12,14},{14,10},{10,6},{6,2},{2,0},{1,5},{5,9},... | collective-permute-start | bytes 786440 | tf_op jit(solution)/shard_map/ppermute | solution.py:113
  19.1 2.1 %collective-permute-start.15 = (bf16[256,512]{1,0:T(8,128)(2,1)S(1)}, bf16[256,512]{1,0:T(8,128)(2,1)S(1)}, u32[]{:S(2)}, u32[]{:S(2)}) collective-permute-start(bf16[256,512]{1,0:T(8,128)(2,1)S(1)} %collective-permute-done.14), channel_id=1, source_target_pairs={{0,4},{4,8},{8,12},{12,14},{14,10},{10,6},{6,2},{2,0},{1,5},{5,9},... | collective-permute-start | bytes 786440 | tf_op jit(solution)/shard_map/ppermute | solution.py:113
  21.7 2.7 %collective-permute-done.1 = bf16[256,512]{1,0:T(8,128)(2,1)S(1)} collective-permute-done((bf16[256,512]{1,0:T(8,128)(2,1)S(1)}, bf16[256,512]{1,0:T(8,128)(2,1)S(1)}, u32[]{:S(2)}, u32[]{:S(2)}) %collective-permute-start.1) | collective-permute-done | bytes 262176 | tf_op jit(solution)/shard_map/ppermute | solution.py:113
  24.5 2.1 %collective-permute-start.2 = (bf16[256,512]{1,0:T(8,128)(2,1)S(1)}, bf16[256,512]{1,0:T(8,128)(2,1)S(1)}, u32[]{:S(2)}, u32[]{:S(2)}) collective-permute-start(bf16[256,512]{1,0:T(8,128)(2,1)S(1)} %collective-permute-done.1), channel_id=1, source_target_pairs={{0,4},{4,8},{8,12},{12,14},{14,10},{10,6},{6,2},{2,0},{1,5},{5,9},... | collective-permute-start | bytes 786440 | tf_op jit(solution)/shard_map/ppermute | solution.py:113
  26.6 1.4 collective-permute-done.8
  28.0 2.1 %collective-permute-done.15 = bf16[256,512]{1,0:T(8,128)(2,1)S(1)} collective-permute-done((bf16[256,512]{1,0:T(8,128)(2,1)S(1)}, bf16[256,512]{1,0:T(8,128)(2,1)S(1)}, u32[]{:S(2)}, u32[]{:S(2)}) %collective-permute-start.15) | collective-permute-done | bytes 262176 | tf_op jit(solution)/shard_map/ppermute | solution.py:113
  30.1 2.1 %collective-permute-start.16 = (bf16[256,512]{1,0:T(8,128)(2,1)S(1)}, bf16[256,512]{1,0:T(8,128)(2,1)S(1)}, u32[]{:S(2)}, u32[]{:S(2)}) collective-permute-start(bf16[256,512]{1,0:T(8,128)(2,1)S(1)} %collective-permute-done.15), channel_id=1, source_target_pairs={{0,4},{4,8},{8,12},{12,14},{14,10},{10,6},{6,2},{2,0},{1,5},{5,9},... | collective-permute-start | bytes 786440 | tf_op jit(solution)/shard_map/ppermute | solution.py:113
  35.7 2.1 %collective-permute-start.3 = (bf16[256,512]{1,0:T(8,128)(2,1)S(1)}, bf16[256,512]{1,0:T(8,128)(2,1)S(1)}, u32[]{:S(2)}, u32[]{:S(2)}) collective-permute-start(bf16[256,512]{1,0:T(8,128)(2,1)S(1)} %collective-permute-done.2), channel_id=1, source_target_pairs={{0,4},{4,8},{8,12},{12,14},{14,10},{10,6},{6,2},{2,0},{1,5},{5,9},... | collective-permute-start | bytes 786440 | tf_op jit(solution)/shard_map/ppermute | solution.py:113
  37.8 1.4 collective-permute-done.9
  39.2 2.1 %collective-permute-done.16 = bf16[256,512]{1,0:T(8,128)(2,1)S(1)} collective-permute-done((bf16[256,512]{1,0:T(8,128)(2,1)S(1)}, bf16[256,512]{1,0:T(8,128)(2,1)S(1)}, u32[]{:S(2)}, u32[]{:S(2)}) %collective-permute-start.16) | collective-permute-done | bytes 262176 | tf_op jit(solution)/shard_map/ppermute | solution.py:113
  41.3 2.1 %collective-permute-start.17 = (bf16[256,512]{1,0:T(8,128)(2,1)S(1)}, bf16[256,512]{1,0:T(8,128)(2,1)S(1)}, u32[]{:S(2)}, u32[]{:S(2)}) collective-permute-start(bf16[256,512]{1,0:T(8,128)(2,1)S(1)} %collective-permute-done.16), channel_id=1, source_target_pairs={{0,4},{4,8},{8,12},{12,14},{14,10},{10,6},{6,2},{2,0},{1,5},{5,9},... | collective-permute-start | bytes 786440 | tf_op jit(solution)/shard_map/ppermute | solution.py:113
  46.9 2.1 %collective-permute-start.4 = (bf16[256,512]{1,0:T(8,128)(2,1)S(1)}, bf16[256,512]{1,0:T(8,128)(2,1)S(1)}, u32[]{:S(2)}, u32[]{:S(2)}) collective-permute-start(bf16[256,512]{1,0:T(8,128)(2,1)S(1)} %collective-permute-done.3), channel_id=1, source_target_pairs={{0,4},{4,8},{8,12},{12,14},{14,10},{10,6},{6,2},{2,0},{1,5},{5,9},... | collective-permute-start | bytes 786440 | tf_op jit(solution)/shard_map/ppermute | solution.py:113
  49.0 1.4 collective-permute-done.10
  50.4 2.1 %collective-permute-done.17 = bf16[256,512]{1,0:T(8,128)(2,1)S(1)} collective-permute-done((bf16[256,512]{1,0:T(8,128)(2,1)S(1)}, bf16[256,512]{1,0:T(8,128)(2,1)S(1)}, u32[]{:S(2)}, u32[]{:S(2)}) %collective-permute-start.17) | collective-permute-done | bytes 262176 | tf_op jit(solution)/shard_map/ppermute | solution.py:113
  52.6 2.1 %collective-permute-start.18 = (bf16[256,512]{1,0:T(8,128)(2,1)S(1)}, bf16[256,512]{1,0:T(8,128)(2,1)S(1)}, u32[]{:S(2)}, u32[]{:S(2)}) collective-permute-start(bf16[256,512]{1,0:T(8,128)(2,1)S(1)} %collective-permute-done.17), channel_id=1, source_target_pairs={{0,4},{4,8},{8,12},{12,14},{14,10},{10,6},{6,2},{2,0},{1,5},{5,9},... | collective-permute-start | bytes 786440 | tf_op jit(solution)/shard_map/ppermute | solution.py:113
  54.7 1.4 collective-permute-done.24
  58.2 2.1 %collective-permute-start.5 = (bf16[256,512]{1,0:T(8,128)(2,1)S(1)}, bf16[256,512]{1,0:T(8,128)(2,1)S(1)}, u32[]{:S(2)}, u32[]{:S(2)}) collective-permute-start(bf16[256,512]{1,0:T(8,128)(2,1)S(1)} %collective-permute-done.4), channel_id=1, source_target_pairs={{0,4},{4,8},{8,12},{12,14},{14,10},{10,6},{6,2},{2,0},{1,5},{5,9},... | collective-permute-start | bytes 786440 | tf_op jit(solution)/shard_map/ppermute | solution.py:113
  60.3 1.4 collective-permute-done.11
  61.7 2.1 %collective-permute-done.18 = bf16[256,512]{1,0:T(8,128)(2,1)S(1)} collective-permute-done((bf16[256,512]{1,0:T(8,128)(2,1)S(1)}, bf16[256,512]{1,0:T(8,128)(2,1)S(1)}, u32[]{:S(2)}, u32[]{:S(2)}) %collective-permute-start.18) | collective-permute-done | bytes 262176 | tf_op jit(solution)/shard_map/ppermute | solution.py:113
  63.8 2.1 %collective-permute-start.19 = (bf16[256,512]{1,0:T(8,128)(2,1)S(1)}, bf16[256,512]{1,0:T(8,128)(2,1)S(1)}, u32[]{:S(2)}, u32[]{:S(2)}) collective-permute-start(bf16[256,512]{1,0:T(8,128)(2,1)S(1)} %collective-permute-done.18), channel_id=1, source_target_pairs={{0,4},{4,8},{8,12},{12,14},{14,10},{10,6},{6,2},{2,0},{1,5},{5,9},... | collective-permute-start | bytes 786440 | tf_op jit(solution)/shard_map/ppermute | solution.py:113
  65.9 1.4 collective-permute-done.25
  69.4 2.1 %collective-permute-start.6 = (bf16[256,512]{1,0:T(8,128)(2,1)S(1)}, bf16[256,512]{1,0:T(8,128)(2,1)S(1)}, u32[]{:S(2)}, u32[]{:S(2)}) collective-permute-start(bf16[256,512]{1,0:T(8,128)(2,1)S(1)} %collective-permute-done.5), channel_id=1, source_target_pairs={{0,4},{4,8},{8,12},{12,14},{14,10},{10,6},{6,2},{2,0},{1,5},{5,9},... | collective-permute-start | bytes 786440 | tf_op jit(solution)/shard_map/ppermute | solution.py:113
  71.5 1.4 collective-permute-done.12
  72.9 2.1 %collective-permute-done.19 = bf16[256,512]{1,0:T(8,128)(2,1)S(1)} collective-permute-done((bf16[256,512]{1,0:T(8,128)(2,1)S(1)}, bf16[256,512]{1,0:T(8,128)(2,1)S(1)}, u32[]{:S(2)}, u32[]{:S(2)}) %collective-permute-start.19) | collective-permute-done | bytes 262176 | tf_op jit(solution)/shard_map/ppermute | solution.py:113
  75.0 2.1 %collective-permute-start.20 = (bf16[256,512]{1,0:T(8,128)(2,1)S(1)}, bf16[256,512]{1,0:T(8,128)(2,1)S(1)}, u32[]{:S(2)}, u32[]{:S(2)}) collective-permute-start(bf16[256,512]{1,0:T(8,128)(2,1)S(1)} %collective-permute-done.19), channel_id=1, source_target_pairs={{0,4},{4,8},{8,12},{12,14},{14,10},{10,6},{6,2},{2,0},{1,5},{5,9},... | collective-permute-start | bytes 786440 | tf_op jit(solution)/shard_map/ppermute | solution.py:113
  77.2 1.4 collective-permute-done.26
  80.9 2.9 %collective-permute-done.13 = bf16[256,512]{1,0:T(8,128)(2,1)S(1)} collective-permute-done((bf16[256,512]{1,0:T(8,128)(2,1)S(1)}, bf16[256,512]{1,0:T(8,128)(2,1)S(1)}, u32[]{:S(2)}, u32[]{:S(2)}) %collective-permute-start.13) | collective-permute-done | bytes 262176 | tf_op jit(solution)/shard_map/ppermute | solution.py:113
  86.8 2.5 %fusion.32 = (f32[256,2048]{1,0:T(8,128)}, bf16[256,2048]{1,0:T(8,128)(2,1)S(1)}) fusion(f32[256,512]{1,0:T(8,128)S(1)} %fusion.40, f32[256,512]{1,0:T(8,128)S(1)} %fusion.41, f32[256,512]{1,0:T(8,128)S(1)} %fusion.42, f32[256,512]{1,0:T(8,128)S(1)} %fusion.43, bf16[256,2048]{1,0:T(8,128)(2,1)S(1)} %bitcast.92), kind=kLoop, calls=%fused_computation.47 | loop fusion | flops 12582912 | bytes 6291456 | tf_op jit(solution)/shard_map/add | solution.py:28
  89.3 1.5 %collective-permute-start.28 = (bf16[256,2048]{1,0:T(8,128)(2,1)S(1)}, bf16[256,2048]{1,0:T(8,128)(2,1)S(1)}, u32[]{:S(2)}, u32[]{:S(2)}) collective-permute-start(bf16[256,2048]{1,0:T(8,128)(2,1)S(1)} %get-tuple-element.37), channel_id=1, source_target_pairs={{0,1},{2,3},{4,5},{6,7},{8,9},{10,11},{12,13},{14,15},{16,17},{18,... | collective-permute-start | bytes 3145736 | tf_op jit(solution)/shard_map/ppermute | solution.py:18
  91.2 1.6 %collective-permute-done.28 = bf16[256,2048]{1,0:T(8,128)(2,1)S(1)} collective-permute-done((bf16[256,2048]{1,0:T(8,128)(2,1)S(1)}, bf16[256,2048]{1,0:T(8,128)(2,1)S(1)}, u32[]{:S(2)}, u32[]{:S(2)}) %collective-permute-start.28) | collective-permute-done | bytes 1048608 | tf_op jit(solution)/shard_map/ppermute | solution.py:18
  93.5 5.4 %fusion.141 = (f32[256,2048]{1,0:T(8,128)S(1)}, bf16[256,2048]{1,0:T(8,128)(2,1)}, f32[256,2048]{1,0:T(8,128)}) fusion(bf16[256,2048]{1,0:T(8,128)(2,1)S(1)} %collective-permute-done.28, bf16[2048,2048]{1,0:T(8,128)(2,1)S(1)} %constant_dynamic-update-slice_fusion, f32[256]{0:T(256)S(1)} %add_rsqrt_fusion, f32[256]{0:T(256)S(1)} %broadcast_multiply_fusion.4, ...), kind=kOutput, calls=%fused_computation.238 | convolution fusion | flops 2161639424 | bytes 14690304 | tf_op jit(solution)/shard_map/dot_general | solution.py:50
  101.1 1.4 slice_convert_fusion.1
  102.5 1.5 %collective-permute-done.29 = f32[7]{0:T(128)S(1)} collective-permute-done((f32[7]{0:T(128)S(1)}, f32[7]{0:T(128)S(1)}, u32[]{:S(2)}, u32[]{:S(2)}) %collective-permute-start.29) | collective-permute-done | bytes 60 | tf_op jit(solution)/shard_map/ppermute | solution.py:128
  104.7 1.6 %collective-permute-start.30 = (f32[7]{0:T(128)S(1)}, f32[7]{0:T(128)S(1)}, u32[]{:S(2)}, u32[]{:S(2)}) collective-permute-start(f32[7]{0:T(128)S(1)} %fusion.176), channel_id=1, source_target_pairs={{0,4},{2,6},{4,0},{6,2},{8,12},{10,14},{12,8},{14,10},{1,5},{3,7},... | collective-permute-start | bytes 92 | tf_op jit(solution)/shard_map/ppermute | solution.py:128
  106.3 2.0 %collective-permute-done.30 = f32[7]{0:T(128)S(1)} collective-permute-done((f32[7]{0:T(128)S(1)}, f32[7]{0:T(128)S(1)}, u32[]{:S(2)}, u32[]{:S(2)}) %collective-permute-start.30) | collective-permute-done | bytes 60 | tf_op jit(solution)/shard_map/ppermute | solution.py:128
  108.3 2.6 %collective-permute-start.31 = (f32[7]{0:T(128)S(1)}, f32[7]{0:T(128)S(1)}, u32[]{:S(2)}, u32[]{:S(2)}) collective-permute-start(f32[7]{0:T(128)S(1)} %add.453), channel_id=1, source_target_pairs={{0,8},{2,10},{4,12},{6,14},{8,0},{10,2},{12,4},{14,6},{1,9},{3,11}... | collective-permute-start | bytes 92 | tf_op jit(solution)/shard_map/ppermute | solution.py:128
  110.9 1.9 %collective-permute-done.31 = f32[7]{0:T(128)S(1)} collective-permute-done((f32[7]{0:T(128)S(1)}, f32[7]{0:T(128)S(1)}, u32[]{:S(2)}, u32[]{:S(2)}) %collective-permute-start.31) | collective-permute-done | bytes 60 | tf_op jit(solution)/shard_map/ppermute | solution.py:128
  116.5 2.5 %fusion.39 = bf16[256,2048]{1,0:T(8,128)(2,1)S(1)} fusion(f32[256,2048]{1,0:T(8,128)} %get-tuple-element.12, f32[128,2048]{1,0:T(8,128)S(1)} %get-tuple-element.39, f32[256]{0:T(256)S(1)} %get-tuple-element.46, f32[128,2048]{1,0:T(8,128)S(1)} %get-tuple-element.38, f32[256]{0:T(256)S(1)} %get-tuple-element.47, f32[128,2048]{1,0:T(8,128)} %convert_element_type.68, ...), kind=kLoop, calls=%fused_computation.58 | loop fusion | flops 3670016 | bytes 6294528 | tf_op jit(solution)/shard_map/convert_element_type | solution.py:56
  119.0 6.1 %fusion.135 = (f32[256]{0:T(256)S(1)}, f32[256]{0:T(256)S(1)}, f32[256,2048]{1,0:T(8,128)S(1)}) fusion(f32[256]{0:T(256)S(1)} %add_rsqrt_fusion, f32[256]{0:T(256)S(1)} %broadcast_multiply_fusion.4, bf16[256,2048]{1,0:T(8,128)(2,1)S(1)} %copy-done.4, f32[2048]{0:T(1024)S(1)} %bitcast.104, bf16[256,2048]{1,0:T(8,128)(2,1)S(1)} %fusion.39, ...), kind=kOutput, calls=%fused_computation.234 | convolution fusion | flops 2151153152 | bytes 12595200 | tf_op jit(solution)/shard_map/dot_general | solution.py:57
  125.2 2.1 %fusion.15 = bf16[256,2048]{1,0:T(8,128)(2,1)} fusion(bf16[256,2048]{1,0:T(8,128)(2,1)S(1)} %copy-done.4, f32[256,2048]{1,0:T(8,128)S(1)} %get-tuple-element.44, f32[256]{0:T(256)S(1)} %broadcast_multiply_fusion.2, f32[256]{0:T(256)S(1)} %broadcast_multiply_fusion.3, f32[128,2048]{1,0:T(8,128)S(1)} %get-tuple-element.39, f32[256]{0:T(256)S(1)} %get-tuple-element.46, ...), kind=kLoop, calls=%fused_computation.30 | loop fusion | flops 7340032 | bytes 7347200 | tf_op jit(solution)/shard_map/convert_element_type | solution.py:66
  129.8 1.5 %collective-permute-start.33 = (f32[1]{0:T(128)}, f32[1]{0:T(128)}, u32[]{:S(2)}, u32[]{:S(2)}) collective-permute-start(f32[1]{0:T(128)} %bitcast.21), channel_id=1, source_target_pairs={{1,0},{3,2},{5,4},{7,6},{9,8},{11,10},{13,12},{15,14},{17,16},{19,... | collective-permute-start | bytes 20 | tf_op jit(solution)/shard_map/ppermute | solution.py:18
  131.3 1.7 %collective-permute-done.33 = f32[1]{0:T(128)} collective-permute-done((f32[1]{0:T(128)}, f32[1]{0:T(128)}, u32[]{:S(2)}, u32[]{:S(2)}) %collective-permute-start.33) | collective-permute-done | bytes 36 | tf_op jit(solution)/shard_map/ppermute | solution.py:18
  133.6 6.7 %fusion.134 = (f32[256]{0:T(256)S(1)}, f32[256]{0:T(256)S(1)}, f32[256,2048]{1,0:T(8,128)S(1)}) fusion(f32[256]{0:T(256)S(1)} %add_rsqrt_fusion.1, f32[256]{0:T(256)S(1)} %broadcast_multiply_fusion.5, bf16[256,2048]{1,0:T(8,128)(2,1)S(1)} %bitcast.93, f32[2048]{0:T(1024)S(1)} %bitcast.105, bf16[2048,2048]{1,0:T(8,128)(2,1)} %copy-done.5, ...), kind=kOutput, calls=%fused_computation.233 | convolution fusion | flops 2152726016 | bytes 14692352 | tf_op jit(solution)/shard_map/dot_general | solution.py:57
  140.3 2.0 %fusion.44 = bf16[256,2048]{1,0:T(8,128)(2,1)} fusion(bf16[256,2048]{1,0:T(8,128)(2,1)} %fusion.15, bf16[256,2048]{1,0:T(8,128)(2,1)S(1)} %bitcast.94, f32[256,2048]{1,0:T(8,128)S(1)} %get-tuple-element.45, bf16[256,2048]{1,0:T(8,128)(2,1)S(1)} %collective-permute-done.32, f32[256]{0:T(256)S(1)} %broadcast_multiply_fusion, ...), kind=kLoop, calls=%fused_computation.87 | loop fusion | flops 5767168 | bytes 6295553 | tf_op jit(solution)/shard_map/jit(_where)/select_n | solution.py:245
  (142 shorter events, 31.6 us)
Async XLA Ops:
  0.6 7.2 %copy-start.6 = (bf16[128,2048]{1,0:T(8,128)(2,1)S(1)}, bf16[128,2048]{1,0:T(8,128)(2,1)}, u32[]{:S(2)}) copy-start(bf16[128,2048]{1,0:T(8,128)(2,1)} %param.5) | copy-start | bytes 1572868
  0.6 12.4 %copy-start = (bf16[2,128,2048]{2,1,0:T(8,128)(2,1)S(1)}, bf16[2,128,2048]{2,1,0:T(8,128)(2,1)}, u32[]{:S(2)}) copy-start(bf16[2,128,2048]{2,1,0:T(8,128)(2,1)} %param.4) | copy-start | bytes 3145732
  2.7 10.3 %collective-permute-start = (bf16[256,512]{1,0:T(8,128)(2,1)}, bf16[256,512]{1,0:T(8,128)(2,1)S(1)}, u32[]{:S(2)}, u32[]{:S(2)}) collective-permute-start(bf16[256,512]{1,0:T(8,128)(2,1)} %get-tuple-element.43), channel_id=1, source_target_pairs={{0,4},{4,8},{8,12},{12,14},{14,10},{10,6},{6,2},{2,0},{1,5},{5,9},... | collective-permute-start | bytes 786440 | tf_op jit(solution)/shard_map/ppermute | solution.py:113
  5.8 12.9 %collective-permute-start.7 = (bf16[256,512]{1,0:T(8,128)(2,1)S(1)}, bf16[256,512]{1,0:T(8,128)(2,1)S(1)}, u32[]{:S(2)}, u32[]{:S(2)}) collective-permute-start(bf16[256,512]{1,0:T(8,128)(2,1)S(1)} %get-tuple-element.40), channel_id=1, source_target_pairs={{4,0},{8,4},{12,8},{14,12},{10,14},{6,10},{2,6},{0,2},{5,1},{9,5},... | collective-permute-start | bytes 786440 | tf_op jit(solution)/shard_map/ppermute | solution.py:113
  5.8 13.3 %collective-permute-start.14 = (bf16[256,512]{1,0:T(8,128)(2,1)S(1)}, bf16[256,512]{1,0:T(8,128)(2,1)S(1)}, u32[]{:S(2)}, u32[]{:S(2)}) collective-permute-start(bf16[256,512]{1,0:T(8,128)(2,1)S(1)} %get-tuple-element.42), channel_id=1, source_target_pairs={{0,4},{4,8},{8,12},{12,14},{14,10},{10,6},{6,2},{2,0},{1,5},{5,9},... | collective-permute-start | bytes 786440 | tf_op jit(solution)/shard_map/ppermute | solution.py:113
  7.8 13.6 %collective-permute-start.21 = (bf16[256,512]{1,0:T(8,128)(2,1)S(1)}, bf16[256,512]{1,0:T(8,128)(2,1)S(1)}, u32[]{:S(2)}, u32[]{:S(2)}) collective-permute-start(bf16[256,512]{1,0:T(8,128)(2,1)S(1)} %get-tuple-element.41), channel_id=1, source_target_pairs={{4,0},{8,4},{12,8},{14,12},{10,14},{6,10},{2,6},{0,2},{5,1},{9,5},... | collective-permute-start | bytes 786440 | tf_op jit(solution)/shard_map/ppermute | solution.py:113
  7.8 5.9 %copy-start.7 = (f32[1,2048]{1,0:T(1,128)S(1)}, f32[1,2048]{1,0:T(1,128)}, u32[]{:S(2)}) copy-start(f32[1,2048]{1,0:T(1,128)} %param.7) | copy-start | bytes 24580
  13.1 1.2 copy-start.1
  15.2 9.2 %collective-permute-start.1 = (bf16[256,512]{1,0:T(8,128)(2,1)S(1)}, bf16[256,512]{1,0:T(8,128)(2,1)S(1)}, u32[]{:S(2)}, u32[]{:S(2)}) collective-permute-start(bf16[256,512]{1,0:T(8,128)(2,1)S(1)} %collective-permute-done), channel_id=1, source_target_pairs={{0,4},{4,8},{8,12},{12,14},{14,10},{10,6},{6,2},{2,0},{1,5},{5,9},... | collective-permute-start | bytes 786440 | tf_op jit(solution)/shard_map/ppermute | solution.py:113
  18.7 9.2 %collective-permute-start.8 = (bf16[256,512]{1,0:T(8,128)(2,1)S(1)}, bf16[256,512]{1,0:T(8,128)(2,1)S(1)}, u32[]{:S(2)}, u32[]{:S(2)}) collective-permute-start(bf16[256,512]{1,0:T(8,128)(2,1)S(1)} %collective-permute-done.7), channel_id=1, source_target_pairs={{4,0},{8,4},{12,8},{14,12},{10,14},{6,10},{2,6},{0,2},{5,1},{9,5},... | collective-permute-start | bytes 786440 | tf_op jit(solution)/shard_map/ppermute | solution.py:113
  19.1 11.0 %collective-permute-start.15 = (bf16[256,512]{1,0:T(8,128)(2,1)S(1)}, bf16[256,512]{1,0:T(8,128)(2,1)S(1)}, u32[]{:S(2)}, u32[]{:S(2)}) collective-permute-start(bf16[256,512]{1,0:T(8,128)(2,1)S(1)} %collective-permute-done.14), channel_id=1, source_target_pairs={{0,4},{4,8},{8,12},{12,14},{14,10},{10,6},{6,2},{2,0},{1,5},{5,9},... | collective-permute-start | bytes 786440 | tf_op jit(solution)/shard_map/ppermute | solution.py:113
  21.4 12.2 %collective-permute-start.22 = (bf16[256,512]{1,0:T(8,128)(2,1)S(1)}, bf16[256,512]{1,0:T(8,128)(2,1)S(1)}, u32[]{:S(2)}, u32[]{:S(2)}) collective-permute-start(bf16[256,512]{1,0:T(8,128)(2,1)S(1)} %collective-permute-done.21), channel_id=1, source_target_pairs={{4,0},{8,4},{12,8},{14,12},{10,14},{6,10},{2,6},{0,2},{5,1},{9,5},... | collective-permute-start | bytes 786440 | tf_op jit(solution)/shard_map/ppermute | solution.py:113
  24.5 11.2 %collective-permute-start.2 = (bf16[256,512]{1,0:T(8,128)(2,1)S(1)}, bf16[256,512]{1,0:T(8,128)(2,1)S(1)}, u32[]{:S(2)}, u32[]{:S(2)}) collective-permute-start(bf16[256,512]{1,0:T(8,128)(2,1)S(1)} %collective-permute-done.1), channel_id=1, source_target_pairs={{0,4},{4,8},{8,12},{12,14},{14,10},{10,6},{6,2},{2,0},{1,5},{5,9},... | collective-permute-start | bytes 786440 | tf_op jit(solution)/shard_map/ppermute | solution.py:113
  28.0 11.2 %collective-permute-start.9 = (bf16[256,512]{1,0:T(8,128)(2,1)S(1)}, bf16[256,512]{1,0:T(8,128)(2,1)S(1)}, u32[]{:S(2)}, u32[]{:S(2)}) collective-permute-start(bf16[256,512]{1,0:T(8,128)(2,1)S(1)} %collective-permute-done.8), channel_id=1, source_target_pairs={{4,0},{8,4},{12,8},{14,12},{10,14},{6,10},{2,6},{0,2},{5,1},{9,5},... | collective-permute-start | bytes 786440 | tf_op jit(solution)/shard_map/ppermute | solution.py:113
  30.1 11.2 %collective-permute-start.16 = (bf16[256,512]{1,0:T(8,128)(2,1)S(1)}, bf16[256,512]{1,0:T(8,128)(2,1)S(1)}, u32[]{:S(2)}, u32[]{:S(2)}) collective-permute-start(bf16[256,512]{1,0:T(8,128)(2,1)S(1)} %collective-permute-done.15), channel_id=1, source_target_pairs={{0,4},{4,8},{8,12},{12,14},{14,10},{10,6},{6,2},{2,0},{1,5},{5,9},... | collective-permute-start | bytes 786440 | tf_op jit(solution)/shard_map/ppermute | solution.py:113
  33.6 11.2 %collective-permute-start.23 = (bf16[256,512]{1,0:T(8,128)(2,1)S(1)}, bf16[256,512]{1,0:T(8,128)(2,1)S(1)}, u32[]{:S(2)}, u32[]{:S(2)}) collective-permute-start(bf16[256,512]{1,0:T(8,128)(2,1)S(1)} %collective-permute-done.22), channel_id=1, source_target_pairs={{4,0},{8,4},{12,8},{14,12},{10,14},{6,10},{2,6},{0,2},{5,1},{9,5},... | collective-permute-start | bytes 786440 | tf_op jit(solution)/shard_map/ppermute | solution.py:113
  35.7 11.2 %collective-permute-start.3 = (bf16[256,512]{1,0:T(8,128)(2,1)S(1)}, bf16[256,512]{1,0:T(8,128)(2,1)S(1)}, u32[]{:S(2)}, u32[]{:S(2)}) collective-permute-start(bf16[256,512]{1,0:T(8,128)(2,1)S(1)} %collective-permute-done.2), channel_id=1, source_target_pairs={{0,4},{4,8},{8,12},{12,14},{14,10},{10,6},{6,2},{2,0},{1,5},{5,9},... | collective-permute-start | bytes 786440 | tf_op jit(solution)/shard_map/ppermute | solution.py:113
  39.2 11.2 %collective-permute-start.10 = (bf16[256,512]{1,0:T(8,128)(2,1)S(1)}, bf16[256,512]{1,0:T(8,128)(2,1)S(1)}, u32[]{:S(2)}, u32[]{:S(2)}) collective-permute-start(bf16[256,512]{1,0:T(8,128)(2,1)S(1)} %collective-permute-done.9), channel_id=1, source_target_pairs={{4,0},{8,4},{12,8},{14,12},{10,14},{6,10},{2,6},{0,2},{5,1},{9,5},... | collective-permute-start | bytes 786440 | tf_op jit(solution)/shard_map/ppermute | solution.py:113
  41.3 11.2 %collective-permute-start.17 = (bf16[256,512]{1,0:T(8,128)(2,1)S(1)}, bf16[256,512]{1,0:T(8,128)(2,1)S(1)}, u32[]{:S(2)}, u32[]{:S(2)}) collective-permute-start(bf16[256,512]{1,0:T(8,128)(2,1)S(1)} %collective-permute-done.16), channel_id=1, source_target_pairs={{0,4},{4,8},{8,12},{12,14},{14,10},{10,6},{6,2},{2,0},{1,5},{5,9},... | collective-permute-start | bytes 786440 | tf_op jit(solution)/shard_map/ppermute | solution.py:113
  44.8 11.2 %collective-permute-start.24 = (bf16[256,512]{1,0:T(8,128)(2,1)S(1)}, bf16[256,512]{1,0:T(8,128)(2,1)S(1)}, u32[]{:S(2)}, u32[]{:S(2)}) collective-permute-start(bf16[256,512]{1,0:T(8,128)(2,1)S(1)} %collective-permute-done.23), channel_id=1, source_target_pairs={{4,0},{8,4},{12,8},{14,12},{10,14},{6,10},{2,6},{0,2},{5,1},{9,5},... | collective-permute-start | bytes 786440 | tf_op jit(solution)/shard_map/ppermute | solution.py:113
  46.9 11.2 %collective-permute-start.4 = (bf16[256,512]{1,0:T(8,128)(2,1)S(1)}, bf16[256,512]{1,0:T(8,128)(2,1)S(1)}, u32[]{:S(2)}, u32[]{:S(2)}) collective-permute-start(bf16[256,512]{1,0:T(8,128)(2,1)S(1)} %collective-permute-done.3), channel_id=1, source_target_pairs={{0,4},{4,8},{8,12},{12,14},{14,10},{10,6},{6,2},{2,0},{1,5},{5,9},... | collective-permute-start | bytes 786440 | tf_op jit(solution)/shard_map/ppermute | solution.py:113
  50.4 11.2 %collective-permute-start.11 = (bf16[256,512]{1,0:T(8,128)(2,1)S(1)}, bf16[256,512]{1,0:T(8,128)(2,1)S(1)}, u32[]{:S(2)}, u32[]{:S(2)}) collective-permute-start(bf16[256,512]{1,0:T(8,128)(2,1)S(1)} %collective-permute-done.10), channel_id=1, source_target_pairs={{4,0},{8,4},{12,8},{14,12},{10,14},{6,10},{2,6},{0,2},{5,1},{9,5},... | collective-permute-start | bytes 786440 | tf_op jit(solution)/shard_map/ppermute | solution.py:113
  52.6 11.2 %collective-permute-start.18 = (bf16[256,512]{1,0:T(8,128)(2,1)S(1)}, bf16[256,512]{1,0:T(8,128)(2,1)S(1)}, u32[]{:S(2)}, u32[]{:S(2)}) collective-permute-start(bf16[256,512]{1,0:T(8,128)(2,1)S(1)} %collective-permute-done.17), channel_id=1, source_target_pairs={{0,4},{4,8},{8,12},{12,14},{14,10},{10,6},{6,2},{2,0},{1,5},{5,9},... | collective-permute-start | bytes 786440 | tf_op jit(solution)/shard_map/ppermute | solution.py:113
  56.1 11.2 %collective-permute-start.25 = (bf16[256,512]{1,0:T(8,128)(2,1)S(1)}, bf16[256,512]{1,0:T(8,128)(2,1)S(1)}, u32[]{:S(2)}, u32[]{:S(2)}) collective-permute-start(bf16[256,512]{1,0:T(8,128)(2,1)S(1)} %collective-permute-done.24), channel_id=1, source_target_pairs={{4,0},{8,4},{12,8},{14,12},{10,14},{6,10},{2,6},{0,2},{5,1},{9,5},... | collective-permute-start | bytes 786440 | tf_op jit(solution)/shard_map/ppermute | solution.py:113
  58.2 11.2 %collective-permute-start.5 = (bf16[256,512]{1,0:T(8,128)(2,1)S(1)}, bf16[256,512]{1,0:T(8,128)(2,1)S(1)}, u32[]{:S(2)}, u32[]{:S(2)}) collective-permute-start(bf16[256,512]{1,0:T(8,128)(2,1)S(1)} %collective-permute-done.4), channel_id=1, source_target_pairs={{0,4},{4,8},{8,12},{12,14},{14,10},{10,6},{6,2},{2,0},{1,5},{5,9},... | collective-permute-start | bytes 786440 | tf_op jit(solution)/shard_map/ppermute | solution.py:113
  61.7 11.2 %collective-permute-start.12 = (bf16[256,512]{1,0:T(8,128)(2,1)S(1)}, bf16[256,512]{1,0:T(8,128)(2,1)S(1)}, u32[]{:S(2)}, u32[]{:S(2)}) collective-permute-start(bf16[256,512]{1,0:T(8,128)(2,1)S(1)} %collective-permute-done.11), channel_id=1, source_target_pairs={{4,0},{8,4},{12,8},{14,12},{10,14},{6,10},{2,6},{0,2},{5,1},{9,5},... | collective-permute-start | bytes 786440 | tf_op jit(solution)/shard_map/ppermute | solution.py:113
  63.8 11.2 %collective-permute-start.19 = (bf16[256,512]{1,0:T(8,128)(2,1)S(1)}, bf16[256,512]{1,0:T(8,128)(2,1)S(1)}, u32[]{:S(2)}, u32[]{:S(2)}) collective-permute-start(bf16[256,512]{1,0:T(8,128)(2,1)S(1)} %collective-permute-done.18), channel_id=1, source_target_pairs={{0,4},{4,8},{8,12},{12,14},{14,10},{10,6},{6,2},{2,0},{1,5},{5,9},... | collective-permute-start | bytes 786440 | tf_op jit(solution)/shard_map/ppermute | solution.py:113
  67.3 11.2 %collective-permute-start.26 = (bf16[256,512]{1,0:T(8,128)(2,1)S(1)}, bf16[256,512]{1,0:T(8,128)(2,1)S(1)}, u32[]{:S(2)}, u32[]{:S(2)}) collective-permute-start(bf16[256,512]{1,0:T(8,128)(2,1)S(1)} %collective-permute-done.25), channel_id=1, source_target_pairs={{4,0},{8,4},{12,8},{14,12},{10,14},{6,10},{2,6},{0,2},{5,1},{9,5},... | collective-permute-start | bytes 786440 | tf_op jit(solution)/shard_map/ppermute | solution.py:113
  69.4 11.2 %collective-permute-start.6 = (bf16[256,512]{1,0:T(8,128)(2,1)S(1)}, bf16[256,512]{1,0:T(8,128)(2,1)S(1)}, u32[]{:S(2)}, u32[]{:S(2)}) collective-permute-start(bf16[256,512]{1,0:T(8,128)(2,1)S(1)} %collective-permute-done.5), channel_id=1, source_target_pairs={{0,4},{4,8},{8,12},{12,14},{14,10},{10,6},{6,2},{2,0},{1,5},{5,9},... | collective-permute-start | bytes 786440 | tf_op jit(solution)/shard_map/ppermute | solution.py:113
  72.9 10.9 %collective-permute-start.13 = (bf16[256,512]{1,0:T(8,128)(2,1)S(1)}, bf16[256,512]{1,0:T(8,128)(2,1)S(1)}, u32[]{:S(2)}, u32[]{:S(2)}) collective-permute-start(bf16[256,512]{1,0:T(8,128)(2,1)S(1)} %collective-permute-done.12), channel_id=1, source_target_pairs={{4,0},{8,4},{12,8},{14,12},{10,14},{6,10},{2,6},{0,2},{5,1},{9,5},... | collective-permute-start | bytes 786440 | tf_op jit(solution)/shard_map/ppermute | solution.py:113
  75.0 10.2 %collective-permute-start.20 = (bf16[256,512]{1,0:T(8,128)(2,1)S(1)}, bf16[256,512]{1,0:T(8,128)(2,1)S(1)}, u32[]{:S(2)}, u32[]{:S(2)}) collective-permute-start(bf16[256,512]{1,0:T(8,128)(2,1)S(1)} %collective-permute-done.19), channel_id=1, source_target_pairs={{0,4},{4,8},{8,12},{12,14},{14,10},{10,6},{6,2},{2,0},{1,5},{5,9},... | collective-permute-start | bytes 786440 | tf_op jit(solution)/shard_map/ppermute | solution.py:113
  78.5 8.1 %collective-permute-start.27 = (bf16[256,512]{1,0:T(8,128)(2,1)S(1)}, bf16[256,512]{1,0:T(8,128)(2,1)S(1)}, u32[]{:S(2)}, u32[]{:S(2)}) collective-permute-start(bf16[256,512]{1,0:T(8,128)(2,1)S(1)} %collective-permute-done.26), channel_id=1, source_target_pairs={{4,0},{8,4},{12,8},{14,12},{10,14},{6,10},{2,6},{0,2},{5,1},{9,5},... | collective-permute-start | bytes 786440 | tf_op jit(solution)/shard_map/ppermute | solution.py:113
  89.3 3.6 %collective-permute-start.28 = (bf16[256,2048]{1,0:T(8,128)(2,1)S(1)}, bf16[256,2048]{1,0:T(8,128)(2,1)S(1)}, u32[]{:S(2)}, u32[]{:S(2)}) collective-permute-start(bf16[256,2048]{1,0:T(8,128)(2,1)S(1)} %get-tuple-element.37), channel_id=1, source_target_pairs={{0,1},{2,3},{4,5},{6,7},{8,9},{10,11},{12,13},{14,15},{16,17},{18,... | collective-permute-start | bytes 3145736 | tf_op jit(solution)/shard_map/ppermute | solution.py:18
  91.2 7.7 %copy-start.5 = (bf16[2048,2048]{1,0:T(8,128)(2,1)}, bf16[2048,2048]{1,0:T(8,128)(2,1)S(1)}, u32[]{:S(2)}) copy-start(bf16[2048,2048]{1,0:T(8,128)(2,1)S(1)} %constant_dynamic-update-slice_fusion) | copy-start | bytes 25165828
  92.9 6.1 %copy-start.3 = (bf16[256,2048]{1,0:T(8,128)(2,1)}, bf16[256,2048]{1,0:T(8,128)(2,1)S(1)}, u32[]{:S(2)}) copy-start(bf16[256,2048]{1,0:T(8,128)(2,1)S(1)} %collective-permute-done.28) | copy-start | bytes 3145732
  100.4 3.6 %collective-permute-start.29 = (f32[7]{0:T(128)S(1)}, f32[7]{0:T(128)S(1)}, u32[]{:S(2)}, u32[]{:S(2)}) collective-permute-start(f32[7]{0:T(128)S(1)} %pad_maximum_fusion.1), channel_id=1, source_target_pairs={{0,2},{2,0},{4,6},{6,4},{8,10},{10,8},{12,14},{14,12},{1,3},{3,1},... | collective-permute-start | bytes 92 | tf_op jit(solution)/shard_map/ppermute | solution.py:128
  104.7 3.6 %collective-permute-start.30 = (f32[7]{0:T(128)S(1)}, f32[7]{0:T(128)S(1)}, u32[]{:S(2)}, u32[]{:S(2)}) collective-permute-start(f32[7]{0:T(128)S(1)} %fusion.176), channel_id=1, source_target_pairs={{0,4},{2,6},{4,0},{6,2},{8,12},{10,14},{12,8},{14,10},{1,5},{3,7},... | collective-permute-start | bytes 92 | tf_op jit(solution)/shard_map/ppermute | solution.py:128
  108.3 4.5 %collective-permute-start.31 = (f32[7]{0:T(128)S(1)}, f32[7]{0:T(128)S(1)}, u32[]{:S(2)}, u32[]{:S(2)}) collective-permute-start(f32[7]{0:T(128)S(1)} %add.453), channel_id=1, source_target_pairs={{0,8},{2,10},{4,12},{6,14},{8,0},{10,2},{12,4},{14,6},{1,9},{3,11}... | collective-permute-start | bytes 92 | tf_op jit(solution)/shard_map/ppermute | solution.py:128
  116.5 2.5 %copy-start.4 = (bf16[256,2048]{1,0:T(8,128)(2,1)S(1)}, bf16[256,2048]{1,0:T(8,128)(2,1)}, u32[]{:S(2)}) copy-start(bf16[256,2048]{1,0:T(8,128)(2,1)} %copy-done.3) | copy-start | bytes 3145732
  119.0 6.1 %copy-start.2 = (f32[128,2048]{1,0:T(8,128)S(1)}, f32[128,2048]{1,0:T(8,128)}, u32[]{:S(2)}) copy-start(f32[128,2048]{1,0:T(8,128)} %convert_element_type.68) | copy-start | bytes 3145732
  127.3 6.3 %collective-permute-start.32 = (bf16[256,2048]{1,0:T(8,128)(2,1)}, bf16[256,2048]{1,0:T(8,128)(2,1)S(1)}, u32[]{:S(2)}, u32[]{:S(2)}) collective-permute-start(bf16[256,2048]{1,0:T(8,128)(2,1)} %fusion.15), channel_id=1, source_target_pairs={{1,0},{3,2},{5,4},{7,6},{9,8},{11,10},{13,12},{15,14},{17,16},{19,... | collective-permute-start | bytes 3145736 | tf_op jit(solution)/shard_map/ppermute | solution.py:18
  129.8 3.3 %collective-permute-start.33 = (f32[1]{0:T(128)}, f32[1]{0:T(128)}, u32[]{:S(2)}, u32[]{:S(2)}) collective-permute-start(f32[1]{0:T(128)} %bitcast.21), channel_id=1, source_target_pairs={{1,0},{3,2},{5,4},{7,6},{9,8},{11,10},{13,12},{15,14},{17,16},{19,... | collective-permute-start | bytes 20 | tf_op jit(solution)/shard_map/ppermute | solution.py:18

commit v10 on v9

--- a/solution.py
+++ b/solution.py
@@ -233,16 +233,22 @@
     energy, member_coeff, obs_coeff = score_terms(member_gram, obs_rows, obs_total, size)
     energy_arr = jnp.reshape(energy, (1,))
 
-    cot = obs_coeff[:, None, None] * obs_f[None]
-    for k in range(members):
-        cot = cot + member_coeff[:, k, None, None] * y[k].astype(jnp.float32)[None]
-    cot = cot.reshape(members * tok_rows, width)
-
-    da = section_backward(cot, gain, weight, fb[1], fb[2], slope_b)
+    def second_backward():
+        cot = obs_coeff[:, None, None] * obs_f[None]
+        for k in range(members):
+            cot = cot + member_coeff[:, k, None, None] * y[k].astype(jnp.float32)[None]
+        cot = cot.reshape(members * tok_rows, width)
+        return section_backward(cot, gain, weight, fb[1], fb[2], slope_b)
+
+    da = lax.cond(on_first, lambda: jnp.zeros((members * tok_rows, width), jnp.bfloat16), second_backward)
     back, energy_peer = shifted((da, energy_arr), "section", -1)
     energy_out = jnp.where(on_first, energy_peer, energy_arr)
-    db = section_backward(back.astype(jnp.float32), gain, weight, fa[1], fa[2], slope_a)
-    grads = jnp.where(on_first, db, da).reshape(members, tok_rows, width)
+    grads = lax.cond(
+        on_first,
+        lambda: section_backward(back.astype(jnp.float32), gain, weight, fa[1], fa[2], slope_a),
+        lambda: da,
+    )
+    grads = grads.reshape(members, tok_rows, width)
     return (grads[None], energy_out)
 
 

time: 145 us -> 141 us (0.972)
  other arithmetic: 18.6 us -> 11.8 us
  waiting for transfers between devices: 49.7 us -> 54.8 us
  matrix products: 25.5 us -> 21.9 us
  local copies, waits for them, and re-layouts: 5.81 us -> 9.36 us
  starting transfers between devices: 39.7 us -> 38.1 us
    dot_general x2 -> x1, matrix products: 12.8 us -> 6.58 us  [section_backward(): lax.dot_general(grad_pre, weight, (((1,), (1,)), ((), ())), preferred_ele...]
    ppermute x3, waiting for transfers between devices: 3.37 us -> 9.31 us  [shifted(): return lax.ppermute(x, axis, pairs)]
    convert_element_type x3 -> x0, other arithmetic: 4.31 us -> none  [the longest x1 2.49 us: section_backward(): grad_pre = (grad_out * slope).astype(jnp.bfloat16)]
    ppermute x28, waiting for transfers between devices: 41 us -> 38.2 us  [ring_gather(): parts[j] = lax.ppermute(parts[j], axis, cw if clockwise else ccw)]
    select_n x1 -> x0, other arithmetic: 2.02 us -> none  [per_device(): grads = jnp.where(on_first, db, da).reshape(members, tok_rows, width)]
    ppermute x3, waiting for transfers between devices: 5.35 us -> 7.31 us  [tree_sum(): v = v + lax.ppermute(v, axis, [(i, i ^ b) for i in range(n)])]
    dynamic_update_slice x28, local copies, waits for them, and re-layouts: 0.74 us -> 2.69 us  [ring_gather(): full = lax.dynamic_update_slice(full, parts[j], (origin * rows, j * width))]
    dot_general x28, matrix products: 6.36 us -> 8.28 us  [on_piece(): term = jnp.dot(lhs, piece, preferred_element_type=jnp.float32)]
  transfers between devices with their start and end apart: 34 -> 34, of which waited for: 30 -> 27; matrix products, arithmetic and copies ran while one was open for 9% -> 11% of each run, Pallas kernels for 0% -> 0%
where the time goes in v10:
time: 141 us; the launch traced here: 140 us
  waiting for transfers between devices  54.8 us (39%)
  starting transfers between devices  38.1 us (27%)
  matrix products  21.9 us (16%)
  other arithmetic  11.8 us (8%)
  local copies, waits for them, and re-layouts  9.36 us (7%)
  between operations  4.35 us (3%)
    ppermute x28, waiting for transfers between devices, ring_gather(): parts[j] = lax.ppermute(parts[j], axis, cw if clockwise else ccw)  38.2 us
    ppermute x28, starting transfers between devices, ring_gather(): parts[j] = lax.ppermute(parts[j], axis, cw if clockwise else ccw)  29.7 us
    ppermute x3, waiting for transfers between devices, shifted(): return lax.ppermute(x, axis, pairs)  9.31 us
    dot_general x28, matrix products, on_piece(): term = jnp.dot(lhs, piece, preferred_element_type=jnp.float32)  8.28 us
    ppermute x3, waiting for transfers between devices, tree_sum(): v = v + lax.ppermute(v, axis, [(i, i ^ b) for i in range(n)])  7.31 us
    dot_general x1, matrix products, section_backward(): lax.dot_general(grad_pre, weight, (((1,), (1,)), ((), ())), preferred_ele...  6.58 us
    dot_general x1, matrix products, section_forward(): pre_act = jnp.dot(normed, weight, preferred_element_type=jnp.float32)  6.1 us
    ppermute x3, starting transfers between devices, tree_sum(): v = v + lax.ppermute(v, axis, [(i, i ^ b) for i in range(n)])  4.3 us
  transfers between devices with their start and end apart: 34, of which 27 were waited for; matrix products, arithmetic and copies ran while one was open for 11% of the time, Pallas kernels for 0%

profile of v10, /device:TPU:0, one launch (start us, length us, event | category | flops | bytes accessed | tf_op | source)
XLA Modules:
  0.0 140.3 jit_solution(9004691853974327092)
XLA Ops:
  0.7 2.2 %fusion.121 = (bf16[256,512]{1,0:T(8,128)(2,1)}, bf16[256,512]{1,0:T(8,128)(2,1)}, bf16[256,512]{1,0:T(8,128)(2,1)}, bf16[256,512]{1,0:T(8,128)(2,1)S(1)}) fusion(bf16[256,2048]{1,0:T(8,128)(2,1)} %bitcast.130), kind=kLoop, calls=%fused_computation.228 | loop fusion | bytes 2097152 | tf_op jit(solution)/shard_map/slice | solution.py:106
  2.8 3.1 %collective-permute-start = (bf16[256,512]{1,0:T(8,128)(2,1)S(1)}, bf16[256,512]{1,0:T(8,128)(2,1)S(1)}, u32[]{:S(2)}, u32[]{:S(2)}) collective-permute-start(bf16[256,512]{1,0:T(8,128)(2,1)S(1)} %get-tuple-element.199), channel_id=1, source_target_pairs={{0,4},{4,8},{8,12},{12,14},{14,10},{10,6},{6,2},{2,0},{1,5},{5,9},... | collective-permute-start | bytes 786440 | tf_op jit(solution)/shard_map/ppermute | solution.py:113
  5.9 2.0 %collective-permute-start.14 = (bf16[256,512]{1,0:T(8,128)(2,1)}, bf16[256,512]{1,0:T(8,128)(2,1)}, u32[]{:S(2)}, u32[]{:S(2)}) collective-permute-start(bf16[256,512]{1,0:T(8,128)(2,1)} %get-tuple-element.197), channel_id=1, source_target_pairs={{0,4},{4,8},{8,12},{12,14},{14,10},{10,6},{6,2},{2,0},{1,5},{5,9},... | collective-permute-start | bytes 786440 | tf_op jit(solution)/shard_map/ppermute | solution.py:113
  10.1 2.9 %collective-permute-done = bf16[256,512]{1,0:T(8,128)(2,1)S(1)} collective-permute-done((bf16[256,512]{1,0:T(8,128)(2,1)S(1)}, bf16[256,512]{1,0:T(8,128)(2,1)S(1)}, u32[]{:S(2)}, u32[]{:S(2)}) %collective-permute-start) | collective-permute-done | bytes 262176 | tf_op jit(solution)/shard_map/ppermute | solution.py:113
  15.9 2.2 %collective-permute-start.1 = (bf16[256,512]{1,0:T(8,128)(2,1)S(1)}, bf16[256,512]{1,0:T(8,128)(2,1)S(1)}, u32[]{:S(2)}, u32[]{:S(2)}) collective-permute-start(bf16[256,512]{1,0:T(8,128)(2,1)S(1)} %copy-done.9), channel_id=1, source_target_pairs={{0,4},{4,8},{8,12},{12,14},{14,10},{10,6},{6,2},{2,0},{1,5},{5,9},... | collective-permute-start | bytes 786440 | tf_op jit(solution)/shard_map/ppermute | solution.py:113
  21.6 2.1 %collective-permute-start.15 = (bf16[256,512]{1,0:T(8,128)(2,1)}, bf16[256,512]{1,0:T(8,128)(2,1)S(1)}, u32[]{:S(2)}, u32[]{:S(2)}) collective-permute-start(bf16[256,512]{1,0:T(8,128)(2,1)} %collective-permute-done.14), channel_id=1, source_target_pairs={{0,4},{4,8},{8,12},{12,14},{14,10},{10,6},{6,2},{2,0},{1,5},{5,9},... | collective-permute-start | bytes 786440 | tf_op jit(solution)/shard_map/ppermute | solution.py:113
  26.2 2.1 %collective-permute-start.2 = (bf16[256,512]{1,0:T(8,128)(2,1)S(1)}, bf16[256,512]{1,0:T(8,128)(2,1)S(1)}, u32[]{:S(2)}, u32[]{:S(2)}) collective-permute-start(bf16[256,512]{1,0:T(8,128)(2,1)S(1)} %collective-permute-done.1), channel_id=1, source_target_pairs={{0,4},{4,8},{8,12},{12,14},{14,10},{10,6},{6,2},{2,0},{1,5},{5,9},... | collective-permute-start | bytes 786440 | tf_op jit(solution)/shard_map/ppermute | solution.py:113
  28.3 2.7 %collective-permute-done.15 = bf16[256,512]{1,0:T(8,128)(2,1)S(1)} collective-permute-done((bf16[256,512]{1,0:T(8,128)(2,1)}, bf16[256,512]{1,0:T(8,128)(2,1)S(1)}, u32[]{:S(2)}, u32[]{:S(2)}) %collective-permute-start.15) | collective-permute-done | bytes 262176 | tf_op jit(solution)/shard_map/ppermute | solution.py:113
  31.1 2.0 %collective-permute-start.16 = (bf16[256,512]{1,0:T(8,128)(2,1)S(1)}, bf16[256,512]{1,0:T(8,128)(2,1)S(1)}, u32[]{:S(2)}, u32[]{:S(2)}) collective-permute-start(bf16[256,512]{1,0:T(8,128)(2,1)S(1)} %collective-permute-done.15), channel_id=1, source_target_pairs={{0,4},{4,8},{8,12},{12,14},{14,10},{10,6},{6,2},{2,0},{1,5},{5,9},... | collective-permute-start | bytes 786440 | tf_op jit(solution)/shard_map/ppermute | solution.py:113
  33.2 1.9 %collective-permute-done.22 = bf16[256,512]{1,0:T(8,128)(2,1)S(1)} collective-permute-done((bf16[256,512]{1,0:T(8,128)(2,1)S(1)}, bf16[256,512]{1,0:T(8,128)(2,1)S(1)}, u32[]{:S(2)}, u32[]{:S(2)}) %collective-permute-start.22) | collective-permute-done | bytes 262176 | tf_op jit(solution)/shard_map/ppermute | solution.py:113
  36.7 2.0 %collective-permute-start.3 = (bf16[256,512]{1,0:T(8,128)(2,1)S(1)}, bf16[256,512]{1,0:T(8,128)(2,1)S(1)}, u32[]{:S(2)}, u32[]{:S(2)}) collective-permute-start(bf16[256,512]{1,0:T(8,128)(2,1)S(1)} %collective-permute-done.2), channel_id=1, source_target_pairs={{0,4},{4,8},{8,12},{12,14},{14,10},{10,6},{6,2},{2,0},{1,5},{5,9},... | collective-permute-start | bytes 786440 | tf_op jit(solution)/shard_map/ppermute | solution.py:113
  38.7 2.1 %collective-permute-done.9 = bf16[256,512]{1,0:T(8,128)(2,1)S(1)} collective-permute-done((bf16[256,512]{1,0:T(8,128)(2,1)S(1)}, bf16[256,512]{1,0:T(8,128)(2,1)S(1)}, u32[]{:S(2)}, u32[]{:S(2)}) %collective-permute-start.9) | collective-permute-done | bytes 262176 | tf_op jit(solution)/shard_map/ppermute | solution.py:113
  40.8 1.5 %collective-permute-done.16 = bf16[256,512]{1,0:T(8,128)(2,1)S(1)} collective-permute-done((bf16[256,512]{1,0:T(8,128)(2,1)S(1)}, bf16[256,512]{1,0:T(8,128)(2,1)S(1)}, u32[]{:S(2)}, u32[]{:S(2)}) %collective-permute-start.16) | collective-permute-done | bytes 262176 | tf_op jit(solution)/shard_map/ppermute | solution.py:113
  42.3 2.0 %collective-permute-start.17 = (bf16[256,512]{1,0:T(8,128)(2,1)S(1)}, bf16[256,512]{1,0:T(8,128)(2,1)S(1)}, u32[]{:S(2)}, u32[]{:S(2)}) collective-permute-start(bf16[256,512]{1,0:T(8,128)(2,1)S(1)} %collective-permute-done.16), channel_id=1, source_target_pairs={{0,4},{4,8},{8,12},{12,14},{14,10},{10,6},{6,2},{2,0},{1,5},{5,9},... | collective-permute-start | bytes 786440 | tf_op jit(solution)/shard_map/ppermute | solution.py:113
  44.4 1.9 %collective-permute-done.23 = bf16[256,512]{1,0:T(8,128)(2,1)S(1)} collective-permute-done((bf16[256,512]{1,0:T(8,128)(2,1)S(1)}, bf16[256,512]{1,0:T(8,128)(2,1)S(1)}, u32[]{:S(2)}, u32[]{:S(2)}) %collective-permute-start.23) | collective-permute-done | bytes 262176 | tf_op jit(solution)/shard_map/ppermute | solution.py:113
  47.9 2.0 %collective-permute-start.4 = (bf16[256,512]{1,0:T(8,128)(2,1)S(1)}, bf16[256,512]{1,0:T(8,128)(2,1)S(1)}, u32[]{:S(2)}, u32[]{:S(2)}) collective-permute-start(bf16[256,512]{1,0:T(8,128)(2,1)S(1)} %collective-permute-done.3), channel_id=1, source_target_pairs={{0,4},{4,8},{8,12},{12,14},{14,10},{10,6},{6,2},{2,0},{1,5},{5,9},... | collective-permute-start | bytes 786440 | tf_op jit(solution)/shard_map/ppermute | solution.py:113
  49.9 2.1 %collective-permute-done.10 = bf16[256,512]{1,0:T(8,128)(2,1)S(1)} collective-permute-done((bf16[256,512]{1,0:T(8,128)(2,1)S(1)}, bf16[256,512]{1,0:T(8,128)(2,1)S(1)}, u32[]{:S(2)}, u32[]{:S(2)}) %collective-permute-start.10) | collective-permute-done | bytes 262176 | tf_op jit(solution)/shard_map/ppermute | solution.py:113
  52.0 1.5 %collective-permute-done.17 = bf16[256,512]{1,0:T(8,128)(2,1)S(1)} collective-permute-done((bf16[256,512]{1,0:T(8,128)(2,1)S(1)}, bf16[256,512]{1,0:T(8,128)(2,1)S(1)}, u32[]{:S(2)}, u32[]{:S(2)}) %collective-permute-start.17) | collective-permute-done | bytes 262176 | tf_op jit(solution)/shard_map/ppermute | solution.py:113
  53.5 2.0 %collective-permute-start.18 = (bf16[256,512]{1,0:T(8,128)(2,1)S(1)}, bf16[256,512]{1,0:T(8,128)(2,1)S(1)}, u32[]{:S(2)}, u32[]{:S(2)}) collective-permute-start(bf16[256,512]{1,0:T(8,128)(2,1)S(1)} %collective-permute-done.17), channel_id=1, source_target_pairs={{0,4},{4,8},{8,12},{12,14},{14,10},{10,6},{6,2},{2,0},{1,5},{5,9},... | collective-permute-start | bytes 786440 | tf_op jit(solution)/shard_map/ppermute | solution.py:113
  55.6 2.1 %collective-permute-done.24 = bf16[256,512]{1,0:T(8,128)(2,1)S(1)} collective-permute-done((bf16[256,512]{1,0:T(8,128)(2,1)S(1)}, bf16[256,512]{1,0:T(8,128)(2,1)S(1)}, u32[]{:S(2)}, u32[]{:S(2)}) %collective-permute-start.24) | collective-permute-done | bytes 262176 | tf_op jit(solution)/shard_map/ppermute | solution.py:113
  59.1 2.0 %collective-permute-start.5 = (bf16[256,512]{1,0:T(8,128)(2,1)S(1)}, bf16[256,512]{1,0:T(8,128)(2,1)S(1)}, u32[]{:S(2)}, u32[]{:S(2)}) collective-permute-start(bf16[256,512]{1,0:T(8,128)(2,1)S(1)} %collective-permute-done.4), channel_id=1, source_target_pairs={{0,4},{4,8},{8,12},{12,14},{14,10},{10,6},{6,2},{2,0},{1,5},{5,9},... | collective-permute-start | bytes 786440 | tf_op jit(solution)/shard_map/ppermute | solution.py:113
  61.2 2.1 %collective-permute-done.11 = bf16[256,512]{1,0:T(8,128)(2,1)S(1)} collective-permute-done((bf16[256,512]{1,0:T(8,128)(2,1)S(1)}, bf16[256,512]{1,0:T(8,128)(2,1)S(1)}, u32[]{:S(2)}, u32[]{:S(2)}) %collective-permute-start.11) | collective-permute-done | bytes 262176 | tf_op jit(solution)/shard_map/ppermute | solution.py:113
  63.2 1.5 %collective-permute-done.18 = bf16[256,512]{1,0:T(8,128)(2,1)S(1)} collective-permute-done((bf16[256,512]{1,0:T(8,128)(2,1)S(1)}, bf16[256,512]{1,0:T(8,128)(2,1)S(1)}, u32[]{:S(2)}, u32[]{:S(2)}) %collective-permute-start.18) | collective-permute-done | bytes 262176 | tf_op jit(solution)/shard_map/ppermute | solution.py:113
  64.8 2.0 %collective-permute-start.19 = (bf16[256,512]{1,0:T(8,128)(2,1)S(1)}, bf16[256,512]{1,0:T(8,128)(2,1)S(1)}, u32[]{:S(2)}, u32[]{:S(2)}) collective-permute-start(bf16[256,512]{1,0:T(8,128)(2,1)S(1)} %collective-permute-done.18), channel_id=1, source_target_pairs={{0,4},{4,8},{8,12},{12,14},{14,10},{10,6},{6,2},{2,0},{1,5},{5,9},... | collective-permute-start | bytes 786440 | tf_op jit(solution)/shard_map/ppermute | solution.py:113
  66.8 2.0 %collective-permute-done.25 = bf16[256,512]{1,0:T(8,128)(2,1)S(1)} collective-permute-done((bf16[256,512]{1,0:T(8,128)(2,1)S(1)}, bf16[256,512]{1,0:T(8,128)(2,1)S(1)}, u32[]{:S(2)}, u32[]{:S(2)}) %collective-permute-start.25) | collective-permute-done | bytes 262176 | tf_op jit(solution)/shard_map/ppermute | solution.py:113
  70.4 2.0 %collective-permute-start.6 = (bf16[256,512]{1,0:T(8,128)(2,1)S(1)}, bf16[256,512]{1,0:T(8,128)(2,1)S(1)}, u32[]{:S(2)}, u32[]{:S(2)}) collective-permute-start(bf16[256,512]{1,0:T(8,128)(2,1)S(1)} %collective-permute-done.5), channel_id=1, source_target_pairs={{0,4},{4,8},{8,12},{12,14},{14,10},{10,6},{6,2},{2,0},{1,5},{5,9},... | collective-permute-start | bytes 786440 | tf_op jit(solution)/shard_map/ppermute | solution.py:113
  72.4 2.1 %collective-permute-done.12 = bf16[256,512]{1,0:T(8,128)(2,1)S(1)} collective-permute-done((bf16[256,512]{1,0:T(8,128)(2,1)S(1)}, bf16[256,512]{1,0:T(8,128)(2,1)S(1)}, u32[]{:S(2)}, u32[]{:S(2)}) %collective-permute-start.12) | collective-permute-done | bytes 262176 | tf_op jit(solution)/shard_map/ppermute | solution.py:113
  74.5 1.5 %collective-permute-done.19 = bf16[256,512]{1,0:T(8,128)(2,1)S(1)} collective-permute-done((bf16[256,512]{1,0:T(8,128)(2,1)S(1)}, bf16[256,512]{1,0:T(8,128)(2,1)S(1)}, u32[]{:S(2)}, u32[]{:S(2)}) %collective-permute-start.19) | collective-permute-done | bytes 262176 | tf_op jit(solution)/shard_map/ppermute | solution.py:113
  76.0 2.0 %collective-permute-start.20 = (bf16[256,512]{1,0:T(8,128)(2,1)S(1)}, bf16[256,512]{1,0:T(8,128)(2,1)S(1)}, u32[]{:S(2)}, u32[]{:S(2)}) collective-permute-start(bf16[256,512]{1,0:T(8,128)(2,1)S(1)} %collective-permute-done.19), channel_id=1, source_target_pairs={{0,4},{4,8},{8,12},{12,14},{14,10},{10,6},{6,2},{2,0},{1,5},{5,9},... | collective-permute-start | bytes 786440 | tf_op jit(solution)/shard_map/ppermute | solution.py:113
  78.1 2.0 %collective-permute-done.26 = bf16[256,512]{1,0:T(8,128)(2,1)S(1)} collective-permute-done((bf16[256,512]{1,0:T(8,128)(2,1)S(1)}, bf16[256,512]{1,0:T(8,128)(2,1)S(1)}, u32[]{:S(2)}, u32[]{:S(2)}) %collective-permute-start.26) | collective-permute-done | bytes 262176 | tf_op jit(solution)/shard_map/ppermute | solution.py:113
  81.9 3.1 %collective-permute-done.13 = bf16[256,512]{1,0:T(8,128)(2,1)S(1)} collective-permute-done((bf16[256,512]{1,0:T(8,128)(2,1)S(1)}, bf16[256,512]{1,0:T(8,128)(2,1)S(1)}, u32[]{:S(2)}, u32[]{:S(2)}) %collective-permute-start.13) | collective-permute-done | bytes 262176 | tf_op jit(solution)/shard_map/ppermute | solution.py:113
  85.5 2.3 %collective-permute-done.27 = bf16[256,512]{1,0:T(8,128)(2,1)S(1)} collective-permute-done((bf16[256,512]{1,0:T(8,128)(2,1)S(1)}, bf16[256,512]{1,0:T(8,128)(2,1)S(1)}, u32[]{:S(2)}, u32[]{:S(2)}) %collective-permute-start.27) | collective-permute-done | bytes 262176 | tf_op jit(solution)/shard_map/ppermute | solution.py:113
  88.0 2.5 %fusion.23 = (f32[256,2048]{1,0:T(8,128)}, bf16[256,2048]{1,0:T(8,128)(2,1)S(1)}) fusion(f32[256,512]{1,0:T(8,128)S(1)} %fusion.27, f32[256,512]{1,0:T(8,128)S(1)} %fusion.28, f32[256,512]{1,0:T(8,128)S(1)} %fusion.29, f32[256,512]{1,0:T(8,128)S(1)} %fusion.30, bf16[256,2048]{1,0:T(8,128)(2,1)S(1)} %bitcast.129), kind=kLoop, calls=%fused_computation.57 | loop fusion | flops 12582912 | bytes 6291456 | tf_op jit(solution)/shard_map/add | solution.py:28
  90.5 1.5 %collective-permute-start.28 = (bf16[256,2048]{1,0:T(8,128)(2,1)S(1)}, bf16[256,2048]{1,0:T(8,128)(2,1)S(1)}, u32[]{:S(2)}, u32[]{:S(2)}) collective-permute-start(bf16[256,2048]{1,0:T(8,128)(2,1)S(1)} %get-tuple-element.192), channel_id=1, source_target_pairs={{0,1},{2,3},{4,5},{6,7},{8,9},{10,11},{12,13},{14,15},{16,17},{18,... | collective-permute-start | bytes 3145736 | tf_op jit(solution)/shard_map/ppermute | solution.py:18
  92.4 1.6 %collective-permute-done.28 = bf16[256,2048]{1,0:T(8,128)(2,1)S(1)} collective-permute-done((bf16[256,2048]{1,0:T(8,128)(2,1)S(1)}, bf16[256,2048]{1,0:T(8,128)(2,1)S(1)}, u32[]{:S(2)}, u32[]{:S(2)}) %collective-permute-start.28) | collective-permute-done | bytes 1048608 | tf_op jit(solution)/shard_map/ppermute | solution.py:18
  94.7 6.1 %bitcast_convert_fusion.2 = (f32[2,128,2048]{2,1,0:T(8,128)S(1)}, bf16[256,2048]{1,0:T(8,128)(2,1)}, f32[256,2048]{1,0:T(8,128)}, f32[256,2048]{1,0:T(8,128)}) fusion(bf16[256,2048]{1,0:T(8,128)(2,1)S(1)} %collective-permute-done.28, f32[256]{0:T(256)S(1)} %add_rsqrt_fusion.1, f32[256]{0:T(256)S(1)} %broadcast_multiply_fusion.4, ...), kind=kOutput, calls=%fused_computation.218 | convolution fusion | flops 2162688000 | bytes 16787456 | tf_op jit(solution)/shard_map/dot_general | solution.py:50
  102.4 3.4 %collective-permute-done.29 = f32[7]{0:T(128)S(1)} collective-permute-done((f32[7]{0:T(128)S(1)}, f32[7]{0:T(128)S(1)}, u32[]{:S(2)}, u32[]{:S(2)}) %collective-permute-start.29) | collective-permute-done | bytes 60 | tf_op jit(solution)/shard_map/ppermute | solution.py:128
  106.5 1.6 %collective-permute-start.30 = (f32[7]{0:T(128)S(1)}, f32[7]{0:T(128)S(1)}, u32[]{:S(2)}, u32[]{:S(2)}) collective-permute-start(f32[7]{0:T(128)S(1)} %fusion.154), channel_id=1, source_target_pairs={{0,4},{2,6},{4,0},{6,2},{8,12},{10,14},{12,8},{14,10},{1,5},{3,7},... | collective-permute-start | bytes 92 | tf_op jit(solution)/shard_map/ppermute | solution.py:128
  108.1 2.0 %collective-permute-done.30 = f32[7]{0:T(128)S(1)} collective-permute-done((f32[7]{0:T(128)S(1)}, f32[7]{0:T(128)S(1)}, u32[]{:S(2)}, u32[]{:S(2)}) %collective-permute-start.30) | collective-permute-done | bytes 60 | tf_op jit(solution)/shard_map/ppermute | solution.py:128
  110.1 2.6 %collective-permute-start.31 = (f32[7]{0:T(128)S(1)}, f32[7]{0:T(128)S(1)}, u32[]{:S(2)}, u32[]{:S(2)}) collective-permute-start(f32[7]{0:T(128)S(1)} %add.463), channel_id=1, source_target_pairs={{0,8},{2,10},{4,12},{6,14},{8,0},{10,2},{12,4},{14,6},{1,9},{3,11}... | collective-permute-start | bytes 92 | tf_op jit(solution)/shard_map/ppermute | solution.py:128
  112.7 1.9 %collective-permute-done.31 = f32[7]{0:T(128)S(1)} collective-permute-done((f32[7]{0:T(128)S(1)}, f32[7]{0:T(128)S(1)}, u32[]{:S(2)}, u32[]{:S(2)}) %collective-permute-start.31) | collective-permute-done | bytes 60 | tf_op jit(solution)/shard_map/ppermute | solution.py:128
  116.6 1.3 fusion.119
  119.0 1.3 collective-permute-start.32
  121.4 1.3 collective-permute-start.33
  122.7 7.7 %collective-permute-done.33 = f32[1]{0:T(128)} collective-permute-done((f32[1]{0:T(128)}, f32[1]{0:T(128)}, u32[]{:S(2)}, u32[]{:S(2)}) %collective-permute-start.33) | collective-permute-done | bytes 36 | tf_op jit(solution)/shard_map/ppermute | solution.py:18
  131.0 8.2 %conditional.3 = (bf16[1,2,128,2048]{3,2,1,0:T(8,128)(2,1)}) conditional(s32[]{:T(128)} %convert_element_type.58, bf16[256,2048]{1,0:T(8,128)(2,1)} %get-tuple-element.202, (bf16[256,2048]{1,0:T(8,128)(2,1)S(1)}, f32[256]{0:T(256)S(1)}, f32[]{:T(128)}, f32[]{:T(128)}, f32[256,2048]{1,0:T(8,128)}, /*index=5*/bf16[2048,2048]{1,0:T(8,128)(2,1)}, ...), branch_computations={%region_15.16_spmd, %region_16.19_spmd} | conditional | flops 2154824192 | bytes 22039568 | solution.py:246
  131.0 6.6 %fusion.114 = (f32[256]{0:T(256)S(1)}, f32[256]{0:T(256)S(1)}, f32[256,2048]{1,0:T(8,128)S(1)}) fusion(f32[256,2048]{1,0:T(8,128)S(1)} %get-tuple-element.67, f32[2048]{0:T(1024)S(1)} %bitcast.142, bf16[2048,2048]{1,0:T(8,128)(2,1)} %get-tuple-element.65, f32[256,2048]{1,0:T(8,128)} %get-tuple-element.64, bf16[256,2048]{1,0:T(8,128)(2,1)S(1)} %get-tuple-element.60), kind=kOutput, calls=%fused_computation.223 | convolution fusion | flops 2151153152 | bytes 15738880 | tf_op jit(solution)/shard_map/cond/branch_1_fun/dot_general | solution.py:57
  137.7 1.6 %fusion.1 = bf16[256,2048]{1,0:T(8,128)(2,1)} fusion(bf16[256,2048]{1,0:T(8,128)(2,1)S(1)} %get-tuple-element.60, f32[256,2048]{1,0:T(8,128)S(1)} %get-tuple-element.67, f32[256,2048]{1,0:T(8,128)S(1)} %get-tuple-element.180, f32[256]{0:T(256)S(1)} %add_rsqrt_fusion, f32[256]{0:T(256)S(1)} %get-tuple-element.181, f32[256]{0:T(256)S(1)} %get-tuple-element.182), kind=kLoop, calls=%fused_computation.5 | loop fusion | flops 3670016 | bytes 6294528 | tf_op jit(solution)/shard_map/cond/branch_1_fun/convert_element_type | solution.py:66
  (137 shorter events, 26.9 us)
Async XLA Ops:
  0.6 7.5 %copy-start.5 = (bf16[128,2048]{1,0:T(8,128)(2,1)S(1)}, bf16[128,2048]{1,0:T(8,128)(2,1)}, u32[]{:S(2)}) copy-start(bf16[128,2048]{1,0:T(8,128)(2,1)} %param.9) | copy-start | bytes 1572868
  0.6 12.3 %copy-start.2 = (bf16[2,128,2048]{2,1,0:T(8,128)(2,1)S(1)}, bf16[2,128,2048]{2,1,0:T(8,128)(2,1)}, u32[]{:S(2)}) copy-start(bf16[2,128,2048]{2,1,0:T(8,128)(2,1)} %param.8) | copy-start | bytes 3145732
  2.8 10.1 %collective-permute-start = (bf16[256,512]{1,0:T(8,128)(2,1)S(1)}, bf16[256,512]{1,0:T(8,128)(2,1)S(1)}, u32[]{:S(2)}, u32[]{:S(2)}) collective-permute-start(bf16[256,512]{1,0:T(8,128)(2,1)S(1)} %get-tuple-element.199), channel_id=1, source_target_pairs={{0,4},{4,8},{8,12},{12,14},{14,10},{10,6},{6,2},{2,0},{1,5},{5,9},... | collective-permute-start | bytes 786440 | tf_op jit(solution)/shard_map/ppermute | solution.py:113
  5.9 13.4 %collective-permute-start.7 = (bf16[256,512]{1,0:T(8,128)(2,1)}, bf16[256,512]{1,0:T(8,128)(2,1)}, u32[]{:S(2)}, u32[]{:S(2)}) collective-permute-start(bf16[256,512]{1,0:T(8,128)(2,1)} %get-tuple-element.198), channel_id=1, source_target_pairs={{4,0},{8,4},{12,8},{14,12},{10,14},{6,10},{2,6},{0,2},{5,1},{9,5},... | collective-permute-start | bytes 786440 | tf_op jit(solution)/shard_map/ppermute | solution.py:113
  5.9 15.7 %collective-permute-start.14 = (bf16[256,512]{1,0:T(8,128)(2,1)}, bf16[256,512]{1,0:T(8,128)(2,1)}, u32[]{:S(2)}, u32[]{:S(2)}) collective-permute-start(bf16[256,512]{1,0:T(8,128)(2,1)} %get-tuple-element.197), channel_id=1, source_target_pairs={{0,4},{4,8},{8,12},{12,14},{14,10},{10,6},{6,2},{2,0},{1,5},{5,9},... | collective-permute-start | bytes 786440 | tf_op jit(solution)/shard_map/ppermute | solution.py:113
  7.9 18.0 %collective-permute-start.21 = (bf16[256,512]{1,0:T(8,128)(2,1)}, bf16[256,512]{1,0:T(8,128)(2,1)S(1)}, u32[]{:S(2)}, u32[]{:S(2)}) collective-permute-start(bf16[256,512]{1,0:T(8,128)(2,1)} %get-tuple-element.196), channel_id=1, source_target_pairs={{4,0},{8,4},{12,8},{14,12},{10,14},{6,10},{2,6},{0,2},{5,1},{9,5},... | collective-permute-start | bytes 786440 | tf_op jit(solution)/shard_map/ppermute | solution.py:113
  8.1 5.6 %copy-start.10 = (f32[1,2048]{1,0:T(1,128)S(1)}, f32[1,2048]{1,0:T(1,128)}, u32[]{:S(2)}) copy-start(f32[1,2048]{1,0:T(1,128)} %param.11) | copy-start | bytes 24580
  13.0 0.7 copy-start.8
  13.7 1.2 copy-start.4
  14.1 1.7 %copy-start.9 = (bf16[256,512]{1,0:T(8,128)(2,1)S(1)}, bf16[256,512]{1,0:T(8,128)(2,1)}, u32[]{:S(2)}) copy-start(bf16[256,512]{1,0:T(8,128)(2,1)} %copy-done.8) | copy-start | bytes 786436
  15.9 10.4 %collective-permute-start.1 = (bf16[256,512]{1,0:T(8,128)(2,1)S(1)}, bf16[256,512]{1,0:T(8,128)(2,1)S(1)}, u32[]{:S(2)}, u32[]{:S(2)}) collective-permute-start(bf16[256,512]{1,0:T(8,128)(2,1)S(1)} %copy-done.9), channel_id=1, source_target_pairs={{0,4},{4,8},{8,12},{12,14},{14,10},{10,6},{6,2},{2,0},{1,5},{5,9},... | collective-permute-start | bytes 786440 | tf_op jit(solution)/shard_map/ppermute | solution.py:113
  19.4 9.0 %collective-permute-start.8 = (bf16[256,512]{1,0:T(8,128)(2,1)}, bf16[256,512]{1,0:T(8,128)(2,1)S(1)}, u32[]{:S(2)}, u32[]{:S(2)}) collective-permute-start(bf16[256,512]{1,0:T(8,128)(2,1)} %collective-permute-done.7), channel_id=1, source_target_pairs={{4,0},{8,4},{12,8},{14,12},{10,14},{6,10},{2,6},{0,2},{5,1},{9,5},... | collective-permute-start | bytes 786440 | tf_op jit(solution)/shard_map/ppermute | solution.py:113
  21.6 9.4 %collective-permute-start.15 = (bf16[256,512]{1,0:T(8,128)(2,1)}, bf16[256,512]{1,0:T(8,128)(2,1)S(1)}, u32[]{:S(2)}, u32[]{:S(2)}) collective-permute-start(bf16[256,512]{1,0:T(8,128)(2,1)} %collective-permute-done.14), channel_id=1, source_target_pairs={{0,4},{4,8},{8,12},{12,14},{14,10},{10,6},{6,2},{2,0},{1,5},{5,9},... | collective-permute-start | bytes 786440 | tf_op jit(solution)/shard_map/ppermute | solution.py:113
  25.9 9.2 %collective-permute-start.22 = (bf16[256,512]{1,0:T(8,128)(2,1)S(1)}, bf16[256,512]{1,0:T(8,128)(2,1)S(1)}, u32[]{:S(2)}, u32[]{:S(2)}) collective-permute-start(bf16[256,512]{1,0:T(8,128)(2,1)S(1)} %collective-permute-done.21), channel_id=1, source_target_pairs={{4,0},{8,4},{12,8},{14,12},{10,14},{6,10},{2,6},{0,2},{5,1},{9,5},... | collective-permute-start | bytes 786440 | tf_op jit(solution)/shard_map/ppermute | solution.py:113
  26.2 10.4 %collective-permute-start.2 = (bf16[256,512]{1,0:T(8,128)(2,1)S(1)}, bf16[256,512]{1,0:T(8,128)(2,1)S(1)}, u32[]{:S(2)}, u32[]{:S(2)}) collective-permute-start(bf16[256,512]{1,0:T(8,128)(2,1)S(1)} %collective-permute-done.1), channel_id=1, source_target_pairs={{0,4},{4,8},{8,12},{12,14},{14,10},{10,6},{6,2},{2,0},{1,5},{5,9},... | collective-permute-start | bytes 786440 | tf_op jit(solution)/shard_map/ppermute | solution.py:113
  28.3 12.4 %collective-permute-start.9 = (bf16[256,512]{1,0:T(8,128)(2,1)S(1)}, bf16[256,512]{1,0:T(8,128)(2,1)S(1)}, u32[]{:S(2)}, u32[]{:S(2)}) collective-permute-start(bf16[256,512]{1,0:T(8,128)(2,1)S(1)} %collective-permute-done.8), channel_id=1, source_target_pairs={{4,0},{8,4},{12,8},{14,12},{10,14},{6,10},{2,6},{0,2},{5,1},{9,5},... | collective-permute-start | bytes 786440 | tf_op jit(solution)/shard_map/ppermute | solution.py:113
  31.1 11.2 %collective-permute-start.16 = (bf16[256,512]{1,0:T(8,128)(2,1)S(1)}, bf16[256,512]{1,0:T(8,128)(2,1)S(1)}, u32[]{:S(2)}, u32[]{:S(2)}) collective-permute-start(bf16[256,512]{1,0:T(8,128)(2,1)S(1)} %collective-permute-done.15), channel_id=1, source_target_pairs={{0,4},{4,8},{8,12},{12,14},{14,10},{10,6},{6,2},{2,0},{1,5},{5,9},... | collective-permute-start | bytes 786440 | tf_op jit(solution)/shard_map/ppermute | solution.py:113
  35.1 11.2 %collective-permute-start.23 = (bf16[256,512]{1,0:T(8,128)(2,1)S(1)}, bf16[256,512]{1,0:T(8,128)(2,1)S(1)}, u32[]{:S(2)}, u32[]{:S(2)}) collective-permute-start(bf16[256,512]{1,0:T(8,128)(2,1)S(1)} %collective-permute-done.22), channel_id=1, source_target_pairs={{4,0},{8,4},{12,8},{14,12},{10,14},{6,10},{2,6},{0,2},{5,1},{9,5},... | collective-permute-start | bytes 786440 | tf_op jit(solution)/shard_map/ppermute | solution.py:113
  36.7 11.2 %collective-permute-start.3 = (bf16[256,512]{1,0:T(8,128)(2,1)S(1)}, bf16[256,512]{1,0:T(8,128)(2,1)S(1)}, u32[]{:S(2)}, u32[]{:S(2)}) collective-permute-start(bf16[256,512]{1,0:T(8,128)(2,1)S(1)} %collective-permute-done.2), channel_id=1, source_target_pairs={{0,4},{4,8},{8,12},{12,14},{14,10},{10,6},{6,2},{2,0},{1,5},{5,9},... | collective-permute-start | bytes 786440 | tf_op jit(solution)/shard_map/ppermute | solution.py:113
  40.8 11.2 %collective-permute-start.10 = (bf16[256,512]{1,0:T(8,128)(2,1)S(1)}, bf16[256,512]{1,0:T(8,128)(2,1)S(1)}, u32[]{:S(2)}, u32[]{:S(2)}) collective-permute-start(bf16[256,512]{1,0:T(8,128)(2,1)S(1)} %collective-permute-done.9), channel_id=1, source_target_pairs={{4,0},{8,4},{12,8},{14,12},{10,14},{6,10},{2,6},{0,2},{5,1},{9,5},... | collective-permute-start | bytes 786440 | tf_op jit(solution)/shard_map/ppermute | solution.py:113
  42.3 11.2 %collective-permute-start.17 = (bf16[256,512]{1,0:T(8,128)(2,1)S(1)}, bf16[256,512]{1,0:T(8,128)(2,1)S(1)}, u32[]{:S(2)}, u32[]{:S(2)}) collective-permute-start(bf16[256,512]{1,0:T(8,128)(2,1)S(1)} %collective-permute-done.16), channel_id=1, source_target_pairs={{0,4},{4,8},{8,12},{12,14},{14,10},{10,6},{6,2},{2,0},{1,5},{5,9},... | collective-permute-start | bytes 786440 | tf_op jit(solution)/shard_map/ppermute | solution.py:113
  46.4 11.2 %collective-permute-start.24 = (bf16[256,512]{1,0:T(8,128)(2,1)S(1)}, bf16[256,512]{1,0:T(8,128)(2,1)S(1)}, u32[]{:S(2)}, u32[]{:S(2)}) collective-permute-start(bf16[256,512]{1,0:T(8,128)(2,1)S(1)} %collective-permute-done.23), channel_id=1, source_target_pairs={{4,0},{8,4},{12,8},{14,12},{10,14},{6,10},{2,6},{0,2},{5,1},{9,5},... | collective-permute-start | bytes 786440 | tf_op jit(solution)/shard_map/ppermute | solution.py:113
  47.9 11.2 %collective-permute-start.4 = (bf16[256,512]{1,0:T(8,128)(2,1)S(1)}, bf16[256,512]{1,0:T(8,128)(2,1)S(1)}, u32[]{:S(2)}, u32[]{:S(2)}) collective-permute-start(bf16[256,512]{1,0:T(8,128)(2,1)S(1)} %collective-permute-done.3), channel_id=1, source_target_pairs={{0,4},{4,8},{8,12},{12,14},{14,10},{10,6},{6,2},{2,0},{1,5},{5,9},... | collective-permute-start | bytes 786440 | tf_op jit(solution)/shard_map/ppermute | solution.py:113
  52.0 11.2 %collective-permute-start.11 = (bf16[256,512]{1,0:T(8,128)(2,1)S(1)}, bf16[256,512]{1,0:T(8,128)(2,1)S(1)}, u32[]{:S(2)}, u32[]{:S(2)}) collective-permute-start(bf16[256,512]{1,0:T(8,128)(2,1)S(1)} %collective-permute-done.10), channel_id=1, source_target_pairs={{4,0},{8,4},{12,8},{14,12},{10,14},{6,10},{2,6},{0,2},{5,1},{9,5},... | collective-permute-start | bytes 786440 | tf_op jit(solution)/shard_map/ppermute | solution.py:113
  53.5 11.2 %collective-permute-start.18 = (bf16[256,512]{1,0:T(8,128)(2,1)S(1)}, bf16[256,512]{1,0:T(8,128)(2,1)S(1)}, u32[]{:S(2)}, u32[]{:S(2)}) collective-permute-start(bf16[256,512]{1,0:T(8,128)(2,1)S(1)} %collective-permute-done.17), channel_id=1, source_target_pairs={{0,4},{4,8},{8,12},{12,14},{14,10},{10,6},{6,2},{2,0},{1,5},{5,9},... | collective-permute-start | bytes 786440 | tf_op jit(solution)/shard_map/ppermute | solution.py:113
  57.6 11.2 %collective-permute-start.25 = (bf16[256,512]{1,0:T(8,128)(2,1)S(1)}, bf16[256,512]{1,0:T(8,128)(2,1)S(1)}, u32[]{:S(2)}, u32[]{:S(2)}) collective-permute-start(bf16[256,512]{1,0:T(8,128)(2,1)S(1)} %collective-permute-done.24), channel_id=1, source_target_pairs={{4,0},{8,4},{12,8},{14,12},{10,14},{6,10},{2,6},{0,2},{5,1},{9,5},... | collective-permute-start | bytes 786440 | tf_op jit(solution)/shard_map/ppermute | solution.py:113
  59.1 11.2 %collective-permute-start.5 = (bf16[256,512]{1,0:T(8,128)(2,1)S(1)}, bf16[256,512]{1,0:T(8,128)(2,1)S(1)}, u32[]{:S(2)}, u32[]{:S(2)}) collective-permute-start(bf16[256,512]{1,0:T(8,128)(2,1)S(1)} %collective-permute-done.4), channel_id=1, source_target_pairs={{0,4},{4,8},{8,12},{12,14},{14,10},{10,6},{6,2},{2,0},{1,5},{5,9},... | collective-permute-start | bytes 786440 | tf_op jit(solution)/shard_map/ppermute | solution.py:113
  63.2 11.2 %collective-permute-start.12 = (bf16[256,512]{1,0:T(8,128)(2,1)S(1)}, bf16[256,512]{1,0:T(8,128)(2,1)S(1)}, u32[]{:S(2)}, u32[]{:S(2)}) collective-permute-start(bf16[256,512]{1,0:T(8,128)(2,1)S(1)} %collective-permute-done.11), channel_id=1, source_target_pairs={{4,0},{8,4},{12,8},{14,12},{10,14},{6,10},{2,6},{0,2},{5,1},{9,5},... | collective-permute-start | bytes 786440 | tf_op jit(solution)/shard_map/ppermute | solution.py:113
  64.8 11.2 %collective-permute-start.19 = (bf16[256,512]{1,0:T(8,128)(2,1)S(1)}, bf16[256,512]{1,0:T(8,128)(2,1)S(1)}, u32[]{:S(2)}, u32[]{:S(2)}) collective-permute-start(bf16[256,512]{1,0:T(8,128)(2,1)S(1)} %collective-permute-done.18), channel_id=1, source_target_pairs={{0,4},{4,8},{8,12},{12,14},{14,10},{10,6},{6,2},{2,0},{1,5},{5,9},... | collective-permute-start | bytes 786440 | tf_op jit(solution)/shard_map/ppermute | solution.py:113
  68.8 11.2 %collective-permute-start.26 = (bf16[256,512]{1,0:T(8,128)(2,1)S(1)}, bf16[256,512]{1,0:T(8,128)(2,1)S(1)}, u32[]{:S(2)}, u32[]{:S(2)}) collective-permute-start(bf16[256,512]{1,0:T(8,128)(2,1)S(1)} %collective-permute-done.25), channel_id=1, source_target_pairs={{4,0},{8,4},{12,8},{14,12},{10,14},{6,10},{2,6},{0,2},{5,1},{9,5},... | collective-permute-start | bytes 786440 | tf_op jit(solution)/shard_map/ppermute | solution.py:113
  70.4 11.2 %collective-permute-start.6 = (bf16[256,512]{1,0:T(8,128)(2,1)S(1)}, bf16[256,512]{1,0:T(8,128)(2,1)S(1)}, u32[]{:S(2)}, u32[]{:S(2)}) collective-permute-start(bf16[256,512]{1,0:T(8,128)(2,1)S(1)} %collective-permute-done.5), channel_id=1, source_target_pairs={{0,4},{4,8},{8,12},{12,14},{14,10},{10,6},{6,2},{2,0},{1,5},{5,9},... | collective-permute-start | bytes 786440 | tf_op jit(solution)/shard_map/ppermute | solution.py:113
  74.5 10.5 %collective-permute-start.13 = (bf16[256,512]{1,0:T(8,128)(2,1)S(1)}, bf16[256,512]{1,0:T(8,128)(2,1)S(1)}, u32[]{:S(2)}, u32[]{:S(2)}) collective-permute-start(bf16[256,512]{1,0:T(8,128)(2,1)S(1)} %collective-permute-done.12), channel_id=1, source_target_pairs={{4,0},{8,4},{12,8},{14,12},{10,14},{6,10},{2,6},{0,2},{5,1},{9,5},... | collective-permute-start | bytes 786440 | tf_op jit(solution)/shard_map/ppermute | solution.py:113
  76.0 9.2 %collective-permute-start.20 = (bf16[256,512]{1,0:T(8,128)(2,1)S(1)}, bf16[256,512]{1,0:T(8,128)(2,1)S(1)}, u32[]{:S(2)}, u32[]{:S(2)}) collective-permute-start(bf16[256,512]{1,0:T(8,128)(2,1)S(1)} %collective-permute-done.19), channel_id=1, source_target_pairs={{0,4},{4,8},{8,12},{12,14},{14,10},{10,6},{6,2},{2,0},{1,5},{5,9},... | collective-permute-start | bytes 786440 | tf_op jit(solution)/shard_map/ppermute | solution.py:113
  80.1 7.7 %collective-permute-start.27 = (bf16[256,512]{1,0:T(8,128)(2,1)S(1)}, bf16[256,512]{1,0:T(8,128)(2,1)S(1)}, u32[]{:S(2)}, u32[]{:S(2)}) collective-permute-start(bf16[256,512]{1,0:T(8,128)(2,1)S(1)} %collective-permute-done.26), channel_id=1, source_target_pairs={{4,0},{8,4},{12,8},{14,12},{10,14},{6,10},{2,6},{0,2},{5,1},{9,5},... | collective-permute-start | bytes 786440 | tf_op jit(solution)/shard_map/ppermute | solution.py:113
  90.5 3.6 %collective-permute-start.28 = (bf16[256,2048]{1,0:T(8,128)(2,1)S(1)}, bf16[256,2048]{1,0:T(8,128)(2,1)S(1)}, u32[]{:S(2)}, u32[]{:S(2)}) collective-permute-start(bf16[256,2048]{1,0:T(8,128)(2,1)S(1)} %get-tuple-element.192), channel_id=1, source_target_pairs={{0,1},{2,3},{4,5},{6,7},{8,9},{10,11},{12,13},{14,15},{16,17},{18,... | collective-permute-start | bytes 3145736 | tf_op jit(solution)/shard_map/ppermute | solution.py:18
  92.4 8.4 %copy-start = (bf16[2048,2048]{1,0:T(8,128)(2,1)}, bf16[2048,2048]{1,0:T(8,128)(2,1)S(1)}, u32[]{:S(2)}) copy-start(bf16[2048,2048]{1,0:T(8,128)(2,1)S(1)} %constant_dynamic-update-slice_fusion) | copy-start | bytes 25165828
  94.7 6.1 %copy-start.6 = (bf16[128,2048]{1,0:T(8,128)(2,1)S(1)}, bf16[128,2048]{1,0:T(8,128)(2,1)}, u32[]{:S(2)}) copy-start(bf16[128,2048]{1,0:T(8,128)(2,1)} %param.9) | copy-start | bytes 1572868
  100.8 17.1 %copy-start.3 = (f32[128,2048]{1,0:T(8,128)S(1)}, f32[128,2048]{1,0:T(8,128)}, u32[]{:S(2)}) copy-start(f32[128,2048]{1,0:T(8,128)} %convert_element_type.66) | copy-start | bytes 3145732
  102.2 3.6 %collective-permute-start.29 = (f32[7]{0:T(128)S(1)}, f32[7]{0:T(128)S(1)}, u32[]{:S(2)}, u32[]{:S(2)}) collective-permute-start(f32[7]{0:T(128)S(1)} %pad_maximum_fusion.1), channel_id=1, source_target_pairs={{0,2},{2,0},{4,6},{6,4},{8,10},{10,8},{12,14},{14,12},{1,3},{3,1},... | collective-permute-start | bytes 92 | tf_op jit(solution)/shard_map/ppermute | solution.py:128
  106.5 3.6 %collective-permute-start.30 = (f32[7]{0:T(128)S(1)}, f32[7]{0:T(128)S(1)}, u32[]{:S(2)}, u32[]{:S(2)}) collective-permute-start(f32[7]{0:T(128)S(1)} %fusion.154), channel_id=1, source_target_pairs={{0,4},{2,6},{4,0},{6,2},{8,12},{10,14},{12,8},{14,10},{1,5},{3,7},... | collective-permute-start | bytes 92 | tf_op jit(solution)/shard_map/ppermute | solution.py:128
  110.1 4.5 %collective-permute-start.31 = (f32[7]{0:T(128)S(1)}, f32[7]{0:T(128)S(1)}, u32[]{:S(2)}, u32[]{:S(2)}) collective-permute-start(f32[7]{0:T(128)S(1)} %add.463), channel_id=1, source_target_pairs={{0,8},{2,10},{4,12},{6,14},{8,0},{10,2},{12,4},{14,6},{1,9},{3,11}... | collective-permute-start | bytes 92 | tf_op jit(solution)/shard_map/ppermute | solution.py:128
  119.0 12.0 %collective-permute-start.32 = (bf16[256,2048]{1,0:T(8,128)(2,1)}, bf16[256,2048]{1,0:T(8,128)(2,1)S(1)}, u32[]{:S(2)}, u32[]{:S(2)}) collective-permute-start(bf16[256,2048]{1,0:T(8,128)(2,1)} %get-tuple-element.202), channel_id=1, source_target_pairs={{1,0},{3,2},{5,4},{7,6},{9,8},{11,10},{13,12},{15,14},{17,16},{19,... | collective-permute-start | bytes 3145736 | tf_op jit(solution)/shard_map/ppermute | solution.py:18
  121.4 9.0 %collective-permute-start.33 = (f32[1]{0:T(128)}, f32[1]{0:T(128)}, u32[]{:S(2)}, u32[]{:S(2)}) collective-permute-start(f32[1]{0:T(128)} %bitcast.20), channel_id=1, source_target_pairs={{1,0},{3,2},{5,4},{7,6},{9,8},{11,10},{13,12},{15,14},{17,16},{19,... | collective-permute-start | bytes 20 | tf_op jit(solution)/shard_map/ppermute | solution.py:18

commit v11 on v10

--- a/solution.py
+++ b/solution.py
@@ -225,7 +225,7 @@
     for m in range(members):
         terms.append(jnp.sum(yf[m] * obs_f, axis=-1))
     terms = jnp.sum(jnp.stack(terms), axis=-1)
-    packed = tree_sum(jnp.concatenate([terms, obs_sq.reshape(1)]), "tok")
+    packed = jnp.sum(lax.all_gather(jnp.concatenate([terms, obs_sq.reshape(1)]), "tok"), axis=0)
     slope_a, slope_b = lax.optimization_barrier((gelu_slope(fa[3]), gelu_slope(fb[3])))
     member_gram = packed[: members * members].reshape(members, members)
     obs_rows = packed[members * members : members * members + members]

time: 141 us -> 149 us (1.057)
  blocking collectives: 0 us -> 20.5 us
  waiting for transfers between devices: 54.8 us -> 45.7 us
  starting transfers between devices: 38.1 us -> 33.9 us
    unnamed x0 -> x1, blocking collectives: none -> 20.5 us
    ppermute x3 -> x0, waiting for transfers between devices: 7.31 us -> none  [tree_sum(): v = v + lax.ppermute(v, axis, [(i, i ^ b) for i in range(n)])]
    ppermute x3 -> x0, starting transfers between devices: 4.3 us -> none  [tree_sum(): v = v + lax.ppermute(v, axis, [(i, i ^ b) for i in range(n)])]
  transfers between devices with their start and end apart: 34 -> 31, of which waited for: 27 -> 24; matrix products, arithmetic and copies ran while one was open for 11% -> 11% of each run, Pallas kernels for 0% -> 0%
where the time goes in v11:
time: 149 us; the launch traced here: 148 us
  waiting for transfers between devices  45.7 us (31%)
  starting transfers between devices  33.9 us (23%)
  matrix products  21.8 us (15%)
  blocking collectives  20.5 us (14%)
  other arithmetic  11.4 us (8%)
  local copies, waits for them, and re-layouts  10.1 us (7%)
  between operations  5.13 us (3%)
    ppermute x28, waiting for transfers between devices, ring_gather(): parts[j] = lax.ppermute(parts[j], axis, cw if clockwise else ccw)  36.8 us
    ppermute x28, starting transfers between devices, ring_gather(): parts[j] = lax.ppermute(parts[j], axis, cw if clockwise else ccw)  29.8 us
    unnamed x1, blocking collectives  20.5 us
    ppermute x3, waiting for transfers between devices, shifted(): return lax.ppermute(x, axis, pairs)  8.88 us
    dot_general x28, matrix products, on_piece(): term = jnp.dot(lhs, piece, preferred_element_type=jnp.float32)  8.27 us
    dot_general x1, matrix products, section_backward(): lax.dot_general(grad_pre, weight, (((1,), (1,)), ((), ())), preferred_ele...  6.58 us
    dot_general x1, matrix products, section_forward(): pre_act = jnp.dot(normed, weight, preferred_element_type=jnp.float32)  6.04 us
    ppermute x3, starting transfers between devices, shifted(): return lax.ppermute(x, axis, pairs)  4.1 us
  transfers between devices with their start and end apart: 31, of which 24 were waited for; matrix products, arithmetic and copies ran while one was open for 11% of the time, Pallas kernels for 0%

profile of v11, /device:TPU:0, one launch (start us, length us, event | category | flops | bytes accessed | tf_op | source)
XLA Modules:
  0.0 148.5 jit_solution(7961452314851198987)
XLA Ops:
  0.7 2.2 %fusion.121 = (bf16[256,512]{1,0:T(8,128)(2,1)}, bf16[256,512]{1,0:T(8,128)(2,1)}, bf16[256,512]{1,0:T(8,128)(2,1)}, bf16[256,512]{1,0:T(8,128)(2,1)S(1)}) fusion(bf16[256,2048]{1,0:T(8,128)(2,1)} %bitcast.131), kind=kLoop, calls=%fused_computation.228 | loop fusion | bytes 2097152 | tf_op jit(solution)/shard_map/slice | solution.py:106
  2.9 3.1 %collective-permute-start = (bf16[256,512]{1,0:T(8,128)(2,1)S(1)}, bf16[256,512]{1,0:T(8,128)(2,1)S(1)}, u32[]{:S(2)}, u32[]{:S(2)}) collective-permute-start(bf16[256,512]{1,0:T(8,128)(2,1)S(1)} %get-tuple-element.199), channel_id=1, source_target_pairs={{0,4},{4,8},{8,12},{12,14},{14,10},{10,6},{6,2},{2,0},{1,5},{5,9},... | collective-permute-start | bytes 786440 | tf_op jit(solution)/shard_map/ppermute | solution.py:113
  5.9 2.0 %collective-permute-start.14 = (bf16[256,512]{1,0:T(8,128)(2,1)}, bf16[256,512]{1,0:T(8,128)(2,1)}, u32[]{:S(2)}, u32[]{:S(2)}) collective-permute-start(bf16[256,512]{1,0:T(8,128)(2,1)} %get-tuple-element.197), channel_id=1, source_target_pairs={{0,4},{4,8},{8,12},{12,14},{14,10},{10,6},{6,2},{2,0},{1,5},{5,9},... | collective-permute-start | bytes 786440 | tf_op jit(solution)/shard_map/ppermute | solution.py:113
  11.4 1.6 %collective-permute-done = bf16[256,512]{1,0:T(8,128)(2,1)S(1)} collective-permute-done((bf16[256,512]{1,0:T(8,128)(2,1)S(1)}, bf16[256,512]{1,0:T(8,128)(2,1)S(1)}, u32[]{:S(2)}, u32[]{:S(2)}) %collective-permute-start) | collective-permute-done | bytes 262176 | tf_op jit(solution)/shard_map/ppermute | solution.py:113
  15.9 2.2 %collective-permute-start.1 = (bf16[256,512]{1,0:T(8,128)(2,1)S(1)}, bf16[256,512]{1,0:T(8,128)(2,1)S(1)}, u32[]{:S(2)}, u32[]{:S(2)}) collective-permute-start(bf16[256,512]{1,0:T(8,128)(2,1)S(1)} %copy-done.9), channel_id=1, source_target_pairs={{0,4},{4,8},{8,12},{12,14},{14,10},{10,6},{6,2},{2,0},{1,5},{5,9},... | collective-permute-start | bytes 786440 | tf_op jit(solution)/shard_map/ppermute | solution.py:113
  20.5 1.2 fusion.45
  21.7 2.1 %collective-permute-start.15 = (bf16[256,512]{1,0:T(8,128)(2,1)}, bf16[256,512]{1,0:T(8,128)(2,1)S(1)}, u32[]{:S(2)}, u32[]{:S(2)}) collective-permute-start(bf16[256,512]{1,0:T(8,128)(2,1)} %collective-permute-done.14), channel_id=1, source_target_pairs={{0,4},{4,8},{8,12},{12,14},{14,10},{10,6},{6,2},{2,0},{1,5},{5,9},... | collective-permute-start | bytes 786440 | tf_op jit(solution)/shard_map/ppermute | solution.py:113
  24.7 1.2 fusion.69
  26.3 2.1 %collective-permute-start.2 = (bf16[256,512]{1,0:T(8,128)(2,1)S(1)}, bf16[256,512]{1,0:T(8,128)(2,1)S(1)}, u32[]{:S(2)}, u32[]{:S(2)}) collective-permute-start(bf16[256,512]{1,0:T(8,128)(2,1)S(1)} %collective-permute-done.1), channel_id=1, source_target_pairs={{0,4},{4,8},{8,12},{12,14},{14,10},{10,6},{6,2},{2,0},{1,5},{5,9},... | collective-permute-start | bytes 786440 | tf_op jit(solution)/shard_map/ppermute | solution.py:113
  28.4 2.7 %collective-permute-done.15 = bf16[256,512]{1,0:T(8,128)(2,1)S(1)} collective-permute-done((bf16[256,512]{1,0:T(8,128)(2,1)}, bf16[256,512]{1,0:T(8,128)(2,1)S(1)}, u32[]{:S(2)}, u32[]{:S(2)}) %collective-permute-start.15) | collective-permute-done | bytes 262176 | tf_op jit(solution)/shard_map/ppermute | solution.py:113
  31.1 2.0 %collective-permute-start.16 = (bf16[256,512]{1,0:T(8,128)(2,1)S(1)}, bf16[256,512]{1,0:T(8,128)(2,1)S(1)}, u32[]{:S(2)}, u32[]{:S(2)}) collective-permute-start(bf16[256,512]{1,0:T(8,128)(2,1)S(1)} %collective-permute-done.15), channel_id=1, source_target_pairs={{0,4},{4,8},{8,12},{12,14},{14,10},{10,6},{6,2},{2,0},{1,5},{5,9},... | collective-permute-start | bytes 786440 | tf_op jit(solution)/shard_map/ppermute | solution.py:113
  33.2 1.9 %collective-permute-done.22 = bf16[256,512]{1,0:T(8,128)(2,1)S(1)} collective-permute-done((bf16[256,512]{1,0:T(8,128)(2,1)S(1)}, bf16[256,512]{1,0:T(8,128)(2,1)S(1)}, u32[]{:S(2)}, u32[]{:S(2)}) %collective-permute-start.22) | collective-permute-done | bytes 262176 | tf_op jit(solution)/shard_map/ppermute | solution.py:113
  36.7 2.0 %collective-permute-start.3 = (bf16[256,512]{1,0:T(8,128)(2,1)S(1)}, bf16[256,512]{1,0:T(8,128)(2,1)S(1)}, u32[]{:S(2)}, u32[]{:S(2)}) collective-permute-start(bf16[256,512]{1,0:T(8,128)(2,1)S(1)} %collective-permute-done.2), channel_id=1, source_target_pairs={{0,4},{4,8},{8,12},{12,14},{14,10},{10,6},{6,2},{2,0},{1,5},{5,9},... | collective-permute-start | bytes 786440 | tf_op jit(solution)/shard_map/ppermute | solution.py:113
  38.7 2.0 %collective-permute-done.9 = bf16[256,512]{1,0:T(8,128)(2,1)S(1)} collective-permute-done((bf16[256,512]{1,0:T(8,128)(2,1)S(1)}, bf16[256,512]{1,0:T(8,128)(2,1)S(1)}, u32[]{:S(2)}, u32[]{:S(2)}) %collective-permute-start.9) | collective-permute-done | bytes 262176 | tf_op jit(solution)/shard_map/ppermute | solution.py:113
  40.8 1.5 %collective-permute-done.16 = bf16[256,512]{1,0:T(8,128)(2,1)S(1)} collective-permute-done((bf16[256,512]{1,0:T(8,128)(2,1)S(1)}, bf16[256,512]{1,0:T(8,128)(2,1)S(1)}, u32[]{:S(2)}, u32[]{:S(2)}) %collective-permute-start.16) | collective-permute-done | bytes 262176 | tf_op jit(solution)/shard_map/ppermute | solution.py:113
  42.3 2.0 %collective-permute-start.17 = (bf16[256,512]{1,0:T(8,128)(2,1)S(1)}, bf16[256,512]{1,0:T(8,128)(2,1)S(1)}, u32[]{:S(2)}, u32[]{:S(2)}) collective-permute-start(bf16[256,512]{1,0:T(8,128)(2,1)S(1)} %collective-permute-done.16), channel_id=1, source_target_pairs={{0,4},{4,8},{8,12},{12,14},{14,10},{10,6},{6,2},{2,0},{1,5},{5,9},... | collective-permute-start | bytes 786440 | tf_op jit(solution)/shard_map/ppermute | solution.py:113
  44.5 1.9 %collective-permute-done.23 = bf16[256,512]{1,0:T(8,128)(2,1)S(1)} collective-permute-done((bf16[256,512]{1,0:T(8,128)(2,1)S(1)}, bf16[256,512]{1,0:T(8,128)(2,1)S(1)}, u32[]{:S(2)}, u32[]{:S(2)}) %collective-permute-start.23) | collective-permute-done | bytes 262176 | tf_op jit(solution)/shard_map/ppermute | solution.py:113
  48.0 2.0 %collective-permute-start.4 = (bf16[256,512]{1,0:T(8,128)(2,1)S(1)}, bf16[256,512]{1,0:T(8,128)(2,1)S(1)}, u32[]{:S(2)}, u32[]{:S(2)}) collective-permute-start(bf16[256,512]{1,0:T(8,128)(2,1)S(1)} %collective-permute-done.3), channel_id=1, source_target_pairs={{0,4},{4,8},{8,12},{12,14},{14,10},{10,6},{6,2},{2,0},{1,5},{5,9},... | collective-permute-start | bytes 786440 | tf_op jit(solution)/shard_map/ppermute | solution.py:113
  50.0 2.0 %collective-permute-done.10 = bf16[256,512]{1,0:T(8,128)(2,1)S(1)} collective-permute-done((bf16[256,512]{1,0:T(8,128)(2,1)S(1)}, bf16[256,512]{1,0:T(8,128)(2,1)S(1)}, u32[]{:S(2)}, u32[]{:S(2)}) %collective-permute-start.10) | collective-permute-done | bytes 262176 | tf_op jit(solution)/shard_map/ppermute | solution.py:113
  52.0 1.5 %collective-permute-done.17 = bf16[256,512]{1,0:T(8,128)(2,1)S(1)} collective-permute-done((bf16[256,512]{1,0:T(8,128)(2,1)S(1)}, bf16[256,512]{1,0:T(8,128)(2,1)S(1)}, u32[]{:S(2)}, u32[]{:S(2)}) %collective-permute-start.17) | collective-permute-done | bytes 262176 | tf_op jit(solution)/shard_map/ppermute | solution.py:113
  53.6 2.0 %collective-permute-start.18 = (bf16[256,512]{1,0:T(8,128)(2,1)S(1)}, bf16[256,512]{1,0:T(8,128)(2,1)S(1)}, u32[]{:S(2)}, u32[]{:S(2)}) collective-permute-start(bf16[256,512]{1,0:T(8,128)(2,1)S(1)} %collective-permute-done.17), channel_id=1, source_target_pairs={{0,4},{4,8},{8,12},{12,14},{14,10},{10,6},{6,2},{2,0},{1,5},{5,9},... | collective-permute-start | bytes 786440 | tf_op jit(solution)/shard_map/ppermute | solution.py:113
  55.6 2.0 %collective-permute-done.24 = bf16[256,512]{1,0:T(8,128)(2,1)S(1)} collective-permute-done((bf16[256,512]{1,0:T(8,128)(2,1)S(1)}, bf16[256,512]{1,0:T(8,128)(2,1)S(1)}, u32[]{:S(2)}, u32[]{:S(2)}) %collective-permute-start.24) | collective-permute-done | bytes 262176 | tf_op jit(solution)/shard_map/ppermute | solution.py:113
  59.2 2.0 %collective-permute-start.5 = (bf16[256,512]{1,0:T(8,128)(2,1)S(1)}, bf16[256,512]{1,0:T(8,128)(2,1)S(1)}, u32[]{:S(2)}, u32[]{:S(2)}) collective-permute-start(bf16[256,512]{1,0:T(8,128)(2,1)S(1)} %collective-permute-done.4), channel_id=1, source_target_pairs={{0,4},{4,8},{8,12},{12,14},{14,10},{10,6},{6,2},{2,0},{1,5},{5,9},... | collective-permute-start | bytes 786440 | tf_op jit(solution)/shard_map/ppermute | solution.py:113
  61.2 2.0 %collective-permute-done.11 = bf16[256,512]{1,0:T(8,128)(2,1)S(1)} collective-permute-done((bf16[256,512]{1,0:T(8,128)(2,1)S(1)}, bf16[256,512]{1,0:T(8,128)(2,1)S(1)}, u32[]{:S(2)}, u32[]{:S(2)}) %collective-permute-start.11) | collective-permute-done | bytes 262176 | tf_op jit(solution)/shard_map/ppermute | solution.py:113
  63.3 1.5 %collective-permute-done.18 = bf16[256,512]{1,0:T(8,128)(2,1)S(1)} collective-permute-done((bf16[256,512]{1,0:T(8,128)(2,1)S(1)}, bf16[256,512]{1,0:T(8,128)(2,1)S(1)}, u32[]{:S(2)}, u32[]{:S(2)}) %collective-permute-start.18) | collective-permute-done | bytes 262176 | tf_op jit(solution)/shard_map/ppermute | solution.py:113
  64.8 2.0 %collective-permute-start.19 = (bf16[256,512]{1,0:T(8,128)(2,1)S(1)}, bf16[256,512]{1,0:T(8,128)(2,1)S(1)}, u32[]{:S(2)}, u32[]{:S(2)}) collective-permute-start(bf16[256,512]{1,0:T(8,128)(2,1)S(1)} %collective-permute-done.18), channel_id=1, source_target_pairs={{0,4},{4,8},{8,12},{12,14},{14,10},{10,6},{6,2},{2,0},{1,5},{5,9},... | collective-permute-start | bytes 786440 | tf_op jit(solution)/shard_map/ppermute | solution.py:113
  66.9 2.0 %collective-permute-done.25 = bf16[256,512]{1,0:T(8,128)(2,1)S(1)} collective-permute-done((bf16[256,512]{1,0:T(8,128)(2,1)S(1)}, bf16[256,512]{1,0:T(8,128)(2,1)S(1)}, u32[]{:S(2)}, u32[]{:S(2)}) %collective-permute-start.25) | collective-permute-done | bytes 262176 | tf_op jit(solution)/shard_map/ppermute | solution.py:113
  70.4 2.0 %collective-permute-start.6 = (bf16[256,512]{1,0:T(8,128)(2,1)S(1)}, bf16[256,512]{1,0:T(8,128)(2,1)S(1)}, u32[]{:S(2)}, u32[]{:S(2)}) collective-permute-start(bf16[256,512]{1,0:T(8,128)(2,1)S(1)} %collective-permute-done.5), channel_id=1, source_target_pairs={{0,4},{4,8},{8,12},{12,14},{14,10},{10,6},{6,2},{2,0},{1,5},{5,9},... | collective-permute-start | bytes 786440 | tf_op jit(solution)/shard_map/ppermute | solution.py:113
  72.5 2.0 %collective-permute-done.12 = bf16[256,512]{1,0:T(8,128)(2,1)S(1)} collective-permute-done((bf16[256,512]{1,0:T(8,128)(2,1)S(1)}, bf16[256,512]{1,0:T(8,128)(2,1)S(1)}, u32[]{:S(2)}, u32[]{:S(2)}) %collective-permute-start.12) | collective-permute-done | bytes 262176 | tf_op jit(solution)/shard_map/ppermute | solution.py:113
  74.5 1.5 %collective-permute-done.19 = bf16[256,512]{1,0:T(8,128)(2,1)S(1)} collective-permute-done((bf16[256,512]{1,0:T(8,128)(2,1)S(1)}, bf16[256,512]{1,0:T(8,128)(2,1)S(1)}, u32[]{:S(2)}, u32[]{:S(2)}) %collective-permute-start.19) | collective-permute-done | bytes 262176 | tf_op jit(solution)/shard_map/ppermute | solution.py:113
  76.0 2.0 %collective-permute-start.20 = (bf16[256,512]{1,0:T(8,128)(2,1)S(1)}, bf16[256,512]{1,0:T(8,128)(2,1)S(1)}, u32[]{:S(2)}, u32[]{:S(2)}) collective-permute-start(bf16[256,512]{1,0:T(8,128)(2,1)S(1)} %collective-permute-done.19), channel_id=1, source_target_pairs={{0,4},{4,8},{8,12},{12,14},{14,10},{10,6},{6,2},{2,0},{1,5},{5,9},... | collective-permute-start | bytes 786440 | tf_op jit(solution)/shard_map/ppermute | solution.py:113
  78.1 2.0 %collective-permute-done.26 = bf16[256,512]{1,0:T(8,128)(2,1)S(1)} collective-permute-done((bf16[256,512]{1,0:T(8,128)(2,1)S(1)}, bf16[256,512]{1,0:T(8,128)(2,1)S(1)}, u32[]{:S(2)}, u32[]{:S(2)}) %collective-permute-start.26) | collective-permute-done | bytes 262176 | tf_op jit(solution)/shard_map/ppermute | solution.py:113
  81.9 3.1 %collective-permute-done.13 = bf16[256,512]{1,0:T(8,128)(2,1)S(1)} collective-permute-done((bf16[256,512]{1,0:T(8,128)(2,1)S(1)}, bf16[256,512]{1,0:T(8,128)(2,1)S(1)}, u32[]{:S(2)}, u32[]{:S(2)}) %collective-permute-start.13) | collective-permute-done | bytes 262176 | tf_op jit(solution)/shard_map/ppermute | solution.py:113
  85.5 2.3 %collective-permute-done.27 = bf16[256,512]{1,0:T(8,128)(2,1)S(1)} collective-permute-done((bf16[256,512]{1,0:T(8,128)(2,1)S(1)}, bf16[256,512]{1,0:T(8,128)(2,1)S(1)}, u32[]{:S(2)}, u32[]{:S(2)}) %collective-permute-start.27) | collective-permute-done | bytes 262176 | tf_op jit(solution)/shard_map/ppermute | solution.py:113
  88.1 2.5 %fusion.23 = (f32[256,2048]{1,0:T(8,128)}, bf16[256,2048]{1,0:T(8,128)(2,1)S(1)}) fusion(f32[256,512]{1,0:T(8,128)S(1)} %fusion.27, f32[256,512]{1,0:T(8,128)S(1)} %fusion.28, f32[256,512]{1,0:T(8,128)S(1)} %fusion.29, f32[256,512]{1,0:T(8,128)S(1)} %fusion.30, bf16[256,2048]{1,0:T(8,128)(2,1)S(1)} %bitcast.130), kind=kLoop, calls=%fused_computation.57 | loop fusion | flops 12582912 | bytes 6291456 | tf_op jit(solution)/shard_map/add | solution.py:28
  90.5 1.5 %collective-permute-start.28 = (bf16[256,2048]{1,0:T(8,128)(2,1)S(1)}, bf16[256,2048]{1,0:T(8,128)(2,1)S(1)}, u32[]{:S(2)}, u32[]{:S(2)}) collective-permute-start(bf16[256,2048]{1,0:T(8,128)(2,1)S(1)} %get-tuple-element.192), channel_id=1, source_target_pairs={{0,1},{2,3},{4,5},{6,7},{8,9},{10,11},{12,13},{14,15},{16,17},{18,... | collective-permute-start | bytes 3145736 | tf_op jit(solution)/shard_map/ppermute | solution.py:18
  92.4 1.6 %collective-permute-done.28 = bf16[256,2048]{1,0:T(8,128)(2,1)S(1)} collective-permute-done((bf16[256,2048]{1,0:T(8,128)(2,1)S(1)}, bf16[256,2048]{1,0:T(8,128)(2,1)S(1)}, u32[]{:S(2)}, u32[]{:S(2)}) %collective-permute-start.28) | collective-permute-done | bytes 1048608 | tf_op jit(solution)/shard_map/ppermute | solution.py:18
  94.8 6.0 %bitcast_convert_fusion.2 = (f32[2,128,2048]{2,1,0:T(8,128)S(1)}, bf16[256,2048]{1,0:T(8,128)(2,1)}, f32[256,2048]{1,0:T(8,128)}, f32[256,2048]{1,0:T(8,128)}) fusion(bf16[256,2048]{1,0:T(8,128)(2,1)S(1)} %collective-permute-done.28, f32[256]{0:T(256)S(1)} %add_rsqrt_fusion.1, f32[256]{0:T(256)S(1)} %broadcast_multiply_fusion.4, ...), kind=kOutput, calls=%fused_computation.218 | convolution fusion | flops 2162688000 | bytes 16787456 | tf_op jit(solution)/shard_map/dot_general | solution.py:50
  102.3 20.5 %all-reduce = f32[56]{0:T(128)S(1)} all-reduce(f32[56]{0:T(128)S(1)} %maximum_dynamic-update-slice_fusion), channel_id=2, replica_groups=mesh['groups'=2,'tok'=8,'section'=2] {'tok'}, use_global_device_ids=true, to_apply=%add | all-reduce | flops 56 | bytes 448
  125.0 1.4 fusion.119
  126.4 1.1 conditional.2
  126.4 1.1 broadcast.190
  127.5 1.3 collective-permute-start.29
  130.0 1.3 collective-permute-start.30
  131.3 7.2 %collective-permute-done.30 = f32[1]{0:T(128)} collective-permute-done((f32[1]{0:T(128)}, f32[1]{0:T(128)}, u32[]{:S(2)}, u32[]{:S(2)}) %collective-permute-start.30) | collective-permute-done | bytes 36 | tf_op jit(solution)/shard_map/ppermute | solution.py:18
  139.2 8.2 %conditional.3 = (bf16[1,2,128,2048]{3,2,1,0:T(8,128)(2,1)}) conditional(s32[]{:T(128)} %convert_element_type.58, bf16[256,2048]{1,0:T(8,128)(2,1)} %get-tuple-element.202, (bf16[256,2048]{1,0:T(8,128)(2,1)S(1)}, f32[256]{0:T(256)S(1)}, f32[]{:T(128)}, f32[]{:T(128)}, f32[256,2048]{1,0:T(8,128)}, /*index=5*/bf16[2048,2048]{1,0:T(8,128)(2,1)}, ...), branch_computations={%region_16.17_spmd, %region_17.20_spmd} | conditional | flops 2154824192 | bytes 22039568 | solution.py:246
  139.2 6.6 %fusion.114 = (f32[256]{0:T(256)S(1)}, f32[256]{0:T(256)S(1)}, f32[256,2048]{1,0:T(8,128)S(1)}) fusion(f32[256,2048]{1,0:T(8,128)S(1)} %get-tuple-element.67, f32[2048]{0:T(1024)S(1)} %bitcast.143, bf16[2048,2048]{1,0:T(8,128)(2,1)} %get-tuple-element.65, f32[256,2048]{1,0:T(8,128)} %get-tuple-element.64, bf16[256,2048]{1,0:T(8,128)(2,1)S(1)} %get-tuple-element.60), kind=kOutput, calls=%fused_computation.223 | convolution fusion | flops 2151153152 | bytes 15738880 | tf_op jit(solution)/shard_map/cond/branch_1_fun/dot_general | solution.py:57
  145.8 1.6 %fusion.1 = bf16[256,2048]{1,0:T(8,128)(2,1)} fusion(bf16[256,2048]{1,0:T(8,128)(2,1)S(1)} %get-tuple-element.60, f32[256,2048]{1,0:T(8,128)S(1)} %get-tuple-element.67, f32[256,2048]{1,0:T(8,128)S(1)} %get-tuple-element.180, f32[256]{0:T(256)S(1)} %add_rsqrt_fusion, f32[256]{0:T(256)S(1)} %get-tuple-element.181, f32[256]{0:T(256)S(1)} %get-tuple-element.182), kind=kLoop, calls=%fused_computation.5 | loop fusion | flops 3670016 | bytes 6294528 | tf_op jit(solution)/shard_map/cond/branch_1_fun/convert_element_type | solution.py:66
  (135 shorter events, 22.4 us)
Async XLA Ops:
  0.6 8.6 %copy-start.11 = (u32[32]{0:T(128)S(1)}, u32[32]{0:T(128)}, u32[]{:S(2)}) copy-start(u32[32]{0:T(128)} %constant.215) | copy-start | bytes 388
  0.6 7.5 %copy-start.5 = (bf16[128,2048]{1,0:T(8,128)(2,1)S(1)}, bf16[128,2048]{1,0:T(8,128)(2,1)}, u32[]{:S(2)}) copy-start(bf16[128,2048]{1,0:T(8,128)(2,1)} %param.9) | copy-start | bytes 1572868
  0.7 12.4 %copy-start.2 = (bf16[2,128,2048]{2,1,0:T(8,128)(2,1)S(1)}, bf16[2,128,2048]{2,1,0:T(8,128)(2,1)}, u32[]{:S(2)}) copy-start(bf16[2,128,2048]{2,1,0:T(8,128)(2,1)} %param.8) | copy-start | bytes 3145732
  2.9 10.1 %collective-permute-start = (bf16[256,512]{1,0:T(8,128)(2,1)S(1)}, bf16[256,512]{1,0:T(8,128)(2,1)S(1)}, u32[]{:S(2)}, u32[]{:S(2)}) collective-permute-start(bf16[256,512]{1,0:T(8,128)(2,1)S(1)} %get-tuple-element.199), channel_id=1, source_target_pairs={{0,4},{4,8},{8,12},{12,14},{14,10},{10,6},{6,2},{2,0},{1,5},{5,9},... | collective-permute-start | bytes 786440 | tf_op jit(solution)/shard_map/ppermute | solution.py:113
  5.9 13.4 %collective-permute-start.7 = (bf16[256,512]{1,0:T(8,128)(2,1)}, bf16[256,512]{1,0:T(8,128)(2,1)}, u32[]{:S(2)}, u32[]{:S(2)}) collective-permute-start(bf16[256,512]{1,0:T(8,128)(2,1)} %get-tuple-element.198), channel_id=1, source_target_pairs={{4,0},{8,4},{12,8},{14,12},{10,14},{6,10},{2,6},{0,2},{5,1},{9,5},... | collective-permute-start | bytes 786440 | tf_op jit(solution)/shard_map/ppermute | solution.py:113
  5.9 15.7 %collective-permute-start.14 = (bf16[256,512]{1,0:T(8,128)(2,1)}, bf16[256,512]{1,0:T(8,128)(2,1)}, u32[]{:S(2)}, u32[]{:S(2)}) collective-permute-start(bf16[256,512]{1,0:T(8,128)(2,1)} %get-tuple-element.197), channel_id=1, source_target_pairs={{0,4},{4,8},{8,12},{12,14},{14,10},{10,6},{6,2},{2,0},{1,5},{5,9},... | collective-permute-start | bytes 786440 | tf_op jit(solution)/shard_map/ppermute | solution.py:113
  8.0 18.0 %collective-permute-start.21 = (bf16[256,512]{1,0:T(8,128)(2,1)}, bf16[256,512]{1,0:T(8,128)(2,1)S(1)}, u32[]{:S(2)}, u32[]{:S(2)}) collective-permute-start(bf16[256,512]{1,0:T(8,128)(2,1)} %get-tuple-element.196), channel_id=1, source_target_pairs={{4,0},{8,4},{12,8},{14,12},{10,14},{6,10},{2,6},{0,2},{5,1},{9,5},... | collective-permute-start | bytes 786440 | tf_op jit(solution)/shard_map/ppermute | solution.py:113
  8.1 5.6 %copy-start.10 = (f32[1,2048]{1,0:T(1,128)S(1)}, f32[1,2048]{1,0:T(1,128)}, u32[]{:S(2)}) copy-start(f32[1,2048]{1,0:T(1,128)} %param.11) | copy-start | bytes 24580
  13.0 0.7 copy-start.8
  13.7 1.2 copy-start.4
  14.2 1.7 %copy-start.9 = (bf16[256,512]{1,0:T(8,128)(2,1)S(1)}, bf16[256,512]{1,0:T(8,128)(2,1)}, u32[]{:S(2)}) copy-start(bf16[256,512]{1,0:T(8,128)(2,1)} %copy-done.8) | copy-start | bytes 786436
  15.9 10.4 %collective-permute-start.1 = (bf16[256,512]{1,0:T(8,128)(2,1)S(1)}, bf16[256,512]{1,0:T(8,128)(2,1)S(1)}, u32[]{:S(2)}, u32[]{:S(2)}) collective-permute-start(bf16[256,512]{1,0:T(8,128)(2,1)S(1)} %copy-done.9), channel_id=1, source_target_pairs={{0,4},{4,8},{8,12},{12,14},{14,10},{10,6},{6,2},{2,0},{1,5},{5,9},... | collective-permute-start | bytes 786440 | tf_op jit(solution)/shard_map/ppermute | solution.py:113
  19.4 9.0 %collective-permute-start.8 = (bf16[256,512]{1,0:T(8,128)(2,1)}, bf16[256,512]{1,0:T(8,128)(2,1)S(1)}, u32[]{:S(2)}, u32[]{:S(2)}) collective-permute-start(bf16[256,512]{1,0:T(8,128)(2,1)} %collective-permute-done.7), channel_id=1, source_target_pairs={{4,0},{8,4},{12,8},{14,12},{10,14},{6,10},{2,6},{0,2},{5,1},{9,5},... | collective-permute-start | bytes 786440 | tf_op jit(solution)/shard_map/ppermute | solution.py:113
  21.7 9.4 %collective-permute-start.15 = (bf16[256,512]{1,0:T(8,128)(2,1)}, bf16[256,512]{1,0:T(8,128)(2,1)S(1)}, u32[]{:S(2)}, u32[]{:S(2)}) collective-permute-start(bf16[256,512]{1,0:T(8,128)(2,1)} %collective-permute-done.14), channel_id=1, source_target_pairs={{0,4},{4,8},{8,12},{12,14},{14,10},{10,6},{6,2},{2,0},{1,5},{5,9},... | collective-permute-start | bytes 786440 | tf_op jit(solution)/shard_map/ppermute | solution.py:113
  25.9 9.2 %collective-permute-start.22 = (bf16[256,512]{1,0:T(8,128)(2,1)S(1)}, bf16[256,512]{1,0:T(8,128)(2,1)S(1)}, u32[]{:S(2)}, u32[]{:S(2)}) collective-permute-start(bf16[256,512]{1,0:T(8,128)(2,1)S(1)} %collective-permute-done.21), channel_id=1, source_target_pairs={{4,0},{8,4},{12,8},{14,12},{10,14},{6,10},{2,6},{0,2},{5,1},{9,5},... | collective-permute-start | bytes 786440 | tf_op jit(solution)/shard_map/ppermute | solution.py:113
  26.3 10.4 %collective-permute-start.2 = (bf16[256,512]{1,0:T(8,128)(2,1)S(1)}, bf16[256,512]{1,0:T(8,128)(2,1)S(1)}, u32[]{:S(2)}, u32[]{:S(2)}) collective-permute-start(bf16[256,512]{1,0:T(8,128)(2,1)S(1)} %collective-permute-done.1), channel_id=1, source_target_pairs={{0,4},{4,8},{8,12},{12,14},{14,10},{10,6},{6,2},{2,0},{1,5},{5,9},... | collective-permute-start | bytes 786440 | tf_op jit(solution)/shard_map/ppermute | solution.py:113
  28.4 12.4 %collective-permute-start.9 = (bf16[256,512]{1,0:T(8,128)(2,1)S(1)}, bf16[256,512]{1,0:T(8,128)(2,1)S(1)}, u32[]{:S(2)}, u32[]{:S(2)}) collective-permute-start(bf16[256,512]{1,0:T(8,128)(2,1)S(1)} %collective-permute-done.8), channel_id=1, source_target_pairs={{4,0},{8,4},{12,8},{14,12},{10,14},{6,10},{2,6},{0,2},{5,1},{9,5},... | collective-permute-start | bytes 786440 | tf_op jit(solution)/shard_map/ppermute | solution.py:113
  31.1 11.2 %collective-permute-start.16 = (bf16[256,512]{1,0:T(8,128)(2,1)S(1)}, bf16[256,512]{1,0:T(8,128)(2,1)S(1)}, u32[]{:S(2)}, u32[]{:S(2)}) collective-permute-start(bf16[256,512]{1,0:T(8,128)(2,1)S(1)} %collective-permute-done.15), channel_id=1, source_target_pairs={{0,4},{4,8},{8,12},{12,14},{14,10},{10,6},{6,2},{2,0},{1,5},{5,9},... | collective-permute-start | bytes 786440 | tf_op jit(solution)/shard_map/ppermute | solution.py:113
  35.2 11.2 %collective-permute-start.23 = (bf16[256,512]{1,0:T(8,128)(2,1)S(1)}, bf16[256,512]{1,0:T(8,128)(2,1)S(1)}, u32[]{:S(2)}, u32[]{:S(2)}) collective-permute-start(bf16[256,512]{1,0:T(8,128)(2,1)S(1)} %collective-permute-done.22), channel_id=1, source_target_pairs={{4,0},{8,4},{12,8},{14,12},{10,14},{6,10},{2,6},{0,2},{5,1},{9,5},... | collective-permute-start | bytes 786440 | tf_op jit(solution)/shard_map/ppermute | solution.py:113
  36.7 11.2 %collective-permute-start.3 = (bf16[256,512]{1,0:T(8,128)(2,1)S(1)}, bf16[256,512]{1,0:T(8,128)(2,1)S(1)}, u32[]{:S(2)}, u32[]{:S(2)}) collective-permute-start(bf16[256,512]{1,0:T(8,128)(2,1)S(1)} %collective-permute-done.2), channel_id=1, source_target_pairs={{0,4},{4,8},{8,12},{12,14},{14,10},{10,6},{6,2},{2,0},{1,5},{5,9},... | collective-permute-start | bytes 786440 | tf_op jit(solution)/shard_map/ppermute | solution.py:113
  40.8 11.2 %collective-permute-start.10 = (bf16[256,512]{1,0:T(8,128)(2,1)S(1)}, bf16[256,512]{1,0:T(8,128)(2,1)S(1)}, u32[]{:S(2)}, u32[]{:S(2)}) collective-permute-start(bf16[256,512]{1,0:T(8,128)(2,1)S(1)} %collective-permute-done.9), channel_id=1, source_target_pairs={{4,0},{8,4},{12,8},{14,12},{10,14},{6,10},{2,6},{0,2},{5,1},{9,5},... | collective-permute-start | bytes 786440 | tf_op jit(solution)/shard_map/ppermute | solution.py:113
  42.3 11.2 %collective-permute-start.17 = (bf16[256,512]{1,0:T(8,128)(2,1)S(1)}, bf16[256,512]{1,0:T(8,128)(2,1)S(1)}, u32[]{:S(2)}, u32[]{:S(2)}) collective-permute-start(bf16[256,512]{1,0:T(8,128)(2,1)S(1)} %collective-permute-done.16), channel_id=1, source_target_pairs={{0,4},{4,8},{8,12},{12,14},{14,10},{10,6},{6,2},{2,0},{1,5},{5,9},... | collective-permute-start | bytes 786440 | tf_op jit(solution)/shard_map/ppermute | solution.py:113
  46.4 11.2 %collective-permute-start.24 = (bf16[256,512]{1,0:T(8,128)(2,1)S(1)}, bf16[256,512]{1,0:T(8,128)(2,1)S(1)}, u32[]{:S(2)}, u32[]{:S(2)}) collective-permute-start(bf16[256,512]{1,0:T(8,128)(2,1)S(1)} %collective-permute-done.23), channel_id=1, source_target_pairs={{4,0},{8,4},{12,8},{14,12},{10,14},{6,10},{2,6},{0,2},{5,1},{9,5},... | collective-permute-start | bytes 786440 | tf_op jit(solution)/shard_map/ppermute | solution.py:113
  48.0 11.2 %collective-permute-start.4 = (bf16[256,512]{1,0:T(8,128)(2,1)S(1)}, bf16[256,512]{1,0:T(8,128)(2,1)S(1)}, u32[]{:S(2)}, u32[]{:S(2)}) collective-permute-start(bf16[256,512]{1,0:T(8,128)(2,1)S(1)} %collective-permute-done.3), channel_id=1, source_target_pairs={{0,4},{4,8},{8,12},{12,14},{14,10},{10,6},{6,2},{2,0},{1,5},{5,9},... | collective-permute-start | bytes 786440 | tf_op jit(solution)/shard_map/ppermute | solution.py:113
  52.0 11.2 %collective-permute-start.11 = (bf16[256,512]{1,0:T(8,128)(2,1)S(1)}, bf16[256,512]{1,0:T(8,128)(2,1)S(1)}, u32[]{:S(2)}, u32[]{:S(2)}) collective-permute-start(bf16[256,512]{1,0:T(8,128)(2,1)S(1)} %collective-permute-done.10), channel_id=1, source_target_pairs={{4,0},{8,4},{12,8},{14,12},{10,14},{6,10},{2,6},{0,2},{5,1},{9,5},... | collective-permute-start | bytes 786440 | tf_op jit(solution)/shard_map/ppermute | solution.py:113
  53.6 11.2 %collective-permute-start.18 = (bf16[256,512]{1,0:T(8,128)(2,1)S(1)}, bf16[256,512]{1,0:T(8,128)(2,1)S(1)}, u32[]{:S(2)}, u32[]{:S(2)}) collective-permute-start(bf16[256,512]{1,0:T(8,128)(2,1)S(1)} %collective-permute-done.17), channel_id=1, source_target_pairs={{0,4},{4,8},{8,12},{12,14},{14,10},{10,6},{6,2},{2,0},{1,5},{5,9},... | collective-permute-start | bytes 786440 | tf_op jit(solution)/shard_map/ppermute | solution.py:113
  57.6 11.2 %collective-permute-start.25 = (bf16[256,512]{1,0:T(8,128)(2,1)S(1)}, bf16[256,512]{1,0:T(8,128)(2,1)S(1)}, u32[]{:S(2)}, u32[]{:S(2)}) collective-permute-start(bf16[256,512]{1,0:T(8,128)(2,1)S(1)} %collective-permute-done.24), channel_id=1, source_target_pairs={{4,0},{8,4},{12,8},{14,12},{10,14},{6,10},{2,6},{0,2},{5,1},{9,5},... | collective-permute-start | bytes 786440 | tf_op jit(solution)/shard_map/ppermute | solution.py:113
  59.2 11.2 %collective-permute-start.5 = (bf16[256,512]{1,0:T(8,128)(2,1)S(1)}, bf16[256,512]{1,0:T(8,128)(2,1)S(1)}, u32[]{:S(2)}, u32[]{:S(2)}) collective-permute-start(bf16[256,512]{1,0:T(8,128)(2,1)S(1)} %collective-permute-done.4), channel_id=1, source_target_pairs={{0,4},{4,8},{8,12},{12,14},{14,10},{10,6},{6,2},{2,0},{1,5},{5,9},... | collective-permute-start | bytes 786440 | tf_op jit(solution)/shard_map/ppermute | solution.py:113
  63.3 11.2 %collective-permute-start.12 = (bf16[256,512]{1,0:T(8,128)(2,1)S(1)}, bf16[256,512]{1,0:T(8,128)(2,1)S(1)}, u32[]{:S(2)}, u32[]{:S(2)}) collective-permute-start(bf16[256,512]{1,0:T(8,128)(2,1)S(1)} %collective-permute-done.11), channel_id=1, source_target_pairs={{4,0},{8,4},{12,8},{14,12},{10,14},{6,10},{2,6},{0,2},{5,1},{9,5},... | collective-permute-start | bytes 786440 | tf_op jit(solution)/shard_map/ppermute | solution.py:113
  64.8 11.2 %collective-permute-start.19 = (bf16[256,512]{1,0:T(8,128)(2,1)S(1)}, bf16[256,512]{1,0:T(8,128)(2,1)S(1)}, u32[]{:S(2)}, u32[]{:S(2)}) collective-permute-start(bf16[256,512]{1,0:T(8,128)(2,1)S(1)} %collective-permute-done.18), channel_id=1, source_target_pairs={{0,4},{4,8},{8,12},{12,14},{14,10},{10,6},{6,2},{2,0},{1,5},{5,9},... | collective-permute-start | bytes 786440 | tf_op jit(solution)/shard_map/ppermute | solution.py:113
  68.9 11.2 %collective-permute-start.26 = (bf16[256,512]{1,0:T(8,128)(2,1)S(1)}, bf16[256,512]{1,0:T(8,128)(2,1)S(1)}, u32[]{:S(2)}, u32[]{:S(2)}) collective-permute-start(bf16[256,512]{1,0:T(8,128)(2,1)S(1)} %collective-permute-done.25), channel_id=1, source_target_pairs={{4,0},{8,4},{12,8},{14,12},{10,14},{6,10},{2,6},{0,2},{5,1},{9,5},... | collective-permute-start | bytes 786440 | tf_op jit(solution)/shard_map/ppermute | solution.py:113
  70.4 11.2 %collective-permute-start.6 = (bf16[256,512]{1,0:T(8,128)(2,1)S(1)}, bf16[256,512]{1,0:T(8,128)(2,1)S(1)}, u32[]{:S(2)}, u32[]{:S(2)}) collective-permute-start(bf16[256,512]{1,0:T(8,128)(2,1)S(1)} %collective-permute-done.5), channel_id=1, source_target_pairs={{0,4},{4,8},{8,12},{12,14},{14,10},{10,6},{6,2},{2,0},{1,5},{5,9},... | collective-permute-start | bytes 786440 | tf_op jit(solution)/shard_map/ppermute | solution.py:113
  74.5 10.5 %collective-permute-start.13 = (bf16[256,512]{1,0:T(8,128)(2,1)S(1)}, bf16[256,512]{1,0:T(8,128)(2,1)S(1)}, u32[]{:S(2)}, u32[]{:S(2)}) collective-permute-start(bf16[256,512]{1,0:T(8,128)(2,1)S(1)} %collective-permute-done.12), channel_id=1, source_target_pairs={{4,0},{8,4},{12,8},{14,12},{10,14},{6,10},{2,6},{0,2},{5,1},{9,5},... | collective-permute-start | bytes 786440 | tf_op jit(solution)/shard_map/ppermute | solution.py:113
  76.0 9.2 %collective-permute-start.20 = (bf16[256,512]{1,0:T(8,128)(2,1)S(1)}, bf16[256,512]{1,0:T(8,128)(2,1)S(1)}, u32[]{:S(2)}, u32[]{:S(2)}) collective-permute-start(bf16[256,512]{1,0:T(8,128)(2,1)S(1)} %collective-permute-done.19), channel_id=1, source_target_pairs={{0,4},{4,8},{8,12},{12,14},{14,10},{10,6},{6,2},{2,0},{1,5},{5,9},... | collective-permute-start | bytes 786440 | tf_op jit(solution)/shard_map/ppermute | solution.py:113
  80.1 7.7 %collective-permute-start.27 = (bf16[256,512]{1,0:T(8,128)(2,1)S(1)}, bf16[256,512]{1,0:T(8,128)(2,1)S(1)}, u32[]{:S(2)}, u32[]{:S(2)}) collective-permute-start(bf16[256,512]{1,0:T(8,128)(2,1)S(1)} %collective-permute-done.26), channel_id=1, source_target_pairs={{4,0},{8,4},{12,8},{14,12},{10,14},{6,10},{2,6},{0,2},{5,1},{9,5},... | collective-permute-start | bytes 786440 | tf_op jit(solution)/shard_map/ppermute | solution.py:113
  90.5 3.6 %collective-permute-start.28 = (bf16[256,2048]{1,0:T(8,128)(2,1)S(1)}, bf16[256,2048]{1,0:T(8,128)(2,1)S(1)}, u32[]{:S(2)}, u32[]{:S(2)}) collective-permute-start(bf16[256,2048]{1,0:T(8,128)(2,1)S(1)} %get-tuple-element.192), channel_id=1, source_target_pairs={{0,1},{2,3},{4,5},{6,7},{8,9},{10,11},{12,13},{14,15},{16,17},{18,... | collective-permute-start | bytes 3145736 | tf_op jit(solution)/shard_map/ppermute | solution.py:18
  92.4 8.4 %copy-start = (bf16[2048,2048]{1,0:T(8,128)(2,1)}, bf16[2048,2048]{1,0:T(8,128)(2,1)S(1)}, u32[]{:S(2)}) copy-start(bf16[2048,2048]{1,0:T(8,128)(2,1)S(1)} %constant_dynamic-update-slice_fusion) | copy-start | bytes 25165828
  94.7 6.1 %copy-start.6 = (bf16[128,2048]{1,0:T(8,128)(2,1)S(1)}, bf16[128,2048]{1,0:T(8,128)(2,1)}, u32[]{:S(2)}) copy-start(bf16[128,2048]{1,0:T(8,128)(2,1)} %param.9) | copy-start | bytes 1572868
  100.8 25.6 %copy-start.3 = (f32[128,2048]{1,0:T(8,128)S(1)}, f32[128,2048]{1,0:T(8,128)}, u32[]{:S(2)}) copy-start(f32[128,2048]{1,0:T(8,128)} %convert_element_type.66) | copy-start | bytes 3145732
  127.5 11.7 %collective-permute-start.29 = (bf16[256,2048]{1,0:T(8,128)(2,1)}, bf16[256,2048]{1,0:T(8,128)(2,1)S(1)}, u32[]{:S(2)}, u32[]{:S(2)}) collective-permute-start(bf16[256,2048]{1,0:T(8,128)(2,1)} %get-tuple-element.202), channel_id=1, source_target_pairs={{1,0},{3,2},{5,4},{7,6},{9,8},{11,10},{13,12},{15,14},{17,16},{19,... | collective-permute-start | bytes 3145736 | tf_op jit(solution)/shard_map/ppermute | solution.py:18
  130.0 8.5 %collective-permute-start.30 = (f32[1]{0:T(128)}, f32[1]{0:T(128)}, u32[]{:S(2)}, u32[]{:S(2)}) collective-permute-start(f32[1]{0:T(128)} %bitcast.21), channel_id=1, source_target_pairs={{1,0},{3,2},{5,4},{7,6},{9,8},{11,10},{13,12},{15,14},{17,16},{19,... | collective-permute-start | bytes 20 | tf_op jit(solution)/shard_map/ppermute | solution.py:18

commit v12 on v10

--- a/solution.py
+++ b/solution.py
@@ -236,7 +236,7 @@
     def second_backward():
         cot = obs_coeff[:, None, None] * obs_f[None]
         for k in range(members):
-            cot = cot + member_coeff[:, k, None, None] * y[k].astype(jnp.float32)[None]
+            cot = cot + member_coeff[:, k, None, None] * yf[k][None]
         cot = cot.reshape(members * tok_rows, width)
         return section_backward(cot, gain, weight, fb[1], fb[2], slope_b)
 

time: 141 us -> 141 us (level)
  no operation moved by 1% of the time
where the time goes in v12:
time: 141 us
  waiting for transfers between devices  54.3 us (39%)
  starting transfers between devices  38.1 us (27%)
  matrix products  21.7 us (15%)
  other arithmetic  11.9 us (8%)
  local copies, waits for them, and re-layouts  10.6 us (8%)
  between operations  4.33 us (3%)
    ppermute x28, waiting for transfers between devices, ring_gather(): parts[j] = lax.ppermute(parts[j], axis, cw if clockwise else ccw)  38.2 us
    ppermute x28, starting transfers between devices, ring_gather(): parts[j] = lax.ppermute(parts[j], axis, cw if clockwise else ccw)  29.7 us
    ppermute x3, waiting for transfers between devices, shifted(): return lax.ppermute(x, axis, pairs)  8.75 us
    dot_general x28, matrix products, on_piece(): term = jnp.dot(lhs, piece, preferred_element_type=jnp.float32)  8.28 us
    ppermute x3, waiting for transfers between devices, tree_sum(): v = v + lax.ppermute(v, axis, [(i, i ^ b) for i in range(n)])  7.37 us
    dot_general x1, matrix products, section_backward(): lax.dot_general(grad_pre, weight, (((1,), (1,)), ((), ())), preferred_ele...  6.58 us
    dot_general x1, matrix products, section_forward(): pre_act = jnp.dot(normed, weight, preferred_element_type=jnp.float32)  5.89 us
    ppermute x3, starting transfers between devices, tree_sum(): v = v + lax.ppermute(v, axis, [(i, i ^ b) for i in range(n)])  4.24 us
  transfers between devices with their start and end apart: 34, of which 27 were waited for; matrix products, arithmetic and copies ran while one was open for 11% of the time, Pallas kernels for 0%

profile of v12, /device:TPU:0, one launch (start us, length us, event | category | flops | bytes accessed | tf_op | source)
XLA Modules:
  0.0 140.9 jit_solution(16298540063463859297)
XLA Ops:
  0.7 2.2 %fusion.122 = (bf16[256,512]{1,0:T(8,128)(2,1)}, bf16[256,512]{1,0:T(8,128)(2,1)}, bf16[256,512]{1,0:T(8,128)(2,1)}, bf16[256,512]{1,0:T(8,128)(2,1)S(1)}) fusion(bf16[256,2048]{1,0:T(8,128)(2,1)} %bitcast.106), kind=kLoop, calls=%fused_computation.225 | loop fusion | bytes 2097152 | tf_op jit(solution)/shard_map/slice | solution.py:106
  2.8 3.1 %collective-permute-start = (bf16[256,512]{1,0:T(8,128)(2,1)S(1)}, bf16[256,512]{1,0:T(8,128)(2,1)S(1)}, u32[]{:S(2)}, u32[]{:S(2)}) collective-permute-start(bf16[256,512]{1,0:T(8,128)(2,1)S(1)} %get-tuple-element.199), channel_id=1, source_target_pairs={{0,4},{4,8},{8,12},{12,14},{14,10},{10,6},{6,2},{2,0},{1,5},{5,9},... | collective-permute-start | bytes 786440 | tf_op jit(solution)/shard_map/ppermute | solution.py:113
  5.9 2.0 %collective-permute-start.14 = (bf16[256,512]{1,0:T(8,128)(2,1)}, bf16[256,512]{1,0:T(8,128)(2,1)}, u32[]{:S(2)}, u32[]{:S(2)}) collective-permute-start(bf16[256,512]{1,0:T(8,128)(2,1)} %get-tuple-element.197), channel_id=1, source_target_pairs={{0,4},{4,8},{8,12},{12,14},{14,10},{10,6},{6,2},{2,0},{1,5},{5,9},... | collective-permute-start | bytes 786440 | tf_op jit(solution)/shard_map/ppermute | solution.py:113
  10.1 2.9 %collective-permute-done = bf16[256,512]{1,0:T(8,128)(2,1)S(1)} collective-permute-done((bf16[256,512]{1,0:T(8,128)(2,1)S(1)}, bf16[256,512]{1,0:T(8,128)(2,1)S(1)}, u32[]{:S(2)}, u32[]{:S(2)}) %collective-permute-start) | collective-permute-done | bytes 262176 | tf_op jit(solution)/shard_map/ppermute | solution.py:113
  15.8 2.2 %collective-permute-start.1 = (bf16[256,512]{1,0:T(8,128)(2,1)S(1)}, bf16[256,512]{1,0:T(8,128)(2,1)S(1)}, u32[]{:S(2)}, u32[]{:S(2)}) collective-permute-start(bf16[256,512]{1,0:T(8,128)(2,1)S(1)} %copy-done.10), channel_id=1, source_target_pairs={{0,4},{4,8},{8,12},{12,14},{14,10},{10,6},{6,2},{2,0},{1,5},{5,9},... | collective-permute-start | bytes 786440 | tf_op jit(solution)/shard_map/ppermute | solution.py:113
  21.6 2.1 %collective-permute-start.15 = (bf16[256,512]{1,0:T(8,128)(2,1)}, bf16[256,512]{1,0:T(8,128)(2,1)S(1)}, u32[]{:S(2)}, u32[]{:S(2)}) collective-permute-start(bf16[256,512]{1,0:T(8,128)(2,1)} %collective-permute-done.14), channel_id=1, source_target_pairs={{0,4},{4,8},{8,12},{12,14},{14,10},{10,6},{6,2},{2,0},{1,5},{5,9},... | collective-permute-start | bytes 786440 | tf_op jit(solution)/shard_map/ppermute | solution.py:113
  26.2 2.1 %collective-permute-start.2 = (bf16[256,512]{1,0:T(8,128)(2,1)S(1)}, bf16[256,512]{1,0:T(8,128)(2,1)S(1)}, u32[]{:S(2)}, u32[]{:S(2)}) collective-permute-start(bf16[256,512]{1,0:T(8,128)(2,1)S(1)} %collective-permute-done.1), channel_id=1, source_target_pairs={{0,4},{4,8},{8,12},{12,14},{14,10},{10,6},{6,2},{2,0},{1,5},{5,9},... | collective-permute-start | bytes 786440 | tf_op jit(solution)/shard_map/ppermute | solution.py:113
  28.3 2.7 %collective-permute-done.15 = bf16[256,512]{1,0:T(8,128)(2,1)S(1)} collective-permute-done((bf16[256,512]{1,0:T(8,128)(2,1)}, bf16[256,512]{1,0:T(8,128)(2,1)S(1)}, u32[]{:S(2)}, u32[]{:S(2)}) %collective-permute-start.15) | collective-permute-done | bytes 262176 | tf_op jit(solution)/shard_map/ppermute | solution.py:113
  31.0 2.0 %collective-permute-start.16 = (bf16[256,512]{1,0:T(8,128)(2,1)S(1)}, bf16[256,512]{1,0:T(8,128)(2,1)S(1)}, u32[]{:S(2)}, u32[]{:S(2)}) collective-permute-start(bf16[256,512]{1,0:T(8,128)(2,1)S(1)} %collective-permute-done.15), channel_id=1, source_target_pairs={{0,4},{4,8},{8,12},{12,14},{14,10},{10,6},{6,2},{2,0},{1,5},{5,9},... | collective-permute-start | bytes 786440 | tf_op jit(solution)/shard_map/ppermute | solution.py:113
  33.2 1.9 %collective-permute-done.22 = bf16[256,512]{1,0:T(8,128)(2,1)S(1)} collective-permute-done((bf16[256,512]{1,0:T(8,128)(2,1)S(1)}, bf16[256,512]{1,0:T(8,128)(2,1)S(1)}, u32[]{:S(2)}, u32[]{:S(2)}) %collective-permute-start.22) | collective-permute-done | bytes 262176 | tf_op jit(solution)/shard_map/ppermute | solution.py:113
  36.7 2.0 %collective-permute-start.3 = (bf16[256,512]{1,0:T(8,128)(2,1)S(1)}, bf16[256,512]{1,0:T(8,128)(2,1)S(1)}, u32[]{:S(2)}, u32[]{:S(2)}) collective-permute-start(bf16[256,512]{1,0:T(8,128)(2,1)S(1)} %collective-permute-done.2), channel_id=1, source_target_pairs={{0,4},{4,8},{8,12},{12,14},{14,10},{10,6},{6,2},{2,0},{1,5},{5,9},... | collective-permute-start | bytes 786440 | tf_op jit(solution)/shard_map/ppermute | solution.py:113
  38.7 2.1 %collective-permute-done.9 = bf16[256,512]{1,0:T(8,128)(2,1)S(1)} collective-permute-done((bf16[256,512]{1,0:T(8,128)(2,1)S(1)}, bf16[256,512]{1,0:T(8,128)(2,1)S(1)}, u32[]{:S(2)}, u32[]{:S(2)}) %collective-permute-start.9) | collective-permute-done | bytes 262176 | tf_op jit(solution)/shard_map/ppermute | solution.py:113
  40.7 1.5 %collective-permute-done.16 = bf16[256,512]{1,0:T(8,128)(2,1)S(1)} collective-permute-done((bf16[256,512]{1,0:T(8,128)(2,1)S(1)}, bf16[256,512]{1,0:T(8,128)(2,1)S(1)}, u32[]{:S(2)}, u32[]{:S(2)}) %collective-permute-start.16) | collective-permute-done | bytes 262176 | tf_op jit(solution)/shard_map/ppermute | solution.py:113
  42.3 2.0 %collective-permute-start.17 = (bf16[256,512]{1,0:T(8,128)(2,1)S(1)}, bf16[256,512]{1,0:T(8,128)(2,1)S(1)}, u32[]{:S(2)}, u32[]{:S(2)}) collective-permute-start(bf16[256,512]{1,0:T(8,128)(2,1)S(1)} %collective-permute-done.16), channel_id=1, source_target_pairs={{0,4},{4,8},{8,12},{12,14},{14,10},{10,6},{6,2},{2,0},{1,5},{5,9},... | collective-permute-start | bytes 786440 | tf_op jit(solution)/shard_map/ppermute | solution.py:113
  44.4 1.9 %collective-permute-done.23 = bf16[256,512]{1,0:T(8,128)(2,1)S(1)} collective-permute-done((bf16[256,512]{1,0:T(8,128)(2,1)S(1)}, bf16[256,512]{1,0:T(8,128)(2,1)S(1)}, u32[]{:S(2)}, u32[]{:S(2)}) %collective-permute-start.23) | collective-permute-done | bytes 262176 | tf_op jit(solution)/shard_map/ppermute | solution.py:113
  47.9 2.0 %collective-permute-start.4 = (bf16[256,512]{1,0:T(8,128)(2,1)S(1)}, bf16[256,512]{1,0:T(8,128)(2,1)S(1)}, u32[]{:S(2)}, u32[]{:S(2)}) collective-permute-start(bf16[256,512]{1,0:T(8,128)(2,1)S(1)} %collective-permute-done.3), channel_id=1, source_target_pairs={{0,4},{4,8},{8,12},{12,14},{14,10},{10,6},{6,2},{2,0},{1,5},{5,9},... | collective-permute-start | bytes 786440 | tf_op jit(solution)/shard_map/ppermute | solution.py:113
  49.9 2.1 %collective-permute-done.10 = bf16[256,512]{1,0:T(8,128)(2,1)S(1)} collective-permute-done((bf16[256,512]{1,0:T(8,128)(2,1)S(1)}, bf16[256,512]{1,0:T(8,128)(2,1)S(1)}, u32[]{:S(2)}, u32[]{:S(2)}) %collective-permute-start.10) | collective-permute-done | bytes 262176 | tf_op jit(solution)/shard_map/ppermute | solution.py:113
  52.0 1.5 %collective-permute-done.17 = bf16[256,512]{1,0:T(8,128)(2,1)S(1)} collective-permute-done((bf16[256,512]{1,0:T(8,128)(2,1)S(1)}, bf16[256,512]{1,0:T(8,128)(2,1)S(1)}, u32[]{:S(2)}, u32[]{:S(2)}) %collective-permute-start.17) | collective-permute-done | bytes 262176 | tf_op jit(solution)/shard_map/ppermute | solution.py:113
  53.5 2.0 %collective-permute-start.18 = (bf16[256,512]{1,0:T(8,128)(2,1)S(1)}, bf16[256,512]{1,0:T(8,128)(2,1)S(1)}, u32[]{:S(2)}, u32[]{:S(2)}) collective-permute-start(bf16[256,512]{1,0:T(8,128)(2,1)S(1)} %collective-permute-done.17), channel_id=1, source_target_pairs={{0,4},{4,8},{8,12},{12,14},{14,10},{10,6},{6,2},{2,0},{1,5},{5,9},... | collective-permute-start | bytes 786440 | tf_op jit(solution)/shard_map/ppermute | solution.py:113
  55.5 2.1 %collective-permute-done.24 = bf16[256,512]{1,0:T(8,128)(2,1)S(1)} collective-permute-done((bf16[256,512]{1,0:T(8,128)(2,1)S(1)}, bf16[256,512]{1,0:T(8,128)(2,1)S(1)}, u32[]{:S(2)}, u32[]{:S(2)}) %collective-permute-start.24) | collective-permute-done | bytes 262176 | tf_op jit(solution)/shard_map/ppermute | solution.py:113
  59.1 2.0 %collective-permute-start.5 = (bf16[256,512]{1,0:T(8,128)(2,1)S(1)}, bf16[256,512]{1,0:T(8,128)(2,1)S(1)}, u32[]{:S(2)}, u32[]{:S(2)}) collective-permute-start(bf16[256,512]{1,0:T(8,128)(2,1)S(1)} %collective-permute-done.4), channel_id=1, source_target_pairs={{0,4},{4,8},{8,12},{12,14},{14,10},{10,6},{6,2},{2,0},{1,5},{5,9},... | collective-permute-start | bytes 786440 | tf_op jit(solution)/shard_map/ppermute | solution.py:113
  61.2 2.1 %collective-permute-done.11 = bf16[256,512]{1,0:T(8,128)(2,1)S(1)} collective-permute-done((bf16[256,512]{1,0:T(8,128)(2,1)S(1)}, bf16[256,512]{1,0:T(8,128)(2,1)S(1)}, u32[]{:S(2)}, u32[]{:S(2)}) %collective-permute-start.11) | collective-permute-done | bytes 262176 | tf_op jit(solution)/shard_map/ppermute | solution.py:113
  63.2 1.5 %collective-permute-done.18 = bf16[256,512]{1,0:T(8,128)(2,1)S(1)} collective-permute-done((bf16[256,512]{1,0:T(8,128)(2,1)S(1)}, bf16[256,512]{1,0:T(8,128)(2,1)S(1)}, u32[]{:S(2)}, u32[]{:S(2)}) %collective-permute-start.18) | collective-permute-done | bytes 262176 | tf_op jit(solution)/shard_map/ppermute | solution.py:113
  64.8 2.0 %collective-permute-start.19 = (bf16[256,512]{1,0:T(8,128)(2,1)S(1)}, bf16[256,512]{1,0:T(8,128)(2,1)S(1)}, u32[]{:S(2)}, u32[]{:S(2)}) collective-permute-start(bf16[256,512]{1,0:T(8,128)(2,1)S(1)} %collective-permute-done.18), channel_id=1, source_target_pairs={{0,4},{4,8},{8,12},{12,14},{14,10},{10,6},{6,2},{2,0},{1,5},{5,9},... | collective-permute-start | bytes 786440 | tf_op jit(solution)/shard_map/ppermute | solution.py:113
  66.8 2.0 %collective-permute-done.25 = bf16[256,512]{1,0:T(8,128)(2,1)S(1)} collective-permute-done((bf16[256,512]{1,0:T(8,128)(2,1)S(1)}, bf16[256,512]{1,0:T(8,128)(2,1)S(1)}, u32[]{:S(2)}, u32[]{:S(2)}) %collective-permute-start.25) | collective-permute-done | bytes 262176 | tf_op jit(solution)/shard_map/ppermute | solution.py:113
  70.4 2.0 %collective-permute-start.6 = (bf16[256,512]{1,0:T(8,128)(2,1)S(1)}, bf16[256,512]{1,0:T(8,128)(2,1)S(1)}, u32[]{:S(2)}, u32[]{:S(2)}) collective-permute-start(bf16[256,512]{1,0:T(8,128)(2,1)S(1)} %collective-permute-done.5), channel_id=1, source_target_pairs={{0,4},{4,8},{8,12},{12,14},{14,10},{10,6},{6,2},{2,0},{1,5},{5,9},... | collective-permute-start | bytes 786440 | tf_op jit(solution)/shard_map/ppermute | solution.py:113
  72.4 2.1 %collective-permute-done.12 = bf16[256,512]{1,0:T(8,128)(2,1)S(1)} collective-permute-done((bf16[256,512]{1,0:T(8,128)(2,1)S(1)}, bf16[256,512]{1,0:T(8,128)(2,1)S(1)}, u32[]{:S(2)}, u32[]{:S(2)}) %collective-permute-start.12) | collective-permute-done | bytes 262176 | tf_op jit(solution)/shard_map/ppermute | solution.py:113
  74.4 1.5 %collective-permute-done.19 = bf16[256,512]{1,0:T(8,128)(2,1)S(1)} collective-permute-done((bf16[256,512]{1,0:T(8,128)(2,1)S(1)}, bf16[256,512]{1,0:T(8,128)(2,1)S(1)}, u32[]{:S(2)}, u32[]{:S(2)}) %collective-permute-start.19) | collective-permute-done | bytes 262176 | tf_op jit(solution)/shard_map/ppermute | solution.py:113
  76.0 2.0 %collective-permute-start.20 = (bf16[256,512]{1,0:T(8,128)(2,1)S(1)}, bf16[256,512]{1,0:T(8,128)(2,1)S(1)}, u32[]{:S(2)}, u32[]{:S(2)}) collective-permute-start(bf16[256,512]{1,0:T(8,128)(2,1)S(1)} %collective-permute-done.19), channel_id=1, source_target_pairs={{0,4},{4,8},{8,12},{12,14},{14,10},{10,6},{6,2},{2,0},{1,5},{5,9},... | collective-permute-start | bytes 786440 | tf_op jit(solution)/shard_map/ppermute | solution.py:113
  78.0 2.0 %collective-permute-done.26 = bf16[256,512]{1,0:T(8,128)(2,1)S(1)} collective-permute-done((bf16[256,512]{1,0:T(8,128)(2,1)S(1)}, bf16[256,512]{1,0:T(8,128)(2,1)S(1)}, u32[]{:S(2)}, u32[]{:S(2)}) %collective-permute-start.26) | collective-permute-done | bytes 262176 | tf_op jit(solution)/shard_map/ppermute | solution.py:113
  81.8 3.1 %collective-permute-done.13 = bf16[256,512]{1,0:T(8,128)(2,1)S(1)} collective-permute-done((bf16[256,512]{1,0:T(8,128)(2,1)S(1)}, bf16[256,512]{1,0:T(8,128)(2,1)S(1)}, u32[]{:S(2)}, u32[]{:S(2)}) %collective-permute-start.13) | collective-permute-done | bytes 262176 | tf_op jit(solution)/shard_map/ppermute | solution.py:113
  85.4 2.3 %collective-permute-done.27 = bf16[256,512]{1,0:T(8,128)(2,1)S(1)} collective-permute-done((bf16[256,512]{1,0:T(8,128)(2,1)S(1)}, bf16[256,512]{1,0:T(8,128)(2,1)S(1)}, u32[]{:S(2)}, u32[]{:S(2)}) %collective-permute-start.27) | collective-permute-done | bytes 262176 | tf_op jit(solution)/shard_map/ppermute | solution.py:113
  88.0 2.5 %fusion.23 = (f32[256,2048]{1,0:T(8,128)}, bf16[256,2048]{1,0:T(8,128)(2,1)S(1)}) fusion(f32[256,512]{1,0:T(8,128)S(1)} %fusion.27, f32[256,512]{1,0:T(8,128)S(1)} %fusion.28, f32[256,512]{1,0:T(8,128)S(1)} %fusion.29, f32[256,512]{1,0:T(8,128)S(1)} %fusion.30, bf16[256,2048]{1,0:T(8,128)(2,1)S(1)} %bitcast.105), kind=kLoop, calls=%fused_computation.55 | loop fusion | flops 12582912 | bytes 6291456 | tf_op jit(solution)/shard_map/add | solution.py:28
  90.5 1.5 %collective-permute-start.28 = (bf16[256,2048]{1,0:T(8,128)(2,1)S(1)}, bf16[256,2048]{1,0:T(8,128)(2,1)S(1)}, u32[]{:S(2)}, u32[]{:S(2)}) collective-permute-start(bf16[256,2048]{1,0:T(8,128)(2,1)S(1)} %get-tuple-element.192), channel_id=1, source_target_pairs={{0,1},{2,3},{4,5},{6,7},{8,9},{10,11},{12,13},{14,15},{16,17},{18,... | collective-permute-start | bytes 3145736 | tf_op jit(solution)/shard_map/ppermute | solution.py:18
  92.4 1.6 %collective-permute-done.28 = bf16[256,2048]{1,0:T(8,128)(2,1)S(1)} collective-permute-done((bf16[256,2048]{1,0:T(8,128)(2,1)S(1)}, bf16[256,2048]{1,0:T(8,128)(2,1)S(1)}, u32[]{:S(2)}, u32[]{:S(2)}) %collective-permute-start.28) | collective-permute-done | bytes 1048608 | tf_op jit(solution)/shard_map/ppermute | solution.py:18
  94.7 5.9 %fusion.26 = (f32[256,2048]{1,0:T(8,128)}, f32[256,2048]{1,0:T(8,128)S(1)}, f32[256,2048]{1,0:T(8,128)}) fusion(bf16[256,2048]{1,0:T(8,128)(2,1)S(1)} %collective-permute-done.28, f32[256]{0:T(256)S(1)} %add_rsqrt_fusion.1, f32[256]{0:T(256)S(1)} %broadcast_multiply_fusion.4, bf16[2048,2048]{1,0:T(8,128)(2,1)S(1)} %constant_dynamic-update-slice_fusion, ...), kind=kOutput, calls=%fused_computation.58 | convolution fusion | flops 2162688000 | bytes 15738880 | tf_op jit(solution)/shard_map/dot_general | solution.py:50
  100.6 1.3 copy-done.5
  103.4 3.5 %collective-permute-done.29 = f32[7]{0:T(128)S(1)} collective-permute-done((f32[7]{0:T(128)S(1)}, f32[7]{0:T(128)S(1)}, u32[]{:S(2)}, u32[]{:S(2)}) %collective-permute-start.29) | collective-permute-done | bytes 60 | tf_op jit(solution)/shard_map/ppermute | solution.py:128
  107.6 1.6 %collective-permute-start.30 = (f32[7]{0:T(128)S(1)}, f32[7]{0:T(128)S(1)}, u32[]{:S(2)}, u32[]{:S(2)}) collective-permute-start(f32[7]{0:T(128)S(1)} %fusion.155), channel_id=1, source_target_pairs={{0,4},{2,6},{4,0},{6,2},{8,12},{10,14},{12,8},{14,10},{1,5},{3,7},... | collective-permute-start | bytes 92 | tf_op jit(solution)/shard_map/ppermute | solution.py:128
  109.2 2.0 %collective-permute-done.30 = f32[7]{0:T(128)S(1)} collective-permute-done((f32[7]{0:T(128)S(1)}, f32[7]{0:T(128)S(1)}, u32[]{:S(2)}, u32[]{:S(2)}) %collective-permute-start.30) | collective-permute-done | bytes 60 | tf_op jit(solution)/shard_map/ppermute | solution.py:128
  111.2 2.6 %collective-permute-start.31 = (f32[7]{0:T(128)S(1)}, f32[7]{0:T(128)S(1)}, u32[]{:S(2)}, u32[]{:S(2)}) collective-permute-start(f32[7]{0:T(128)S(1)} %add.463), channel_id=1, source_target_pairs={{0,8},{2,10},{4,12},{6,14},{8,0},{10,2},{12,4},{14,6},{1,9},{3,11}... | collective-permute-start | bytes 92 | tf_op jit(solution)/shard_map/ppermute | solution.py:128
  113.8 1.9 %collective-permute-done.31 = f32[7]{0:T(128)S(1)} collective-permute-done((f32[7]{0:T(128)S(1)}, f32[7]{0:T(128)S(1)}, u32[]{:S(2)}, u32[]{:S(2)}) %collective-permute-start.31) | collective-permute-done | bytes 60 | tf_op jit(solution)/shard_map/ppermute | solution.py:128
  117.6 1.4 fusion.120
  122.6 1.3 collective-permute-start.33
  123.9 7.1 %collective-permute-done.33 = f32[1]{0:T(128)} collective-permute-done((f32[1]{0:T(128)}, f32[1]{0:T(128)}, u32[]{:S(2)}, u32[]{:S(2)}) %collective-permute-start.33) | collective-permute-done | bytes 36 | tf_op jit(solution)/shard_map/ppermute | solution.py:18
  131.6 8.2 %conditional.3 = (bf16[1,2,128,2048]{3,2,1,0:T(8,128)(2,1)}) conditional(s32[]{:T(128)} %convert_element_type.57, bf16[256,2048]{1,0:T(8,128)(2,1)} %get-tuple-element.202, (bf16[256,2048]{1,0:T(8,128)(2,1)S(1)}, f32[256]{0:T(256)S(1)}, f32[]{:T(128)}, f32[]{:T(128)}, f32[256,2048]{1,0:T(8,128)}, /*index=5*/bf16[2048,2048]{1,0:T(8,128)(2,1)}, ...), branch_computations={%region_15.16_spmd, %region_16.19_spmd} | conditional | flops 2154824192 | bytes 22039568 | solution.py:246
  131.6 6.6 %fusion.115 = (f32[256]{0:T(256)S(1)}, f32[256]{0:T(256)S(1)}, f32[256,2048]{1,0:T(8,128)S(1)}) fusion(f32[256,2048]{1,0:T(8,128)S(1)} %get-tuple-element.67, f32[2048]{0:T(1024)S(1)} %bitcast.117, bf16[2048,2048]{1,0:T(8,128)(2,1)} %get-tuple-element.65, f32[256,2048]{1,0:T(8,128)} %get-tuple-element.64, bf16[256,2048]{1,0:T(8,128)(2,1)S(1)} %get-tuple-element.60), kind=kOutput, calls=%fused_computation.219 | convolution fusion | flops 2151153152 | bytes 15738880 | tf_op jit(solution)/shard_map/cond/branch_1_fun/dot_general | solution.py:57
  138.2 1.6 %fusion.1 = bf16[256,2048]{1,0:T(8,128)(2,1)} fusion(bf16[256,2048]{1,0:T(8,128)(2,1)S(1)} %get-tuple-element.60, f32[256,2048]{1,0:T(8,128)S(1)} %get-tuple-element.67, f32[256,2048]{1,0:T(8,128)S(1)} %get-tuple-element.179, f32[256]{0:T(256)S(1)} %add_rsqrt_fusion, f32[256]{0:T(256)S(1)} %get-tuple-element.180, f32[256]{0:T(256)S(1)} %get-tuple-element.181), kind=kLoop, calls=%fused_computation.5 | loop fusion | flops 3670016 | bytes 6294528 | tf_op jit(solution)/shard_map/cond/branch_1_fun/convert_element_type | solution.py:66
  (139 shorter events, 28.2 us)
Async XLA Ops:
  0.6 7.5 %copy-start.6 = (bf16[128,2048]{1,0:T(8,128)(2,1)S(1)}, bf16[128,2048]{1,0:T(8,128)(2,1)}, u32[]{:S(2)}) copy-start(bf16[128,2048]{1,0:T(8,128)(2,1)} %param.9) | copy-start | bytes 1572868
  0.6 12.3 %copy-start.2 = (bf16[2,128,2048]{2,1,0:T(8,128)(2,1)S(1)}, bf16[2,128,2048]{2,1,0:T(8,128)(2,1)}, u32[]{:S(2)}) copy-start(bf16[2,128,2048]{2,1,0:T(8,128)(2,1)} %param.8) | copy-start | bytes 3145732
  2.8 10.1 %collective-permute-start = (bf16[256,512]{1,0:T(8,128)(2,1)S(1)}, bf16[256,512]{1,0:T(8,128)(2,1)S(1)}, u32[]{:S(2)}, u32[]{:S(2)}) collective-permute-start(bf16[256,512]{1,0:T(8,128)(2,1)S(1)} %get-tuple-element.199), channel_id=1, source_target_pairs={{0,4},{4,8},{8,12},{12,14},{14,10},{10,6},{6,2},{2,0},{1,5},{5,9},... | collective-permute-start | bytes 786440 | tf_op jit(solution)/shard_map/ppermute | solution.py:113
  5.9 13.4 %collective-permute-start.7 = (bf16[256,512]{1,0:T(8,128)(2,1)}, bf16[256,512]{1,0:T(8,128)(2,1)}, u32[]{:S(2)}, u32[]{:S(2)}) collective-permute-start(bf16[256,512]{1,0:T(8,128)(2,1)} %get-tuple-element.198), channel_id=1, source_target_pairs={{4,0},{8,4},{12,8},{14,12},{10,14},{6,10},{2,6},{0,2},{5,1},{9,5},... | collective-permute-start | bytes 786440 | tf_op jit(solution)/shard_map/ppermute | solution.py:113
  5.9 15.7 %collective-permute-start.14 = (bf16[256,512]{1,0:T(8,128)(2,1)}, bf16[256,512]{1,0:T(8,128)(2,1)}, u32[]{:S(2)}, u32[]{:S(2)}) collective-permute-start(bf16[256,512]{1,0:T(8,128)(2,1)} %get-tuple-element.197), channel_id=1, source_target_pairs={{0,4},{4,8},{8,12},{12,14},{14,10},{10,6},{6,2},{2,0},{1,5},{5,9},... | collective-permute-start | bytes 786440 | tf_op jit(solution)/shard_map/ppermute | solution.py:113
  7.9 18.0 %collective-permute-start.21 = (bf16[256,512]{1,0:T(8,128)(2,1)}, bf16[256,512]{1,0:T(8,128)(2,1)S(1)}, u32[]{:S(2)}, u32[]{:S(2)}) collective-permute-start(bf16[256,512]{1,0:T(8,128)(2,1)} %get-tuple-element.196), channel_id=1, source_target_pairs={{4,0},{8,4},{12,8},{14,12},{10,14},{6,10},{2,6},{0,2},{5,1},{9,5},... | collective-permute-start | bytes 786440 | tf_op jit(solution)/shard_map/ppermute | solution.py:113
  8.1 5.6 %copy-start.11 = (f32[1,2048]{1,0:T(1,128)S(1)}, f32[1,2048]{1,0:T(1,128)}, u32[]{:S(2)}) copy-start(f32[1,2048]{1,0:T(1,128)} %param.11) | copy-start | bytes 24580
  13.0 0.7 copy-start.9
  13.7 1.2 copy-start.4
  14.1 1.7 %copy-start.10 = (bf16[256,512]{1,0:T(8,128)(2,1)S(1)}, bf16[256,512]{1,0:T(8,128)(2,1)}, u32[]{:S(2)}) copy-start(bf16[256,512]{1,0:T(8,128)(2,1)} %copy-done.9) | copy-start | bytes 786436
  15.8 10.4 %collective-permute-start.1 = (bf16[256,512]{1,0:T(8,128)(2,1)S(1)}, bf16[256,512]{1,0:T(8,128)(2,1)S(1)}, u32[]{:S(2)}, u32[]{:S(2)}) collective-permute-start(bf16[256,512]{1,0:T(8,128)(2,1)S(1)} %copy-done.10), channel_id=1, source_target_pairs={{0,4},{4,8},{8,12},{12,14},{14,10},{10,6},{6,2},{2,0},{1,5},{5,9},... | collective-permute-start | bytes 786440 | tf_op jit(solution)/shard_map/ppermute | solution.py:113
  19.3 9.0 %collective-permute-start.8 = (bf16[256,512]{1,0:T(8,128)(2,1)}, bf16[256,512]{1,0:T(8,128)(2,1)S(1)}, u32[]{:S(2)}, u32[]{:S(2)}) collective-permute-start(bf16[256,512]{1,0:T(8,128)(2,1)} %collective-permute-done.7), channel_id=1, source_target_pairs={{4,0},{8,4},{12,8},{14,12},{10,14},{6,10},{2,6},{0,2},{5,1},{9,5},... | collective-permute-start | bytes 786440 | tf_op jit(solution)/shard_map/ppermute | solution.py:113
  21.6 9.4 %collective-permute-start.15 = (bf16[256,512]{1,0:T(8,128)(2,1)}, bf16[256,512]{1,0:T(8,128)(2,1)S(1)}, u32[]{:S(2)}, u32[]{:S(2)}) collective-permute-start(bf16[256,512]{1,0:T(8,128)(2,1)} %collective-permute-done.14), channel_id=1, source_target_pairs={{0,4},{4,8},{8,12},{12,14},{14,10},{10,6},{6,2},{2,0},{1,5},{5,9},... | collective-permute-start | bytes 786440 | tf_op jit(solution)/shard_map/ppermute | solution.py:113
  25.9 9.2 %collective-permute-start.22 = (bf16[256,512]{1,0:T(8,128)(2,1)S(1)}, bf16[256,512]{1,0:T(8,128)(2,1)S(1)}, u32[]{:S(2)}, u32[]{:S(2)}) collective-permute-start(bf16[256,512]{1,0:T(8,128)(2,1)S(1)} %collective-permute-done.21), channel_id=1, source_target_pairs={{4,0},{8,4},{12,8},{14,12},{10,14},{6,10},{2,6},{0,2},{5,1},{9,5},... | collective-permute-start | bytes 786440 | tf_op jit(solution)/shard_map/ppermute | solution.py:113
  26.2 10.4 %collective-permute-start.2 = (bf16[256,512]{1,0:T(8,128)(2,1)S(1)}, bf16[256,512]{1,0:T(8,128)(2,1)S(1)}, u32[]{:S(2)}, u32[]{:S(2)}) collective-permute-start(bf16[256,512]{1,0:T(8,128)(2,1)S(1)} %collective-permute-done.1), channel_id=1, source_target_pairs={{0,4},{4,8},{8,12},{12,14},{14,10},{10,6},{6,2},{2,0},{1,5},{5,9},... | collective-permute-start | bytes 786440 | tf_op jit(solution)/shard_map/ppermute | solution.py:113
  28.3 12.4 %collective-permute-start.9 = (bf16[256,512]{1,0:T(8,128)(2,1)S(1)}, bf16[256,512]{1,0:T(8,128)(2,1)S(1)}, u32[]{:S(2)}, u32[]{:S(2)}) collective-permute-start(bf16[256,512]{1,0:T(8,128)(2,1)S(1)} %collective-permute-done.8), channel_id=1, source_target_pairs={{4,0},{8,4},{12,8},{14,12},{10,14},{6,10},{2,6},{0,2},{5,1},{9,5},... | collective-permute-start | bytes 786440 | tf_op jit(solution)/shard_map/ppermute | solution.py:113
  31.0 11.2 %collective-permute-start.16 = (bf16[256,512]{1,0:T(8,128)(2,1)S(1)}, bf16[256,512]{1,0:T(8,128)(2,1)S(1)}, u32[]{:S(2)}, u32[]{:S(2)}) collective-permute-start(bf16[256,512]{1,0:T(8,128)(2,1)S(1)} %collective-permute-done.15), channel_id=1, source_target_pairs={{0,4},{4,8},{8,12},{12,14},{14,10},{10,6},{6,2},{2,0},{1,5},{5,9},... | collective-permute-start | bytes 786440 | tf_op jit(solution)/shard_map/ppermute | solution.py:113
  35.1 11.2 %collective-permute-start.23 = (bf16[256,512]{1,0:T(8,128)(2,1)S(1)}, bf16[256,512]{1,0:T(8,128)(2,1)S(1)}, u32[]{:S(2)}, u32[]{:S(2)}) collective-permute-start(bf16[256,512]{1,0:T(8,128)(2,1)S(1)} %collective-permute-done.22), channel_id=1, source_target_pairs={{4,0},{8,4},{12,8},{14,12},{10,14},{6,10},{2,6},{0,2},{5,1},{9,5},... | collective-permute-start | bytes 786440 | tf_op jit(solution)/shard_map/ppermute | solution.py:113
  36.7 11.2 %collective-permute-start.3 = (bf16[256,512]{1,0:T(8,128)(2,1)S(1)}, bf16[256,512]{1,0:T(8,128)(2,1)S(1)}, u32[]{:S(2)}, u32[]{:S(2)}) collective-permute-start(bf16[256,512]{1,0:T(8,128)(2,1)S(1)} %collective-permute-done.2), channel_id=1, source_target_pairs={{0,4},{4,8},{8,12},{12,14},{14,10},{10,6},{6,2},{2,0},{1,5},{5,9},... | collective-permute-start | bytes 786440 | tf_op jit(solution)/shard_map/ppermute | solution.py:113
  40.7 11.2 %collective-permute-start.10 = (bf16[256,512]{1,0:T(8,128)(2,1)S(1)}, bf16[256,512]{1,0:T(8,128)(2,1)S(1)}, u32[]{:S(2)}, u32[]{:S(2)}) collective-permute-start(bf16[256,512]{1,0:T(8,128)(2,1)S(1)} %collective-permute-done.9), channel_id=1, source_target_pairs={{4,0},{8,4},{12,8},{14,12},{10,14},{6,10},{2,6},{0,2},{5,1},{9,5},... | collective-permute-start | bytes 786440 | tf_op jit(solution)/shard_map/ppermute | solution.py:113
  42.3 11.2 %collective-permute-start.17 = (bf16[256,512]{1,0:T(8,128)(2,1)S(1)}, bf16[256,512]{1,0:T(8,128)(2,1)S(1)}, u32[]{:S(2)}, u32[]{:S(2)}) collective-permute-start(bf16[256,512]{1,0:T(8,128)(2,1)S(1)} %collective-permute-done.16), channel_id=1, source_target_pairs={{0,4},{4,8},{8,12},{12,14},{14,10},{10,6},{6,2},{2,0},{1,5},{5,9},... | collective-permute-start | bytes 786440 | tf_op jit(solution)/shard_map/ppermute | solution.py:113
  46.4 11.2 %collective-permute-start.24 = (bf16[256,512]{1,0:T(8,128)(2,1)S(1)}, bf16[256,512]{1,0:T(8,128)(2,1)S(1)}, u32[]{:S(2)}, u32[]{:S(2)}) collective-permute-start(bf16[256,512]{1,0:T(8,128)(2,1)S(1)} %collective-permute-done.23), channel_id=1, source_target_pairs={{4,0},{8,4},{12,8},{14,12},{10,14},{6,10},{2,6},{0,2},{5,1},{9,5},... | collective-permute-start | bytes 786440 | tf_op jit(solution)/shard_map/ppermute | solution.py:113
  47.9 11.2 %collective-permute-start.4 = (bf16[256,512]{1,0:T(8,128)(2,1)S(1)}, bf16[256,512]{1,0:T(8,128)(2,1)S(1)}, u32[]{:S(2)}, u32[]{:S(2)}) collective-permute-start(bf16[256,512]{1,0:T(8,128)(2,1)S(1)} %collective-permute-done.3), channel_id=1, source_target_pairs={{0,4},{4,8},{8,12},{12,14},{14,10},{10,6},{6,2},{2,0},{1,5},{5,9},... | collective-permute-start | bytes 786440 | tf_op jit(solution)/shard_map/ppermute | solution.py:113
  52.0 11.2 %collective-permute-start.11 = (bf16[256,512]{1,0:T(8,128)(2,1)S(1)}, bf16[256,512]{1,0:T(8,128)(2,1)S(1)}, u32[]{:S(2)}, u32[]{:S(2)}) collective-permute-start(bf16[256,512]{1,0:T(8,128)(2,1)S(1)} %collective-permute-done.10), channel_id=1, source_target_pairs={{4,0},{8,4},{12,8},{14,12},{10,14},{6,10},{2,6},{0,2},{5,1},{9,5},... | collective-permute-start | bytes 786440 | tf_op jit(solution)/shard_map/ppermute | solution.py:113
  53.5 11.2 %collective-permute-start.18 = (bf16[256,512]{1,0:T(8,128)(2,1)S(1)}, bf16[256,512]{1,0:T(8,128)(2,1)S(1)}, u32[]{:S(2)}, u32[]{:S(2)}) collective-permute-start(bf16[256,512]{1,0:T(8,128)(2,1)S(1)} %collective-permute-done.17), channel_id=1, source_target_pairs={{0,4},{4,8},{8,12},{12,14},{14,10},{10,6},{6,2},{2,0},{1,5},{5,9},... | collective-permute-start | bytes 786440 | tf_op jit(solution)/shard_map/ppermute | solution.py:113
  57.6 11.2 %collective-permute-start.25 = (bf16[256,512]{1,0:T(8,128)(2,1)S(1)}, bf16[256,512]{1,0:T(8,128)(2,1)S(1)}, u32[]{:S(2)}, u32[]{:S(2)}) collective-permute-start(bf16[256,512]{1,0:T(8,128)(2,1)S(1)} %collective-permute-done.24), channel_id=1, source_target_pairs={{4,0},{8,4},{12,8},{14,12},{10,14},{6,10},{2,6},{0,2},{5,1},{9,5},... | collective-permute-start | bytes 786440 | tf_op jit(solution)/shard_map/ppermute | solution.py:113
  59.1 11.2 %collective-permute-start.5 = (bf16[256,512]{1,0:T(8,128)(2,1)S(1)}, bf16[256,512]{1,0:T(8,128)(2,1)S(1)}, u32[]{:S(2)}, u32[]{:S(2)}) collective-permute-start(bf16[256,512]{1,0:T(8,128)(2,1)S(1)} %collective-permute-done.4), channel_id=1, source_target_pairs={{0,4},{4,8},{8,12},{12,14},{14,10},{10,6},{6,2},{2,0},{1,5},{5,9},... | collective-permute-start | bytes 786440 | tf_op jit(solution)/shard_map/ppermute | solution.py:113
  63.2 11.2 %collective-permute-start.12 = (bf16[256,512]{1,0:T(8,128)(2,1)S(1)}, bf16[256,512]{1,0:T(8,128)(2,1)S(1)}, u32[]{:S(2)}, u32[]{:S(2)}) collective-permute-start(bf16[256,512]{1,0:T(8,128)(2,1)S(1)} %collective-permute-done.11), channel_id=1, source_target_pairs={{4,0},{8,4},{12,8},{14,12},{10,14},{6,10},{2,6},{0,2},{5,1},{9,5},... | collective-permute-start | bytes 786440 | tf_op jit(solution)/shard_map/ppermute | solution.py:113
  64.8 11.2 %collective-permute-start.19 = (bf16[256,512]{1,0:T(8,128)(2,1)S(1)}, bf16[256,512]{1,0:T(8,128)(2,1)S(1)}, u32[]{:S(2)}, u32[]{:S(2)}) collective-permute-start(bf16[256,512]{1,0:T(8,128)(2,1)S(1)} %collective-permute-done.18), channel_id=1, source_target_pairs={{0,4},{4,8},{8,12},{12,14},{14,10},{10,6},{6,2},{2,0},{1,5},{5,9},... | collective-permute-start | bytes 786440 | tf_op jit(solution)/shard_map/ppermute | solution.py:113
  68.8 11.2 %collective-permute-start.26 = (bf16[256,512]{1,0:T(8,128)(2,1)S(1)}, bf16[256,512]{1,0:T(8,128)(2,1)S(1)}, u32[]{:S(2)}, u32[]{:S(2)}) collective-permute-start(bf16[256,512]{1,0:T(8,128)(2,1)S(1)} %collective-permute-done.25), channel_id=1, source_target_pairs={{4,0},{8,4},{12,8},{14,12},{10,14},{6,10},{2,6},{0,2},{5,1},{9,5},... | collective-permute-start | bytes 786440 | tf_op jit(solution)/shard_map/ppermute | solution.py:113
  70.4 11.2 %collective-permute-start.6 = (bf16[256,512]{1,0:T(8,128)(2,1)S(1)}, bf16[256,512]{1,0:T(8,128)(2,1)S(1)}, u32[]{:S(2)}, u32[]{:S(2)}) collective-permute-start(bf16[256,512]{1,0:T(8,128)(2,1)S(1)} %collective-permute-done.5), channel_id=1, source_target_pairs={{0,4},{4,8},{8,12},{12,14},{14,10},{10,6},{6,2},{2,0},{1,5},{5,9},... | collective-permute-start | bytes 786440 | tf_op jit(solution)/shard_map/ppermute | solution.py:113
  74.4 10.5 %collective-permute-start.13 = (bf16[256,512]{1,0:T(8,128)(2,1)S(1)}, bf16[256,512]{1,0:T(8,128)(2,1)S(1)}, u32[]{:S(2)}, u32[]{:S(2)}) collective-permute-start(bf16[256,512]{1,0:T(8,128)(2,1)S(1)} %collective-permute-done.12), channel_id=1, source_target_pairs={{4,0},{8,4},{12,8},{14,12},{10,14},{6,10},{2,6},{0,2},{5,1},{9,5},... | collective-permute-start | bytes 786440 | tf_op jit(solution)/shard_map/ppermute | solution.py:113
  76.0 9.2 %collective-permute-start.20 = (bf16[256,512]{1,0:T(8,128)(2,1)S(1)}, bf16[256,512]{1,0:T(8,128)(2,1)S(1)}, u32[]{:S(2)}, u32[]{:S(2)}) collective-permute-start(bf16[256,512]{1,0:T(8,128)(2,1)S(1)} %collective-permute-done.19), channel_id=1, source_target_pairs={{0,4},{4,8},{8,12},{12,14},{14,10},{10,6},{6,2},{2,0},{1,5},{5,9},... | collective-permute-start | bytes 786440 | tf_op jit(solution)/shard_map/ppermute | solution.py:113
  80.1 7.7 %collective-permute-start.27 = (bf16[256,512]{1,0:T(8,128)(2,1)S(1)}, bf16[256,512]{1,0:T(8,128)(2,1)S(1)}, u32[]{:S(2)}, u32[]{:S(2)}) collective-permute-start(bf16[256,512]{1,0:T(8,128)(2,1)S(1)} %collective-permute-done.26), channel_id=1, source_target_pairs={{4,0},{8,4},{12,8},{14,12},{10,14},{6,10},{2,6},{0,2},{5,1},{9,5},... | collective-permute-start | bytes 786440 | tf_op jit(solution)/shard_map/ppermute | solution.py:113
  90.5 3.6 %collective-permute-start.28 = (bf16[256,2048]{1,0:T(8,128)(2,1)S(1)}, bf16[256,2048]{1,0:T(8,128)(2,1)S(1)}, u32[]{:S(2)}, u32[]{:S(2)}) collective-permute-start(bf16[256,2048]{1,0:T(8,128)(2,1)S(1)} %get-tuple-element.192), channel_id=1, source_target_pairs={{0,1},{2,3},{4,5},{6,7},{8,9},{10,11},{12,13},{14,15},{16,17},{18,... | collective-permute-start | bytes 3145736 | tf_op jit(solution)/shard_map/ppermute | solution.py:18
  92.4 8.2 %copy-start = (bf16[2048,2048]{1,0:T(8,128)(2,1)}, bf16[2048,2048]{1,0:T(8,128)(2,1)S(1)}, u32[]{:S(2)}) copy-start(bf16[2048,2048]{1,0:T(8,128)(2,1)S(1)} %constant_dynamic-update-slice_fusion) | copy-start | bytes 25165828
  94.7 7.2 %copy-start.7 = (bf16[128,2048]{1,0:T(8,128)(2,1)S(1)}, bf16[128,2048]{1,0:T(8,128)(2,1)}, u32[]{:S(2)}) copy-start(bf16[128,2048]{1,0:T(8,128)(2,1)} %param.9) | copy-start | bytes 1572868
  100.6 1.3 copy-start.5
  100.6 18.4 %copy-start.3 = (f32[128,2048]{1,0:T(8,128)S(1)}, f32[128,2048]{1,0:T(8,128)}, u32[]{:S(2)}) copy-start(f32[128,2048]{1,0:T(8,128)} %convert_element_type.65) | copy-start | bytes 3145732
  103.3 3.6 %collective-permute-start.29 = (f32[7]{0:T(128)S(1)}, f32[7]{0:T(128)S(1)}, u32[]{:S(2)}, u32[]{:S(2)}) collective-permute-start(f32[7]{0:T(128)S(1)} %pad_maximum_fusion.1), channel_id=1, source_target_pairs={{0,2},{2,0},{4,6},{6,4},{8,10},{10,8},{12,14},{14,12},{1,3},{3,1},... | collective-permute-start | bytes 92 | tf_op jit(solution)/shard_map/ppermute | solution.py:128
  107.6 3.6 %collective-permute-start.30 = (f32[7]{0:T(128)S(1)}, f32[7]{0:T(128)S(1)}, u32[]{:S(2)}, u32[]{:S(2)}) collective-permute-start(f32[7]{0:T(128)S(1)} %fusion.155), channel_id=1, source_target_pairs={{0,4},{2,6},{4,0},{6,2},{8,12},{10,14},{12,8},{14,10},{1,5},{3,7},... | collective-permute-start | bytes 92 | tf_op jit(solution)/shard_map/ppermute | solution.py:128
  111.2 4.5 %collective-permute-start.31 = (f32[7]{0:T(128)S(1)}, f32[7]{0:T(128)S(1)}, u32[]{:S(2)}, u32[]{:S(2)}) collective-permute-start(f32[7]{0:T(128)S(1)} %add.463), channel_id=1, source_target_pairs={{0,8},{2,10},{4,12},{6,14},{8,0},{10,2},{12,4},{14,6},{1,9},{3,11}... | collective-permute-start | bytes 92 | tf_op jit(solution)/shard_map/ppermute | solution.py:128
  120.1 11.4 %collective-permute-start.32 = (bf16[256,2048]{1,0:T(8,128)(2,1)}, bf16[256,2048]{1,0:T(8,128)(2,1)S(1)}, u32[]{:S(2)}, u32[]{:S(2)}) collective-permute-start(bf16[256,2048]{1,0:T(8,128)(2,1)} %get-tuple-element.202), channel_id=1, source_target_pairs={{1,0},{3,2},{5,4},{7,6},{9,8},{11,10},{13,12},{15,14},{17,16},{19,... | collective-permute-start | bytes 3145736 | tf_op jit(solution)/shard_map/ppermute | solution.py:18
  122.6 8.4 %collective-permute-start.33 = (f32[1]{0:T(128)}, f32[1]{0:T(128)}, u32[]{:S(2)}, u32[]{:S(2)}) collective-permute-start(f32[1]{0:T(128)} %bitcast.17), channel_id=1, source_target_pairs={{1,0},{3,2},{5,4},{7,6},{9,8},{11,10},{13,12},{15,14},{17,16},{19,... | collective-permute-start | bytes 20 | tf_op jit(solution)/shard_map/ppermute | solution.py:18

commit v13 on v10

--- a/solution.py
+++ b/solution.py
@@ -4,6 +4,7 @@
 import jax.numpy as jnp
 from jax import lax
 from jax.sharding import PartitionSpec as P
+
 
 epsilon = 1e-05
 gelu_scale = math.sqrt(2.0 / math.pi)
@@ -130,38 +131,7 @@
     return v
 
 
-def packed_score(packed, count, size):
-    gram = [[packed[m * count + k] for k in range(count)] for m in range(count)]
-    member_obs = [packed[count * count + m] for m in range(count)]
-    obs_sq = packed[count * count + count]
-    diag = [gram[m][m] for m in range(count)]
-    to_obs = [jnp.sqrt((diag[m] - 2.0 * member_obs[m] + obs_sq) / size + epsilon) for m in range(count)]
-    pair = [[None] * count for _ in range(count)]
-    pair_total = 0.0
-    for m in range(count):
-        for k in range(count):
-            if m != k:
-                pair[m][k] = jnp.sqrt((diag[m] + diag[k] - 2.0 * gram[m][k]) / size + epsilon)
-                pair_total = pair_total + pair[m][k]
-    energy = sum(to_obs) / count - pair_total / (2.0 * count * (count - 1))
-    obs_coeff = [1.0 / (count * to_obs[m]) for m in range(count)]
-    rows = []
-    for m in range(count):
-        row = []
-        off = 0.0
-        for k in range(count):
-            if m != k:
-                c = 1.0 / (count * (count - 1) * pair[m][k])
-                off = off + c
-                row.append(c)
-            else:
-                row.append(None)
-        row[m] = obs_coeff[m] - off
-        rows.append(jnp.stack(row))
-    return (energy, jnp.stack(rows), -jnp.stack(obs_coeff))
-
-
-def per_device(inputs, obs, weights, gains):
+def device_body(inputs, obs, weights, gains):
     sec = lax.axis_index("section")
     on_first = sec == 0
     gain = gains[0]
@@ -182,25 +152,20 @@
 
     if overlap:
         acc = [None] * (2 * pieces)
-        normed = []
+        me = lax.axis_index("tok")
+        values_a, unit_a, std_a, normed_a = norm_part(rows_all, gain)
+        lhs = lax.dynamic_slice(normed_a, (0, me * rows_w), (normed_a.shape[0], rows_w))
+        for j in range(2 * pieces):
+            acc[j] = jnp.dot(
+                lhs, local[:, j * piece_w:(j + 1) * piece_w], preferred_element_type=jnp.float32
+            )
 
         def on_piece(origin, j, piece):
-            if not normed:
-                rows_in, piece = lax.optimization_barrier((rows_all, piece))
-                normed.append(norm_part(rows_in, gain))
-            normed_a = normed[0][3]
             lhs = lax.dynamic_slice(normed_a, (0, origin * rows_w), (normed_a.shape[0], rows_w))
             term = jnp.dot(lhs, piece, preferred_element_type=jnp.float32)
             acc[j] = term if acc[j] is None else acc[j] + term
 
         weight = ring_gather(local, "tok", pieces, on_piece)
-        values_a, unit_a, std_a, normed_a = normed[0]
-        me = lax.axis_index("tok")
-        lhs = lax.dynamic_slice(normed_a, (0, me * rows_w), (normed_a.shape[0], rows_w))
-        for j in range(2 * pieces):
-            acc[j] = acc[j] + jnp.dot(
-                lhs, local[:, j * piece_w:(j + 1) * piece_w], preferred_element_type=jnp.float32
-            )
         pre_a = jnp.concatenate(acc, axis=1)
         out_a = (values_a + gelu_value(pre_a)).astype(jnp.bfloat16)
         fa = (out_a, unit_a, std_a, pre_a)
@@ -261,5 +226,5 @@
     )
     out_specs = (P("section", "groups", "tok", None), P("groups"))
     return jax.shard_map(
-        per_device, mesh=mesh, in_specs=in_specs, out_specs=out_specs, check_vma=False
-    )
+        device_body, mesh=mesh, in_specs=in_specs, out_specs=out_specs, check_vma=False
+    )

time: 141 us -> 142 us (level)
  waiting for transfers between devices: 54.8 us -> 48.8 us
  matrix products: 21.9 us -> 26.1 us
  other arithmetic: 11.8 us -> 14.4 us
    ppermute x28, waiting for transfers between devices: 38.2 us -> 32.1 us  [ring_gather(): parts[j] = lax.ppermute(parts[j], axis, cw if clockwise else ccw)]
    dot_general x4, matrix products: 0.9 us -> 4.26 us  [device_body(): jnp.dot(lhs, local[:, j * piece_w:(j + 1) * piece_w], preferred_element_t...]
  transfers between devices with their start and end apart: 34 -> 34, of which waited for: 27 -> 17; matrix products, arithmetic and copies ran while one was open for 11% -> 17% of each run, Pallas kernels for 0% -> 0%
where the time goes in v13:
time: 142 us
  waiting for transfers between devices  48.8 us (34%)
  starting transfers between devices  38.6 us (27%)
  matrix products  26.1 us (18%)
  other arithmetic  14.4 us (10%)
  local copies, waits for them, and re-layouts  9.62 us (7%)
  between operations  4.42 us (3%)
    ppermute x28, waiting for transfers between devices, ring_gather(): parts[j] = lax.ppermute(parts[j], axis, cw if clockwise else ccw)  32.1 us
    ppermute x28, starting transfers between devices, ring_gather(): parts[j] = lax.ppermute(parts[j], axis, cw if clockwise else ccw)  29.8 us
    ppermute x3, waiting for transfers between devices, shifted(): return lax.ppermute(x, axis, pairs)  9.63 us
    dot_general x28, matrix products, on_piece(): term = jnp.dot(lhs, piece, preferred_element_type=jnp.float32)  9.23 us
    ppermute x3, waiting for transfers between devices, tree_sum(): v = v + lax.ppermute(v, axis, [(i, i ^ b) for i in range(n)])  7.1 us
    dot_general x1, matrix products, section_backward(): lax.dot_general(grad_pre, weight, (((1,), (1,)), ((), ())), preferred_ele...  6.58 us
    dot_general x1, matrix products, section_forward(): pre_act = jnp.dot(normed, weight, preferred_element_type=jnp.float32)  6.04 us
    ppermute x3, starting transfers between devices, tree_sum(): v = v + lax.ppermute(v, axis, [(i, i ^ b) for i in range(n)])  4.51 us
  transfers between devices with their start and end apart: 34, of which 17 were waited for; matrix products, arithmetic and copies ran while one was open for 17% of the time, Pallas kernels for 0%

profile of v13, /device:TPU:0, one launch (start us, length us, event | category | flops | bytes accessed | tf_op | source)
XLA Modules:
  0.0 141.9 jit_solution(8962239881345723497)
XLA Ops:
  0.7 2.3 %fusion.114 = (bf16[256,512]{1,0:T(8,128)(2,1)}, bf16[256,512]{1,0:T(8,128)(2,1)}, bf16[256,512]{1,0:T(8,128)(2,1)}, bf16[256,512]{1,0:T(8,128)(2,1)}) fusion(bf16[256,2048]{1,0:T(8,128)(2,1)} %bitcast.140), kind=kLoop, calls=%fused_computation.226 | loop fusion | bytes 2097152 | tf_op jit(solution)/shard_map/slice | solution.py:160
  2.9 3.1 %collective-permute-start = (bf16[256,512]{1,0:T(8,128)(2,1)}, bf16[256,512]{1,0:T(8,128)(2,1)}, u32[]{:S(2)}, u32[]{:S(2)}) collective-permute-start(bf16[256,512]{1,0:T(8,128)(2,1)} %get-tuple-element.195), channel_id=1, source_target_pairs={{0,4},{4,8},{8,12},{12,14},{14,10},{10,6},{6,2},{2,0},{1,5},{5,9},... | collective-permute-start | bytes 786440 | tf_op jit(solution)/shard_map/ppermute | solution.py:114
  6.0 2.0 %collective-permute-start.14 = (bf16[256,512]{1,0:T(8,128)(2,1)}, bf16[256,512]{1,0:T(8,128)(2,1)}, u32[]{:S(2)}, u32[]{:S(2)}) collective-permute-start(bf16[256,512]{1,0:T(8,128)(2,1)} %get-tuple-element.193), channel_id=1, source_target_pairs={{0,4},{4,8},{8,12},{12,14},{14,10},{10,6},{6,2},{2,0},{1,5},{5,9},... | collective-permute-start | bytes 786440 | tf_op jit(solution)/shard_map/ppermute | solution.py:114
  8.7 1.7 %fusion.25 = (f32[256,2048]{1,0:T(8,128)S(1)}, bf16[256,2048]{1,0:T(8,128)(2,1)S(1)}) fusion(bf16[2,128,2048]{2,1,0:T(8,128)(2,1)} %param.8, f32[256]{0:T(256)S(1)} %rsqrt_bitcast_fusion.1, f32[256]{0:T(256)S(1)} %get-tuple-element.196, f32[2048]{0:T(1024)S(1)} %bitcast.149), kind=kLoop, calls=%fused_computation.61 | loop fusion | flops 2621440 | bytes 4204544 | tf_op jit(solution)/shard_map/mul | solution.py:39
  14.5 2.1 %convert_element_type.75 = f32[128,2048]{1,0:T(8,128)} convert(bf16[128,2048]{1,0:T(8,128)(2,1)} %param.9) | non-fusion elementwise | flops 262144 | bytes 1572864 | tf_op jit(solution)/shard_map/convert_element_type | solution.py:184
  16.6 1.2 fusion.58
  17.8 2.1 %collective-permute-start.1 = (bf16[256,512]{1,0:T(8,128)(2,1)}, bf16[256,512]{1,0:T(8,128)(2,1)S(1)}, u32[]{:S(2)}, u32[]{:S(2)}) collective-permute-start(bf16[256,512]{1,0:T(8,128)(2,1)} %collective-permute-done), channel_id=1, source_target_pairs={{0,4},{4,8},{8,12},{12,14},{14,10},{10,6},{6,2},{2,0},{1,5},{5,9},... | collective-permute-start | bytes 786440 | tf_op jit(solution)/shard_map/ppermute | solution.py:114
  19.9 2.0 %collective-permute-start.15 = (bf16[256,512]{1,0:T(8,128)(2,1)}, bf16[256,512]{1,0:T(8,128)(2,1)S(1)}, u32[]{:S(2)}, u32[]{:S(2)}) collective-permute-start(bf16[256,512]{1,0:T(8,128)(2,1)} %collective-permute-done.14), channel_id=1, source_target_pairs={{0,4},{4,8},{8,12},{12,14},{14,10},{10,6},{6,2},{2,0},{1,5},{5,9},... | collective-permute-start | bytes 786440 | tf_op jit(solution)/shard_map/ppermute | solution.py:114
  26.2 1.2 convolution_add_fusion.27
  27.4 1.2 convolution_add_fusion.20
  28.6 1.2 convolution_add_fusion.13
  30.0 2.0 %collective-permute-start.2 = (bf16[256,512]{1,0:T(8,128)(2,1)S(1)}, bf16[256,512]{1,0:T(8,128)(2,1)S(1)}, u32[]{:S(2)}, u32[]{:S(2)}) collective-permute-start(bf16[256,512]{1,0:T(8,128)(2,1)S(1)} %collective-permute-done.1), channel_id=1, source_target_pairs={{0,4},{4,8},{8,12},{12,14},{14,10},{10,6},{6,2},{2,0},{1,5},{5,9},... | collective-permute-start | bytes 786440 | tf_op jit(solution)/shard_map/ppermute | solution.py:114
  32.1 2.0 %collective-permute-start.16 = (bf16[256,512]{1,0:T(8,128)(2,1)S(1)}, bf16[256,512]{1,0:T(8,128)(2,1)S(1)}, u32[]{:S(2)}, u32[]{:S(2)}) collective-permute-start(bf16[256,512]{1,0:T(8,128)(2,1)S(1)} %collective-permute-done.15), channel_id=1, source_target_pairs={{0,4},{4,8},{8,12},{12,14},{14,10},{10,6},{6,2},{2,0},{1,5},{5,9},... | collective-permute-start | bytes 786440 | tf_op jit(solution)/shard_map/ppermute | solution.py:114
  35.3 4.0 %collective-permute-done.2 = bf16[256,512]{1,0:T(8,128)(2,1)S(1)} collective-permute-done((bf16[256,512]{1,0:T(8,128)(2,1)S(1)}, bf16[256,512]{1,0:T(8,128)(2,1)S(1)}, u32[]{:S(2)}, u32[]{:S(2)}) %collective-permute-start.2) | collective-permute-done | bytes 262176 | tf_op jit(solution)/shard_map/ppermute | solution.py:114
  39.3 2.0 %collective-permute-start.3 = (bf16[256,512]{1,0:T(8,128)(2,1)S(1)}, bf16[256,512]{1,0:T(8,128)(2,1)S(1)}, u32[]{:S(2)}, u32[]{:S(2)}) collective-permute-start(bf16[256,512]{1,0:T(8,128)(2,1)S(1)} %collective-permute-done.2), channel_id=1, source_target_pairs={{0,4},{4,8},{8,12},{12,14},{14,10},{10,6},{6,2},{2,0},{1,5},{5,9},... | collective-permute-start | bytes 786440 | tf_op jit(solution)/shard_map/ppermute | solution.py:114
  41.3 3.6 %collective-permute-done.16 = bf16[256,512]{1,0:T(8,128)(2,1)S(1)} collective-permute-done((bf16[256,512]{1,0:T(8,128)(2,1)S(1)}, bf16[256,512]{1,0:T(8,128)(2,1)S(1)}, u32[]{:S(2)}, u32[]{:S(2)}) %collective-permute-start.16) | collective-permute-done | bytes 262176 | tf_op jit(solution)/shard_map/ppermute | solution.py:114
  44.9 2.0 %collective-permute-start.17 = (bf16[256,512]{1,0:T(8,128)(2,1)S(1)}, bf16[256,512]{1,0:T(8,128)(2,1)S(1)}, u32[]{:S(2)}, u32[]{:S(2)}) collective-permute-start(bf16[256,512]{1,0:T(8,128)(2,1)S(1)} %collective-permute-done.16), channel_id=1, source_target_pairs={{0,4},{4,8},{8,12},{12,14},{14,10},{10,6},{6,2},{2,0},{1,5},{5,9},... | collective-permute-start | bytes 786440 | tf_op jit(solution)/shard_map/ppermute | solution.py:114
  48.0 2.5 %collective-permute-done.3 = bf16[256,512]{1,0:T(8,128)(2,1)S(1)} collective-permute-done((bf16[256,512]{1,0:T(8,128)(2,1)S(1)}, bf16[256,512]{1,0:T(8,128)(2,1)S(1)}, u32[]{:S(2)}, u32[]{:S(2)}) %collective-permute-start.3) | collective-permute-done | bytes 262176 | tf_op jit(solution)/shard_map/ppermute | solution.py:114
  50.5 2.0 %collective-permute-start.4 = (bf16[256,512]{1,0:T(8,128)(2,1)S(1)}, bf16[256,512]{1,0:T(8,128)(2,1)S(1)}, u32[]{:S(2)}, u32[]{:S(2)}) collective-permute-start(bf16[256,512]{1,0:T(8,128)(2,1)S(1)} %collective-permute-done.3), channel_id=1, source_target_pairs={{0,4},{4,8},{8,12},{12,14},{14,10},{10,6},{6,2},{2,0},{1,5},{5,9},... | collective-permute-start | bytes 786440 | tf_op jit(solution)/shard_map/ppermute | solution.py:114
  52.5 3.6 %collective-permute-done.17 = bf16[256,512]{1,0:T(8,128)(2,1)S(1)} collective-permute-done((bf16[256,512]{1,0:T(8,128)(2,1)S(1)}, bf16[256,512]{1,0:T(8,128)(2,1)S(1)}, u32[]{:S(2)}, u32[]{:S(2)}) %collective-permute-start.17) | collective-permute-done | bytes 262176 | tf_op jit(solution)/shard_map/ppermute | solution.py:114
  56.1 2.0 %collective-permute-start.18 = (bf16[256,512]{1,0:T(8,128)(2,1)S(1)}, bf16[256,512]{1,0:T(8,128)(2,1)S(1)}, u32[]{:S(2)}, u32[]{:S(2)}) collective-permute-start(bf16[256,512]{1,0:T(8,128)(2,1)S(1)} %collective-permute-done.17), channel_id=1, source_target_pairs={{0,4},{4,8},{8,12},{12,14},{14,10},{10,6},{6,2},{2,0},{1,5},{5,9},... | collective-permute-start | bytes 786440 | tf_op jit(solution)/shard_map/ppermute | solution.py:114
  59.2 2.5 %collective-permute-done.4 = bf16[256,512]{1,0:T(8,128)(2,1)S(1)} collective-permute-done((bf16[256,512]{1,0:T(8,128)(2,1)S(1)}, bf16[256,512]{1,0:T(8,128)(2,1)S(1)}, u32[]{:S(2)}, u32[]{:S(2)}) %collective-permute-start.4) | collective-permute-done | bytes 262176 | tf_op jit(solution)/shard_map/ppermute | solution.py:114
  61.7 2.0 %collective-permute-start.5 = (bf16[256,512]{1,0:T(8,128)(2,1)S(1)}, bf16[256,512]{1,0:T(8,128)(2,1)S(1)}, u32[]{:S(2)}, u32[]{:S(2)}) collective-permute-start(bf16[256,512]{1,0:T(8,128)(2,1)S(1)} %collective-permute-done.4), channel_id=1, source_target_pairs={{0,4},{4,8},{8,12},{12,14},{14,10},{10,6},{6,2},{2,0},{1,5},{5,9},... | collective-permute-start | bytes 786440 | tf_op jit(solution)/shard_map/ppermute | solution.py:114
  63.9 3.5 %collective-permute-done.18 = bf16[256,512]{1,0:T(8,128)(2,1)S(1)} collective-permute-done((bf16[256,512]{1,0:T(8,128)(2,1)S(1)}, bf16[256,512]{1,0:T(8,128)(2,1)S(1)}, u32[]{:S(2)}, u32[]{:S(2)}) %collective-permute-start.18) | collective-permute-done | bytes 262176 | tf_op jit(solution)/shard_map/ppermute | solution.py:114
  67.4 2.0 %collective-permute-start.19 = (bf16[256,512]{1,0:T(8,128)(2,1)S(1)}, bf16[256,512]{1,0:T(8,128)(2,1)S(1)}, u32[]{:S(2)}, u32[]{:S(2)}) collective-permute-start(bf16[256,512]{1,0:T(8,128)(2,1)S(1)} %collective-permute-done.18), channel_id=1, source_target_pairs={{0,4},{4,8},{8,12},{12,14},{14,10},{10,6},{6,2},{2,0},{1,5},{5,9},... | collective-permute-start | bytes 786440 | tf_op jit(solution)/shard_map/ppermute | solution.py:114
  70.5 2.5 %collective-permute-done.5 = bf16[256,512]{1,0:T(8,128)(2,1)S(1)} collective-permute-done((bf16[256,512]{1,0:T(8,128)(2,1)S(1)}, bf16[256,512]{1,0:T(8,128)(2,1)S(1)}, u32[]{:S(2)}, u32[]{:S(2)}) %collective-permute-start.5) | collective-permute-done | bytes 262176 | tf_op jit(solution)/shard_map/ppermute | solution.py:114
  73.0 2.0 %collective-permute-start.6 = (bf16[256,512]{1,0:T(8,128)(2,1)S(1)}, bf16[256,512]{1,0:T(8,128)(2,1)S(1)}, u32[]{:S(2)}, u32[]{:S(2)}) collective-permute-start(bf16[256,512]{1,0:T(8,128)(2,1)S(1)} %collective-permute-done.5), channel_id=1, source_target_pairs={{0,4},{4,8},{8,12},{12,14},{14,10},{10,6},{6,2},{2,0},{1,5},{5,9},... | collective-permute-start | bytes 786440 | tf_op jit(solution)/shard_map/ppermute | solution.py:114
  75.0 3.6 %collective-permute-done.19 = bf16[256,512]{1,0:T(8,128)(2,1)S(1)} collective-permute-done((bf16[256,512]{1,0:T(8,128)(2,1)S(1)}, bf16[256,512]{1,0:T(8,128)(2,1)S(1)}, u32[]{:S(2)}, u32[]{:S(2)}) %collective-permute-start.19) | collective-permute-done | bytes 262176 | tf_op jit(solution)/shard_map/ppermute | solution.py:114
  78.6 2.0 %collective-permute-start.20 = (bf16[256,512]{1,0:T(8,128)(2,1)S(1)}, bf16[256,512]{1,0:T(8,128)(2,1)S(1)}, u32[]{:S(2)}, u32[]{:S(2)}) collective-permute-start(bf16[256,512]{1,0:T(8,128)(2,1)S(1)} %collective-permute-done.19), channel_id=1, source_target_pairs={{0,4},{4,8},{8,12},{12,14},{14,10},{10,6},{6,2},{2,0},{1,5},{5,9},... | collective-permute-start | bytes 786440 | tf_op jit(solution)/shard_map/ppermute | solution.py:114
  81.6 2.6 %collective-permute-done.6 = bf16[256,512]{1,0:T(8,128)(2,1)S(1)} collective-permute-done((bf16[256,512]{1,0:T(8,128)(2,1)S(1)}, bf16[256,512]{1,0:T(8,128)(2,1)S(1)}, u32[]{:S(2)}, u32[]{:S(2)}) %collective-permute-start.6) | collective-permute-done | bytes 262176 | tf_op jit(solution)/shard_map/ppermute | solution.py:114
  84.5 1.4 collective-permute-done.13
  87.3 1.4 collective-permute-done.27
  88.9 2.5 %fusion.19 = (f32[256,2048]{1,0:T(8,128)}, bf16[256,2048]{1,0:T(8,128)(2,1)S(1)}) fusion(f32[256,512]{1,0:T(8,128)S(1)} %convolution_add_fusion, f32[256,512]{1,0:T(8,128)S(1)} %convolution_add_fusion.7, f32[256,512]{1,0:T(8,128)S(1)} %convolution_add_fusion.14, f32[256,512]{1,0:T(8,128)S(1)} %convolution_add_fusion.21, bf16[2,128,2048]{2,1,0:T(8,128)(2,1)S(1)} %copy-done.3), kind=kLoop, calls=%fused_computation.50 | loop fusion | flops 12582912 | bytes 6291456 | tf_op jit(solution)/shard_map/add | solution.py:29
  91.4 1.7 %collective-permute-start.28 = (bf16[256,2048]{1,0:T(8,128)(2,1)S(1)}, bf16[256,2048]{1,0:T(8,128)(2,1)S(1)}, u32[]{:S(2)}, u32[]{:S(2)}) collective-permute-start(bf16[256,2048]{1,0:T(8,128)(2,1)S(1)} %get-tuple-element.188), channel_id=1, source_target_pairs={{0,1},{2,3},{4,5},{6,7},{8,9},{10,11},{12,13},{14,15},{16,17},{18,... | collective-permute-start | bytes 3145736 | tf_op jit(solution)/shard_map/ppermute | solution.py:19
  93.4 1.7 %collective-permute-done.28 = bf16[256,2048]{1,0:T(8,128)(2,1)S(1)} collective-permute-done((bf16[256,2048]{1,0:T(8,128)(2,1)S(1)}, bf16[256,2048]{1,0:T(8,128)(2,1)S(1)}, u32[]{:S(2)}, u32[]{:S(2)}) %collective-permute-start.28) | collective-permute-done | bytes 1048608 | tf_op jit(solution)/shard_map/ppermute | solution.py:19
  95.7 6.0 %bitcast_convert_fusion.2 = (f32[2,128,2048]{2,1,0:T(8,128)S(1)}, bf16[256,2048]{1,0:T(8,128)(2,1)}, f32[256,2048]{1,0:T(8,128)}, f32[256,2048]{1,0:T(8,128)}) fusion(bf16[256,2048]{1,0:T(8,128)(2,1)S(1)} %collective-permute-done.28, f32[256]{0:T(256)S(1)} %add_rsqrt_fusion, f32[256]{0:T(256)S(1)} %broadcast_multiply_fusion.4, ...), kind=kOutput, calls=%fused_computation.215 | convolution fusion | flops 2162688000 | bytes 16787456 | tf_op jit(solution)/shard_map/dot_general | solution.py:51
  103.5 3.3 %collective-permute-done.29 = f32[7]{0:T(128)S(1)} collective-permute-done((f32[7]{0:T(128)S(1)}, f32[7]{0:T(128)S(1)}, u32[]{:S(2)}, u32[]{:S(2)}) %collective-permute-start.29) | collective-permute-done | bytes 60 | tf_op jit(solution)/shard_map/ppermute | solution.py:129
  107.5 1.6 %collective-permute-start.30 = (f32[7]{0:T(128)S(1)}, f32[7]{0:T(128)S(1)}, u32[]{:S(2)}, u32[]{:S(2)}) collective-permute-start(f32[7]{0:T(128)S(1)} %fusion.147), channel_id=1, source_target_pairs={{0,4},{2,6},{4,0},{6,2},{8,12},{10,14},{12,8},{14,10},{1,5},{3,7},... | collective-permute-start | bytes 92 | tf_op jit(solution)/shard_map/ppermute | solution.py:129
  109.1 2.0 %collective-permute-done.30 = f32[7]{0:T(128)S(1)} collective-permute-done((f32[7]{0:T(128)S(1)}, f32[7]{0:T(128)S(1)}, u32[]{:S(2)}, u32[]{:S(2)}) %collective-permute-start.30) | collective-permute-done | bytes 60 | tf_op jit(solution)/shard_map/ppermute | solution.py:129
  111.1 2.6 %collective-permute-start.31 = (f32[7]{0:T(128)S(1)}, f32[7]{0:T(128)S(1)}, u32[]{:S(2)}, u32[]{:S(2)}) collective-permute-start(f32[7]{0:T(128)S(1)} %add.464), channel_id=1, source_target_pairs={{0,8},{2,10},{4,12},{6,14},{8,0},{10,2},{12,4},{14,6},{1,9},{3,11}... | collective-permute-start | bytes 92 | tf_op jit(solution)/shard_map/ppermute | solution.py:129
  113.7 1.9 %collective-permute-done.31 = f32[7]{0:T(128)S(1)} collective-permute-done((f32[7]{0:T(128)S(1)}, f32[7]{0:T(128)S(1)}, u32[]{:S(2)}, u32[]{:S(2)}) %collective-permute-start.31) | collective-permute-done | bytes 60 | tf_op jit(solution)/shard_map/ppermute | solution.py:129
  117.6 1.4 fusion.112
  120.1 1.3 collective-permute-start.32
  122.7 1.3 collective-permute-start.33
  124.0 8.0 %collective-permute-done.33 = f32[1]{0:T(128)} collective-permute-done((f32[1]{0:T(128)}, f32[1]{0:T(128)}, u32[]{:S(2)}, u32[]{:S(2)}) %collective-permute-start.33) | collective-permute-done | bytes 36 | tf_op jit(solution)/shard_map/ppermute | solution.py:19
  132.6 8.2 %conditional.3 = (bf16[1,2,128,2048]{3,2,1,0:T(8,128)(2,1)}) conditional(s32[]{:T(128)} %convert_element_type.65, bf16[256,2048]{1,0:T(8,128)(2,1)} %get-tuple-element.200, (bf16[256,2048]{1,0:T(8,128)(2,1)S(1)}, f32[2,128]{1,0:T(2,128)S(1)}, f32[]{:T(128)}, f32[]{:T(128)}, f32[256,2048]{1,0:T(8,128)}, /*index=5*/bf16[2048,2048]{1,0:T(8,128)(2,1)}, ...), branch_computations={%region_15.16_spmd, %region_16.19_spmd} | conditional | flops 2154824192 | bytes 22039568 | solution.py:211
  132.6 6.6 %fusion.107 = (f32[256]{0:T(256)S(1)}, f32[256]{0:T(256)S(1)}, f32[256,2048]{1,0:T(8,128)S(1)}) fusion(f32[256,2048]{1,0:T(8,128)S(1)} %get-tuple-element.67, f32[2048]{0:T(1024)S(1)} %bitcast.152, bf16[2048,2048]{1,0:T(8,128)(2,1)} %get-tuple-element.65, f32[256,2048]{1,0:T(8,128)} %get-tuple-element.64, bf16[256,2048]{1,0:T(8,128)(2,1)S(1)} %get-tuple-element.60), kind=kOutput, calls=%fused_computation.221 | convolution fusion | flops 2151153152 | bytes 15738880 | tf_op jit(solution)/shard_map/cond/branch_1_fun/dot_general | solution.py:58
  139.2 1.6 %fusion.1 = bf16[256,2048]{1,0:T(8,128)(2,1)} fusion(bf16[256,2048]{1,0:T(8,128)(2,1)S(1)} %get-tuple-element.60, f32[256,2048]{1,0:T(8,128)S(1)} %get-tuple-element.67, f32[256,2048]{1,0:T(8,128)S(1)} %get-tuple-element.176, f32[256]{0:T(256)S(1)} %get-tuple-element.177, f32[256]{0:T(256)S(1)} %get-tuple-element.178, f32[256]{0:T(256)S(1)} %rsqrt_bitcast_fusion), kind=kLoop, calls=%fused_computation.5 | loop fusion | flops 3670016 | bytes 6294528 | tf_op jit(solution)/shard_map/cond/branch_1_fun/convert_element_type | solution.py:67
  (141 shorter events, 24.6 us)
Async XLA Ops:
  0.6 7.4 %copy-start.2 = (bf16[2,128,2048]{2,1,0:T(8,128)(2,1)S(1)}, bf16[2,128,2048]{2,1,0:T(8,128)(2,1)}, u32[]{:S(2)}) copy-start(bf16[2,128,2048]{2,1,0:T(8,128)(2,1)} %param.8) | copy-start | bytes 3145732
  0.6 8.0 %copy-start.13 = (f32[1,2048]{1,0:T(1,128)S(1)}, f32[1,2048]{1,0:T(1,128)}, u32[]{:S(2)}) copy-start(f32[1,2048]{1,0:T(1,128)} %param.11) | copy-start | bytes 24580
  2.9 14.8 %collective-permute-start = (bf16[256,512]{1,0:T(8,128)(2,1)}, bf16[256,512]{1,0:T(8,128)(2,1)}, u32[]{:S(2)}, u32[]{:S(2)}) collective-permute-start(bf16[256,512]{1,0:T(8,128)(2,1)} %get-tuple-element.195), channel_id=1, source_target_pairs={{0,4},{4,8},{8,12},{12,14},{14,10},{10,6},{6,2},{2,0},{1,5},{5,9},... | collective-permute-start | bytes 786440 | tf_op jit(solution)/shard_map/ppermute | solution.py:114
  6.0 13.9 %collective-permute-start.7 = (bf16[256,512]{1,0:T(8,128)(2,1)}, bf16[256,512]{1,0:T(8,128)(2,1)}, u32[]{:S(2)}, u32[]{:S(2)}) collective-permute-start(bf16[256,512]{1,0:T(8,128)(2,1)} %get-tuple-element.194), channel_id=1, source_target_pairs={{4,0},{8,4},{12,8},{14,12},{10,14},{6,10},{2,6},{0,2},{5,1},{9,5},... | collective-permute-start | bytes 786440 | tf_op jit(solution)/shard_map/ppermute | solution.py:114
  6.0 13.9 %collective-permute-start.14 = (bf16[256,512]{1,0:T(8,128)(2,1)}, bf16[256,512]{1,0:T(8,128)(2,1)}, u32[]{:S(2)}, u32[]{:S(2)}) collective-permute-start(bf16[256,512]{1,0:T(8,128)(2,1)} %get-tuple-element.193), channel_id=1, source_target_pairs={{0,4},{4,8},{8,12},{12,14},{14,10},{10,6},{6,2},{2,0},{1,5},{5,9},... | collective-permute-start | bytes 786440 | tf_op jit(solution)/shard_map/ppermute | solution.py:114
  8.0 18.0 %collective-permute-start.21 = (bf16[256,512]{1,0:T(8,128)(2,1)}, bf16[256,512]{1,0:T(8,128)(2,1)S(1)}, u32[]{:S(2)}, u32[]{:S(2)}) collective-permute-start(bf16[256,512]{1,0:T(8,128)(2,1)} %get-tuple-element.192), channel_id=1, source_target_pairs={{4,0},{8,4},{12,8},{14,12},{10,14},{6,10},{2,6},{0,2},{5,1},{9,5},... | collective-permute-start | bytes 786440 | tf_op jit(solution)/shard_map/ppermute | solution.py:114
  8.7 1.8 %copy-start.5 = (bf16[1,256,2048]{2,1,0:T(8,128)(2,1)S(1)}, bf16[1,256,2048]{2,1,0:T(8,128)(2,1)}, u32[]{:S(2)}) copy-start(bf16[1,256,2048]{2,1,0:T(8,128)(2,1)} %param.10) | copy-start | bytes 3145732
  10.4 3.1 %copy-start.7 = (bf16[128,2048]{1,0:T(8,128)(2,1)S(1)}, bf16[128,2048]{1,0:T(8,128)(2,1)}, u32[]{:S(2)}) copy-start(bf16[128,2048]{1,0:T(8,128)(2,1)} %param.9) | copy-start | bytes 1572868
  17.8 8.4 %copy-start.11 = (f32[256,512]{1,0:T(8,128)S(1)}, f32[256,512]{1,0:T(8,128)}, u32[]{:S(2)}) copy-start(f32[256,512]{1,0:T(8,128)} %fusion.64) | copy-start | bytes 1572868
  17.8 12.2 %collective-permute-start.1 = (bf16[256,512]{1,0:T(8,128)(2,1)}, bf16[256,512]{1,0:T(8,128)(2,1)S(1)}, u32[]{:S(2)}, u32[]{:S(2)}) collective-permute-start(bf16[256,512]{1,0:T(8,128)(2,1)} %collective-permute-done), channel_id=1, source_target_pairs={{0,4},{4,8},{8,12},{12,14},{14,10},{10,6},{6,2},{2,0},{1,5},{5,9},... | collective-permute-start | bytes 786440 | tf_op jit(solution)/shard_map/ppermute | solution.py:114
  19.9 12.2 %collective-permute-start.8 = (bf16[256,512]{1,0:T(8,128)(2,1)}, bf16[256,512]{1,0:T(8,128)(2,1)S(1)}, u32[]{:S(2)}, u32[]{:S(2)}) collective-permute-start(bf16[256,512]{1,0:T(8,128)(2,1)} %collective-permute-done.7), channel_id=1, source_target_pairs={{4,0},{8,4},{12,8},{14,12},{10,14},{6,10},{2,6},{0,2},{5,1},{9,5},... | collective-permute-start | bytes 786440 | tf_op jit(solution)/shard_map/ppermute | solution.py:114
  19.9 12.3 %collective-permute-start.15 = (bf16[256,512]{1,0:T(8,128)(2,1)}, bf16[256,512]{1,0:T(8,128)(2,1)S(1)}, u32[]{:S(2)}, u32[]{:S(2)}) collective-permute-start(bf16[256,512]{1,0:T(8,128)(2,1)} %collective-permute-done.14), channel_id=1, source_target_pairs={{0,4},{4,8},{8,12},{12,14},{14,10},{10,6},{6,2},{2,0},{1,5},{5,9},... | collective-permute-start | bytes 786440 | tf_op jit(solution)/shard_map/ppermute | solution.py:114
  22.9 4.4 %copy-start.10 = (f32[256,512]{1,0:T(8,128)S(1)}, f32[256,512]{1,0:T(8,128)}, u32[]{:S(2)}) copy-start(f32[256,512]{1,0:T(8,128)} %fusion.62) | copy-start | bytes 1572868
  24.0 4.6 %copy-start.9 = (f32[256,512]{1,0:T(8,128)S(1)}, f32[256,512]{1,0:T(8,128)}, u32[]{:S(2)}) copy-start(f32[256,512]{1,0:T(8,128)} %fusion.60) | copy-start | bytes 1572868
  26.0 8.1 %collective-permute-start.22 = (bf16[256,512]{1,0:T(8,128)(2,1)S(1)}, bf16[256,512]{1,0:T(8,128)(2,1)S(1)}, u32[]{:S(2)}, u32[]{:S(2)}) collective-permute-start(bf16[256,512]{1,0:T(8,128)(2,1)S(1)} %collective-permute-done.21), channel_id=1, source_target_pairs={{4,0},{8,4},{12,8},{14,12},{10,14},{6,10},{2,6},{0,2},{5,1},{9,5},... | collective-permute-start | bytes 786440 | tf_op jit(solution)/shard_map/ppermute | solution.py:114
  30.0 9.2 %collective-permute-start.2 = (bf16[256,512]{1,0:T(8,128)(2,1)S(1)}, bf16[256,512]{1,0:T(8,128)(2,1)S(1)}, u32[]{:S(2)}, u32[]{:S(2)}) collective-permute-start(bf16[256,512]{1,0:T(8,128)(2,1)S(1)} %collective-permute-done.1), channel_id=1, source_target_pairs={{0,4},{4,8},{8,12},{12,14},{14,10},{10,6},{6,2},{2,0},{1,5},{5,9},... | collective-permute-start | bytes 786440 | tf_op jit(solution)/shard_map/ppermute | solution.py:114
  32.1 9.2 %collective-permute-start.9 = (bf16[256,512]{1,0:T(8,128)(2,1)S(1)}, bf16[256,512]{1,0:T(8,128)(2,1)S(1)}, u32[]{:S(2)}, u32[]{:S(2)}) collective-permute-start(bf16[256,512]{1,0:T(8,128)(2,1)S(1)} %collective-permute-done.8), channel_id=1, source_target_pairs={{4,0},{8,4},{12,8},{14,12},{10,14},{6,10},{2,6},{0,2},{5,1},{9,5},... | collective-permute-start | bytes 786440 | tf_op jit(solution)/shard_map/ppermute | solution.py:114
  32.1 12.8 %collective-permute-start.16 = (bf16[256,512]{1,0:T(8,128)(2,1)S(1)}, bf16[256,512]{1,0:T(8,128)(2,1)S(1)}, u32[]{:S(2)}, u32[]{:S(2)}) collective-permute-start(bf16[256,512]{1,0:T(8,128)(2,1)S(1)} %collective-permute-done.15), channel_id=1, source_target_pairs={{0,4},{4,8},{8,12},{12,14},{14,10},{10,6},{6,2},{2,0},{1,5},{5,9},... | collective-permute-start | bytes 786440 | tf_op jit(solution)/shard_map/ppermute | solution.py:114
  34.2 12.8 %collective-permute-start.23 = (bf16[256,512]{1,0:T(8,128)(2,1)S(1)}, bf16[256,512]{1,0:T(8,128)(2,1)S(1)}, u32[]{:S(2)}, u32[]{:S(2)}) collective-permute-start(bf16[256,512]{1,0:T(8,128)(2,1)S(1)} %collective-permute-done.22), channel_id=1, source_target_pairs={{4,0},{8,4},{12,8},{14,12},{10,14},{6,10},{2,6},{0,2},{5,1},{9,5},... | collective-permute-start | bytes 786440 | tf_op jit(solution)/shard_map/ppermute | solution.py:114
  39.3 11.2 %collective-permute-start.3 = (bf16[256,512]{1,0:T(8,128)(2,1)S(1)}, bf16[256,512]{1,0:T(8,128)(2,1)S(1)}, u32[]{:S(2)}, u32[]{:S(2)}) collective-permute-start(bf16[256,512]{1,0:T(8,128)(2,1)S(1)} %collective-permute-done.2), channel_id=1, source_target_pairs={{0,4},{4,8},{8,12},{12,14},{14,10},{10,6},{6,2},{2,0},{1,5},{5,9},... | collective-permute-start | bytes 786440 | tf_op jit(solution)/shard_map/ppermute | solution.py:114
  41.2 11.2 %collective-permute-start.10 = (bf16[256,512]{1,0:T(8,128)(2,1)S(1)}, bf16[256,512]{1,0:T(8,128)(2,1)S(1)}, u32[]{:S(2)}, u32[]{:S(2)}) collective-permute-start(bf16[256,512]{1,0:T(8,128)(2,1)S(1)} %collective-permute-done.9), channel_id=1, source_target_pairs={{4,0},{8,4},{12,8},{14,12},{10,14},{6,10},{2,6},{0,2},{5,1},{9,5},... | collective-permute-start | bytes 786440 | tf_op jit(solution)/shard_map/ppermute | solution.py:114
  44.9 11.2 %collective-permute-start.17 = (bf16[256,512]{1,0:T(8,128)(2,1)S(1)}, bf16[256,512]{1,0:T(8,128)(2,1)S(1)}, u32[]{:S(2)}, u32[]{:S(2)}) collective-permute-start(bf16[256,512]{1,0:T(8,128)(2,1)S(1)} %collective-permute-done.16), channel_id=1, source_target_pairs={{0,4},{4,8},{8,12},{12,14},{14,10},{10,6},{6,2},{2,0},{1,5},{5,9},... | collective-permute-start | bytes 786440 | tf_op jit(solution)/shard_map/ppermute | solution.py:114
  47.0 11.1 %collective-permute-start.24 = (bf16[256,512]{1,0:T(8,128)(2,1)S(1)}, bf16[256,512]{1,0:T(8,128)(2,1)S(1)}, u32[]{:S(2)}, u32[]{:S(2)}) collective-permute-start(bf16[256,512]{1,0:T(8,128)(2,1)S(1)} %collective-permute-done.23), channel_id=1, source_target_pairs={{4,0},{8,4},{12,8},{14,12},{10,14},{6,10},{2,6},{0,2},{5,1},{9,5},... | collective-permute-start | bytes 786440 | tf_op jit(solution)/shard_map/ppermute | solution.py:114
  50.5 11.2 %collective-permute-start.4 = (bf16[256,512]{1,0:T(8,128)(2,1)S(1)}, bf16[256,512]{1,0:T(8,128)(2,1)S(1)}, u32[]{:S(2)}, u32[]{:S(2)}) collective-permute-start(bf16[256,512]{1,0:T(8,128)(2,1)S(1)} %collective-permute-done.3), channel_id=1, source_target_pairs={{0,4},{4,8},{8,12},{12,14},{14,10},{10,6},{6,2},{2,0},{1,5},{5,9},... | collective-permute-start | bytes 786440 | tf_op jit(solution)/shard_map/ppermute | solution.py:114
  52.5 11.3 %collective-permute-start.11 = (bf16[256,512]{1,0:T(8,128)(2,1)S(1)}, bf16[256,512]{1,0:T(8,128)(2,1)S(1)}, u32[]{:S(2)}, u32[]{:S(2)}) collective-permute-start(bf16[256,512]{1,0:T(8,128)(2,1)S(1)} %collective-permute-done.10), channel_id=1, source_target_pairs={{4,0},{8,4},{12,8},{14,12},{10,14},{6,10},{2,6},{0,2},{5,1},{9,5},... | collective-permute-start | bytes 786440 | tf_op jit(solution)/shard_map/ppermute | solution.py:114
  56.1 11.2 %collective-permute-start.18 = (bf16[256,512]{1,0:T(8,128)(2,1)S(1)}, bf16[256,512]{1,0:T(8,128)(2,1)S(1)}, u32[]{:S(2)}, u32[]{:S(2)}) collective-permute-start(bf16[256,512]{1,0:T(8,128)(2,1)S(1)} %collective-permute-done.17), channel_id=1, source_target_pairs={{0,4},{4,8},{8,12},{12,14},{14,10},{10,6},{6,2},{2,0},{1,5},{5,9},... | collective-permute-start | bytes 786440 | tf_op jit(solution)/shard_map/ppermute | solution.py:114
  58.1 11.3 %collective-permute-start.25 = (bf16[256,512]{1,0:T(8,128)(2,1)S(1)}, bf16[256,512]{1,0:T(8,128)(2,1)S(1)}, u32[]{:S(2)}, u32[]{:S(2)}) collective-permute-start(bf16[256,512]{1,0:T(8,128)(2,1)S(1)} %collective-permute-done.24), channel_id=1, source_target_pairs={{4,0},{8,4},{12,8},{14,12},{10,14},{6,10},{2,6},{0,2},{5,1},{9,5},... | collective-permute-start | bytes 786440 | tf_op jit(solution)/shard_map/ppermute | solution.py:114
  61.7 11.2 %collective-permute-start.5 = (bf16[256,512]{1,0:T(8,128)(2,1)S(1)}, bf16[256,512]{1,0:T(8,128)(2,1)S(1)}, u32[]{:S(2)}, u32[]{:S(2)}) collective-permute-start(bf16[256,512]{1,0:T(8,128)(2,1)S(1)} %collective-permute-done.4), channel_id=1, source_target_pairs={{0,4},{4,8},{8,12},{12,14},{14,10},{10,6},{6,2},{2,0},{1,5},{5,9},... | collective-permute-start | bytes 786440 | tf_op jit(solution)/shard_map/ppermute | solution.py:114
  63.7 11.2 %collective-permute-start.12 = (bf16[256,512]{1,0:T(8,128)(2,1)S(1)}, bf16[256,512]{1,0:T(8,128)(2,1)S(1)}, u32[]{:S(2)}, u32[]{:S(2)}) collective-permute-start(bf16[256,512]{1,0:T(8,128)(2,1)S(1)} %collective-permute-done.11), channel_id=1, source_target_pairs={{4,0},{8,4},{12,8},{14,12},{10,14},{6,10},{2,6},{0,2},{5,1},{9,5},... | collective-permute-start | bytes 786440 | tf_op jit(solution)/shard_map/ppermute | solution.py:114
  67.4 11.2 %collective-permute-start.19 = (bf16[256,512]{1,0:T(8,128)(2,1)S(1)}, bf16[256,512]{1,0:T(8,128)(2,1)S(1)}, u32[]{:S(2)}, u32[]{:S(2)}) collective-permute-start(bf16[256,512]{1,0:T(8,128)(2,1)S(1)} %collective-permute-done.18), channel_id=1, source_target_pairs={{0,4},{4,8},{8,12},{12,14},{14,10},{10,6},{6,2},{2,0},{1,5},{5,9},... | collective-permute-start | bytes 786440 | tf_op jit(solution)/shard_map/ppermute | solution.py:114
  69.4 11.2 %collective-permute-start.26 = (bf16[256,512]{1,0:T(8,128)(2,1)S(1)}, bf16[256,512]{1,0:T(8,128)(2,1)S(1)}, u32[]{:S(2)}, u32[]{:S(2)}) collective-permute-start(bf16[256,512]{1,0:T(8,128)(2,1)S(1)} %collective-permute-done.25), channel_id=1, source_target_pairs={{4,0},{8,4},{12,8},{14,12},{10,14},{6,10},{2,6},{0,2},{5,1},{9,5},... | collective-permute-start | bytes 786440 | tf_op jit(solution)/shard_map/ppermute | solution.py:114
  73.0 11.2 %collective-permute-start.6 = (bf16[256,512]{1,0:T(8,128)(2,1)S(1)}, bf16[256,512]{1,0:T(8,128)(2,1)S(1)}, u32[]{:S(2)}, u32[]{:S(2)}) collective-permute-start(bf16[256,512]{1,0:T(8,128)(2,1)S(1)} %collective-permute-done.5), channel_id=1, source_target_pairs={{0,4},{4,8},{8,12},{12,14},{14,10},{10,6},{6,2},{2,0},{1,5},{5,9},... | collective-permute-start | bytes 786440 | tf_op jit(solution)/shard_map/ppermute | solution.py:114
  74.9 10.9 %collective-permute-start.13 = (bf16[256,512]{1,0:T(8,128)(2,1)S(1)}, bf16[256,512]{1,0:T(8,128)(2,1)S(1)}, u32[]{:S(2)}, u32[]{:S(2)}) collective-permute-start(bf16[256,512]{1,0:T(8,128)(2,1)S(1)} %collective-permute-done.12), channel_id=1, source_target_pairs={{4,0},{8,4},{12,8},{14,12},{10,14},{6,10},{2,6},{0,2},{5,1},{9,5},... | collective-permute-start | bytes 786440 | tf_op jit(solution)/shard_map/ppermute | solution.py:114
  78.6 8.5 %collective-permute-start.20 = (bf16[256,512]{1,0:T(8,128)(2,1)S(1)}, bf16[256,512]{1,0:T(8,128)(2,1)S(1)}, u32[]{:S(2)}, u32[]{:S(2)}) collective-permute-start(bf16[256,512]{1,0:T(8,128)(2,1)S(1)} %collective-permute-done.19), channel_id=1, source_target_pairs={{0,4},{4,8},{8,12},{12,14},{14,10},{10,6},{6,2},{2,0},{1,5},{5,9},... | collective-permute-start | bytes 786440 | tf_op jit(solution)/shard_map/ppermute | solution.py:114
  80.6 8.1 %collective-permute-start.27 = (bf16[256,512]{1,0:T(8,128)(2,1)S(1)}, bf16[256,512]{1,0:T(8,128)(2,1)S(1)}, u32[]{:S(2)}, u32[]{:S(2)}) collective-permute-start(bf16[256,512]{1,0:T(8,128)(2,1)S(1)} %collective-permute-done.26), channel_id=1, source_target_pairs={{4,0},{8,4},{12,8},{14,12},{10,14},{6,10},{2,6},{0,2},{5,1},{9,5},... | collective-permute-start | bytes 786440 | tf_op jit(solution)/shard_map/ppermute | solution.py:114
  84.4 4.4 %copy-start.3 = (bf16[2,128,2048]{2,1,0:T(8,128)(2,1)S(1)}, bf16[2,128,2048]{2,1,0:T(8,128)(2,1)}, u32[]{:S(2)}) copy-start(bf16[2,128,2048]{2,1,0:T(8,128)(2,1)} %param.8) | copy-start | bytes 3145732
  91.4 1.9 %copy-start.6 = (bf16[1,256,2048]{2,1,0:T(8,128)(2,1)S(1)}, bf16[1,256,2048]{2,1,0:T(8,128)(2,1)}, u32[]{:S(2)}) copy-start(bf16[1,256,2048]{2,1,0:T(8,128)(2,1)} %param.10) | copy-start | bytes 3145732
  91.4 3.7 %collective-permute-start.28 = (bf16[256,2048]{1,0:T(8,128)(2,1)S(1)}, bf16[256,2048]{1,0:T(8,128)(2,1)S(1)}, u32[]{:S(2)}, u32[]{:S(2)}) collective-permute-start(bf16[256,2048]{1,0:T(8,128)(2,1)S(1)} %get-tuple-element.188), channel_id=1, source_target_pairs={{0,1},{2,3},{4,5},{6,7},{8,9},{10,11},{12,13},{14,15},{16,17},{18,... | collective-permute-start | bytes 3145736 | tf_op jit(solution)/shard_map/ppermute | solution.py:19
  93.4 8.4 %copy-start = (bf16[2048,2048]{1,0:T(8,128)(2,1)}, bf16[2048,2048]{1,0:T(8,128)(2,1)S(1)}, u32[]{:S(2)}) copy-start(bf16[2048,2048]{1,0:T(8,128)(2,1)S(1)} %constant_dynamic-update-slice_fusion) | copy-start | bytes 25165828
  95.7 6.1 %copy-start.8 = (bf16[128,2048]{1,0:T(8,128)(2,1)S(1)}, bf16[128,2048]{1,0:T(8,128)(2,1)}, u32[]{:S(2)}) copy-start(bf16[128,2048]{1,0:T(8,128)(2,1)} %param.9) | copy-start | bytes 1572868
  103.2 3.6 %collective-permute-start.29 = (f32[7]{0:T(128)S(1)}, f32[7]{0:T(128)S(1)}, u32[]{:S(2)}, u32[]{:S(2)}) collective-permute-start(f32[7]{0:T(128)S(1)} %pad_maximum_fusion.1), channel_id=1, source_target_pairs={{0,2},{2,0},{4,6},{6,4},{8,10},{10,8},{12,14},{14,12},{1,3},{3,1},... | collective-permute-start | bytes 92 | tf_op jit(solution)/shard_map/ppermute | solution.py:129
  107.5 3.6 %collective-permute-start.30 = (f32[7]{0:T(128)S(1)}, f32[7]{0:T(128)S(1)}, u32[]{:S(2)}, u32[]{:S(2)}) collective-permute-start(f32[7]{0:T(128)S(1)} %fusion.147), channel_id=1, source_target_pairs={{0,4},{2,6},{4,0},{6,2},{8,12},{10,14},{12,8},{14,10},{1,5},{3,7},... | collective-permute-start | bytes 92 | tf_op jit(solution)/shard_map/ppermute | solution.py:129
  111.1 4.5 %collective-permute-start.31 = (f32[7]{0:T(128)S(1)}, f32[7]{0:T(128)S(1)}, u32[]{:S(2)}, u32[]{:S(2)}) collective-permute-start(f32[7]{0:T(128)S(1)} %add.464), channel_id=1, source_target_pairs={{0,8},{2,10},{4,12},{6,14},{8,0},{10,2},{12,4},{14,6},{1,9},{3,11}... | collective-permute-start | bytes 92 | tf_op jit(solution)/shard_map/ppermute | solution.py:129
  120.1 12.5 %collective-permute-start.32 = (bf16[256,2048]{1,0:T(8,128)(2,1)}, bf16[256,2048]{1,0:T(8,128)(2,1)S(1)}, u32[]{:S(2)}, u32[]{:S(2)}) collective-permute-start(bf16[256,2048]{1,0:T(8,128)(2,1)} %get-tuple-element.200), channel_id=1, source_target_pairs={{1,0},{3,2},{5,4},{7,6},{9,8},{11,10},{13,12},{15,14},{17,16},{19,... | collective-permute-start | bytes 3145736 | tf_op jit(solution)/shard_map/ppermute | solution.py:19
  122.7 9.3 %collective-permute-start.33 = (f32[1]{0:T(128)}, f32[1]{0:T(128)}, u32[]{:S(2)}, u32[]{:S(2)}) collective-permute-start(f32[1]{0:T(128)} %bitcast.23), channel_id=1, source_target_pairs={{1,0},{3,2},{5,4},{7,6},{9,8},{11,10},{13,12},{15,14},{17,16},{19,... | collective-permute-start | bytes 20 | tf_op jit(solution)/shard_map/ppermute | solution.py:19

commit v14 on v10

--- a/solution.py
+++ b/solution.py
@@ -212,7 +212,15 @@
         inputs, weight = lax.optimization_barrier((inputs, weight))
         rows_all = inputs.reshape(members * tok_rows, width)
         fa = section_forward(rows_all, gain, weight)
-    arrived = shifted(fa[0], "section", 1)
+    if overlap:
+        halves = []
+        for m in range(members):
+            rows_m = slice(m * tok_rows, (m + 1) * tok_rows)
+            out_m = (values_a[rows_m] + gelu_value(pre_a[rows_m])).astype(jnp.bfloat16)
+            halves.append(shifted(out_m, "section", 1))
+        arrived = jnp.concatenate(halves, axis=0)
+    else:
+        arrived = shifted(fa[0], "section", 1)
     fb = section_forward(arrived, gain, weight)
 
     y = fb[0].reshape(members, tok_rows, width)

time: 141 us -> 147 us (1.043)
  starting transfers between devices: 38.1 us -> 40.7 us
    ppermute x28, waiting for transfers between devices: 38.2 us -> 39.9 us  [ring_gather(): parts[j] = lax.ppermute(parts[j], axis, cw if clockwise else ccw)]
    ppermute x3 -> x4, starting transfers between devices: 4.1 us -> 5.44 us  [shifted(): return lax.ppermute(x, axis, pairs)]
    ppermute x3 -> x4, waiting for transfers between devices: 9.31 us -> 8.91 us  [shifted(): return lax.ppermute(x, axis, pairs)]
  transfers between devices with their start and end apart: 34 -> 35, of which waited for: 27 -> 30; matrix products, arithmetic and copies ran while one was open for 11% -> 11% of each run, Pallas kernels for 0% -> 0%
where the time goes in v14:
time: 147 us; the launch traced here: 146 us
  waiting for transfers between devices  55.7 us (38%)
  starting transfers between devices  40.7 us (28%)
  matrix products  22.9 us (16%)
  other arithmetic  13 us (9%)
  local copies, waits for them, and re-layouts  9.32 us (6%)
  between operations  4.49 us (3%)
    ppermute x28, waiting for transfers between devices, ring_gather(): parts[j] = lax.ppermute(parts[j], axis, cw if clockwise else ccw)  39.9 us
    ppermute x28, starting transfers between devices, ring_gather(): parts[j] = lax.ppermute(parts[j], axis, cw if clockwise else ccw)  30.6 us
    ppermute x4, waiting for transfers between devices, shifted(): return lax.ppermute(x, axis, pairs)  8.91 us
    dot_general x28, matrix products, on_piece(): term = jnp.dot(lhs, piece, preferred_element_type=jnp.float32)  8.31 us
    dot_general x1, matrix products, section_forward(): pre_act = jnp.dot(normed, weight, preferred_element_type=jnp.float32)  7.12 us
    ppermute x3, waiting for transfers between devices, tree_sum(): v = v + lax.ppermute(v, axis, [(i, i ^ b) for i in range(n)])  6.95 us
    dot_general x1, matrix products, section_backward(): lax.dot_general(grad_pre, weight, (((1,), (1,)), ((), ())), preferred_ele...  6.58 us
    ppermute x4, starting transfers between devices, shifted(): return lax.ppermute(x, axis, pairs)  5.44 us
  transfers between devices with their start and end apart: 35, of which 30 were waited for; matrix products, arithmetic and copies ran while one was open for 11% of the time, Pallas kernels for 0%

profile of v14, /device:TPU:0, one launch (start us, length us, event | category | flops | bytes accessed | tf_op | source)
XLA Modules:
  0.0 146.1 jit_solution(3780818618295702642)
XLA Ops:
  0.7 2.2 %fusion.129 = (bf16[256,512]{1,0:T(8,128)(2,1)}, bf16[256,512]{1,0:T(8,128)(2,1)}, bf16[256,512]{1,0:T(8,128)(2,1)}, bf16[256,512]{1,0:T(8,128)(2,1)S(1)}) fusion(bf16[256,2048]{1,0:T(8,128)(2,1)} %bitcast.130), kind=kLoop, calls=%fused_computation.239 | loop fusion | bytes 2097152 | tf_op jit(solution)/shard_map/slice | solution.py:106
  2.9 3.1 %collective-permute-start = (bf16[256,512]{1,0:T(8,128)(2,1)S(1)}, bf16[256,512]{1,0:T(8,128)(2,1)S(1)}, u32[]{:S(2)}, u32[]{:S(2)}) collective-permute-start(bf16[256,512]{1,0:T(8,128)(2,1)S(1)} %get-tuple-element.201), channel_id=1, source_target_pairs={{0,4},{4,8},{8,12},{12,14},{14,10},{10,6},{6,2},{2,0},{1,5},{5,9},... | collective-permute-start | bytes 786440 | tf_op jit(solution)/shard_map/ppermute | solution.py:113
  5.9 2.0 %collective-permute-start.14 = (bf16[256,512]{1,0:T(8,128)(2,1)}, bf16[256,512]{1,0:T(8,128)(2,1)}, u32[]{:S(2)}, u32[]{:S(2)}) collective-permute-start(bf16[256,512]{1,0:T(8,128)(2,1)} %get-tuple-element.199), channel_id=1, source_target_pairs={{0,4},{4,8},{8,12},{12,14},{14,10},{10,6},{6,2},{2,0},{1,5},{5,9},... | collective-permute-start | bytes 786440 | tf_op jit(solution)/shard_map/ppermute | solution.py:113
  10.1 2.9 %collective-permute-done = bf16[256,512]{1,0:T(8,128)(2,1)S(1)} collective-permute-done((bf16[256,512]{1,0:T(8,128)(2,1)S(1)}, bf16[256,512]{1,0:T(8,128)(2,1)S(1)}, u32[]{:S(2)}, u32[]{:S(2)}) %collective-permute-start) | collective-permute-done | bytes 262176 | tf_op jit(solution)/shard_map/ppermute | solution.py:113
  18.2 1.2 fusion.53
  20.6 2.2 %collective-permute-start.1 = (bf16[256,512]{1,0:T(8,128)(2,1)S(1)}, bf16[256,512]{1,0:T(8,128)(2,1)S(1)}, u32[]{:S(2)}, u32[]{:S(2)}) collective-permute-start(bf16[256,512]{1,0:T(8,128)(2,1)S(1)} %copy-done.9), channel_id=1, source_target_pairs={{0,4},{4,8},{8,12},{12,14},{14,10},{10,6},{6,2},{2,0},{1,5},{5,9},... | collective-permute-start | bytes 786440 | tf_op jit(solution)/shard_map/ppermute | solution.py:113
  22.8 2.0 %collective-permute-start.15 = (bf16[256,512]{1,0:T(8,128)(2,1)}, bf16[256,512]{1,0:T(8,128)(2,1)S(1)}, u32[]{:S(2)}, u32[]{:S(2)}) collective-permute-start(bf16[256,512]{1,0:T(8,128)(2,1)} %collective-permute-done.14), channel_id=1, source_target_pairs={{0,4},{4,8},{8,12},{12,14},{14,10},{10,6},{6,2},{2,0},{1,5},{5,9},... | collective-permute-start | bytes 786440 | tf_op jit(solution)/shard_map/ppermute | solution.py:113
  24.8 1.2 fusion.77
  26.4 3.5 %collective-permute-done.1 = bf16[256,512]{1,0:T(8,128)(2,1)S(1)} collective-permute-done((bf16[256,512]{1,0:T(8,128)(2,1)S(1)}, bf16[256,512]{1,0:T(8,128)(2,1)S(1)}, u32[]{:S(2)}, u32[]{:S(2)}) %collective-permute-start.1) | collective-permute-done | bytes 262176 | tf_op jit(solution)/shard_map/ppermute | solution.py:113
  29.9 2.1 %collective-permute-start.2 = (bf16[256,512]{1,0:T(8,128)(2,1)S(1)}, bf16[256,512]{1,0:T(8,128)(2,1)S(1)}, u32[]{:S(2)}, u32[]{:S(2)}) collective-permute-start(bf16[256,512]{1,0:T(8,128)(2,1)S(1)} %collective-permute-done.1), channel_id=1, source_target_pairs={{0,4},{4,8},{8,12},{12,14},{14,10},{10,6},{6,2},{2,0},{1,5},{5,9},... | collective-permute-start | bytes 786440 | tf_op jit(solution)/shard_map/ppermute | solution.py:113
  32.2 3.3 %collective-permute-done.15 = bf16[256,512]{1,0:T(8,128)(2,1)S(1)} collective-permute-done((bf16[256,512]{1,0:T(8,128)(2,1)}, bf16[256,512]{1,0:T(8,128)(2,1)S(1)}, u32[]{:S(2)}, u32[]{:S(2)}) %collective-permute-start.15) | collective-permute-done | bytes 262176 | tf_op jit(solution)/shard_map/ppermute | solution.py:113
  35.5 2.1 %collective-permute-start.16 = (bf16[256,512]{1,0:T(8,128)(2,1)S(1)}, bf16[256,512]{1,0:T(8,128)(2,1)S(1)}, u32[]{:S(2)}, u32[]{:S(2)}) collective-permute-start(bf16[256,512]{1,0:T(8,128)(2,1)S(1)} %collective-permute-done.15), channel_id=1, source_target_pairs={{0,4},{4,8},{8,12},{12,14},{14,10},{10,6},{6,2},{2,0},{1,5},{5,9},... | collective-permute-start | bytes 786440 | tf_op jit(solution)/shard_map/ppermute | solution.py:113
  38.8 2.3 %collective-permute-done.2 = bf16[256,512]{1,0:T(8,128)(2,1)S(1)} collective-permute-done((bf16[256,512]{1,0:T(8,128)(2,1)S(1)}, bf16[256,512]{1,0:T(8,128)(2,1)S(1)}, u32[]{:S(2)}, u32[]{:S(2)}) %collective-permute-start.2) | collective-permute-done | bytes 262176 | tf_op jit(solution)/shard_map/ppermute | solution.py:113
  41.1 2.1 %collective-permute-start.3 = (bf16[256,512]{1,0:T(8,128)(2,1)S(1)}, bf16[256,512]{1,0:T(8,128)(2,1)S(1)}, u32[]{:S(2)}, u32[]{:S(2)}) collective-permute-start(bf16[256,512]{1,0:T(8,128)(2,1)S(1)} %collective-permute-done.2), channel_id=1, source_target_pairs={{0,4},{4,8},{8,12},{12,14},{14,10},{10,6},{6,2},{2,0},{1,5},{5,9},... | collective-permute-start | bytes 786440 | tf_op jit(solution)/shard_map/ppermute | solution.py:113
  43.4 3.3 %collective-permute-done.16 = bf16[256,512]{1,0:T(8,128)(2,1)S(1)} collective-permute-done((bf16[256,512]{1,0:T(8,128)(2,1)S(1)}, bf16[256,512]{1,0:T(8,128)(2,1)S(1)}, u32[]{:S(2)}, u32[]{:S(2)}) %collective-permute-start.16) | collective-permute-done | bytes 262176 | tf_op jit(solution)/shard_map/ppermute | solution.py:113
  46.7 2.1 %collective-permute-start.17 = (bf16[256,512]{1,0:T(8,128)(2,1)S(1)}, bf16[256,512]{1,0:T(8,128)(2,1)S(1)}, u32[]{:S(2)}, u32[]{:S(2)}) collective-permute-start(bf16[256,512]{1,0:T(8,128)(2,1)S(1)} %collective-permute-done.16), channel_id=1, source_target_pairs={{0,4},{4,8},{8,12},{12,14},{14,10},{10,6},{6,2},{2,0},{1,5},{5,9},... | collective-permute-start | bytes 786440 | tf_op jit(solution)/shard_map/ppermute | solution.py:113
  50.0 2.3 %collective-permute-done.3 = bf16[256,512]{1,0:T(8,128)(2,1)S(1)} collective-permute-done((bf16[256,512]{1,0:T(8,128)(2,1)S(1)}, bf16[256,512]{1,0:T(8,128)(2,1)S(1)}, u32[]{:S(2)}, u32[]{:S(2)}) %collective-permute-start.3) | collective-permute-done | bytes 262176 | tf_op jit(solution)/shard_map/ppermute | solution.py:113
  52.3 2.1 %collective-permute-start.4 = (bf16[256,512]{1,0:T(8,128)(2,1)S(1)}, bf16[256,512]{1,0:T(8,128)(2,1)S(1)}, u32[]{:S(2)}, u32[]{:S(2)}) collective-permute-start(bf16[256,512]{1,0:T(8,128)(2,1)S(1)} %collective-permute-done.3), channel_id=1, source_target_pairs={{0,4},{4,8},{8,12},{12,14},{14,10},{10,6},{6,2},{2,0},{1,5},{5,9},... | collective-permute-start | bytes 786440 | tf_op jit(solution)/shard_map/ppermute | solution.py:113
  54.6 3.3 %collective-permute-done.17 = bf16[256,512]{1,0:T(8,128)(2,1)S(1)} collective-permute-done((bf16[256,512]{1,0:T(8,128)(2,1)S(1)}, bf16[256,512]{1,0:T(8,128)(2,1)S(1)}, u32[]{:S(2)}, u32[]{:S(2)}) %collective-permute-start.17) | collective-permute-done | bytes 262176 | tf_op jit(solution)/shard_map/ppermute | solution.py:113
  57.9 2.1 %collective-permute-start.18 = (bf16[256,512]{1,0:T(8,128)(2,1)S(1)}, bf16[256,512]{1,0:T(8,128)(2,1)S(1)}, u32[]{:S(2)}, u32[]{:S(2)}) collective-permute-start(bf16[256,512]{1,0:T(8,128)(2,1)S(1)} %collective-permute-done.17), channel_id=1, source_target_pairs={{0,4},{4,8},{8,12},{12,14},{14,10},{10,6},{6,2},{2,0},{1,5},{5,9},... | collective-permute-start | bytes 786440 | tf_op jit(solution)/shard_map/ppermute | solution.py:113
  61.3 2.2 %collective-permute-done.4 = bf16[256,512]{1,0:T(8,128)(2,1)S(1)} collective-permute-done((bf16[256,512]{1,0:T(8,128)(2,1)S(1)}, bf16[256,512]{1,0:T(8,128)(2,1)S(1)}, u32[]{:S(2)}, u32[]{:S(2)}) %collective-permute-start.4) | collective-permute-done | bytes 262176 | tf_op jit(solution)/shard_map/ppermute | solution.py:113
  63.6 2.1 %collective-permute-start.5 = (bf16[256,512]{1,0:T(8,128)(2,1)S(1)}, bf16[256,512]{1,0:T(8,128)(2,1)S(1)}, u32[]{:S(2)}, u32[]{:S(2)}) collective-permute-start(bf16[256,512]{1,0:T(8,128)(2,1)S(1)} %collective-permute-done.4), channel_id=1, source_target_pairs={{0,4},{4,8},{8,12},{12,14},{14,10},{10,6},{6,2},{2,0},{1,5},{5,9},... | collective-permute-start | bytes 786440 | tf_op jit(solution)/shard_map/ppermute | solution.py:113
  65.9 3.3 %collective-permute-done.18 = bf16[256,512]{1,0:T(8,128)(2,1)S(1)} collective-permute-done((bf16[256,512]{1,0:T(8,128)(2,1)S(1)}, bf16[256,512]{1,0:T(8,128)(2,1)S(1)}, u32[]{:S(2)}, u32[]{:S(2)}) %collective-permute-start.18) | collective-permute-done | bytes 262176 | tf_op jit(solution)/shard_map/ppermute | solution.py:113
  69.2 2.1 %collective-permute-start.19 = (bf16[256,512]{1,0:T(8,128)(2,1)S(1)}, bf16[256,512]{1,0:T(8,128)(2,1)S(1)}, u32[]{:S(2)}, u32[]{:S(2)}) collective-permute-start(bf16[256,512]{1,0:T(8,128)(2,1)S(1)} %collective-permute-done.18), channel_id=1, source_target_pairs={{0,4},{4,8},{8,12},{12,14},{14,10},{10,6},{6,2},{2,0},{1,5},{5,9},... | collective-permute-start | bytes 786440 | tf_op jit(solution)/shard_map/ppermute | solution.py:113
  72.5 2.3 %collective-permute-done.5 = bf16[256,512]{1,0:T(8,128)(2,1)S(1)} collective-permute-done((bf16[256,512]{1,0:T(8,128)(2,1)S(1)}, bf16[256,512]{1,0:T(8,128)(2,1)S(1)}, u32[]{:S(2)}, u32[]{:S(2)}) %collective-permute-start.5) | collective-permute-done | bytes 262176 | tf_op jit(solution)/shard_map/ppermute | solution.py:113
  74.8 2.1 %collective-permute-start.6 = (bf16[256,512]{1,0:T(8,128)(2,1)S(1)}, bf16[256,512]{1,0:T(8,128)(2,1)S(1)}, u32[]{:S(2)}, u32[]{:S(2)}) collective-permute-start(bf16[256,512]{1,0:T(8,128)(2,1)S(1)} %collective-permute-done.5), channel_id=1, source_target_pairs={{0,4},{4,8},{8,12},{12,14},{14,10},{10,6},{6,2},{2,0},{1,5},{5,9},... | collective-permute-start | bytes 786440 | tf_op jit(solution)/shard_map/ppermute | solution.py:113
  77.1 3.3 %collective-permute-done.19 = bf16[256,512]{1,0:T(8,128)(2,1)S(1)} collective-permute-done((bf16[256,512]{1,0:T(8,128)(2,1)S(1)}, bf16[256,512]{1,0:T(8,128)(2,1)S(1)}, u32[]{:S(2)}, u32[]{:S(2)}) %collective-permute-start.19) | collective-permute-done | bytes 262176 | tf_op jit(solution)/shard_map/ppermute | solution.py:113
  80.4 2.1 %collective-permute-start.20 = (bf16[256,512]{1,0:T(8,128)(2,1)S(1)}, bf16[256,512]{1,0:T(8,128)(2,1)S(1)}, u32[]{:S(2)}, u32[]{:S(2)}) collective-permute-start(bf16[256,512]{1,0:T(8,128)(2,1)S(1)} %collective-permute-done.19), channel_id=1, source_target_pairs={{0,4},{4,8},{8,12},{12,14},{14,10},{10,6},{6,2},{2,0},{1,5},{5,9},... | collective-permute-start | bytes 786440 | tf_op jit(solution)/shard_map/ppermute | solution.py:113
  83.8 2.2 %collective-permute-done.6 = bf16[256,512]{1,0:T(8,128)(2,1)S(1)} collective-permute-done((bf16[256,512]{1,0:T(8,128)(2,1)S(1)}, bf16[256,512]{1,0:T(8,128)(2,1)S(1)}, u32[]{:S(2)}, u32[]{:S(2)}) %collective-permute-start.6) | collective-permute-done | bytes 262176 | tf_op jit(solution)/shard_map/ppermute | solution.py:113
  86.3 1.6 %collective-permute-done.13 = bf16[256,512]{1,0:T(8,128)(2,1)S(1)} collective-permute-done((bf16[256,512]{1,0:T(8,128)(2,1)S(1)}, bf16[256,512]{1,0:T(8,128)(2,1)S(1)}, u32[]{:S(2)}, u32[]{:S(2)}) %collective-permute-start.13) | collective-permute-done | bytes 262176 | tf_op jit(solution)/shard_map/ppermute | solution.py:113
  89.4 1.2 collective-permute-done.27
  90.9 2.6 %fusion.19 = (f32[256,2048]{1,0:T(8,128)}, f32[256,2048]{1,0:T(8,128)S(1)}) fusion(f32[256,512]{1,0:T(8,128)S(1)} %fusion.23, f32[256,512]{1,0:T(8,128)S(1)} %fusion.24, f32[256,512]{1,0:T(8,128)S(1)} %fusion.25, f32[256,512]{1,0:T(8,128)S(1)} %fusion.26), kind=kLoop, calls=%fused_computation.50 | loop fusion | flops 10485760 | bytes 6291456 | tf_op jit(solution)/shard_map/add | solution.py:28
  94.2 1.3 collective-permute-start.28
  95.6 1.3 collective-permute-start.29
  97.2 1.2 collective-permute-done.29
  99.0 7.1 %bitcast_convert_fusion.2 = (f32[2,128,2048]{2,1,0:T(8,128)S(1)}, bf16[256,2048]{1,0:T(8,128)(2,1)}, f32[256,2048]{1,0:T(8,128)}, f32[256,2048]{1,0:T(8,128)}) fusion(bf16[128,2048]{1,0:T(8,128)(2,1)S(1)} %collective-permute-done.29, bf16[128,2048]{1,0:T(8,128)(2,1)S(1)} %collective-permute-done.28, f32[256]{0:T(256)S(1)} %add_rsqrt_fusion.1, ...), kind=kOutput, calls=%fused_computation.229 | convolution fusion | flops 2165833728 | bytes 16787456 | tf_op jit(solution)/shard_map/dot_general | solution.py:50
  108.1 3.1 %collective-permute-done.30 = f32[7]{0:T(128)S(1)} collective-permute-done((f32[7]{0:T(128)S(1)}, f32[7]{0:T(128)S(1)}, u32[]{:S(2)}, u32[]{:S(2)}) %collective-permute-start.30) | collective-permute-done | bytes 60 | tf_op jit(solution)/shard_map/ppermute | solution.py:128
  111.9 1.6 %collective-permute-start.31 = (f32[7]{0:T(128)S(1)}, f32[7]{0:T(128)S(1)}, u32[]{:S(2)}, u32[]{:S(2)}) collective-permute-start(f32[7]{0:T(128)S(1)} %fusion.162), channel_id=1, source_target_pairs={{0,4},{2,6},{4,0},{6,2},{8,12},{10,14},{12,8},{14,10},{1,5},{3,7},... | collective-permute-start | bytes 92 | tf_op jit(solution)/shard_map/ppermute | solution.py:128
  113.5 2.0 %collective-permute-done.31 = f32[7]{0:T(128)S(1)} collective-permute-done((f32[7]{0:T(128)S(1)}, f32[7]{0:T(128)S(1)}, u32[]{:S(2)}, u32[]{:S(2)}) %collective-permute-start.31) | collective-permute-done | bytes 60 | tf_op jit(solution)/shard_map/ppermute | solution.py:128
  115.5 2.6 %collective-permute-start.32 = (f32[7]{0:T(128)S(1)}, f32[7]{0:T(128)S(1)}, u32[]{:S(2)}, u32[]{:S(2)}) collective-permute-start(f32[7]{0:T(128)S(1)} %add.479), channel_id=1, source_target_pairs={{0,8},{2,10},{4,12},{6,14},{8,0},{10,2},{12,4},{14,6},{1,9},{3,11}... | collective-permute-start | bytes 92 | tf_op jit(solution)/shard_map/ppermute | solution.py:128
  118.1 1.9 %collective-permute-done.32 = f32[7]{0:T(128)S(1)} collective-permute-done((f32[7]{0:T(128)S(1)}, f32[7]{0:T(128)S(1)}, u32[]{:S(2)}, u32[]{:S(2)}) %collective-permute-start.32) | collective-permute-done | bytes 60 | tf_op jit(solution)/shard_map/ppermute | solution.py:128
  121.9 1.3 fusion.127
  124.4 1.3 collective-permute-start.33
  126.9 1.5 %collective-permute-start.34 = (f32[1]{0:T(128)}, f32[1]{0:T(128)}, u32[]{:S(2)}, u32[]{:S(2)}) collective-permute-start(f32[1]{0:T(128)} %bitcast.20), channel_id=1, source_target_pairs={{1,0},{3,2},{5,4},{7,6},{9,8},{11,10},{13,12},{15,14},{17,16},{19,... | collective-permute-start | bytes 20 | tf_op jit(solution)/shard_map/ppermute | solution.py:18
  128.4 7.7 %collective-permute-done.34 = f32[1]{0:T(128)} collective-permute-done((f32[1]{0:T(128)}, f32[1]{0:T(128)}, u32[]{:S(2)}, u32[]{:S(2)}) %collective-permute-start.34) | collective-permute-done | bytes 36 | tf_op jit(solution)/shard_map/ppermute | solution.py:18
  136.8 8.2 %conditional.3 = (bf16[1,2,128,2048]{3,2,1,0:T(8,128)(2,1)}) conditional(s32[]{:T(128)} %convert_element_type.61, bf16[256,2048]{1,0:T(8,128)(2,1)} %get-tuple-element.204, (bf16[256,2048]{1,0:T(8,128)(2,1)S(1)}, f32[256]{0:T(256)S(1)}, f32[]{:T(128)}, f32[]{:T(128)}, f32[256,2048]{1,0:T(8,128)}, /*index=5*/bf16[2048,2048]{1,0:T(8,128)(2,1)}, ...), branch_computations={%region_15.16_spmd, %region_16.19_spmd} | conditional | flops 2154824192 | bytes 22039568 | solution.py:254
  136.8 6.6 %fusion.122 = (f32[256]{0:T(256)S(1)}, f32[256]{0:T(256)S(1)}, f32[256,2048]{1,0:T(8,128)S(1)}) fusion(f32[256,2048]{1,0:T(8,128)S(1)} %get-tuple-element.67, f32[2048]{0:T(1024)S(1)} %bitcast.142, bf16[2048,2048]{1,0:T(8,128)(2,1)} %get-tuple-element.65, f32[256,2048]{1,0:T(8,128)} %get-tuple-element.64, bf16[256,2048]{1,0:T(8,128)(2,1)S(1)} %get-tuple-element.60), kind=kOutput, calls=%fused_computation.234 | convolution fusion | flops 2151153152 | bytes 15738880 | tf_op jit(solution)/shard_map/cond/branch_1_fun/dot_general | solution.py:57
  143.4 1.6 %fusion.1 = bf16[256,2048]{1,0:T(8,128)(2,1)} fusion(bf16[256,2048]{1,0:T(8,128)(2,1)S(1)} %get-tuple-element.60, f32[256,2048]{1,0:T(8,128)S(1)} %get-tuple-element.67, f32[256,2048]{1,0:T(8,128)S(1)} %get-tuple-element.180, f32[256]{0:T(256)S(1)} %add_rsqrt_fusion, f32[256]{0:T(256)S(1)} %get-tuple-element.181, f32[256]{0:T(256)S(1)} %get-tuple-element.182), kind=kLoop, calls=%fused_computation.5 | loop fusion | flops 3670016 | bytes 6294528 | tf_op jit(solution)/shard_map/cond/branch_1_fun/convert_element_type | solution.py:66
  (141 shorter events, 26.1 us)
Async XLA Ops:
  0.6 7.5 %copy-start.5 = (bf16[128,2048]{1,0:T(8,128)(2,1)S(1)}, bf16[128,2048]{1,0:T(8,128)(2,1)}, u32[]{:S(2)}) copy-start(bf16[128,2048]{1,0:T(8,128)(2,1)} %param.9) | copy-start | bytes 1572868
  0.6 12.3 %copy-start.2 = (bf16[2,128,2048]{2,1,0:T(8,128)(2,1)S(1)}, bf16[2,128,2048]{2,1,0:T(8,128)(2,1)}, u32[]{:S(2)}) copy-start(bf16[2,128,2048]{2,1,0:T(8,128)(2,1)} %param.8) | copy-start | bytes 3145732
  2.9 10.1 %collective-permute-start = (bf16[256,512]{1,0:T(8,128)(2,1)S(1)}, bf16[256,512]{1,0:T(8,128)(2,1)S(1)}, u32[]{:S(2)}, u32[]{:S(2)}) collective-permute-start(bf16[256,512]{1,0:T(8,128)(2,1)S(1)} %get-tuple-element.201), channel_id=1, source_target_pairs={{0,4},{4,8},{8,12},{12,14},{14,10},{10,6},{6,2},{2,0},{1,5},{5,9},... | collective-permute-start | bytes 786440 | tf_op jit(solution)/shard_map/ppermute | solution.py:113
  5.9 11.3 %collective-permute-start.7 = (bf16[256,512]{1,0:T(8,128)(2,1)}, bf16[256,512]{1,0:T(8,128)(2,1)}, u32[]{:S(2)}, u32[]{:S(2)}) collective-permute-start(bf16[256,512]{1,0:T(8,128)(2,1)} %get-tuple-element.200), channel_id=1, source_target_pairs={{4,0},{8,4},{12,8},{14,12},{10,14},{6,10},{2,6},{0,2},{5,1},{9,5},... | collective-permute-start | bytes 786440 | tf_op jit(solution)/shard_map/ppermute | solution.py:113
  5.9 13.5 %collective-permute-start.14 = (bf16[256,512]{1,0:T(8,128)(2,1)}, bf16[256,512]{1,0:T(8,128)(2,1)}, u32[]{:S(2)}, u32[]{:S(2)}) collective-permute-start(bf16[256,512]{1,0:T(8,128)(2,1)} %get-tuple-element.199), channel_id=1, source_target_pairs={{0,4},{4,8},{8,12},{12,14},{14,10},{10,6},{6,2},{2,0},{1,5},{5,9},... | collective-permute-start | bytes 786440 | tf_op jit(solution)/shard_map/ppermute | solution.py:113
  7.9 18.1 %collective-permute-start.21 = (bf16[256,512]{1,0:T(8,128)(2,1)}, bf16[256,512]{1,0:T(8,128)(2,1)S(1)}, u32[]{:S(2)}, u32[]{:S(2)}) collective-permute-start(bf16[256,512]{1,0:T(8,128)(2,1)} %get-tuple-element.198), channel_id=1, source_target_pairs={{4,0},{8,4},{12,8},{14,12},{10,14},{6,10},{2,6},{0,2},{5,1},{9,5},... | collective-permute-start | bytes 786440 | tf_op jit(solution)/shard_map/ppermute | solution.py:113
  8.1 5.6 %copy-start.10 = (f32[1,2048]{1,0:T(1,128)S(1)}, f32[1,2048]{1,0:T(1,128)}, u32[]{:S(2)}) copy-start(f32[1,2048]{1,0:T(1,128)} %param.11) | copy-start | bytes 24580
  13.0 0.7 copy-start.8
  13.7 1.2 copy-start.4
  15.8 1.1 copy-start.9
  20.6 9.2 %collective-permute-start.1 = (bf16[256,512]{1,0:T(8,128)(2,1)S(1)}, bf16[256,512]{1,0:T(8,128)(2,1)S(1)}, u32[]{:S(2)}, u32[]{:S(2)}) collective-permute-start(bf16[256,512]{1,0:T(8,128)(2,1)S(1)} %copy-done.9), channel_id=1, source_target_pairs={{0,4},{4,8},{8,12},{12,14},{14,10},{10,6},{6,2},{2,0},{1,5},{5,9},... | collective-permute-start | bytes 786440 | tf_op jit(solution)/shard_map/ppermute | solution.py:113
  22.8 9.4 %collective-permute-start.8 = (bf16[256,512]{1,0:T(8,128)(2,1)}, bf16[256,512]{1,0:T(8,128)(2,1)S(1)}, u32[]{:S(2)}, u32[]{:S(2)}) collective-permute-start(bf16[256,512]{1,0:T(8,128)(2,1)} %collective-permute-done.7), channel_id=1, source_target_pairs={{4,0},{8,4},{12,8},{14,12},{10,14},{6,10},{2,6},{0,2},{5,1},{9,5},... | collective-permute-start | bytes 786440 | tf_op jit(solution)/shard_map/ppermute | solution.py:113
  22.8 12.7 %collective-permute-start.15 = (bf16[256,512]{1,0:T(8,128)(2,1)}, bf16[256,512]{1,0:T(8,128)(2,1)S(1)}, u32[]{:S(2)}, u32[]{:S(2)}) collective-permute-start(bf16[256,512]{1,0:T(8,128)(2,1)} %collective-permute-done.14), channel_id=1, source_target_pairs={{0,4},{4,8},{8,12},{12,14},{14,10},{10,6},{6,2},{2,0},{1,5},{5,9},... | collective-permute-start | bytes 786440 | tf_op jit(solution)/shard_map/ppermute | solution.py:113
  26.0 11.8 %collective-permute-start.22 = (bf16[256,512]{1,0:T(8,128)(2,1)S(1)}, bf16[256,512]{1,0:T(8,128)(2,1)S(1)}, u32[]{:S(2)}, u32[]{:S(2)}) collective-permute-start(bf16[256,512]{1,0:T(8,128)(2,1)S(1)} %collective-permute-done.21), channel_id=1, source_target_pairs={{4,0},{8,4},{12,8},{14,12},{10,14},{6,10},{2,6},{0,2},{5,1},{9,5},... | collective-permute-start | bytes 786440 | tf_op jit(solution)/shard_map/ppermute | solution.py:113
  29.9 11.2 %collective-permute-start.2 = (bf16[256,512]{1,0:T(8,128)(2,1)S(1)}, bf16[256,512]{1,0:T(8,128)(2,1)S(1)}, u32[]{:S(2)}, u32[]{:S(2)}) collective-permute-start(bf16[256,512]{1,0:T(8,128)(2,1)S(1)} %collective-permute-done.1), channel_id=1, source_target_pairs={{0,4},{4,8},{8,12},{12,14},{14,10},{10,6},{6,2},{2,0},{1,5},{5,9},... | collective-permute-start | bytes 786440 | tf_op jit(solution)/shard_map/ppermute | solution.py:113
  32.2 11.2 %collective-permute-start.9 = (bf16[256,512]{1,0:T(8,128)(2,1)S(1)}, bf16[256,512]{1,0:T(8,128)(2,1)S(1)}, u32[]{:S(2)}, u32[]{:S(2)}) collective-permute-start(bf16[256,512]{1,0:T(8,128)(2,1)S(1)} %collective-permute-done.8), channel_id=1, source_target_pairs={{4,0},{8,4},{12,8},{14,12},{10,14},{6,10},{2,6},{0,2},{5,1},{9,5},... | collective-permute-start | bytes 786440 | tf_op jit(solution)/shard_map/ppermute | solution.py:113
  35.5 11.2 %collective-permute-start.16 = (bf16[256,512]{1,0:T(8,128)(2,1)S(1)}, bf16[256,512]{1,0:T(8,128)(2,1)S(1)}, u32[]{:S(2)}, u32[]{:S(2)}) collective-permute-start(bf16[256,512]{1,0:T(8,128)(2,1)S(1)} %collective-permute-done.15), channel_id=1, source_target_pairs={{0,4},{4,8},{8,12},{12,14},{14,10},{10,6},{6,2},{2,0},{1,5},{5,9},... | collective-permute-start | bytes 786440 | tf_op jit(solution)/shard_map/ppermute | solution.py:113
  37.8 11.2 %collective-permute-start.23 = (bf16[256,512]{1,0:T(8,128)(2,1)S(1)}, bf16[256,512]{1,0:T(8,128)(2,1)S(1)}, u32[]{:S(2)}, u32[]{:S(2)}) collective-permute-start(bf16[256,512]{1,0:T(8,128)(2,1)S(1)} %collective-permute-done.22), channel_id=1, source_target_pairs={{4,0},{8,4},{12,8},{14,12},{10,14},{6,10},{2,6},{0,2},{5,1},{9,5},... | collective-permute-start | bytes 786440 | tf_op jit(solution)/shard_map/ppermute | solution.py:113
  41.1 11.2 %collective-permute-start.3 = (bf16[256,512]{1,0:T(8,128)(2,1)S(1)}, bf16[256,512]{1,0:T(8,128)(2,1)S(1)}, u32[]{:S(2)}, u32[]{:S(2)}) collective-permute-start(bf16[256,512]{1,0:T(8,128)(2,1)S(1)} %collective-permute-done.2), channel_id=1, source_target_pairs={{0,4},{4,8},{8,12},{12,14},{14,10},{10,6},{6,2},{2,0},{1,5},{5,9},... | collective-permute-start | bytes 786440 | tf_op jit(solution)/shard_map/ppermute | solution.py:113
  43.4 11.2 %collective-permute-start.10 = (bf16[256,512]{1,0:T(8,128)(2,1)S(1)}, bf16[256,512]{1,0:T(8,128)(2,1)S(1)}, u32[]{:S(2)}, u32[]{:S(2)}) collective-permute-start(bf16[256,512]{1,0:T(8,128)(2,1)S(1)} %collective-permute-done.9), channel_id=1, source_target_pairs={{4,0},{8,4},{12,8},{14,12},{10,14},{6,10},{2,6},{0,2},{5,1},{9,5},... | collective-permute-start | bytes 786440 | tf_op jit(solution)/shard_map/ppermute | solution.py:113
  46.7 11.2 %collective-permute-start.17 = (bf16[256,512]{1,0:T(8,128)(2,1)S(1)}, bf16[256,512]{1,0:T(8,128)(2,1)S(1)}, u32[]{:S(2)}, u32[]{:S(2)}) collective-permute-start(bf16[256,512]{1,0:T(8,128)(2,1)S(1)} %collective-permute-done.16), channel_id=1, source_target_pairs={{0,4},{4,8},{8,12},{12,14},{14,10},{10,6},{6,2},{2,0},{1,5},{5,9},... | collective-permute-start | bytes 786440 | tf_op jit(solution)/shard_map/ppermute | solution.py:113
  49.0 11.2 %collective-permute-start.24 = (bf16[256,512]{1,0:T(8,128)(2,1)S(1)}, bf16[256,512]{1,0:T(8,128)(2,1)S(1)}, u32[]{:S(2)}, u32[]{:S(2)}) collective-permute-start(bf16[256,512]{1,0:T(8,128)(2,1)S(1)} %collective-permute-done.23), channel_id=1, source_target_pairs={{4,0},{8,4},{12,8},{14,12},{10,14},{6,10},{2,6},{0,2},{5,1},{9,5},... | collective-permute-start | bytes 786440 | tf_op jit(solution)/shard_map/ppermute | solution.py:113
  52.3 11.2 %collective-permute-start.4 = (bf16[256,512]{1,0:T(8,128)(2,1)S(1)}, bf16[256,512]{1,0:T(8,128)(2,1)S(1)}, u32[]{:S(2)}, u32[]{:S(2)}) collective-permute-start(bf16[256,512]{1,0:T(8,128)(2,1)S(1)} %collective-permute-done.3), channel_id=1, source_target_pairs={{0,4},{4,8},{8,12},{12,14},{14,10},{10,6},{6,2},{2,0},{1,5},{5,9},... | collective-permute-start | bytes 786440 | tf_op jit(solution)/shard_map/ppermute | solution.py:113
  54.6 11.2 %collective-permute-start.11 = (bf16[256,512]{1,0:T(8,128)(2,1)S(1)}, bf16[256,512]{1,0:T(8,128)(2,1)S(1)}, u32[]{:S(2)}, u32[]{:S(2)}) collective-permute-start(bf16[256,512]{1,0:T(8,128)(2,1)S(1)} %collective-permute-done.10), channel_id=1, source_target_pairs={{4,0},{8,4},{12,8},{14,12},{10,14},{6,10},{2,6},{0,2},{5,1},{9,5},... | collective-permute-start | bytes 786440 | tf_op jit(solution)/shard_map/ppermute | solution.py:113
  57.9 11.2 %collective-permute-start.18 = (bf16[256,512]{1,0:T(8,128)(2,1)S(1)}, bf16[256,512]{1,0:T(8,128)(2,1)S(1)}, u32[]{:S(2)}, u32[]{:S(2)}) collective-permute-start(bf16[256,512]{1,0:T(8,128)(2,1)S(1)} %collective-permute-done.17), channel_id=1, source_target_pairs={{0,4},{4,8},{8,12},{12,14},{14,10},{10,6},{6,2},{2,0},{1,5},{5,9},... | collective-permute-start | bytes 786440 | tf_op jit(solution)/shard_map/ppermute | solution.py:113
  60.3 11.2 %collective-permute-start.25 = (bf16[256,512]{1,0:T(8,128)(2,1)S(1)}, bf16[256,512]{1,0:T(8,128)(2,1)S(1)}, u32[]{:S(2)}, u32[]{:S(2)}) collective-permute-start(bf16[256,512]{1,0:T(8,128)(2,1)S(1)} %collective-permute-done.24), channel_id=1, source_target_pairs={{4,0},{8,4},{12,8},{14,12},{10,14},{6,10},{2,6},{0,2},{5,1},{9,5},... | collective-permute-start | bytes 786440 | tf_op jit(solution)/shard_map/ppermute | solution.py:113
  63.6 11.2 %collective-permute-start.5 = (bf16[256,512]{1,0:T(8,128)(2,1)S(1)}, bf16[256,512]{1,0:T(8,128)(2,1)S(1)}, u32[]{:S(2)}, u32[]{:S(2)}) collective-permute-start(bf16[256,512]{1,0:T(8,128)(2,1)S(1)} %collective-permute-done.4), channel_id=1, source_target_pairs={{0,4},{4,8},{8,12},{12,14},{14,10},{10,6},{6,2},{2,0},{1,5},{5,9},... | collective-permute-start | bytes 786440 | tf_op jit(solution)/shard_map/ppermute | solution.py:113
  65.9 11.2 %collective-permute-start.12 = (bf16[256,512]{1,0:T(8,128)(2,1)S(1)}, bf16[256,512]{1,0:T(8,128)(2,1)S(1)}, u32[]{:S(2)}, u32[]{:S(2)}) collective-permute-start(bf16[256,512]{1,0:T(8,128)(2,1)S(1)} %collective-permute-done.11), channel_id=1, source_target_pairs={{4,0},{8,4},{12,8},{14,12},{10,14},{6,10},{2,6},{0,2},{5,1},{9,5},... | collective-permute-start | bytes 786440 | tf_op jit(solution)/shard_map/ppermute | solution.py:113
  69.2 11.2 %collective-permute-start.19 = (bf16[256,512]{1,0:T(8,128)(2,1)S(1)}, bf16[256,512]{1,0:T(8,128)(2,1)S(1)}, u32[]{:S(2)}, u32[]{:S(2)}) collective-permute-start(bf16[256,512]{1,0:T(8,128)(2,1)S(1)} %collective-permute-done.18), channel_id=1, source_target_pairs={{0,4},{4,8},{8,12},{12,14},{14,10},{10,6},{6,2},{2,0},{1,5},{5,9},... | collective-permute-start | bytes 786440 | tf_op jit(solution)/shard_map/ppermute | solution.py:113
  71.5 11.2 %collective-permute-start.26 = (bf16[256,512]{1,0:T(8,128)(2,1)S(1)}, bf16[256,512]{1,0:T(8,128)(2,1)S(1)}, u32[]{:S(2)}, u32[]{:S(2)}) collective-permute-start(bf16[256,512]{1,0:T(8,128)(2,1)S(1)} %collective-permute-done.25), channel_id=1, source_target_pairs={{4,0},{8,4},{12,8},{14,12},{10,14},{6,10},{2,6},{0,2},{5,1},{9,5},... | collective-permute-start | bytes 786440 | tf_op jit(solution)/shard_map/ppermute | solution.py:113
  74.8 11.2 %collective-permute-start.6 = (bf16[256,512]{1,0:T(8,128)(2,1)S(1)}, bf16[256,512]{1,0:T(8,128)(2,1)S(1)}, u32[]{:S(2)}, u32[]{:S(2)}) collective-permute-start(bf16[256,512]{1,0:T(8,128)(2,1)S(1)} %collective-permute-done.5), channel_id=1, source_target_pairs={{0,4},{4,8},{8,12},{12,14},{14,10},{10,6},{6,2},{2,0},{1,5},{5,9},... | collective-permute-start | bytes 786440 | tf_op jit(solution)/shard_map/ppermute | solution.py:113
  77.1 10.7 %collective-permute-start.13 = (bf16[256,512]{1,0:T(8,128)(2,1)S(1)}, bf16[256,512]{1,0:T(8,128)(2,1)S(1)}, u32[]{:S(2)}, u32[]{:S(2)}) collective-permute-start(bf16[256,512]{1,0:T(8,128)(2,1)S(1)} %collective-permute-done.12), channel_id=1, source_target_pairs={{4,0},{8,4},{12,8},{14,12},{10,14},{6,10},{2,6},{0,2},{5,1},{9,5},... | collective-permute-start | bytes 786440 | tf_op jit(solution)/shard_map/ppermute | solution.py:113
  80.4 8.8 %collective-permute-start.20 = (bf16[256,512]{1,0:T(8,128)(2,1)S(1)}, bf16[256,512]{1,0:T(8,128)(2,1)S(1)}, u32[]{:S(2)}, u32[]{:S(2)}) collective-permute-start(bf16[256,512]{1,0:T(8,128)(2,1)S(1)} %collective-permute-done.19), channel_id=1, source_target_pairs={{0,4},{4,8},{8,12},{12,14},{14,10},{10,6},{6,2},{2,0},{1,5},{5,9},... | collective-permute-start | bytes 786440 | tf_op jit(solution)/shard_map/ppermute | solution.py:113
  82.7 7.9 %collective-permute-start.27 = (bf16[256,512]{1,0:T(8,128)(2,1)S(1)}, bf16[256,512]{1,0:T(8,128)(2,1)S(1)}, u32[]{:S(2)}, u32[]{:S(2)}) collective-permute-start(bf16[256,512]{1,0:T(8,128)(2,1)S(1)} %collective-permute-done.26), channel_id=1, source_target_pairs={{4,0},{8,4},{12,8},{14,12},{10,14},{6,10},{2,6},{0,2},{5,1},{9,5},... | collective-permute-start | bytes 786440 | tf_op jit(solution)/shard_map/ppermute | solution.py:113
  94.2 2.9 %collective-permute-start.28 = (bf16[128,2048]{1,0:T(8,128)(2,1)S(1)}, bf16[128,2048]{1,0:T(8,128)(2,1)S(1)}, u32[]{:S(2)}, u32[]{:S(2)}) collective-permute-start(bf16[128,2048]{1,0:T(8,128)(2,1)S(1)} %get-tuple-element.190), channel_id=1, source_target_pairs={{0,1},{2,3},{4,5},{6,7},{8,9},{10,11},{12,13},{14,15},{16,17},{18,... | collective-permute-start | bytes 1572872 | tf_op jit(solution)/shard_map/ppermute | solution.py:18
  95.6 2.8 %collective-permute-start.29 = (bf16[128,2048]{1,0:T(8,128)(2,1)S(1)}, bf16[128,2048]{1,0:T(8,128)(2,1)S(1)}, u32[]{:S(2)}, u32[]{:S(2)}) collective-permute-start(bf16[128,2048]{1,0:T(8,128)(2,1)S(1)} %get-tuple-element.191), channel_id=1, source_target_pairs={{0,1},{2,3},{4,5},{6,7},{8,9},{10,11},{12,13},{14,15},{16,17},{18,... | collective-permute-start | bytes 1572872 | tf_op jit(solution)/shard_map/ppermute | solution.py:18
  97.2 9.0 %copy-start = (bf16[2048,2048]{1,0:T(8,128)(2,1)}, bf16[2048,2048]{1,0:T(8,128)(2,1)S(1)}, u32[]{:S(2)}) copy-start(bf16[2048,2048]{1,0:T(8,128)(2,1)S(1)} %constant_dynamic-update-slice_fusion) | copy-start | bytes 25165828
  99.0 7.1 %copy-start.6 = (bf16[128,2048]{1,0:T(8,128)(2,1)S(1)}, bf16[128,2048]{1,0:T(8,128)(2,1)}, u32[]{:S(2)}) copy-start(bf16[128,2048]{1,0:T(8,128)(2,1)} %param.9) | copy-start | bytes 1572868
  106.2 17.1 %copy-start.3 = (f32[128,2048]{1,0:T(8,128)S(1)}, f32[128,2048]{1,0:T(8,128)}, u32[]{:S(2)}) copy-start(f32[128,2048]{1,0:T(8,128)} %convert_element_type.70) | copy-start | bytes 3145732
  107.6 3.6 %collective-permute-start.30 = (f32[7]{0:T(128)S(1)}, f32[7]{0:T(128)S(1)}, u32[]{:S(2)}, u32[]{:S(2)}) collective-permute-start(f32[7]{0:T(128)S(1)} %pad_maximum_fusion.2), channel_id=1, source_target_pairs={{0,2},{2,0},{4,6},{6,4},{8,10},{10,8},{12,14},{14,12},{1,3},{3,1},... | collective-permute-start | bytes 92 | tf_op jit(solution)/shard_map/ppermute | solution.py:128
  111.9 3.6 %collective-permute-start.31 = (f32[7]{0:T(128)S(1)}, f32[7]{0:T(128)S(1)}, u32[]{:S(2)}, u32[]{:S(2)}) collective-permute-start(f32[7]{0:T(128)S(1)} %fusion.162), channel_id=1, source_target_pairs={{0,4},{2,6},{4,0},{6,2},{8,12},{10,14},{12,8},{14,10},{1,5},{3,7},... | collective-permute-start | bytes 92 | tf_op jit(solution)/shard_map/ppermute | solution.py:128
  115.5 4.5 %collective-permute-start.32 = (f32[7]{0:T(128)S(1)}, f32[7]{0:T(128)S(1)}, u32[]{:S(2)}, u32[]{:S(2)}) collective-permute-start(f32[7]{0:T(128)S(1)} %add.479), channel_id=1, source_target_pairs={{0,8},{2,10},{4,12},{6,14},{8,0},{10,2},{12,4},{14,6},{1,9},{3,11}... | collective-permute-start | bytes 92 | tf_op jit(solution)/shard_map/ppermute | solution.py:128
  124.4 12.4 %collective-permute-start.33 = (bf16[256,2048]{1,0:T(8,128)(2,1)}, bf16[256,2048]{1,0:T(8,128)(2,1)S(1)}, u32[]{:S(2)}, u32[]{:S(2)}) collective-permute-start(bf16[256,2048]{1,0:T(8,128)(2,1)} %get-tuple-element.204), channel_id=1, source_target_pairs={{1,0},{3,2},{5,4},{7,6},{9,8},{11,10},{13,12},{15,14},{17,16},{19,... | collective-permute-start | bytes 3145736 | tf_op jit(solution)/shard_map/ppermute | solution.py:18
  126.9 9.2 %collective-permute-start.34 = (f32[1]{0:T(128)}, f32[1]{0:T(128)}, u32[]{:S(2)}, u32[]{:S(2)}) collective-permute-start(f32[1]{0:T(128)} %bitcast.20), channel_id=1, source_target_pairs={{1,0},{3,2},{5,4},{7,6},{9,8},{11,10},{13,12},{15,14},{17,16},{19,... | collective-permute-start | bytes 20 | tf_op jit(solution)/shard_map/ppermute | solution.py:18

commit v15 on v10

--- a/solution.py
+++ b/solution.py
@@ -52,8 +52,10 @@
     return (output, unit_rows, inv_std, pre_act)
 
 
-def section_backward(grad_out, gain, weight, unit_rows, inv_std, slope):
+def section_backward(grad_out, gain, weight, unit_rows, inv_std, slope, split=False):
     grad_pre = (grad_out * slope).astype(jnp.bfloat16)
+    if split:
+        grad_pre = lax.optimization_barrier(grad_pre)
     grad_norm = lax.dot_general(
         grad_pre, weight, (((1,), (1,)), ((), ())), preferred_element_type=jnp.float32
     )
@@ -245,7 +247,7 @@
     energy_out = jnp.where(on_first, energy_peer, energy_arr)
     grads = lax.cond(
         on_first,
-        lambda: section_backward(back.astype(jnp.float32), gain, weight, fa[1], fa[2], slope_a),
+        lambda: section_backward(back.astype(jnp.float32), gain, weight, fa[1], fa[2], slope_a, True),
         lambda: da,
     )
     grads = grads.reshape(members, tok_rows, width)

time: 141 us -> 144 us (1.021)
  waiting for transfers between devices: 54.8 us -> 58.6 us
  other arithmetic: 11.8 us -> 14.3 us
  matrix products: 21.9 us -> 20.2 us
  local copies, waits for them, and re-layouts: 9.36 us -> 7.77 us
    ppermute x28, waiting for transfers between devices: 38.2 us -> 42.3 us  [ring_gather(): parts[j] = lax.ppermute(parts[j], axis, cw if clockwise else ccw)]
    convert_element_type x0 -> x1, other arithmetic: none -> 2.02 us  [section_backward(): grad_pre = (grad_out * slope).astype(jnp.bfloat16)]
  transfers between devices with their start and end apart: 34 -> 34, of which waited for: 27 -> 23; matrix products, arithmetic and copies ran while one was open for 11% -> 10% of each run, Pallas kernels for 0% -> 0%
where the time goes in v15:
time: 144 us
  waiting for transfers between devices  58.6 us (41%)
  starting transfers between devices  38.6 us (27%)
  matrix products  20.2 us (14%)
  other arithmetic  14.3 us (10%)
  local copies, waits for them, and re-layouts  7.77 us (5%)
  between operations  4.54 us (3%)
    ppermute x28, waiting for transfers between devices, ring_gather(): parts[j] = lax.ppermute(parts[j], axis, cw if clockwise else ccw)  42.3 us
    ppermute x28, starting transfers between devices, ring_gather(): parts[j] = lax.ppermute(parts[j], axis, cw if clockwise else ccw)  29.8 us
    ppermute x3, waiting for transfers between devices, shifted(): return lax.ppermute(x, axis, pairs)  9.33 us
    dot_general x28, matrix products, on_piece(): term = jnp.dot(lhs, piece, preferred_element_type=jnp.float32)  7.32 us
    ppermute x3, waiting for transfers between devices, tree_sum(): v = v + lax.ppermute(v, axis, [(i, i ^ b) for i in range(n)])  6.97 us
    dot_general x1, matrix products, section_forward(): pre_act = jnp.dot(normed, weight, preferred_element_type=jnp.float32)  6.05 us
    dot_general x1, matrix products, section_backward(): lax.dot_general(grad_pre, weight, (((1,), (1,)), ((), ())), preferred_ele...  5.93 us
    ppermute x3, starting transfers between devices, tree_sum(): v = v + lax.ppermute(v, axis, [(i, i ^ b) for i in range(n)])  4.64 us
  transfers between devices with their start and end apart: 34, of which 23 were waited for; matrix products, arithmetic and copies ran while one was open for 10% of the time, Pallas kernels for 0%

profile of v15, /device:TPU:0, one launch (start us, length us, event | category | flops | bytes accessed | tf_op | source)
XLA Modules:
  0.0 144.1 jit_solution(11043455642551726575)
XLA Ops:
  0.6 2.3 %fusion.120 = (bf16[256,512]{1,0:T(8,128)(2,1)}, bf16[256,512]{1,0:T(8,128)(2,1)}, bf16[256,512]{1,0:T(8,128)(2,1)}, bf16[256,512]{1,0:T(8,128)(2,1)}) fusion(bf16[256,2048]{1,0:T(8,128)(2,1)} %bitcast.131), kind=kLoop, calls=%fused_computation.228 | loop fusion | bytes 2097152 | tf_op jit(solution)/shard_map/slice | solution.py:108
  2.9 3.1 %collective-permute-start = (bf16[256,512]{1,0:T(8,128)(2,1)}, bf16[256,512]{1,0:T(8,128)(2,1)}, u32[]{:S(2)}, u32[]{:S(2)}) collective-permute-start(bf16[256,512]{1,0:T(8,128)(2,1)} %get-tuple-element.199), channel_id=1, source_target_pairs={{0,4},{4,8},{8,12},{12,14},{14,10},{10,6},{6,2},{2,0},{1,5},{5,9},... | collective-permute-start | bytes 786440 | tf_op jit(solution)/shard_map/ppermute | solution.py:115
  6.0 2.0 %collective-permute-start.14 = (bf16[256,512]{1,0:T(8,128)(2,1)}, bf16[256,512]{1,0:T(8,128)(2,1)S(1)}, u32[]{:S(2)}, u32[]{:S(2)}) collective-permute-start(bf16[256,512]{1,0:T(8,128)(2,1)} %get-tuple-element.197), channel_id=1, source_target_pairs={{0,4},{4,8},{8,12},{12,14},{14,10},{10,6},{6,2},{2,0},{1,5},{5,9},... | collective-permute-start | bytes 786440 | tf_op jit(solution)/shard_map/ppermute | solution.py:115
  9.2 4.1 %collective-permute-done = bf16[256,512]{1,0:T(8,128)(2,1)} collective-permute-done((bf16[256,512]{1,0:T(8,128)(2,1)}, bf16[256,512]{1,0:T(8,128)(2,1)}, u32[]{:S(2)}, u32[]{:S(2)}) %collective-permute-start) | collective-permute-done | bytes 262176 | tf_op jit(solution)/shard_map/ppermute | solution.py:115
  14.1 1.8 %fusion.8 = (f32[256,2048]{1,0:T(8,128)}, bf16[256,2048]{1,0:T(8,128)(2,1)S(1)}) fusion(bf16[256,2048]{1,0:T(8,128)(2,1)S(1)} %bitcast.129, f32[256]{0:T(256)S(1)} %add_rsqrt_fusion.2, f32[256]{0:T(256)S(1)} %broadcast_multiply_fusion.5, f32[2048]{0:T(1024)S(1)} %bitcast.140), kind=kLoop, calls=%fused_computation.43 | loop fusion | flops 2621440 | bytes 4204544 | tf_op jit(solution)/shard_map/mul | solution.py:38
  16.8 2.2 %collective-permute-start.1 = (bf16[256,512]{1,0:T(8,128)(2,1)}, bf16[256,512]{1,0:T(8,128)(2,1)S(1)}, u32[]{:S(2)}, u32[]{:S(2)}) collective-permute-start(bf16[256,512]{1,0:T(8,128)(2,1)} %collective-permute-done), channel_id=1, source_target_pairs={{0,4},{4,8},{8,12},{12,14},{14,10},{10,6},{6,2},{2,0},{1,5},{5,9},... | collective-permute-start | bytes 786440 | tf_op jit(solution)/shard_map/ppermute | solution.py:115
  21.0 1.2 fusion.71
  22.5 2.1 %collective-permute-start.15 = (bf16[256,512]{1,0:T(8,128)(2,1)S(1)}, bf16[256,512]{1,0:T(8,128)(2,1)S(1)}, u32[]{:S(2)}, u32[]{:S(2)}) collective-permute-start(bf16[256,512]{1,0:T(8,128)(2,1)S(1)} %collective-permute-done.14), channel_id=1, source_target_pairs={{0,4},{4,8},{8,12},{12,14},{14,10},{10,6},{6,2},{2,0},{1,5},{5,9},... | collective-permute-start | bytes 786440 | tf_op jit(solution)/shard_map/ppermute | solution.py:115
  25.2 2.1 %collective-permute-start.2 = (bf16[256,512]{1,0:T(8,128)(2,1)S(1)}, bf16[256,512]{1,0:T(8,128)(2,1)S(1)}, u32[]{:S(2)}, u32[]{:S(2)}) collective-permute-start(bf16[256,512]{1,0:T(8,128)(2,1)S(1)} %collective-permute-done.1), channel_id=1, source_target_pairs={{0,4},{4,8},{8,12},{12,14},{14,10},{10,6},{6,2},{2,0},{1,5},{5,9},... | collective-permute-start | bytes 786440 | tf_op jit(solution)/shard_map/ppermute | solution.py:115
  27.2 4.2 %collective-permute-done.8 = bf16[256,512]{1,0:T(8,128)(2,1)S(1)} collective-permute-done((bf16[256,512]{1,0:T(8,128)(2,1)S(1)}, bf16[256,512]{1,0:T(8,128)(2,1)S(1)}, u32[]{:S(2)}, u32[]{:S(2)}) %collective-permute-start.8) | collective-permute-done | bytes 262176 | tf_op jit(solution)/shard_map/ppermute | solution.py:115
  31.7 2.0 %collective-permute-start.16 = (bf16[256,512]{1,0:T(8,128)(2,1)S(1)}, bf16[256,512]{1,0:T(8,128)(2,1)S(1)}, u32[]{:S(2)}, u32[]{:S(2)}) collective-permute-start(bf16[256,512]{1,0:T(8,128)(2,1)S(1)} %collective-permute-done.15), channel_id=1, source_target_pairs={{0,4},{4,8},{8,12},{12,14},{14,10},{10,6},{6,2},{2,0},{1,5},{5,9},... | collective-permute-start | bytes 786440 | tf_op jit(solution)/shard_map/ppermute | solution.py:115
  33.8 3.2 %collective-permute-done.22 = bf16[256,512]{1,0:T(8,128)(2,1)S(1)} collective-permute-done((bf16[256,512]{1,0:T(8,128)(2,1)S(1)}, bf16[256,512]{1,0:T(8,128)(2,1)S(1)}, u32[]{:S(2)}, u32[]{:S(2)}) %collective-permute-start.22) | collective-permute-done | bytes 262176 | tf_op jit(solution)/shard_map/ppermute | solution.py:115
  38.0 2.1 %collective-permute-start.3 = (bf16[256,512]{1,0:T(8,128)(2,1)S(1)}, bf16[256,512]{1,0:T(8,128)(2,1)S(1)}, u32[]{:S(2)}, u32[]{:S(2)}) collective-permute-start(bf16[256,512]{1,0:T(8,128)(2,1)S(1)} %collective-permute-done.2), channel_id=1, source_target_pairs={{0,4},{4,8},{8,12},{12,14},{14,10},{10,6},{6,2},{2,0},{1,5},{5,9},... | collective-permute-start | bytes 786440 | tf_op jit(solution)/shard_map/ppermute | solution.py:115
  40.1 2.5 %collective-permute-done.9 = bf16[256,512]{1,0:T(8,128)(2,1)S(1)} collective-permute-done((bf16[256,512]{1,0:T(8,128)(2,1)S(1)}, bf16[256,512]{1,0:T(8,128)(2,1)S(1)}, u32[]{:S(2)}, u32[]{:S(2)}) %collective-permute-start.9) | collective-permute-done | bytes 262176 | tf_op jit(solution)/shard_map/ppermute | solution.py:115
  43.0 2.0 %collective-permute-start.17 = (bf16[256,512]{1,0:T(8,128)(2,1)S(1)}, bf16[256,512]{1,0:T(8,128)(2,1)S(1)}, u32[]{:S(2)}, u32[]{:S(2)}) collective-permute-start(bf16[256,512]{1,0:T(8,128)(2,1)S(1)} %collective-permute-done.16), channel_id=1, source_target_pairs={{0,4},{4,8},{8,12},{12,14},{14,10},{10,6},{6,2},{2,0},{1,5},{5,9},... | collective-permute-start | bytes 786440 | tf_op jit(solution)/shard_map/ppermute | solution.py:115
  45.1 3.2 %collective-permute-done.23 = bf16[256,512]{1,0:T(8,128)(2,1)S(1)} collective-permute-done((bf16[256,512]{1,0:T(8,128)(2,1)S(1)}, bf16[256,512]{1,0:T(8,128)(2,1)S(1)}, u32[]{:S(2)}, u32[]{:S(2)}) %collective-permute-start.23) | collective-permute-done | bytes 262176 | tf_op jit(solution)/shard_map/ppermute | solution.py:115
  49.2 2.1 %collective-permute-start.4 = (bf16[256,512]{1,0:T(8,128)(2,1)S(1)}, bf16[256,512]{1,0:T(8,128)(2,1)S(1)}, u32[]{:S(2)}, u32[]{:S(2)}) collective-permute-start(bf16[256,512]{1,0:T(8,128)(2,1)S(1)} %collective-permute-done.3), channel_id=1, source_target_pairs={{0,4},{4,8},{8,12},{12,14},{14,10},{10,6},{6,2},{2,0},{1,5},{5,9},... | collective-permute-start | bytes 786440 | tf_op jit(solution)/shard_map/ppermute | solution.py:115
  51.3 2.6 %collective-permute-done.10 = bf16[256,512]{1,0:T(8,128)(2,1)S(1)} collective-permute-done((bf16[256,512]{1,0:T(8,128)(2,1)S(1)}, bf16[256,512]{1,0:T(8,128)(2,1)S(1)}, u32[]{:S(2)}, u32[]{:S(2)}) %collective-permute-start.10) | collective-permute-done | bytes 262176 | tf_op jit(solution)/shard_map/ppermute | solution.py:115
  54.2 2.0 %collective-permute-start.18 = (bf16[256,512]{1,0:T(8,128)(2,1)S(1)}, bf16[256,512]{1,0:T(8,128)(2,1)S(1)}, u32[]{:S(2)}, u32[]{:S(2)}) collective-permute-start(bf16[256,512]{1,0:T(8,128)(2,1)S(1)} %collective-permute-done.17), channel_id=1, source_target_pairs={{0,4},{4,8},{8,12},{12,14},{14,10},{10,6},{6,2},{2,0},{1,5},{5,9},... | collective-permute-start | bytes 786440 | tf_op jit(solution)/shard_map/ppermute | solution.py:115
  56.2 3.3 %collective-permute-done.24 = bf16[256,512]{1,0:T(8,128)(2,1)S(1)} collective-permute-done((bf16[256,512]{1,0:T(8,128)(2,1)S(1)}, bf16[256,512]{1,0:T(8,128)(2,1)S(1)}, u32[]{:S(2)}, u32[]{:S(2)}) %collective-permute-start.24) | collective-permute-done | bytes 262176 | tf_op jit(solution)/shard_map/ppermute | solution.py:115
  60.6 2.1 %collective-permute-start.5 = (bf16[256,512]{1,0:T(8,128)(2,1)S(1)}, bf16[256,512]{1,0:T(8,128)(2,1)S(1)}, u32[]{:S(2)}, u32[]{:S(2)}) collective-permute-start(bf16[256,512]{1,0:T(8,128)(2,1)S(1)} %collective-permute-done.4), channel_id=1, source_target_pairs={{0,4},{4,8},{8,12},{12,14},{14,10},{10,6},{6,2},{2,0},{1,5},{5,9},... | collective-permute-start | bytes 786440 | tf_op jit(solution)/shard_map/ppermute | solution.py:115
  62.7 2.4 %collective-permute-done.11 = bf16[256,512]{1,0:T(8,128)(2,1)S(1)} collective-permute-done((bf16[256,512]{1,0:T(8,128)(2,1)S(1)}, bf16[256,512]{1,0:T(8,128)(2,1)S(1)}, u32[]{:S(2)}, u32[]{:S(2)}) %collective-permute-start.11) | collective-permute-done | bytes 262176 | tf_op jit(solution)/shard_map/ppermute | solution.py:115
  65.5 2.0 %collective-permute-start.19 = (bf16[256,512]{1,0:T(8,128)(2,1)S(1)}, bf16[256,512]{1,0:T(8,128)(2,1)S(1)}, u32[]{:S(2)}, u32[]{:S(2)}) collective-permute-start(bf16[256,512]{1,0:T(8,128)(2,1)S(1)} %collective-permute-done.18), channel_id=1, source_target_pairs={{0,4},{4,8},{8,12},{12,14},{14,10},{10,6},{6,2},{2,0},{1,5},{5,9},... | collective-permute-start | bytes 786440 | tf_op jit(solution)/shard_map/ppermute | solution.py:115
  67.5 3.2 %collective-permute-done.25 = bf16[256,512]{1,0:T(8,128)(2,1)S(1)} collective-permute-done((bf16[256,512]{1,0:T(8,128)(2,1)S(1)}, bf16[256,512]{1,0:T(8,128)(2,1)S(1)}, u32[]{:S(2)}, u32[]{:S(2)}) %collective-permute-start.25) | collective-permute-done | bytes 262176 | tf_op jit(solution)/shard_map/ppermute | solution.py:115
  71.8 2.1 %collective-permute-start.6 = (bf16[256,512]{1,0:T(8,128)(2,1)S(1)}, bf16[256,512]{1,0:T(8,128)(2,1)S(1)}, u32[]{:S(2)}, u32[]{:S(2)}) collective-permute-start(bf16[256,512]{1,0:T(8,128)(2,1)S(1)} %collective-permute-done.5), channel_id=1, source_target_pairs={{0,4},{4,8},{8,12},{12,14},{14,10},{10,6},{6,2},{2,0},{1,5},{5,9},... | collective-permute-start | bytes 786440 | tf_op jit(solution)/shard_map/ppermute | solution.py:115
  73.8 2.5 %collective-permute-done.12 = bf16[256,512]{1,0:T(8,128)(2,1)S(1)} collective-permute-done((bf16[256,512]{1,0:T(8,128)(2,1)S(1)}, bf16[256,512]{1,0:T(8,128)(2,1)S(1)}, u32[]{:S(2)}, u32[]{:S(2)}) %collective-permute-start.12) | collective-permute-done | bytes 262176 | tf_op jit(solution)/shard_map/ppermute | solution.py:115
  76.7 2.0 %collective-permute-start.20 = (bf16[256,512]{1,0:T(8,128)(2,1)S(1)}, bf16[256,512]{1,0:T(8,128)(2,1)S(1)}, u32[]{:S(2)}, u32[]{:S(2)}) collective-permute-start(bf16[256,512]{1,0:T(8,128)(2,1)S(1)} %collective-permute-done.19), channel_id=1, source_target_pairs={{0,4},{4,8},{8,12},{12,14},{14,10},{10,6},{6,2},{2,0},{1,5},{5,9},... | collective-permute-start | bytes 786440 | tf_op jit(solution)/shard_map/ppermute | solution.py:115
  78.7 3.2 %collective-permute-done.26 = bf16[256,512]{1,0:T(8,128)(2,1)S(1)} collective-permute-done((bf16[256,512]{1,0:T(8,128)(2,1)S(1)}, bf16[256,512]{1,0:T(8,128)(2,1)S(1)}, u32[]{:S(2)}, u32[]{:S(2)}) %collective-permute-start.26) | collective-permute-done | bytes 262176 | tf_op jit(solution)/shard_map/ppermute | solution.py:115
  83.1 3.8 %collective-permute-done.13 = bf16[256,512]{1,0:T(8,128)(2,1)S(1)} collective-permute-done((bf16[256,512]{1,0:T(8,128)(2,1)S(1)}, bf16[256,512]{1,0:T(8,128)(2,1)S(1)}, u32[]{:S(2)}, u32[]{:S(2)}) %collective-permute-start.13) | collective-permute-done | bytes 262176 | tf_op jit(solution)/shard_map/ppermute | solution.py:115
  87.5 2.3 %collective-permute-done.27 = bf16[256,512]{1,0:T(8,128)(2,1)S(1)} collective-permute-done((bf16[256,512]{1,0:T(8,128)(2,1)S(1)}, bf16[256,512]{1,0:T(8,128)(2,1)S(1)}, u32[]{:S(2)}, u32[]{:S(2)}) %collective-permute-start.27) | collective-permute-done | bytes 262176 | tf_op jit(solution)/shard_map/ppermute | solution.py:115
  90.0 2.5 %fusion.22 = (f32[256,2048]{1,0:T(8,128)}, bf16[256,2048]{1,0:T(8,128)(2,1)S(1)}) fusion(f32[256,512]{1,0:T(8,128)S(1)} %fusion.26, f32[256,512]{1,0:T(8,128)S(1)} %fusion.27, f32[256,512]{1,0:T(8,128)S(1)} %fusion.28, f32[256,512]{1,0:T(8,128)S(1)} %fusion.29, bf16[256,2048]{1,0:T(8,128)(2,1)S(1)} %bitcast.130), kind=kLoop, calls=%fused_computation.57 | loop fusion | flops 12582912 | bytes 6291456 | tf_op jit(solution)/shard_map/add | solution.py:28
  92.5 1.5 %collective-permute-start.28 = (bf16[256,2048]{1,0:T(8,128)(2,1)S(1)}, bf16[256,2048]{1,0:T(8,128)(2,1)S(1)}, u32[]{:S(2)}, u32[]{:S(2)}) collective-permute-start(bf16[256,2048]{1,0:T(8,128)(2,1)S(1)} %get-tuple-element.192), channel_id=1, source_target_pairs={{0,1},{2,3},{4,5},{6,7},{8,9},{10,11},{12,13},{14,15},{16,17},{18,... | collective-permute-start | bytes 3145736 | tf_op jit(solution)/shard_map/ppermute | solution.py:18
  94.5 1.6 %collective-permute-done.28 = bf16[256,2048]{1,0:T(8,128)(2,1)S(1)} collective-permute-done((bf16[256,2048]{1,0:T(8,128)(2,1)S(1)}, bf16[256,2048]{1,0:T(8,128)(2,1)S(1)}, u32[]{:S(2)}, u32[]{:S(2)}) %collective-permute-start.28) | collective-permute-done | bytes 1048608 | tf_op jit(solution)/shard_map/ppermute | solution.py:18
  96.7 6.0 %bitcast_convert_fusion.2 = (f32[2,128,2048]{2,1,0:T(8,128)S(1)}, bf16[256,2048]{1,0:T(8,128)(2,1)}, f32[256,2048]{1,0:T(8,128)}, f32[256,2048]{1,0:T(8,128)}) fusion(bf16[256,2048]{1,0:T(8,128)(2,1)S(1)} %collective-permute-done.28, f32[256]{0:T(256)S(1)} %add_rsqrt_fusion.1, f32[256]{0:T(256)S(1)} %broadcast_multiply_fusion.4, ...), kind=kOutput, calls=%fused_computation.218 | convolution fusion | flops 2162688000 | bytes 16787456 | tf_op jit(solution)/shard_map/dot_general | solution.py:50
  104.7 3.1 %collective-permute-done.29 = f32[7]{0:T(128)S(1)} collective-permute-done((f32[7]{0:T(128)S(1)}, f32[7]{0:T(128)S(1)}, u32[]{:S(2)}, u32[]{:S(2)}) %collective-permute-start.29) | collective-permute-done | bytes 60 | tf_op jit(solution)/shard_map/ppermute | solution.py:130
  108.5 1.6 %collective-permute-start.30 = (f32[7]{0:T(128)S(1)}, f32[7]{0:T(128)S(1)}, u32[]{:S(2)}, u32[]{:S(2)}) collective-permute-start(f32[7]{0:T(128)S(1)} %fusion.154), channel_id=1, source_target_pairs={{0,4},{2,6},{4,0},{6,2},{8,12},{10,14},{12,8},{14,10},{1,5},{3,7},... | collective-permute-start | bytes 92 | tf_op jit(solution)/shard_map/ppermute | solution.py:130
  110.1 2.0 %collective-permute-done.30 = f32[7]{0:T(128)S(1)} collective-permute-done((f32[7]{0:T(128)S(1)}, f32[7]{0:T(128)S(1)}, u32[]{:S(2)}, u32[]{:S(2)}) %collective-permute-start.30) | collective-permute-done | bytes 60 | tf_op jit(solution)/shard_map/ppermute | solution.py:130
  112.1 2.6 %collective-permute-start.31 = (f32[7]{0:T(128)S(1)}, f32[7]{0:T(128)S(1)}, u32[]{:S(2)}, u32[]{:S(2)}) collective-permute-start(f32[7]{0:T(128)S(1)} %add.463), channel_id=1, source_target_pairs={{0,8},{2,10},{4,12},{6,14},{8,0},{10,2},{12,4},{14,6},{1,9},{3,11}... | collective-permute-start | bytes 92 | tf_op jit(solution)/shard_map/ppermute | solution.py:130
  114.7 1.9 %collective-permute-done.31 = f32[7]{0:T(128)S(1)} collective-permute-done((f32[7]{0:T(128)S(1)}, f32[7]{0:T(128)S(1)}, u32[]{:S(2)}, u32[]{:S(2)}) %collective-permute-start.31) | collective-permute-done | bytes 60 | tf_op jit(solution)/shard_map/ppermute | solution.py:130
  118.6 1.3 fusion.118
  120.0 1.1 conditional.2
  121.1 1.3 collective-permute-start.32
  123.6 1.3 collective-permute-start.33
  124.9 7.7 %collective-permute-done.33 = f32[1]{0:T(128)} collective-permute-done((f32[1]{0:T(128)}, f32[1]{0:T(128)}, u32[]{:S(2)}, u32[]{:S(2)}) %collective-permute-start.33) | collective-permute-done | bytes 36 | tf_op jit(solution)/shard_map/ppermute | solution.py:18
  133.2 9.7 %conditional.3 = (bf16[1,2,128,2048]{3,2,1,0:T(8,128)(2,1)}) conditional(s32[]{:T(128)} %convert_element_type.58, bf16[256,2048]{1,0:T(8,128)(2,1)} %get-tuple-element.202, (bf16[256,2048]{1,0:T(8,128)(2,1)S(1)}, f32[256]{0:T(256)S(1)}, f32[]{:T(128)}, f32[]{:T(128)}, f32[256,2048]{1,0:T(8,128)}, /*index=5*/bf16[2048,2048]{1,0:T(8,128)(2,1)}, ...), branch_computations={%region_15.16_spmd, %region_16.19_spmd} | conditional | flops 2154824192 | bytes 32525356 | solution.py:248
  133.3 2.0 %fusion = bf16[256,2048]{1,0:T(8,128)(2,1)S(1)} fusion(f32[256,2048]{1,0:T(8,128)} %get-tuple-element.64, bf16[256,2048]{1,0:T(8,128)(2,1)S(1)} %get-tuple-element.60), kind=kLoop, calls=%fused_computation.4 | loop fusion | flops 1572864 | bytes 4194304 | tf_op jit(solution)/shard_map/cond/branch_1_fun/convert_element_type | solution.py:56
  135.5 5.9 %fusion.113 = (f32[256]{0:T(256)S(1)}, f32[256]{0:T(256)S(1)}, f32[256,2048]{1,0:T(8,128)S(1)}) fusion(f32[256,2048]{1,0:T(8,128)S(1)} %copy-done.4, f32[2048]{0:T(1024)S(1)} %bitcast.143, bf16[256,2048]{1,0:T(8,128)(2,1)S(1)} %fusion, bf16[2048,2048]{1,0:T(8,128)(2,1)} %get-tuple-element.65), kind=kOutput, calls=%fused_computation.223 | convolution fusion | flops 2149580288 | bytes 13641728 | tf_op jit(solution)/shard_map/cond/branch_1_fun/dot_general | solution.py:59
  141.4 1.5 %fusion.1 = bf16[256,2048]{1,0:T(8,128)(2,1)} fusion(bf16[256,2048]{1,0:T(8,128)(2,1)S(1)} %get-tuple-element.60, f32[256,2048]{1,0:T(8,128)S(1)} %copy-done.4, f32[256,2048]{1,0:T(8,128)S(1)} %get-tuple-element.180, f32[256]{0:T(256)S(1)} %add_rsqrt_fusion, f32[256]{0:T(256)S(1)} %get-tuple-element.181, f32[256]{0:T(256)S(1)} %get-tuple-element.182), kind=kLoop, calls=%fused_computation.5 | loop fusion | flops 3670016 | bytes 6294528 | tf_op jit(solution)/shard_map/cond/branch_1_fun/convert_element_type | solution.py:68
  (132 shorter events, 20.1 us)
Async XLA Ops:
  0.6 7.5 %copy-start.5 = (bf16[128,2048]{1,0:T(8,128)(2,1)S(1)}, bf16[128,2048]{1,0:T(8,128)(2,1)}, u32[]{:S(2)}) copy-start(bf16[128,2048]{1,0:T(8,128)(2,1)} %param.9) | copy-start | bytes 1572868
  0.6 12.7 %copy-start = (bf16[2,128,2048]{2,1,0:T(8,128)(2,1)S(1)}, bf16[2,128,2048]{2,1,0:T(8,128)(2,1)}, u32[]{:S(2)}) copy-start(bf16[2,128,2048]{2,1,0:T(8,128)(2,1)} %param.8) | copy-start | bytes 3145732
  2.9 10.4 %collective-permute-start = (bf16[256,512]{1,0:T(8,128)(2,1)}, bf16[256,512]{1,0:T(8,128)(2,1)}, u32[]{:S(2)}, u32[]{:S(2)}) collective-permute-start(bf16[256,512]{1,0:T(8,128)(2,1)} %get-tuple-element.199), channel_id=1, source_target_pairs={{0,4},{4,8},{8,12},{12,14},{14,10},{10,6},{6,2},{2,0},{1,5},{5,9},... | collective-permute-start | bytes 786440 | tf_op jit(solution)/shard_map/ppermute | solution.py:115
  6.0 16.2 %collective-permute-start.7 = (bf16[256,512]{1,0:T(8,128)(2,1)}, bf16[256,512]{1,0:T(8,128)(2,1)S(1)}, u32[]{:S(2)}, u32[]{:S(2)}) collective-permute-start(bf16[256,512]{1,0:T(8,128)(2,1)} %get-tuple-element.198), channel_id=1, source_target_pairs={{4,0},{8,4},{12,8},{14,12},{10,14},{6,10},{2,6},{0,2},{5,1},{9,5},... | collective-permute-start | bytes 786440 | tf_op jit(solution)/shard_map/ppermute | solution.py:115
  6.0 16.5 %collective-permute-start.14 = (bf16[256,512]{1,0:T(8,128)(2,1)}, bf16[256,512]{1,0:T(8,128)(2,1)S(1)}, u32[]{:S(2)}, u32[]{:S(2)}) collective-permute-start(bf16[256,512]{1,0:T(8,128)(2,1)} %get-tuple-element.197), channel_id=1, source_target_pairs={{0,4},{4,8},{8,12},{12,14},{14,10},{10,6},{6,2},{2,0},{1,5},{5,9},... | collective-permute-start | bytes 786440 | tf_op jit(solution)/shard_map/ppermute | solution.py:115
  8.0 16.8 %collective-permute-start.21 = (bf16[256,512]{1,0:T(8,128)(2,1)}, bf16[256,512]{1,0:T(8,128)(2,1)S(1)}, u32[]{:S(2)}, u32[]{:S(2)}) collective-permute-start(bf16[256,512]{1,0:T(8,128)(2,1)} %get-tuple-element.196), channel_id=1, source_target_pairs={{4,0},{8,4},{12,8},{14,12},{10,14},{6,10},{2,6},{0,2},{5,1},{9,5},... | collective-permute-start | bytes 786440 | tf_op jit(solution)/shard_map/ppermute | solution.py:115
  8.2 5.8 %copy-start.7 = (f32[1,2048]{1,0:T(1,128)S(1)}, f32[1,2048]{1,0:T(1,128)}, u32[]{:S(2)}) copy-start(f32[1,2048]{1,0:T(1,128)} %param.11) | copy-start | bytes 24580
  14.0 1.8 %copy-start.1 = (bf16[1,256,2048]{2,1,0:T(8,128)(2,1)S(1)}, bf16[1,256,2048]{2,1,0:T(8,128)(2,1)}, u32[]{:S(2)}) copy-start(bf16[1,256,2048]{2,1,0:T(8,128)(2,1)} %param.10) | copy-start | bytes 3145732
  16.8 8.4 %collective-permute-start.1 = (bf16[256,512]{1,0:T(8,128)(2,1)}, bf16[256,512]{1,0:T(8,128)(2,1)S(1)}, u32[]{:S(2)}, u32[]{:S(2)}) collective-permute-start(bf16[256,512]{1,0:T(8,128)(2,1)} %collective-permute-done), channel_id=1, source_target_pairs={{0,4},{4,8},{8,12},{12,14},{14,10},{10,6},{6,2},{2,0},{1,5},{5,9},... | collective-permute-start | bytes 786440 | tf_op jit(solution)/shard_map/ppermute | solution.py:115
  22.2 9.2 %collective-permute-start.8 = (bf16[256,512]{1,0:T(8,128)(2,1)S(1)}, bf16[256,512]{1,0:T(8,128)(2,1)S(1)}, u32[]{:S(2)}, u32[]{:S(2)}) collective-permute-start(bf16[256,512]{1,0:T(8,128)(2,1)S(1)} %collective-permute-done.7), channel_id=1, source_target_pairs={{4,0},{8,4},{12,8},{14,12},{10,14},{6,10},{2,6},{0,2},{5,1},{9,5},... | collective-permute-start | bytes 786440 | tf_op jit(solution)/shard_map/ppermute | solution.py:115
  22.5 9.2 %collective-permute-start.15 = (bf16[256,512]{1,0:T(8,128)(2,1)S(1)}, bf16[256,512]{1,0:T(8,128)(2,1)S(1)}, u32[]{:S(2)}, u32[]{:S(2)}) collective-permute-start(bf16[256,512]{1,0:T(8,128)(2,1)S(1)} %collective-permute-done.14), channel_id=1, source_target_pairs={{0,4},{4,8},{8,12},{12,14},{14,10},{10,6},{6,2},{2,0},{1,5},{5,9},... | collective-permute-start | bytes 786440 | tf_op jit(solution)/shard_map/ppermute | solution.py:115
  24.8 12.2 %collective-permute-start.22 = (bf16[256,512]{1,0:T(8,128)(2,1)S(1)}, bf16[256,512]{1,0:T(8,128)(2,1)S(1)}, u32[]{:S(2)}, u32[]{:S(2)}) collective-permute-start(bf16[256,512]{1,0:T(8,128)(2,1)S(1)} %collective-permute-done.21), channel_id=1, source_target_pairs={{4,0},{8,4},{12,8},{14,12},{10,14},{6,10},{2,6},{0,2},{5,1},{9,5},... | collective-permute-start | bytes 786440 | tf_op jit(solution)/shard_map/ppermute | solution.py:115
  25.2 12.8 %collective-permute-start.2 = (bf16[256,512]{1,0:T(8,128)(2,1)S(1)}, bf16[256,512]{1,0:T(8,128)(2,1)S(1)}, u32[]{:S(2)}, u32[]{:S(2)}) collective-permute-start(bf16[256,512]{1,0:T(8,128)(2,1)S(1)} %collective-permute-done.1), channel_id=1, source_target_pairs={{0,4},{4,8},{8,12},{12,14},{14,10},{10,6},{6,2},{2,0},{1,5},{5,9},... | collective-permute-start | bytes 786440 | tf_op jit(solution)/shard_map/ppermute | solution.py:115
  31.4 11.2 %collective-permute-start.9 = (bf16[256,512]{1,0:T(8,128)(2,1)S(1)}, bf16[256,512]{1,0:T(8,128)(2,1)S(1)}, u32[]{:S(2)}, u32[]{:S(2)}) collective-permute-start(bf16[256,512]{1,0:T(8,128)(2,1)S(1)} %collective-permute-done.8), channel_id=1, source_target_pairs={{4,0},{8,4},{12,8},{14,12},{10,14},{6,10},{2,6},{0,2},{5,1},{9,5},... | collective-permute-start | bytes 786440 | tf_op jit(solution)/shard_map/ppermute | solution.py:115
  31.7 11.2 %collective-permute-start.16 = (bf16[256,512]{1,0:T(8,128)(2,1)S(1)}, bf16[256,512]{1,0:T(8,128)(2,1)S(1)}, u32[]{:S(2)}, u32[]{:S(2)}) collective-permute-start(bf16[256,512]{1,0:T(8,128)(2,1)S(1)} %collective-permute-done.15), channel_id=1, source_target_pairs={{0,4},{4,8},{8,12},{12,14},{14,10},{10,6},{6,2},{2,0},{1,5},{5,9},... | collective-permute-start | bytes 786440 | tf_op jit(solution)/shard_map/ppermute | solution.py:115
  37.0 11.2 %collective-permute-start.23 = (bf16[256,512]{1,0:T(8,128)(2,1)S(1)}, bf16[256,512]{1,0:T(8,128)(2,1)S(1)}, u32[]{:S(2)}, u32[]{:S(2)}) collective-permute-start(bf16[256,512]{1,0:T(8,128)(2,1)S(1)} %collective-permute-done.22), channel_id=1, source_target_pairs={{4,0},{8,4},{12,8},{14,12},{10,14},{6,10},{2,6},{0,2},{5,1},{9,5},... | collective-permute-start | bytes 786440 | tf_op jit(solution)/shard_map/ppermute | solution.py:115
  38.0 11.2 %collective-permute-start.3 = (bf16[256,512]{1,0:T(8,128)(2,1)S(1)}, bf16[256,512]{1,0:T(8,128)(2,1)S(1)}, u32[]{:S(2)}, u32[]{:S(2)}) collective-permute-start(bf16[256,512]{1,0:T(8,128)(2,1)S(1)} %collective-permute-done.2), channel_id=1, source_target_pairs={{0,4},{4,8},{8,12},{12,14},{14,10},{10,6},{6,2},{2,0},{1,5},{5,9},... | collective-permute-start | bytes 786440 | tf_op jit(solution)/shard_map/ppermute | solution.py:115
  42.6 11.2 %collective-permute-start.10 = (bf16[256,512]{1,0:T(8,128)(2,1)S(1)}, bf16[256,512]{1,0:T(8,128)(2,1)S(1)}, u32[]{:S(2)}, u32[]{:S(2)}) collective-permute-start(bf16[256,512]{1,0:T(8,128)(2,1)S(1)} %collective-permute-done.9), channel_id=1, source_target_pairs={{4,0},{8,4},{12,8},{14,12},{10,14},{6,10},{2,6},{0,2},{5,1},{9,5},... | collective-permute-start | bytes 786440 | tf_op jit(solution)/shard_map/ppermute | solution.py:115
  43.0 11.2 %collective-permute-start.17 = (bf16[256,512]{1,0:T(8,128)(2,1)S(1)}, bf16[256,512]{1,0:T(8,128)(2,1)S(1)}, u32[]{:S(2)}, u32[]{:S(2)}) collective-permute-start(bf16[256,512]{1,0:T(8,128)(2,1)S(1)} %collective-permute-done.16), channel_id=1, source_target_pairs={{0,4},{4,8},{8,12},{12,14},{14,10},{10,6},{6,2},{2,0},{1,5},{5,9},... | collective-permute-start | bytes 786440 | tf_op jit(solution)/shard_map/ppermute | solution.py:115
  48.2 11.2 %collective-permute-start.24 = (bf16[256,512]{1,0:T(8,128)(2,1)S(1)}, bf16[256,512]{1,0:T(8,128)(2,1)S(1)}, u32[]{:S(2)}, u32[]{:S(2)}) collective-permute-start(bf16[256,512]{1,0:T(8,128)(2,1)S(1)} %collective-permute-done.23), channel_id=1, source_target_pairs={{4,0},{8,4},{12,8},{14,12},{10,14},{6,10},{2,6},{0,2},{5,1},{9,5},... | collective-permute-start | bytes 786440 | tf_op jit(solution)/shard_map/ppermute | solution.py:115
  49.2 11.3 %collective-permute-start.4 = (bf16[256,512]{1,0:T(8,128)(2,1)S(1)}, bf16[256,512]{1,0:T(8,128)(2,1)S(1)}, u32[]{:S(2)}, u32[]{:S(2)}) collective-permute-start(bf16[256,512]{1,0:T(8,128)(2,1)S(1)} %collective-permute-done.3), channel_id=1, source_target_pairs={{0,4},{4,8},{8,12},{12,14},{14,10},{10,6},{6,2},{2,0},{1,5},{5,9},... | collective-permute-start | bytes 786440 | tf_op jit(solution)/shard_map/ppermute | solution.py:115
  53.9 11.2 %collective-permute-start.11 = (bf16[256,512]{1,0:T(8,128)(2,1)S(1)}, bf16[256,512]{1,0:T(8,128)(2,1)S(1)}, u32[]{:S(2)}, u32[]{:S(2)}) collective-permute-start(bf16[256,512]{1,0:T(8,128)(2,1)S(1)} %collective-permute-done.10), channel_id=1, source_target_pairs={{4,0},{8,4},{12,8},{14,12},{10,14},{6,10},{2,6},{0,2},{5,1},{9,5},... | collective-permute-start | bytes 786440 | tf_op jit(solution)/shard_map/ppermute | solution.py:115
  54.2 11.2 %collective-permute-start.18 = (bf16[256,512]{1,0:T(8,128)(2,1)S(1)}, bf16[256,512]{1,0:T(8,128)(2,1)S(1)}, u32[]{:S(2)}, u32[]{:S(2)}) collective-permute-start(bf16[256,512]{1,0:T(8,128)(2,1)S(1)} %collective-permute-done.17), channel_id=1, source_target_pairs={{0,4},{4,8},{8,12},{12,14},{14,10},{10,6},{6,2},{2,0},{1,5},{5,9},... | collective-permute-start | bytes 786440 | tf_op jit(solution)/shard_map/ppermute | solution.py:115
  59.5 11.2 %collective-permute-start.25 = (bf16[256,512]{1,0:T(8,128)(2,1)S(1)}, bf16[256,512]{1,0:T(8,128)(2,1)S(1)}, u32[]{:S(2)}, u32[]{:S(2)}) collective-permute-start(bf16[256,512]{1,0:T(8,128)(2,1)S(1)} %collective-permute-done.24), channel_id=1, source_target_pairs={{4,0},{8,4},{12,8},{14,12},{10,14},{6,10},{2,6},{0,2},{5,1},{9,5},... | collective-permute-start | bytes 786440 | tf_op jit(solution)/shard_map/ppermute | solution.py:115
  60.6 11.2 %collective-permute-start.5 = (bf16[256,512]{1,0:T(8,128)(2,1)S(1)}, bf16[256,512]{1,0:T(8,128)(2,1)S(1)}, u32[]{:S(2)}, u32[]{:S(2)}) collective-permute-start(bf16[256,512]{1,0:T(8,128)(2,1)S(1)} %collective-permute-done.4), channel_id=1, source_target_pairs={{0,4},{4,8},{8,12},{12,14},{14,10},{10,6},{6,2},{2,0},{1,5},{5,9},... | collective-permute-start | bytes 786440 | tf_op jit(solution)/shard_map/ppermute | solution.py:115
  65.1 11.2 %collective-permute-start.12 = (bf16[256,512]{1,0:T(8,128)(2,1)S(1)}, bf16[256,512]{1,0:T(8,128)(2,1)S(1)}, u32[]{:S(2)}, u32[]{:S(2)}) collective-permute-start(bf16[256,512]{1,0:T(8,128)(2,1)S(1)} %collective-permute-done.11), channel_id=1, source_target_pairs={{4,0},{8,4},{12,8},{14,12},{10,14},{6,10},{2,6},{0,2},{5,1},{9,5},... | collective-permute-start | bytes 786440 | tf_op jit(solution)/shard_map/ppermute | solution.py:115
  65.5 11.2 %collective-permute-start.19 = (bf16[256,512]{1,0:T(8,128)(2,1)S(1)}, bf16[256,512]{1,0:T(8,128)(2,1)S(1)}, u32[]{:S(2)}, u32[]{:S(2)}) collective-permute-start(bf16[256,512]{1,0:T(8,128)(2,1)S(1)} %collective-permute-done.18), channel_id=1, source_target_pairs={{0,4},{4,8},{8,12},{12,14},{14,10},{10,6},{6,2},{2,0},{1,5},{5,9},... | collective-permute-start | bytes 786440 | tf_op jit(solution)/shard_map/ppermute | solution.py:115
  70.7 11.2 %collective-permute-start.26 = (bf16[256,512]{1,0:T(8,128)(2,1)S(1)}, bf16[256,512]{1,0:T(8,128)(2,1)S(1)}, u32[]{:S(2)}, u32[]{:S(2)}) collective-permute-start(bf16[256,512]{1,0:T(8,128)(2,1)S(1)} %collective-permute-done.25), channel_id=1, source_target_pairs={{4,0},{8,4},{12,8},{14,12},{10,14},{6,10},{2,6},{0,2},{5,1},{9,5},... | collective-permute-start | bytes 786440 | tf_op jit(solution)/shard_map/ppermute | solution.py:115
  71.8 11.1 %collective-permute-start.6 = (bf16[256,512]{1,0:T(8,128)(2,1)S(1)}, bf16[256,512]{1,0:T(8,128)(2,1)S(1)}, u32[]{:S(2)}, u32[]{:S(2)}) collective-permute-start(bf16[256,512]{1,0:T(8,128)(2,1)S(1)} %collective-permute-done.5), channel_id=1, source_target_pairs={{0,4},{4,8},{8,12},{12,14},{14,10},{10,6},{6,2},{2,0},{1,5},{5,9},... | collective-permute-start | bytes 786440 | tf_op jit(solution)/shard_map/ppermute | solution.py:115
  76.3 10.6 %collective-permute-start.13 = (bf16[256,512]{1,0:T(8,128)(2,1)S(1)}, bf16[256,512]{1,0:T(8,128)(2,1)S(1)}, u32[]{:S(2)}, u32[]{:S(2)}) collective-permute-start(bf16[256,512]{1,0:T(8,128)(2,1)S(1)} %collective-permute-done.12), channel_id=1, source_target_pairs={{4,0},{8,4},{12,8},{14,12},{10,14},{6,10},{2,6},{0,2},{5,1},{9,5},... | collective-permute-start | bytes 786440 | tf_op jit(solution)/shard_map/ppermute | solution.py:115
  76.7 10.5 %collective-permute-start.20 = (bf16[256,512]{1,0:T(8,128)(2,1)S(1)}, bf16[256,512]{1,0:T(8,128)(2,1)S(1)}, u32[]{:S(2)}, u32[]{:S(2)}) collective-permute-start(bf16[256,512]{1,0:T(8,128)(2,1)S(1)} %collective-permute-done.19), channel_id=1, source_target_pairs={{0,4},{4,8},{8,12},{12,14},{14,10},{10,6},{6,2},{2,0},{1,5},{5,9},... | collective-permute-start | bytes 786440 | tf_op jit(solution)/shard_map/ppermute | solution.py:115
  82.0 7.8 %collective-permute-start.27 = (bf16[256,512]{1,0:T(8,128)(2,1)S(1)}, bf16[256,512]{1,0:T(8,128)(2,1)S(1)}, u32[]{:S(2)}, u32[]{:S(2)}) collective-permute-start(bf16[256,512]{1,0:T(8,128)(2,1)S(1)} %collective-permute-done.26), channel_id=1, source_target_pairs={{4,0},{8,4},{12,8},{14,12},{10,14},{6,10},{2,6},{0,2},{5,1},{9,5},... | collective-permute-start | bytes 786440 | tf_op jit(solution)/shard_map/ppermute | solution.py:115
  92.5 3.6 %collective-permute-start.28 = (bf16[256,2048]{1,0:T(8,128)(2,1)S(1)}, bf16[256,2048]{1,0:T(8,128)(2,1)S(1)}, u32[]{:S(2)}, u32[]{:S(2)}) collective-permute-start(bf16[256,2048]{1,0:T(8,128)(2,1)S(1)} %get-tuple-element.192), channel_id=1, source_target_pairs={{0,1},{2,3},{4,5},{6,7},{8,9},{10,11},{12,13},{14,15},{16,17},{18,... | collective-permute-start | bytes 3145736 | tf_op jit(solution)/shard_map/ppermute | solution.py:18
  94.4 8.4 %copy-start.2 = (bf16[2048,2048]{1,0:T(8,128)(2,1)}, bf16[2048,2048]{1,0:T(8,128)(2,1)S(1)}, u32[]{:S(2)}) copy-start(bf16[2048,2048]{1,0:T(8,128)(2,1)S(1)} %constant_dynamic-update-slice_fusion) | copy-start | bytes 25165828
  104.2 3.6 %collective-permute-start.29 = (f32[7]{0:T(128)S(1)}, f32[7]{0:T(128)S(1)}, u32[]{:S(2)}, u32[]{:S(2)}) collective-permute-start(f32[7]{0:T(128)S(1)} %pad_maximum_fusion.1), channel_id=1, source_target_pairs={{0,2},{2,0},{4,6},{6,4},{8,10},{10,8},{12,14},{14,12},{1,3},{3,1},... | collective-permute-start | bytes 92 | tf_op jit(solution)/shard_map/ppermute | solution.py:130
  108.5 3.6 %collective-permute-start.30 = (f32[7]{0:T(128)S(1)}, f32[7]{0:T(128)S(1)}, u32[]{:S(2)}, u32[]{:S(2)}) collective-permute-start(f32[7]{0:T(128)S(1)} %fusion.154), channel_id=1, source_target_pairs={{0,4},{2,6},{4,0},{6,2},{8,12},{10,14},{12,8},{14,10},{1,5},{3,7},... | collective-permute-start | bytes 92 | tf_op jit(solution)/shard_map/ppermute | solution.py:130
  112.1 4.5 %collective-permute-start.31 = (f32[7]{0:T(128)S(1)}, f32[7]{0:T(128)S(1)}, u32[]{:S(2)}, u32[]{:S(2)}) collective-permute-start(f32[7]{0:T(128)S(1)} %add.463), channel_id=1, source_target_pairs={{0,8},{2,10},{4,12},{6,14},{8,0},{10,2},{12,4},{14,6},{1,9},{3,11}... | collective-permute-start | bytes 92 | tf_op jit(solution)/shard_map/ppermute | solution.py:130
  121.1 12.2 %collective-permute-start.32 = (bf16[256,2048]{1,0:T(8,128)(2,1)}, bf16[256,2048]{1,0:T(8,128)(2,1)S(1)}, u32[]{:S(2)}, u32[]{:S(2)}) collective-permute-start(bf16[256,2048]{1,0:T(8,128)(2,1)} %get-tuple-element.202), channel_id=1, source_target_pairs={{1,0},{3,2},{5,4},{7,6},{9,8},{11,10},{13,12},{15,14},{17,16},{19,... | collective-permute-start | bytes 3145736 | tf_op jit(solution)/shard_map/ppermute | solution.py:18
  123.6 9.0 %collective-permute-start.33 = (f32[1]{0:T(128)}, f32[1]{0:T(128)}, u32[]{:S(2)}, u32[]{:S(2)}) collective-permute-start(f32[1]{0:T(128)} %bitcast.20), channel_id=1, source_target_pairs={{1,0},{3,2},{5,4},{7,6},{9,8},{11,10},{13,12},{15,14},{17,16},{19,... | collective-permute-start | bytes 20 | tf_op jit(solution)/shard_map/ppermute | solution.py:18
  133.2 2.2 %copy-start.4 = (f32[256,2048]{1,0:T(8,128)S(1)}, f32[256,2048]{1,0:T(8,128)}, u32[]{:S(2)}) copy-start(f32[256,2048]{1,0:T(8,128)} %get-tuple-element.67) | copy-start | bytes 6291460 | tf_op jit(solution)/shard_map/cond

commit v16 on v10

--- a/solution.py
+++ b/solution.py
@@ -183,6 +183,7 @@
     if overlap:
         acc = [None] * (2 * pieces)
         normed = []
+        calls = []
 
         def on_piece(origin, j, piece):
             if not normed:
@@ -192,15 +193,21 @@
             lhs = lax.dynamic_slice(normed_a, (0, origin * rows_w), (normed_a.shape[0], rows_w))
             term = jnp.dot(lhs, piece, preferred_element_type=jnp.float32)
             acc[j] = term if acc[j] is None else acc[j] + term
+            calls.append(j)
+            if len(calls) == 4 * pieces + 1:
+                me = lax.axis_index("tok")
+                own, _ = lax.optimization_barrier((
+                    lax.dynamic_slice(normed_a, (0, me * rows_w), (normed_a.shape[0], rows_w)),
+                    piece,
+                ))
+                for i in range(2 * pieces):
+                    acc[i] = acc[i] + jnp.dot(
+                        own, local[:, i * piece_w:(i + 1) * piece_w],
+                        preferred_element_type=jnp.float32,
+                    )
 
         weight = ring_gather(local, "tok", pieces, on_piece)
         values_a, unit_a, std_a, normed_a = normed[0]
-        me = lax.axis_index("tok")
-        lhs = lax.dynamic_slice(normed_a, (0, me * rows_w), (normed_a.shape[0], rows_w))
-        for j in range(2 * pieces):
-            acc[j] = acc[j] + jnp.dot(
-                lhs, local[:, j * piece_w:(j + 1) * piece_w], preferred_element_type=jnp.float32
-            )
         pre_a = jnp.concatenate(acc, axis=1)
         out_a = (values_a + gelu_value(pre_a)).astype(jnp.bfloat16)
         fa = (out_a, unit_a, std_a, pre_a)

time: 141 us -> 142 us (level)
  transfers between devices with their start and end apart: 34 -> 34, of which waited for: 27 -> 22; matrix products, arithmetic and copies ran while one was open for 11% -> 11% of each run, Pallas kernels for 0% -> 0%
where the time goes in v16:
time: 142 us
  waiting for transfers between devices  55.8 us (39%)
  starting transfers between devices  38.7 us (27%)
  matrix products  21.8 us (15%)
  other arithmetic  11.8 us (8%)
  local copies, waits for them, and re-layouts  9.28 us (7%)
  between operations  4.36 us (3%)
    ppermute x28, waiting for transfers between devices, ring_gather(): parts[j] = lax.ppermute(parts[j], axis, cw if clockwise else ccw)  39.5 us
    ppermute x28, starting transfers between devices, ring_gather(): parts[j] = lax.ppermute(parts[j], axis, cw if clockwise else ccw)  29.9 us
    ppermute x3, waiting for transfers between devices, shifted(): return lax.ppermute(x, axis, pairs)  9.33 us
    dot_general x28, matrix products, on_piece(): term = jnp.dot(lhs, piece, preferred_element_type=jnp.float32)  8.23 us
    ppermute x3, waiting for transfers between devices, tree_sum(): v = v + lax.ppermute(v, axis, [(i, i ^ b) for i in range(n)])  6.96 us
    dot_general x1, matrix products, section_backward(): lax.dot_general(grad_pre, weight, (((1,), (1,)), ((), ())), preferred_ele...  6.58 us
    dot_general x1, matrix products, section_forward(): pre_act = jnp.dot(normed, weight, preferred_element_type=jnp.float32)  6.07 us
    ppermute x3, starting transfers between devices, tree_sum(): v = v + lax.ppermute(v, axis, [(i, i ^ b) for i in range(n)])  4.66 us
  transfers between devices with their start and end apart: 34, of which 22 were waited for; matrix products, arithmetic and copies ran while one was open for 11% of the time, Pallas kernels for 0%

profile of v16, /device:TPU:0, one launch (start us, length us, event | category | flops | bytes accessed | tf_op | source)
XLA Modules:
  0.0 141.8 jit_solution(11907150525082015114)
XLA Ops:
  0.7 2.2 %fusion.113 = (bf16[256,512]{1,0:T(8,128)(2,1)}, bf16[256,512]{1,0:T(8,128)(2,1)}, bf16[256,512]{1,0:T(8,128)(2,1)}, bf16[256,512]{1,0:T(8,128)(2,1)S(1)}) fusion(bf16[256,2048]{1,0:T(8,128)(2,1)} %bitcast.134), kind=kLoop, calls=%fused_computation.221 | loop fusion | bytes 2097152 | tf_op jit(solution)/shard_map/slice | solution.py:106
  2.8 3.1 %collective-permute-start = (bf16[256,512]{1,0:T(8,128)(2,1)S(1)}, bf16[256,512]{1,0:T(8,128)(2,1)S(1)}, u32[]{:S(2)}, u32[]{:S(2)}) collective-permute-start(bf16[256,512]{1,0:T(8,128)(2,1)S(1)} %get-tuple-element.201), channel_id=1, source_target_pairs={{0,4},{4,8},{8,12},{12,14},{14,10},{10,6},{6,2},{2,0},{1,5},{5,9},... | collective-permute-start | bytes 786440 | tf_op jit(solution)/shard_map/ppermute | solution.py:113
  5.9 2.0 %collective-permute-start.14 = (bf16[256,512]{1,0:T(8,128)(2,1)}, bf16[256,512]{1,0:T(8,128)(2,1)}, u32[]{:S(2)}, u32[]{:S(2)}) collective-permute-start(bf16[256,512]{1,0:T(8,128)(2,1)} %get-tuple-element.199), channel_id=1, source_target_pairs={{0,4},{4,8},{8,12},{12,14},{14,10},{10,6},{6,2},{2,0},{1,5},{5,9},... | collective-permute-start | bytes 786440 | tf_op jit(solution)/shard_map/ppermute | solution.py:113
  10.1 2.9 %collective-permute-done = bf16[256,512]{1,0:T(8,128)(2,1)S(1)} collective-permute-done((bf16[256,512]{1,0:T(8,128)(2,1)S(1)}, bf16[256,512]{1,0:T(8,128)(2,1)S(1)}, u32[]{:S(2)}, u32[]{:S(2)}) %collective-permute-start) | collective-permute-done | bytes 262176 | tf_op jit(solution)/shard_map/ppermute | solution.py:113
  14.6 2.1 %collective-permute-start.1 = (bf16[256,512]{1,0:T(8,128)(2,1)S(1)}, bf16[256,512]{1,0:T(8,128)(2,1)S(1)}, u32[]{:S(2)}, u32[]{:S(2)}) collective-permute-start(bf16[256,512]{1,0:T(8,128)(2,1)S(1)} %copy-done.9), channel_id=1, source_target_pairs={{0,4},{4,8},{8,12},{12,14},{14,10},{10,6},{6,2},{2,0},{1,5},{5,9},... | collective-permute-start | bytes 786440 | tf_op jit(solution)/shard_map/ppermute | solution.py:113
  19.2 1.2 fusion.37
  20.3 2.1 %collective-permute-start.15 = (bf16[256,512]{1,0:T(8,128)(2,1)}, bf16[256,512]{1,0:T(8,128)(2,1)S(1)}, u32[]{:S(2)}, u32[]{:S(2)}) collective-permute-start(bf16[256,512]{1,0:T(8,128)(2,1)} %collective-permute-done.14), channel_id=1, source_target_pairs={{0,4},{4,8},{8,12},{12,14},{14,10},{10,6},{6,2},{2,0},{1,5},{5,9},... | collective-permute-start | bytes 786440 | tf_op jit(solution)/shard_map/ppermute | solution.py:113
  23.4 1.2 fusion.64
  25.0 2.1 %collective-permute-start.2 = (bf16[256,512]{1,0:T(8,128)(2,1)S(1)}, bf16[256,512]{1,0:T(8,128)(2,1)S(1)}, u32[]{:S(2)}, u32[]{:S(2)}) collective-permute-start(bf16[256,512]{1,0:T(8,128)(2,1)S(1)} %collective-permute-done.1), channel_id=1, source_target_pairs={{0,4},{4,8},{8,12},{12,14},{14,10},{10,6},{6,2},{2,0},{1,5},{5,9},... | collective-permute-start | bytes 786440 | tf_op jit(solution)/shard_map/ppermute | solution.py:113
  27.1 2.7 %collective-permute-done.15 = bf16[256,512]{1,0:T(8,128)(2,1)S(1)} collective-permute-done((bf16[256,512]{1,0:T(8,128)(2,1)}, bf16[256,512]{1,0:T(8,128)(2,1)S(1)}, u32[]{:S(2)}, u32[]{:S(2)}) %collective-permute-start.15) | collective-permute-done | bytes 262176 | tf_op jit(solution)/shard_map/ppermute | solution.py:113
  29.8 2.1 %collective-permute-start.16 = (bf16[256,512]{1,0:T(8,128)(2,1)S(1)}, bf16[256,512]{1,0:T(8,128)(2,1)S(1)}, u32[]{:S(2)}, u32[]{:S(2)}) collective-permute-start(bf16[256,512]{1,0:T(8,128)(2,1)S(1)} %collective-permute-done.15), channel_id=1, source_target_pairs={{0,4},{4,8},{8,12},{12,14},{14,10},{10,6},{6,2},{2,0},{1,5},{5,9},... | collective-permute-start | bytes 786440 | tf_op jit(solution)/shard_map/ppermute | solution.py:113
  31.9 1.9 %collective-permute-done.22 = bf16[256,512]{1,0:T(8,128)(2,1)S(1)} collective-permute-done((bf16[256,512]{1,0:T(8,128)(2,1)S(1)}, bf16[256,512]{1,0:T(8,128)(2,1)S(1)}, u32[]{:S(2)}, u32[]{:S(2)}) %collective-permute-start.22) | collective-permute-done | bytes 262176 | tf_op jit(solution)/shard_map/ppermute | solution.py:113
  35.8 3.3 %collective-permute-done.9 = bf16[256,512]{1,0:T(8,128)(2,1)S(1)} collective-permute-done((bf16[256,512]{1,0:T(8,128)(2,1)S(1)}, bf16[256,512]{1,0:T(8,128)(2,1)S(1)}, u32[]{:S(2)}, u32[]{:S(2)}) %collective-permute-start.9) | collective-permute-done | bytes 262176 | tf_op jit(solution)/shard_map/ppermute | solution.py:113
  40.7 1.3 collective-permute-done.23
  42.4 1.6 %collective-permute-start.3 = (bf16[256,512]{1,0:T(8,128)(2,1)S(1)}, bf16[256,512]{1,0:T(8,128)(2,1)S(1)}, u32[]{:S(2)}, u32[]{:S(2)}) collective-permute-start(bf16[256,512]{1,0:T(8,128)(2,1)S(1)} %collective-permute-done.2), channel_id=1, source_target_pairs={{0,4},{4,8},{8,12},{12,14},{14,10},{10,6},{6,2},{2,0},{1,5},{5,9},... | collective-permute-start | bytes 786440 | tf_op jit(solution)/shard_map/ppermute | solution.py:113
  44.5 1.6 %collective-permute-start.17 = (bf16[256,512]{1,0:T(8,128)(2,1)S(1)}, bf16[256,512]{1,0:T(8,128)(2,1)S(1)}, u32[]{:S(2)}, u32[]{:S(2)}) collective-permute-start(bf16[256,512]{1,0:T(8,128)(2,1)S(1)} %collective-permute-done.16), channel_id=1, source_target_pairs={{0,4},{4,8},{8,12},{12,14},{14,10},{10,6},{6,2},{2,0},{1,5},{5,9},... | collective-permute-start | bytes 786440 | tf_op jit(solution)/shard_map/ppermute | solution.py:113
  46.9 4.7 %collective-permute-done.3 = bf16[256,512]{1,0:T(8,128)(2,1)S(1)} collective-permute-done((bf16[256,512]{1,0:T(8,128)(2,1)S(1)}, bf16[256,512]{1,0:T(8,128)(2,1)S(1)}, u32[]{:S(2)}, u32[]{:S(2)}) %collective-permute-start.3) | collective-permute-done | bytes 262176 | tf_op jit(solution)/shard_map/ppermute | solution.py:113
  51.7 1.6 %collective-permute-start.4 = (bf16[256,512]{1,0:T(8,128)(2,1)S(1)}, bf16[256,512]{1,0:T(8,128)(2,1)S(1)}, u32[]{:S(2)}, u32[]{:S(2)}) collective-permute-start(bf16[256,512]{1,0:T(8,128)(2,1)S(1)} %collective-permute-done.3), channel_id=1, source_target_pairs={{0,4},{4,8},{8,12},{12,14},{14,10},{10,6},{6,2},{2,0},{1,5},{5,9},... | collective-permute-start | bytes 786440 | tf_op jit(solution)/shard_map/ppermute | solution.py:113
  53.7 3.6 %collective-permute-done.17 = bf16[256,512]{1,0:T(8,128)(2,1)S(1)} collective-permute-done((bf16[256,512]{1,0:T(8,128)(2,1)S(1)}, bf16[256,512]{1,0:T(8,128)(2,1)S(1)}, u32[]{:S(2)}, u32[]{:S(2)}) %collective-permute-start.17) | collective-permute-done | bytes 262176 | tf_op jit(solution)/shard_map/ppermute | solution.py:113
  57.3 1.6 %collective-permute-start.18 = (bf16[256,512]{1,0:T(8,128)(2,1)S(1)}, bf16[256,512]{1,0:T(8,128)(2,1)S(1)}, u32[]{:S(2)}, u32[]{:S(2)}) collective-permute-start(bf16[256,512]{1,0:T(8,128)(2,1)S(1)} %collective-permute-done.17), channel_id=1, source_target_pairs={{0,4},{4,8},{8,12},{12,14},{14,10},{10,6},{6,2},{2,0},{1,5},{5,9},... | collective-permute-start | bytes 786440 | tf_op jit(solution)/shard_map/ppermute | solution.py:113
  60.4 2.5 %collective-permute-done.4 = bf16[256,512]{1,0:T(8,128)(2,1)S(1)} collective-permute-done((bf16[256,512]{1,0:T(8,128)(2,1)S(1)}, bf16[256,512]{1,0:T(8,128)(2,1)S(1)}, u32[]{:S(2)}, u32[]{:S(2)}) %collective-permute-start.4) | collective-permute-done | bytes 262176 | tf_op jit(solution)/shard_map/ppermute | solution.py:113
  62.9 1.6 %collective-permute-start.5 = (bf16[256,512]{1,0:T(8,128)(2,1)S(1)}, bf16[256,512]{1,0:T(8,128)(2,1)S(1)}, u32[]{:S(2)}, u32[]{:S(2)}) collective-permute-start(bf16[256,512]{1,0:T(8,128)(2,1)S(1)} %collective-permute-done.4), channel_id=1, source_target_pairs={{0,4},{4,8},{8,12},{12,14},{14,10},{10,6},{6,2},{2,0},{1,5},{5,9},... | collective-permute-start | bytes 786440 | tf_op jit(solution)/shard_map/ppermute | solution.py:113
  65.0 3.5 %collective-permute-done.18 = bf16[256,512]{1,0:T(8,128)(2,1)S(1)} collective-permute-done((bf16[256,512]{1,0:T(8,128)(2,1)S(1)}, bf16[256,512]{1,0:T(8,128)(2,1)S(1)}, u32[]{:S(2)}, u32[]{:S(2)}) %collective-permute-start.18) | collective-permute-done | bytes 262176 | tf_op jit(solution)/shard_map/ppermute | solution.py:113
  68.5 1.6 %collective-permute-start.19 = (bf16[256,512]{1,0:T(8,128)(2,1)S(1)}, bf16[256,512]{1,0:T(8,128)(2,1)S(1)}, u32[]{:S(2)}, u32[]{:S(2)}) collective-permute-start(bf16[256,512]{1,0:T(8,128)(2,1)S(1)} %collective-permute-done.18), channel_id=1, source_target_pairs={{0,4},{4,8},{8,12},{12,14},{14,10},{10,6},{6,2},{2,0},{1,5},{5,9},... | collective-permute-start | bytes 786440 | tf_op jit(solution)/shard_map/ppermute | solution.py:113
  71.6 2.5 %collective-permute-done.5 = bf16[256,512]{1,0:T(8,128)(2,1)S(1)} collective-permute-done((bf16[256,512]{1,0:T(8,128)(2,1)S(1)}, bf16[256,512]{1,0:T(8,128)(2,1)S(1)}, u32[]{:S(2)}, u32[]{:S(2)}) %collective-permute-start.5) | collective-permute-done | bytes 262176 | tf_op jit(solution)/shard_map/ppermute | solution.py:113
  74.1 1.6 %collective-permute-start.6 = (bf16[256,512]{1,0:T(8,128)(2,1)S(1)}, bf16[256,512]{1,0:T(8,128)(2,1)S(1)}, u32[]{:S(2)}, u32[]{:S(2)}) collective-permute-start(bf16[256,512]{1,0:T(8,128)(2,1)S(1)} %collective-permute-done.5), channel_id=1, source_target_pairs={{0,4},{4,8},{8,12},{12,14},{14,10},{10,6},{6,2},{2,0},{1,5},{5,9},... | collective-permute-start | bytes 786440 | tf_op jit(solution)/shard_map/ppermute | solution.py:113
  76.2 3.6 %collective-permute-done.19 = bf16[256,512]{1,0:T(8,128)(2,1)S(1)} collective-permute-done((bf16[256,512]{1,0:T(8,128)(2,1)S(1)}, bf16[256,512]{1,0:T(8,128)(2,1)S(1)}, u32[]{:S(2)}, u32[]{:S(2)}) %collective-permute-start.19) | collective-permute-done | bytes 262176 | tf_op jit(solution)/shard_map/ppermute | solution.py:113
  79.7 1.6 %collective-permute-start.20 = (bf16[256,512]{1,0:T(8,128)(2,1)S(1)}, bf16[256,512]{1,0:T(8,128)(2,1)S(1)}, u32[]{:S(2)}, u32[]{:S(2)}) collective-permute-start(bf16[256,512]{1,0:T(8,128)(2,1)S(1)} %collective-permute-done.19), channel_id=1, source_target_pairs={{0,4},{4,8},{8,12},{12,14},{14,10},{10,6},{6,2},{2,0},{1,5},{5,9},... | collective-permute-start | bytes 786440 | tf_op jit(solution)/shard_map/ppermute | solution.py:113
  82.7 2.4 %collective-permute-done.6 = bf16[256,512]{1,0:T(8,128)(2,1)S(1)} collective-permute-done((bf16[256,512]{1,0:T(8,128)(2,1)S(1)}, bf16[256,512]{1,0:T(8,128)(2,1)S(1)}, u32[]{:S(2)}, u32[]{:S(2)}) %collective-permute-start.6) | collective-permute-done | bytes 262176 | tf_op jit(solution)/shard_map/ppermute | solution.py:113
  86.7 1.3 collective-permute-done.20
  89.5 2.5 %fusion.23 = (f32[256,2048]{1,0:T(8,128)}, bf16[256,2048]{1,0:T(8,128)(2,1)S(1)}) fusion(f32[256,512]{1,0:T(8,128)S(1)} %convolution_add_fusion, f32[256,512]{1,0:T(8,128)S(1)} %convolution_add_fusion.6, f32[256,512]{1,0:T(8,128)S(1)} %convolution_add_fusion.12, f32[256,512]{1,0:T(8,128)S(1)} %convolution_add_fusion.18, bf16[256,2048]{1,0:T(8,128)(2,1)S(1)} %bitcast.133), kind=kLoop, calls=%fused_computation.57 | loop fusion | flops 12582912 | bytes 6291456 | tf_op jit(solution)/shard_map/add | solution.py:28
  92.0 1.5 %collective-permute-start.28 = (bf16[256,2048]{1,0:T(8,128)(2,1)S(1)}, bf16[256,2048]{1,0:T(8,128)(2,1)S(1)}, u32[]{:S(2)}, u32[]{:S(2)}) collective-permute-start(bf16[256,2048]{1,0:T(8,128)(2,1)S(1)} %get-tuple-element.194), channel_id=1, source_target_pairs={{0,1},{2,3},{4,5},{6,7},{8,9},{10,11},{12,13},{14,15},{16,17},{18,... | collective-permute-start | bytes 3145736 | tf_op jit(solution)/shard_map/ppermute | solution.py:18
  93.9 1.6 %collective-permute-done.28 = bf16[256,2048]{1,0:T(8,128)(2,1)S(1)} collective-permute-done((bf16[256,2048]{1,0:T(8,128)(2,1)S(1)}, bf16[256,2048]{1,0:T(8,128)(2,1)S(1)}, u32[]{:S(2)}, u32[]{:S(2)}) %collective-permute-start.28) | collective-permute-done | bytes 1048608 | tf_op jit(solution)/shard_map/ppermute | solution.py:18
  96.2 6.1 %bitcast_convert_fusion.2 = (f32[2,128,2048]{2,1,0:T(8,128)S(1)}, bf16[256,2048]{1,0:T(8,128)(2,1)}, f32[256,2048]{1,0:T(8,128)}, f32[256,2048]{1,0:T(8,128)}) fusion(bf16[256,2048]{1,0:T(8,128)(2,1)S(1)} %collective-permute-done.28, f32[256]{0:T(256)S(1)} %add_rsqrt_fusion.1, f32[256]{0:T(256)S(1)} %broadcast_multiply_fusion.4, ...), kind=kOutput, calls=%fused_computation.210 | convolution fusion | flops 2162688000 | bytes 16787456 | tf_op jit(solution)/shard_map/dot_general | solution.py:50
  104.2 3.1 %collective-permute-done.29 = f32[7]{0:T(128)S(1)} collective-permute-done((f32[7]{0:T(128)S(1)}, f32[7]{0:T(128)S(1)}, u32[]{:S(2)}, u32[]{:S(2)}) %collective-permute-start.29) | collective-permute-done | bytes 60 | tf_op jit(solution)/shard_map/ppermute | solution.py:128
  108.0 1.6 %collective-permute-start.30 = (f32[7]{0:T(128)S(1)}, f32[7]{0:T(128)S(1)}, u32[]{:S(2)}, u32[]{:S(2)}) collective-permute-start(f32[7]{0:T(128)S(1)} %fusion.150), channel_id=1, source_target_pairs={{0,4},{2,6},{4,0},{6,2},{8,12},{10,14},{12,8},{14,10},{1,5},{3,7},... | collective-permute-start | bytes 92 | tf_op jit(solution)/shard_map/ppermute | solution.py:128
  109.6 2.0 %collective-permute-done.30 = f32[7]{0:T(128)S(1)} collective-permute-done((f32[7]{0:T(128)S(1)}, f32[7]{0:T(128)S(1)}, u32[]{:S(2)}, u32[]{:S(2)}) %collective-permute-start.30) | collective-permute-done | bytes 60 | tf_op jit(solution)/shard_map/ppermute | solution.py:128
  111.6 2.6 %collective-permute-start.31 = (f32[7]{0:T(128)S(1)}, f32[7]{0:T(128)S(1)}, u32[]{:S(2)}, u32[]{:S(2)}) collective-permute-start(f32[7]{0:T(128)S(1)} %add.463), channel_id=1, source_target_pairs={{0,8},{2,10},{4,12},{6,14},{8,0},{10,2},{12,4},{14,6},{1,9},{3,11}... | collective-permute-start | bytes 92 | tf_op jit(solution)/shard_map/ppermute | solution.py:128
  114.2 1.9 %collective-permute-done.31 = f32[7]{0:T(128)S(1)} collective-permute-done((f32[7]{0:T(128)S(1)}, f32[7]{0:T(128)S(1)}, u32[]{:S(2)}, u32[]{:S(2)}) %collective-permute-start.31) | collective-permute-done | bytes 60 | tf_op jit(solution)/shard_map/ppermute | solution.py:128
  118.0 1.3 fusion.111
  119.4 1.1 conditional.2
  119.4 1.1 broadcast.190
  120.5 1.3 collective-permute-start.32
  122.9 1.3 collective-permute-start.33
  124.2 7.7 %collective-permute-done.33 = f32[1]{0:T(128)} collective-permute-done((f32[1]{0:T(128)}, f32[1]{0:T(128)}, u32[]{:S(2)}, u32[]{:S(2)}) %collective-permute-start.33) | collective-permute-done | bytes 36 | tf_op jit(solution)/shard_map/ppermute | solution.py:18
  132.5 8.2 %conditional.3 = (bf16[1,2,128,2048]{3,2,1,0:T(8,128)(2,1)}) conditional(s32[]{:T(128)} %convert_element_type.58, bf16[256,2048]{1,0:T(8,128)(2,1)} %get-tuple-element.204, (bf16[256,2048]{1,0:T(8,128)(2,1)S(1)}, f32[256]{0:T(256)S(1)}, f32[]{:T(128)}, f32[]{:T(128)}, f32[256,2048]{1,0:T(8,128)}, /*index=5*/bf16[2048,2048]{1,0:T(8,128)(2,1)}, ...), branch_computations={%region_15.16_spmd, %region_16.19_spmd} | conditional | flops 2154824192 | bytes 22039568 | solution.py:253
  132.5 6.6 %fusion.106 = (f32[256]{0:T(256)S(1)}, f32[256]{0:T(256)S(1)}, f32[256,2048]{1,0:T(8,128)S(1)}) fusion(f32[256,2048]{1,0:T(8,128)S(1)} %get-tuple-element.67, f32[2048]{0:T(1024)S(1)} %bitcast.146, bf16[2048,2048]{1,0:T(8,128)(2,1)} %get-tuple-element.65, f32[256,2048]{1,0:T(8,128)} %get-tuple-element.64, bf16[256,2048]{1,0:T(8,128)(2,1)S(1)} %get-tuple-element.60), kind=kOutput, calls=%fused_computation.216 | convolution fusion | flops 2151153152 | bytes 15738880 | tf_op jit(solution)/shard_map/cond/branch_1_fun/dot_general | solution.py:57
  139.1 1.6 %fusion.1 = bf16[256,2048]{1,0:T(8,128)(2,1)} fusion(bf16[256,2048]{1,0:T(8,128)(2,1)S(1)} %get-tuple-element.60, f32[256,2048]{1,0:T(8,128)S(1)} %get-tuple-element.67, f32[256,2048]{1,0:T(8,128)S(1)} %get-tuple-element.182, f32[256]{0:T(256)S(1)} %add_rsqrt_fusion, f32[256]{0:T(256)S(1)} %get-tuple-element.183, f32[256]{0:T(256)S(1)} %get-tuple-element.184), kind=kLoop, calls=%fused_computation.5 | loop fusion | flops 3670016 | bytes 6294528 | tf_op jit(solution)/shard_map/cond/branch_1_fun/convert_element_type | solution.py:66
  (138 shorter events, 26.8 us)
Async XLA Ops:
  0.6 7.5 %copy-start.5 = (bf16[128,2048]{1,0:T(8,128)(2,1)S(1)}, bf16[128,2048]{1,0:T(8,128)(2,1)}, u32[]{:S(2)}) copy-start(bf16[128,2048]{1,0:T(8,128)(2,1)} %param.9) | copy-start | bytes 1572868
  0.6 12.3 %copy-start.2 = (bf16[2,128,2048]{2,1,0:T(8,128)(2,1)S(1)}, bf16[2,128,2048]{2,1,0:T(8,128)(2,1)}, u32[]{:S(2)}) copy-start(bf16[2,128,2048]{2,1,0:T(8,128)(2,1)} %param.8) | copy-start | bytes 3145732
  2.8 10.1 %collective-permute-start = (bf16[256,512]{1,0:T(8,128)(2,1)S(1)}, bf16[256,512]{1,0:T(8,128)(2,1)S(1)}, u32[]{:S(2)}, u32[]{:S(2)}) collective-permute-start(bf16[256,512]{1,0:T(8,128)(2,1)S(1)} %get-tuple-element.201), channel_id=1, source_target_pairs={{0,4},{4,8},{8,12},{12,14},{14,10},{10,6},{6,2},{2,0},{1,5},{5,9},... | collective-permute-start | bytes 786440 | tf_op jit(solution)/shard_map/ppermute | solution.py:113
  5.9 12.2 %collective-permute-start.7 = (bf16[256,512]{1,0:T(8,128)(2,1)}, bf16[256,512]{1,0:T(8,128)(2,1)}, u32[]{:S(2)}, u32[]{:S(2)}) collective-permute-start(bf16[256,512]{1,0:T(8,128)(2,1)} %get-tuple-element.200), channel_id=1, source_target_pairs={{4,0},{8,4},{12,8},{14,12},{10,14},{6,10},{2,6},{0,2},{5,1},{9,5},... | collective-permute-start | bytes 786440 | tf_op jit(solution)/shard_map/ppermute | solution.py:113
  5.9 14.4 %collective-permute-start.14 = (bf16[256,512]{1,0:T(8,128)(2,1)}, bf16[256,512]{1,0:T(8,128)(2,1)}, u32[]{:S(2)}, u32[]{:S(2)}) collective-permute-start(bf16[256,512]{1,0:T(8,128)(2,1)} %get-tuple-element.199), channel_id=1, source_target_pairs={{0,4},{4,8},{8,12},{12,14},{14,10},{10,6},{6,2},{2,0},{1,5},{5,9},... | collective-permute-start | bytes 786440 | tf_op jit(solution)/shard_map/ppermute | solution.py:113
  7.9 16.7 %collective-permute-start.21 = (bf16[256,512]{1,0:T(8,128)(2,1)}, bf16[256,512]{1,0:T(8,128)(2,1)S(1)}, u32[]{:S(2)}, u32[]{:S(2)}) collective-permute-start(bf16[256,512]{1,0:T(8,128)(2,1)} %get-tuple-element.198), channel_id=1, source_target_pairs={{4,0},{8,4},{12,8},{14,12},{10,14},{6,10},{2,6},{0,2},{5,1},{9,5},... | collective-permute-start | bytes 786440 | tf_op jit(solution)/shard_map/ppermute | solution.py:113
  8.1 5.6 %copy-start.10 = (f32[1,2048]{1,0:T(1,128)S(1)}, f32[1,2048]{1,0:T(1,128)}, u32[]{:S(2)}) copy-start(f32[1,2048]{1,0:T(1,128)} %param.11) | copy-start | bytes 24580
  13.0 0.7 copy-start.8
  13.7 1.0 copy-start.9
  14.6 10.4 %collective-permute-start.1 = (bf16[256,512]{1,0:T(8,128)(2,1)S(1)}, bf16[256,512]{1,0:T(8,128)(2,1)S(1)}, u32[]{:S(2)}, u32[]{:S(2)}) collective-permute-start(bf16[256,512]{1,0:T(8,128)(2,1)S(1)} %copy-done.9), channel_id=1, source_target_pairs={{0,4},{4,8},{8,12},{12,14},{14,10},{10,6},{6,2},{2,0},{1,5},{5,9},... | collective-permute-start | bytes 786440 | tf_op jit(solution)/shard_map/ppermute | solution.py:113
  18.1 9.0 %collective-permute-start.8 = (bf16[256,512]{1,0:T(8,128)(2,1)}, bf16[256,512]{1,0:T(8,128)(2,1)S(1)}, u32[]{:S(2)}, u32[]{:S(2)}) collective-permute-start(bf16[256,512]{1,0:T(8,128)(2,1)} %collective-permute-done.7), channel_id=1, source_target_pairs={{4,0},{8,4},{12,8},{14,12},{10,14},{6,10},{2,6},{0,2},{5,1},{9,5},... | collective-permute-start | bytes 786440 | tf_op jit(solution)/shard_map/ppermute | solution.py:113
  20.3 9.5 %collective-permute-start.15 = (bf16[256,512]{1,0:T(8,128)(2,1)}, bf16[256,512]{1,0:T(8,128)(2,1)S(1)}, u32[]{:S(2)}, u32[]{:S(2)}) collective-permute-start(bf16[256,512]{1,0:T(8,128)(2,1)} %collective-permute-done.14), channel_id=1, source_target_pairs={{0,4},{4,8},{8,12},{12,14},{14,10},{10,6},{6,2},{2,0},{1,5},{5,9},... | collective-permute-start | bytes 786440 | tf_op jit(solution)/shard_map/ppermute | solution.py:113
  24.6 9.2 %collective-permute-start.22 = (bf16[256,512]{1,0:T(8,128)(2,1)S(1)}, bf16[256,512]{1,0:T(8,128)(2,1)S(1)}, u32[]{:S(2)}, u32[]{:S(2)}) collective-permute-start(bf16[256,512]{1,0:T(8,128)(2,1)S(1)} %collective-permute-done.21), channel_id=1, source_target_pairs={{4,0},{8,4},{12,8},{14,12},{10,14},{6,10},{2,6},{0,2},{5,1},{9,5},... | collective-permute-start | bytes 786440 | tf_op jit(solution)/shard_map/ppermute | solution.py:113
  25.0 10.4 %collective-permute-start.2 = (bf16[256,512]{1,0:T(8,128)(2,1)S(1)}, bf16[256,512]{1,0:T(8,128)(2,1)S(1)}, u32[]{:S(2)}, u32[]{:S(2)}) collective-permute-start(bf16[256,512]{1,0:T(8,128)(2,1)S(1)} %collective-permute-done.1), channel_id=1, source_target_pairs={{0,4},{4,8},{8,12},{12,14},{14,10},{10,6},{6,2},{2,0},{1,5},{5,9},... | collective-permute-start | bytes 786440 | tf_op jit(solution)/shard_map/ppermute | solution.py:113
  27.1 12.1 %collective-permute-start.9 = (bf16[256,512]{1,0:T(8,128)(2,1)S(1)}, bf16[256,512]{1,0:T(8,128)(2,1)S(1)}, u32[]{:S(2)}, u32[]{:S(2)}) collective-permute-start(bf16[256,512]{1,0:T(8,128)(2,1)S(1)} %collective-permute-done.8), channel_id=1, source_target_pairs={{4,0},{8,4},{12,8},{14,12},{10,14},{6,10},{2,6},{0,2},{5,1},{9,5},... | collective-permute-start | bytes 786440 | tf_op jit(solution)/shard_map/ppermute | solution.py:113
  29.8 10.4 %collective-permute-start.16 = (bf16[256,512]{1,0:T(8,128)(2,1)S(1)}, bf16[256,512]{1,0:T(8,128)(2,1)S(1)}, u32[]{:S(2)}, u32[]{:S(2)}) collective-permute-start(bf16[256,512]{1,0:T(8,128)(2,1)S(1)} %collective-permute-done.15), channel_id=1, source_target_pairs={{0,4},{4,8},{8,12},{12,14},{14,10},{10,6},{6,2},{2,0},{1,5},{5,9},... | collective-permute-start | bytes 786440 | tf_op jit(solution)/shard_map/ppermute | solution.py:113
  33.9 8.1 %collective-permute-start.23 = (bf16[256,512]{1,0:T(8,128)(2,1)S(1)}, bf16[256,512]{1,0:T(8,128)(2,1)S(1)}, u32[]{:S(2)}, u32[]{:S(2)}) collective-permute-start(bf16[256,512]{1,0:T(8,128)(2,1)S(1)} %collective-permute-done.22), channel_id=1, source_target_pairs={{4,0},{8,4},{12,8},{14,12},{10,14},{6,10},{2,6},{0,2},{5,1},{9,5},... | collective-permute-start | bytes 786440 | tf_op jit(solution)/shard_map/ppermute | solution.py:113
  34.4 1.2 copy-start.4
  42.4 9.2 %collective-permute-start.3 = (bf16[256,512]{1,0:T(8,128)(2,1)S(1)}, bf16[256,512]{1,0:T(8,128)(2,1)S(1)}, u32[]{:S(2)}, u32[]{:S(2)}) collective-permute-start(bf16[256,512]{1,0:T(8,128)(2,1)S(1)} %collective-permute-done.2), channel_id=1, source_target_pairs={{0,4},{4,8},{8,12},{12,14},{14,10},{10,6},{6,2},{2,0},{1,5},{5,9},... | collective-permute-start | bytes 786440 | tf_op jit(solution)/shard_map/ppermute | solution.py:113
  44.1 9.2 %collective-permute-start.10 = (bf16[256,512]{1,0:T(8,128)(2,1)S(1)}, bf16[256,512]{1,0:T(8,128)(2,1)S(1)}, u32[]{:S(2)}, u32[]{:S(2)}) collective-permute-start(bf16[256,512]{1,0:T(8,128)(2,1)S(1)} %collective-permute-done.9), channel_id=1, source_target_pairs={{4,0},{8,4},{12,8},{14,12},{10,14},{6,10},{2,6},{0,2},{5,1},{9,5},... | collective-permute-start | bytes 786440 | tf_op jit(solution)/shard_map/ppermute | solution.py:113
  44.5 12.8 %collective-permute-start.17 = (bf16[256,512]{1,0:T(8,128)(2,1)S(1)}, bf16[256,512]{1,0:T(8,128)(2,1)S(1)}, u32[]{:S(2)}, u32[]{:S(2)}) collective-permute-start(bf16[256,512]{1,0:T(8,128)(2,1)S(1)} %collective-permute-done.16), channel_id=1, source_target_pairs={{0,4},{4,8},{8,12},{12,14},{14,10},{10,6},{6,2},{2,0},{1,5},{5,9},... | collective-permute-start | bytes 786440 | tf_op jit(solution)/shard_map/ppermute | solution.py:113
  46.1 12.8 %collective-permute-start.24 = (bf16[256,512]{1,0:T(8,128)(2,1)S(1)}, bf16[256,512]{1,0:T(8,128)(2,1)S(1)}, u32[]{:S(2)}, u32[]{:S(2)}) collective-permute-start(bf16[256,512]{1,0:T(8,128)(2,1)S(1)} %collective-permute-done.23), channel_id=1, source_target_pairs={{4,0},{8,4},{12,8},{14,12},{10,14},{6,10},{2,6},{0,2},{5,1},{9,5},... | collective-permute-start | bytes 786440 | tf_op jit(solution)/shard_map/ppermute | solution.py:113
  51.7 11.2 %collective-permute-start.4 = (bf16[256,512]{1,0:T(8,128)(2,1)S(1)}, bf16[256,512]{1,0:T(8,128)(2,1)S(1)}, u32[]{:S(2)}, u32[]{:S(2)}) collective-permute-start(bf16[256,512]{1,0:T(8,128)(2,1)S(1)} %collective-permute-done.3), channel_id=1, source_target_pairs={{0,4},{4,8},{8,12},{12,14},{14,10},{10,6},{6,2},{2,0},{1,5},{5,9},... | collective-permute-start | bytes 786440 | tf_op jit(solution)/shard_map/ppermute | solution.py:113
  53.2 11.3 %collective-permute-start.11 = (bf16[256,512]{1,0:T(8,128)(2,1)S(1)}, bf16[256,512]{1,0:T(8,128)(2,1)S(1)}, u32[]{:S(2)}, u32[]{:S(2)}) collective-permute-start(bf16[256,512]{1,0:T(8,128)(2,1)S(1)} %collective-permute-done.10), channel_id=1, source_target_pairs={{4,0},{8,4},{12,8},{14,12},{10,14},{6,10},{2,6},{0,2},{5,1},{9,5},... | collective-permute-start | bytes 786440 | tf_op jit(solution)/shard_map/ppermute | solution.py:113
  57.3 11.2 %collective-permute-start.18 = (bf16[256,512]{1,0:T(8,128)(2,1)S(1)}, bf16[256,512]{1,0:T(8,128)(2,1)S(1)}, u32[]{:S(2)}, u32[]{:S(2)}) collective-permute-start(bf16[256,512]{1,0:T(8,128)(2,1)S(1)} %collective-permute-done.17), channel_id=1, source_target_pairs={{0,4},{4,8},{8,12},{12,14},{14,10},{10,6},{6,2},{2,0},{1,5},{5,9},... | collective-permute-start | bytes 786440 | tf_op jit(solution)/shard_map/ppermute | solution.py:113
  58.9 11.3 %collective-permute-start.25 = (bf16[256,512]{1,0:T(8,128)(2,1)S(1)}, bf16[256,512]{1,0:T(8,128)(2,1)S(1)}, u32[]{:S(2)}, u32[]{:S(2)}) collective-permute-start(bf16[256,512]{1,0:T(8,128)(2,1)S(1)} %collective-permute-done.24), channel_id=1, source_target_pairs={{4,0},{8,4},{12,8},{14,12},{10,14},{6,10},{2,6},{0,2},{5,1},{9,5},... | collective-permute-start | bytes 786440 | tf_op jit(solution)/shard_map/ppermute | solution.py:113
  62.9 11.2 %collective-permute-start.5 = (bf16[256,512]{1,0:T(8,128)(2,1)S(1)}, bf16[256,512]{1,0:T(8,128)(2,1)S(1)}, u32[]{:S(2)}, u32[]{:S(2)}) collective-permute-start(bf16[256,512]{1,0:T(8,128)(2,1)S(1)} %collective-permute-done.4), channel_id=1, source_target_pairs={{0,4},{4,8},{8,12},{12,14},{14,10},{10,6},{6,2},{2,0},{1,5},{5,9},... | collective-permute-start | bytes 786440 | tf_op jit(solution)/shard_map/ppermute | solution.py:113
  64.5 11.2 %collective-permute-start.12 = (bf16[256,512]{1,0:T(8,128)(2,1)S(1)}, bf16[256,512]{1,0:T(8,128)(2,1)S(1)}, u32[]{:S(2)}, u32[]{:S(2)}) collective-permute-start(bf16[256,512]{1,0:T(8,128)(2,1)S(1)} %collective-permute-done.11), channel_id=1, source_target_pairs={{4,0},{8,4},{12,8},{14,12},{10,14},{6,10},{2,6},{0,2},{5,1},{9,5},... | collective-permute-start | bytes 786440 | tf_op jit(solution)/shard_map/ppermute | solution.py:113
  68.5 11.2 %collective-permute-start.19 = (bf16[256,512]{1,0:T(8,128)(2,1)S(1)}, bf16[256,512]{1,0:T(8,128)(2,1)S(1)}, u32[]{:S(2)}, u32[]{:S(2)}) collective-permute-start(bf16[256,512]{1,0:T(8,128)(2,1)S(1)} %collective-permute-done.18), channel_id=1, source_target_pairs={{0,4},{4,8},{8,12},{12,14},{14,10},{10,6},{6,2},{2,0},{1,5},{5,9},... | collective-permute-start | bytes 786440 | tf_op jit(solution)/shard_map/ppermute | solution.py:113
  70.2 11.2 %collective-permute-start.26 = (bf16[256,512]{1,0:T(8,128)(2,1)S(1)}, bf16[256,512]{1,0:T(8,128)(2,1)S(1)}, u32[]{:S(2)}, u32[]{:S(2)}) collective-permute-start(bf16[256,512]{1,0:T(8,128)(2,1)S(1)} %collective-permute-done.25), channel_id=1, source_target_pairs={{4,0},{8,4},{12,8},{14,12},{10,14},{6,10},{2,6},{0,2},{5,1},{9,5},... | collective-permute-start | bytes 786440 | tf_op jit(solution)/shard_map/ppermute | solution.py:113
  74.1 11.1 %collective-permute-start.6 = (bf16[256,512]{1,0:T(8,128)(2,1)S(1)}, bf16[256,512]{1,0:T(8,128)(2,1)S(1)}, u32[]{:S(2)}, u32[]{:S(2)}) collective-permute-start(bf16[256,512]{1,0:T(8,128)(2,1)S(1)} %collective-permute-done.5), channel_id=1, source_target_pairs={{0,4},{4,8},{8,12},{12,14},{14,10},{10,6},{6,2},{2,0},{1,5},{5,9},... | collective-permute-start | bytes 786440 | tf_op jit(solution)/shard_map/ppermute | solution.py:113
  75.7 10.8 %collective-permute-start.13 = (bf16[256,512]{1,0:T(8,128)(2,1)S(1)}, bf16[256,512]{1,0:T(8,128)(2,1)S(1)}, u32[]{:S(2)}, u32[]{:S(2)}) collective-permute-start(bf16[256,512]{1,0:T(8,128)(2,1)S(1)} %collective-permute-done.12), channel_id=1, source_target_pairs={{4,0},{8,4},{12,8},{14,12},{10,14},{6,10},{2,6},{0,2},{5,1},{9,5},... | collective-permute-start | bytes 786440 | tf_op jit(solution)/shard_map/ppermute | solution.py:113
  79.7 8.2 %collective-permute-start.20 = (bf16[256,512]{1,0:T(8,128)(2,1)S(1)}, bf16[256,512]{1,0:T(8,128)(2,1)S(1)}, u32[]{:S(2)}, u32[]{:S(2)}) collective-permute-start(bf16[256,512]{1,0:T(8,128)(2,1)S(1)} %collective-permute-done.19), channel_id=1, source_target_pairs={{0,4},{4,8},{8,12},{12,14},{14,10},{10,6},{6,2},{2,0},{1,5},{5,9},... | collective-permute-start | bytes 786440 | tf_op jit(solution)/shard_map/ppermute | solution.py:113
  81.3 7.9 %collective-permute-start.27 = (bf16[256,512]{1,0:T(8,128)(2,1)S(1)}, bf16[256,512]{1,0:T(8,128)(2,1)S(1)}, u32[]{:S(2)}, u32[]{:S(2)}) collective-permute-start(bf16[256,512]{1,0:T(8,128)(2,1)S(1)} %collective-permute-done.26), channel_id=1, source_target_pairs={{4,0},{8,4},{12,8},{14,12},{10,14},{6,10},{2,6},{0,2},{5,1},{9,5},... | collective-permute-start | bytes 786440 | tf_op jit(solution)/shard_map/ppermute | solution.py:113
  92.0 3.6 %collective-permute-start.28 = (bf16[256,2048]{1,0:T(8,128)(2,1)S(1)}, bf16[256,2048]{1,0:T(8,128)(2,1)S(1)}, u32[]{:S(2)}, u32[]{:S(2)}) collective-permute-start(bf16[256,2048]{1,0:T(8,128)(2,1)S(1)} %get-tuple-element.194), channel_id=1, source_target_pairs={{0,1},{2,3},{4,5},{6,7},{8,9},{10,11},{12,13},{14,15},{16,17},{18,... | collective-permute-start | bytes 3145736 | tf_op jit(solution)/shard_map/ppermute | solution.py:18
  93.9 8.4 %copy-start = (bf16[2048,2048]{1,0:T(8,128)(2,1)}, bf16[2048,2048]{1,0:T(8,128)(2,1)S(1)}, u32[]{:S(2)}) copy-start(bf16[2048,2048]{1,0:T(8,128)(2,1)S(1)} %constant_dynamic-update-slice_fusion) | copy-start | bytes 25165828
  96.2 6.1 %copy-start.6 = (bf16[128,2048]{1,0:T(8,128)(2,1)S(1)}, bf16[128,2048]{1,0:T(8,128)(2,1)}, u32[]{:S(2)}) copy-start(bf16[128,2048]{1,0:T(8,128)(2,1)} %param.9) | copy-start | bytes 1572868
  102.3 17.1 %copy-start.3 = (f32[128,2048]{1,0:T(8,128)S(1)}, f32[128,2048]{1,0:T(8,128)}, u32[]{:S(2)}) copy-start(f32[128,2048]{1,0:T(8,128)} %convert_element_type.66) | copy-start | bytes 3145732
  103.7 3.6 %collective-permute-start.29 = (f32[7]{0:T(128)S(1)}, f32[7]{0:T(128)S(1)}, u32[]{:S(2)}, u32[]{:S(2)}) collective-permute-start(f32[7]{0:T(128)S(1)} %pad_maximum_fusion.1), channel_id=1, source_target_pairs={{0,2},{2,0},{4,6},{6,4},{8,10},{10,8},{12,14},{14,12},{1,3},{3,1},... | collective-permute-start | bytes 92 | tf_op jit(solution)/shard_map/ppermute | solution.py:128
  108.0 3.6 %collective-permute-start.30 = (f32[7]{0:T(128)S(1)}, f32[7]{0:T(128)S(1)}, u32[]{:S(2)}, u32[]{:S(2)}) collective-permute-start(f32[7]{0:T(128)S(1)} %fusion.150), channel_id=1, source_target_pairs={{0,4},{2,6},{4,0},{6,2},{8,12},{10,14},{12,8},{14,10},{1,5},{3,7},... | collective-permute-start | bytes 92 | tf_op jit(solution)/shard_map/ppermute | solution.py:128
  111.6 4.5 %collective-permute-start.31 = (f32[7]{0:T(128)S(1)}, f32[7]{0:T(128)S(1)}, u32[]{:S(2)}, u32[]{:S(2)}) collective-permute-start(f32[7]{0:T(128)S(1)} %add.463), channel_id=1, source_target_pairs={{0,8},{2,10},{4,12},{6,14},{8,0},{10,2},{12,4},{14,6},{1,9},{3,11}... | collective-permute-start | bytes 92 | tf_op jit(solution)/shard_map/ppermute | solution.py:128
  120.5 12.0 %collective-permute-start.32 = (bf16[256,2048]{1,0:T(8,128)(2,1)}, bf16[256,2048]{1,0:T(8,128)(2,1)S(1)}, u32[]{:S(2)}, u32[]{:S(2)}) collective-permute-start(bf16[256,2048]{1,0:T(8,128)(2,1)} %get-tuple-element.204), channel_id=1, source_target_pairs={{1,0},{3,2},{5,4},{7,6},{9,8},{11,10},{13,12},{15,14},{17,16},{19,... | collective-permute-start | bytes 3145736 | tf_op jit(solution)/shard_map/ppermute | solution.py:18
  122.9 9.0 %collective-permute-start.33 = (f32[1]{0:T(128)}, f32[1]{0:T(128)}, u32[]{:S(2)}, u32[]{:S(2)}) collective-permute-start(f32[1]{0:T(128)} %bitcast.20), channel_id=1, source_target_pairs={{1,0},{3,2},{5,4},{7,6},{9,8},{11,10},{13,12},{15,14},{17,16},{19,... | collective-permute-start | bytes 20 | tf_op jit(solution)/shard_map/ppermute | solution.py:18
